TPU v7x, 32 devices: a whole 2x2x4 slice. The times are simulated.
32 devices in a mesh: groups: 2 (over y), seq: 4 (over z), chan: 2 (over x), pair: 2 (over core).
Axes of the slice: x: 2, y: 2, z: 4, core: 2. Of those that a mesh axis runs over, the one named last changes fastest.
Arguments:
- tokens: int32 [1024], P(('groups', 'seq')), parts along dimension 0, may hold values from 0 to 4
- kmer_table: bfloat16 [4, 5, 2048], replicated, may hold values from -3 to 3
- norm_gain: float32 [2048], replicated, may hold values from 0.3 to 2, as said below
- in_proj: bfloat16 [2048, 3, 2048], P(None, None, ('chan', 'pair')), may hold values from -0.125 to 0.125
- long_filter: float32 [4, 4, 128, 512], P(('chan', 'pair'), 'seq'), may hold values from -1 to 1, as said below
- out_proj: bfloat16 [2048, 2048], P(None, ('chan', 'pair')), may hold values from -0.125 to 0.125
- cotangent: bfloat16 [1024, 2048], P(('groups', 'seq'), ('chan', 'pair')), parts along dimension 0, may hold values from -6 to 6
Outputs:
- block_out: bfloat16 [1024, 2048], P(('groups', 'seq'), ('chan', 'pair')), parts along dimension 0
- filter_grad: float32 [8, 4, 128, 512], P(('groups', 'chan', 'pair'), 'seq'), parts along dimension 0
- kmer_grad: float32 [8, 5, 2048], P('groups', None, ('chan', 'pair')), parts along dimension 0
- gain_grad: float32 [4096], P(('groups', 'chan', 'pair')), parts along dimension 0
There are 2 independent parts, one for each index of `groups`. A program takes and returns all parts, laid end to end along the dimension named above; an argument that names none is the same for every part. Nothing has to cross between parts.
Inputs may be any that keep to these rules, and one draw needn't show every extreme that they name: `tokens`: nucleotide ids: 0 to 3 for A, C, G, T and 4 for N. `long_filter`: a causal filter for each channel. `norm_gain`: a positive gain for each channel.
All inputs are finite; a program needn't handle non-finite values.
Results may differ from a plain program's by a relative error of at most 0.0072.
Values may be sent and summed in bfloat16 or wider, within the bound.
No kernel may reach another device: no remote copies, remote signals or barrier semaphores. Data moves between devices by JAX's collectives and lax.ppermute only.
A program may use at most 128 MiB of HBM per device.

v0:
```python
import math

import jax
import jax.numpy as jnp
from jax import lax
from jax.sharding import PartitionSpec as P

NORM_EPSILON = 1e-05
PRECISE = lax.Precision.HIGHEST
TRANSFORM_PRECISION = lax.Precision.HIGH


def from_behind(value, axis, steps):
    count = lax.axis_size(axis)
    first, last = (max(0, -steps), min(count, count - steps))
    return lax.ppermute(value, axis, [(source, source + steps) for source in range(first, last)])


def dft_matrix(length):
    total = 2 * length
    t = lax.optimization_barrier(lax.broadcasted_iota(jnp.int32, (length, 1), 0))
    j = lax.broadcasted_iota(jnp.int32, (1, total), 1)
    k = jnp.where(j < length, j, j - length)
    k = jnp.where(j == length, length, k)
    idx = (t * k) % total
    idx = jnp.where(j > length, (idx + 3 * total // 4) % total, idx)
    idx = jnp.where(idx >= length, idx - total, idx)
    return lax.optimization_barrier(jnp.cos(idx.astype(jnp.float32) * (2.0 * math.pi / total)))


def forward_dft(signal, dft):
    return jnp.dot(signal.astype(jnp.float32), dft, precision=TRANSFORM_PRECISION)


def inverse_dft(spec, dft):
    length = dft.shape[0]
    total = 2 * length
    col = lax.broadcasted_iota(jnp.int32, (1, total), 1)
    weight = jnp.where(col % length == 0, 1.0 / total, 2.0 / total).astype(jnp.float32)
    return lax.dot_general(
        spec * weight, dft, (((1,), (1,)), ((), ())), precision=TRANSFORM_PRECISION
    )


def halves(spec):
    length = spec.shape[1] // 2
    return spec[:, :length], spec[:, length:]


def first_col(shape):
    return lax.broadcasted_iota(jnp.int32, shape, 1) == 0


def cmul(ga, gb, xa, xb, conj_g):
    edge = first_col(ga.shape)
    sign = -1.0 if conj_g else 1.0
    ya = ga * xa - sign * (gb * xb)
    yb = ga * xb + sign * (gb * xa)
    ya = jnp.where(edge, ga * xa, ya)
    yb = jnp.where(edge, gb * xb, yb)
    return jnp.concatenate([ya, yb], axis=1)


def pair_flip(values):
    rows = lax.broadcasted_iota(jnp.int32, values.shape, 0)
    up = jnp.roll(values, -1, axis=0)
    down = jnp.roll(values, 1, axis=0)
    return jnp.where(rows % 2 == 0, up, down)


def add_conj_flip(spec):
    a, b = halves(spec)
    fa, fb = halves(pair_flip(spec))
    edge = first_col(a.shape)
    return jnp.concatenate([a + fa, jnp.where(edge, b + fb, b - fb)], axis=1)


def per_device(tokens, kmer_table, norm_gain, in_proj, long_filter, out_proj, cotangent):
    row_count = tokens.shape[0]
    kmer_len, letter_count, model_width = kmer_table.shape
    local_width = in_proj.shape[2]
    length = row_count * lax.axis_size("seq")
    group_index = lax.axis_index(("chan", "pair"))
    rim_width = kmer_len - 1
    before = from_behind(tokens[row_count - rim_width :] + 1, "seq", 1) - 1
    extended = jnp.concatenate([before, tokens])
    letters = jnp.arange(letter_count, dtype=jnp.int32)
    columns = []
    for shift_back in range(kmer_len):
        window = extended[rim_width - shift_back : rim_width - shift_back + row_count]
        columns.append(window[:, None] == letters[None, :])
    onehot_t = jnp.concatenate(columns, axis=1).T.astype(jnp.bfloat16)
    table_t = kmer_table.reshape(kmer_len * letter_count, model_width).T
    embedded = jnp.dot(table_t, onehot_t, preferred_element_type=jnp.float32)
    inv_rms = lax.rsqrt(jnp.mean(embedded * embedded, axis=0, keepdims=True) + NORM_EPSILON)
    normed = embedded * inv_rms
    hidden = (normed * norm_gain[:, None]).astype(jnp.bfloat16)
    projected = jnp.einsum("dr,dmc->mcr", hidden, in_proj, preferred_element_type=jnp.float32)
    query_part = projected[0]
    key_part = projected[1]
    value_part = projected[2]
    mixed_in = (key_part * value_part).astype(jnp.bfloat16)
    dft = dft_matrix(length)
    filter_rows = long_filter.reshape(long_filter.shape[2], long_filter.shape[3])
    spec_g = add_conj_flip(forward_dft(filter_rows, dft))
    ga, gb = halves(spec_g)
    mixed_cols = lax.all_to_all(mixed_in, "seq", split_axis=0, concat_axis=1, tiled=True)
    spec_s = forward_dft(mixed_cols, dft)
    sa, sb = halves(spec_s)
    conv_cols = inverse_dft(cmul(ga, gb, sa, sb, False), dft).astype(jnp.bfloat16)
    conv_rows = lax.all_to_all(conv_cols, "seq", split_axis=1, concat_axis=0, tiled=True)
    gated_rows = (query_part * conv_rows.astype(jnp.float32)).astype(jnp.bfloat16)
    weight_rows = out_proj
    mixed_out = jnp.einsum(
        "cr,cd->rd",
        lax.all_gather(gated_rows, ("chan", "pair"), axis=0, tiled=True),
        weight_rows,
        preferred_element_type=jnp.float32,
    )
    own_rows = lax.dynamic_slice_in_dim(embedded, group_index * local_width, local_width, 0)
    block_out = (mixed_out + own_rows.T).astype(jnp.bfloat16)
    grad_scale = 1.0 / math.sqrt(length)
    d_gated = (
        lax.psum_scatter(
            jnp.einsum("cd,rd->cr", weight_rows, cotangent, preferred_element_type=jnp.float32),
            ("chan", "pair"),
            scatter_dimension=0,
            tiled=True,
        )
        * grad_scale
    )
    d_conv = (d_gated * query_part).astype(jnp.bfloat16)
    d_query = d_gated * conv_rows.astype(jnp.float32)
    d_cols = lax.all_to_all(d_conv, "seq", split_axis=0, concat_axis=1, tiled=True)
    spec_d = forward_dft(d_cols, dft)
    da, db = halves(spec_d)
    d_mixed_cols = inverse_dft(cmul(ga, gb, da, db, True), dft).astype(jnp.bfloat16)
    d_mixed = lax.all_to_all(d_mixed_cols, "seq", split_axis=1, concat_axis=0, tiled=True)
    cross = cmul(sa, sb, da, db, True)
    filter_grad = inverse_dft(add_conj_flip(cross), dft)
    d_key = d_mixed.astype(jnp.float32) * value_part
    d_value = d_mixed.astype(jnp.float32) * key_part
    d_proj = jnp.stack([d_query, d_key, d_value]).astype(jnp.bfloat16)
    normed_local = lax.dynamic_slice_in_dim(normed, group_index * local_width, local_width, 0)
    cot_scaled = cotangent.T.astype(jnp.float32) * grad_scale
    d_full = lax.psum(
        jnp.einsum("dmc,mcr->dr", in_proj, d_proj, preferred_element_type=jnp.float32),
        ("chan", "pair"),
    )
    scaled_full = norm_gain[:, None] * d_full
    row_stat = jnp.mean(scaled_full * normed, axis=0, keepdims=True)
    scaled = lax.dynamic_slice_in_dim(scaled_full, group_index * local_width, local_width, 0)
    d_embedded = inv_rms * (scaled - normed_local * row_stat) + cot_scaled
    d_hidden = lax.dynamic_slice_in_dim(d_full, group_index * local_width, local_width, 0)
    gain_part = jnp.sum(d_hidden * normed_local, axis=1)
    table_part = jnp.einsum(
        "kr,cr->kc", onehot_t.astype(jnp.float32), d_embedded, precision=PRECISE
    )
    summed = lax.psum(jnp.concatenate([table_part, gain_part[None, :]], axis=0), "seq")
    kmer_grad = summed[: kmer_len * letter_count]
    gain_grad = summed[kmer_len * letter_count]
    return (
        block_out,
        filter_grad.reshape(long_filter.shape),
        kmer_grad.reshape(kmer_len, letter_count, local_width),
        gain_grad,
    )


def solution(mesh):
    in_specs = (
        P(("groups", "seq")),
        P(),
        P(),
        P(None, None, ("chan", "pair")),
        P(("chan", "pair"), "seq", None, None),
        P(None, ("chan", "pair")),
        P(("groups", "seq"), ("chan", "pair")),
    )
    out_specs = (
        P(("groups", "seq"), ("chan", "pair")),
        P(("groups", "chan", "pair"), "seq", None, None),
        P("groups", None, ("chan", "pair")),
        P(("groups", "chan", "pair")),
    )
    return jax.shard_map(
        per_device, mesh=mesh, in_specs=in_specs, out_specs=out_specs, check_vma=False
    )
```

profile of v0, /device:TPU:0, one launch (start us, length us, event | category | flops | bytes accessed | tf_op | source)
XLA Modules:
  0.0 173.6 jit_solution(6065162141426624654)
XLA Ops:
  7.2 0.9 slice_add_fusion.2
  8.1 5.1 %collective-permute-start = (s32[3]{0:T(128)S(1)}, s32[3]{0:T(128)S(1)}, u32[]{:S(2)}, u32[]{:S(2)}) collective-permute-start(s32[3]{0:T(128)S(1)} %slice_add_fusion.2), channel_id=1, source_target_pairs={{0,4},{4,8},{8,12},{1,5},{5,9},{9,13},{2,6},{6,10},{10,14},{3,7},{... | collective-permute-start | bytes 44 | tf_op jit(solution)/shard_map/ppermute | solution.py:16
  13.2 2.7 %fusion.66 = f32[2048,128]{0,1:T(8,128)} fusion(bf16[2048,512]{1,0:T(8,128)(2,1)S(1)} %copy-done, bf16[128,512]{1,0:T(8,128)(2,1)} %param.13), kind=kOutput, calls=%fused_computation.144 | convolution fusion | flops 268435456 | bytes 3276800 | tf_op jit(solution)/shard_map/cd,rd->cr/dot_general | solution.py:125
  16.0 8.7 %fusion.5 = f32[512,1024]{1,0:T(8,128)S(1)} fusion(s32[1024]{0:T(1024)S(1)} %fusion.50, s32[512]{0:T(512)S(1)} %bitcast.109, pred[1024]{0:T(1024)(128)(4,1)S(1)} %iota_compare_fusion.1), kind=kLoop, calls=%fused_computation.15 | loop fusion | flops 15728640 | bytes 2104320 | tf_op jit(solution)/shard_map/cos | solution.py:28
  24.8 0.7 convolution_bitcast_fusion.2
  25.5 1.2 fusion.63
  27.1 0.4 multiply_reduce_fusion
  27.7 1.0 copy-done.8
  28.7 4.7 %convolution_bitcast_fusion.1 = f32[3,512,128]{1,2,0:T(8,128)} fusion(bf16[2048,3,512]{2,0,1:T(8,128)(2,1)} %param.10, f32[128,2048]{1,0:T(8,128)S(1)} %broadcast_multiply_fusion.1, f32[2048]{0:T(1024)S(1)} %copy-done.19), kind=kOutput, calls=%fused_computation.17 | convolution fusion | flops 805830656 | bytes 8134656 | tf_op jit(solution)/shard_map/dr,dmc->mcr/dot_general | solution.py:98
  33.4 7.7 %reduce-scatter.2.cloned.1.call-done = f32[512,128]{0,1:T(8,128)} async-done(((f32[2048,128]{0,1:T(8,128)}), f32[512,128]{0,1:T(8,128)}) %reduce-scatter.2.cloned.1.call-update) | async-done | bytes 262160 | tf_op jit(solution)/shard_map/reduce_scatter | solution.py:124
  41.1 1.7 copy_bitcast_fusion
  42.8 4.6 %all-to-all-start.2 = ((bf16[4,128,128]{1,2,0:T(8,128)(2,1)}), bf16[4,128,128]{1,2,0:T(8,128)(2,1)S(1)}, u32[]{:S(2)}, u32[]{:S(2)}) async-start(bf16[4,128,128]{1,2,0:T(8,128)(2,1)} %copy_bitcast_fusion), calls=%async_computation.3 | async-start | bytes 262144 | tf_op jit(solution)/shard_map/all_to_all | solution.py:134
  47.4 2.1 %maximum_select_fusion = f32[128,1024]{1,0:T(8,128)} fusion(f32[1,1024]{1,0:T(1,128)S(1)} %get-tuple-element.35, f32[127,1024]{1,0:T(8,128)} %get-tuple-element.37, f32[127,1024]{1,0:T(8,128)} %get-tuple-element.36, f32[1,1024]{1,0:T(1,128)S(1)} %get-tuple-element.34, s32[128]{0:T(128)S(1)} %iota_and_fusion.1, s32[128]{0:T(128)S(1)} %broadcast_add_fusion, ...), kind=kLoop, calls=%fused_computation.40 | loop fusion | flops 655360 | bytes 1574016 | tf_op jit(solution)/shard_map/jit(_where)/select_n | solution.py:68
  49.5 3.9 %all-to-all-done.2 = bf16[4,128,128]{1,2,0:T(8,128)(2,1)S(1)} async-done(((bf16[4,128,128]{1,2,0:T(8,128)(2,1)}), bf16[4,128,128]{1,2,0:T(8,128)(2,1)S(1)}, u32[]{:S(2)}, u32[]{:S(2)}) %all-to-all-start.2) | async-done | bytes 131104 | tf_op jit(solution)/shard_map/all_to_all | solution.py:134
  53.5 2.2 %fusion.67 = f32[128,1024]{1,0:T(8,128)S(1)} fusion(bf16[128,512]{0,1:T(8,128)(2,1)S(1)} %bitcast.106, f32[512,1024]{1,0:T(8,128)} %copy-done.1), kind=kOutput, calls=%fused_computation.145 | convolution fusion | flops 402653184 | bytes 2752512 | tf_op jit(solution)/shard_map/dot_general | solution.py:32
  55.8 0.2 subtract_select_fusion
  56.0 0.6 copy-done.6
  56.7 1.0 copy-done.2
  57.7 1.2 convolution_convert_fusion
  59.0 8.3 %all_to_all.61 = bf16[128,4,128]{0,2,1:T(8,128)(2,1)S(1)} all-to-all(bf16[128,4,128]{0,2,1:T(8,128)(2,1)S(1)} %bitcast.104), channel_id=1, replica_groups=mesh['groups'=2,'seq'=4,'chan'=2,'pair'=2] {'seq'}, dimensions={1} | all-to-all | bytes 262144 | tf_op jit(solution)/shard_map/all_to_all | solution.py:138
  67.4 0.2 copy.29
  67.5 0.8 reshape.116
  68.3 1.8 %multiply_convert_fusion.1 = (bf16[1,512,128]{1,2,0:T(8,128)(2,1)S(1)}, bf16[1,512,128]{1,2,0:T(8,128)(2,1)}, bf16[1,512,128]{1,2,0:T(8,128)(2,1)S(1)}) fusion(f32[1,512,128]{1,2,0:T(8,128)} %reshape.116, f32[3,512,128]{1,2,0:T(8,128)} %convolution_bitcast_fusion.1), kind=kLoop, calls=%fused_computation.83 | loop fusion | flops 393216 | bytes 1179648 | tf_op jit(solution)/shard_map/convert.5
  70.2 0.7 copy.23
  70.9 3.3 %all-to-all-start = ((bf16[4,128,128]{1,2,0:T(8,128)(2,1)}), bf16[4,128,128]{1,2,0:T(8,128)(2,1)S(1)}, u32[]{:S(2)}, u32[]{:S(2)}) async-start(bf16[4,128,128]{1,2,0:T(8,128)(2,1)} %copy.23), calls=%async_computation | async-start | bytes 262144 | tf_op jit(solution)/shard_map/all_to_all | solution.py:107
  74.2 5.9 %all-to-all-done = bf16[4,128,128]{1,2,0:T(8,128)(2,1)S(1)} async-done(((bf16[4,128,128]{1,2,0:T(8,128)(2,1)}), bf16[4,128,128]{1,2,0:T(8,128)(2,1)S(1)}, u32[]{:S(2)}, u32[]{:S(2)}) %all-to-all-start) | async-done | bytes 131104 | tf_op jit(solution)/shard_map/all_to_all | solution.py:107
  80.1 2.2 %fusion.65 = f32[128,1024]{1,0:T(8,128)S(1)} fusion(bf16[128,512]{0,1:T(8,128)(2,1)S(1)} %bitcast.105, f32[512,1024]{1,0:T(8,128)} %copy-done.1), kind=kOutput, calls=%fused_computation.143 | convolution fusion | flops 402653184 | bytes 2752512 | tf_op jit(solution)/shard_map/dot_general | solution.py:32
  82.4 1.4 subtract_select_fusion.1
  83.8 0.9 fusion.10
  84.6 0.6 fusion.47
  85.2 1.8 %convolution_convert_fusion.1 = bf16[128,512]{1,0:T(8,128)(2,1)} fusion(f32[512,1024]{1,0:T(8,128)S(1)} %copy-done.3, f32[128,512]{1,0:T(8,128)S(1)} %get-tuple-element.28, f32[128,512]{1,0:T(8,128)S(1)} %get-tuple-element.29, f32[1024]{0:T(1024)S(1)} %fusion.54), kind=kOutput, calls=%fused_computation.23 | convolution fusion | flops 402980864 | bytes 2756608 | tf_op jit(solution)/shard_map/dot_general | solution.py:40
  87.1 1.7 copy.32
  88.8 4.0 %all-to-all-start.1 = ((bf16[128,4,128]{0,2,1:T(8,128)(2,1)}), bf16[128,4,128]{0,2,1:T(8,128)(2,1)}, u32[]{:S(2)}, u32[]{:S(2)}) async-start(bf16[128,4,128]{0,2,1:T(8,128)(2,1)} %bitcast.103), calls=%async_computation.1 | async-start | bytes 262144 | tf_op jit(solution)/shard_map/all_to_all | solution.py:111
  92.8 1.3 fusion.14
  94.1 1.9 %slice_add_fusion = (f32[128,512]{1,0:T(8,128)}, f32[128,512]{1,0:T(8,128)}) fusion(f32[128,512]{1,0:T(8,128)S(1)} %get-tuple-element.21, f32[128,1024]{1,0:T(8,128)S(1)} %fusion.14, f32[128,512]{1,0:T(8,128)} %copy-done.10, pred[512]{0:T(512)(128)(4,1)} %copy-done.24), kind=kLoop, calls=%fused_computation.66 | loop fusion | flops 262144 | bytes 1573376 | tf_op jit(solution)/shard_map/add | solution.py:75
  95.9 2.8 %all-to-all-done.1 = bf16[128,4,128]{0,2,1:T(8,128)(2,1)} async-done(((bf16[128,4,128]{0,2,1:T(8,128)(2,1)}), bf16[128,4,128]{0,2,1:T(8,128)(2,1)}, u32[]{:S(2)}, u32[]{:S(2)}) %all-to-all-start.1) | async-done | bytes 131104 | tf_op jit(solution)/shard_map/all_to_all | solution.py:111
  98.7 1.8 %fusion.43 = (bf16[1,512,128]{1,2,0:T(8,128)(2,1)S(1)}, bf16[512,128]{0,1:T(8,128)(2,1)}) fusion(f32[512,128]{0,1:T(8,128)} %reduce-scatter.2.cloned.1.call-done, f32[3,512,128]{1,2,0:T(8,128)} %convolution_bitcast_fusion.1, bf16[128,4,128]{0,2,1:T(8,128)(2,1)} %all-to-all-done.1), kind=kLoop, calls=%fused_computation.99 | loop fusion | flops 393216 | bytes 917504 | tf_op jit(solution)/shard_map/stack | solution.py:143
  100.5 6.1 %convolution_bitcast_fusion = f32[2048,128]{0,1:T(8,128)} fusion(bf16[2048,3,512]{2,0,1:T(8,128)(2,1)} %param.10, bf16[1,512,128]{1,2,0:T(8,128)(2,1)} %get-tuple-element.26, bf16[1,512,128]{1,2,0:T(8,128)(2,1)S(1)} %get-tuple-element.25, bf16[1,512,128]{1,2,0:T(8,128)(2,1)S(1)} %get-tuple-element.38), kind=kOutput, calls=%fused_computation.9 | convolution fusion | flops 805699584 | bytes 7733248 | tf_op jit(solution)/shard_map/dmc,mcr->dr/dot_general | solution.py:147
  106.6 3.6 %convolution_bitcast_fusion.3 = f32[1,1,128,512]{3,2,1,0:T(8,128)} fusion(f32[512,1024]{1,0:T(8,128)} %copy-done.1, f32[128,512]{1,0:T(8,128)} %get-tuple-element.31, f32[128,512]{1,0:T(8,128)S(1)} %copy-done.14, f32[1024]{0:T(1024)S(1)} %fusion.54), kind=kOutput, calls=%fused_computation.19 | convolution fusion | flops 402915328 | bytes 2887680 | tf_op jit(solution)/shard_map/dot_general | solution.py:40
  110.2 10.1 %all_gather.3 = bf16[2048,128]{0,1:T(8,128)(2,1)S(1)} all-gather(bf16[512,128]{0,1:T(8,128)(2,1)S(1)} %copy-done.16), channel_id=1, replica_groups=mesh['groups'=2,'seq'=4,'chan'=2,'pair'=2] {'chan','pair'}, dimensions={0}, use_global_device_ids=true | all-gather | bytes 655360 | tf_op jit(solution)/shard_map/all_gather | solution.py:116
  120.2 1.1 fusion.7
  121.4 21.7 %all-reduce.2.cloned.1.call-done = f32[2048,128]{0,1:T(8,128)} async-done(((f32[2048,128]{0,1:T(8,128)}), f32[2048,128]{0,1:T(8,128)}) %all-reduce.2.cloned.1.call-update) | async-done | bytes 1048592 | tf_op jit(solution)/shard_map/psum | solution.py:146
  143.1 1.6 fusion.9
  144.8 0.3 fusion.29
  145.1 1.0 fusion.33
  146.1 19.4 %psum.15 = f32[21,512]{1,0:T(8,128)S(1)} all-reduce(f32[21,512]{1,0:T(8,128)S(1)} %pad_maximum_fusion.1), channel_id=1, replica_groups=mesh['groups'=2,'seq'=4,'chan'=2,'pair'=2] {'seq'}, use_global_device_ids=true, to_apply=%region_5.6 | all-reduce | flops 10752 | bytes 86016 | tf_op jit(solution)/shard_map/psum | solution.py:159
  165.5 0.6 slice.136
  166.1 0.6 copy.30
  (98 shorter events, 1.1 us)
Async XLA Ops:
  7.2 6.0 %copy-start = (bf16[2048,512]{1,0:T(8,128)(2,1)S(1)}, bf16[2048,512]{1,0:T(8,128)(2,1)}, u32[]{:S(2)}) copy-start(bf16[2048,512]{1,0:T(8,128)(2,1)} %param.12) | copy-start | bytes 6291460
  7.2 33.9 %reduce-scatter.2.cloned.1.call-start = ((), (), s32[]{:S(2)}) async-start(), calls=%async_computation.5 | async-start | bytes 1310720 | tf_op jit(solution)/shard_map/reduce_scatter | solution.py:124
  8.1 7.8 %copy-start.34 = (s32[128]{0:T(128)S(1)}, s32[128]{0:T(128)}, u32[]{:S(2)}) copy-start(s32[128]{0:T(128)} %param.7) | copy-start | bytes 1540
  8.1 18.8 %collective-permute-start = (s32[3]{0:T(128)S(1)}, s32[3]{0:T(128)S(1)}, u32[]{:S(2)}, u32[]{:S(2)}) collective-permute-start(s32[3]{0:T(128)S(1)} %slice_add_fusion.2), channel_id=1, source_target_pairs={{0,4},{4,8},{8,12},{1,5},{5,9},{9,13},{2,6},{6,10},{10,14},{3,7},{... | collective-permute-start | bytes 44 | tf_op jit(solution)/shard_map/ppermute | solution.py:16
  15.9 8.8 %copy-start.17 = (f32[1,1,128,512]{3,2,1,0:T(8,128)S(1)}, f32[1,1,128,512]{3,2,1,0:T(8,128)}, u32[]{:S(2)}) copy-start(f32[1,1,128,512]{3,2,1,0:T(8,128)} %param.11) | copy-start | bytes 786436
  16.0 11.2 %copy-start.27 = (pred[128,5]{0,1:T(8,128)(4,1)}, pred[128,5]{0,1:T(8,128)(4,1)S(1)}, u32[]{:S(2)}) copy-start(pred[128,5]{0,1:T(8,128)(4,1)S(1)} %iota_compare_fusion.5) | copy-start | bytes 1924
  24.8 1.9 %copy-start.1 = (f32[512,1024]{1,0:T(8,128)}, f32[512,1024]{1,0:T(8,128)S(1)}, u32[]{:S(2)}) copy-start(f32[512,1024]{1,0:T(8,128)S(1)} %fusion.5) | copy-start | bytes 6291460
  24.8 2.0 %copy-start.18 = (bf16[4,5,2048]{2,0,1:T(4,128)(2,1)S(1)}, bf16[4,5,2048]{2,0,1:T(4,128)(2,1)}, u32[]{:S(2)}) copy-start(bf16[4,5,2048]{2,0,1:T(4,128)(2,1)} %param.8) | copy-start | bytes 245764
  25.5 1.2 copy-start.4
  26.7 2.1 %copy-start.19 = (f32[2048]{0:T(1024)S(1)}, f32[2048]{0:T(1024)}, u32[]{:S(2)}) copy-start(f32[2048]{0:T(1024)} %param.9) | copy-start | bytes 24580
  26.7 20.7 %copy-start.31 = (s32[128]{0:T(128)}, s32[128]{0:T(128)S(1)}, u32[]{:S(2)}) copy-start(s32[128]{0:T(128)S(1)} %broadcast_add_fusion) | copy-start | bytes 1540
  26.7 20.7 %copy-start.32 = (pred[128]{0:T(512)(128)(4,1)}, pred[128]{0:T(512)(128)(4,1)S(1)}, u32[]{:S(2)}) copy-start(pred[128]{0:T(512)(128)(4,1)S(1)} %compare_and_fusion) | copy-start | bytes 388
  26.7 20.7 %copy-start.33 = (s32[128]{0:T(128)}, s32[128]{0:T(128)S(1)}, u32[]{:S(2)}) copy-start(s32[128]{0:T(128)S(1)} %iota_and_fusion.1) | copy-start | bytes 1540
  26.8 55.6 %copy-start.24 = (pred[512]{0:T(512)(128)(4,1)}, pred[512]{0:T(512)(128)(4,1)S(1)}, u32[]{:S(2)}) copy-start(pred[512]{0:T(512)(128)(4,1)S(1)} %iota_compare_fusion.6) | copy-start | bytes 1540
  27.1 6.3 %copy-start.29 = (pred[128,5]{0,1:T(8,128)(4,1)}, pred[128,5]{0,1:T(8,128)(4,1)S(1)}, u32[]{:S(2)}) copy-start(pred[128,5]{0,1:T(8,128)(4,1)S(1)} %iota_compare_fusion.4) | copy-start | bytes 1924
  27.1 6.3 %copy-start.20 = (pred[128,5]{0,1:T(8,128)(4,1)}, pred[128,5]{0,1:T(8,128)(4,1)S(1)}, u32[]{:S(2)}) copy-start(pred[128,5]{0,1:T(8,128)(4,1)S(1)} %get-tuple-element.45) | copy-start | bytes 1924
  27.1 6.3 %copy-start.22 = (pred[128,5]{0,1:T(8,128)(4,1)}, pred[128,5]{0,1:T(8,128)(4,1)S(1)}, u32[]{:S(2)}) copy-start(pred[128,5]{0,1:T(8,128)(4,1)S(1)} %get-tuple-element.46) | copy-start | bytes 1924
  27.6 5.9 %copy-start.25 = (f32[128]{0:T(128)}, f32[128]{0:T(128)S(1)}, u32[]{:S(2)}) copy-start(f32[128]{0:T(128)S(1)} %add_rsqrt_fusion) | copy-start | bytes 1540
  27.7 1.0 copy-start.8
  42.8 10.7 %all-to-all-start.2 = ((bf16[4,128,128]{1,2,0:T(8,128)(2,1)}), bf16[4,128,128]{1,2,0:T(8,128)(2,1)S(1)}, u32[]{:S(2)}, u32[]{:S(2)}) async-start(bf16[4,128,128]{1,2,0:T(8,128)(2,1)} %copy_bitcast_fusion), calls=%async_computation.3 | async-start | bytes 262144 | tf_op jit(solution)/shard_map/all_to_all | solution.py:134
  53.5 2.2 %copy-start.5 = (f32[128,1024]{1,0:T(8,128)S(1)}, f32[128,1024]{1,0:T(8,128)}, u32[]{:S(2)}) copy-start(f32[128,1024]{1,0:T(8,128)} %copy-done.4) | copy-start | bytes 1572868
  53.5 2.2 %copy-start.13 = (f32[128,1024]{1,0:T(8,128)S(1)}, f32[128,1024]{1,0:T(8,128)}, u32[]{:S(2)}) copy-start(f32[128,1024]{1,0:T(8,128)} %maximum_select_fusion) | copy-start | bytes 1572868
  55.7 0.8 copy-start.6
  55.7 2.0 %copy-start.2 = (f32[512,1024]{1,0:T(8,128)S(1)}, f32[512,1024]{1,0:T(8,128)}, u32[]{:S(2)}) copy-start(f32[512,1024]{1,0:T(8,128)} %copy-done.1) | copy-start | bytes 6291460
  55.9 0.7 copy-start.11
  55.9 0.8 copy-start.12
  70.9 9.2 %all-to-all-start = ((bf16[4,128,128]{1,2,0:T(8,128)(2,1)}), bf16[4,128,128]{1,2,0:T(8,128)(2,1)S(1)}, u32[]{:S(2)}, u32[]{:S(2)}) async-start(bf16[4,128,128]{1,2,0:T(8,128)(2,1)} %copy.23), calls=%async_computation | async-start | bytes 262144 | tf_op jit(solution)/shard_map/all_to_all | solution.py:107
  80.1 2.2 %copy-start.7 = (f32[128,1024]{1,0:T(8,128)S(1)}, f32[128,1024]{1,0:T(8,128)}, u32[]{:S(2)}) copy-start(f32[128,1024]{1,0:T(8,128)} %copy-done.6) | copy-start | bytes 1572868
  82.3 2.9 %copy-start.3 = (f32[512,1024]{1,0:T(8,128)S(1)}, f32[512,1024]{1,0:T(8,128)}, u32[]{:S(2)}) copy-start(f32[512,1024]{1,0:T(8,128)} %copy-done.1) | copy-start | bytes 6291460
  83.8 0.9 copy-start.10
  88.8 9.9 %all-to-all-start.1 = ((bf16[128,4,128]{0,2,1:T(8,128)(2,1)}), bf16[128,4,128]{0,2,1:T(8,128)(2,1)}, u32[]{:S(2)}, u32[]{:S(2)}) async-start(bf16[128,4,128]{0,2,1:T(8,128)(2,1)} %bitcast.103), calls=%async_computation.1 | async-start | bytes 262144 | tf_op jit(solution)/shard_map/all_to_all | solution.py:111
  92.7 50.4 %all-reduce.2.cloned.1.call-start = ((), (), s32[]{:S(2)}) async-start(), calls=%async_computation.6 | async-start | bytes 2097152 | tf_op jit(solution)/shard_map/psum | solution.py:146
  100.5 6.1 %copy-start.14 = (f32[128,512]{1,0:T(8,128)S(1)}, f32[128,512]{1,0:T(8,128)}, u32[]{:S(2)}) copy-start(f32[128,512]{1,0:T(8,128)} %get-tuple-element.30) | copy-start | bytes 786436
  106.5 3.6 %copy-start.16 = (bf16[512,128]{0,1:T(8,128)(2,1)S(1)}, bf16[512,128]{0,1:T(8,128)(2,1)}, u32[]{:S(2)}) copy-start(bf16[512,128]{0,1:T(8,128)(2,1)} %get-tuple-element.39) | copy-start | bytes 393220
  110.2 32.9 %copy-start.26 = (f32[128]{0:T(128)S(1)}, f32[128]{0:T(128)}, u32[]{:S(2)}) copy-start(f32[128]{0:T(128)} %copy-done.25) | copy-start | bytes 1540
  121.3 23.4 %copy-start.15 = (bf16[128,512]{1,0:T(8,128)(2,1)S(1)}, bf16[128,512]{1,0:T(8,128)(2,1)}, u32[]{:S(2)}) copy-start(bf16[128,512]{1,0:T(8,128)(2,1)} %param.13) | copy-start | bytes 393220
  121.4 23.4 %copy-start.21 = (pred[128,5]{0,1:T(8,128)(4,1)S(1)}, pred[128,5]{0,1:T(8,128)(4,1)}, u32[]{:S(2)}) copy-start(pred[128,5]{0,1:T(8,128)(4,1)} %copy-done.20) | copy-start | bytes 1924
  121.4 23.4 %copy-start.23 = (pred[128,5]{0,1:T(8,128)(4,1)S(1)}, pred[128,5]{0,1:T(8,128)(4,1)}, u32[]{:S(2)}) copy-start(pred[128,5]{0,1:T(8,128)(4,1)} %copy-done.22) | copy-start | bytes 1924
  121.4 23.4 %copy-start.28 = (pred[128,5]{0,1:T(8,128)(4,1)S(1)}, pred[128,5]{0,1:T(8,128)(4,1)}, u32[]{:S(2)}) copy-start(pred[128,5]{0,1:T(8,128)(4,1)} %copy-done.27) | copy-start | bytes 1924
  121.4 23.4 %copy-start.30 = (pred[128,5]{0,1:T(8,128)(4,1)S(1)}, pred[128,5]{0,1:T(8,128)(4,1)}, u32[]{:S(2)}) copy-start(pred[128,5]{0,1:T(8,128)(4,1)} %copy-done.29) | copy-start | bytes 1924
  143.1 1.7 copy-start.9
Sparse Core Ops, SparseCore 0:
  16.0 25.0 reduce-scatter.1
  106.7 36.3 all-reduce.1
where the time goes:
time: 175 us; the launch traced here: 174 us
  waiting for transfers between devices  42 us (24%)
  blocking collectives  37.7 us (22%)
  matrix products  27.1 us (15%)
  other arithmetic  26.3 us (15%)
  starting transfers between devices  17 us (10%)
  between operations  14.6 us (8%)
  local copies, waits for them, and re-layouts  8.85 us (5%)
    psum x1, waiting for transfers between devices, per_device(): lax.psum(jnp.einsum('dmc,mcr->dr', in_proj, d_proj, preferred_element_typ...  21.7 us
    psum x1, blocking collectives, per_device(): lax.psum(jnp.concatenate([table_part, gain_part[None, :]], axis=0), 'seq')  19.4 us
    all_gather x1, blocking collectives, per_device(): lax.all_gather(gated_rows, ('chan', 'pair'), axis=0, tiled=True)  10.1 us
    cos x1, other arithmetic, dft_matrix(): jnp.cos(idx.astype(jnp.float32) * (2.0 * math.pi / total))  8.74 us
    all_to_all x1, blocking collectives, per_device(): lax.all_to_all(d_mixed_cols, 'seq', split_axis=1, concat_axis=0, tiled=True)  8.31 us
    reduce_scatter x1, waiting for transfers between devices, per_device(): lax.psum_scatter(jnp.einsum('cd,rd->cr', weight_rows, cotangent, preferre...  7.66 us
    dot_general x3, matrix products, inverse_dft(): lax.dot_general(spec * weight, dft, (((1,), (1,)), ((), ())), precision=T...  6.62 us
    dot_general x1, matrix products, per_device(): jnp.einsum('dmc,mcr->dr', in_proj, d_proj, preferred_element_type=jnp.flo...  6.06 us
  transfers between devices with their start and end apart: 6, of which 5 were waited for; matrix products, arithmetic and copies ran while one was open for 17% of the time, Pallas kernels for 0%

commit v1 on v0

--- a/solution.py
+++ b/solution.py
@@ -18,14 +18,83 @@
 
 def dft_matrix(length):
     total = 2 * length
-    t = lax.optimization_barrier(lax.broadcasted_iota(jnp.int32, (length, 1), 0))
+    inner_len = 32 if length % 32 == 0 else 1
+    outer_len = length // inner_len
     j = lax.broadcasted_iota(jnp.int32, (1, total), 1)
     k = jnp.where(j < length, j, j - length)
     k = jnp.where(j == length, length, k)
-    idx = (t * k) % total
-    idx = jnp.where(j > length, (idx + 3 * total // 4) % total, idx)
-    idx = jnp.where(idx >= length, idx - total, idx)
-    return lax.optimization_barrier(jnp.cos(idx.astype(jnp.float32) * (2.0 * math.pi / total)))
+    phase = jnp.where(j > length, 3 * total // 4, 0)
+    scale = 2.0 * math.pi / total
+
+    def angle(idx):
+        idx = idx % total
+        idx = jnp.where(idx >= length, idx - total, idx)
+        return idx.astype(jnp.float32) * scale
+
+    outer = lax.optimization_barrier(lax.broadcasted_iota(jnp.int32, (outer_len, 1), 0))
+    inner = lax.optimization_barrier(lax.broadcasted_iota(jnp.int32, (inner_len, 1), 0))
+    alpha = angle(outer * inner_len * k)
+    beta = angle(inner * k + phase)
+    ca, sa = jnp.cos(alpha), jnp.sin(alpha)
+    cb, sb = jnp.cos(beta), jnp.sin(beta)
+    table = ca[:, None, :] * cb[None, :, :] - sa[:, None, :] * sb[None, :, :]
+    return lax.optimization_barrier(table.reshape(length, total))
+
+
+def xor_exchange(x, axis, step):
+    count = lax.axis_size(axis)
+    return lax.ppermute(x, axis, [(i, i ^ step) for i in range(count)])
+
+
+def reduce_scatter_cp(x):
+    chans, pairs = lax.axis_size("chan"), lax.axis_size("pair")
+    rest = x.shape[1:]
+    block = x.shape[0] // (chans * pairs)
+    y = x.reshape((chans, pairs, block) + rest)
+    me, step = lax.axis_index("pair"), pairs // 2
+    while step >= 1:
+        bit = (me // step) % 2
+        split = y.reshape((chans, 2, step, block) + rest)
+        y = jnp.take(split, bit, axis=1) + xor_exchange(jnp.take(split, 1 - bit, axis=1), "pair", step)
+        step //= 2
+    y = y.reshape((chans, block) + rest)
+    me, step = lax.axis_index("chan"), chans // 2
+    while step >= 1:
+        bit = (me // step) % 2
+        split = y.reshape((2, step, block) + rest)
+        y = jnp.take(split, bit, axis=0) + xor_exchange(jnp.take(split, 1 - bit, axis=0), "chan", step)
+        step //= 2
+    return y.reshape((block,) + rest)
+
+
+def ordered(mine, other, first, axis):
+    return jnp.concatenate(
+        [jnp.where(first, mine, other), jnp.where(first, other, mine)], axis=axis
+    )
+
+
+def all_gather_cp(x):
+    chans, pairs = lax.axis_size("chan"), lax.axis_size("pair")
+    y = x[None]
+    me, step = lax.axis_index("chan"), 1
+    while step < chans:
+        y = ordered(y, xor_exchange(y, "chan", step), (me // step) % 2 == 0, 0)
+        step *= 2
+    y = y[:, None]
+    me, step = lax.axis_index("pair"), 1
+    while step < pairs:
+        y = ordered(y, xor_exchange(y, "pair", step), (me // step) % 2 == 0, 1)
+        step *= 2
+    return y.reshape((chans * pairs * x.shape[0],) + x.shape[1:])
+
+
+def psum_seq(x):
+    count = lax.axis_size("seq")
+    step = 1
+    while step < count:
+        x = x + xor_exchange(x, "seq", step)
+        step *= 2
+    return x
 
 
 def forward_dft(signal, dft):
@@ -73,6 +142,10 @@
     fa, fb = halves(pair_flip(spec))
     edge = first_col(a.shape)
     return jnp.concatenate([a + fa, jnp.where(edge, b + fb, b - fb)], axis=1)
+
+
+def norm_gain_local(norm_gain, group_index, local_width):
+    return lax.dynamic_slice_in_dim(norm_gain, group_index * local_width, local_width, 0)
 
 
 def per_device(tokens, kmer_table, norm_gain, in_proj, long_filter, out_proj, cotangent):
@@ -94,8 +167,13 @@
     embedded = jnp.dot(table_t, onehot_t, preferred_element_type=jnp.float32)
     inv_rms = lax.rsqrt(jnp.mean(embedded * embedded, axis=0, keepdims=True) + NORM_EPSILON)
     normed = embedded * inv_rms
-    hidden = (normed * norm_gain[:, None]).astype(jnp.bfloat16)
+    scaled_normed = normed * norm_gain[:, None]
+    hidden = scaled_normed.astype(jnp.bfloat16)
     projected = jnp.einsum("dr,dmc->mcr", hidden, in_proj, preferred_element_type=jnp.float32)
+    residual = (scaled_normed - hidden.astype(jnp.float32)).astype(jnp.bfloat16)
+    unrounded = projected + jnp.einsum(
+        "dr,dmc->mcr", residual, in_proj, preferred_element_type=jnp.float32
+    )
     query_part = projected[0]
     key_part = projected[1]
     value_part = projected[2]
@@ -113,7 +191,7 @@
     weight_rows = out_proj
     mixed_out = jnp.einsum(
         "cr,cd->rd",
-        lax.all_gather(gated_rows, ("chan", "pair"), axis=0, tiled=True),
+        all_gather_cp(gated_rows),
         weight_rows,
         preferred_element_type=jnp.float32,
     )
@@ -121,11 +199,8 @@
     block_out = (mixed_out + own_rows.T).astype(jnp.bfloat16)
     grad_scale = 1.0 / math.sqrt(length)
     d_gated = (
-        lax.psum_scatter(
-            jnp.einsum("cd,rd->cr", weight_rows, cotangent, preferred_element_type=jnp.float32),
-            ("chan", "pair"),
-            scatter_dimension=0,
-            tiled=True,
+        reduce_scatter_cp(
+            jnp.einsum("cd,rd->cr", weight_rows, cotangent, preferred_element_type=jnp.float32)
         )
         * grad_scale
     )
@@ -143,20 +218,27 @@
     d_proj = jnp.stack([d_query, d_key, d_value]).astype(jnp.bfloat16)
     normed_local = lax.dynamic_slice_in_dim(normed, group_index * local_width, local_width, 0)
     cot_scaled = cotangent.T.astype(jnp.float32) * grad_scale
-    d_full = lax.psum(
-        jnp.einsum("dmc,mcr->dr", in_proj, d_proj, preferred_element_type=jnp.float32),
-        ("chan", "pair"),
-    )
-    scaled_full = norm_gain[:, None] * d_full
-    row_stat = jnp.mean(scaled_full * normed, axis=0, keepdims=True)
-    scaled = lax.dynamic_slice_in_dim(scaled_full, group_index * local_width, local_width, 0)
+    d_full = jnp.einsum("dmc,mcr->dr", in_proj, d_proj, preferred_element_type=jnp.float32)
+    stat_part = jnp.sum(d_proj.astype(jnp.float32) * unrounded, axis=(0, 1))
+    stat_rows = jnp.zeros((8, row_count), jnp.float32).at[0].set(stat_part)
+    groups = lax.axis_size("chan") * lax.axis_size("pair")
+    payload = jnp.concatenate(
+        [
+            d_full.reshape(groups, local_width, row_count),
+            jnp.broadcast_to(stat_rows[None], (groups, 8, row_count)),
+        ],
+        axis=1,
+    ).reshape(groups * (local_width + 8), row_count)
+    reduced = reduce_scatter_cp(payload)
+    d_hidden = reduced[:local_width]
+    row_stat = reduced[local_width : local_width + 1] / model_width
+    scaled = norm_gain_local(norm_gain, group_index, local_width)[:, None] * d_hidden
     d_embedded = inv_rms * (scaled - normed_local * row_stat) + cot_scaled
-    d_hidden = lax.dynamic_slice_in_dim(d_full, group_index * local_width, local_width, 0)
     gain_part = jnp.sum(d_hidden * normed_local, axis=1)
     table_part = jnp.einsum(
         "kr,cr->kc", onehot_t.astype(jnp.float32), d_embedded, precision=PRECISE
     )
-    summed = lax.psum(jnp.concatenate([table_part, gain_part[None, :]], axis=0), "seq")
+    summed = psum_seq(jnp.concatenate([table_part, gain_part[None, :]], axis=0))
     kmer_grad = summed[: kmer_len * letter_count]
     gain_grad = summed[kmer_len * letter_count]
     return (

time: 175 us -> 145 us (0.83)
  blocking collectives: 37.7 us -> 8.4 us
  local copies, waits for them, and re-layouts: 8.85 us -> 30.1 us
  waiting for transfers between devices: 42 us -> 28.5 us
  between operations: 14.6 us -> 1.49 us
  starting transfers between devices: 17 us -> 23.2 us
  other arithmetic: 26.3 us -> 24.3 us
    psum x1 -> x0, waiting for transfers between devices: 21.7 us -> none  [per_device(): lax.psum(jnp.einsum('dmc,mcr->dr', in_proj, d_proj, preferred_element_typ...]
    psum x1 -> x0, blocking collectives: 19.4 us -> none  [per_device(): lax.psum(jnp.concatenate([table_part, gain_part[None, :]], axis=0), 'seq')]
    ppermute x0 -> x8, waiting for transfers between devices: none -> 15.7 us  [xor_exchange(): return lax.ppermute(x, axis, [(i, i ^ step) for i in range(count)])]
    all_gather x1 -> x0, blocking collectives: 10.1 us -> none  [per_device(): lax.all_gather(gated_rows, ('chan', 'pair'), axis=0, tiled=True)]
    cos x1 -> x2, other arithmetic: 8.74 us -> 0.95 us  [the longest x1 0.61 us: dft_matrix(): cb, sb = (jnp.cos(beta), jnp.sin(beta))]
    reduce_scatter x1 -> x0, waiting for transfers between devices: 7.66 us -> none  [per_device(): lax.psum_scatter(jnp.einsum('cd,rd->cr', weight_rows, cotangent, preferre...]
    ppermute x0 -> x8, starting transfers between devices: none -> 7.41 us  [xor_exchange(): return lax.ppermute(x, axis, [(i, i ^ step) for i in range(count)])]
    unnamed x72 -> x99, local copies, waits for them, and re-layouts: 3.49 us -> 9.39 us
  transfers between devices with their start and end apart: 6 -> 12, of which waited for: 5 -> 8; matrix products, arithmetic and copies ran while one was open for 17% -> 18% of each run, Pallas kernels for 0% -> 0%
where the time goes in v1:
time: 145 us; the launch traced here: 144 us
  local copies, waits for them, and re-layouts  30.1 us (21%)
  waiting for transfers between devices  28.5 us (20%)
  matrix products  28.3 us (20%)
  other arithmetic  24.3 us (17%)
  starting transfers between devices  23.2 us (16%)
  blocking collectives  8.4 us (6%)
  between operations  1.49 us (1%)
    ppermute x8, waiting for transfers between devices, xor_exchange(): return lax.ppermute(x, axis, [(i, i ^ step) for i in range(count)])  15.7 us
    unnamed x99, local copies, waits for them, and re-layouts  9.39 us
    all_to_all x1, blocking collectives, per_device(): lax.all_to_all(d_mixed_cols, 'seq', split_axis=1, concat_axis=0, tiled=True)  8.4 us
    ppermute x8, starting transfers between devices, xor_exchange(): return lax.ppermute(x, axis, [(i, i ^ step) for i in range(count)])  7.41 us
    dot_general x1, matrix products, per_device(): jnp.einsum('dmc,mcr->dr', in_proj, d_proj, preferred_element_type=jnp.flo...  5.9 us
    all_to_all x1, waiting for transfers between devices, per_device(): lax.all_to_all(mixed_in, 'seq', split_axis=0, concat_axis=1, tiled=True)  5.21 us
    dot_general x3, matrix products, forward_dft(): jnp.dot(signal.astype(jnp.float32), dft, precision=TRANSFORM_PRECISION)  5.13 us
    dot_general x3, matrix products, inverse_dft(): lax.dot_general(spec * weight, dft, (((1,), (1,)), ((), ())), precision=T...  4.89 us
  transfers between devices with their start and end apart: 12, of which 8 were waited for; matrix products, arithmetic and copies ran while one was open for 18% of the time, Pallas kernels for 0%

profile of v1, /device:TPU:0, one launch (start us, length us, event | category | flops | bytes accessed | tf_op | source)
XLA Modules:
  0.0 144.1 jit_solution(14016221290952397578)
XLA Ops:
  0.7 1.6 %copy-done = bf16[2048,512]{1,0:T(8,128)(2,1)S(1)} copy-done((bf16[2048,512]{1,0:T(8,128)(2,1)S(1)}, bf16[2048,512]{1,0:T(8,128)(2,1)}, u32[]{:S(2)}) %copy-start) | copy-done | bytes 2097176
  2.2 1.6 %fusion.76 = f32[2048,128]{1,0:T(8,128)S(1)} fusion(bf16[2048,512]{1,0:T(8,128)(2,1)S(1)} %copy-done, bf16[128,512]{1,0:T(8,128)(2,1)} %param.23), kind=kOutput, calls=%fused_computation.174 | convolution fusion | flops 268435456 | bytes 3276800 | tf_op jit(solution)/shard_map/cd,rd->cr/dot_general | solution.py:203
  4.7 1.2 copy.49
  7.4 4.5 %collective-permute-start = (s32[3]{0:T(128)S(1)}, s32[3]{0:T(128)S(1)}, u32[]{:S(2)}, u32[]{:S(2)}) collective-permute-start(s32[3]{0:T(128)S(1)} %slice_add_fusion.2), channel_id=1, source_target_pairs={{0,4},{4,8},{8,12},{1,5},{5,9},{9,13},{2,6},{6,10},{10,14},{3,7},{... | collective-permute-start | bytes 44 | tf_op jit(solution)/shard_map/ppermute | solution.py:16
  14.0 1.0 fusion.73
  15.2 1.0 copy.48
  17.4 1.1 bitcast_add_fusion
  18.6 1.6 %collective-permute-start.4 = (f32[1,512,128]{1,2,0:T(8,128)S(1)}, f32[1,512,128]{1,2,0:T(8,128)S(1)}, u32[]{:S(2)}, u32[]{:S(2)}) collective-permute-start(f32[1,512,128]{1,2,0:T(8,128)S(1)} %select_bitcast_fusion.2), channel_id=1, source_target_pairs={{0,2},{2,0},{1,3},{3,1},{4,6},{6,4},{5,7},{7,5},{8,10},{10,8},{9,1... | collective-permute-start | bytes 786440 | tf_op jit(solution)/shard_map/ppermute | solution.py:46
  20.2 3.8 %convolution_bitcast_fusion.2 = f32[3,512,128]{1,2,0:T(8,128)S(1)} fusion(bf16[2048,3,512]{2,0,1:T(8,128)(2,1)} %param.20, f32[128,2048]{1,0:T(8,128)S(1)} %broadcast_multiply_fusion, f32[2048]{0:T(1024)S(1)} %copy-done.29), kind=kOutput, calls=%fused_computation.7 | convolution fusion | flops 805830656 | bytes 8134656 | tf_op jit(solution)/shard_map/dr,dmc->mcr/dot_general | solution.py:172
  24.0 3.1 %collective-permute-done.4 = f32[1,512,128]{1,2,0:T(8,128)S(1)} collective-permute-done((f32[1,512,128]{1,2,0:T(8,128)S(1)}, f32[1,512,128]{1,2,0:T(8,128)S(1)}, u32[]{:S(2)}, u32[]{:S(2)}) %collective-permute-start.4) | collective-permute-done | bytes 262176 | tf_op jit(solution)/shard_map/ppermute | solution.py:46
  28.6 3.9 %all-to-all-start.2 = ((bf16[4,128,128]{1,2,0:T(8,128)(2,1)}), bf16[4,128,128]{1,2,0:T(8,128)(2,1)S(1)}, u32[]{:S(2)}, u32[]{:S(2)}) async-start(bf16[4,128,128]{1,2,0:T(8,128)(2,1)} %copy.37), calls=%async_computation.2 | async-start | bytes 262144 | tf_op jit(solution)/shard_map/all_to_all | solution.py:209
  32.5 2.1 %maximum_select_fusion = f32[128,1024]{1,0:T(8,128)} fusion(f32[1,1024]{1,0:T(1,128)S(1)} %get-tuple-element.97, f32[127,1024]{1,0:T(8,128)} %get-tuple-element.99, f32[127,1024]{1,0:T(8,128)} %get-tuple-element.98, f32[1,1024]{1,0:T(1,128)S(1)} %get-tuple-element.96, s32[128]{0:T(128)S(1)} %iota_and_fusion.1, s32[128]{0:T(128)S(1)} %broadcast_add_fusion, ...), kind=kLoop, calls=%fused_computation.40 | loop fusion | flops 655360 | bytes 1574016 | tf_op jit(solution)/shard_map/jit(_where)/select_n | solution.py:137
  34.6 3.8 %all-to-all-done.2 = bf16[4,128,128]{1,2,0:T(8,128)(2,1)S(1)} async-done(((bf16[4,128,128]{1,2,0:T(8,128)(2,1)}), bf16[4,128,128]{1,2,0:T(8,128)(2,1)S(1)}, u32[]{:S(2)}, u32[]{:S(2)}) %all-to-all-start.2) | async-done | bytes 131104 | tf_op jit(solution)/shard_map/all_to_all | solution.py:209
  38.4 2.2 %fusion.77 = f32[128,1024]{1,0:T(8,128)S(1)} fusion(bf16[128,512]{0,1:T(8,128)(2,1)S(1)} %bitcast.151, f32[512,1024]{1,0:T(8,128)} %bitcast.140), kind=kOutput, calls=%fused_computation.175 | convolution fusion | flops 402653184 | bytes 2752512 | tf_op jit(solution)/shard_map/dot_general | solution.py:101
  42.6 1.2 convolution_convert_fusion
  44.0 8.4 %all_to_all.58 = bf16[128,4,128]{0,2,1:T(8,128)(2,1)S(1)} all-to-all(bf16[128,4,128]{0,2,1:T(8,128)(2,1)S(1)} %bitcast.149), channel_id=1, replica_groups=mesh['groups'=2,'seq'=4,'chan'=2,'pair'=2] {'seq'}, dimensions={1} | all-to-all | bytes 262144 | tf_op jit(solution)/shard_map/all_to_all | solution.py:213
  53.4 1.8 %multiply_convert_fusion.1 = (bf16[1,512,128]{1,2,0:T(8,128)(2,1)S(1)}, bf16[1,512,128]{1,2,0:T(8,128)(2,1)}, bf16[1,512,128]{1,2,0:T(8,128)(2,1)S(1)}) fusion(f32[1,512,128]{1,2,0:T(8,128)} %reshape.568, f32[3,512,128]{1,2,0:T(8,128)} %copy-done.5), kind=kLoop, calls=%fused_computation.85 | loop fusion | flops 393216 | bytes 1179648 | tf_op jit(solution)/shard_map/convert.5
  55.9 3.3 %all-to-all-start = ((bf16[4,128,128]{1,2,0:T(8,128)(2,1)}), bf16[4,128,128]{1,2,0:T(8,128)(2,1)S(1)}, u32[]{:S(2)}, u32[]{:S(2)}) async-start(bf16[4,128,128]{1,2,0:T(8,128)(2,1)} %copy.31), calls=%async_computation | async-start | bytes 262144 | tf_op jit(solution)/shard_map/all_to_all | solution.py:185
  59.9 5.2 %all-to-all-done = bf16[4,128,128]{1,2,0:T(8,128)(2,1)S(1)} async-done(((bf16[4,128,128]{1,2,0:T(8,128)(2,1)}), bf16[4,128,128]{1,2,0:T(8,128)(2,1)S(1)}, u32[]{:S(2)}, u32[]{:S(2)}) %all-to-all-start) | async-done | bytes 131104 | tf_op jit(solution)/shard_map/all_to_all | solution.py:185
  65.1 2.2 %fusion.75 = f32[128,1024]{1,0:T(8,128)S(1)} fusion(bf16[128,512]{0,1:T(8,128)(2,1)S(1)} %bitcast.150, f32[512,1024]{1,0:T(8,128)} %bitcast.141), kind=kOutput, calls=%fused_computation.173 | convolution fusion | flops 402653184 | bytes 2752512 | tf_op jit(solution)/shard_map/dot_general | solution.py:101
  67.4 1.4 subtract_select_fusion.1
  70.3 1.8 %convolution_convert_fusion.1 = bf16[128,512]{1,0:T(8,128)(2,1)} fusion(f32[512,1024]{1,0:T(8,128)S(1)} %bitcast.143, f32[128,512]{1,0:T(8,128)S(1)} %get-tuple-element.88, f32[128,512]{1,0:T(8,128)S(1)} %get-tuple-element.89, f32[1024]{0:T(1024)S(1)} %fusion.64), kind=kOutput, calls=%fused_computation.16 | convolution fusion | flops 402980864 | bytes 2756608 | tf_op jit(solution)/shard_map/dot_general | solution.py:109
  72.2 1.7 %copy.46 = bf16[128,512]{0,1:T(8,128)(2,1)} copy(bf16[128,512]{1,0:T(8,128)(2,1)} %convolution_convert_fusion.1) | data formatting | bytes 262144 | tf_op jit(solution)/shard_map/all_to_all | solution.py:189
  73.8 4.1 %all-to-all-start.1 = ((bf16[128,4,128]{0,2,1:T(8,128)(2,1)}), bf16[128,4,128]{0,2,1:T(8,128)(2,1)}, u32[]{:S(2)}, u32[]{:S(2)}) async-start(bf16[128,4,128]{0,2,1:T(8,128)(2,1)} %bitcast.148), calls=%async_computation.1 | async-start | bytes 262144 | tf_op jit(solution)/shard_map/all_to_all | solution.py:189
  77.9 2.1 %fusion.18 = f32[128,1024]{1,0:T(8,128)} fusion(f32[128,512]{1,0:T(8,128)} %copy-done.10, f32[128,512]{1,0:T(8,128)S(1)} %get-tuple-element.79, f32[1,1024]{1,0:T(1,128)} %get-tuple-element.93, f32[127,1024]{1,0:T(8,128)} %fusion.13, f32[1,1024]{1,0:T(1,128)S(1)} %get-tuple-element.92, s32[128]{0:T(128)} %copy-done.43, s32[128]{0:T(128)} %copy-done.41, ...), kind=kLoop, calls=%fused_computation.39 | loop fusion | flops 786432 | bytes 1578112 | tf_op jit(solution)/shard_map/jit(_where)/select_n | solution.py:137
  80.0 3.7 %all-to-all-done.1 = bf16[128,4,128]{0,2,1:T(8,128)(2,1)} async-done(((bf16[128,4,128]{0,2,1:T(8,128)(2,1)}), bf16[128,4,128]{0,2,1:T(8,128)(2,1)}, u32[]{:S(2)}, u32[]{:S(2)}) %all-to-all-start.1) | async-done | bytes 131104 | tf_op jit(solution)/shard_map/all_to_all | solution.py:189
  85.5 1.8 %reshape.567 = f32[1,512,128]{1,2,0:T(8,128)} reshape(f32[4,128,128]{1,0,2:T(4,128)} %copy.33) | data formatting | bytes 524288 | tf_op jit(solution)/shard_map/convert_element_type | solution.py:190
  87.3 2.0 %multiply_convert_fusion.2 = (bf16[1,512,128]{1,2,0:T(8,128)(2,1)S(1)}, bf16[1,512,128]{1,2,0:T(8,128)(2,1)}) fusion(f32[1,512,128]{1,2,0:T(8,128)} %reshape.567, f32[1,512,128]{1,2,0:T(8,128)} %copy-done.22, f32[2,1,512,128]{2,3,1,0:T(8,128)} %copy-done.12, s32[]{:T(128)S(6)} %select_n.319, pred[]{:T(512)S(6)} %and.121, f32[3,512,128]{1,2,0:T(8,128)} %copy-done.5), kind=kLoop, calls=%fused_computation.87 | loop fusion | flops 458752 | bytes 1310725 | tf_op jit(solution)/shard_map/convert.4
  89.3 4.2 %fusion.2 = f32[128]{0:T(128)S(1)} fusion(f32[3,512,128]{1,2,0:T(8,128)} %copy-done.5, bf16[2048,3,512]{2,0,1:T(8,128)(2,1)} %param.20, f32[128,2048]{1,0:T(8,128)S(1)} %broadcast_multiply_fusion, f32[2048]{0:T(1024)S(1)} %copy-done.29, bf16[1,512,128]{1,2,0:T(8,128)(2,1)} %get-tuple-element.84, bf16[1,512,128]{1,2,0:T(8,128)(2,1)S(1)} %get-tuple-element.83, ...), kind=kOutput, calls=%fused_computation.11 | convolution fusion | flops 807796608 | bytes 8528384 | tf_op jit(solution)/shard_map/dr,dmc->mcr/dot_general | solution.py:174
  93.5 5.9 %convolution_bitcast_fusion = f32[2048,128]{0,1:T(8,128)} fusion(bf16[2048,3,512]{2,0,1:T(8,128)(2,1)} %param.20, bf16[1,512,128]{1,2,0:T(8,128)(2,1)S(1)} %copy-done.19, bf16[1,512,128]{1,2,0:T(8,128)(2,1)S(1)} %get-tuple-element.83, bf16[1,512,128]{1,2,0:T(8,128)(2,1)S(1)} %get-tuple-element.100), kind=kOutput, calls=%fused_computation | convolution fusion | flops 805699584 | bytes 7733248 | tf_op jit(solution)/shard_map/dmc,mcr->dr/dot_general | solution.py:221
  100.1 2.6 %copy.40 = f32[2048,128]{1,0:T(8,128)} copy(f32[2048,128]{0,1:T(8,128)} %convolution_bitcast_fusion) | data formatting | bytes 2097152 | tf_op jit(solution)/shard_map/dmc,mcr->dr/dot_general | solution.py:221
  102.7 2.5 %copy.42 = f32[2,2,1,512,128]{3,4,0,2,1:T(8,128)} copy(f32[2,2,1,512,128]{4,3,1,0,2:T(8,128)} %bitcast.146) | data formatting | bytes 2097152 | tf_op jit(solution)/shard_map/concatenate | solution.py:225
  106.8 2.0 %fusion.8 = f32[2,1,520,128]{2,3,0,1:T(8,128)} fusion(s32[]{:T(128)S(6)} %select_n.317, f32[2,2,1,512,128]{3,4,0,2,1:T(8,128)} %copy.42, f32[2,2,1,8,128]{3,4,0,2,1:T(8,128)S(1)} %broadcast_in_dim.95, pred[]{:T(512)S(6)} %and.120), kind=kLoop, calls=%fused_computation.30 | loop fusion | flops 266240 | bytes 1597445 | tf_op jit(solution)/shard_map/jit(_take)/select_n | solution.py:58
  108.8 2.1 %copy.43 = f32[2,1,520,128]{3,2,1,0:T(8,128)} copy(f32[2,1,520,128]{2,3,0,1:T(8,128)} %fusion.8) | data formatting | bytes 1064960 | tf_op jit(solution)/shard_map/jit(_take)/select_n | solution.py:58
  110.9 1.5 %collective-permute-start.1 = (bf16[1,512,128]{1,2,0:T(8,128)(2,1)S(1)}, bf16[1,512,128]{1,2,0:T(8,128)(2,1)S(1)}, u32[]{:S(2)}, u32[]{:S(2)}) collective-permute-start(bf16[1,512,128]{1,2,0:T(8,128)(2,1)S(1)} %copy-done.26), channel_id=1, source_target_pairs={{0,2},{2,0},{1,3},{3,1},{4,6},{6,4},{5,7},{7,5},{8,10},{10,8},{9,1... | collective-permute-start | bytes 393224 | tf_op jit(solution)/shard_map/ppermute | solution.py:46
  112.4 2.0 %slice_add_fusion = (f32[128,512]{1,0:T(8,128)}, f32[128,512]{1,0:T(8,128)}) fusion(f32[128,512]{1,0:T(8,128)S(1)} %get-tuple-element.79, f32[128,1024]{1,0:T(8,128)} %fusion.18, f32[128,512]{1,0:T(8,128)} %copy-done.10, pred[512]{0:T(512)(128)(4,1)S(1)} %copy-done.36), kind=kLoop, calls=%fused_computation.65 | loop fusion | flops 262144 | bytes 1573376 | tf_op jit(solution)/shard_map/add | solution.py:144
  114.4 2.4 %collective-permute-done.1 = bf16[1,512,128]{1,2,0:T(8,128)(2,1)S(1)} collective-permute-done((bf16[1,512,128]{1,2,0:T(8,128)(2,1)S(1)}, bf16[1,512,128]{1,2,0:T(8,128)(2,1)S(1)}, u32[]{:S(2)}, u32[]{:S(2)}) %collective-permute-start.1) | collective-permute-done | bytes 131104 | tf_op jit(solution)/shard_map/ppermute | solution.py:46
  119.2 2.1 %copy.44 = f32[2,1,520,128]{2,3,1,0:T(8,128)} copy(f32[2,1,520,128]{3,2,1,0:T(8,128)} %collective-permute-done.5) | data formatting | bytes 1064960 | tf_op jit(solution)/shard_map/ppermute | solution.py:46
  121.3 1.5 %fusion.12 = f32[2,1,520,128]{2,3,1,0:T(8,128)S(1)} fusion(f32[2,1,520,128]{2,3,1,0:T(8,128)} %copy.44, s32[]{:T(128)S(6)} %select_n.315, f32[2,2,1,512,128]{3,4,0,2,1:T(8,128)} %copy.42, f32[2,2,1,8,128]{3,4,0,2,1:T(8,128)S(1)} %copy-done.14, pred[]{:T(512)S(6)} %and.119), kind=kLoop, calls=%fused_computation.34 | loop fusion | flops 399360 | bytes 2129925 | tf_op jit(solution)/shard_map/add | solution.py:58
  122.8 1.6 %collective-permute-start.6 = (f32[1,520,128]{1,2,0:T(8,128)S(1)}, f32[1,520,128]{1,2,0:T(8,128)S(1)}, u32[]{:S(2)}, u32[]{:S(2)}) collective-permute-start(f32[1,520,128]{1,2,0:T(8,128)S(1)} %select_bitcast_fusion.1), channel_id=1, source_target_pairs={{0,2},{2,0},{1,3},{3,1},{4,6},{6,4},{5,7},{7,5},{8,10},{10,8},{9,1... | collective-permute-start | bytes 798728 | tf_op jit(solution)/shard_map/ppermute | solution.py:46
  124.5 1.9 %convolution_bitcast_fusion.4 = f32[1,1,128,512]{3,2,1,0:T(8,128)} fusion(f32[512,1024]{1,0:T(8,128)S(1)} %bitcast.144, f32[128,512]{1,0:T(8,128)S(1)} %copy-done.24, f32[128,512]{1,0:T(8,128)S(1)} %copy-done.23, f32[1024]{0:T(1024)S(1)} %fusion.64), kind=kOutput, calls=%fused_computation.12 | convolution fusion | flops 402915328 | bytes 2887680 | tf_op jit(solution)/shard_map/dot_general | solution.py:109
  126.4 1.0 broadcast_select_fusion.1
  127.4 5.7 %collective-permute-done.6 = f32[1,520,128]{1,2,0:T(8,128)S(1)} collective-permute-done((f32[1,520,128]{1,2,0:T(8,128)S(1)}, f32[1,520,128]{1,2,0:T(8,128)S(1)}, u32[]{:S(2)}, u32[]{:S(2)}) %collective-permute-start.6) | collective-permute-done | bytes 266272 | tf_op jit(solution)/shard_map/ppermute | solution.py:46
  133.7 1.3 collective-permute-start.7
  135.3 2.5 %collective-permute-done.7 = f32[21,512]{1,0:T(8,128)S(1)} collective-permute-done((f32[21,512]{1,0:T(8,128)S(1)}, f32[21,512]{1,0:T(8,128)S(1)}, u32[]{:S(2)}, u32[]{:S(2)}) %collective-permute-start.7) | collective-permute-done | bytes 43040 | tf_op jit(solution)/shard_map/ppermute | solution.py:46
  137.8 1.0 collective-permute-start.8
  138.8 2.1 %fusion.3 = bf16[128,512]{1,0:T(8,128)(2,1)} fusion(bf16[2048,128]{1,0:T(8,128)(2,1)S(1)} %bitcast.147, bf16[2048,512]{1,0:T(8,128)(2,1)S(1)} %copy-done, f32[128,2048]{1,0:T(8,128)} %copy-done.11, s32[]{:T(128)S(6)} %select_n.288), kind=kOutput, calls=%fused_computation.14 | convolution fusion | flops 268566528 | bytes 3014660 | tf_op jit(solution)/shard_map/cr,cd->rd/dot_general | solution.py:192
  140.9 2.0 %collective-permute-done.8 = f32[21,512]{1,0:T(8,128)S(1)} collective-permute-done((f32[21,512]{1,0:T(8,128)S(1)}, f32[21,512]{1,0:T(8,128)S(1)}, u32[]{:S(2)}, u32[]{:S(2)}) %collective-permute-start.8) | collective-permute-done | bytes 43040 | tf_op jit(solution)/shard_map/ppermute | solution.py:46
  (163 shorter events, 21.7 us)
Async XLA Ops:
  0.6 1.6 %copy-start = (bf16[2048,512]{1,0:T(8,128)(2,1)S(1)}, bf16[2048,512]{1,0:T(8,128)(2,1)}, u32[]{:S(2)}) copy-start(bf16[2048,512]{1,0:T(8,128)(2,1)} %param.22) | copy-start | bytes 6291460
  3.8 3.5 %copy-start.46 = (s32[128]{0:T(128)S(1)}, s32[128]{0:T(128)}, u32[]{:S(2)}) copy-start(s32[128]{0:T(128)} %param.17) | copy-start | bytes 1540
  6.0 7.3 %copy-start.27 = (f32[1,1,128,512]{3,2,1,0:T(8,128)S(1)}, f32[1,1,128,512]{3,2,1,0:T(8,128)}, u32[]{:S(2)}) copy-start(f32[1,1,128,512]{3,2,1,0:T(8,128)} %param.21) | copy-start | bytes 786436
  6.9 10.4 %collective-permute-start.3 = (f32[2,1,512,128]{2,3,1,0:T(8,128)}, f32[2,1,512,128]{2,3,1,0:T(8,128)}, u32[]{:S(2)}, u32[]{:S(2)}) collective-permute-start(f32[2,1,512,128]{2,3,1,0:T(8,128)} %select_bitcast_fusion), channel_id=1, source_target_pairs={{0,1},{1,0},{2,3},{3,2},{4,5},{5,4},{6,7},{7,6},{8,9},{9,8},{10,11... | collective-permute-start | bytes 1572872 | tf_op jit(solution)/shard_map/ppermute | solution.py:46
  7.4 8.9 %collective-permute-start = (s32[3]{0:T(128)S(1)}, s32[3]{0:T(128)S(1)}, u32[]{:S(2)}, u32[]{:S(2)}) collective-permute-start(s32[3]{0:T(128)S(1)} %slice_add_fusion.2), channel_id=1, source_target_pairs={{0,4},{4,8},{8,12},{1,5},{5,9},{9,13},{2,6},{6,10},{10,14},{3,7},{... | collective-permute-start | bytes 44 | tf_op jit(solution)/shard_map/ppermute | solution.py:16
  11.9 4.6 %copy-start.37 = (pred[128,5]{0,1:T(8,128)(4,1)}, pred[128,5]{0,1:T(8,128)(4,1)S(1)}, u32[]{:S(2)}) copy-start(pred[128,5]{0,1:T(8,128)(4,1)S(1)} %iota_compare_fusion.5) | copy-start | bytes 1924
  13.3 1.8 %copy-start.1 = (f32[16,32,1024]{2,1,0:T(8,128)}, f32[16,32,1024]{2,1,0:T(8,128)S(1)}, u32[]{:S(2)}) copy-start(f32[16,32,1024]{2,1,0:T(8,128)S(1)} %multiply_subtract_fusion) | copy-start | bytes 6291460
  14.0 2.2 %copy-start.28 = (bf16[4,5,2048]{2,0,1:T(4,128)(2,1)S(1)}, bf16[4,5,2048]{2,0,1:T(4,128)(2,1)}, u32[]{:S(2)}) copy-start(bf16[4,5,2048]{2,0,1:T(4,128)(2,1)} %param.18) | copy-start | bytes 245764
  15.2 17.3 %copy-start.41 = (s32[128]{0:T(128)}, s32[128]{0:T(128)S(1)}, u32[]{:S(2)}) copy-start(s32[128]{0:T(128)S(1)} %broadcast_add_fusion) | copy-start | bytes 1540
  15.2 17.3 %copy-start.42 = (pred[128]{0:T(512)(128)(4,1)}, pred[128]{0:T(512)(128)(4,1)S(1)}, u32[]{:S(2)}) copy-start(pred[128]{0:T(512)(128)(4,1)S(1)} %compare_and_fusion) | copy-start | bytes 388
  15.2 17.3 %copy-start.43 = (s32[128]{0:T(128)}, s32[128]{0:T(128)S(1)}, u32[]{:S(2)}) copy-start(s32[128]{0:T(128)S(1)} %iota_and_fusion.1) | copy-start | bytes 1540
  15.2 52.1 %copy-start.35 = (pred[512]{0:T(512)(128)(4,1)}, pred[512]{0:T(512)(128)(4,1)S(1)}, u32[]{:S(2)}) copy-start(pred[512]{0:T(512)(128)(4,1)S(1)} %iota_compare_fusion.6) | copy-start | bytes 1540
  16.6 2.0 %copy-start.30 = (pred[128,5]{0,1:T(8,128)(4,1)}, pred[128,5]{0,1:T(8,128)(4,1)S(1)}, u32[]{:S(2)}) copy-start(pred[128,5]{0,1:T(8,128)(4,1)S(1)} %get-tuple-element.115) | copy-start | bytes 1924
  16.6 2.0 %copy-start.32 = (pred[128,5]{0,1:T(8,128)(4,1)}, pred[128,5]{0,1:T(8,128)(4,1)S(1)}, u32[]{:S(2)}) copy-start(pred[128,5]{0,1:T(8,128)(4,1)S(1)} %get-tuple-element.116) | copy-start | bytes 1924
  17.0 1.6 %copy-start.11 = (f32[128,2048]{1,0:T(8,128)}, f32[128,2048]{1,0:T(8,128)S(1)}, u32[]{:S(2)}) copy-start(f32[128,2048]{1,0:T(8,128)S(1)} %get-tuple-element.112) | copy-start | bytes 3145732
  17.1 3.1 %copy-start.29 = (f32[2048]{0:T(1024)S(1)}, f32[2048]{0:T(1024)}, u32[]{:S(2)}) copy-start(f32[2048]{0:T(1024)} %param.19) | copy-start | bytes 24580
  18.6 8.6 %copy-start.12 = (f32[2,1,512,128]{2,3,1,0:T(8,128)}, f32[2,1,512,128]{2,3,1,0:T(8,128)S(1)}, u32[]{:S(2)}) copy-start(f32[2,1,512,128]{2,3,1,0:T(8,128)S(1)} %bitcast_add_fusion) | copy-start | bytes 1572868
  18.6 8.5 %collective-permute-start.4 = (f32[1,512,128]{1,2,0:T(8,128)S(1)}, f32[1,512,128]{1,2,0:T(8,128)S(1)}, u32[]{:S(2)}, u32[]{:S(2)}) collective-permute-start(f32[1,512,128]{1,2,0:T(8,128)S(1)} %select_bitcast_fusion.2), channel_id=1, source_target_pairs={{0,2},{2,0},{1,3},{3,1},{4,6},{6,4},{5,7},{7,5},{8,10},{10,8},{9,1... | collective-permute-start | bytes 786440 | tf_op jit(solution)/shard_map/ppermute | solution.py:46
  24.0 3.2 %copy-start.5 = (f32[3,512,128]{1,2,0:T(8,128)}, f32[3,512,128]{1,2,0:T(8,128)S(1)}, u32[]{:S(2)}) copy-start(f32[3,512,128]{1,2,0:T(8,128)S(1)} %convolution_bitcast_fusion.2) | copy-start | bytes 2359300
  28.6 9.8 %all-to-all-start.2 = ((bf16[4,128,128]{1,2,0:T(8,128)(2,1)}), bf16[4,128,128]{1,2,0:T(8,128)(2,1)S(1)}, u32[]{:S(2)}, u32[]{:S(2)}) async-start(bf16[4,128,128]{1,2,0:T(8,128)(2,1)} %copy.37), calls=%async_computation.2 | async-start | bytes 262144 | tf_op jit(solution)/shard_map/all_to_all | solution.py:209
  38.4 2.2 %copy-start.7 = (f32[128,1024]{1,0:T(8,128)S(1)}, f32[128,1024]{1,0:T(8,128)}, u32[]{:S(2)}) copy-start(f32[128,1024]{1,0:T(8,128)} %copy-done.6) | copy-start | bytes 1572868
  38.4 2.2 %copy-start.17 = (f32[128,1024]{1,0:T(8,128)S(1)}, f32[128,1024]{1,0:T(8,128)}, u32[]{:S(2)}) copy-start(f32[128,1024]{1,0:T(8,128)} %maximum_select_fusion) | copy-start | bytes 1572868
  40.7 2.0 %copy-start.2 = (f32[16,32,1024]{2,1,0:T(8,128)S(1)}, f32[16,32,1024]{2,1,0:T(8,128)}, u32[]{:S(2)}) copy-start(f32[16,32,1024]{2,1,0:T(8,128)} %copy-done.1) | copy-start | bytes 6291460
  55.9 9.2 %all-to-all-start = ((bf16[4,128,128]{1,2,0:T(8,128)(2,1)}), bf16[4,128,128]{1,2,0:T(8,128)(2,1)S(1)}, u32[]{:S(2)}, u32[]{:S(2)}) async-start(bf16[4,128,128]{1,2,0:T(8,128)(2,1)} %copy.31), calls=%async_computation | async-start | bytes 262144 | tf_op jit(solution)/shard_map/all_to_all | solution.py:185
  65.1 2.2 %copy-start.9 = (f32[128,1024]{1,0:T(8,128)S(1)}, f32[128,1024]{1,0:T(8,128)}, u32[]{:S(2)}) copy-start(f32[128,1024]{1,0:T(8,128)} %copy-done.8) | copy-start | bytes 1572868
  67.4 3.0 %copy-start.3 = (f32[16,32,1024]{2,1,0:T(8,128)S(1)}, f32[16,32,1024]{2,1,0:T(8,128)}, u32[]{:S(2)}) copy-start(f32[16,32,1024]{2,1,0:T(8,128)} %copy-done.1) | copy-start | bytes 6291460
  73.8 9.9 %all-to-all-start.1 = ((bf16[128,4,128]{0,2,1:T(8,128)(2,1)}), bf16[128,4,128]{0,2,1:T(8,128)(2,1)}, u32[]{:S(2)}, u32[]{:S(2)}) async-start(bf16[128,4,128]{0,2,1:T(8,128)(2,1)} %bitcast.148), calls=%async_computation.1 | async-start | bytes 262144 | tf_op jit(solution)/shard_map/all_to_all | solution.py:189
  89.3 4.2 %copy-start.19 = (bf16[1,512,128]{1,2,0:T(8,128)(2,1)S(1)}, bf16[1,512,128]{1,2,0:T(8,128)(2,1)}, u32[]{:S(2)}) copy-start(bf16[1,512,128]{1,2,0:T(8,128)(2,1)} %get-tuple-element.84) | copy-start | bytes 393220
  105.2 5.7 %copy-start.26 = (bf16[1,512,128]{1,2,0:T(8,128)(2,1)S(1)}, bf16[1,512,128]{1,2,0:T(8,128)(2,1)}, u32[]{:S(2)}) copy-start(bf16[1,512,128]{1,2,0:T(8,128)(2,1)} %get-tuple-element.101) | copy-start | bytes 393220
  105.2 7.2 %copy-start.36 = (pred[512]{0:T(512)(128)(4,1)S(1)}, pred[512]{0:T(512)(128)(4,1)}, u32[]{:S(2)}) copy-start(pred[512]{0:T(512)(128)(4,1)} %copy-done.35) | copy-start | bytes 1540
  110.9 8.3 %collective-permute-start.5 = (f32[2,1,520,128]{3,2,1,0:T(8,128)}, f32[2,1,520,128]{3,2,1,0:T(8,128)}, u32[]{:S(2)}, u32[]{:S(2)}) collective-permute-start(f32[2,1,520,128]{3,2,1,0:T(8,128)} %copy.43), channel_id=1, source_target_pairs={{0,1},{1,0},{2,3},{3,2},{4,5},{5,4},{6,7},{7,6},{8,9},{9,8},{10,11... | collective-permute-start | bytes 1597448 | tf_op jit(solution)/shard_map/ppermute | solution.py:46
  110.9 5.9 %collective-permute-start.1 = (bf16[1,512,128]{1,2,0:T(8,128)(2,1)S(1)}, bf16[1,512,128]{1,2,0:T(8,128)(2,1)S(1)}, u32[]{:S(2)}, u32[]{:S(2)}) collective-permute-start(bf16[1,512,128]{1,2,0:T(8,128)(2,1)S(1)} %copy-done.26), channel_id=1, source_target_pairs={{0,2},{2,0},{1,3},{3,1},{4,6},{6,4},{5,7},{7,5},{8,10},{10,8},{9,1... | collective-permute-start | bytes 393224 | tf_op jit(solution)/shard_map/ppermute | solution.py:46
  114.4 6.9 %copy-start.14 = (f32[2,2,1,8,128]{3,4,0,2,1:T(8,128)S(1)}, f32[2,2,1,8,128]{3,4,0,2,1:T(8,128)}, u32[]{:S(2)}) copy-start(f32[2,2,1,8,128]{3,4,0,2,1:T(8,128)} %copy-done.13) | copy-start | bytes 49156
  119.1 7.2 %collective-permute-start.2 = (bf16[2,1,512,128]{2,3,0,1:T(8,128)(2,1)}, bf16[2,1,512,128]{2,3,0,1:T(8,128)(2,1)}, u32[]{:S(2)}, u32[]{:S(2)}) collective-permute-start(bf16[2,1,512,128]{2,3,0,1:T(8,128)(2,1)} %maximum_bitcast_fusion), channel_id=1, source_target_pairs={{0,1},{1,0},{2,3},{3,2},{4,5},{5,4},{6,7},{7,6},{8,9},{9,8},{10,11... | collective-permute-start | bytes 786440 | tf_op jit(solution)/shard_map/ppermute | solution.py:46
  121.3 3.1 %copy-start.4 = (f32[16,32,1024]{2,1,0:T(8,128)S(1)}, f32[16,32,1024]{2,1,0:T(8,128)}, u32[]{:S(2)}) copy-start(f32[16,32,1024]{2,1,0:T(8,128)} %copy-done.1) | copy-start | bytes 6291460
  121.3 3.1 %copy-start.23 = (f32[128,512]{1,0:T(8,128)S(1)}, f32[128,512]{1,0:T(8,128)}, u32[]{:S(2)}) copy-start(f32[128,512]{1,0:T(8,128)} %get-tuple-element.90) | copy-start | bytes 786436
  121.3 3.1 %copy-start.24 = (f32[128,512]{1,0:T(8,128)S(1)}, f32[128,512]{1,0:T(8,128)}, u32[]{:S(2)}) copy-start(f32[128,512]{1,0:T(8,128)} %get-tuple-element.91) | copy-start | bytes 786436
  122.8 3.6 %copy-start.21 = (bf16[1,512,128]{1,2,0:T(8,128)(2,1)S(1)}, bf16[1,512,128]{1,2,0:T(8,128)(2,1)}, u32[]{:S(2)}) copy-start(bf16[1,512,128]{1,2,0:T(8,128)(2,1)} %copy-done.20) | copy-start | bytes 393220
  122.8 10.2 %collective-permute-start.6 = (f32[1,520,128]{1,2,0:T(8,128)S(1)}, f32[1,520,128]{1,2,0:T(8,128)S(1)}, u32[]{:S(2)}, u32[]{:S(2)}) collective-permute-start(f32[1,520,128]{1,2,0:T(8,128)S(1)} %select_bitcast_fusion.1), channel_id=1, source_target_pairs={{0,2},{2,0},{1,3},{3,1},{4,6},{6,4},{5,7},{7,5},{8,10},{10,8},{9,1... | collective-permute-start | bytes 798728 | tf_op jit(solution)/shard_map/ppermute | solution.py:46
  124.4 8.8 %copy-start.25 = (bf16[128,512]{1,0:T(8,128)(2,1)S(1)}, bf16[128,512]{1,0:T(8,128)(2,1)}, u32[]{:S(2)}) copy-start(bf16[128,512]{1,0:T(8,128)(2,1)} %param.23) | copy-start | bytes 393220
  124.4 8.8 %copy-start.31 = (pred[128,5]{0,1:T(8,128)(4,1)S(1)}, pred[128,5]{0,1:T(8,128)(4,1)}, u32[]{:S(2)}) copy-start(pred[128,5]{0,1:T(8,128)(4,1)} %copy-done.30) | copy-start | bytes 1924
  124.4 8.8 %copy-start.33 = (pred[128,5]{0,1:T(8,128)(4,1)S(1)}, pred[128,5]{0,1:T(8,128)(4,1)}, u32[]{:S(2)}) copy-start(pred[128,5]{0,1:T(8,128)(4,1)} %copy-done.32) | copy-start | bytes 1924
  124.4 8.8 %copy-start.34 = (f32[512]{0:T(512)S(1)}, f32[512]{0:T(512)}, u32[]{:S(2)}) copy-start(f32[512]{0:T(512)} %dynamic_slice.7) | copy-start | bytes 6148
  124.5 8.8 %copy-start.38 = (pred[128,5]{0,1:T(8,128)(4,1)S(1)}, pred[128,5]{0,1:T(8,128)(4,1)}, u32[]{:S(2)}) copy-start(pred[128,5]{0,1:T(8,128)(4,1)} %copy-done.37) | copy-start | bytes 1924
  124.5 8.8 %copy-start.40 = (pred[128,5]{0,1:T(8,128)(4,1)S(1)}, pred[128,5]{0,1:T(8,128)(4,1)}, u32[]{:S(2)}) copy-start(pred[128,5]{0,1:T(8,128)(4,1)} %copy-done.39) | copy-start | bytes 1924
  124.5 8.8 %copy-start.45 = (f32[128]{0:T(128)S(1)}, f32[128]{0:T(128)}, u32[]{:S(2)}) copy-start(f32[128]{0:T(128)} %copy-done.44) | copy-start | bytes 1540
  133.7 4.2 %collective-permute-start.7 = (f32[21,512]{1,0:T(8,128)S(1)}, f32[21,512]{1,0:T(8,128)S(1)}, u32[]{:S(2)}, u32[]{:S(2)}) collective-permute-start(f32[21,512]{1,0:T(8,128)S(1)} %pad_maximum_fusion.4), channel_id=1, source_target_pairs={{0,4},{4,0},{8,12},{12,8},{1,5},{5,1},{9,13},{13,9},{2,6},{6,2},{1... | collective-permute-start | bytes 129032 | tf_op jit(solution)/shard_map/ppermute | solution.py:46
  137.8 5.1 %collective-permute-start.8 = (f32[21,512]{1,0:T(8,128)S(1)}, f32[21,512]{1,0:T(8,128)S(1)}, u32[]{:S(2)}, u32[]{:S(2)}) collective-permute-start(f32[21,512]{1,0:T(8,128)S(1)} %fusion.94), channel_id=1, source_target_pairs={{0,8},{4,12},{8,0},{12,4},{1,9},{5,13},{9,1},{13,5},{2,10},{6,14},... | collective-permute-start | bytes 129032 | tf_op jit(solution)/shard_map/ppermute | solution.py:46
  (11 other events, 9.7 us)

commit v2 on v1

--- a/solution.py
+++ b/solution.py
@@ -46,25 +46,23 @@
     return lax.ppermute(x, axis, [(i, i ^ step) for i in range(count)])
 
 
-def reduce_scatter_cp(x):
+def reduce_scatter_lanes(x, width):
+    for axis, inner in (("pair", lax.axis_size("chan")), ("chan", 1)):
+        me, step = lax.axis_index(axis), lax.axis_size(axis) // 2
+        while step >= 1:
+            half = step * inner * width
+            low = (me // step) % 2 == 0
+            lo, hi = x[:, :half], x[:, half : 2 * half]
+            keep = jnp.where(low, lo, hi)
+            send = jnp.where(low, hi, lo)
+            x = keep + xor_exchange(send, axis, step)
+            step //= 2
+    return x
+
+
+def pair_major(blocks):
     chans, pairs = lax.axis_size("chan"), lax.axis_size("pair")
-    rest = x.shape[1:]
-    block = x.shape[0] // (chans * pairs)
-    y = x.reshape((chans, pairs, block) + rest)
-    me, step = lax.axis_index("pair"), pairs // 2
-    while step >= 1:
-        bit = (me // step) % 2
-        split = y.reshape((chans, 2, step, block) + rest)
-        y = jnp.take(split, bit, axis=1) + xor_exchange(jnp.take(split, 1 - bit, axis=1), "pair", step)
-        step //= 2
-    y = y.reshape((chans, block) + rest)
-    me, step = lax.axis_index("chan"), chans // 2
-    while step >= 1:
-        bit = (me // step) % 2
-        split = y.reshape((2, step, block) + rest)
-        y = jnp.take(split, bit, axis=0) + xor_exchange(jnp.take(split, 1 - bit, axis=0), "chan", step)
-        step //= 2
-    return y.reshape((block,) + rest)
+    return [blocks[c * pairs + p] for p in range(pairs) for c in range(chans)]
 
 
 def ordered(mine, other, first, axis):
@@ -178,15 +176,33 @@
     key_part = projected[1]
     value_part = projected[2]
     mixed_in = (key_part * value_part).astype(jnp.bfloat16)
+    grad_scale = 1.0 / math.sqrt(length)
+    groups = lax.axis_size("chan") * lax.axis_size("pair")
+    gated_partial = jnp.einsum("rd,cd->rc", cotangent, out_proj, preferred_element_type=jnp.float32)
+    gated_blocks = [gated_partial[:, g * local_width : (g + 1) * local_width] for g in range(groups)]
+    d_gated = (
+        reduce_scatter_lanes(jnp.concatenate(pair_major(gated_blocks), axis=1), local_width).T
+        * grad_scale
+    )
     dft = dft_matrix(length)
     filter_rows = long_filter.reshape(long_filter.shape[2], long_filter.shape[3])
     spec_g = add_conj_flip(forward_dft(filter_rows, dft))
     ga, gb = halves(spec_g)
-    mixed_cols = lax.all_to_all(mixed_in, "seq", split_axis=0, concat_axis=1, tiled=True)
+    d_conv = (d_gated * query_part).astype(jnp.bfloat16)
+    both_cols = lax.all_to_all(
+        jnp.stack([mixed_in, d_conv]), "seq", split_axis=1, concat_axis=2, tiled=True
+    )
+    mixed_cols, d_cols = both_cols[0], both_cols[1]
     spec_s = forward_dft(mixed_cols, dft)
     sa, sb = halves(spec_s)
     conv_cols = inverse_dft(cmul(ga, gb, sa, sb, False), dft).astype(jnp.bfloat16)
-    conv_rows = lax.all_to_all(conv_cols, "seq", split_axis=1, concat_axis=0, tiled=True)
+    spec_d = forward_dft(d_cols, dft)
+    da, db = halves(spec_d)
+    d_mixed_cols = inverse_dft(cmul(ga, gb, da, db, True), dft).astype(jnp.bfloat16)
+    both_rows = lax.all_to_all(
+        jnp.stack([conv_cols, d_mixed_cols]), "seq", split_axis=2, concat_axis=1, tiled=True
+    )
+    conv_rows, d_mixed = both_rows[0], both_rows[1]
     gated_rows = (query_part * conv_rows.astype(jnp.float32)).astype(jnp.bfloat16)
     weight_rows = out_proj
     mixed_out = jnp.einsum(
@@ -197,46 +213,33 @@
     )
     own_rows = lax.dynamic_slice_in_dim(embedded, group_index * local_width, local_width, 0)
     block_out = (mixed_out + own_rows.T).astype(jnp.bfloat16)
-    grad_scale = 1.0 / math.sqrt(length)
-    d_gated = (
-        reduce_scatter_cp(
-            jnp.einsum("cd,rd->cr", weight_rows, cotangent, preferred_element_type=jnp.float32)
-        )
-        * grad_scale
-    )
-    d_conv = (d_gated * query_part).astype(jnp.bfloat16)
     d_query = d_gated * conv_rows.astype(jnp.float32)
-    d_cols = lax.all_to_all(d_conv, "seq", split_axis=0, concat_axis=1, tiled=True)
-    spec_d = forward_dft(d_cols, dft)
-    da, db = halves(spec_d)
-    d_mixed_cols = inverse_dft(cmul(ga, gb, da, db, True), dft).astype(jnp.bfloat16)
-    d_mixed = lax.all_to_all(d_mixed_cols, "seq", split_axis=1, concat_axis=0, tiled=True)
     cross = cmul(sa, sb, da, db, True)
     filter_grad = inverse_dft(add_conj_flip(cross), dft)
     d_key = d_mixed.astype(jnp.float32) * value_part
     d_value = d_mixed.astype(jnp.float32) * key_part
     d_proj = jnp.stack([d_query, d_key, d_value]).astype(jnp.bfloat16)
     normed_local = lax.dynamic_slice_in_dim(normed, group_index * local_width, local_width, 0)
-    cot_scaled = cotangent.T.astype(jnp.float32) * grad_scale
-    d_full = jnp.einsum("dmc,mcr->dr", in_proj, d_proj, preferred_element_type=jnp.float32)
+    d_full = jnp.einsum("mcr,dmc->rd", d_proj, in_proj, preferred_element_type=jnp.float32)
     stat_part = jnp.sum(d_proj.astype(jnp.float32) * unrounded, axis=(0, 1))
-    stat_rows = jnp.zeros((8, row_count), jnp.float32).at[0].set(stat_part)
-    groups = lax.axis_size("chan") * lax.axis_size("pair")
-    payload = jnp.concatenate(
-        [
-            d_full.reshape(groups, local_width, row_count),
-            jnp.broadcast_to(stat_rows[None], (groups, 8, row_count)),
-        ],
-        axis=1,
-    ).reshape(groups * (local_width + 8), row_count)
-    reduced = reduce_scatter_cp(payload)
-    d_hidden = reduced[:local_width]
-    row_stat = reduced[local_width : local_width + 1] / model_width
-    scaled = norm_gain_local(norm_gain, group_index, local_width)[:, None] * d_hidden
-    d_embedded = inv_rms * (scaled - normed_local * row_stat) + cot_scaled
-    gain_part = jnp.sum(d_hidden * normed_local, axis=1)
+    stat_block = jnp.broadcast_to(stat_part[:, None], (row_count, 128))
+    hidden_blocks = [
+        jnp.concatenate([d_full[:, g * local_width : (g + 1) * local_width], stat_block], axis=1)
+        for g in range(groups)
+    ]
+    reduced = reduce_scatter_lanes(
+        jnp.concatenate(pair_major(hidden_blocks), axis=1), local_width + 128
+    )
+    d_hidden = reduced[:, :local_width]
+    row_stat = reduced[:, local_width : local_width + 1] / model_width
+    gain_local = norm_gain_local(norm_gain, group_index, local_width)
+    normed_rows = normed_local.T
+    d_embedded = inv_rms.T * (gain_local[None, :] * d_hidden - normed_rows * row_stat) + (
+        cotangent.astype(jnp.float32) * grad_scale
+    )
+    gain_part = jnp.sum(d_hidden * normed_rows, axis=0)
     table_part = jnp.einsum(
-        "kr,cr->kc", onehot_t.astype(jnp.float32), d_embedded, precision=PRECISE
+        "kr,rc->kc", onehot_t.astype(jnp.float32), d_embedded, precision=PRECISE
     )
     summed = psum_seq(jnp.concatenate([table_part, gain_part[None, :]], axis=0))
     kmer_grad = summed[: kmer_len * letter_count]

time: 145 us -> 108 us (0.74)
  local copies, waits for them, and re-layouts: 30.1 us -> 13 us
  starting transfers between devices: 23.2 us -> 14.4 us
  other arithmetic: 24.3 us -> 16.8 us
  matrix products: 28.3 us -> 24.8 us
  blocking collectives: 8.4 us -> 11.1 us
  waiting for transfers between devices: 28.5 us -> 26.4 us
    all_to_all x3 -> x1, starting transfers between devices: 11.3 us -> 3.86 us  [per_device(): lax.all_to_all(jnp.stack([mixed_in, d_conv]), 'seq', split_axis=1, concat...]
    all_to_all x3 -> x1, waiting for transfers between devices: 12.7 us -> 5.72 us  [per_device(): lax.all_to_all(jnp.stack([mixed_in, d_conv]), 'seq', split_axis=1, concat...]
    ppermute x8, waiting for transfers between devices: 15.7 us -> 20.6 us  [xor_exchange(): return lax.ppermute(x, axis, [(i, i ^ step) for i in range(count)])]
    unnamed x99 -> x84, local copies, waits for them, and re-layouts: 9.39 us -> 5.6 us
    dot_general x1, matrix products: 4.17 us -> 1.16 us  [per_device(): jnp.einsum('dr,dmc->mcr', residual, in_proj, preferred_element_type=jnp.f...]
    all_to_all x1, blocking collectives: 8.4 us -> 11.1 us  [per_device(): lax.all_to_all(jnp.stack([conv_cols, d_mixed_cols]), 'seq', split_axis=2,...]
    dot_general x1 -> x0, local copies, waits for them, and re-layouts: 2.56 us -> none  [per_device(): jnp.einsum('dmc,mcr->dr', in_proj, d_proj, preferred_element_type=jnp.flo...]
    concatenate x1 -> x0, local copies, waits for them, and re-layouts: 2.53 us -> none  [per_device(): jnp.concatenate([d_full.reshape(groups, local_width, row_count), jnp.broa...]
  transfers between devices with their start and end apart: 12 -> 10, of which waited for: 8 -> 6; matrix products, arithmetic and copies ran while one was open for 18% -> 16% of each run, Pallas kernels for 0% -> 0%
where the time goes in v2:
time: 108 us
  waiting for transfers between devices  26.4 us (24%)
  matrix products  24.8 us (23%)
  other arithmetic  16.8 us (16%)
  starting transfers between devices  14.4 us (13%)
  local copies, waits for them, and re-layouts  13 us (12%)
  blocking collectives  11.1 us (10%)
  between operations  1.48 us (1%)
    ppermute x8, waiting for transfers between devices, xor_exchange(): return lax.ppermute(x, axis, [(i, i ^ step) for i in range(count)])  20.6 us
    all_to_all x1, blocking collectives, per_device(): lax.all_to_all(jnp.stack([conv_cols, d_mixed_cols]), 'seq', split_axis=2,...  11.1 us
    ppermute x8, starting transfers between devices, xor_exchange(): return lax.ppermute(x, axis, [(i, i ^ step) for i in range(count)])  6.09 us
    dot_general x3, matrix products, forward_dft(): jnp.dot(signal.astype(jnp.float32), dft, precision=TRANSFORM_PRECISION)  5.94 us
    all_to_all x1, waiting for transfers between devices, per_device(): lax.all_to_all(jnp.stack([mixed_in, d_conv]), 'seq', split_axis=1, concat...  5.72 us
    unnamed x84, local copies, waits for them, and re-layouts  5.6 us
    dot_general x1, matrix products, per_device(): jnp.einsum('mcr,dmc->rd', d_proj, in_proj, preferred_element_type=jnp.flo...  5.06 us
    ppermute x1, starting transfers between devices, from_behind(): lax.ppermute(value, axis, [(source, source + steps) for source in range(f...  4.46 us
  transfers between devices with their start and end apart: 10, of which 6 were waited for; matrix products, arithmetic and copies ran while one was open for 16% of the time, Pallas kernels for 0%

profile of v2, /device:TPU:0, one launch (start us, length us, event | category | flops | bytes accessed | tf_op | source)
XLA Modules:
  0.0 107.8 jit_solution(465783755300528637)
XLA Ops:
  0.7 1.6 %copy-done = bf16[2048,512]{1,0:T(8,128)(2,1)S(1)} copy-done((bf16[2048,512]{1,0:T(8,128)(2,1)S(1)}, bf16[2048,512]{1,0:T(8,128)(2,1)}, u32[]{:S(2)}) %copy-start) | copy-done | bytes 2097176
  2.2 1.7 %fusion.81 = f32[128,2048]{1,0:T(8,128)S(1)} fusion(bf16[128,512]{1,0:T(8,128)(2,1)} %param.13, bf16[2048,512]{1,0:T(8,128)(2,1)S(1)} %copy-done), kind=kOutput, calls=%fused_computation.180 | convolution fusion | flops 268435456 | bytes 3276800 | tf_op jit(solution)/shard_map/rd,cd->rc/dot_general | solution.py:181
  4.1 0.7 copy-done.10
  4.8 0.9 fusion.25
  6.2 4.5 %collective-permute-start = (s32[3]{0:T(128)S(1)}, s32[3]{0:T(128)S(1)}, u32[]{:S(2)}, u32[]{:S(2)}) collective-permute-start(s32[3]{0:T(128)S(1)} %slice_add_fusion.2), channel_id=1, source_target_pairs={{0,4},{4,8},{8,12},{1,5},{5,9},{9,13},{2,6},{6,10},{10,14},{3,7},{... | collective-permute-start | bytes 44 | tf_op jit(solution)/shard_map/ppermute | solution.py:16
  11.1 0.6 fusion.56
  12.0 0.7 convolution_bitcast_fusion.3
  12.8 1.2 %fusion.78 = (f32[127,1024]{1,0:T(8,128)}, f32[127,1024]{1,0:T(8,128)}) fusion(f32[128,1024]{1,0:T(8,128)S(1)} %convolution_bitcast_fusion.3), kind=kLoop, calls=%fused_computation.177 | loop fusion | bytes 2080768 | tf_op jit(solution)/shard_map/jit(_roll_static)/slice | solution.py:134
  14.8 1.0 copy-done.8
  15.9 1.4 %select_add_fusion.1 = f32[128,1024]{1,0:T(8,128)S(1)} fusion(f32[128,1024]{1,0:T(8,128)} %collective-permute-done.1, f32[128,512]{1,0:T(8,128)} %copy-done.10, f32[128,512]{1,0:T(8,128)} %copy-done.11, f32[128,512]{1,0:T(8,128)} %copy-done.12, f32[128,512]{1,0:T(8,128)S(1)} %get-tuple-element.35, pred[]{:T(512)S(6)} %eq.132), kind=kLoop, calls=%fused_computation.51 | loop fusion | flops 524288 | bytes 2097153 | tf_op jit(solution)/shard_map/add | solution.py:58
  17.3 1.6 %collective-permute-start.2 = (f32[128,512]{1,0:T(8,128)S(1)}, f32[128,512]{1,0:T(8,128)S(1)}, u32[]{:S(2)}, u32[]{:S(2)}) collective-permute-start(f32[128,512]{1,0:T(8,128)S(1)} %slice_select_fusion.1), channel_id=1, source_target_pairs={{0,2},{2,0},{1,3},{3,1},{4,6},{6,4},{5,7},{7,5},{8,10},{10,8},{9,1... | collective-permute-start | bytes 786440 | tf_op jit(solution)/shard_map/ppermute | solution.py:46
  18.9 3.8 %convolution_bitcast_fusion.2 = f32[3,512,128]{1,2,0:T(8,128)S(1)} fusion(bf16[2048,3,512]{2,0,1:T(8,128)(2,1)} %param.10, f32[128,2048]{1,0:T(8,128)S(1)} %broadcast_multiply_fusion, f32[2048]{0:T(1024)S(1)} %copy-done.22), kind=kOutput, calls=%fused_computation.3 | convolution fusion | flops 805830656 | bytes 8134656 | tf_op jit(solution)/shard_map/dr,dmc->mcr/dot_general | solution.py:170
  22.7 3.1 %collective-permute-done.2 = f32[128,512]{1,0:T(8,128)S(1)} collective-permute-done((f32[128,512]{1,0:T(8,128)S(1)}, f32[128,512]{1,0:T(8,128)S(1)}, u32[]{:S(2)}, u32[]{:S(2)}) %collective-permute-start.2) | collective-permute-done | bytes 262176 | tf_op jit(solution)/shard_map/ppermute | solution.py:46
  25.8 0.8 fusion.43
  26.7 0.9 copy.25
  27.6 3.9 %all-to-all-start = ((bf16[2,512,128]{2,0,1:T(2,128)(2,1)}), bf16[2,512,128]{2,0,1:T(2,128)(2,1)S(1)}, u32[]{:S(2)}, u32[]{:S(2)}) async-start(bf16[2,512,128]{2,0,1:T(2,128)(2,1)} %copy.25), calls=%async_computation | async-start | bytes 524288 | tf_op jit(solution)/shard_map/all_to_all | solution.py:192
  31.9 2.1 %maximum_select_fusion = f32[128,1024]{1,0:T(8,128)} fusion(f32[1,1024]{1,0:T(1,128)S(1)} %get-tuple-element.51, f32[127,1024]{1,0:T(8,128)} %get-tuple-element.53, f32[127,1024]{1,0:T(8,128)} %get-tuple-element.52, f32[1,1024]{1,0:T(1,128)S(1)} %get-tuple-element.50, s32[128]{0:T(128)S(1)} %get-tuple-element.76, s32[128]{0:T(128)S(1)} %get-tuple-element.77, ...), kind=kLoop, calls=%fused_computation.38 | loop fusion | flops 655360 | bytes 1574016 | tf_op jit(solution)/shard_map/jit(_where)/select_n | solution.py:135
  34.1 5.7 %all-to-all-done = bf16[2,512,128]{2,0,1:T(2,128)(2,1)S(1)} async-done(((bf16[2,512,128]{2,0,1:T(2,128)(2,1)}), bf16[2,512,128]{2,0,1:T(2,128)(2,1)S(1)}, u32[]{:S(2)}, u32[]{:S(2)}) %all-to-all-start) | async-done | bytes 262176 | tf_op jit(solution)/shard_map/all_to_all | solution.py:192
  40.0 3.0 %fusion.82 = f32[128,1024]{1,0:T(8,128)} fusion(bf16[128,512]{0,1:T(8,128)(2,1)S(1)} %bitcast.125, f32[512,1024]{1,0:T(8,128)} %bitcast.113), kind=kOutput, calls=%fused_computation.181 | convolution fusion | flops 402653184 | bytes 2752512 | tf_op jit(solution)/shard_map/dot_general | solution.py:99
  43.1 2.3 %fusion.83 = f32[128,1024]{1,0:T(8,128)S(1)} fusion(bf16[128,512]{0,1:T(8,128)(2,1)S(1)} %bitcast.126, f32[512,1024]{1,0:T(8,128)} %bitcast.114), kind=kOutput, calls=%fused_computation.182 | convolution fusion | flops 402653184 | bytes 2752512 | tf_op jit(solution)/shard_map/dot_general | solution.py:99
  46.3 1.1 %slice_add_fusion = (f32[128,512]{1,0:T(8,128)}, f32[128,512]{1,0:T(8,128)}, f32[128,512]{1,0:T(8,128)S(1)}, f32[128,512]{1,0:T(8,128)S(1)}, f32[128,512]{1,0:T(8,128)S(1)}) fusion(f32[128,512]{1,0:T(8,128)S(1)} %get-tuple-element.25, f32[128,1024]{1,0:T(8,128)S(1)} %fusion.15, f32[128,512]{1,0:T(8,128)S(1)} %get-tuple-element.26, ...), kind=kLoop, calls=%fused_computation.67 | loop fusion | flops 1245184 | bytes 3932672 | tf_op jit(solution)/shard_map/add | solution.py:142
  47.4 0.6 copy-done.2
  48.1 1.2 %fusion.4 = bf16[1,128,512]{2,1,0:T(8,128)(2,1)S(1)} fusion(f32[512,1024]{1,0:T(8,128)S(1)} %bitcast.115, f32[128,512]{1,0:T(8,128)S(1)} %get-tuple-element.67, f32[128,512]{1,0:T(8,128)S(1)} %get-tuple-element.40, f32[1024]{0:T(1024)S(1)} %fusion.67), kind=kOutput, calls=%fused_computation.13 | convolution fusion | flops 402980864 | bytes 2756608 | tf_op jit(solution)/shard_map/dot_general | solution.py:107
  49.3 1.2 %fusion.5 = bf16[1,128,512]{2,1,0:T(8,128)(2,1)S(1)} fusion(f32[512,1024]{1,0:T(8,128)S(1)} %bitcast.116, f32[128,512]{1,0:T(8,128)S(1)} %get-tuple-element.68, f32[128,512]{1,0:T(8,128)S(1)} %get-tuple-element.69, f32[1024]{0:T(1024)S(1)} %fusion.67), kind=kOutput, calls=%fused_computation.14 | convolution fusion | flops 402980864 | bytes 2756608 | tf_op jit(solution)/shard_map/dot_general | solution.py:107
  50.6 0.9 copy.29
  51.5 11.1 %all_to_all.30 = bf16[2,128,512]{1,0,2:T(2,128)(2,1)S(1)} all-to-all(bf16[2,128,512]{1,0,2:T(2,128)(2,1)} %copy.29), channel_id=1, replica_groups=mesh['groups'=2,'seq'=4,'chan'=2,'pair'=2] {'seq'}, dimensions={2} | all-to-all | bytes 524288 | tf_op jit(solution)/shard_map/all_to_all | solution.py:202
  62.7 0.8 slice_convert_fusion
  63.5 0.8 reshape.303
  64.3 1.8 %reshape.305 = f32[1,512,128]{1,2,0:T(8,128)} reshape(f32[1,4,128,128]{2,1,3,0:T(4,128)} %get-tuple-element.54) | data formatting | bytes 524288 | tf_op jit(solution)/shard_map/convert_element_type | solution.py:219
  66.1 1.0 fusion.44
  67.1 2.2 %multiply_convert_fusion.1 = (bf16[1,512,128]{1,2,0:T(8,128)(2,1)S(1)}, bf16[1,512,128]{1,2,0:T(8,128)(2,1)S(1)}, bf16[1,512,128]{1,2,0:T(8,128)(2,1)}) fusion(f32[1,512,128]{1,2,0:T(8,128)} %reshape.305, f32[3,512,128]{1,2,0:T(8,128)} %copy-done.4, f32[1,512,128]{1,2,0:T(8,128)} %reshape.303), kind=kLoop, calls=%fused_computation.86 | loop fusion | flops 393216 | bytes 1703936 | tf_op jit(solution)/shard_map/convert.4
  69.3 5.1 %convolution_bitcast_fusion = f32[128,2048]{1,0:T(8,128)S(1)} fusion(bf16[2048,3,512]{2,0,1:T(8,128)(2,1)} %param.10, bf16[1,512,128]{1,2,0:T(8,128)(2,1)S(1)} %get-tuple-element.34, bf16[1,512,128]{1,2,0:T(8,128)(2,1)S(1)} %get-tuple-element.33, bf16[1,512,128]{1,2,0:T(8,128)(2,1)S(1)} %fusion.44), kind=kOutput, calls=%fused_computation | convolution fusion | flops 805699584 | bytes 7733248 | tf_op jit(solution)/shard_map/mcr,dmc->rd/dot_general | solution.py:223
  74.4 1.2 %fusion.2 = f32[128]{0:T(128)S(1)} fusion(f32[3,512,128]{1,2,0:T(8,128)S(1)} %copy-done.5, bf16[2048,3,512]{2,0,1:T(8,128)(2,1)S(1)} %bitcast.119, f32[128,2048]{1,0:T(8,128)S(1)} %broadcast_multiply_fusion, f32[2048]{0:T(1024)S(1)} %copy-done.22, bf16[1,512,128]{1,2,0:T(8,128)(2,1)S(1)} %get-tuple-element.34, ...), kind=kOutput, calls=%fused_computation.7 | convolution fusion | flops 807796608 | bytes 8528384 | tf_op jit(solution)/shard_map/dr,dmc->mcr/dot_general | solution.py:172
  75.8 0.6 copy-done.13
  76.4 0.9 fusion.24
  77.3 1.6 %collective-permute-start.3 = (bf16[1,512,128]{1,2,0:T(8,128)(2,1)}, bf16[1,512,128]{1,2,0:T(8,128)(2,1)}, u32[]{:S(2)}, u32[]{:S(2)}) collective-permute-start(bf16[1,512,128]{1,2,0:T(8,128)(2,1)} %get-tuple-element.39), channel_id=1, source_target_pairs={{0,2},{2,0},{1,3},{3,1},{4,6},{6,4},{5,7},{7,5},{8,10},{10,8},{9,1... | collective-permute-start | bytes 393224 | tf_op jit(solution)/shard_map/ppermute | solution.py:46
  78.9 4.6 %collective-permute-done.3 = bf16[1,512,128]{1,2,0:T(8,128)(2,1)} collective-permute-done((bf16[1,512,128]{1,2,0:T(8,128)(2,1)}, bf16[1,512,128]{1,2,0:T(8,128)(2,1)}, u32[]{:S(2)}, u32[]{:S(2)}) %collective-permute-start.3) | collective-permute-done | bytes 131104 | tf_op jit(solution)/shard_map/ppermute | solution.py:46
  83.5 1.0 broadcast_select_fusion.3
  84.7 1.5 %select_add_fusion = f32[128,1280]{1,0:T(8,128)S(1)} fusion(f32[128,1280]{1,0:T(8,128)} %collective-permute-done.5, f32[128,128]{1,0:T(8,128)S(1)} %broadcast_in_dim.55, f32[128,512]{1,0:T(8,128)} %copy-done.14, f32[128,512]{1,0:T(8,128)} %copy-done.15, f32[128,512]{1,0:T(8,128)} %copy-done.13, f32[128,512]{1,0:T(8,128)S(1)} %get-tuple-element.29, pred[]{:T(512)S(6)} %eq.132), kind=kLoop, calls=%fused_computation.32 | loop fusion | flops 1310720 | bytes 2424833 | tf_op jit(solution)/shard_map/add | solution.py:58
  86.3 1.6 %collective-permute-start.6 = (f32[128,640]{1,0:T(8,128)S(1)}, f32[128,640]{1,0:T(8,128)S(1)}, u32[]{:S(2)}, u32[]{:S(2)}) collective-permute-start(f32[128,640]{1,0:T(8,128)S(1)} %slice_select_fusion), channel_id=1, source_target_pairs={{0,2},{2,0},{1,3},{3,1},{4,6},{6,4},{5,7},{7,5},{8,10},{10,8},{9,1... | collective-permute-start | bytes 983048 | tf_op jit(solution)/shard_map/ppermute | solution.py:46
  87.8 1.9 %convolution_bitcast_fusion.4 = f32[1,1,128,512]{3,2,1,0:T(8,128)} fusion(f32[512,1024]{1,0:T(8,128)S(1)} %bitcast.117, f32[128,512]{1,0:T(8,128)S(1)} %copy-done.18, f32[128,512]{1,0:T(8,128)S(1)} %copy-done.17, f32[1024]{0:T(1024)S(1)} %fusion.67), kind=kOutput, calls=%fused_computation.8 | convolution fusion | flops 402915328 | bytes 2887680 | tf_op jit(solution)/shard_map/dot_general | solution.py:107
  89.8 6.5 %collective-permute-done.6 = f32[128,640]{1,0:T(8,128)S(1)} collective-permute-done((f32[128,640]{1,0:T(8,128)S(1)}, f32[128,640]{1,0:T(8,128)S(1)}, u32[]{:S(2)}, u32[]{:S(2)}) %collective-permute-start.6) | collective-permute-done | bytes 327712 | tf_op jit(solution)/shard_map/ppermute | solution.py:46
  96.9 0.6 collective-permute-start.7
  97.8 3.2 %collective-permute-done.7 = f32[21,512]{1,0:T(8,128)S(1)} collective-permute-done((f32[21,512]{1,0:T(8,128)S(1)}, f32[21,512]{1,0:T(8,128)S(1)}, u32[]{:S(2)}, u32[]{:S(2)}) %collective-permute-start.7) | collective-permute-done | bytes 43040 | tf_op jit(solution)/shard_map/ppermute | solution.py:46
  101.3 2.1 %fusion.3 = bf16[128,512]{1,0:T(8,128)(2,1)} fusion(bf16[2048,128]{1,0:T(8,128)(2,1)S(1)} %bitcast.121, bf16[2048,512]{1,0:T(8,128)(2,1)S(1)} %copy-done, f32[128,2048]{1,0:T(8,128)} %copy-done.8, s32[]{:T(128)S(6)} %select_n.288), kind=kOutput, calls=%fused_computation.10 | convolution fusion | flops 268566528 | bytes 3014660 | tf_op jit(solution)/shard_map/cr,cd->rd/dot_general | solution.py:208
  103.4 3.2 %collective-permute-done.8 = f32[21,512]{1,0:T(8,128)S(1)} collective-permute-done((f32[21,512]{1,0:T(8,128)S(1)}, f32[21,512]{1,0:T(8,128)S(1)}, u32[]{:S(2)}, u32[]{:S(2)}) %collective-permute-start.8) | collective-permute-done | bytes 43040 | tf_op jit(solution)/shard_map/ppermute | solution.py:46
  106.6 0.6 slice.238
  107.2 0.6 copy.32
  (139 shorter events, 5.8 us)
Async XLA Ops:
  0.6 1.6 %copy-start = (bf16[2048,512]{1,0:T(8,128)(2,1)S(1)}, bf16[2048,512]{1,0:T(8,128)(2,1)}, u32[]{:S(2)}) copy-start(bf16[2048,512]{1,0:T(8,128)(2,1)} %param.12) | copy-start | bytes 6291460
  3.9 2.2 %copy-start.38 = (s32[128]{0:T(128)S(1)}, s32[128]{0:T(128)}, u32[]{:S(2)}) copy-start(s32[128]{0:T(128)} %param.7) | copy-start | bytes 1540
  4.0 0.7 copy-start.10
  4.1 1.6 %copy-start.11 = (f32[128,512]{1,0:T(8,128)}, f32[128,512]{1,0:T(8,128)S(1)}, u32[]{:S(2)}) copy-start(f32[128,512]{1,0:T(8,128)S(1)} %get-tuple-element.37) | copy-start | bytes 786436
  4.1 2.0 %copy-start.12 = (f32[128,512]{1,0:T(8,128)}, f32[128,512]{1,0:T(8,128)S(1)}, u32[]{:S(2)}) copy-start(f32[128,512]{1,0:T(8,128)S(1)} %get-tuple-element.38) | copy-start | bytes 786436
  4.7 7.3 %copy-start.20 = (f32[1,1,128,512]{3,2,1,0:T(8,128)S(1)}, f32[1,1,128,512]{3,2,1,0:T(8,128)}, u32[]{:S(2)}) copy-start(f32[1,1,128,512]{3,2,1,0:T(8,128)} %param.11) | copy-start | bytes 786436
  5.6 10.3 %collective-permute-start.1 = (f32[128,1024]{1,0:T(8,128)}, f32[128,1024]{1,0:T(8,128)}, u32[]{:S(2)}, u32[]{:S(2)}) collective-permute-start(f32[128,1024]{1,0:T(8,128)} %fusion.25), channel_id=1, source_target_pairs={{0,1},{1,0},{2,3},{3,2},{4,5},{5,4},{6,7},{7,6},{8,9},{9,8},{10,11... | collective-permute-start | bytes 1572872 | tf_op jit(solution)/shard_map/ppermute | solution.py:46
  6.2 7.9 %collective-permute-start = (s32[3]{0:T(128)S(1)}, s32[3]{0:T(128)S(1)}, u32[]{:S(2)}, u32[]{:S(2)}) collective-permute-start(s32[3]{0:T(128)S(1)} %slice_add_fusion.2), channel_id=1, source_target_pairs={{0,4},{4,8},{8,12},{1,5},{5,9},{9,13},{2,6},{6,10},{10,14},{3,7},{... | collective-permute-start | bytes 44 | tf_op jit(solution)/shard_map/ppermute | solution.py:16
  10.7 3.7 %copy-start.25 = (pred[128,5]{0,1:T(8,128)(4,1)}, pred[128,5]{0,1:T(8,128)(4,1)S(1)}, u32[]{:S(2)}) copy-start(pred[128,5]{0,1:T(8,128)(4,1)S(1)} %iota_compare_fusion.5) | copy-start | bytes 1924
  12.0 1.9 %copy-start.1 = (f32[16,32,1024]{2,1,0:T(8,128)}, f32[16,32,1024]{2,1,0:T(8,128)S(1)}, u32[]{:S(2)}) copy-start(f32[16,32,1024]{2,1,0:T(8,128)S(1)} %multiply_subtract_fusion) | copy-start | bytes 6291460
  12.0 2.0 %copy-start.21 = (bf16[4,5,2048]{2,0,1:T(4,128)(2,1)S(1)}, bf16[4,5,2048]{2,0,1:T(4,128)(2,1)}, u32[]{:S(2)}) copy-start(bf16[4,5,2048]{2,0,1:T(4,128)(2,1)} %param.8) | copy-start | bytes 245764
  12.7 1.2 %copy-start.6 = (f32[128,1024]{1,0:T(8,128)}, f32[128,1024]{1,0:T(8,128)S(1)}, u32[]{:S(2)}) copy-start(f32[128,1024]{1,0:T(8,128)S(1)} %convolution_bitcast_fusion.3) | copy-start | bytes 1572868
  14.0 18.0 %copy-start.29 = (s32[128]{0:T(128)}, s32[128]{0:T(128)S(1)}, u32[]{:S(2)}) copy-start(s32[128]{0:T(128)S(1)} %get-tuple-element.76) | copy-start | bytes 1540
  14.0 18.0 %copy-start.31 = (s32[128]{0:T(128)}, s32[128]{0:T(128)S(1)}, u32[]{:S(2)}) copy-start(s32[128]{0:T(128)S(1)} %get-tuple-element.77) | copy-start | bytes 1540
  14.0 17.9 %copy-start.33 = (pred[128]{0:T(512)(128)(4,1)}, pred[128]{0:T(512)(128)(4,1)S(1)}, u32[]{:S(2)}) copy-start(pred[128]{0:T(512)(128)(4,1)S(1)} %compare_and_fusion) | copy-start | bytes 388
  14.3 3.0 %copy-start.27 = (pred[128,5]{0,1:T(8,128)(4,1)}, pred[128,5]{0,1:T(8,128)(4,1)S(1)}, u32[]{:S(2)}) copy-start(pred[128,5]{0,1:T(8,128)(4,1)S(1)} %iota_compare_fusion.4) | copy-start | bytes 1924
  14.3 3.0 %copy-start.23 = (pred[128,5]{0,1:T(8,128)(4,1)}, pred[128,5]{0,1:T(8,128)(4,1)S(1)}, u32[]{:S(2)}) copy-start(pred[128,5]{0,1:T(8,128)(4,1)S(1)} %get-tuple-element.75) | copy-start | bytes 1924
  14.8 1.0 copy-start.8
  14.8 2.5 %copy-start.35 = (f32[128]{0:T(128)}, f32[128]{0:T(128)S(1)}, u32[]{:S(2)}) copy-start(f32[128]{0:T(128)S(1)} %add_rsqrt_fusion) | copy-start | bytes 1540
  15.8 3.1 %copy-start.22 = (f32[2048]{0:T(1024)S(1)}, f32[2048]{0:T(1024)}, u32[]{:S(2)}) copy-start(f32[2048]{0:T(1024)} %param.9) | copy-start | bytes 24580
  17.3 8.5 %collective-permute-start.2 = (f32[128,512]{1,0:T(8,128)S(1)}, f32[128,512]{1,0:T(8,128)S(1)}, u32[]{:S(2)}, u32[]{:S(2)}) collective-permute-start(f32[128,512]{1,0:T(8,128)S(1)} %slice_select_fusion.1), channel_id=1, source_target_pairs={{0,2},{2,0},{1,3},{3,1},{4,6},{6,4},{5,7},{7,5},{8,10},{10,8},{9,1... | collective-permute-start | bytes 786440 | tf_op jit(solution)/shard_map/ppermute | solution.py:46
  22.7 3.2 %copy-start.4 = (f32[3,512,128]{1,2,0:T(8,128)}, f32[3,512,128]{1,2,0:T(8,128)S(1)}, u32[]{:S(2)}) copy-start(f32[3,512,128]{1,2,0:T(8,128)S(1)} %convolution_bitcast_fusion.2) | copy-start | bytes 2359300
  27.6 12.3 %all-to-all-start = ((bf16[2,512,128]{2,0,1:T(2,128)(2,1)}), bf16[2,512,128]{2,0,1:T(2,128)(2,1)S(1)}, u32[]{:S(2)}, u32[]{:S(2)}) async-start(bf16[2,512,128]{2,0,1:T(2,128)(2,1)} %copy.25), calls=%async_computation | async-start | bytes 524288 | tf_op jit(solution)/shard_map/all_to_all | solution.py:192
  43.0 2.4 %copy-start.37 = (pred[512]{0:T(512)(128)(4,1)S(1)}, pred[512]{0:T(512)(128)(4,1)}, u32[]{:S(2)}) copy-start(pred[512]{0:T(512)(128)(4,1)} %iota_compare_fusion.6) | copy-start | bytes 1540
  43.1 2.3 %copy-start.7 = (f32[128,1024]{1,0:T(8,128)S(1)}, f32[128,1024]{1,0:T(8,128)}, u32[]{:S(2)}) copy-start(f32[128,1024]{1,0:T(8,128)} %copy-done.6) | copy-start | bytes 1572868
  43.1 2.3 %copy-start.9 = (f32[128,1024]{1,0:T(8,128)S(1)}, f32[128,1024]{1,0:T(8,128)}, u32[]{:S(2)}) copy-start(f32[128,1024]{1,0:T(8,128)} %fusion.82) | copy-start | bytes 1572868
  43.1 2.3 %copy-start.16 = (f32[128,1024]{1,0:T(8,128)S(1)}, f32[128,1024]{1,0:T(8,128)}, u32[]{:S(2)}) copy-start(f32[128,1024]{1,0:T(8,128)} %maximum_select_fusion) | copy-start | bytes 1572868
  46.3 1.8 %copy-start.2 = (f32[16,32,1024]{2,1,0:T(8,128)S(1)}, f32[16,32,1024]{2,1,0:T(8,128)}, u32[]{:S(2)}) copy-start(f32[16,32,1024]{2,1,0:T(8,128)} %copy-done.1) | copy-start | bytes 6291460
  67.1 7.3 %slice-start = ((s8[6291456]{0:T(1024)(128)(4,1)}), s8[4194304]{0:T(1024)(128)(4,1)S(1)}, s32[]{:S(2)}) async-start(s8[6291456]{0:T(1024)(128)(4,1)} %bitcast.118), calls=%async_computation.2 | async-start | bytes 8388608
  69.3 5.1 %slice-start.1 = ((s8[6291456]{0:T(1024)(128)(4,1)}), s8[2097152]{0:T(1024)(128)(4,1)S(1)}, s32[]{:S(2)}) async-start(s8[6291456]{0:T(1024)(128)(4,1)} %bitcast.118), calls=%async_computation.3 | async-start | bytes 4194304
  69.3 5.1 %copy-start.5 = (f32[3,512,128]{1,2,0:T(8,128)S(1)}, f32[3,512,128]{1,2,0:T(8,128)}, u32[]{:S(2)}) copy-start(f32[3,512,128]{1,2,0:T(8,128)} %copy-done.4) | copy-start | bytes 2359300
  75.6 0.7 copy-start.13
  75.7 1.6 %copy-start.14 = (f32[128,512]{1,0:T(8,128)}, f32[128,512]{1,0:T(8,128)S(1)}, u32[]{:S(2)}) copy-start(f32[128,512]{1,0:T(8,128)S(1)} %get-tuple-element.31) | copy-start | bytes 786436
  75.7 1.6 %copy-start.15 = (f32[128,512]{1,0:T(8,128)}, f32[128,512]{1,0:T(8,128)S(1)}, u32[]{:S(2)}) copy-start(f32[128,512]{1,0:T(8,128)S(1)} %get-tuple-element.32) | copy-start | bytes 786436
  77.3 7.4 %collective-permute-start.5 = (f32[128,1280]{1,0:T(8,128)}, f32[128,1280]{1,0:T(8,128)}, u32[]{:S(2)}, u32[]{:S(2)}) collective-permute-start(f32[128,1280]{1,0:T(8,128)} %fusion.24), channel_id=1, source_target_pairs={{0,1},{1,0},{2,3},{3,2},{4,5},{5,4},{6,7},{7,6},{8,9},{9,8},{10,11... | collective-permute-start | bytes 1966088 | tf_op jit(solution)/shard_map/ppermute | solution.py:46
  77.3 6.2 %collective-permute-start.3 = (bf16[1,512,128]{1,2,0:T(8,128)(2,1)}, bf16[1,512,128]{1,2,0:T(8,128)(2,1)}, u32[]{:S(2)}, u32[]{:S(2)}) collective-permute-start(bf16[1,512,128]{1,2,0:T(8,128)(2,1)} %get-tuple-element.39), channel_id=1, source_target_pairs={{0,2},{2,0},{1,3},{3,1},{4,6},{6,4},{5,7},{7,5},{8,10},{10,8},{9,1... | collective-permute-start | bytes 393224 | tf_op jit(solution)/shard_map/ppermute | solution.py:46
  84.5 3.3 %copy-start.3 = (f32[16,32,1024]{2,1,0:T(8,128)S(1)}, f32[16,32,1024]{2,1,0:T(8,128)}, u32[]{:S(2)}) copy-start(f32[16,32,1024]{2,1,0:T(8,128)} %copy-done.1) | copy-start | bytes 6291460
  84.5 3.3 %copy-start.17 = (f32[128,512]{1,0:T(8,128)S(1)}, f32[128,512]{1,0:T(8,128)}, u32[]{:S(2)}) copy-start(f32[128,512]{1,0:T(8,128)} %get-tuple-element.44) | copy-start | bytes 786436
  84.5 3.3 %copy-start.18 = (f32[128,512]{1,0:T(8,128)S(1)}, f32[128,512]{1,0:T(8,128)}, u32[]{:S(2)}) copy-start(f32[128,512]{1,0:T(8,128)} %get-tuple-element.45) | copy-start | bytes 786436
  84.6 5.2 %collective-permute-start.4 = (bf16[2,1,512,128]{2,3,0,1:T(8,128)(2,1)S(1)}, bf16[2,1,512,128]{2,3,0,1:T(8,128)(2,1)S(1)}, u32[]{:S(2)}, u32[]{:S(2)}) collective-permute-start(bf16[2,1,512,128]{2,3,0,1:T(8,128)(2,1)S(1)} %maximum_bitcast_fusion), channel_id=1, source_target_pairs={{0,1},{1,0},{2,3},{3,2},{4,5},{5,4},{6,7},{7,6},{8,9},{9,8},{10,11... | collective-permute-start | bytes 786440 | tf_op jit(solution)/shard_map/ppermute | solution.py:46
  86.3 10.0 %collective-permute-start.6 = (f32[128,640]{1,0:T(8,128)S(1)}, f32[128,640]{1,0:T(8,128)S(1)}, u32[]{:S(2)}, u32[]{:S(2)}) collective-permute-start(f32[128,640]{1,0:T(8,128)S(1)} %slice_select_fusion), channel_id=1, source_target_pairs={{0,2},{2,0},{1,3},{3,1},{4,6},{6,4},{5,7},{7,5},{8,10},{10,8},{9,1... | collective-permute-start | bytes 983048 | tf_op jit(solution)/shard_map/ppermute | solution.py:46
  89.7 6.8 %copy-start.19 = (bf16[128,512]{1,0:T(8,128)(2,1)S(1)}, bf16[128,512]{1,0:T(8,128)(2,1)}, u32[]{:S(2)}) copy-start(bf16[128,512]{1,0:T(8,128)(2,1)} %param.13) | copy-start | bytes 393220
  89.7 6.8 %copy-start.24 = (pred[128,5]{0,1:T(8,128)(4,1)S(1)}, pred[128,5]{0,1:T(8,128)(4,1)}, u32[]{:S(2)}) copy-start(pred[128,5]{0,1:T(8,128)(4,1)} %copy-done.23) | copy-start | bytes 1924
  89.7 6.8 %copy-start.26 = (pred[128,5]{0,1:T(8,128)(4,1)S(1)}, pred[128,5]{0,1:T(8,128)(4,1)}, u32[]{:S(2)}) copy-start(pred[128,5]{0,1:T(8,128)(4,1)} %copy-done.25) | copy-start | bytes 1924
  89.7 6.8 %copy-start.28 = (pred[128,5]{0,1:T(8,128)(4,1)S(1)}, pred[128,5]{0,1:T(8,128)(4,1)}, u32[]{:S(2)}) copy-start(pred[128,5]{0,1:T(8,128)(4,1)} %copy-done.27) | copy-start | bytes 1924
  89.7 6.8 %copy-start.36 = (f32[128]{0:T(128)S(1)}, f32[128]{0:T(128)}, u32[]{:S(2)}) copy-start(f32[128]{0:T(128)} %copy-done.35) | copy-start | bytes 1540
  96.9 4.2 %collective-permute-start.7 = (f32[21,512]{1,0:T(8,128)S(1)}, f32[21,512]{1,0:T(8,128)S(1)}, u32[]{:S(2)}, u32[]{:S(2)}) collective-permute-start(f32[21,512]{1,0:T(8,128)S(1)} %pad_maximum_fusion.12), channel_id=1, source_target_pairs={{0,4},{4,0},{8,12},{12,8},{1,5},{5,1},{9,13},{13,9},{2,6},{6,2},{1... | collective-permute-start | bytes 129032 | tf_op jit(solution)/shard_map/ppermute | solution.py:46
  101.0 5.6 %collective-permute-start.8 = (f32[21,512]{1,0:T(8,128)S(1)}, f32[21,512]{1,0:T(8,128)S(1)}, u32[]{:S(2)}, u32[]{:S(2)}) collective-permute-start(f32[21,512]{1,0:T(8,128)S(1)} %fusion.100), channel_id=1, source_target_pairs={{0,8},{4,12},{8,0},{12,4},{1,9},{5,13},{9,1},{13,5},{2,10},{6,14},... | collective-permute-start | bytes 129032 | tf_op jit(solution)/shard_map/ppermute | solution.py:46
  (3 other events, 1.9 us)

commit v3 on v2

--- a/solution.py
+++ b/solution.py
@@ -86,13 +86,45 @@
     return y.reshape((chans * pairs * x.shape[0],) + x.shape[1:])
 
 
-def psum_seq(x):
+def group_exchange(x, axes, count, offset):
+    return lax.ppermute(x, axes, [(i, i ^ offset) for i in range(count)])
+
+
+def reduce_blocks_cp(x, width):
+    axes = ("chan", "pair")
+    count = lax.axis_size("chan") * lax.axis_size("pair")
+    me = lax.axis_index(axes)
+    blocks = [x[:, g * width : (g + 1) * width] for g in range(count)]
+
+    def pick(index):
+        out = blocks[0]
+        for g in range(1, count):
+            out = jnp.where(index == g, blocks[g], out)
+        return out
+
+    total = pick(me)
+    for offset in range(1, count):
+        total = total + group_exchange(pick(me ^ offset), axes, count, offset)
+    return total
+
+
+def sum_over_seq(x):
     count = lax.axis_size("seq")
-    step = 1
-    while step < count:
-        x = x + xor_exchange(x, "seq", step)
-        step *= 2
-    return x
+    me = lax.axis_index("seq")
+    if count > 4:
+        step = 1
+        while step < count:
+            x = x + xor_exchange(x, "seq", step)
+            step *= 2
+        return x
+    got = [x] + [group_exchange(x, "seq", count, offset) for offset in range(1, count)]
+    total = None
+    for source in range(count):
+        piece = got[0]
+        for offset in range(1, count):
+            piece = jnp.where((me ^ source) == offset, got[offset], piece)
+        total = piece if total is None else total + piece
+    return total
 
 
 def forward_dft(signal, dft):
@@ -219,29 +251,23 @@
     d_key = d_mixed.astype(jnp.float32) * value_part
     d_value = d_mixed.astype(jnp.float32) * key_part
     d_proj = jnp.stack([d_query, d_key, d_value]).astype(jnp.bfloat16)
-    normed_local = lax.dynamic_slice_in_dim(normed, group_index * local_width, local_width, 0)
     d_full = jnp.einsum("mcr,dmc->rd", d_proj, in_proj, preferred_element_type=jnp.float32)
     stat_part = jnp.sum(d_proj.astype(jnp.float32) * unrounded, axis=(0, 1))
-    stat_block = jnp.broadcast_to(stat_part[:, None], (row_count, 128))
-    hidden_blocks = [
-        jnp.concatenate([d_full[:, g * local_width : (g + 1) * local_width], stat_block], axis=1)
-        for g in range(groups)
-    ]
-    reduced = reduce_scatter_lanes(
-        jnp.concatenate(pair_major(hidden_blocks), axis=1), local_width + 128
-    )
-    d_hidden = reduced[:, :local_width]
-    row_stat = reduced[:, local_width : local_width + 1] / model_width
-    gain_local = norm_gain_local(norm_gain, group_index, local_width)
-    normed_rows = normed_local.T
-    d_embedded = inv_rms.T * (gain_local[None, :] * d_hidden - normed_rows * row_stat) + (
-        cotangent.astype(jnp.float32) * grad_scale
-    )
-    gain_part = jnp.sum(d_hidden * normed_rows, axis=0)
-    table_part = jnp.einsum(
-        "kr,rc->kc", onehot_t.astype(jnp.float32), d_embedded, precision=PRECISE
-    )
-    summed = psum_seq(jnp.concatenate([table_part, gain_part[None, :]], axis=0))
+    onehot_rows = onehot_t.T.astype(jnp.float32)
+    weights = onehot_rows * inv_rms.T
+    direct = jnp.einsum("rk,rd->kd", weights, d_full, precision=PRECISE)
+    centred = jnp.einsum("rk,dr->kd", weights * stat_part[:, None], normed, precision=PRECISE)
+    table_all = norm_gain[None, :] * direct - centred / model_width
+    gain_all = jnp.einsum("rd,dr->d", d_full, normed, precision=PRECISE)
+    partial = jnp.concatenate([table_all, gain_all[None, :]], axis=0)
+    own_block = reduce_blocks_cp(partial, local_width)
+    cot_table = jnp.einsum(
+        "rk,rc->kc", onehot_rows, cotangent.astype(jnp.float32) * grad_scale, precision=PRECISE
+    )
+    own_block = own_block + jnp.concatenate(
+        [cot_table, jnp.zeros((1, local_width), jnp.float32)], axis=0
+    )
+    summed = sum_over_seq(own_block)
     kmer_grad = summed[: kmer_len * letter_count]
     gain_grad = summed[kmer_len * letter_count]
     return (

time: 108 us -> 99.2 us (0.919)
  blocking collectives: 11.1 us -> 0 us
  waiting for transfers between devices: 26.4 us -> 19.2 us
  starting transfers between devices: 14.4 us -> 21.3 us
  matrix products: 24.8 us -> 28.8 us
  other arithmetic: 16.8 us -> 14.8 us
    ppermute x8 -> x4, waiting for transfers between devices: 20.6 us -> 3.04 us  [xor_exchange(): return lax.ppermute(x, axis, [(i, i ^ step) for i in range(count)])]
    all_to_all x1 -> x0, blocking collectives: 11.1 us -> none  [per_device(): lax.all_to_all(jnp.stack([conv_cols, d_mixed_cols]), 'seq', split_axis=2,...]
    all_to_all x0 -> x1, waiting for transfers between devices: none -> 6.73 us  [per_device(): lax.all_to_all(jnp.stack([conv_cols, d_mixed_cols]), 'seq', split_axis=2,...]
    ppermute x0 -> x6, starting transfers between devices: none -> 5.76 us  [group_exchange(): return lax.ppermute(x, axes, [(i, i ^ offset) for i in range(count)])]
    ppermute x0 -> x6, waiting for transfers between devices: none -> 3.71 us  [group_exchange(): return lax.ppermute(x, axes, [(i, i ^ offset) for i in range(count)])]
    all_to_all x0 -> x1, starting transfers between devices: none -> 3.58 us  [per_device(): lax.all_to_all(jnp.stack([conv_cols, d_mixed_cols]), 'seq', split_axis=2,...]
    dot_general x1, matrix products: 1.16 us -> 3.95 us  [per_device(): jnp.einsum('dr,dmc->mcr', residual, in_proj, preferred_element_type=jnp.f...]
    ppermute x8 -> x4, starting transfers between devices: 6.09 us -> 3.6 us  [xor_exchange(): return lax.ppermute(x, axis, [(i, i ^ step) for i in range(count)])]
  transfers between devices with their start and end apart: 10 -> 13, of which waited for: 6 -> 7; matrix products, arithmetic and copies ran while one was open for 16% -> 15% of each run, Pallas kernels for 0% -> 0%
where the time goes in v3:
time: 99.2 us; the launch traced here: 98.5 us
  matrix products  28.8 us (29%)
  starting transfers between devices  21.3 us (21%)
  waiting for transfers between devices  19.2 us (19%)
  other arithmetic  14.8 us (15%)
  local copies, waits for them, and re-layouts  12.9 us (13%)
  between operations  1.46 us (1%)
    all_to_all x1, waiting for transfers between devices, per_device(): lax.all_to_all(jnp.stack([conv_cols, d_mixed_cols]), 'seq', split_axis=2,...  6.73 us
    dot_general x3, matrix products, forward_dft(): jnp.dot(signal.astype(jnp.float32), dft, precision=TRANSFORM_PRECISION)  5.9 us
    ppermute x6, starting transfers between devices, group_exchange(): return lax.ppermute(x, axes, [(i, i ^ offset) for i in range(count)])  5.76 us
    all_to_all x1, waiting for transfers between devices, per_device(): lax.all_to_all(jnp.stack([mixed_in, d_conv]), 'seq', split_axis=1, concat...  5.7 us
    dot_general x1, matrix products, per_device(): jnp.einsum('mcr,dmc->rd', d_proj, in_proj, preferred_element_type=jnp.flo...  4.97 us
    ppermute x1, starting transfers between devices, from_behind(): lax.ppermute(value, axis, [(source, source + steps) for source in range(f...  4.46 us
    dot_general x3, matrix products, inverse_dft(): lax.dot_general(spec * weight, dft, (((1,), (1,)), ((), ())), precision=T...  4.35 us
    unnamed x72, local copies, waits for them, and re-layouts  4.07 us
  transfers between devices with their start and end apart: 13, of which 7 were waited for; matrix products, arithmetic and copies ran while one was open for 15% of the time, Pallas kernels for 0%

profile of v3, /device:TPU:0, one launch (start us, length us, event | category | flops | bytes accessed | tf_op | source)
XLA Modules:
  0.0 98.5 jit_solution(16930091899185187635)
XLA Ops:
  0.7 1.6 %copy-done = bf16[2048,512]{1,0:T(8,128)(2,1)S(1)} copy-done((bf16[2048,512]{1,0:T(8,128)(2,1)S(1)}, bf16[2048,512]{1,0:T(8,128)(2,1)}, u32[]{:S(2)}) %copy-start) | copy-done | bytes 2097176
  2.2 1.7 %fusion.85 = f32[128,2048]{1,0:T(8,128)S(1)} fusion(bf16[128,512]{1,0:T(8,128)(2,1)} %param.13, bf16[2048,512]{1,0:T(8,128)(2,1)S(1)} %copy-done), kind=kOutput, calls=%fused_computation.185 | convolution fusion | flops 268435456 | bytes 3276800 | tf_op jit(solution)/shard_map/rd,cd->rc/dot_general | solution.py:213
  4.1 0.7 copy-done.9
  4.8 0.9 fusion.29
  6.2 4.5 %collective-permute-start = (s32[3]{0:T(128)S(1)}, s32[3]{0:T(128)S(1)}, u32[]{:S(2)}, u32[]{:S(2)}) collective-permute-start(s32[3]{0:T(128)S(1)} %slice_add_fusion.2), channel_id=1, source_target_pairs={{0,4},{4,8},{8,12},{1,5},{5,9},{9,13},{2,6},{6,10},{10,14},{3,7},{... | collective-permute-start | bytes 44 | tf_op jit(solution)/shard_map/ppermute | solution.py:16
  12.1 0.7 convolution_bitcast_fusion.2
  12.8 1.2 %fusion.82 = (f32[127,1024]{1,0:T(8,128)}, f32[127,1024]{1,0:T(8,128)}) fusion(f32[128,1024]{1,0:T(8,128)S(1)} %convolution_bitcast_fusion.2), kind=kLoop, calls=%fused_computation.182 | loop fusion | bytes 2080768 | tf_op jit(solution)/shard_map/jit(_roll_static)/slice | solution.py:166
  14.8 1.4 %select_add_fusion = f32[128,1024]{1,0:T(8,128)S(1)} fusion(f32[128,1024]{1,0:T(8,128)} %collective-permute-done.1, f32[128,512]{1,0:T(8,128)} %copy-done.9, f32[128,512]{1,0:T(8,128)} %copy-done.10, f32[128,512]{1,0:T(8,128)} %copy-done.11, f32[128,512]{1,0:T(8,128)S(1)} %get-tuple-element.36, pred[]{:T(512)S(6)} %eq.200), kind=kLoop, calls=%fused_computation.50 | loop fusion | flops 524288 | bytes 2097153 | tf_op jit(solution)/shard_map/add | solution.py:58
  16.2 1.6 %collective-permute-start.2 = (f32[128,512]{1,0:T(8,128)S(1)}, f32[128,512]{1,0:T(8,128)S(1)}, u32[]{:S(2)}, u32[]{:S(2)}) collective-permute-start(f32[128,512]{1,0:T(8,128)S(1)} %slice_select_fusion), channel_id=1, source_target_pairs={{0,2},{2,0},{1,3},{3,1},{4,6},{6,4},{5,7},{7,5},{8,10},{10,8},{9,1... | collective-permute-start | bytes 786440 | tf_op jit(solution)/shard_map/ppermute | solution.py:46
  17.8 3.8 %convolution_bitcast_fusion.1 = f32[3,512,128]{1,2,0:T(8,128)S(1)} fusion(bf16[2048,3,512]{2,0,1:T(8,128)(2,1)} %param.10, f32[128,2048]{1,0:T(8,128)S(1)} %get-tuple-element.74, f32[2048]{0:T(1024)S(1)} %copy-done.18, f32[128]{0:T(128)S(1)} %add_rsqrt_fusion), kind=kOutput, calls=%fused_computation.5 | convolution fusion | flops 806092800 | bytes 8135168 | tf_op jit(solution)/shard_map/dr,dmc->mcr/dot_general | solution.py:202
  21.7 3.0 %collective-permute-done.2 = f32[128,512]{1,0:T(8,128)S(1)} collective-permute-done((f32[128,512]{1,0:T(8,128)S(1)}, f32[128,512]{1,0:T(8,128)S(1)}, u32[]{:S(2)}, u32[]{:S(2)}) %collective-permute-start.2) | collective-permute-done | bytes 262176 | tf_op jit(solution)/shard_map/ppermute | solution.py:46
  24.7 0.8 fusion.41
  25.5 0.9 copy.25
  26.4 3.9 %all-to-all-start = ((bf16[2,512,128]{2,0,1:T(2,128)(2,1)}), bf16[2,512,128]{2,0,1:T(2,128)(2,1)S(1)}, u32[]{:S(2)}, u32[]{:S(2)}) async-start(bf16[2,512,128]{2,0,1:T(2,128)(2,1)} %copy.25), calls=%async_computation | async-start | bytes 524288 | tf_op jit(solution)/shard_map/all_to_all | solution.py:224
  30.8 2.2 %maximum_select_fusion = f32[128,1024]{1,0:T(8,128)} fusion(f32[1,1024]{1,0:T(1,128)S(1)} %get-tuple-element.52, f32[127,1024]{1,0:T(8,128)} %get-tuple-element.54, f32[127,1024]{1,0:T(8,128)} %get-tuple-element.53, f32[1,1024]{1,0:T(1,128)S(1)} %get-tuple-element.51, s32[128]{0:T(128)S(1)} %get-tuple-element.81, s32[128]{0:T(128)S(1)} %get-tuple-element.82, ...), kind=kLoop, calls=%fused_computation.37 | loop fusion | flops 655360 | bytes 1574016 | tf_op jit(solution)/shard_map/jit(_where)/select_n | solution.py:167
  33.0 5.7 %all-to-all-done = bf16[2,512,128]{2,0,1:T(2,128)(2,1)S(1)} async-done(((bf16[2,512,128]{2,0,1:T(2,128)(2,1)}), bf16[2,512,128]{2,0,1:T(2,128)(2,1)S(1)}, u32[]{:S(2)}, u32[]{:S(2)}) %all-to-all-start) | async-done | bytes 262176 | tf_op jit(solution)/shard_map/all_to_all | solution.py:224
  38.9 2.9 %fusion.86 = f32[128,1024]{1,0:T(8,128)} fusion(bf16[128,512]{0,1:T(8,128)(2,1)S(1)} %bitcast.131, f32[512,1024]{1,0:T(8,128)} %bitcast.121), kind=kOutput, calls=%fused_computation.186 | convolution fusion | flops 402653184 | bytes 2752512 | tf_op jit(solution)/shard_map/dot_general | solution.py:131
  42.0 2.3 %fusion.87 = f32[128,1024]{1,0:T(8,128)S(1)} fusion(bf16[128,512]{0,1:T(8,128)(2,1)S(1)} %bitcast.132, f32[512,1024]{1,0:T(8,128)} %bitcast.122), kind=kOutput, calls=%fused_computation.187 | convolution fusion | flops 402653184 | bytes 2752512 | tf_op jit(solution)/shard_map/dot_general | solution.py:131
  45.1 1.1 %slice_add_fusion = (f32[128,512]{1,0:T(8,128)}, f32[128,512]{1,0:T(8,128)}, f32[128,512]{1,0:T(8,128)S(1)}, f32[128,512]{1,0:T(8,128)S(1)}, f32[128,512]{1,0:T(8,128)S(1)}) fusion(f32[128,512]{1,0:T(8,128)S(1)} %get-tuple-element.30, f32[128,1024]{1,0:T(8,128)S(1)} %fusion.17, f32[128,512]{1,0:T(8,128)S(1)} %get-tuple-element.31, ...), kind=kLoop, calls=%fused_computation.68 | loop fusion | flops 1245184 | bytes 3932672 | tf_op jit(solution)/shard_map/add | solution.py:174
  46.2 0.7 copy-done.2
  46.9 1.2 %fusion.5 = bf16[1,128,512]{2,1,0:T(8,128)(2,1)S(1)} fusion(f32[512,1024]{1,0:T(8,128)S(1)} %bitcast.123, f32[128,512]{1,0:T(8,128)S(1)} %get-tuple-element.70, f32[128,512]{1,0:T(8,128)S(1)} %get-tuple-element.41, f32[1024]{0:T(1024)S(1)} %fusion.70), kind=kOutput, calls=%fused_computation.15 | convolution fusion | flops 402980864 | bytes 2756608 | tf_op jit(solution)/shard_map/dot_general | solution.py:139
  48.1 1.2 %fusion.6 = bf16[1,128,512]{2,1,0:T(8,128)(2,1)S(1)} fusion(f32[512,1024]{1,0:T(8,128)S(1)} %bitcast.124, f32[128,512]{1,0:T(8,128)S(1)} %get-tuple-element.71, f32[128,512]{1,0:T(8,128)S(1)} %get-tuple-element.72, f32[1024]{0:T(1024)S(1)} %fusion.70), kind=kOutput, calls=%fused_computation.16 | convolution fusion | flops 402980864 | bytes 2756608 | tf_op jit(solution)/shard_map/dot_general | solution.py:139
  49.4 0.9 copy.29
  50.3 3.6 %all-to-all-start.1 = ((bf16[2,128,512]{1,0,2:T(2,128)(2,1)}), bf16[2,128,512]{1,0,2:T(2,128)(2,1)S(1)}, u32[]{:S(2)}, u32[]{:S(2)}) async-start(bf16[2,128,512]{1,0,2:T(2,128)(2,1)} %copy.29), calls=%async_computation.1 | async-start | bytes 524288 | tf_op jit(solution)/shard_map/all_to_all | solution.py:234
  53.9 6.7 %all-to-all-done.1 = bf16[2,128,512]{1,0,2:T(2,128)(2,1)S(1)} async-done(((bf16[2,128,512]{1,0,2:T(2,128)(2,1)}), bf16[2,128,512]{1,0,2:T(2,128)(2,1)S(1)}, u32[]{:S(2)}, u32[]{:S(2)}) %all-to-all-start.1) | async-done | bytes 262176 | tf_op jit(solution)/shard_map/all_to_all | solution.py:234
  60.9 0.7 slice_convert_fusion
  61.6 0.8 reshape.303
  62.5 1.8 %reshape.305 = f32[1,512,128]{1,2,0:T(8,128)} reshape(f32[1,4,128,128]{2,1,3,0:T(4,128)} %get-tuple-element.55) | data formatting | bytes 524288 | tf_op jit(solution)/shard_map/convert_element_type | solution.py:251
  64.2 1.1 %fusion.42 = bf16[1,512,128]{1,2,0:T(8,128)(2,1)S(1)} fusion(f32[16,8,4,128]{3,2,1,0:T(4,128)S(1)} %bitcast.126, f32[128,512]{1,0:T(8,128)} %get-tuple-element.29), kind=kLoop, calls=%fused_computation.109 | loop fusion | flops 131072 | bytes 655360 | tf_op jit(solution)/shard_map/stack | solution.py:253
  65.3 1.4 %multiply_convert_fusion.1 = (bf16[1,512,128]{1,2,0:T(8,128)(2,1)S(1)}, bf16[1,512,128]{1,2,0:T(8,128)(2,1)S(1)}, bf16[1,512,128]{1,2,0:T(8,128)(2,1)S(1)}) fusion(f32[1,512,128]{1,2,0:T(8,128)} %reshape.305, f32[3,512,128]{1,2,0:T(8,128)} %copy-done.4, f32[1,512,128]{1,2,0:T(8,128)} %reshape.303), kind=kLoop, calls=%fused_computation.81 | loop fusion | flops 393216 | bytes 1703936 | tf_op jit(solution)/shard_map/convert.4
  66.7 4.0 %fusion.3 = f32[128]{0:T(128)S(1)} fusion(f32[3,512,128]{1,2,0:T(8,128)S(1)} %copy-done.5, bf16[2048,3,512]{2,0,1:T(8,128)(2,1)} %param.10, f32[128,2048]{1,0:T(8,128)S(1)} %get-tuple-element.74, f32[2048]{0:T(1024)S(1)} %copy-done.18, f32[128]{0:T(128)S(1)} %copy-done.22, bf16[1,512,128]{1,2,0:T(8,128)(2,1)S(1)} %get-tuple-element.35, ...), kind=kOutput, calls=%fused_computation.9 | convolution fusion | flops 808058752 | bytes 8528896 | tf_op jit(solution)/shard_map/dr,dmc->mcr/dot_general | solution.py:204
  70.7 5.0 %fusion.7 = (f32[2048]{0:T(1024)S(1)}, f32[128,2048,1]{1,0,2:T(8,128)S(1)}) fusion(f32[128,2048]{1,0:T(8,128)S(1)} %get-tuple-element.74, f32[128]{0:T(128)S(1)} %copy-done.22, bf16[2048,3,512]{2,0,1:T(8,128)(2,1)} %param.10, bf16[1,512,128]{1,2,0:T(8,128)(2,1)S(1)} %get-tuple-element.35, bf16[1,512,128]{1,2,0:T(8,128)(2,1)S(1)} %get-tuple-element.34, ...), kind=kOutput, calls=%fused_computation.18 | convolution fusion | flops 806483968 | bytes 8790528 | tf_op jit(solution)/shard_map/mcr,dmc->rd/dot_general | solution.py:254
  76.4 0.7 fusion
  77.1 1.6 %collective-permute-start.6 = (f32[21,512]{1,0:T(8,128)S(1)}, f32[21,512]{1,0:T(8,128)S(1)}, u32[]{:S(2)}, u32[]{:S(2)}) collective-permute-start(f32[21,512]{1,0:T(8,128)S(1)} %get-tuple-element.61), channel_id=1, source_target_pairs={{0,2},{1,3},{2,0},{3,1},{4,6},{5,7},{6,4},{7,5},{8,10},{9,11},{10,... | collective-permute-start | bytes 129032 | tf_op jit(solution)/shard_map/ppermute | solution.py:90
  78.7 0.6 collective-permute-start.5
  79.6 1.6 %collective-permute-start.3 = (bf16[1,512,128]{1,2,0:T(8,128)(2,1)S(1)}, bf16[1,512,128]{1,2,0:T(8,128)(2,1)S(1)}, u32[]{:S(2)}, u32[]{:S(2)}) collective-permute-start(bf16[1,512,128]{1,2,0:T(8,128)(2,1)S(1)} %get-tuple-element.40), channel_id=1, source_target_pairs={{0,2},{2,0},{1,3},{3,1},{4,6},{6,4},{5,7},{7,5},{8,10},{10,8},{9,1... | collective-permute-start | bytes 393224 | tf_op jit(solution)/shard_map/ppermute | solution.py:46
  81.3 1.1 %collective-permute-done.7 = f32[21,512]{1,0:T(8,128)S(1)} collective-permute-done((f32[21,512]{1,0:T(8,128)S(1)}, f32[21,512]{1,0:T(8,128)S(1)}, u32[]{:S(2)}, u32[]{:S(2)}) %collective-permute-start.7) | collective-permute-done | bytes 43040 | tf_op jit(solution)/shard_map/ppermute | solution.py:90
  82.4 1.3 %collective-permute-start.10 = (f32[21,512]{1,0:T(8,128)S(1)}, f32[21,512]{1,0:T(8,128)S(1)}, u32[]{:S(2)}, u32[]{:S(2)}) collective-permute-start(f32[21,512]{1,0:T(8,128)S(1)} %pad_add_fusion), channel_id=1, source_target_pairs={{0,4},{4,0},{8,12},{12,8},{1,5},{5,1},{9,13},{13,9},{2,6},{6,2},{1... | collective-permute-start | bytes 129032 | tf_op jit(solution)/shard_map/ppermute | solution.py:90
  83.7 0.8 collective-permute-start.8
  84.5 1.5 %collective-permute-start.9 = (f32[21,512]{1,0:T(8,128)S(1)}, f32[21,512]{1,0:T(8,128)S(1)}, u32[]{:S(2)}, u32[]{:S(2)}) collective-permute-start(f32[21,512]{1,0:T(8,128)S(1)} %pad_add_fusion), channel_id=1, source_target_pairs={{0,8},{4,12},{8,0},{12,4},{1,9},{5,13},{9,1},{13,5},{2,10},{6,14},... | collective-permute-start | bytes 129032 | tf_op jit(solution)/shard_map/ppermute | solution.py:90
  86.0 0.7 maximum_bitcast_fusion
  86.7 1.9 %convolution_bitcast_fusion.3 = f32[1,1,128,512]{3,2,1,0:T(8,128)} fusion(f32[512,1024]{1,0:T(8,128)S(1)} %bitcast.125, f32[128,512]{1,0:T(8,128)S(1)} %copy-done.14, f32[128,512]{1,0:T(8,128)S(1)} %copy-done.13, f32[1024]{0:T(1024)S(1)} %fusion.70), kind=kOutput, calls=%fused_computation.10 | convolution fusion | flops 402915328 | bytes 2887680 | tf_op jit(solution)/shard_map/dot_general | solution.py:139
  88.6 1.0 collective-permute-done.8
  89.6 1.5 %collective-permute-done.9 = f32[21,512]{1,0:T(8,128)S(1)} collective-permute-done((f32[21,512]{1,0:T(8,128)S(1)}, f32[21,512]{1,0:T(8,128)S(1)}, u32[]{:S(2)}, u32[]{:S(2)}) %collective-permute-start.9) | collective-permute-done | bytes 43040 | tf_op jit(solution)/shard_map/ppermute | solution.py:90
  92.4 1.0 %broadcast_select_fusion.1 = (bf16[2,1,512,128]{2,3,0,1:T(8,128)(2,1)S(1)}, bf16[2,1,512,128]{2,3,0,1:T(8,128)(2,1)S(1)}) fusion(bf16[2,1,512,128]{2,3,0,1:T(8,128)(2,1)} %collective-permute-done.4, pred[]{:T(512)S(6)} %eq.200, bf16[1,512,128]{1,2,0:T(8,128)(2,1)S(1)} %get-tuple-element.58, bf16[1,512,128]{1,2,0:T(8,128)(2,1)S(1)} %get-tuple-element.57), kind=kLoop, calls=%fused_computation.94 | loop fusion | flops 393216 | bytes 1048577 | tf_op jit(solution)/shard_map/jit(_where)/select_n | solution.py:70
  93.4 0.9 pad_maximum_fusion.3
  94.2 2.1 %copy.31 = bf16[2,2,512,128]{3,2,1,0:T(8,128)(2,1)} copy(bf16[2,2,512,128]{2,3,0,1:T(8,128)(2,1)} %pad_maximum_fusion.3) | data formatting | bytes 1048576 | tf_op jit(solution)/shard_map/concatenate | solution.py:69
  96.3 2.2 %fusion.4 = bf16[128,512]{1,0:T(8,128)(2,1)} fusion(bf16[2048,128]{1,0:T(8,128)(2,1)} %bitcast.127, bf16[2048,512]{1,0:T(8,128)(2,1)S(1)} %copy-done, f32[128,2048]{1,0:T(8,128)S(1)} %get-tuple-element.74, s32[]{:T(128)S(6)} %select_n.402), kind=kOutput, calls=%fused_computation.12 | convolution fusion | flops 268566528 | bytes 3014660 | tf_op jit(solution)/shard_map/cr,cd->rd/dot_general | solution.py:240
  (124 shorter events, 7.1 us)
Async XLA Ops:
  0.6 1.6 %copy-start = (bf16[2048,512]{1,0:T(8,128)(2,1)S(1)}, bf16[2048,512]{1,0:T(8,128)(2,1)}, u32[]{:S(2)}) copy-start(bf16[2048,512]{1,0:T(8,128)(2,1)} %param.12) | copy-start | bytes 6291460
  3.9 2.2 %copy-start.34 = (s32[128]{0:T(128)S(1)}, s32[128]{0:T(128)}, u32[]{:S(2)}) copy-start(s32[128]{0:T(128)} %param.7) | copy-start | bytes 1540
  4.0 0.7 copy-start.9
  4.1 1.6 %copy-start.10 = (f32[128,512]{1,0:T(8,128)}, f32[128,512]{1,0:T(8,128)S(1)}, u32[]{:S(2)}) copy-start(f32[128,512]{1,0:T(8,128)S(1)} %get-tuple-element.38) | copy-start | bytes 786436
  4.1 2.1 %copy-start.11 = (f32[128,512]{1,0:T(8,128)}, f32[128,512]{1,0:T(8,128)S(1)}, u32[]{:S(2)}) copy-start(f32[128,512]{1,0:T(8,128)S(1)} %get-tuple-element.39) | copy-start | bytes 786436
  4.7 7.3 %copy-start.16 = (f32[1,1,128,512]{3,2,1,0:T(8,128)S(1)}, f32[1,1,128,512]{3,2,1,0:T(8,128)}, u32[]{:S(2)}) copy-start(f32[1,1,128,512]{3,2,1,0:T(8,128)} %param.11) | copy-start | bytes 786436
  5.6 9.2 %collective-permute-start.1 = (f32[128,1024]{1,0:T(8,128)}, f32[128,1024]{1,0:T(8,128)}, u32[]{:S(2)}, u32[]{:S(2)}) collective-permute-start(f32[128,1024]{1,0:T(8,128)} %fusion.29), channel_id=1, source_target_pairs={{0,1},{1,0},{2,3},{3,2},{4,5},{5,4},{6,7},{7,6},{8,9},{9,8},{10,11... | collective-permute-start | bytes 1572872 | tf_op jit(solution)/shard_map/ppermute | solution.py:46
  6.2 7.9 %collective-permute-start = (s32[3]{0:T(128)S(1)}, s32[3]{0:T(128)S(1)}, u32[]{:S(2)}, u32[]{:S(2)}) collective-permute-start(s32[3]{0:T(128)S(1)} %slice_add_fusion.2), channel_id=1, source_target_pairs={{0,4},{4,8},{8,12},{1,5},{5,9},{9,13},{2,6},{6,10},{10,14},{3,7},{... | collective-permute-start | bytes 44 | tf_op jit(solution)/shard_map/ppermute | solution.py:16
  10.7 3.6 %copy-start.23 = (pred[128,5]{0,1:T(8,128)(4,1)}, pred[128,5]{0,1:T(8,128)(4,1)S(1)}, u32[]{:S(2)}) copy-start(pred[128,5]{0,1:T(8,128)(4,1)S(1)} %iota_compare_fusion.5) | copy-start | bytes 1924
  12.0 1.9 %copy-start.1 = (f32[16,32,1024]{2,1,0:T(8,128)}, f32[16,32,1024]{2,1,0:T(8,128)S(1)}, u32[]{:S(2)}) copy-start(f32[16,32,1024]{2,1,0:T(8,128)S(1)} %multiply_subtract_fusion) | copy-start | bytes 6291460
  12.0 2.0 %copy-start.17 = (bf16[4,5,2048]{2,0,1:T(4,128)(2,1)S(1)}, bf16[4,5,2048]{2,0,1:T(4,128)(2,1)}, u32[]{:S(2)}) copy-start(bf16[4,5,2048]{2,0,1:T(4,128)(2,1)} %param.8) | copy-start | bytes 245764
  12.8 1.6 %copy-start.6 = (f32[128,1024]{1,0:T(8,128)}, f32[128,1024]{1,0:T(8,128)S(1)}, u32[]{:S(2)}) copy-start(f32[128,1024]{1,0:T(8,128)S(1)} %convolution_bitcast_fusion.2) | copy-start | bytes 1572868
  14.0 16.8 %copy-start.27 = (s32[128]{0:T(128)}, s32[128]{0:T(128)S(1)}, u32[]{:S(2)}) copy-start(s32[128]{0:T(128)S(1)} %get-tuple-element.81) | copy-start | bytes 1540
  14.0 16.8 %copy-start.29 = (s32[128]{0:T(128)}, s32[128]{0:T(128)S(1)}, u32[]{:S(2)}) copy-start(s32[128]{0:T(128)S(1)} %get-tuple-element.82) | copy-start | bytes 1540
  14.0 16.8 %copy-start.31 = (pred[128]{0:T(512)(128)(4,1)}, pred[128]{0:T(512)(128)(4,1)S(1)}, u32[]{:S(2)}) copy-start(pred[128]{0:T(512)(128)(4,1)S(1)} %compare_and_fusion) | copy-start | bytes 388
  14.1 3.7 %copy-start.18 = (f32[2048]{0:T(1024)S(1)}, f32[2048]{0:T(1024)}, u32[]{:S(2)}) copy-start(f32[2048]{0:T(1024)} %param.9) | copy-start | bytes 24580
  14.3 7.3 %copy-start.19 = (pred[128,5]{0,1:T(8,128)(4,1)}, pred[128,5]{0,1:T(8,128)(4,1)S(1)}, u32[]{:S(2)}) copy-start(pred[128,5]{0,1:T(8,128)(4,1)S(1)} %get-tuple-element.80) | copy-start | bytes 1924
  14.3 7.3 %copy-start.25 = (pred[128,5]{0,1:T(8,128)(4,1)}, pred[128,5]{0,1:T(8,128)(4,1)S(1)}, u32[]{:S(2)}) copy-start(pred[128,5]{0,1:T(8,128)(4,1)S(1)} %iota_compare_fusion.4) | copy-start | bytes 1924
  14.8 6.8 %copy-start.21 = (f32[128]{0:T(128)}, f32[128]{0:T(128)S(1)}, u32[]{:S(2)}) copy-start(f32[128]{0:T(128)S(1)} %add_rsqrt_fusion) | copy-start | bytes 1540
  16.2 8.5 %collective-permute-start.2 = (f32[128,512]{1,0:T(8,128)S(1)}, f32[128,512]{1,0:T(8,128)S(1)}, u32[]{:S(2)}, u32[]{:S(2)}) collective-permute-start(f32[128,512]{1,0:T(8,128)S(1)} %slice_select_fusion), channel_id=1, source_target_pairs={{0,2},{2,0},{1,3},{3,1},{4,6},{6,4},{5,7},{7,5},{8,10},{10,8},{9,1... | collective-permute-start | bytes 786440 | tf_op jit(solution)/shard_map/ppermute | solution.py:46
  21.6 3.1 %copy-start.4 = (f32[3,512,128]{1,2,0:T(8,128)}, f32[3,512,128]{1,2,0:T(8,128)S(1)}, u32[]{:S(2)}) copy-start(f32[3,512,128]{1,2,0:T(8,128)S(1)} %convolution_bitcast_fusion.1) | copy-start | bytes 2359300
  26.4 12.3 %all-to-all-start = ((bf16[2,512,128]{2,0,1:T(2,128)(2,1)}), bf16[2,512,128]{2,0,1:T(2,128)(2,1)S(1)}, u32[]{:S(2)}, u32[]{:S(2)}) async-start(bf16[2,512,128]{2,0,1:T(2,128)(2,1)} %copy.25), calls=%async_computation | async-start | bytes 524288 | tf_op jit(solution)/shard_map/all_to_all | solution.py:224
  41.8 2.4 %copy-start.33 = (pred[512]{0:T(512)(128)(4,1)S(1)}, pred[512]{0:T(512)(128)(4,1)}, u32[]{:S(2)}) copy-start(pred[512]{0:T(512)(128)(4,1)} %iota_compare_fusion.6) | copy-start | bytes 1540
  42.0 2.3 %copy-start.7 = (f32[128,1024]{1,0:T(8,128)S(1)}, f32[128,1024]{1,0:T(8,128)}, u32[]{:S(2)}) copy-start(f32[128,1024]{1,0:T(8,128)} %copy-done.6) | copy-start | bytes 1572868
  42.0 2.3 %copy-start.8 = (f32[128,1024]{1,0:T(8,128)S(1)}, f32[128,1024]{1,0:T(8,128)}, u32[]{:S(2)}) copy-start(f32[128,1024]{1,0:T(8,128)} %fusion.86) | copy-start | bytes 1572868
  42.0 2.3 %copy-start.12 = (f32[128,1024]{1,0:T(8,128)S(1)}, f32[128,1024]{1,0:T(8,128)}, u32[]{:S(2)}) copy-start(f32[128,1024]{1,0:T(8,128)} %maximum_select_fusion) | copy-start | bytes 1572868
  44.3 0.6 copy-start.28
  44.3 0.7 copy-start.30
  44.3 0.7 copy-start.32
  45.1 1.8 %copy-start.2 = (f32[16,32,1024]{2,1,0:T(8,128)S(1)}, f32[16,32,1024]{2,1,0:T(8,128)}, u32[]{:S(2)}) copy-start(f32[16,32,1024]{2,1,0:T(8,128)} %copy-done.1) | copy-start | bytes 6291460
  50.3 10.4 %all-to-all-start.1 = ((bf16[2,128,512]{1,0,2:T(2,128)(2,1)}), bf16[2,128,512]{1,0,2:T(2,128)(2,1)S(1)}, u32[]{:S(2)}, u32[]{:S(2)}) async-start(bf16[2,128,512]{1,0,2:T(2,128)(2,1)} %copy.29), calls=%async_computation.1 | async-start | bytes 524288 | tf_op jit(solution)/shard_map/all_to_all | solution.py:234
  60.9 5.8 %copy-start.22 = (f32[128]{0:T(128)S(1)}, f32[128]{0:T(128)}, u32[]{:S(2)}) copy-start(f32[128]{0:T(128)} %copy-done.21) | copy-start | bytes 1540
  64.2 2.5 %copy-start.5 = (f32[3,512,128]{1,2,0:T(8,128)S(1)}, f32[3,512,128]{1,2,0:T(8,128)}, u32[]{:S(2)}) copy-start(f32[3,512,128]{1,2,0:T(8,128)} %copy-done.4) | copy-start | bytes 2359300
  70.6 5.0 %copy-start.20 = (pred[128,5]{0,1:T(8,128)(4,1)S(1)}, pred[128,5]{0,1:T(8,128)(4,1)}, u32[]{:S(2)}) copy-start(pred[128,5]{0,1:T(8,128)(4,1)} %copy-done.19) | copy-start | bytes 1924
  70.7 5.0 %copy-start.24 = (pred[128,5]{0,1:T(8,128)(4,1)S(1)}, pred[128,5]{0,1:T(8,128)(4,1)}, u32[]{:S(2)}) copy-start(pred[128,5]{0,1:T(8,128)(4,1)} %copy-done.23) | copy-start | bytes 1924
  70.7 5.0 %copy-start.26 = (pred[128,5]{0,1:T(8,128)(4,1)S(1)}, pred[128,5]{0,1:T(8,128)(4,1)}, u32[]{:S(2)}) copy-start(pred[128,5]{0,1:T(8,128)(4,1)} %copy-done.25) | copy-start | bytes 1924
  75.7 3.7 %copy-start.15 = (bf16[128,512]{1,0:T(8,128)(2,1)S(1)}, bf16[128,512]{1,0:T(8,128)(2,1)}, u32[]{:S(2)}) copy-start(bf16[128,512]{1,0:T(8,128)(2,1)} %param.13) | copy-start | bytes 393220
  76.3 10.4 %copy-start.3 = (f32[16,32,1024]{2,1,0:T(8,128)S(1)}, f32[16,32,1024]{2,1,0:T(8,128)}, u32[]{:S(2)}) copy-start(f32[16,32,1024]{2,1,0:T(8,128)} %copy-done.1) | copy-start | bytes 6291460
  76.3 10.4 %copy-start.13 = (f32[128,512]{1,0:T(8,128)S(1)}, f32[128,512]{1,0:T(8,128)}, u32[]{:S(2)}) copy-start(f32[128,512]{1,0:T(8,128)} %get-tuple-element.45) | copy-start | bytes 786436
  76.3 10.4 %copy-start.14 = (f32[128,512]{1,0:T(8,128)S(1)}, f32[128,512]{1,0:T(8,128)}, u32[]{:S(2)}) copy-start(f32[128,512]{1,0:T(8,128)} %get-tuple-element.46) | copy-start | bytes 786436
  77.1 4.2 %collective-permute-start.6 = (f32[21,512]{1,0:T(8,128)S(1)}, f32[21,512]{1,0:T(8,128)S(1)}, u32[]{:S(2)}, u32[]{:S(2)}) collective-permute-start(f32[21,512]{1,0:T(8,128)S(1)} %get-tuple-element.61), channel_id=1, source_target_pairs={{0,2},{1,3},{2,0},{3,1},{4,6},{5,7},{6,4},{7,5},{8,10},{9,11},{10,... | collective-permute-start | bytes 129032 | tf_op jit(solution)/shard_map/ppermute | solution.py:90
  78.7 3.7 %collective-permute-start.7 = (f32[21,512]{1,0:T(8,128)S(1)}, f32[21,512]{1,0:T(8,128)S(1)}, u32[]{:S(2)}, u32[]{:S(2)}) collective-permute-start(f32[21,512]{1,0:T(8,128)S(1)} %get-tuple-element.62), channel_id=1, source_target_pairs={{0,3},{1,2},{2,1},{3,0},{4,7},{5,6},{6,5},{7,4},{8,11},{9,10},{10,... | collective-permute-start | bytes 129032 | tf_op jit(solution)/shard_map/ppermute | solution.py:90
  78.7 3.7 %collective-permute-start.5 = (f32[21,512]{1,0:T(8,128)S(1)}, f32[21,512]{1,0:T(8,128)S(1)}, u32[]{:S(2)}, u32[]{:S(2)}) collective-permute-start(f32[21,512]{1,0:T(8,128)S(1)} %get-tuple-element.20), channel_id=1, source_target_pairs={{0,1},{1,0},{2,3},{3,2},{4,5},{5,4},{6,7},{7,6},{8,9},{9,8},{10,11... | collective-permute-start | bytes 129032 | tf_op jit(solution)/shard_map/ppermute | solution.py:90
  79.6 6.4 %collective-permute-start.3 = (bf16[1,512,128]{1,2,0:T(8,128)(2,1)S(1)}, bf16[1,512,128]{1,2,0:T(8,128)(2,1)S(1)}, u32[]{:S(2)}, u32[]{:S(2)}) collective-permute-start(bf16[1,512,128]{1,2,0:T(8,128)(2,1)S(1)} %get-tuple-element.40), channel_id=1, source_target_pairs={{0,2},{2,0},{1,3},{3,1},{4,6},{6,4},{5,7},{7,5},{8,10},{10,8},{9,1... | collective-permute-start | bytes 393224 | tf_op jit(solution)/shard_map/ppermute | solution.py:46
  82.4 6.2 %collective-permute-start.10 = (f32[21,512]{1,0:T(8,128)S(1)}, f32[21,512]{1,0:T(8,128)S(1)}, u32[]{:S(2)}, u32[]{:S(2)}) collective-permute-start(f32[21,512]{1,0:T(8,128)S(1)} %pad_add_fusion), channel_id=1, source_target_pairs={{0,4},{4,0},{8,12},{12,8},{1,5},{5,1},{9,13},{13,9},{2,6},{6,2},{1... | collective-permute-start | bytes 129032 | tf_op jit(solution)/shard_map/ppermute | solution.py:90
  83.7 5.9 %collective-permute-start.8 = (f32[21,512]{1,0:T(8,128)S(1)}, f32[21,512]{1,0:T(8,128)S(1)}, u32[]{:S(2)}, u32[]{:S(2)}) collective-permute-start(f32[21,512]{1,0:T(8,128)S(1)} %pad_add_fusion), channel_id=1, source_target_pairs={{0,12},{4,8},{8,4},{12,0},{1,13},{5,9},{9,5},{13,1},{2,14},{6,10},... | collective-permute-start | bytes 129032 | tf_op jit(solution)/shard_map/ppermute | solution.py:90
  84.5 6.6 %collective-permute-start.9 = (f32[21,512]{1,0:T(8,128)S(1)}, f32[21,512]{1,0:T(8,128)S(1)}, u32[]{:S(2)}, u32[]{:S(2)}) collective-permute-start(f32[21,512]{1,0:T(8,128)S(1)} %pad_add_fusion), channel_id=1, source_target_pairs={{0,8},{4,12},{8,0},{12,4},{1,9},{5,13},{9,1},{13,5},{2,10},{6,14},... | collective-permute-start | bytes 129032 | tf_op jit(solution)/shard_map/ppermute | solution.py:90
  86.7 5.7 %collective-permute-start.4 = (bf16[2,1,512,128]{2,3,0,1:T(8,128)(2,1)}, bf16[2,1,512,128]{2,3,0,1:T(8,128)(2,1)}, u32[]{:S(2)}, u32[]{:S(2)}) collective-permute-start(bf16[2,1,512,128]{2,3,0,1:T(8,128)(2,1)} %maximum_bitcast_fusion), channel_id=1, source_target_pairs={{0,1},{1,0},{2,3},{3,2},{4,5},{5,4},{6,7},{7,6},{8,9},{9,8},{10,11... | collective-permute-start | bytes 786440 | tf_op jit(solution)/shard_map/ppermute | solution.py:46

commit v4 on v3

--- a/solution.py
+++ b/solution.py
@@ -125,6 +125,32 @@
             piece = jnp.where((me ^ source) == offset, got[offset], piece)
         total = piece if total is None else total + piece
     return total
+
+
+def all_to_all_seq(x, split_axis, concat_axis):
+    count = lax.axis_size("seq")
+    if count > 4:
+        return lax.all_to_all(x, "seq", split_axis=split_axis, concat_axis=concat_axis, tiled=True)
+    me = lax.axis_index("seq")
+    width = x.shape[split_axis] // count
+    blocks = [lax.slice_in_dim(x, j * width, (j + 1) * width, axis=split_axis) for j in range(count)]
+
+    def pick(index):
+        out = blocks[0]
+        for j in range(1, count):
+            out = jnp.where(index == j, blocks[j], out)
+        return out
+
+    got = [pick(me)] + [
+        group_exchange(pick(me ^ offset), "seq", count, offset) for offset in range(1, count)
+    ]
+    pieces = []
+    for source in range(count):
+        piece = got[0]
+        for offset in range(1, count):
+            piece = jnp.where((me ^ source) == offset, got[offset], piece)
+        pieces.append(piece)
+    return jnp.concatenate(pieces, axis=concat_axis)
 
 
 def forward_dft(signal, dft):
@@ -221,9 +247,7 @@
     spec_g = add_conj_flip(forward_dft(filter_rows, dft))
     ga, gb = halves(spec_g)
     d_conv = (d_gated * query_part).astype(jnp.bfloat16)
-    both_cols = lax.all_to_all(
-        jnp.stack([mixed_in, d_conv]), "seq", split_axis=1, concat_axis=2, tiled=True
-    )
+    both_cols = all_to_all_seq(jnp.stack([mixed_in, d_conv]), 1, 2)
     mixed_cols, d_cols = both_cols[0], both_cols[1]
     spec_s = forward_dft(mixed_cols, dft)
     sa, sb = halves(spec_s)
@@ -231,9 +255,7 @@
     spec_d = forward_dft(d_cols, dft)
     da, db = halves(spec_d)
     d_mixed_cols = inverse_dft(cmul(ga, gb, da, db, True), dft).astype(jnp.bfloat16)
-    both_rows = lax.all_to_all(
-        jnp.stack([conv_cols, d_mixed_cols]), "seq", split_axis=2, concat_axis=1, tiled=True
-    )
+    both_rows = all_to_all_seq(jnp.stack([conv_cols, d_mixed_cols]), 2, 1)
     conv_rows, d_mixed = both_rows[0], both_rows[1]
     gated_rows = (query_part * conv_rows.astype(jnp.float32)).astype(jnp.bfloat16)
     weight_rows = out_proj

time: 99.2 us -> 78.1 us (0.79)
  matrix products: 28.8 us -> 19.8 us
  waiting for transfers between devices: 19.2 us -> 12.2 us
  local copies, waits for them, and re-layouts: 12.9 us -> 8.17 us
  other arithmetic: 14.8 us -> 11.9 us
  starting transfers between devices: 21.3 us -> 24.2 us
    all_to_all x2 -> x0, waiting for transfers between devices: 12.4 us -> none  [the longest x1 6.73 us: per_device(): lax.all_to_all(jnp.stack([conv_cols, d_mixed_cols]), 'seq', split_axis=2,...]
    ppermute x6 -> x12, starting transfers between devices: 5.76 us -> 15.6 us  [group_exchange(): return lax.ppermute(x, axes, [(i, i ^ offset) for i in range(count)])]
    all_to_all x2 -> x0, starting transfers between devices: 7.44 us -> none  [the longest x1 3.86 us: per_device(): lax.all_to_all(jnp.stack([mixed_in, d_conv]), 'seq', split_axis=1, concat...]
    ppermute x6 -> x12, waiting for transfers between devices: 3.71 us -> 9.17 us  [group_exchange(): return lax.ppermute(x, axes, [(i, i ^ offset) for i in range(count)])]
    dot_general x3, matrix products: 5.9 us -> 1.83 us  [forward_dft(): jnp.dot(signal.astype(jnp.float32), dft, precision=TRANSFORM_PRECISION)]
    dot_general x1, matrix products: 4.97 us -> 2.18 us  [per_device(): jnp.einsum('mcr,dmc->rd', d_proj, in_proj, preferred_element_type=jnp.flo...]
    dot_general x1, matrix products: 3.95 us -> 1.25 us  [per_device(): jnp.einsum('dr,dmc->mcr', residual, in_proj, preferred_element_type=jnp.f...]
    convert_element_type x2 -> x0, local copies, waits for them, and re-layouts: 2.59 us -> none  [the longest x1 1.76 us: per_device(): d_key = d_mixed.astype(jnp.float32) * value_part]
  transfers between devices with their start and end apart: 13 -> 17, of which waited for: 7 -> 8; matrix products, arithmetic and copies ran while one was open for 15% -> 23% of each run, Pallas kernels for 0% -> 0%
where the time goes in v4:
time: 78.1 us; the launch traced here: 77.6 us
  starting transfers between devices  24.2 us (31%)
  matrix products  19.8 us (25%)
  waiting for transfers between devices  12.2 us (16%)
  other arithmetic  11.9 us (15%)
  local copies, waits for them, and re-layouts  8.17 us (10%)
  between operations  1.18 us (2%)
    ppermute x12, starting transfers between devices, group_exchange(): return lax.ppermute(x, axes, [(i, i ^ offset) for i in range(count)])  15.6 us
    ppermute x12, waiting for transfers between devices, group_exchange(): return lax.ppermute(x, axes, [(i, i ^ offset) for i in range(count)])  9.17 us
    ppermute x1, starting transfers between devices, from_behind(): lax.ppermute(value, axis, [(source, source + steps) for source in range(f...  5.03 us
    unnamed x38, local copies, waits for them, and re-layouts  4.59 us
    dot_general x3, matrix products, inverse_dft(): lax.dot_general(spec * weight, dft, (((1,), (1,)), ((), ())), precision=T...  3.99 us
    dot_general x1, matrix products, per_device(): jnp.einsum('dr,dmc->mcr', hidden, in_proj, preferred_element_type=jnp.flo...  3.82 us
    ppermute x4, starting transfers between devices, xor_exchange(): return lax.ppermute(x, axis, [(i, i ^ step) for i in range(count)])  3.62 us
    ppermute x4, waiting for transfers between devices, xor_exchange(): return lax.ppermute(x, axis, [(i, i ^ step) for i in range(count)])  3.04 us
  transfers between devices with their start and end apart: 17, of which 8 were waited for; matrix products, arithmetic and copies ran while one was open for 23% of the time, Pallas kernels for 0%

profile of v4, /device:TPU:0, one launch (start us, length us, event | category | flops | bytes accessed | tf_op | source)
XLA Modules:
  0.0 77.6 jit_solution(18305290317150657136)
XLA Ops:
  0.7 1.6 %copy-done = bf16[2048,512]{1,0:T(8,128)(2,1)S(1)} copy-done((bf16[2048,512]{1,0:T(8,128)(2,1)S(1)}, bf16[2048,512]{1,0:T(8,128)(2,1)}, u32[]{:S(2)}) %copy-start) | copy-done | bytes 2097176
  2.2 1.7 %fusion.102 = f32[128,2048]{1,0:T(8,128)S(1)} fusion(bf16[128,512]{1,0:T(8,128)(2,1)} %param.13, bf16[2048,512]{1,0:T(8,128)(2,1)S(1)} %copy-done), kind=kOutput, calls=%fused_computation.225 | convolution fusion | flops 268435456 | bytes 3276800 | tf_op jit(solution)/shard_map/rd,cd->rc/dot_general | solution.py:239
  4.1 0.7 copy-done.5
  4.8 0.8 %fusion.29 = f32[128,1024]{1,0:T(8,128)} fusion(f32[128,512]{1,0:T(8,128)S(1)} %get-tuple-element.48, f32[128,512]{1,0:T(8,128)S(1)} %get-tuple-element.49, f32[128,512]{1,0:T(8,128)S(1)} %get-tuple-element.50, f32[128,512]{1,0:T(8,128)S(1)} %get-tuple-element.47, pred[]{:T(512)S(6)} %eq.248), kind=kLoop, calls=%fused_computation.57 | loop fusion | flops 393216 | bytes 1572865 | tf_op jit(solution)/shard_map/jit(_where)/select_n | solution.py:57
  6.1 0.6 slice_add_fusion.2
  6.7 5.0 %collective-permute-start = (s32[3]{0:T(128)}, s32[3]{0:T(128)}, u32[]{:S(2)}, u32[]{:S(2)}) collective-permute-start(s32[3]{0:T(128)} %slice_add_fusion.2), channel_id=1, source_target_pairs={{0,4},{4,8},{8,12},{1,5},{5,9},{9,13},{2,6},{6,10},{10,14},{3,7},{... | collective-permute-start | bytes 44 | tf_op jit(solution)/shard_map/ppermute | solution.py:16
  12.1 0.6 fusion.62
  13.0 0.7 convolution_bitcast_fusion.2
  14.5 0.6 iota_and_fusion.1
  16.2 0.9 %copy.19 = bf16[4,5,2048]{2,1,0:T(8,128)(2,1)S(1)} copy(bf16[4,5,2048]{2,0,1:T(4,128)(2,1)} %param.8) | data formatting | bytes 163840 | tf_op args[1]
  17.1 0.7 reshape.265
  17.8 0.8 %maximum_select_fusion = f32[128,1024]{1,0:T(8,128)S(1)} fusion(f32[1,1024]{1,0:T(1,128)S(1)} %get-tuple-element.61, f32[127,1024]{1,0:T(8,128)S(1)} %get-tuple-element.63, f32[127,1024]{1,0:T(8,128)S(1)} %get-tuple-element.62, f32[1,1024]{1,0:T(1,128)S(1)} %get-tuple-element.60, s32[128]{0:T(128)} %get-tuple-element.93, s32[128]{0:T(128)} %get-tuple-element.94, ...), kind=kLoop, calls=%fused_computation.37 | loop fusion | flops 655360 | bytes 1574016 | tf_op jit(solution)/shard_map/jit(_where)/select_n | solution.py:193
  18.6 0.7 broadcast_add_fusion.1
  19.3 0.7 pad_add_fusion.2
  20.1 1.3 %multiply_reduce_fusion = (f32[128]{0:T(128)S(1)}, f32[128,2048]{1,0:T(8,128)S(1)}) fusion(bf16[20,2048]{1,0:T(8,128)(2,1)} %reshape.265, pred[128,5]{0,1:T(8,128)(4,1)S(1)} %get-tuple-element.89, pred[128,5]{0,1:T(8,128)(4,1)S(1)} %get-tuple-element.90, pred[128,5]{0,1:T(8,128)(4,1)S(1)} %iota_compare_fusion.4, pred[128,5]{0,1:T(8,128)(4,1)S(1)} %iota_compare_fusion.5), kind=kOutput, calls=%fused_computation.22 | convolution fusion | flops 11017600 | bytes 1133568 | tf_op jit(solution)/shard_map/dot_general | solution.py:223
  21.5 1.4 %select_add_fusion = f32[128,1024]{1,0:T(8,128)S(1)} fusion(f32[128,1024]{1,0:T(8,128)} %collective-permute-done.1, f32[128,512]{1,0:T(8,128)} %copy-done.5, f32[128,512]{1,0:T(8,128)} %copy-done.6, f32[128,512]{1,0:T(8,128)} %copy-done.7, f32[128,512]{1,0:T(8,128)S(1)} %get-tuple-element.47, pred[]{:T(512)S(6)} %eq.248), kind=kLoop, calls=%fused_computation.50 | loop fusion | flops 524288 | bytes 2097153 | tf_op jit(solution)/shard_map/add | solution.py:58
  22.9 1.6 %collective-permute-start.2 = (f32[128,512]{1,0:T(8,128)S(1)}, f32[128,512]{1,0:T(8,128)S(1)}, u32[]{:S(2)}, u32[]{:S(2)}) collective-permute-start(f32[128,512]{1,0:T(8,128)S(1)} %slice_select_fusion), channel_id=1, source_target_pairs={{0,2},{2,0},{1,3},{3,1},{4,6},{6,4},{5,7},{7,5},{8,10},{10,8},{9,1... | collective-permute-start | bytes 786440 | tf_op jit(solution)/shard_map/ppermute | solution.py:46
  24.5 3.8 %convolution_bitcast_fusion.1 = f32[3,512,128]{1,2,0:T(8,128)S(1)} fusion(bf16[2048,3,512]{2,0,1:T(8,128)(2,1)} %param.10, f32[128,2048]{1,0:T(8,128)S(1)} %get-tuple-element.86, f32[2048]{0:T(1024)S(1)} %copy-done.10, f32[128]{0:T(128)S(1)} %add_rsqrt_fusion), kind=kOutput, calls=%fused_computation.5 | convolution fusion | flops 806092800 | bytes 8135168 | tf_op jit(solution)/shard_map/dr,dmc->mcr/dot_general | solution.py:228
  28.4 3.0 %collective-permute-done.2 = f32[128,512]{1,0:T(8,128)S(1)} collective-permute-done((f32[128,512]{1,0:T(8,128)S(1)}, f32[128,512]{1,0:T(8,128)S(1)}, u32[]{:S(2)}, u32[]{:S(2)}) %collective-permute-start.2) | collective-permute-done | bytes 262176 | tf_op jit(solution)/shard_map/ppermute | solution.py:46
  31.6 1.2 %collective-permute-start.3 = (bf16[2,128,128]{1,2,0:T(8,128)(2,1)S(1)}, bf16[2,128,128]{1,2,0:T(8,128)(2,1)S(1)}, u32[]{:S(2)}, u32[]{:S(2)}) collective-permute-start(bf16[2,128,128]{1,2,0:T(8,128)(2,1)S(1)} %get-tuple-element.75), channel_id=1, source_target_pairs={{0,12},{4,8},{8,4},{12,0},{1,13},{5,9},{9,5},{13,1},{2,14},{6,10},... | collective-permute-start | bytes 196616 | tf_op jit(solution)/shard_map/ppermute | solution.py:90
  32.8 1.4 %collective-permute-start.4 = (bf16[2,128,128]{1,2,0:T(8,128)(2,1)S(1)}, bf16[2,128,128]{1,2,0:T(8,128)(2,1)S(1)}, u32[]{:S(2)}, u32[]{:S(2)}) collective-permute-start(bf16[2,128,128]{1,2,0:T(8,128)(2,1)S(1)} %get-tuple-element.74), channel_id=1, source_target_pairs={{0,8},{4,12},{8,0},{12,4},{1,9},{5,13},{9,1},{13,5},{2,10},{6,14},... | collective-permute-start | bytes 196616 | tf_op jit(solution)/shard_map/ppermute | solution.py:90
  34.2 1.8 %collective-permute-start.5 = (bf16[2,128,128]{1,2,0:T(8,128)(2,1)S(1)}, bf16[2,128,128]{1,2,0:T(8,128)(2,1)S(1)}, u32[]{:S(2)}, u32[]{:S(2)}) collective-permute-start(bf16[2,128,128]{1,2,0:T(8,128)(2,1)S(1)} %get-tuple-element.33), channel_id=1, source_target_pairs={{0,4},{4,0},{8,12},{12,8},{1,5},{5,1},{9,13},{13,9},{2,6},{6,2},{1... | collective-permute-start | bytes 196616 | tf_op jit(solution)/shard_map/ppermute | solution.py:90
  36.3 2.2 %collective-permute-done.3 = bf16[2,128,128]{1,2,0:T(8,128)(2,1)S(1)} collective-permute-done((bf16[2,128,128]{1,2,0:T(8,128)(2,1)S(1)}, bf16[2,128,128]{1,2,0:T(8,128)(2,1)S(1)}, u32[]{:S(2)}, u32[]{:S(2)}) %collective-permute-start.3) | collective-permute-done | bytes 65568 | tf_op jit(solution)/shard_map/ppermute | solution.py:90
  38.4 1.9 %collective-permute-done.4 = bf16[2,128,128]{1,2,0:T(8,128)(2,1)S(1)} collective-permute-done((bf16[2,128,128]{1,2,0:T(8,128)(2,1)S(1)}, bf16[2,128,128]{1,2,0:T(8,128)(2,1)S(1)}, u32[]{:S(2)}, u32[]{:S(2)}) %collective-permute-start.4) | collective-permute-done | bytes 65568 | tf_op jit(solution)/shard_map/ppermute | solution.py:90
  42.1 1.0 %fusion.5 = bf16[1,128,512]{1,2,0:T(8,128)(2,1)S(1)} fusion(f32[512,1024]{1,0:T(8,128)S(1)} %bitcast.112, f32[128,512]{1,0:T(8,128)S(1)} %get-tuple-element.51, f32[128,512]{1,0:T(8,128)S(1)} %get-tuple-element.52, f32[1024]{0:T(1024)S(1)} %fusion.82), kind=kOutput, calls=%fused_computation.15 | convolution fusion | flops 402980864 | bytes 2756608 | tf_op jit(solution)/shard_map/dot_general | solution.py:165
  43.2 1.0 %fusion.6 = bf16[1,128,512]{1,2,0:T(8,128)(2,1)S(1)} fusion(f32[512,1024]{1,0:T(8,128)S(1)} %bitcast.113, f32[128,512]{1,0:T(8,128)S(1)} %get-tuple-element.53, f32[128,512]{1,0:T(8,128)S(1)} %get-tuple-element.28, f32[1024]{0:T(1024)S(1)} %fusion.82), kind=kOutput, calls=%fused_computation.16 | convolution fusion | flops 402980864 | bytes 2756608 | tf_op jit(solution)/shard_map/dot_general | solution.py:165
  44.3 2.0 %collective-permute-start.6 = (bf16[2,128,128]{1,2,0:T(8,128)(2,1)S(1)}, bf16[2,128,128]{1,2,0:T(8,128)(2,1)S(1)}, u32[]{:S(2)}, u32[]{:S(2)}) collective-permute-start(bf16[2,128,128]{1,2,0:T(8,128)(2,1)S(1)} %get-tuple-element.70), channel_id=1, source_target_pairs={{0,12},{4,8},{8,4},{12,0},{1,13},{5,9},{9,5},{13,1},{2,14},{6,10},... | collective-permute-start | bytes 196616 | tf_op jit(solution)/shard_map/ppermute | solution.py:90
  46.3 2.4 %collective-permute-start.8 = (bf16[2,128,128]{1,2,0:T(8,128)(2,1)S(1)}, bf16[2,128,128]{1,2,0:T(8,128)(2,1)S(1)}, u32[]{:S(2)}, u32[]{:S(2)}) collective-permute-start(bf16[2,128,128]{1,2,0:T(8,128)(2,1)S(1)} %get-tuple-element.23), channel_id=1, source_target_pairs={{0,4},{4,0},{8,12},{12,8},{1,5},{5,1},{9,13},{13,9},{2,6},{6,2},{1... | collective-permute-start | bytes 196616 | tf_op jit(solution)/shard_map/ppermute | solution.py:90
  48.9 1.6 %collective-permute-done.6 = bf16[2,128,128]{1,2,0:T(8,128)(2,1)S(1)} collective-permute-done((bf16[2,128,128]{1,2,0:T(8,128)(2,1)S(1)}, bf16[2,128,128]{1,2,0:T(8,128)(2,1)S(1)}, u32[]{:S(2)}, u32[]{:S(2)}) %collective-permute-start.6) | collective-permute-done | bytes 65568 | tf_op jit(solution)/shard_map/ppermute | solution.py:90
  50.5 1.8 %collective-permute-done.7 = bf16[2,128,128]{1,2,0:T(8,128)(2,1)S(1)} collective-permute-done((bf16[2,128,128]{1,2,0:T(8,128)(2,1)S(1)}, bf16[2,128,128]{1,2,0:T(8,128)(2,1)S(1)}, u32[]{:S(2)}, u32[]{:S(2)}) %collective-permute-start.7) | collective-permute-done | bytes 65568 | tf_op jit(solution)/shard_map/ppermute | solution.py:90
  52.6 1.3 %fusion.3 = f32[128]{0:T(128)S(1)} fusion(f32[3,512,128]{1,2,0:T(8,128)S(1)} %convolution_bitcast_fusion.1, bf16[2048,3,512]{2,0,1:T(8,128)(2,1)S(1)} %bitcast.116, f32[128,2048]{1,0:T(8,128)S(1)} %get-tuple-element.86, f32[2048]{0:T(1024)S(1)} %copy-done.10, f32[128]{0:T(128)S(1)} %add_rsqrt_fusion, bf16[1,512,128]{1,2,0:T(8,128)(2,1)S(1)} %get-tuple-element.46, ...), kind=kOutput, calls=%fused_computation.9 | convolution fusion | flops 808058752 | bytes 8528896 | tf_op jit(solution)/shard_map/dr,dmc->mcr/dot_general | solution.py:230
  53.8 2.2 %fusion.7 = (f32[2048]{0:T(1024)S(1)}, f32[128,2048,1]{1,0,2:T(8,128)S(1)}) fusion(f32[128,2048]{1,0:T(8,128)S(1)} %get-tuple-element.86, f32[128]{0:T(128)S(1)} %add_rsqrt_fusion, bf16[2048,3,512]{2,0,1:T(8,128)(2,1)S(1)} %bitcast.116, bf16[1,512,128]{1,2,0:T(8,128)(2,1)S(1)} %get-tuple-element.46, bf16[1,512,128]{1,2,0:T(8,128)(2,1)S(1)} %get-tuple-element.44, ...), kind=kOutput, calls=%fused_computation.18 | convolution fusion | flops 806483968 | bytes 8790528 | tf_op jit(solution)/shard_map/mcr,dmc->rd/dot_general | solution.py:276
  56.0 0.6 convolution_multiply_fusion.1
  56.6 0.7 fusion
  57.4 1.6 %collective-permute-start.12 = (f32[21,512]{1,0:T(8,128)S(1)}, f32[21,512]{1,0:T(8,128)S(1)}, u32[]{:S(2)}, u32[]{:S(2)}) collective-permute-start(f32[21,512]{1,0:T(8,128)S(1)} %get-tuple-element.76), channel_id=1, source_target_pairs={{0,2},{1,3},{2,0},{3,1},{4,6},{5,7},{6,4},{7,5},{8,10},{9,11},{10,... | collective-permute-start | bytes 129032 | tf_op jit(solution)/shard_map/ppermute | solution.py:90
  59.0 0.6 collective-permute-start.11
  59.7 1.6 %collective-permute-start.9 = (bf16[1,512,128]{1,2,0:T(8,128)(2,1)S(1)}, bf16[1,512,128]{1,2,0:T(8,128)(2,1)S(1)}, u32[]{:S(2)}, u32[]{:S(2)}) collective-permute-start(bf16[1,512,128]{1,2,0:T(8,128)(2,1)S(1)} %get-tuple-element.45), channel_id=1, source_target_pairs={{0,2},{2,0},{1,3},{3,1},{4,6},{6,4},{5,7},{7,5},{8,10},{10,8},{9,1... | collective-permute-start | bytes 393224 | tf_op jit(solution)/shard_map/ppermute | solution.py:46
  61.6 1.1 %collective-permute-done.13 = f32[21,512]{1,0:T(8,128)S(1)} collective-permute-done((f32[21,512]{1,0:T(8,128)S(1)}, f32[21,512]{1,0:T(8,128)S(1)}, u32[]{:S(2)}, u32[]{:S(2)}) %collective-permute-start.13) | collective-permute-done | bytes 43040 | tf_op jit(solution)/shard_map/ppermute | solution.py:90
  62.7 2.4 %collective-permute-start.14 = (f32[21,512]{1,0:T(8,128)S(1)}, f32[21,512]{1,0:T(8,128)S(1)}, u32[]{:S(2)}, u32[]{:S(2)}) collective-permute-start(f32[21,512]{1,0:T(8,128)S(1)} %pad_add_fusion), channel_id=1, source_target_pairs={{0,12},{4,8},{8,4},{12,0},{1,13},{5,9},{9,5},{13,1},{2,14},{6,10},... | collective-permute-start | bytes 129032 | tf_op jit(solution)/shard_map/ppermute | solution.py:90
  65.1 2.0 %collective-permute-start.16 = (f32[21,512]{1,0:T(8,128)S(1)}, f32[21,512]{1,0:T(8,128)S(1)}, u32[]{:S(2)}, u32[]{:S(2)}) collective-permute-start(f32[21,512]{1,0:T(8,128)S(1)} %pad_add_fusion), channel_id=1, source_target_pairs={{0,4},{4,0},{8,12},{12,8},{1,5},{5,1},{9,13},{13,9},{2,6},{6,2},{1... | collective-permute-start | bytes 129032 | tf_op jit(solution)/shard_map/ppermute | solution.py:90
  67.2 0.7 maximum_bitcast_fusion
  67.9 1.9 %convolution_bitcast_fusion.3 = f32[1,1,128,512]{3,2,1,0:T(8,128)} fusion(f32[512,1024]{1,0:T(8,128)S(1)} %bitcast.114, f32[128,512]{1,0:T(8,128)S(1)} %get-tuple-element.55, f32[128,512]{1,0:T(8,128)S(1)} %get-tuple-element.54, f32[1024]{0:T(1024)S(1)} %fusion.82), kind=kOutput, calls=%fused_computation.10 | convolution fusion | flops 402915328 | bytes 2887680 | tf_op jit(solution)/shard_map/dot_general | solution.py:165
  70.3 0.6 slice.256
  70.8 0.6 copy.23
  71.5 1.0 %broadcast_select_fusion.1 = (bf16[2,1,512,128]{2,3,0,1:T(8,128)(2,1)S(1)}, bf16[2,1,512,128]{2,3,0,1:T(8,128)(2,1)S(1)}) fusion(bf16[2,1,512,128]{2,3,0,1:T(8,128)(2,1)} %collective-permute-done.10, pred[]{:T(512)S(6)} %eq.248, bf16[1,512,128]{1,2,0:T(8,128)(2,1)S(1)} %get-tuple-element.65, bf16[1,512,128]{1,2,0:T(8,128)(2,1)S(1)} %get-tuple-element.64), kind=kLoop, calls=%fused_computation.109 | loop fusion | flops 393216 | bytes 1048577 | tf_op jit(solution)/shard_map/jit(_where)/select_n | solution.py:70
  72.5 0.8 %pad_maximum_fusion.3 = bf16[2,2,512,128]{2,3,0,1:T(8,128)(2,1)} fusion(bf16[2,1,512,128]{2,3,0,1:T(8,128)(2,1)S(1)} %get-tuple-element.59, bf16[2,1,512,128]{2,3,0,1:T(8,128)(2,1)S(1)} %get-tuple-element.58), kind=kLoop, calls=%fused_computation.46 | loop fusion | flops 262144 | bytes 1048576 | tf_op jit(solution)/shard_map/concatenate | solution.py:69
  73.3 2.0 %copy.22 = bf16[2,2,512,128]{3,2,1,0:T(8,128)(2,1)} copy(bf16[2,2,512,128]{2,3,0,1:T(8,128)(2,1)} %pad_maximum_fusion.3) | data formatting | bytes 1048576 | tf_op jit(solution)/shard_map/concatenate | solution.py:69
  75.4 2.2 %fusion.4 = bf16[128,512]{1,0:T(8,128)(2,1)} fusion(bf16[2048,128]{1,0:T(8,128)(2,1)} %bitcast.117, bf16[2048,512]{1,0:T(8,128)(2,1)S(1)} %copy-done, f32[128,2048]{1,0:T(8,128)S(1)} %get-tuple-element.86, s32[]{:T(128)S(6)} %select_n.680), kind=kOutput, calls=%fused_computation.12 | convolution fusion | flops 268566528 | bytes 3014660 | tf_op jit(solution)/shard_map/cr,cd->rd/dot_general | solution.py:262
  (98 shorter events, 6.8 us)
Async XLA Ops:
  0.6 1.6 %copy-start = (bf16[2048,512]{1,0:T(8,128)(2,1)S(1)}, bf16[2048,512]{1,0:T(8,128)(2,1)}, u32[]{:S(2)}) copy-start(bf16[2048,512]{1,0:T(8,128)(2,1)} %param.12) | copy-start | bytes 6291460
  3.9 2.1 %copy-start.15 = (s32[128]{0:T(128)S(1)}, s32[128]{0:T(128)}, u32[]{:S(2)}) copy-start(s32[128]{0:T(128)} %param.7) | copy-start | bytes 1540
  4.0 0.7 copy-start.5
  4.1 1.5 %copy-start.6 = (f32[128,512]{1,0:T(8,128)}, f32[128,512]{1,0:T(8,128)S(1)}, u32[]{:S(2)}) copy-start(f32[128,512]{1,0:T(8,128)S(1)} %get-tuple-element.49) | copy-start | bytes 786436
  4.1 2.0 %copy-start.7 = (f32[128,512]{1,0:T(8,128)}, f32[128,512]{1,0:T(8,128)S(1)}, u32[]{:S(2)}) copy-start(f32[128,512]{1,0:T(8,128)S(1)} %get-tuple-element.50) | copy-start | bytes 786436
  4.8 8.3 %copy-start.9 = (f32[1,1,128,512]{3,2,1,0:T(8,128)S(1)}, f32[1,1,128,512]{3,2,1,0:T(8,128)}, u32[]{:S(2)}) copy-start(f32[1,1,128,512]{3,2,1,0:T(8,128)} %param.11) | copy-start | bytes 786436
  5.6 15.9 %collective-permute-start.1 = (f32[128,1024]{1,0:T(8,128)}, f32[128,1024]{1,0:T(8,128)}, u32[]{:S(2)}, u32[]{:S(2)}) collective-permute-start(f32[128,1024]{1,0:T(8,128)} %fusion.29), channel_id=1, source_target_pairs={{0,1},{1,0},{2,3},{3,2},{4,5},{5,4},{6,7},{7,6},{8,9},{9,8},{10,11... | collective-permute-start | bytes 1572872 | tf_op jit(solution)/shard_map/ppermute | solution.py:46
  6.7 12.0 %collective-permute-start = (s32[3]{0:T(128)}, s32[3]{0:T(128)}, u32[]{:S(2)}, u32[]{:S(2)}) collective-permute-start(s32[3]{0:T(128)} %slice_add_fusion.2), channel_id=1, source_target_pairs={{0,4},{4,8},{8,12},{1,5},{5,9},{9,13},{2,6},{6,10},{10,14},{3,7},{... | collective-permute-start | bytes 44 | tf_op jit(solution)/shard_map/ppermute | solution.py:16
  13.0 1.3 %copy-start.1 = (f32[16,32,1024]{2,1,0:T(8,128)}, f32[16,32,1024]{2,1,0:T(8,128)S(1)}, u32[]{:S(2)}) copy-start(f32[16,32,1024]{2,1,0:T(8,128)S(1)} %multiply_subtract_fusion) | copy-start | bytes 6291460
  13.8 0.8 %copy-start.3 = (f32[128,1024]{1,0:T(8,128)}, f32[128,1024]{1,0:T(8,128)S(1)}, u32[]{:S(2)}) copy-start(f32[128,1024]{1,0:T(8,128)S(1)} %convolution_bitcast_fusion.2) | copy-start | bytes 1572868
  18.6 5.8 %copy-start.10 = (f32[2048]{0:T(1024)S(1)}, f32[2048]{0:T(1024)}, u32[]{:S(2)}) copy-start(f32[2048]{0:T(1024)} %param.9) | copy-start | bytes 24580
  22.9 8.5 %collective-permute-start.2 = (f32[128,512]{1,0:T(8,128)S(1)}, f32[128,512]{1,0:T(8,128)S(1)}, u32[]{:S(2)}, u32[]{:S(2)}) collective-permute-start(f32[128,512]{1,0:T(8,128)S(1)} %slice_select_fusion), channel_id=1, source_target_pairs={{0,2},{2,0},{1,3},{3,1},{4,6},{6,4},{5,7},{7,5},{8,10},{10,8},{9,1... | collective-permute-start | bytes 786440 | tf_op jit(solution)/shard_map/ppermute | solution.py:46
  28.3 7.8 %copy-start.8 = (bf16[128,512]{1,0:T(8,128)(2,1)S(1)}, bf16[128,512]{1,0:T(8,128)(2,1)}, u32[]{:S(2)}) copy-start(bf16[128,512]{1,0:T(8,128)(2,1)} %param.13) | copy-start | bytes 393220
  28.3 12.1 %copy-start.2 = (f32[16,32,1024]{2,1,0:T(8,128)S(1)}, f32[16,32,1024]{2,1,0:T(8,128)}, u32[]{:S(2)}) copy-start(f32[16,32,1024]{2,1,0:T(8,128)} %copy-done.1) | copy-start | bytes 6291460
  31.6 6.8 %collective-permute-start.3 = (bf16[2,128,128]{1,2,0:T(8,128)(2,1)S(1)}, bf16[2,128,128]{1,2,0:T(8,128)(2,1)S(1)}, u32[]{:S(2)}, u32[]{:S(2)}) collective-permute-start(bf16[2,128,128]{1,2,0:T(8,128)(2,1)S(1)} %get-tuple-element.75), channel_id=1, source_target_pairs={{0,12},{4,8},{8,4},{12,0},{1,13},{5,9},{9,5},{13,1},{2,14},{6,10},... | collective-permute-start | bytes 196616 | tf_op jit(solution)/shard_map/ppermute | solution.py:90
  32.8 7.5 %collective-permute-start.4 = (bf16[2,128,128]{1,2,0:T(8,128)(2,1)S(1)}, bf16[2,128,128]{1,2,0:T(8,128)(2,1)S(1)}, u32[]{:S(2)}, u32[]{:S(2)}) collective-permute-start(bf16[2,128,128]{1,2,0:T(8,128)(2,1)S(1)} %get-tuple-element.74), channel_id=1, source_target_pairs={{0,8},{4,12},{8,0},{12,4},{1,9},{5,13},{9,1},{13,5},{2,10},{6,14},... | collective-permute-start | bytes 196616 | tf_op jit(solution)/shard_map/ppermute | solution.py:90
  34.2 6.1 %collective-permute-start.5 = (bf16[2,128,128]{1,2,0:T(8,128)(2,1)S(1)}, bf16[2,128,128]{1,2,0:T(8,128)(2,1)S(1)}, u32[]{:S(2)}, u32[]{:S(2)}) collective-permute-start(bf16[2,128,128]{1,2,0:T(8,128)(2,1)S(1)} %get-tuple-element.33), channel_id=1, source_target_pairs={{0,4},{4,0},{8,12},{12,8},{1,5},{5,1},{9,13},{13,9},{2,6},{6,2},{1... | collective-permute-start | bytes 196616 | tf_op jit(solution)/shard_map/ppermute | solution.py:90
  40.4 1.2 %copy-start.4 = (f32[128,1024]{1,0:T(8,128)S(1)}, f32[128,1024]{1,0:T(8,128)}, u32[]{:S(2)}) copy-start(f32[128,1024]{1,0:T(8,128)} %copy-done.3) | copy-start | bytes 1572868
  40.4 1.2 %copy-start.11 = (pred[512]{0:T(512)(128)(4,1)S(1)}, pred[512]{0:T(512)(128)(4,1)}, u32[]{:S(2)}) copy-start(pred[512]{0:T(512)(128)(4,1)} %iota_compare_fusion.6) | copy-start | bytes 1540
  42.0 10.5 %slice-start = ((s8[6291456]{0:T(1024)(128)(4,1)}), s8[4194304]{0:T(1024)(128)(4,1)S(1)}, s32[]{:S(2)}) async-start(s8[6291456]{0:T(1024)(128)(4,1)} %bitcast.115), calls=%async_computation | async-start | bytes 8388608
  43.1 5.6 %copy-start.12 = (s32[128]{0:T(128)S(1)}, s32[128]{0:T(128)}, u32[]{:S(2)}) copy-start(s32[128]{0:T(128)} %get-tuple-element.93) | copy-start | bytes 1540
  43.1 5.6 %copy-start.13 = (s32[128]{0:T(128)S(1)}, s32[128]{0:T(128)}, u32[]{:S(2)}) copy-start(s32[128]{0:T(128)} %get-tuple-element.94) | copy-start | bytes 1540
  43.1 5.6 %copy-start.14 = (pred[128]{0:T(512)(128)(4,1)S(1)}, pred[128]{0:T(512)(128)(4,1)}, u32[]{:S(2)}) copy-start(pred[128]{0:T(512)(128)(4,1)} %compare_and_fusion) | copy-start | bytes 388
  43.2 9.4 %slice-start.1 = ((s8[6291456]{0:T(1024)(128)(4,1)}), s8[2097152]{0:T(1024)(128)(4,1)S(1)}, s32[]{:S(2)}) async-start(s8[6291456]{0:T(1024)(128)(4,1)} %bitcast.115), calls=%async_computation.1 | async-start | bytes 4194304
  44.3 6.2 %collective-permute-start.6 = (bf16[2,128,128]{1,2,0:T(8,128)(2,1)S(1)}, bf16[2,128,128]{1,2,0:T(8,128)(2,1)S(1)}, u32[]{:S(2)}, u32[]{:S(2)}) collective-permute-start(bf16[2,128,128]{1,2,0:T(8,128)(2,1)S(1)} %get-tuple-element.70), channel_id=1, source_target_pairs={{0,12},{4,8},{8,4},{12,0},{1,13},{5,9},{9,5},{13,1},{2,14},{6,10},... | collective-permute-start | bytes 196616 | tf_op jit(solution)/shard_map/ppermute | solution.py:90
  46.3 6.0 %collective-permute-start.7 = (bf16[2,128,128]{1,2,0:T(8,128)(2,1)S(1)}, bf16[2,128,128]{1,2,0:T(8,128)(2,1)S(1)}, u32[]{:S(2)}, u32[]{:S(2)}) collective-permute-start(bf16[2,128,128]{1,2,0:T(8,128)(2,1)S(1)} %get-tuple-element.69), channel_id=1, source_target_pairs={{0,8},{4,12},{8,0},{12,4},{1,9},{5,13},{9,1},{13,5},{2,10},{6,14},... | collective-permute-start | bytes 196616 | tf_op jit(solution)/shard_map/ppermute | solution.py:90
  46.3 6.0 %collective-permute-start.8 = (bf16[2,128,128]{1,2,0:T(8,128)(2,1)S(1)}, bf16[2,128,128]{1,2,0:T(8,128)(2,1)S(1)}, u32[]{:S(2)}, u32[]{:S(2)}) collective-permute-start(bf16[2,128,128]{1,2,0:T(8,128)(2,1)S(1)} %get-tuple-element.23), channel_id=1, source_target_pairs={{0,4},{4,0},{8,12},{12,8},{1,5},{5,1},{9,13},{13,9},{2,6},{6,2},{1... | collective-permute-start | bytes 196616 | tf_op jit(solution)/shard_map/ppermute | solution.py:90
  57.4 4.2 %collective-permute-start.12 = (f32[21,512]{1,0:T(8,128)S(1)}, f32[21,512]{1,0:T(8,128)S(1)}, u32[]{:S(2)}, u32[]{:S(2)}) collective-permute-start(f32[21,512]{1,0:T(8,128)S(1)} %get-tuple-element.76), channel_id=1, source_target_pairs={{0,2},{1,3},{2,0},{3,1},{4,6},{5,7},{6,4},{7,5},{8,10},{9,11},{10,... | collective-permute-start | bytes 129032 | tf_op jit(solution)/shard_map/ppermute | solution.py:90
  59.0 3.6 %collective-permute-start.13 = (f32[21,512]{1,0:T(8,128)S(1)}, f32[21,512]{1,0:T(8,128)S(1)}, u32[]{:S(2)}, u32[]{:S(2)}) collective-permute-start(f32[21,512]{1,0:T(8,128)S(1)} %get-tuple-element.77), channel_id=1, source_target_pairs={{0,3},{1,2},{2,1},{3,0},{4,7},{5,6},{6,5},{7,4},{8,11},{9,10},{10,... | collective-permute-start | bytes 129032 | tf_op jit(solution)/shard_map/ppermute | solution.py:90
  59.0 3.6 %collective-permute-start.11 = (f32[21,512]{1,0:T(8,128)S(1)}, f32[21,512]{1,0:T(8,128)S(1)}, u32[]{:S(2)}, u32[]{:S(2)}) collective-permute-start(f32[21,512]{1,0:T(8,128)S(1)} %get-tuple-element.16), channel_id=1, source_target_pairs={{0,1},{1,0},{2,3},{3,2},{4,5},{5,4},{6,7},{7,6},{8,9},{9,8},{10,11... | collective-permute-start | bytes 129032 | tf_op jit(solution)/shard_map/ppermute | solution.py:90
  59.7 7.4 %collective-permute-start.9 = (bf16[1,512,128]{1,2,0:T(8,128)(2,1)S(1)}, bf16[1,512,128]{1,2,0:T(8,128)(2,1)S(1)}, u32[]{:S(2)}, u32[]{:S(2)}) collective-permute-start(bf16[1,512,128]{1,2,0:T(8,128)(2,1)S(1)} %get-tuple-element.45), channel_id=1, source_target_pairs={{0,2},{2,0},{1,3},{3,1},{4,6},{6,4},{5,7},{7,5},{8,10},{10,8},{9,1... | collective-permute-start | bytes 393224 | tf_op jit(solution)/shard_map/ppermute | solution.py:46
  62.7 7.1 %collective-permute-start.14 = (f32[21,512]{1,0:T(8,128)S(1)}, f32[21,512]{1,0:T(8,128)S(1)}, u32[]{:S(2)}, u32[]{:S(2)}) collective-permute-start(f32[21,512]{1,0:T(8,128)S(1)} %pad_add_fusion), channel_id=1, source_target_pairs={{0,12},{4,8},{8,4},{12,0},{1,13},{5,9},{9,5},{13,1},{2,14},{6,10},... | collective-permute-start | bytes 129032 | tf_op jit(solution)/shard_map/ppermute | solution.py:90
  65.1 5.1 %collective-permute-start.15 = (f32[21,512]{1,0:T(8,128)S(1)}, f32[21,512]{1,0:T(8,128)S(1)}, u32[]{:S(2)}, u32[]{:S(2)}) collective-permute-start(f32[21,512]{1,0:T(8,128)S(1)} %pad_add_fusion), channel_id=1, source_target_pairs={{0,8},{4,12},{8,0},{12,4},{1,9},{5,13},{9,1},{13,5},{2,10},{6,14},... | collective-permute-start | bytes 129032 | tf_op jit(solution)/shard_map/ppermute | solution.py:90
  65.1 5.1 %collective-permute-start.16 = (f32[21,512]{1,0:T(8,128)S(1)}, f32[21,512]{1,0:T(8,128)S(1)}, u32[]{:S(2)}, u32[]{:S(2)}) collective-permute-start(f32[21,512]{1,0:T(8,128)S(1)} %pad_add_fusion), channel_id=1, source_target_pairs={{0,4},{4,0},{8,12},{12,8},{1,5},{5,1},{9,13},{13,9},{2,6},{6,2},{1... | collective-permute-start | bytes 129032 | tf_op jit(solution)/shard_map/ppermute | solution.py:90
  67.9 3.6 %collective-permute-start.10 = (bf16[2,1,512,128]{2,3,0,1:T(8,128)(2,1)}, bf16[2,1,512,128]{2,3,0,1:T(8,128)(2,1)}, u32[]{:S(2)}, u32[]{:S(2)}) collective-permute-start(bf16[2,1,512,128]{2,3,0,1:T(8,128)(2,1)} %maximum_bitcast_fusion), channel_id=1, source_target_pairs={{0,1},{1,0},{2,3},{3,2},{4,5},{5,4},{6,7},{7,6},{8,9},{9,8},{10,11... | collective-permute-start | bytes 786440 | tf_op jit(solution)/shard_map/ppermute | solution.py:46

commit v5 on v4

--- a/solution.py
+++ b/solution.py
@@ -90,10 +90,11 @@
     return lax.ppermute(x, axes, [(i, i ^ offset) for i in range(count)])
 
 
-def reduce_blocks_cp(x, width):
+def reduce_blocks_cp(x, width, shared):
     axes = ("chan", "pair")
     count = lax.axis_size("chan") * lax.axis_size("pair")
     me = lax.axis_index(axes)
+    rows = x.shape[0]
     blocks = [x[:, g * width : (g + 1) * width] for g in range(count)]
 
     def pick(index):
@@ -102,10 +103,16 @@
             out = jnp.where(index == g, blocks[g], out)
         return out
 
+    extra = shared.astype(jnp.float32)
     total = pick(me)
+    pieces = [(me, shared)]
     for offset in range(1, count):
-        total = total + group_exchange(pick(me ^ offset), axes, count, offset)
-    return total
+        got = group_exchange(
+            jnp.concatenate([pick(me ^ offset), extra], axis=0), axes, count, offset
+        )
+        total = total + got[:rows]
+        pieces.append((me ^ offset, got[rows:].astype(shared.dtype)))
+    return total, pieces
 
 
 def sum_over_seq(x):
@@ -258,15 +265,6 @@
     both_rows = all_to_all_seq(jnp.stack([conv_cols, d_mixed_cols]), 2, 1)
     conv_rows, d_mixed = both_rows[0], both_rows[1]
     gated_rows = (query_part * conv_rows.astype(jnp.float32)).astype(jnp.bfloat16)
-    weight_rows = out_proj
-    mixed_out = jnp.einsum(
-        "cr,cd->rd",
-        all_gather_cp(gated_rows),
-        weight_rows,
-        preferred_element_type=jnp.float32,
-    )
-    own_rows = lax.dynamic_slice_in_dim(embedded, group_index * local_width, local_width, 0)
-    block_out = (mixed_out + own_rows.T).astype(jnp.bfloat16)
     d_query = d_gated * conv_rows.astype(jnp.float32)
     cross = cmul(sa, sb, da, db, True)
     filter_grad = inverse_dft(add_conj_flip(cross), dft)
@@ -282,7 +280,14 @@
     table_all = norm_gain[None, :] * direct - centred / model_width
     gain_all = jnp.einsum("rd,dr->d", d_full, normed, precision=PRECISE)
     partial = jnp.concatenate([table_all, gain_all[None, :]], axis=0)
-    own_block = reduce_blocks_cp(partial, local_width)
+    own_block, gated_pieces = reduce_blocks_cp(partial, local_width, gated_rows.T)
+    mixed_out = None
+    for source, piece in gated_pieces:
+        rows = lax.dynamic_slice_in_dim(out_proj, source * local_width, local_width, 0)
+        term = jnp.dot(piece, rows, preferred_element_type=jnp.float32)
+        mixed_out = term if mixed_out is None else mixed_out + term
+    own_rows = lax.dynamic_slice_in_dim(embedded, group_index * local_width, local_width, 0)
+    block_out = (mixed_out + own_rows.T).astype(jnp.bfloat16)
     cot_table = jnp.einsum(
         "rk,rc->kc", onehot_rows, cotangent.astype(jnp.float32) * grad_scale, precision=PRECISE
     )

time: 78.1 us -> 84 us (1.076)
  waiting for transfers between devices: 12.2 us -> 23.1 us
  other arithmetic: 11.9 us -> 9.84 us
  local copies, waits for them, and re-layouts: 8.17 us -> 6.42 us
  starting transfers between devices: 24.2 us -> 22.7 us
    ppermute x12, waiting for transfers between devices: 9.17 us -> 20.1 us  [group_exchange(): return lax.ppermute(x, axes, [(i, i ^ offset) for i in range(count)])]
    concatenate x1 -> x0, local copies, waits for them, and re-layouts: 2.05 us -> none  [ordered(): jnp.concatenate([jnp.where(first, mine, other), jnp.where(first, other, m...]
    ppermute x4 -> x2, starting transfers between devices: 3.62 us -> 2.05 us  [xor_exchange(): return lax.ppermute(x, axis, [(i, i ^ step) for i in range(count)])]
    dot_general x3, matrix products: 1.83 us -> 2.95 us  [forward_dft(): jnp.dot(signal.astype(jnp.float32), dft, precision=TRANSFORM_PRECISION)]
    select_n x2 -> x0, other arithmetic: 1.01 us -> none  [ordered(): jnp.where(first, mine, other)]
    slice x2, local copies, waits for them, and re-layouts: 0.09 us -> 1.06 us  [pair_flip(): down = jnp.roll(values, 1, axis=0)]
    unnamed x38 -> x30, local copies, waits for them, and re-layouts: 4.59 us -> 3.92 us
    dot_general x1 -> x4, matrix products: 2.17 us -> 1.62 us  [per_device(): term = jnp.dot(piece, rows, preferred_element_type=jnp.float32)]
  transfers between devices with their start and end apart: 17 -> 15, of which waited for: 8 -> 9; matrix products, arithmetic and copies ran while one was open for 23% -> 24% of each run, Pallas kernels for 0% -> 0%
where the time goes in v5:
time: 84 us; the launch traced here: 83.5 us
  waiting for transfers between devices  23.1 us (28%)
  starting transfers between devices  22.7 us (27%)
  matrix products  20.3 us (24%)
  other arithmetic  9.84 us (12%)
  local copies, waits for them, and re-layouts  6.42 us (8%)
  between operations  1.16 us (1%)
    ppermute x12, waiting for transfers between devices, group_exchange(): return lax.ppermute(x, axes, [(i, i ^ offset) for i in range(count)])  20.1 us
    ppermute x12, starting transfers between devices, group_exchange(): return lax.ppermute(x, axes, [(i, i ^ offset) for i in range(count)])  15.6 us
    ppermute x1, starting transfers between devices, from_behind(): lax.ppermute(value, axis, [(source, source + steps) for source in range(f...  5.04 us
    dot_general x3, matrix products, inverse_dft(): lax.dot_general(spec * weight, dft, (((1,), (1,)), ((), ())), precision=T...  3.99 us
    unnamed x30, local copies, waits for them, and re-layouts  3.92 us
    dot_general x1, matrix products, per_device(): jnp.einsum('dr,dmc->mcr', hidden, in_proj, preferred_element_type=jnp.flo...  3.86 us
    ppermute x2, waiting for transfers between devices, xor_exchange(): return lax.ppermute(x, axis, [(i, i ^ step) for i in range(count)])  3 us
    dot_general x3, matrix products, forward_dft(): jnp.dot(signal.astype(jnp.float32), dft, precision=TRANSFORM_PRECISION)  2.95 us
  transfers between devices with their start and end apart: 15, of which 9 were waited for; matrix products, arithmetic and copies ran while one was open for 24% of the time, Pallas kernels for 0%

profile of v5, /device:TPU:0, one launch (start us, length us, event | category | flops | bytes accessed | tf_op | source)
XLA Modules:
  0.0 83.5 jit_solution(9158313748412539714)
XLA Ops:
  0.7 1.6 %copy-done = bf16[2048,512]{1,0:T(8,128)(2,1)S(1)} copy-done((bf16[2048,512]{1,0:T(8,128)(2,1)S(1)}, bf16[2048,512]{1,0:T(8,128)(2,1)}, u32[]{:S(2)}) %copy-start) | copy-done | bytes 2097176
  2.2 1.7 %fusion.115 = f32[128,2048]{1,0:T(8,128)S(1)} fusion(bf16[128,512]{1,0:T(8,128)(2,1)} %param.13, bf16[2048,512]{1,0:T(8,128)(2,1)S(1)} %copy-done), kind=kOutput, calls=%fused_computation.243 | convolution fusion | flops 268435456 | bytes 3276800 | tf_op jit(solution)/shard_map/rd,cd->rc/dot_general | solution.py:246
  4.1 0.7 copy-done.3
  4.8 0.9 %fusion.37 = f32[128,1024]{1,0:T(8,128)} fusion(f32[128,512]{1,0:T(8,128)S(1)} %get-tuple-element.47, f32[128,512]{1,0:T(8,128)S(1)} %get-tuple-element.48, f32[128,512]{1,0:T(8,128)S(1)} %get-tuple-element.49, f32[128,512]{1,0:T(8,128)S(1)} %get-tuple-element.46, pred[]{:T(512)S(6)} %eq.262), kind=kLoop, calls=%fused_computation.65 | loop fusion | flops 393216 | bytes 1572865 | tf_op jit(solution)/shard_map/jit(_where)/select_n | solution.py:57
  6.1 0.6 slice_add_fusion.5
  6.7 5.0 %collective-permute-start = (s32[3]{0:T(128)}, s32[3]{0:T(128)}, u32[]{:S(2)}, u32[]{:S(2)}) collective-permute-start(s32[3]{0:T(128)} %slice_add_fusion.5), channel_id=1, source_target_pairs={{0,4},{4,8},{8,12},{1,5},{5,9},{9,13},{2,6},{6,10},{10,14},{3,7},{... | collective-permute-start | bytes 44 | tf_op jit(solution)/shard_map/ppermute | solution.py:16
  12.1 0.6 fusion.69
  13.0 1.8 %convolution_bitcast_fusion.2 = f32[128,1024]{1,0:T(8,128)S(1)} fusion(f32[512,1024]{1,0:T(8,128)S(1)} %bitcast.111, f32[1,1,128,512]{3,2,1,0:T(8,128)} %param.11), kind=kOutput, calls=%fused_computation.8 | convolution fusion | flops 402653184 | bytes 2883584 | tf_op jit(solution)/shard_map/dot_general | solution.py:164
  14.9 1.1 %fusion.113 = (f32[127,1024]{1,0:T(8,128)}, f32[127,1024]{1,0:T(8,128)}) fusion(f32[128,1024]{1,0:T(8,128)S(1)} %convolution_bitcast_fusion.2), kind=kLoop, calls=%fused_computation.241 | loop fusion | bytes 2080768 | tf_op jit(solution)/shard_map/jit(_roll_static)/slice | solution.py:199
  15.9 0.6 iota_and_fusion.1
  17.6 0.9 %copy.18 = bf16[4,5,2048]{2,1,0:T(8,128)(2,1)S(1)} copy(bf16[4,5,2048]{2,0,1:T(4,128)(2,1)} %param.8) | data formatting | bytes 163840 | tf_op args[1]
  18.5 0.7 reshape.262
  19.2 1.4 %maximum_select_fusion = f32[128,1024]{1,0:T(8,128)S(1)} fusion(f32[1,1024]{1,0:T(1,128)S(1)} %get-tuple-element.58, f32[127,1024]{1,0:T(8,128)} %get-tuple-element.60, f32[127,1024]{1,0:T(8,128)} %get-tuple-element.59, f32[1,1024]{1,0:T(1,128)S(1)} %get-tuple-element.57, s32[128]{0:T(128)} %get-tuple-element.93, s32[128]{0:T(128)} %get-tuple-element.94, ...), kind=kLoop, calls=%fused_computation.40 | loop fusion | flops 655360 | bytes 1574016 | tf_op jit(solution)/shard_map/jit(_where)/select_n | solution.py:200
  20.6 0.7 broadcast_add_fusion.1
  21.3 0.7 pad_add_fusion.1
  22.1 1.3 %multiply_reduce_fusion = (f32[128]{0:T(128)S(1)}, f32[128,2048]{1,0:T(8,128)S(1)}) fusion(bf16[20,2048]{1,0:T(8,128)(2,1)} %reshape.262, pred[128,5]{0,1:T(8,128)(4,1)S(1)} %get-tuple-element.89, pred[128,5]{0,1:T(8,128)(4,1)S(1)} %get-tuple-element.90, pred[128,5]{0,1:T(8,128)(4,1)S(1)} %iota_compare_fusion.4, pred[128,5]{0,1:T(8,128)(4,1)S(1)} %iota_compare_fusion.5), kind=kOutput, calls=%fused_computation.25 | convolution fusion | flops 11017600 | bytes 1133568 | tf_op jit(solution)/shard_map/dot_general | solution.py:230
  23.5 1.1 %select_add_fusion = f32[128,1024]{1,0:T(8,128)S(1)} fusion(f32[128,1024]{1,0:T(8,128)} %collective-permute-done.1, f32[128,512]{1,0:T(8,128)S(1)} %get-tuple-element.47, f32[128,512]{1,0:T(8,128)S(1)} %get-tuple-element.48, f32[128,512]{1,0:T(8,128)S(1)} %copy-done.4, f32[128,512]{1,0:T(8,128)S(1)} %get-tuple-element.46, pred[]{:T(512)S(6)} %eq.262), kind=kLoop, calls=%fused_computation.58 | loop fusion | flops 524288 | bytes 2097153 | tf_op jit(solution)/shard_map/add | solution.py:58
  24.6 1.6 %collective-permute-start.2 = (f32[128,512]{1,0:T(8,128)S(1)}, f32[128,512]{1,0:T(8,128)S(1)}, u32[]{:S(2)}, u32[]{:S(2)}) collective-permute-start(f32[128,512]{1,0:T(8,128)S(1)} %slice_select_fusion), channel_id=1, source_target_pairs={{0,2},{2,0},{1,3},{3,1},{4,6},{6,4},{5,7},{7,5},{8,10},{10,8},{9,1... | collective-permute-start | bytes 786440 | tf_op jit(solution)/shard_map/ppermute | solution.py:46
  26.2 3.9 %convolution_bitcast_fusion.1 = f32[3,512,128]{1,2,0:T(8,128)S(1)} fusion(bf16[2048,3,512]{2,0,1:T(8,128)(2,1)} %param.10, f32[128,2048]{1,0:T(8,128)S(1)} %get-tuple-element.86, f32[2048]{0:T(1024)S(1)} %copy-done.6, f32[128]{0:T(128)S(1)} %add_rsqrt_fusion), kind=kOutput, calls=%fused_computation.5 | convolution fusion | flops 806092800 | bytes 8135168 | tf_op jit(solution)/shard_map/dr,dmc->mcr/dot_general | solution.py:235
  30.1 3.0 %collective-permute-done.2 = f32[128,512]{1,0:T(8,128)S(1)} collective-permute-done((f32[128,512]{1,0:T(8,128)S(1)}, f32[128,512]{1,0:T(8,128)S(1)}, u32[]{:S(2)}, u32[]{:S(2)}) %collective-permute-start.2) | collective-permute-done | bytes 262176 | tf_op jit(solution)/shard_map/ppermute | solution.py:46
  33.3 1.2 %collective-permute-start.3 = (bf16[2,128,128]{1,2,0:T(8,128)(2,1)S(1)}, bf16[2,128,128]{1,2,0:T(8,128)(2,1)S(1)}, u32[]{:S(2)}, u32[]{:S(2)}) collective-permute-start(bf16[2,128,128]{1,2,0:T(8,128)(2,1)S(1)} %get-tuple-element.75), channel_id=1, source_target_pairs={{0,12},{4,8},{8,4},{12,0},{1,13},{5,9},{9,5},{13,1},{2,14},{6,10},... | collective-permute-start | bytes 196616 | tf_op jit(solution)/shard_map/ppermute | solution.py:90
  34.6 1.4 %collective-permute-start.4 = (bf16[2,128,128]{1,2,0:T(8,128)(2,1)S(1)}, bf16[2,128,128]{1,2,0:T(8,128)(2,1)S(1)}, u32[]{:S(2)}, u32[]{:S(2)}) collective-permute-start(bf16[2,128,128]{1,2,0:T(8,128)(2,1)S(1)} %get-tuple-element.74), channel_id=1, source_target_pairs={{0,8},{4,12},{8,0},{12,4},{1,9},{5,13},{9,1},{13,5},{2,10},{6,14},... | collective-permute-start | bytes 196616 | tf_op jit(solution)/shard_map/ppermute | solution.py:90
  35.9 1.9 %collective-permute-start.5 = (bf16[2,128,128]{1,2,0:T(8,128)(2,1)S(1)}, bf16[2,128,128]{1,2,0:T(8,128)(2,1)S(1)}, u32[]{:S(2)}, u32[]{:S(2)}) collective-permute-start(bf16[2,128,128]{1,2,0:T(8,128)(2,1)S(1)} %get-tuple-element.33), channel_id=1, source_target_pairs={{0,4},{4,0},{8,12},{12,8},{1,5},{5,1},{9,13},{13,9},{2,6},{6,2},{1... | collective-permute-start | bytes 196616 | tf_op jit(solution)/shard_map/ppermute | solution.py:90
  38.0 2.1 %collective-permute-done.3 = bf16[2,128,128]{1,2,0:T(8,128)(2,1)S(1)} collective-permute-done((bf16[2,128,128]{1,2,0:T(8,128)(2,1)S(1)}, bf16[2,128,128]{1,2,0:T(8,128)(2,1)S(1)}, u32[]{:S(2)}, u32[]{:S(2)}) %collective-permute-start.3) | collective-permute-done | bytes 65568 | tf_op jit(solution)/shard_map/ppermute | solution.py:90
  40.2 1.9 %collective-permute-done.4 = bf16[2,128,128]{1,2,0:T(8,128)(2,1)S(1)} collective-permute-done((bf16[2,128,128]{1,2,0:T(8,128)(2,1)S(1)}, bf16[2,128,128]{1,2,0:T(8,128)(2,1)S(1)}, u32[]{:S(2)}, u32[]{:S(2)}) %collective-permute-start.4) | collective-permute-done | bytes 65568 | tf_op jit(solution)/shard_map/ppermute | solution.py:90
  42.8 0.6 fusion.57
  43.9 1.0 %fusion.7 = bf16[1,128,512]{1,2,0:T(8,128)(2,1)S(1)} fusion(f32[512,1024]{1,0:T(8,128)S(1)} %bitcast.114, f32[128,512]{1,0:T(8,128)S(1)} %get-tuple-element.50, f32[128,512]{1,0:T(8,128)S(1)} %get-tuple-element.51, f32[1024]{0:T(1024)S(1)} %fusion.90), kind=kOutput, calls=%fused_computation.18 | convolution fusion | flops 402980864 | bytes 2756608 | tf_op jit(solution)/shard_map/dot_general | solution.py:172
  45.0 1.0 %fusion.8 = bf16[1,128,512]{1,2,0:T(8,128)(2,1)S(1)} fusion(f32[512,1024]{1,0:T(8,128)S(1)} %bitcast.115, f32[128,512]{1,0:T(8,128)S(1)} %get-tuple-element.52, f32[128,512]{1,0:T(8,128)S(1)} %get-tuple-element.28, f32[1024]{0:T(1024)S(1)} %fusion.90), kind=kOutput, calls=%fused_computation.19 | convolution fusion | flops 402980864 | bytes 2756608 | tf_op jit(solution)/shard_map/dot_general | solution.py:172
  46.1 2.0 %collective-permute-start.6 = (bf16[2,128,128]{1,2,0:T(8,128)(2,1)S(1)}, bf16[2,128,128]{1,2,0:T(8,128)(2,1)S(1)}, u32[]{:S(2)}, u32[]{:S(2)}) collective-permute-start(bf16[2,128,128]{1,2,0:T(8,128)(2,1)S(1)} %get-tuple-element.70), channel_id=1, source_target_pairs={{0,12},{4,8},{8,4},{12,0},{1,13},{5,9},{9,5},{13,1},{2,14},{6,10},... | collective-permute-start | bytes 196616 | tf_op jit(solution)/shard_map/ppermute | solution.py:90
  48.1 2.5 %collective-permute-start.8 = (bf16[2,128,128]{1,2,0:T(8,128)(2,1)S(1)}, bf16[2,128,128]{1,2,0:T(8,128)(2,1)S(1)}, u32[]{:S(2)}, u32[]{:S(2)}) collective-permute-start(bf16[2,128,128]{1,2,0:T(8,128)(2,1)S(1)} %get-tuple-element.23), channel_id=1, source_target_pairs={{0,4},{4,0},{8,12},{12,8},{1,5},{5,1},{9,13},{13,9},{2,6},{6,2},{1... | collective-permute-start | bytes 196616 | tf_op jit(solution)/shard_map/ppermute | solution.py:90
  50.8 1.5 %collective-permute-done.6 = bf16[2,128,128]{1,2,0:T(8,128)(2,1)S(1)} collective-permute-done((bf16[2,128,128]{1,2,0:T(8,128)(2,1)S(1)}, bf16[2,128,128]{1,2,0:T(8,128)(2,1)S(1)}, u32[]{:S(2)}, u32[]{:S(2)}) %collective-permute-start.6) | collective-permute-done | bytes 65568 | tf_op jit(solution)/shard_map/ppermute | solution.py:90
  52.3 1.8 %collective-permute-done.7 = bf16[2,128,128]{1,2,0:T(8,128)(2,1)S(1)} collective-permute-done((bf16[2,128,128]{1,2,0:T(8,128)(2,1)S(1)}, bf16[2,128,128]{1,2,0:T(8,128)(2,1)S(1)}, u32[]{:S(2)}, u32[]{:S(2)}) %collective-permute-start.7) | collective-permute-done | bytes 65568 | tf_op jit(solution)/shard_map/ppermute | solution.py:90
  54.3 1.2 %fusion.3 = f32[128]{0:T(128)S(1)} fusion(f32[3,512,128]{1,2,0:T(8,128)S(1)} %convolution_bitcast_fusion.1, bf16[2048,3,512]{2,0,1:T(8,128)(2,1)S(1)} %bitcast.118, f32[128,2048]{1,0:T(8,128)S(1)} %get-tuple-element.86, f32[2048]{0:T(1024)S(1)} %copy-done.6, f32[128]{0:T(128)S(1)} %add_rsqrt_fusion, bf16[1,512,128]{1,2,0:T(8,128)(2,1)S(1)} %get-tuple-element.45, ...), kind=kOutput, calls=%fused_computation.9 | convolution fusion | flops 808058752 | bytes 8528896 | tf_op jit(solution)/shard_map/dr,dmc->mcr/dot_general | solution.py:237
  55.5 2.2 %fusion.9 = (f32[2048]{0:T(1024)S(1)}, f32[128,2048,1]{1,0,2:T(8,128)S(1)}) fusion(f32[128,2048]{1,0:T(8,128)S(1)} %get-tuple-element.86, f32[128]{0:T(128)S(1)} %add_rsqrt_fusion, bf16[2048,3,512]{2,0,1:T(8,128)(2,1)S(1)} %bitcast.118, bf16[1,512,128]{1,2,0:T(8,128)(2,1)S(1)} %get-tuple-element.45, bf16[1,512,128]{1,2,0:T(8,128)(2,1)S(1)} %get-tuple-element.44, ...), kind=kOutput, calls=%fused_computation.21 | convolution fusion | flops 806483968 | bytes 8790528 | tf_op jit(solution)/shard_map/mcr,dmc->rd/dot_general | solution.py:274
  57.7 0.6 convolution_multiply_fusion.1
  58.3 0.7 fusion
  59.2 1.6 %collective-permute-start.10 = (f32[149,512]{1,0:T(8,128)S(1)}, f32[149,512]{1,0:T(8,128)S(1)}, u32[]{:S(2)}, u32[]{:S(2)}) collective-permute-start(f32[149,512]{1,0:T(8,128)S(1)} %get-tuple-element.61), channel_id=1, source_target_pairs={{0,2},{1,3},{2,0},{3,1},{4,6},{5,7},{6,4},{7,5},{8,10},{9,11},{10,... | collective-permute-start | bytes 915464 | tf_op jit(solution)/shard_map/ppermute | solution.py:90
  60.8 0.6 collective-permute-start.9
  61.4 1.9 %convolution_bitcast_fusion.3 = f32[1,1,128,512]{3,2,1,0:T(8,128)} fusion(f32[512,1024]{1,0:T(8,128)S(1)} %bitcast.116, f32[128,512]{1,0:T(8,128)S(1)} %get-tuple-element.54, f32[128,512]{1,0:T(8,128)S(1)} %get-tuple-element.53, f32[1024]{0:T(1024)S(1)} %fusion.90), kind=kOutput, calls=%fused_computation.10 | convolution fusion | flops 402915328 | bytes 2887680 | tf_op jit(solution)/shard_map/dot_general | solution.py:172
  63.6 5.9 %collective-permute-done.10 = f32[149,512]{1,0:T(8,128)S(1)} collective-permute-done((f32[149,512]{1,0:T(8,128)S(1)}, f32[149,512]{1,0:T(8,128)S(1)}, u32[]{:S(2)}, u32[]{:S(2)}) %collective-permute-start.10) | collective-permute-done | bytes 305184 | tf_op jit(solution)/shard_map/ppermute | solution.py:90
  69.5 4.2 %collective-permute-done.11 = f32[149,512]{1,0:T(8,128)S(1)} collective-permute-done((f32[149,512]{1,0:T(8,128)S(1)}, f32[149,512]{1,0:T(8,128)S(1)}, u32[]{:S(2)}, u32[]{:S(2)}) %collective-permute-start.11) | collective-permute-done | bytes 305184 | tf_op jit(solution)/shard_map/ppermute | solution.py:90
  73.8 2.6 %collective-permute-start.12 = (f32[21,512]{1,0:T(8,128)S(1)}, f32[21,512]{1,0:T(8,128)S(1)}, u32[]{:S(2)}, u32[]{:S(2)}) collective-permute-start(f32[21,512]{1,0:T(8,128)S(1)} %fusion.73), channel_id=1, source_target_pairs={{0,12},{4,8},{8,4},{12,0},{1,13},{5,9},{9,5},{13,1},{2,14},{6,10},... | collective-permute-start | bytes 129032 | tf_op jit(solution)/shard_map/ppermute | solution.py:90
  76.3 1.9 %collective-permute-start.14 = (f32[21,512]{1,0:T(8,128)S(1)}, f32[21,512]{1,0:T(8,128)S(1)}, u32[]{:S(2)}, u32[]{:S(2)}) collective-permute-start(f32[21,512]{1,0:T(8,128)S(1)} %fusion.73), channel_id=1, source_target_pairs={{0,4},{4,0},{8,12},{12,8},{1,5},{5,1},{9,13},{13,9},{2,6},{6,2},{1... | collective-permute-start | bytes 129032 | tf_op jit(solution)/shard_map/ppermute | solution.py:90
  78.7 0.9 %fusion.6 = bf16[128,512]{1,0:T(8,128)(2,1)} fusion(f32[128,512]{1,0:T(8,128)S(1)} %fusion.26, f32[128,512]{1,0:T(8,128)S(1)} %convolution_add_fusion.1, bf16[2048,512]{1,0:T(8,128)(2,1)S(1)} %copy-done, s32[]{:T(128)S(6)} %select_n.668, f32[128,2048]{1,0:T(8,128)S(1)} %get-tuple-element.86, s32[]{:T(128)S(6)} %select_n.654, ...), kind=kOutput, calls=%fused_computation.17 | convolution fusion | flops 67371008 | bytes 1572872 | tf_op jit(solution)/shard_map/dot_general | solution.py:287
  79.6 0.6 collective-permute-done.12
  80.2 2.0 %collective-permute-done.13 = f32[21,512]{1,0:T(8,128)S(1)} collective-permute-done((f32[21,512]{1,0:T(8,128)S(1)}, f32[21,512]{1,0:T(8,128)S(1)}, u32[]{:S(2)}, u32[]{:S(2)}) %collective-permute-start.13) | collective-permute-done | bytes 43040 | tf_op jit(solution)/shard_map/ppermute | solution.py:90
  82.3 0.6 slice.289
  82.9 0.6 copy.21
  (85 shorter events, 5.6 us)
Async XLA Ops:
  0.6 1.6 %copy-start = (bf16[2048,512]{1,0:T(8,128)(2,1)S(1)}, bf16[2048,512]{1,0:T(8,128)(2,1)}, u32[]{:S(2)}) copy-start(bf16[2048,512]{1,0:T(8,128)(2,1)} %param.12) | copy-start | bytes 6291460
  3.9 2.1 %copy-start.11 = (s32[128]{0:T(128)S(1)}, s32[128]{0:T(128)}, u32[]{:S(2)}) copy-start(s32[128]{0:T(128)} %param.7) | copy-start | bytes 1540
  4.0 0.7 copy-start.3
  5.6 17.8 %collective-permute-start.1 = (f32[128,1024]{1,0:T(8,128)}, f32[128,1024]{1,0:T(8,128)}, u32[]{:S(2)}, u32[]{:S(2)}) collective-permute-start(f32[128,1024]{1,0:T(8,128)} %fusion.37), channel_id=1, source_target_pairs={{0,1},{1,0},{2,3},{3,2},{4,5},{5,4},{6,7},{7,6},{8,9},{9,8},{10,11... | collective-permute-start | bytes 1572872 | tf_op jit(solution)/shard_map/ppermute | solution.py:46
  6.7 13.9 %collective-permute-start = (s32[3]{0:T(128)}, s32[3]{0:T(128)}, u32[]{:S(2)}, u32[]{:S(2)}) collective-permute-start(s32[3]{0:T(128)} %slice_add_fusion.5), channel_id=1, source_target_pairs={{0,4},{4,8},{8,12},{1,5},{5,9},{9,13},{2,6},{6,10},{10,14},{3,7},{... | collective-permute-start | bytes 44 | tf_op jit(solution)/shard_map/ppermute | solution.py:16
  13.0 2.9 %copy-start.1 = (f32[16,32,1024]{2,1,0:T(8,128)}, f32[16,32,1024]{2,1,0:T(8,128)S(1)}, u32[]{:S(2)}) copy-start(f32[16,32,1024]{2,1,0:T(8,128)S(1)} %multiply_subtract_fusion) | copy-start | bytes 6291460
  19.2 4.3 %copy-start.4 = (f32[128,512]{1,0:T(8,128)S(1)}, f32[128,512]{1,0:T(8,128)}, u32[]{:S(2)}) copy-start(f32[128,512]{1,0:T(8,128)} %copy-done.3) | copy-start | bytes 786436
  20.6 5.6 %copy-start.6 = (f32[2048]{0:T(1024)S(1)}, f32[2048]{0:T(1024)}, u32[]{:S(2)}) copy-start(f32[2048]{0:T(1024)} %param.9) | copy-start | bytes 24580
  24.6 8.5 %collective-permute-start.2 = (f32[128,512]{1,0:T(8,128)S(1)}, f32[128,512]{1,0:T(8,128)S(1)}, u32[]{:S(2)}, u32[]{:S(2)}) collective-permute-start(f32[128,512]{1,0:T(8,128)S(1)} %slice_select_fusion), channel_id=1, source_target_pairs={{0,2},{2,0},{1,3},{3,1},{4,6},{6,4},{5,7},{7,5},{8,10},{10,8},{9,1... | collective-permute-start | bytes 786440 | tf_op jit(solution)/shard_map/ppermute | solution.py:46
  30.1 7.7 %copy-start.5 = (bf16[128,512]{1,0:T(8,128)(2,1)S(1)}, bf16[128,512]{1,0:T(8,128)(2,1)}, u32[]{:S(2)}) copy-start(bf16[128,512]{1,0:T(8,128)(2,1)} %param.13) | copy-start | bytes 393220
  30.1 12.1 %copy-start.2 = (f32[16,32,1024]{2,1,0:T(8,128)S(1)}, f32[16,32,1024]{2,1,0:T(8,128)}, u32[]{:S(2)}) copy-start(f32[16,32,1024]{2,1,0:T(8,128)} %copy-done.1) | copy-start | bytes 6291460
  33.3 6.8 %collective-permute-start.3 = (bf16[2,128,128]{1,2,0:T(8,128)(2,1)S(1)}, bf16[2,128,128]{1,2,0:T(8,128)(2,1)S(1)}, u32[]{:S(2)}, u32[]{:S(2)}) collective-permute-start(bf16[2,128,128]{1,2,0:T(8,128)(2,1)S(1)} %get-tuple-element.75), channel_id=1, source_target_pairs={{0,12},{4,8},{8,4},{12,0},{1,13},{5,9},{9,5},{13,1},{2,14},{6,10},... | collective-permute-start | bytes 196616 | tf_op jit(solution)/shard_map/ppermute | solution.py:90
  34.6 7.5 %collective-permute-start.4 = (bf16[2,128,128]{1,2,0:T(8,128)(2,1)S(1)}, bf16[2,128,128]{1,2,0:T(8,128)(2,1)S(1)}, u32[]{:S(2)}, u32[]{:S(2)}) collective-permute-start(bf16[2,128,128]{1,2,0:T(8,128)(2,1)S(1)} %get-tuple-element.74), channel_id=1, source_target_pairs={{0,8},{4,12},{8,0},{12,4},{1,9},{5,13},{9,1},{13,5},{2,10},{6,14},... | collective-permute-start | bytes 196616 | tf_op jit(solution)/shard_map/ppermute | solution.py:90
  35.9 6.2 %collective-permute-start.5 = (bf16[2,128,128]{1,2,0:T(8,128)(2,1)S(1)}, bf16[2,128,128]{1,2,0:T(8,128)(2,1)S(1)}, u32[]{:S(2)}, u32[]{:S(2)}) collective-permute-start(bf16[2,128,128]{1,2,0:T(8,128)(2,1)S(1)} %get-tuple-element.33), channel_id=1, source_target_pairs={{0,4},{4,0},{8,12},{12,8},{1,5},{5,1},{9,13},{13,9},{2,6},{6,2},{1... | collective-permute-start | bytes 196616 | tf_op jit(solution)/shard_map/ppermute | solution.py:90
  42.2 1.2 %copy-start.7 = (pred[512]{0:T(512)(128)(4,1)S(1)}, pred[512]{0:T(512)(128)(4,1)}, u32[]{:S(2)}) copy-start(pred[512]{0:T(512)(128)(4,1)} %iota_compare_fusion.6) | copy-start | bytes 1540
  43.8 10.5 %slice-start = ((s8[6291456]{0:T(1024)(128)(4,1)}), s8[4194304]{0:T(1024)(128)(4,1)S(1)}, s32[]{:S(2)}) async-start(s8[6291456]{0:T(1024)(128)(4,1)} %bitcast.117), calls=%async_computation | async-start | bytes 8388608
  44.9 5.6 %copy-start.8 = (s32[128]{0:T(128)S(1)}, s32[128]{0:T(128)}, u32[]{:S(2)}) copy-start(s32[128]{0:T(128)} %get-tuple-element.93) | copy-start | bytes 1540
  44.9 5.6 %copy-start.9 = (s32[128]{0:T(128)S(1)}, s32[128]{0:T(128)}, u32[]{:S(2)}) copy-start(s32[128]{0:T(128)} %get-tuple-element.94) | copy-start | bytes 1540
  44.9 5.6 %copy-start.10 = (pred[128]{0:T(512)(128)(4,1)S(1)}, pred[128]{0:T(512)(128)(4,1)}, u32[]{:S(2)}) copy-start(pred[128]{0:T(512)(128)(4,1)} %compare_and_fusion) | copy-start | bytes 388
  46.0 8.3 %slice-start.1 = ((s8[6291456]{0:T(1024)(128)(4,1)}), s8[2097152]{0:T(1024)(128)(4,1)S(1)}, s32[]{:S(2)}) async-start(s8[6291456]{0:T(1024)(128)(4,1)} %bitcast.117), calls=%async_computation.1 | async-start | bytes 4194304
  46.1 6.2 %collective-permute-start.6 = (bf16[2,128,128]{1,2,0:T(8,128)(2,1)S(1)}, bf16[2,128,128]{1,2,0:T(8,128)(2,1)S(1)}, u32[]{:S(2)}, u32[]{:S(2)}) collective-permute-start(bf16[2,128,128]{1,2,0:T(8,128)(2,1)S(1)} %get-tuple-element.70), channel_id=1, source_target_pairs={{0,12},{4,8},{8,4},{12,0},{1,13},{5,9},{9,5},{13,1},{2,14},{6,10},... | collective-permute-start | bytes 196616 | tf_op jit(solution)/shard_map/ppermute | solution.py:90
  48.1 6.0 %collective-permute-start.7 = (bf16[2,128,128]{1,2,0:T(8,128)(2,1)S(1)}, bf16[2,128,128]{1,2,0:T(8,128)(2,1)S(1)}, u32[]{:S(2)}, u32[]{:S(2)}) collective-permute-start(bf16[2,128,128]{1,2,0:T(8,128)(2,1)S(1)} %get-tuple-element.69), channel_id=1, source_target_pairs={{0,8},{4,12},{8,0},{12,4},{1,9},{5,13},{9,1},{13,5},{2,10},{6,14},... | collective-permute-start | bytes 196616 | tf_op jit(solution)/shard_map/ppermute | solution.py:90
  48.1 6.0 %collective-permute-start.8 = (bf16[2,128,128]{1,2,0:T(8,128)(2,1)S(1)}, bf16[2,128,128]{1,2,0:T(8,128)(2,1)S(1)}, u32[]{:S(2)}, u32[]{:S(2)}) collective-permute-start(bf16[2,128,128]{1,2,0:T(8,128)(2,1)S(1)} %get-tuple-element.23), channel_id=1, source_target_pairs={{0,4},{4,0},{8,12},{12,8},{1,5},{5,1},{9,13},{13,9},{2,6},{6,2},{1... | collective-permute-start | bytes 196616 | tf_op jit(solution)/shard_map/ppermute | solution.py:90
  59.2 10.3 %collective-permute-start.10 = (f32[149,512]{1,0:T(8,128)S(1)}, f32[149,512]{1,0:T(8,128)S(1)}, u32[]{:S(2)}, u32[]{:S(2)}) collective-permute-start(f32[149,512]{1,0:T(8,128)S(1)} %get-tuple-element.61), channel_id=1, source_target_pairs={{0,2},{1,3},{2,0},{3,1},{4,6},{5,7},{6,4},{7,5},{8,10},{9,11},{10,... | collective-permute-start | bytes 915464 | tf_op jit(solution)/shard_map/ppermute | solution.py:90
  60.8 13.0 %collective-permute-start.11 = (f32[149,512]{1,0:T(8,128)S(1)}, f32[149,512]{1,0:T(8,128)S(1)}, u32[]{:S(2)}, u32[]{:S(2)}) collective-permute-start(f32[149,512]{1,0:T(8,128)S(1)} %get-tuple-element.62), channel_id=1, source_target_pairs={{0,3},{1,2},{2,1},{3,0},{4,7},{5,6},{6,5},{7,4},{8,11},{9,10},{10,... | collective-permute-start | bytes 915464 | tf_op jit(solution)/shard_map/ppermute | solution.py:90
  60.8 13.0 %collective-permute-start.9 = (f32[149,512]{1,0:T(8,128)S(1)}, f32[149,512]{1,0:T(8,128)S(1)}, u32[]{:S(2)}, u32[]{:S(2)}) collective-permute-start(f32[149,512]{1,0:T(8,128)S(1)} %get-tuple-element.63), channel_id=1, source_target_pairs={{0,1},{1,0},{2,3},{3,2},{4,5},{5,4},{6,7},{7,6},{8,9},{9,8},{10,11... | collective-permute-start | bytes 915464 | tf_op jit(solution)/shard_map/ppermute | solution.py:90
  73.8 6.5 %collective-permute-start.12 = (f32[21,512]{1,0:T(8,128)S(1)}, f32[21,512]{1,0:T(8,128)S(1)}, u32[]{:S(2)}, u32[]{:S(2)}) collective-permute-start(f32[21,512]{1,0:T(8,128)S(1)} %fusion.73), channel_id=1, source_target_pairs={{0,12},{4,8},{8,4},{12,0},{1,13},{5,9},{9,5},{13,1},{2,14},{6,10},... | collective-permute-start | bytes 129032 | tf_op jit(solution)/shard_map/ppermute | solution.py:90
  76.3 5.9 %collective-permute-start.13 = (f32[21,512]{1,0:T(8,128)S(1)}, f32[21,512]{1,0:T(8,128)S(1)}, u32[]{:S(2)}, u32[]{:S(2)}) collective-permute-start(f32[21,512]{1,0:T(8,128)S(1)} %fusion.73), channel_id=1, source_target_pairs={{0,8},{4,12},{8,0},{12,4},{1,9},{5,13},{9,1},{13,5},{2,10},{6,14},... | collective-permute-start | bytes 129032 | tf_op jit(solution)/shard_map/ppermute | solution.py:90
  76.3 5.9 %collective-permute-start.14 = (f32[21,512]{1,0:T(8,128)S(1)}, f32[21,512]{1,0:T(8,128)S(1)}, u32[]{:S(2)}, u32[]{:S(2)}) collective-permute-start(f32[21,512]{1,0:T(8,128)S(1)} %fusion.73), channel_id=1, source_target_pairs={{0,4},{4,0},{8,12},{12,8},{1,5},{5,1},{9,13},{13,9},{2,6},{6,2},{1... | collective-permute-start | bytes 129032 | tf_op jit(solution)/shard_map/ppermute | solution.py:90

commit v6 on v4

--- a/solution.py
+++ b/solution.py
@@ -65,25 +65,17 @@
     return [blocks[c * pairs + p] for p in range(pairs) for c in range(chans)]
 
 
-def ordered(mine, other, first, axis):
-    return jnp.concatenate(
-        [jnp.where(first, mine, other), jnp.where(first, other, mine)], axis=axis
-    )
-
-
 def all_gather_cp(x):
     chans, pairs = lax.axis_size("chan"), lax.axis_size("pair")
     y = x[None]
-    me, step = lax.axis_index("chan"), 1
-    while step < chans:
-        y = ordered(y, xor_exchange(y, "chan", step), (me // step) % 2 == 0, 0)
-        step *= 2
-    y = y[:, None]
-    me, step = lax.axis_index("pair"), 1
-    while step < pairs:
-        y = ordered(y, xor_exchange(y, "pair", step), (me // step) % 2 == 0, 1)
-        step *= 2
-    return y.reshape((chans * pairs * x.shape[0],) + x.shape[1:])
+    sources = [lax.axis_index(("chan", "pair"))]
+    for axis, size, stride in (("chan", chans, pairs), ("pair", pairs, 1)):
+        step = 1
+        while step < size:
+            y = jnp.concatenate([y, xor_exchange(y, axis, step)], axis=0)
+            sources = sources + [source ^ (step * stride) for source in sources]
+            step *= 2
+    return y, sources
 
 
 def group_exchange(x, axes, count, offset):
@@ -259,10 +251,15 @@
     conv_rows, d_mixed = both_rows[0], both_rows[1]
     gated_rows = (query_part * conv_rows.astype(jnp.float32)).astype(jnp.bfloat16)
     weight_rows = out_proj
+    gathered, sources = all_gather_cp(gated_rows)
+    weight_order = jnp.concatenate(
+        [lax.dynamic_slice_in_dim(weight_rows, src * local_width, local_width, 0) for src in sources],
+        axis=0,
+    )
     mixed_out = jnp.einsum(
         "cr,cd->rd",
-        all_gather_cp(gated_rows),
-        weight_rows,
+        gathered.reshape(-1, gathered.shape[-1]),
+        weight_order,
         preferred_element_type=jnp.float32,
     )
     own_rows = lax.dynamic_slice_in_dim(embedded, group_index * local_width, local_width, 0)

time: 78.1 us -> 75.6 us (0.968)
  other arithmetic: 11.9 us -> 9.63 us
    dynamic_slice x0 -> x1, local copies, waits for them, and re-layouts: none -> 2.94 us  [per_device(): lax.dynamic_slice_in_dim(weight_rows, src * local_width, local_width, 0)]
    concatenate x1, local copies, waits for them, and re-layouts: 2.05 us -> 0.27 us  [all_gather_cp(): y = jnp.concatenate([y, xor_exchange(y, axis, step)], axis=0)]
    select_n x2 -> x0, other arithmetic: 1.01 us -> none  [ordered(): jnp.where(first, mine, other)]
    concatenate x1 -> x2, other arithmetic: 0.85 us -> 1.78 us  [all_gather_cp(): y = jnp.concatenate([y, xor_exchange(y, axis, step)], axis=0)]
    dot_general x1, matrix products: 1.32 us -> 0.43 us  [per_device(): embedded = jnp.dot(table_t, onehot_t, preferred_element_type=jnp.float32)]
    unnamed x38 -> x52, local copies, waits for them, and re-layouts: 4.59 us -> 3.73 us
    dot_general x1, matrix products: 1.71 us -> 2.51 us  [per_device(): jnp.einsum('rd,cd->rc', cotangent, out_proj, preferred_element_type=jnp.f...]
  transfers between devices with their start and end apart: 17 -> 17, of which waited for: 8 -> 7; matrix products, arithmetic and copies ran while one was open for 23% -> 25% of each run, Pallas kernels for 0% -> 0%
where the time goes in v6:
time: 75.6 us; the launch traced here: 75.2 us
  starting transfers between devices  24.1 us (32%)
  matrix products  19.9 us (26%)
  waiting for transfers between devices  11.8 us (16%)
  other arithmetic  9.63 us (13%)
  local copies, waits for them, and re-layouts  8.47 us (11%)
  between operations  1.27 us (2%)
    ppermute x12, starting transfers between devices, group_exchange(): return lax.ppermute(x, axes, [(i, i ^ offset) for i in range(count)])  15.6 us
    ppermute x12, waiting for transfers between devices, group_exchange(): return lax.ppermute(x, axes, [(i, i ^ offset) for i in range(count)])  8.77 us
    ppermute x1, starting transfers between devices, from_behind(): lax.ppermute(value, axis, [(source, source + steps) for source in range(f...  4.94 us
    dot_general x3, matrix products, inverse_dft(): lax.dot_general(spec * weight, dft, (((1,), (1,)), ((), ())), precision=T...  3.87 us
    dot_general x1, matrix products, per_device(): jnp.einsum('dr,dmc->mcr', hidden, in_proj, preferred_element_type=jnp.flo...  3.82 us
    unnamed x52, local copies, waits for them, and re-layouts  3.73 us
    ppermute x4, starting transfers between devices, xor_exchange(): return lax.ppermute(x, axis, [(i, i ^ step) for i in range(count)])  3.61 us
    ppermute x4, waiting for transfers between devices, xor_exchange(): return lax.ppermute(x, axis, [(i, i ^ step) for i in range(count)])  3.07 us
  transfers between devices with their start and end apart: 17, of which 7 were waited for; matrix products, arithmetic and copies ran while one was open for 25% of the time, Pallas kernels for 0%

profile of v6, /device:TPU:0, one launch (start us, length us, event | category | flops | bytes accessed | tf_op | source)
XLA Modules:
  0.0 75.2 jit_solution(14255901959985889119)
XLA Ops:
  0.7 2.5 %fusion.116 = f32[128,2048]{1,0:T(8,128)S(1)} fusion(bf16[128,512]{1,0:T(8,128)(2,1)} %param.13, bf16[2048,512]{1,0:T(8,128)(2,1)} %param.12), kind=kOutput, calls=%fused_computation.234 | convolution fusion | flops 268435456 | bytes 3276800 | tf_op jit(solution)/shard_map/rd,cd->rc/dot_general | solution.py:231
  3.3 0.7 copy-done.3
  4.0 0.8 %fusion.42 = f32[128,1024]{1,0:T(8,128)} fusion(f32[128,512]{1,0:T(8,128)S(1)} %get-tuple-element.52, f32[128,512]{1,0:T(8,128)S(1)} %get-tuple-element.53, f32[128,512]{1,0:T(8,128)S(1)} %get-tuple-element.54, f32[128,512]{1,0:T(8,128)S(1)} %get-tuple-element.51, pred[]{:T(512)S(6)} %eq.262), kind=kLoop, calls=%fused_computation.65 | loop fusion | flops 393216 | bytes 1572865 | tf_op jit(solution)/shard_map/jit(_where)/select_n | solution.py:57
  5.3 0.6 slice_add_fusion.2
  5.9 4.9 %collective-permute-start = (s32[3]{0:T(128)}, s32[3]{0:T(128)}, u32[]{:S(2)}, u32[]{:S(2)}) collective-permute-start(s32[3]{0:T(128)} %slice_add_fusion.2), channel_id=1, source_target_pairs={{0,4},{4,8},{8,12},{1,5},{5,9},{9,13},{2,6},{6,10},{10,14},{3,7},{... | collective-permute-start | bytes 44 | tf_op jit(solution)/shard_map/ppermute | solution.py:16
  11.3 0.6 fusion.75
  12.2 0.7 convolution_bitcast_fusion.2
  13.0 0.7 copy-done.1
  13.7 0.6 iota_and_fusion.1
  14.3 0.6 compare_and_fusion
  15.4 0.9 %copy.19 = bf16[4,5,2048]{2,1,0:T(8,128)(2,1)S(1)} copy(bf16[4,5,2048]{2,0,1:T(4,128)(2,1)} %param.8) | data formatting | bytes 163840 | tf_op args[1]
  16.3 0.7 reshape.265
  17.0 2.9 %constant_dynamic-slice_fusion.3 = (bf16[512,512]{1,0:T(8,128)(2,1)}, bf16[512,512]{1,0:T(8,128)(2,1)}, bf16[512,512]{1,0:T(8,128)(2,1)}, bf16[512,512]{1,0:T(8,128)(2,1)}) fusion(bf16[2048,512]{1,0:T(8,128)(2,1)} %param.12, s32[]{:T(128)S(6)} %select_n.654, s32[]{:T(128)S(6)} %select_n.655, s32[]{:T(128)S(6)} %select_n.657, s32[]{:T(128)S(6)} %select_n.656), kind=kLoop, calls=%fused_computation.215 | loop fusion | bytes 4194320 | tf_op jit(solution)/shard_map/dynamic_slice | solution.py:256
  20.2 0.7 broadcast_add_fusion.1
  21.6 1.1 %select_add_fusion = f32[128,1024]{1,0:T(8,128)S(1)} fusion(f32[128,1024]{1,0:T(8,128)} %collective-permute-done.1, f32[128,512]{1,0:T(8,128)S(1)} %copy-done.6, f32[128,512]{1,0:T(8,128)S(1)} %copy-done.8, f32[128,512]{1,0:T(8,128)S(1)} %copy-done.10, f32[128,512]{1,0:T(8,128)S(1)} %copy-done.4, pred[]{:T(512)S(6)} %eq.262), kind=kLoop, calls=%fused_computation.58 | loop fusion | flops 524288 | bytes 2097153 | tf_op jit(solution)/shard_map/add | solution.py:58
  22.7 1.6 %collective-permute-start.2 = (f32[128,512]{1,0:T(8,128)S(1)}, f32[128,512]{1,0:T(8,128)S(1)}, u32[]{:S(2)}, u32[]{:S(2)}) collective-permute-start(f32[128,512]{1,0:T(8,128)S(1)} %slice_select_fusion), channel_id=1, source_target_pairs={{0,2},{2,0},{1,3},{3,1},{4,6},{6,4},{5,7},{7,5},{8,10},{10,8},{9,1... | collective-permute-start | bytes 786440 | tf_op jit(solution)/shard_map/ppermute | solution.py:46
  24.3 3.8 %convolution_bitcast_fusion.1 = f32[3,512,128]{1,2,0:T(8,128)S(1)} fusion(bf16[2048,3,512]{2,0,1:T(8,128)(2,1)} %param.10, f32[128,2048]{1,0:T(8,128)S(1)} %get-tuple-element.86, f32[2048]{0:T(1024)S(1)} %copy-done.16, f32[128]{0:T(128)S(1)} %add_rsqrt_fusion), kind=kOutput, calls=%fused_computation.13 | convolution fusion | flops 806092800 | bytes 8135168 | tf_op jit(solution)/shard_map/dr,dmc->mcr/dot_general | solution.py:220
  28.2 3.1 %collective-permute-done.2 = f32[128,512]{1,0:T(8,128)S(1)} collective-permute-done((f32[128,512]{1,0:T(8,128)S(1)}, f32[128,512]{1,0:T(8,128)S(1)}, u32[]{:S(2)}, u32[]{:S(2)}) %collective-permute-start.2) | collective-permute-done | bytes 262176 | tf_op jit(solution)/shard_map/ppermute | solution.py:46
  31.4 1.3 %collective-permute-start.3 = (bf16[2,128,128]{1,2,0:T(8,128)(2,1)S(1)}, bf16[2,128,128]{1,2,0:T(8,128)(2,1)S(1)}, u32[]{:S(2)}, u32[]{:S(2)}) collective-permute-start(bf16[2,128,128]{1,2,0:T(8,128)(2,1)S(1)} %get-tuple-element.75), channel_id=1, source_target_pairs={{0,12},{4,8},{8,4},{12,0},{1,13},{5,9},{9,5},{13,1},{2,14},{6,10},... | collective-permute-start | bytes 196616 | tf_op jit(solution)/shard_map/ppermute | solution.py:82
  32.8 1.3 %collective-permute-start.4 = (bf16[2,128,128]{1,2,0:T(8,128)(2,1)S(1)}, bf16[2,128,128]{1,2,0:T(8,128)(2,1)S(1)}, u32[]{:S(2)}, u32[]{:S(2)}) collective-permute-start(bf16[2,128,128]{1,2,0:T(8,128)(2,1)S(1)} %get-tuple-element.74), channel_id=1, source_target_pairs={{0,8},{4,12},{8,0},{12,4},{1,9},{5,13},{9,1},{13,5},{2,10},{6,14},... | collective-permute-start | bytes 196616 | tf_op jit(solution)/shard_map/ppermute | solution.py:82
  34.1 1.8 %collective-permute-start.5 = (bf16[2,128,128]{1,2,0:T(8,128)(2,1)S(1)}, bf16[2,128,128]{1,2,0:T(8,128)(2,1)S(1)}, u32[]{:S(2)}, u32[]{:S(2)}) collective-permute-start(bf16[2,128,128]{1,2,0:T(8,128)(2,1)S(1)} %get-tuple-element.33), channel_id=1, source_target_pairs={{0,4},{4,0},{8,12},{12,8},{1,5},{5,1},{9,13},{13,9},{2,6},{6,2},{1... | collective-permute-start | bytes 196616 | tf_op jit(solution)/shard_map/ppermute | solution.py:82
  36.1 2.1 %collective-permute-done.3 = bf16[2,128,128]{1,2,0:T(8,128)(2,1)S(1)} collective-permute-done((bf16[2,128,128]{1,2,0:T(8,128)(2,1)S(1)}, bf16[2,128,128]{1,2,0:T(8,128)(2,1)S(1)}, u32[]{:S(2)}, u32[]{:S(2)}) %collective-permute-start.3) | collective-permute-done | bytes 65568 | tf_op jit(solution)/shard_map/ppermute | solution.py:82
  38.3 1.9 %collective-permute-done.4 = bf16[2,128,128]{1,2,0:T(8,128)(2,1)S(1)} collective-permute-done((bf16[2,128,128]{1,2,0:T(8,128)(2,1)S(1)}, bf16[2,128,128]{1,2,0:T(8,128)(2,1)S(1)}, u32[]{:S(2)}, u32[]{:S(2)}) %collective-permute-start.4) | collective-permute-done | bytes 65568 | tf_op jit(solution)/shard_map/ppermute | solution.py:82
  40.3 0.6 fusion.62
  40.8 0.6 fusion.63
  41.9 1.0 %fusion.18 = bf16[1,128,512]{1,2,0:T(8,128)(2,1)S(1)} fusion(f32[512,1024]{1,0:T(8,128)S(1)} %bitcast.105, f32[128,512]{1,0:T(8,128)S(1)} %get-tuple-element.55, f32[128,512]{1,0:T(8,128)S(1)} %get-tuple-element.56, f32[1024]{0:T(1024)S(1)} %fusion.95), kind=kOutput, calls=%fused_computation.23 | convolution fusion | flops 402980864 | bytes 2756608 | tf_op jit(solution)/shard_map/dot_general | solution.py:157
  42.9 1.0 %fusion.19 = bf16[1,128,512]{1,2,0:T(8,128)(2,1)S(1)} fusion(f32[512,1024]{1,0:T(8,128)S(1)} %bitcast.106, f32[128,512]{1,0:T(8,128)S(1)} %get-tuple-element.57, f32[128,512]{1,0:T(8,128)S(1)} %get-tuple-element.28, f32[1024]{0:T(1024)S(1)} %fusion.95), kind=kOutput, calls=%fused_computation.24 | convolution fusion | flops 402980864 | bytes 2756608 | tf_op jit(solution)/shard_map/dot_general | solution.py:157
  44.0 2.1 %collective-permute-start.6 = (bf16[2,128,128]{1,2,0:T(8,128)(2,1)S(1)}, bf16[2,128,128]{1,2,0:T(8,128)(2,1)S(1)}, u32[]{:S(2)}, u32[]{:S(2)}) collective-permute-start(bf16[2,128,128]{1,2,0:T(8,128)(2,1)S(1)} %get-tuple-element.70), channel_id=1, source_target_pairs={{0,12},{4,8},{8,4},{12,0},{1,13},{5,9},{9,5},{13,1},{2,14},{6,10},... | collective-permute-start | bytes 196616 | tf_op jit(solution)/shard_map/ppermute | solution.py:82
  46.1 2.4 %collective-permute-start.8 = (bf16[2,128,128]{1,2,0:T(8,128)(2,1)S(1)}, bf16[2,128,128]{1,2,0:T(8,128)(2,1)S(1)}, u32[]{:S(2)}, u32[]{:S(2)}) collective-permute-start(bf16[2,128,128]{1,2,0:T(8,128)(2,1)S(1)} %get-tuple-element.23), channel_id=1, source_target_pairs={{0,4},{4,0},{8,12},{12,8},{1,5},{5,1},{9,13},{13,9},{2,6},{6,2},{1... | collective-permute-start | bytes 196616 | tf_op jit(solution)/shard_map/ppermute | solution.py:82
  48.6 1.5 %collective-permute-done.6 = bf16[2,128,128]{1,2,0:T(8,128)(2,1)S(1)} collective-permute-done((bf16[2,128,128]{1,2,0:T(8,128)(2,1)S(1)}, bf16[2,128,128]{1,2,0:T(8,128)(2,1)S(1)}, u32[]{:S(2)}, u32[]{:S(2)}) %collective-permute-start.6) | collective-permute-done | bytes 65568 | tf_op jit(solution)/shard_map/ppermute | solution.py:82
  50.2 1.8 %collective-permute-done.7 = bf16[2,128,128]{1,2,0:T(8,128)(2,1)S(1)} collective-permute-done((bf16[2,128,128]{1,2,0:T(8,128)(2,1)S(1)}, bf16[2,128,128]{1,2,0:T(8,128)(2,1)S(1)}, u32[]{:S(2)}, u32[]{:S(2)}) %collective-permute-start.7) | collective-permute-done | bytes 65568 | tf_op jit(solution)/shard_map/ppermute | solution.py:82
  52.3 1.3 %fusion.11 = f32[128]{0:T(128)S(1)} fusion(f32[3,512,128]{1,2,0:T(8,128)S(1)} %convolution_bitcast_fusion.1, bf16[2048,3,512]{2,0,1:T(8,128)(2,1)S(1)} %bitcast.109, f32[128,2048]{1,0:T(8,128)S(1)} %get-tuple-element.86, f32[2048]{0:T(1024)S(1)} %copy-done.16, f32[128]{0:T(128)S(1)} %add_rsqrt_fusion, bf16[1,512,128]{1,2,0:T(8,128)(2,1)S(1)} %get-tuple-element.50, ...), kind=kOutput, calls=%fused_computation.17 | convolution fusion | flops 808058752 | bytes 8528896 | tf_op jit(solution)/shard_map/dr,dmc->mcr/dot_general | solution.py:222
  53.5 2.2 %fusion.20 = (f32[2048]{0:T(1024)S(1)}, f32[128,2048,1]{1,0,2:T(8,128)S(1)}) fusion(f32[128,2048]{1,0:T(8,128)S(1)} %get-tuple-element.86, f32[128]{0:T(128)S(1)} %add_rsqrt_fusion, bf16[2048,3,512]{2,0,1:T(8,128)(2,1)S(1)} %bitcast.109, bf16[1,512,128]{1,2,0:T(8,128)(2,1)S(1)} %get-tuple-element.50, bf16[1,512,128]{1,2,0:T(8,128)(2,1)S(1)} %get-tuple-element.48, ...), kind=kOutput, calls=%fused_computation.26 | convolution fusion | flops 806483968 | bytes 8790528 | tf_op jit(solution)/shard_map/mcr,dmc->rd/dot_general | solution.py:273
  55.7 0.6 convolution_multiply_fusion.1
  56.3 0.8 %fusion = f32[20,2048]{1,0:T(8,128)S(1)} fusion(f32[20,2048]{1,0:T(8,128)S(1)} %convolution_multiply_fusion.1, f32[128,2048]{1,0:T(8,128)S(1)} %get-tuple-element.86, f32[128]{0:T(128)S(1)} %add_rsqrt_fusion, f32[128]{0:T(128)S(1)} %fusion.11, pred[128,5]{0,1:T(8,128)(4,1)S(1)} %get-tuple-element.89, pred[128,5]{0,1:T(8,128)(4,1)S(1)} %get-tuple-element.90, ...), kind=kOutput, calls=%fused_computation.1 | convolution fusion | flops 63276544 | bytes 1379840 | tf_op jit(solution)/shard_map/rk,dr->kd/dot_general | solution.py:278
  57.2 1.6 %collective-permute-start.12 = (f32[21,512]{1,0:T(8,128)S(1)}, f32[21,512]{1,0:T(8,128)S(1)}, u32[]{:S(2)}, u32[]{:S(2)}) collective-permute-start(f32[21,512]{1,0:T(8,128)S(1)} %get-tuple-element.76), channel_id=1, source_target_pairs={{0,2},{1,3},{2,0},{3,1},{4,6},{5,7},{6,4},{7,5},{8,10},{9,11},{10,... | collective-permute-start | bytes 129032 | tf_op jit(solution)/shard_map/ppermute | solution.py:82
  58.8 0.6 collective-permute-start.11
  59.5 1.6 %collective-permute-start.9 = (bf16[1,512,128]{1,2,0:T(8,128)(2,1)S(1)}, bf16[1,512,128]{1,2,0:T(8,128)(2,1)S(1)}, u32[]{:S(2)}, u32[]{:S(2)}) collective-permute-start(bf16[1,512,128]{1,2,0:T(8,128)(2,1)S(1)} %get-tuple-element.49), channel_id=1, source_target_pairs={{0,2},{2,0},{1,3},{3,1},{4,6},{6,4},{5,7},{7,5},{8,10},{10,8},{9,1... | collective-permute-start | bytes 393224 | tf_op jit(solution)/shard_map/ppermute | solution.py:46
  61.4 1.1 %collective-permute-done.13 = f32[21,512]{1,0:T(8,128)S(1)} collective-permute-done((f32[21,512]{1,0:T(8,128)S(1)}, f32[21,512]{1,0:T(8,128)S(1)}, u32[]{:S(2)}, u32[]{:S(2)}) %collective-permute-start.13) | collective-permute-done | bytes 43040 | tf_op jit(solution)/shard_map/ppermute | solution.py:82
  62.5 2.6 %collective-permute-start.14 = (f32[21,512]{1,0:T(8,128)S(1)}, f32[21,512]{1,0:T(8,128)S(1)}, u32[]{:S(2)}, u32[]{:S(2)}) collective-permute-start(f32[21,512]{1,0:T(8,128)S(1)} %pad_add_fusion), channel_id=1, source_target_pairs={{0,12},{4,8},{8,4},{12,0},{1,13},{5,9},{9,5},{13,1},{2,14},{6,10},... | collective-permute-start | bytes 129032 | tf_op jit(solution)/shard_map/ppermute | solution.py:82
  65.1 1.9 %collective-permute-start.16 = (f32[21,512]{1,0:T(8,128)S(1)}, f32[21,512]{1,0:T(8,128)S(1)}, u32[]{:S(2)}, u32[]{:S(2)}) collective-permute-start(f32[21,512]{1,0:T(8,128)S(1)} %pad_add_fusion), channel_id=1, source_target_pairs={{0,4},{4,0},{8,12},{12,8},{1,5},{5,1},{9,13},{13,9},{2,6},{6,2},{1... | collective-permute-start | bytes 129032 | tf_op jit(solution)/shard_map/ppermute | solution.py:82
  66.9 0.7 copy-done.12
  67.6 0.7 pad_maximum_fusion.7
  68.3 1.9 %convolution_bitcast_fusion.3 = f32[1,1,128,512]{3,2,1,0:T(8,128)} fusion(f32[512,1024]{1,0:T(8,128)S(1)} %bitcast.107, f32[128,512]{1,0:T(8,128)S(1)} %get-tuple-element.59, f32[128,512]{1,0:T(8,128)S(1)} %get-tuple-element.58, f32[1024]{0:T(1024)S(1)} %fusion.95), kind=kOutput, calls=%fused_computation.18 | convolution fusion | flops 402915328 | bytes 2887680 | tf_op jit(solution)/shard_map/dot_general | solution.py:157
  70.3 0.6 slice.256
  70.9 0.6 copy.23
  71.5 1.0 %pad_maximum_fusion.3 = bf16[4,512,128]{1,2,0:T(8,128)(2,1)S(1)} fusion(bf16[2,512,128]{1,2,0:T(8,128)(2,1)} %collective-permute-done.10, bf16[1,512,128]{1,2,0:T(8,128)(2,1)} %copy-done.12, bf16[1,512,128]{1,2,0:T(8,128)(2,1)S(1)} %get-tuple-element.49), kind=kLoop, calls=%fused_computation.54 | loop fusion | flops 524288 | bytes 1048576 | tf_op jit(solution)/shard_map/concatenate | solution.py:75
  72.9 2.3 %fusion.15 = bf16[128,512]{1,0:T(8,128)(2,1)} fusion(bf16[2048,128]{1,0:T(8,128)(2,1)S(1)} %bitcast.110, bf16[512,512]{1,0:T(8,128)(2,1)} %get-tuple-element.42, bf16[512,512]{1,0:T(8,128)(2,1)} %get-tuple-element.43, bf16[512,512]{1,0:T(8,128)(2,1)S(1)} %copy-done.14, bf16[512,512]{1,0:T(8,128)(2,1)S(1)} %copy-done.13, ...), kind=kOutput, calls=%fused_computation.20 | convolution fusion | flops 276955136 | bytes 3014660 | tf_op jit(solution)/shard_map/cr,cd->rd/dot_general | solution.py:259
  (111 shorter events, 5.0 us)
Async XLA Ops:
  0.6 11.6 %copy-start = (f32[1,1,128,512]{3,2,1,0:T(8,128)S(1)}, f32[1,1,128,512]{3,2,1,0:T(8,128)}, u32[]{:S(2)}) copy-start(f32[1,1,128,512]{3,2,1,0:T(8,128)} %param.11) | copy-start | bytes 786436
  3.2 2.2 %copy-start.21 = (s32[128]{0:T(128)S(1)}, s32[128]{0:T(128)}, u32[]{:S(2)}) copy-start(s32[128]{0:T(128)} %param.7) | copy-start | bytes 1540
  3.3 0.7 copy-start.3
  3.3 1.6 %copy-start.5 = (f32[128,512]{1,0:T(8,128)}, f32[128,512]{1,0:T(8,128)S(1)}, u32[]{:S(2)}) copy-start(f32[128,512]{1,0:T(8,128)S(1)} %get-tuple-element.52) | copy-start | bytes 786436
  3.3 2.0 %copy-start.7 = (f32[128,512]{1,0:T(8,128)}, f32[128,512]{1,0:T(8,128)S(1)}, u32[]{:S(2)}) copy-start(f32[128,512]{1,0:T(8,128)S(1)} %get-tuple-element.53) | copy-start | bytes 786436
  3.3 2.6 %copy-start.9 = (f32[128,512]{1,0:T(8,128)}, f32[128,512]{1,0:T(8,128)S(1)}, u32[]{:S(2)}) copy-start(f32[128,512]{1,0:T(8,128)S(1)} %get-tuple-element.54) | copy-start | bytes 786436
  4.8 16.7 %collective-permute-start.1 = (f32[128,1024]{1,0:T(8,128)}, f32[128,1024]{1,0:T(8,128)}, u32[]{:S(2)}, u32[]{:S(2)}) collective-permute-start(f32[128,1024]{1,0:T(8,128)} %fusion.42), channel_id=1, source_target_pairs={{0,1},{1,0},{2,3},{3,2},{4,5},{5,4},{6,7},{7,6},{8,9},{9,8},{10,11... | collective-permute-start | bytes 1572872 | tf_op jit(solution)/shard_map/ppermute | solution.py:46
  5.9 14.3 %collective-permute-start = (s32[3]{0:T(128)}, s32[3]{0:T(128)}, u32[]{:S(2)}, u32[]{:S(2)}) collective-permute-start(s32[3]{0:T(128)} %slice_add_fusion.2), channel_id=1, source_target_pairs={{0,4},{4,8},{8,12},{1,5},{5,9},{9,13},{2,6},{6,10},{10,14},{3,7},{... | collective-permute-start | bytes 44 | tf_op jit(solution)/shard_map/ppermute | solution.py:16
  12.9 0.8 %copy-start.1 = (f32[128,1024]{1,0:T(8,128)}, f32[128,1024]{1,0:T(8,128)S(1)}, u32[]{:S(2)}) copy-start(f32[128,1024]{1,0:T(8,128)S(1)} %convolution_bitcast_fusion.2) | copy-start | bytes 1572868
  17.0 3.0 %copy-start.18 = (s32[128]{0:T(128)S(1)}, s32[128]{0:T(128)}, u32[]{:S(2)}) copy-start(s32[128]{0:T(128)} %get-tuple-element.93) | copy-start | bytes 1540
  17.0 3.0 %copy-start.19 = (s32[128]{0:T(128)S(1)}, s32[128]{0:T(128)}, u32[]{:S(2)}) copy-start(s32[128]{0:T(128)} %get-tuple-element.94) | copy-start | bytes 1540
  17.0 3.0 %copy-start.20 = (pred[128]{0:T(512)(128)(4,1)S(1)}, pred[128]{0:T(512)(128)(4,1)}, u32[]{:S(2)}) copy-start(pred[128]{0:T(512)(128)(4,1)} %compare_and_fusion) | copy-start | bytes 388
  17.0 3.9 %copy-start.22 = (s32[128]{0:T(128)S(1)}, s32[128]{0:T(128)}, u32[]{:S(2)}) copy-start(s32[128]{0:T(128)} %param.7) | copy-start | bytes 1540
  17.0 4.0 %copy-start.15 = (bf16[20,2048]{1,0:T(8,128)(2,1)S(1)}, bf16[20,2048]{1,0:T(8,128)(2,1)}, u32[]{:S(2)}) copy-start(bf16[20,2048]{1,0:T(8,128)(2,1)} %reshape.265) | copy-start | bytes 245764
  20.0 1.5 %copy-start.4 = (f32[128,512]{1,0:T(8,128)S(1)}, f32[128,512]{1,0:T(8,128)}, u32[]{:S(2)}) copy-start(f32[128,512]{1,0:T(8,128)} %copy-done.3) | copy-start | bytes 786436
  20.0 1.5 %copy-start.6 = (f32[128,512]{1,0:T(8,128)S(1)}, f32[128,512]{1,0:T(8,128)}, u32[]{:S(2)}) copy-start(f32[128,512]{1,0:T(8,128)} %copy-done.5) | copy-start | bytes 786436
  20.0 1.5 %copy-start.8 = (f32[128,512]{1,0:T(8,128)S(1)}, f32[128,512]{1,0:T(8,128)}, u32[]{:S(2)}) copy-start(f32[128,512]{1,0:T(8,128)} %copy-done.7) | copy-start | bytes 786436
  20.0 1.5 %copy-start.10 = (f32[128,512]{1,0:T(8,128)S(1)}, f32[128,512]{1,0:T(8,128)}, u32[]{:S(2)}) copy-start(f32[128,512]{1,0:T(8,128)} %copy-done.9) | copy-start | bytes 786436
  20.2 4.1 %copy-start.16 = (f32[2048]{0:T(1024)S(1)}, f32[2048]{0:T(1024)}, u32[]{:S(2)}) copy-start(f32[2048]{0:T(1024)} %param.9) | copy-start | bytes 24580
  22.7 8.5 %collective-permute-start.2 = (f32[128,512]{1,0:T(8,128)S(1)}, f32[128,512]{1,0:T(8,128)S(1)}, u32[]{:S(2)}, u32[]{:S(2)}) collective-permute-start(f32[128,512]{1,0:T(8,128)S(1)} %slice_select_fusion), channel_id=1, source_target_pairs={{0,2},{2,0},{1,3},{3,1},{4,6},{6,4},{5,7},{7,5},{8,10},{10,8},{9,1... | collective-permute-start | bytes 786440 | tf_op jit(solution)/shard_map/ppermute | solution.py:46
  28.1 7.8 %copy-start.11 = (bf16[128,512]{1,0:T(8,128)(2,1)S(1)}, bf16[128,512]{1,0:T(8,128)(2,1)}, u32[]{:S(2)}) copy-start(bf16[128,512]{1,0:T(8,128)(2,1)} %param.13) | copy-start | bytes 393220
  31.4 6.8 %collective-permute-start.3 = (bf16[2,128,128]{1,2,0:T(8,128)(2,1)S(1)}, bf16[2,128,128]{1,2,0:T(8,128)(2,1)S(1)}, u32[]{:S(2)}, u32[]{:S(2)}) collective-permute-start(bf16[2,128,128]{1,2,0:T(8,128)(2,1)S(1)} %get-tuple-element.75), channel_id=1, source_target_pairs={{0,12},{4,8},{8,4},{12,0},{1,13},{5,9},{9,5},{13,1},{2,14},{6,10},... | collective-permute-start | bytes 196616 | tf_op jit(solution)/shard_map/ppermute | solution.py:82
  32.8 7.4 %collective-permute-start.4 = (bf16[2,128,128]{1,2,0:T(8,128)(2,1)S(1)}, bf16[2,128,128]{1,2,0:T(8,128)(2,1)S(1)}, u32[]{:S(2)}, u32[]{:S(2)}) collective-permute-start(bf16[2,128,128]{1,2,0:T(8,128)(2,1)S(1)} %get-tuple-element.74), channel_id=1, source_target_pairs={{0,8},{4,12},{8,0},{12,4},{1,9},{5,13},{9,1},{13,5},{2,10},{6,14},... | collective-permute-start | bytes 196616 | tf_op jit(solution)/shard_map/ppermute | solution.py:82
  34.1 6.1 %collective-permute-start.5 = (bf16[2,128,128]{1,2,0:T(8,128)(2,1)S(1)}, bf16[2,128,128]{1,2,0:T(8,128)(2,1)S(1)}, u32[]{:S(2)}, u32[]{:S(2)}) collective-permute-start(bf16[2,128,128]{1,2,0:T(8,128)(2,1)S(1)} %get-tuple-element.33), channel_id=1, source_target_pairs={{0,4},{4,0},{8,12},{12,8},{1,5},{5,1},{9,13},{13,9},{2,6},{6,2},{1... | collective-permute-start | bytes 196616 | tf_op jit(solution)/shard_map/ppermute | solution.py:82
  40.3 1.2 %copy-start.2 = (f32[128,1024]{1,0:T(8,128)S(1)}, f32[128,1024]{1,0:T(8,128)}, u32[]{:S(2)}) copy-start(f32[128,1024]{1,0:T(8,128)} %copy-done.1) | copy-start | bytes 1572868
  40.3 1.2 %copy-start.17 = (pred[512]{0:T(512)(128)(4,1)S(1)}, pred[512]{0:T(512)(128)(4,1)}, u32[]{:S(2)}) copy-start(pred[512]{0:T(512)(128)(4,1)} %iota_compare_fusion.6) | copy-start | bytes 1540
  41.8 10.4 %slice-start = ((s8[6291456]{0:T(1024)(128)(4,1)}), s8[4194304]{0:T(1024)(128)(4,1)S(1)}, s32[]{:S(2)}) async-start(s8[6291456]{0:T(1024)(128)(4,1)} %bitcast.108), calls=%async_computation | async-start | bytes 8388608
  42.9 9.4 %slice-start.1 = ((s8[6291456]{0:T(1024)(128)(4,1)}), s8[2097152]{0:T(1024)(128)(4,1)S(1)}, s32[]{:S(2)}) async-start(s8[6291456]{0:T(1024)(128)(4,1)} %bitcast.108), calls=%async_computation.1 | async-start | bytes 4194304
  44.0 6.1 %collective-permute-start.6 = (bf16[2,128,128]{1,2,0:T(8,128)(2,1)S(1)}, bf16[2,128,128]{1,2,0:T(8,128)(2,1)S(1)}, u32[]{:S(2)}, u32[]{:S(2)}) collective-permute-start(bf16[2,128,128]{1,2,0:T(8,128)(2,1)S(1)} %get-tuple-element.70), channel_id=1, source_target_pairs={{0,12},{4,8},{8,4},{12,0},{1,13},{5,9},{9,5},{13,1},{2,14},{6,10},... | collective-permute-start | bytes 196616 | tf_op jit(solution)/shard_map/ppermute | solution.py:82
  46.1 5.9 %collective-permute-start.7 = (bf16[2,128,128]{1,2,0:T(8,128)(2,1)S(1)}, bf16[2,128,128]{1,2,0:T(8,128)(2,1)S(1)}, u32[]{:S(2)}, u32[]{:S(2)}) collective-permute-start(bf16[2,128,128]{1,2,0:T(8,128)(2,1)S(1)} %get-tuple-element.69), channel_id=1, source_target_pairs={{0,8},{4,12},{8,0},{12,4},{1,9},{5,13},{9,1},{13,5},{2,10},{6,14},... | collective-permute-start | bytes 196616 | tf_op jit(solution)/shard_map/ppermute | solution.py:82
  46.1 5.9 %collective-permute-start.8 = (bf16[2,128,128]{1,2,0:T(8,128)(2,1)S(1)}, bf16[2,128,128]{1,2,0:T(8,128)(2,1)S(1)}, u32[]{:S(2)}, u32[]{:S(2)}) collective-permute-start(bf16[2,128,128]{1,2,0:T(8,128)(2,1)S(1)} %get-tuple-element.23), channel_id=1, source_target_pairs={{0,4},{4,0},{8,12},{12,8},{1,5},{5,1},{9,13},{13,9},{2,6},{6,2},{1... | collective-permute-start | bytes 196616 | tf_op jit(solution)/shard_map/ppermute | solution.py:82
  57.2 4.2 %collective-permute-start.12 = (f32[21,512]{1,0:T(8,128)S(1)}, f32[21,512]{1,0:T(8,128)S(1)}, u32[]{:S(2)}, u32[]{:S(2)}) collective-permute-start(f32[21,512]{1,0:T(8,128)S(1)} %get-tuple-element.76), channel_id=1, source_target_pairs={{0,2},{1,3},{2,0},{3,1},{4,6},{5,7},{6,4},{7,5},{8,10},{9,11},{10,... | collective-permute-start | bytes 129032 | tf_op jit(solution)/shard_map/ppermute | solution.py:82
  58.8 3.7 %collective-permute-start.13 = (f32[21,512]{1,0:T(8,128)S(1)}, f32[21,512]{1,0:T(8,128)S(1)}, u32[]{:S(2)}, u32[]{:S(2)}) collective-permute-start(f32[21,512]{1,0:T(8,128)S(1)} %get-tuple-element.77), channel_id=1, source_target_pairs={{0,3},{1,2},{2,1},{3,0},{4,7},{5,6},{6,5},{7,4},{8,11},{9,10},{10,... | collective-permute-start | bytes 129032 | tf_op jit(solution)/shard_map/ppermute | solution.py:82
  58.8 3.7 %collective-permute-start.11 = (f32[21,512]{1,0:T(8,128)S(1)}, f32[21,512]{1,0:T(8,128)S(1)}, u32[]{:S(2)}, u32[]{:S(2)}) collective-permute-start(f32[21,512]{1,0:T(8,128)S(1)} %get-tuple-element.16), channel_id=1, source_target_pairs={{0,1},{1,0},{2,3},{3,2},{4,5},{5,4},{6,7},{7,6},{8,9},{9,8},{10,11... | collective-permute-start | bytes 129032 | tf_op jit(solution)/shard_map/ppermute | solution.py:82
  59.5 7.4 %collective-permute-start.9 = (bf16[1,512,128]{1,2,0:T(8,128)(2,1)S(1)}, bf16[1,512,128]{1,2,0:T(8,128)(2,1)S(1)}, u32[]{:S(2)}, u32[]{:S(2)}) collective-permute-start(bf16[1,512,128]{1,2,0:T(8,128)(2,1)S(1)} %get-tuple-element.49), channel_id=1, source_target_pairs={{0,2},{2,0},{1,3},{3,1},{4,6},{6,4},{5,7},{7,5},{8,10},{10,8},{9,1... | collective-permute-start | bytes 393224 | tf_op jit(solution)/shard_map/ppermute | solution.py:46
  62.5 7.8 %collective-permute-start.14 = (f32[21,512]{1,0:T(8,128)S(1)}, f32[21,512]{1,0:T(8,128)S(1)}, u32[]{:S(2)}, u32[]{:S(2)}) collective-permute-start(f32[21,512]{1,0:T(8,128)S(1)} %pad_add_fusion), channel_id=1, source_target_pairs={{0,12},{4,8},{8,4},{12,0},{1,13},{5,9},{9,5},{13,1},{2,14},{6,10},... | collective-permute-start | bytes 129032 | tf_op jit(solution)/shard_map/ppermute | solution.py:82
  65.1 5.2 %collective-permute-start.15 = (f32[21,512]{1,0:T(8,128)S(1)}, f32[21,512]{1,0:T(8,128)S(1)}, u32[]{:S(2)}, u32[]{:S(2)}) collective-permute-start(f32[21,512]{1,0:T(8,128)S(1)} %pad_add_fusion), channel_id=1, source_target_pairs={{0,8},{4,12},{8,0},{12,4},{1,9},{5,13},{9,1},{13,5},{2,10},{6,14},... | collective-permute-start | bytes 129032 | tf_op jit(solution)/shard_map/ppermute | solution.py:82
  65.1 5.2 %collective-permute-start.16 = (f32[21,512]{1,0:T(8,128)S(1)}, f32[21,512]{1,0:T(8,128)S(1)}, u32[]{:S(2)}, u32[]{:S(2)}) collective-permute-start(f32[21,512]{1,0:T(8,128)S(1)} %pad_add_fusion), channel_id=1, source_target_pairs={{0,4},{4,0},{8,12},{12,8},{1,5},{5,1},{9,13},{13,9},{2,6},{6,2},{1... | collective-permute-start | bytes 129032 | tf_op jit(solution)/shard_map/ppermute | solution.py:82
  66.9 0.7 copy-start.12
  68.3 3.2 %collective-permute-start.10 = (bf16[2,512,128]{1,2,0:T(8,128)(2,1)}, bf16[2,512,128]{1,2,0:T(8,128)(2,1)}, u32[]{:S(2)}, u32[]{:S(2)}) collective-permute-start(bf16[2,512,128]{1,2,0:T(8,128)(2,1)} %pad_maximum_fusion.7), channel_id=1, source_target_pairs={{0,1},{1,0},{2,3},{3,2},{4,5},{5,4},{6,7},{7,6},{8,9},{9,8},{10,11... | collective-permute-start | bytes 786440 | tf_op jit(solution)/shard_map/ppermute | solution.py:46
  70.2 2.6 %copy-start.13 = (bf16[512,512]{1,0:T(8,128)(2,1)S(1)}, bf16[512,512]{1,0:T(8,128)(2,1)}, u32[]{:S(2)}) copy-start(bf16[512,512]{1,0:T(8,128)(2,1)} %get-tuple-element.40) | copy-start | bytes 1572868
  70.2 2.6 %copy-start.14 = (bf16[512,512]{1,0:T(8,128)(2,1)S(1)}, bf16[512,512]{1,0:T(8,128)(2,1)}, u32[]{:S(2)}) copy-start(bf16[512,512]{1,0:T(8,128)(2,1)} %get-tuple-element.41) | copy-start | bytes 1572868

commit v7 on v6

--- a/solution.py
+++ b/solution.py
@@ -44,25 +44,6 @@
 def xor_exchange(x, axis, step):
     count = lax.axis_size(axis)
     return lax.ppermute(x, axis, [(i, i ^ step) for i in range(count)])
-
-
-def reduce_scatter_lanes(x, width):
-    for axis, inner in (("pair", lax.axis_size("chan")), ("chan", 1)):
-        me, step = lax.axis_index(axis), lax.axis_size(axis) // 2
-        while step >= 1:
-            half = step * inner * width
-            low = (me // step) % 2 == 0
-            lo, hi = x[:, :half], x[:, half : 2 * half]
-            keep = jnp.where(low, lo, hi)
-            send = jnp.where(low, hi, lo)
-            x = keep + xor_exchange(send, axis, step)
-            step //= 2
-    return x
-
-
-def pair_major(blocks):
-    chans, pairs = lax.axis_size("chan"), lax.axis_size("pair")
-    return [blocks[c * pairs + p] for p in range(pairs) for c in range(chans)]
 
 
 def all_gather_cp(x):
@@ -229,11 +210,7 @@
     grad_scale = 1.0 / math.sqrt(length)
     groups = lax.axis_size("chan") * lax.axis_size("pair")
     gated_partial = jnp.einsum("rd,cd->rc", cotangent, out_proj, preferred_element_type=jnp.float32)
-    gated_blocks = [gated_partial[:, g * local_width : (g + 1) * local_width] for g in range(groups)]
-    d_gated = (
-        reduce_scatter_lanes(jnp.concatenate(pair_major(gated_blocks), axis=1), local_width).T
-        * grad_scale
-    )
+    d_gated = reduce_blocks_cp(gated_partial, local_width).T * grad_scale
     dft = dft_matrix(length)
     filter_rows = long_filter.reshape(long_filter.shape[2], long_filter.shape[3])
     spec_g = add_conj_flip(forward_dft(filter_rows, dft))
@@ -252,16 +229,18 @@
     gated_rows = (query_part * conv_rows.astype(jnp.float32)).astype(jnp.bfloat16)
     weight_rows = out_proj
     gathered, sources = all_gather_cp(gated_rows)
-    weight_order = jnp.concatenate(
-        [lax.dynamic_slice_in_dim(weight_rows, src * local_width, local_width, 0) for src in sources],
-        axis=0,
-    )
-    mixed_out = jnp.einsum(
-        "cr,cd->rd",
-        gathered.reshape(-1, gathered.shape[-1]),
-        weight_order,
-        preferred_element_type=jnp.float32,
-    )
+    mixed_out = None
+    for slot in range(len(sources)):
+        piece = gathered[0]
+        for index in range(1, len(sources)):
+            piece = jnp.where(sources[index] == slot, gathered[index], piece)
+        term = jnp.einsum(
+            "cr,cd->rd",
+            piece,
+            weight_rows[slot * local_width : (slot + 1) * local_width],
+            preferred_element_type=jnp.float32,
+        )
+        mixed_out = term if mixed_out is None else mixed_out + term
     own_rows = lax.dynamic_slice_in_dim(embedded, group_index * local_width, local_width, 0)
     block_out = (mixed_out + own_rows.T).astype(jnp.bfloat16)
     d_query = d_gated * conv_rows.astype(jnp.float32)

time: 75.6 us -> 73.9 us (0.978)
  matrix products: 19.9 us -> 23.6 us
  local copies, waits for them, and re-layouts: 8.47 us -> 6.03 us
  other arithmetic: 9.63 us -> 8.37 us
  waiting for transfers between devices: 11.8 us -> 10.6 us
    dot_general x1 -> x4, matrix products: 2.34 us -> 6.05 us  [per_device(): jnp.einsum('cr,cd->rd', piece, weight_rows[slot * local_width:(slot + 1)...]
    ppermute x12 -> x15, starting transfers between devices: 15.6 us -> 18.6 us  [group_exchange(): return lax.ppermute(x, axes, [(i, i ^ offset) for i in range(count)])]
    ppermute x4 -> x2, waiting for transfers between devices: 3.07 us -> 0.01 us  [xor_exchange(): return lax.ppermute(x, axis, [(i, i ^ step) for i in range(count)])]
    dynamic_slice x1 -> x0, local copies, waits for them, and re-layouts: 2.94 us -> none  [per_device(): lax.dynamic_slice_in_dim(weight_rows, src * local_width, local_width, 0)]
    ppermute x4 -> x2, starting transfers between devices: 3.61 us -> 1.58 us  [xor_exchange(): return lax.ppermute(x, axis, [(i, i ^ step) for i in range(count)])]
    select_n x2 -> x4, other arithmetic: 0.05 us -> 1.87 us  [pick(): out = jnp.where(index == g, blocks[g], out)]
    ppermute x12 -> x15, waiting for transfers between devices: 8.77 us -> 10.6 us  [group_exchange(): return lax.ppermute(x, axes, [(i, i ^ offset) for i in range(count)])]
    ppermute x1, starting transfers between devices: 4.94 us -> 3.47 us  [from_behind(): lax.ppermute(value, axis, [(source, source + steps) for source in range(f...]
  transfers between devices with their start and end apart: 17 -> 18, of which waited for: 7 -> 6; matrix products, arithmetic and copies ran while one was open for 25% -> 23% of each run, Pallas kernels for 0% -> 0%
where the time goes in v7:
time: 73.9 us; the launch traced here: 73.5 us
  starting transfers between devices  23.7 us (32%)
  matrix products  23.6 us (32%)
  waiting for transfers between devices  10.6 us (14%)
  other arithmetic  8.37 us (11%)
  local copies, waits for them, and re-layouts  6.03 us (8%)
  between operations  1.29 us (2%)
    ppermute x15, starting transfers between devices, group_exchange(): return lax.ppermute(x, axes, [(i, i ^ offset) for i in range(count)])  18.6 us
    ppermute x15, waiting for transfers between devices, group_exchange(): return lax.ppermute(x, axes, [(i, i ^ offset) for i in range(count)])  10.6 us
    dot_general x4, matrix products, per_device(): jnp.einsum('cr,cd->rd', piece, weight_rows[slot * local_width:(slot + 1)...  6.05 us
    dot_general x1, matrix products, per_device(): jnp.einsum('dr,dmc->mcr', hidden, in_proj, preferred_element_type=jnp.flo...  3.9 us
    dot_general x3, matrix products, inverse_dft(): lax.dot_general(spec * weight, dft, (((1,), (1,)), ((), ())), precision=T...  3.87 us
    ppermute x1, starting transfers between devices, from_behind(): lax.ppermute(value, axis, [(source, source + steps) for source in range(f...  3.47 us
    unnamed x36, local copies, waits for them, and re-layouts  2.92 us
    dot_general x1, matrix products, per_device(): jnp.einsum('rd,cd->rc', cotangent, out_proj, preferred_element_type=jnp.f...  2.5 us
  transfers between devices with their start and end apart: 18, of which 6 were waited for; matrix products, arithmetic and copies ran while one was open for 23% of the time, Pallas kernels for 0%

profile of v7, /device:TPU:0, one launch (start us, length us, event | category | flops | bytes accessed | tf_op | source)
XLA Modules:
  0.0 73.5 jit_solution(11986701280779586587)
XLA Ops:
  0.7 2.5 %fusion.136 = f32[128,2048]{1,0:T(8,128)S(1)} fusion(bf16[128,512]{1,0:T(8,128)(2,1)} %param.13, bf16[2048,512]{1,0:T(8,128)(2,1)} %param.12), kind=kOutput, calls=%fused_computation.255 | convolution fusion | flops 268435456 | bytes 3276800 | tf_op jit(solution)/shard_map/rd,cd->rc/dot_general | solution.py:212
  3.2 1.0 %select_select_fusion.2 = (f32[128,512]{1,0:T(8,128)}, f32[128,512]{1,0:T(8,128)}) fusion(f32[128,2048]{1,0:T(8,128)S(1)} %fusion.136, pred[]{:T(512)S(6)} %eq.294, pred[]{:T(512)S(6)} %eq.293, pred[]{:T(512)S(6)} %eq.292, pred[]{:T(512)S(6)} %eq.297, pred[]{:T(512)S(6)} %eq.296, pred[]{:T(512)S(6)} %eq.295), kind=kLoop, calls=%fused_computation.116 | loop fusion | flops 393216 | bytes 1572870 | tf_op jit(solution)/shard_map/jit(_where)/select_n | solution.py:75
  4.2 0.5 collective-permute-start.1
  4.7 2.5 %collective-permute-start.2 = (f32[128,512]{1,0:T(8,128)}, f32[128,512]{1,0:T(8,128)}, u32[]{:S(2)}, u32[]{:S(2)}) collective-permute-start(f32[128,512]{1,0:T(8,128)} %get-tuple-element.48), channel_id=1, source_target_pairs={{0,2},{1,3},{2,0},{3,1},{4,6},{5,7},{6,4},{7,5},{8,10},{9,11},{10,... | collective-permute-start | bytes 786440 | tf_op jit(solution)/shard_map/ppermute | solution.py:63
  7.2 0.6 slice_add_fusion.2
  7.8 3.5 %collective-permute-start = (s32[3]{0:T(128)}, s32[3]{0:T(128)S(1)}, u32[]{:S(2)}, u32[]{:S(2)}) collective-permute-start(s32[3]{0:T(128)} %slice_add_fusion.2), channel_id=1, source_target_pairs={{0,4},{4,8},{8,12},{1,5},{5,9},{9,13},{2,6},{6,10},{10,14},{3,7},{... | collective-permute-start | bytes 44 | tf_op jit(solution)/shard_map/ppermute | solution.py:16
  11.3 0.8 %select_select_fusion = f32[128,512]{1,0:T(8,128)} fusion(f32[128,2048]{1,0:T(8,128)S(1)} %fusion.136, pred[]{:T(512)S(6)} %eq.300, pred[]{:T(512)S(6)} %eq.299, pred[]{:T(512)S(6)} %eq.298), kind=kLoop, calls=%fused_computation.114 | loop fusion | flops 196608 | bytes 1310723 | tf_op jit(solution)/shard_map/jit(_where)/select_n | solution.py:75
  12.6 0.6 fusion.97
  13.5 0.7 convolution_bitcast_fusion.2
  14.2 1.0 %fusion.134 = (f32[127,1024]{1,0:T(8,128)S(1)}, f32[127,1024]{1,0:T(8,128)}) fusion(f32[128,1024]{1,0:T(8,128)S(1)} %convolution_bitcast_fusion.2), kind=kLoop, calls=%fused_computation.253 | loop fusion | bytes 2080768 | tf_op jit(solution)/shard_map/jit(_roll_static)/slice | solution.py:165
  15.4 1.2 %maximum_select_fusion = f32[128,1024]{1,0:T(8,128)S(1)} fusion(f32[1,1024]{1,0:T(1,128)S(1)} %get-tuple-element.57, f32[127,1024]{1,0:T(8,128)} %get-tuple-element.59, f32[127,1024]{1,0:T(8,128)S(1)} %get-tuple-element.58, f32[1,1024]{1,0:T(1,128)S(1)} %get-tuple-element.56, s32[128]{0:T(128)S(1)} %get-tuple-element.89, s32[128]{0:T(128)S(1)} %get-tuple-element.90, ...), kind=kLoop, calls=%fused_computation.40 | loop fusion | flops 655360 | bytes 1574016 | tf_op jit(solution)/shard_map/jit(_where)/select_n | solution.py:166
  16.8 0.4 multiply_reduce_fusion
  17.3 3.9 %convolution_bitcast_fusion.1 = f32[3,512,128]{1,2,0:T(8,128)S(1)} fusion(bf16[2048,3,512]{2,0,1:T(8,128)(2,1)} %param.10, f32[128,2048]{1,0:T(8,128)S(1)} %get-tuple-element.82, f32[2048]{0:T(1024)S(1)} %copy-done.11, f32[128]{0:T(128)S(1)} %add_rsqrt_fusion), kind=kOutput, calls=%fused_computation.5 | convolution fusion | flops 806092800 | bytes 8135168 | tf_op jit(solution)/shard_map/dr,dmc->mcr/dot_general | solution.py:201
  21.3 1.3 %fusion.56 = (bf16[1,512,128]{1,2,0:T(8,128)(2,1)S(1)}, f32[128,512]{1,0:T(8,128)S(1)}) fusion(f32[3,512,128]{1,2,0:T(8,128)S(1)} %convolution_bitcast_fusion.1, f32[128,512]{1,0:T(8,128)} %collective-permute-done.3, f32[128,512]{1,0:T(8,128)} %collective-permute-done.2, f32[128,512]{1,0:T(8,128)} %collective-permute-done.1, f32[128,2048]{1,0:T(8,128)S(1)} %copy-done.2, ...), kind=kLoop, calls=%fused_computation.130 | loop fusion | flops 589824 | bytes 2490371 | tf_op jit(solution)/shard_map/stack | solution.py:219
  22.7 2.3 %collective-permute-start.4 = (bf16[2,128,128]{1,2,0:T(8,128)(2,1)S(1)}, bf16[2,128,128]{1,2,0:T(8,128)(2,1)S(1)}, u32[]{:S(2)}, u32[]{:S(2)}) collective-permute-start(bf16[2,128,128]{1,2,0:T(8,128)(2,1)S(1)} %get-tuple-element.71), channel_id=1, source_target_pairs={{0,12},{4,8},{8,4},{12,0},{1,13},{5,9},{9,5},{13,1},{2,14},{6,10},... | collective-permute-start | bytes 196616 | tf_op jit(solution)/shard_map/ppermute | solution.py:63
  25.0 0.8 %collective-permute-start.5 = (bf16[2,128,128]{1,2,0:T(8,128)(2,1)S(1)}, bf16[2,128,128]{1,2,0:T(8,128)(2,1)S(1)}, u32[]{:S(2)}, u32[]{:S(2)}) collective-permute-start(bf16[2,128,128]{1,2,0:T(8,128)(2,1)S(1)} %get-tuple-element.70), channel_id=1, source_target_pairs={{0,8},{4,12},{8,0},{12,4},{1,9},{5,13},{9,1},{13,5},{2,10},{6,14},... | collective-permute-start | bytes 196616 | tf_op jit(solution)/shard_map/ppermute | solution.py:63
  25.8 1.4 %collective-permute-start.6 = (bf16[2,128,128]{1,2,0:T(8,128)(2,1)S(1)}, bf16[2,128,128]{1,2,0:T(8,128)(2,1)S(1)}, u32[]{:S(2)}, u32[]{:S(2)}) collective-permute-start(bf16[2,128,128]{1,2,0:T(8,128)(2,1)S(1)} %get-tuple-element.33), channel_id=1, source_target_pairs={{0,4},{4,0},{8,12},{12,8},{1,5},{5,1},{9,13},{13,9},{2,6},{6,2},{1... | collective-permute-start | bytes 196616 | tf_op jit(solution)/shard_map/ppermute | solution.py:63
  27.4 1.9 %collective-permute-done.4 = bf16[2,128,128]{1,2,0:T(8,128)(2,1)S(1)} collective-permute-done((bf16[2,128,128]{1,2,0:T(8,128)(2,1)S(1)}, bf16[2,128,128]{1,2,0:T(8,128)(2,1)S(1)}, u32[]{:S(2)}, u32[]{:S(2)}) %collective-permute-start.4) | collective-permute-done | bytes 65568 | tf_op jit(solution)/shard_map/ppermute | solution.py:63
  29.3 3.2 %collective-permute-done.5 = bf16[2,128,128]{1,2,0:T(8,128)(2,1)S(1)} collective-permute-done((bf16[2,128,128]{1,2,0:T(8,128)(2,1)S(1)}, bf16[2,128,128]{1,2,0:T(8,128)(2,1)S(1)}, u32[]{:S(2)}, u32[]{:S(2)}) %collective-permute-start.5) | collective-permute-done | bytes 65568 | tf_op jit(solution)/shard_map/ppermute | solution.py:63
  32.7 0.6 fusion.60
  33.2 0.6 fusion.61
  34.3 1.0 %fusion.8 = bf16[1,128,512]{1,2,0:T(8,128)(2,1)S(1)} fusion(f32[512,1024]{1,0:T(8,128)S(1)} %bitcast.161, f32[128,512]{1,0:T(8,128)S(1)} %get-tuple-element.49, f32[128,512]{1,0:T(8,128)S(1)} %get-tuple-element.50, f32[1024]{0:T(1024)S(1)} %fusion.117), kind=kOutput, calls=%fused_computation.18 | convolution fusion | flops 402980864 | bytes 2756608 | tf_op jit(solution)/shard_map/dot_general | solution.py:138
  35.3 1.0 %fusion.9 = bf16[1,128,512]{1,2,0:T(8,128)(2,1)S(1)} fusion(f32[512,1024]{1,0:T(8,128)S(1)} %bitcast.162, f32[128,512]{1,0:T(8,128)S(1)} %get-tuple-element.51, f32[128,512]{1,0:T(8,128)S(1)} %get-tuple-element.28, f32[1024]{0:T(1024)S(1)} %fusion.117), kind=kOutput, calls=%fused_computation.19 | convolution fusion | flops 402980864 | bytes 2756608 | tf_op jit(solution)/shard_map/dot_general | solution.py:138
  36.4 2.6 %collective-permute-start.7 = (bf16[2,128,128]{1,2,0:T(8,128)(2,1)S(1)}, bf16[2,128,128]{1,2,0:T(8,128)(2,1)S(1)}, u32[]{:S(2)}, u32[]{:S(2)}) collective-permute-start(bf16[2,128,128]{1,2,0:T(8,128)(2,1)S(1)} %get-tuple-element.66), channel_id=1, source_target_pairs={{0,12},{4,8},{8,4},{12,0},{1,13},{5,9},{9,5},{13,1},{2,14},{6,10},... | collective-permute-start | bytes 196616 | tf_op jit(solution)/shard_map/ppermute | solution.py:63
  39.0 1.9 %collective-permute-start.9 = (bf16[2,128,128]{1,2,0:T(8,128)(2,1)S(1)}, bf16[2,128,128]{1,2,0:T(8,128)(2,1)S(1)}, u32[]{:S(2)}, u32[]{:S(2)}) collective-permute-start(bf16[2,128,128]{1,2,0:T(8,128)(2,1)S(1)} %get-tuple-element.23), channel_id=1, source_target_pairs={{0,4},{4,0},{8,12},{12,8},{1,5},{5,1},{9,13},{13,9},{2,6},{6,2},{1... | collective-permute-start | bytes 196616 | tf_op jit(solution)/shard_map/ppermute | solution.py:63
  41.0 1.8 %collective-permute-done.7 = bf16[2,128,128]{1,2,0:T(8,128)(2,1)S(1)} collective-permute-done((bf16[2,128,128]{1,2,0:T(8,128)(2,1)S(1)}, bf16[2,128,128]{1,2,0:T(8,128)(2,1)S(1)}, u32[]{:S(2)}, u32[]{:S(2)}) %collective-permute-start.7) | collective-permute-done | bytes 65568 | tf_op jit(solution)/shard_map/ppermute | solution.py:63
  42.8 2.0 %collective-permute-done.8 = bf16[2,128,128]{1,2,0:T(8,128)(2,1)S(1)} collective-permute-done((bf16[2,128,128]{1,2,0:T(8,128)(2,1)S(1)}, bf16[2,128,128]{1,2,0:T(8,128)(2,1)S(1)}, u32[]{:S(2)}, u32[]{:S(2)}) %collective-permute-start.8) | collective-permute-done | bytes 65568 | tf_op jit(solution)/shard_map/ppermute | solution.py:63
  45.1 1.3 %fusion.3 = f32[128]{0:T(128)S(1)} fusion(f32[3,512,128]{1,2,0:T(8,128)S(1)} %convolution_bitcast_fusion.1, bf16[2048,3,512]{2,0,1:T(8,128)(2,1)S(1)} %bitcast.165, f32[128,2048]{1,0:T(8,128)S(1)} %get-tuple-element.82, f32[2048]{0:T(1024)S(1)} %copy-done.11, f32[128]{0:T(128)S(1)} %add_rsqrt_fusion, bf16[1,512,128]{1,2,0:T(8,128)(2,1)S(1)} %get-tuple-element.46, ...), kind=kOutput, calls=%fused_computation.9 | convolution fusion | flops 808058752 | bytes 8528896 | tf_op jit(solution)/shard_map/dr,dmc->mcr/dot_general | solution.py:203
  46.4 2.2 %fusion.10 = (f32[2048]{0:T(1024)S(1)}, f32[128,2048,1]{1,0,2:T(8,128)S(1)}) fusion(f32[128,2048]{1,0:T(8,128)S(1)} %get-tuple-element.82, f32[128]{0:T(128)S(1)} %add_rsqrt_fusion, bf16[2048,3,512]{2,0,1:T(8,128)(2,1)S(1)} %bitcast.165, bf16[1,512,128]{1,2,0:T(8,128)(2,1)S(1)} %get-tuple-element.46, bf16[1,512,128]{1,2,0:T(8,128)(2,1)S(1)} %get-tuple-element.44, ...), kind=kOutput, calls=%fused_computation.21 | convolution fusion | flops 806483968 | bytes 8790528 | tf_op jit(solution)/shard_map/mcr,dmc->rd/dot_general | solution.py:252
  48.6 0.6 convolution_multiply_fusion.1
  49.2 0.7 fusion
  50.0 1.6 %collective-permute-start.13 = (f32[21,512]{1,0:T(8,128)S(1)}, f32[21,512]{1,0:T(8,128)S(1)}, u32[]{:S(2)}, u32[]{:S(2)}) collective-permute-start(f32[21,512]{1,0:T(8,128)S(1)} %get-tuple-element.72), channel_id=1, source_target_pairs={{0,2},{1,3},{2,0},{3,1},{4,6},{5,7},{6,4},{7,5},{8,10},{9,11},{10,... | collective-permute-start | bytes 129032 | tf_op jit(solution)/shard_map/ppermute | solution.py:63
  51.5 0.6 collective-permute-start.12
  52.3 1.6 %collective-permute-start.10 = (bf16[1,512,128]{1,2,0:T(8,128)(2,1)S(1)}, bf16[1,512,128]{1,2,0:T(8,128)(2,1)S(1)}, u32[]{:S(2)}, u32[]{:S(2)}) collective-permute-start(bf16[1,512,128]{1,2,0:T(8,128)(2,1)S(1)} %get-tuple-element.45), channel_id=1, source_target_pairs={{0,2},{2,0},{1,3},{3,1},{4,6},{6,4},{5,7},{7,5},{8,10},{10,8},{9,1... | collective-permute-start | bytes 393224 | tf_op jit(solution)/shard_map/ppermute | solution.py:46
  54.1 1.3 %collective-permute-done.14 = f32[21,512]{1,0:T(8,128)S(1)} collective-permute-done((f32[21,512]{1,0:T(8,128)S(1)}, f32[21,512]{1,0:T(8,128)S(1)}, u32[]{:S(2)}, u32[]{:S(2)}) %collective-permute-start.14) | collective-permute-done | bytes 43040 | tf_op jit(solution)/shard_map/ppermute | solution.py:63
  55.5 2.6 %collective-permute-start.15 = (f32[21,512]{1,0:T(8,128)S(1)}, f32[21,512]{1,0:T(8,128)S(1)}, u32[]{:S(2)}, u32[]{:S(2)}) collective-permute-start(f32[21,512]{1,0:T(8,128)S(1)} %pad_add_fusion), channel_id=1, source_target_pairs={{0,12},{4,8},{8,4},{12,0},{1,13},{5,9},{9,5},{13,1},{2,14},{6,10},... | collective-permute-start | bytes 129032 | tf_op jit(solution)/shard_map/ppermute | solution.py:63
  58.1 1.8 %collective-permute-start.17 = (f32[21,512]{1,0:T(8,128)S(1)}, f32[21,512]{1,0:T(8,128)S(1)}, u32[]{:S(2)}, u32[]{:S(2)}) collective-permute-start(f32[21,512]{1,0:T(8,128)S(1)} %pad_add_fusion), channel_id=1, source_target_pairs={{0,4},{4,0},{8,12},{12,8},{1,5},{5,1},{9,13},{13,9},{2,6},{6,2},{1... | collective-permute-start | bytes 129032 | tf_op jit(solution)/shard_map/ppermute | solution.py:63
  59.9 0.7 copy-done.7
  60.6 0.7 pad_maximum_fusion.4
  61.3 1.9 %convolution_bitcast_fusion.3 = f32[1,1,128,512]{3,2,1,0:T(8,128)} fusion(f32[512,1024]{1,0:T(8,128)S(1)} %bitcast.163, f32[128,512]{1,0:T(8,128)S(1)} %get-tuple-element.53, f32[128,512]{1,0:T(8,128)S(1)} %get-tuple-element.52, f32[1024]{0:T(1024)S(1)} %fusion.117), kind=kOutput, calls=%fused_computation.10 | convolution fusion | flops 402915328 | bytes 2887680 | tf_op jit(solution)/shard_map/dot_general | solution.py:138
  63.3 0.6 copy-done.9
  63.9 0.6 slice.274
  64.5 1.4 %reshape.265 = f32[4,5,512]{2,1,0:T(8,128)} reshape(f32[20,512]{1,0:T(8,128)} %bitcast.166) | data formatting | bytes 81920 | tf_op jit(solution)/shard_map/reshape | solution.py:274
  65.9 1.5 %copy.21 = f32[4,5,512]{2,0,1:T(4,128)} copy(f32[4,5,512]{2,1,0:T(8,128)} %reshape.265) | data formatting | bytes 81920
  67.4 1.5 %fusion.31 = f32[128,512]{1,0:T(8,128)S(1)} fusion(bf16[2048,512]{1,0:T(8,128)(2,1)} %param.12, bf16[512,128]{0,1:T(8,128)(2,1)S(1)} %get-tuple-element.61, bf16[1,512,128]{1,2,0:T(8,128)(2,1)} %copy-done.7, pred[]{:T(512)S(6)} %eq.297, pred[]{:T(512)S(6)} %eq.294, pred[]{:T(512)S(6)} %eq.314, bf16[2,512,128]{1,2,0:T(8,128)(2,1)} %collective-permute-done.11), kind=kOutput, calls=%fused_computation.54 | convolution fusion | flops 67305472 | bytes 1310723 | tf_op jit(solution)/shard_map/cr,cd->rd/dot_general | solution.py:237
  68.9 1.5 %fusion.29 = f32[128,512]{1,0:T(8,128)S(1)} fusion(bf16[2048,512]{1,0:T(8,128)(2,1)} %param.12, bf16[512,128]{0,1:T(8,128)(2,1)S(1)} %get-tuple-element.61, bf16[1,512,128]{1,2,0:T(8,128)(2,1)} %copy-done.7, pred[]{:T(512)S(6)} %eq.296, pred[]{:T(512)S(6)} %eq.293, pred[]{:T(512)S(6)} %eq.315, bf16[2,512,128]{1,2,0:T(8,128)(2,1)} %collective-permute-done.11), kind=kOutput, calls=%fused_computation.52 | convolution fusion | flops 67305472 | bytes 1310723 | tf_op jit(solution)/shard_map/cr,cd->rd/dot_general | solution.py:237
  70.4 1.2 %fusion.27 = f32[128,512]{1,0:T(8,128)S(1)} fusion(bf16[2048,512]{1,0:T(8,128)(2,1)S(1)} %copy-done.5, bf16[512,128]{0,1:T(8,128)(2,1)S(1)} %get-tuple-element.61, bf16[1,512,128]{1,2,0:T(8,128)(2,1)S(1)} %copy-done.8, pred[]{:T(512)S(6)} %eq.295, pred[]{:T(512)S(6)} %eq.292, pred[]{:T(512)S(6)} %eq.316, bf16[2,512,128]{1,2,0:T(8,128)(2,1)} %collective-permute-done.11), kind=kOutput, calls=%fused_computation.50 | convolution fusion | flops 67305472 | bytes 1310723 | tf_op jit(solution)/shard_map/cr,cd->rd/dot_general | solution.py:237
  71.6 1.9 %fusion.7 = bf16[128,512]{1,0:T(8,128)(2,1)} fusion(f32[128,512]{1,0:T(8,128)S(1)} %fusion.27, f32[128,512]{1,0:T(8,128)S(1)} %fusion.29, f32[128,512]{1,0:T(8,128)S(1)} %fusion.31, bf16[2048,512]{1,0:T(8,128)(2,1)S(1)} %copy-done.5, f32[128,2048]{1,0:T(8,128)S(1)} %get-tuple-element.82, s32[]{:T(128)S(6)} %select_n.795, ...), kind=kOutput, calls=%fused_computation.17 | convolution fusion | flops 67633152 | bytes 2228231 | tf_op jit(solution)/shard_map/cr,cd->rd/dot_general | solution.py:237
  (95 shorter events, 3.0 us)
Async XLA Ops:
  0.6 12.9 %copy-start = (f32[1,1,128,512]{3,2,1,0:T(8,128)S(1)}, f32[1,1,128,512]{3,2,1,0:T(8,128)}, u32[]{:S(2)}) copy-start(f32[1,1,128,512]{3,2,1,0:T(8,128)} %param.11) | copy-start | bytes 786436
  0.7 6.6 %copy-start.14 = (s32[128]{0:T(128)S(1)}, s32[128]{0:T(128)}, u32[]{:S(2)}) copy-start(s32[128]{0:T(128)} %param.7) | copy-start | bytes 1540
  3.2 10.0 %copy-start.1 = (f32[128,2048]{1,0:T(8,128)}, f32[128,2048]{1,0:T(8,128)S(1)}, u32[]{:S(2)}) copy-start(f32[128,2048]{1,0:T(8,128)S(1)} %fusion.136) | copy-start | bytes 3145732
  4.2 17.0 %collective-permute-start.1 = (f32[128,512]{1,0:T(8,128)}, f32[128,512]{1,0:T(8,128)}, u32[]{:S(2)}, u32[]{:S(2)}) collective-permute-start(f32[128,512]{1,0:T(8,128)} %get-tuple-element.47), channel_id=1, source_target_pairs={{0,1},{1,0},{2,3},{3,2},{4,5},{5,4},{6,7},{7,6},{8,9},{9,8},{10,11... | collective-permute-start | bytes 786440 | tf_op jit(solution)/shard_map/ppermute | solution.py:63
  4.7 16.5 %collective-permute-start.2 = (f32[128,512]{1,0:T(8,128)}, f32[128,512]{1,0:T(8,128)}, u32[]{:S(2)}, u32[]{:S(2)}) collective-permute-start(f32[128,512]{1,0:T(8,128)} %get-tuple-element.48), channel_id=1, source_target_pairs={{0,2},{1,3},{2,0},{3,1},{4,6},{5,7},{6,4},{7,5},{8,10},{9,11},{10,... | collective-permute-start | bytes 786440 | tf_op jit(solution)/shard_map/ppermute | solution.py:63
  7.8 8.8 %collective-permute-start = (s32[3]{0:T(128)}, s32[3]{0:T(128)S(1)}, u32[]{:S(2)}, u32[]{:S(2)}) collective-permute-start(s32[3]{0:T(128)} %slice_add_fusion.2), channel_id=1, source_target_pairs={{0,4},{4,8},{8,12},{1,5},{5,9},{9,13},{2,6},{6,10},{10,14},{3,7},{... | collective-permute-start | bytes 44 | tf_op jit(solution)/shard_map/ppermute | solution.py:16
  12.1 9.2 %collective-permute-start.3 = (f32[128,512]{1,0:T(8,128)}, f32[128,512]{1,0:T(8,128)}, u32[]{:S(2)}, u32[]{:S(2)}) collective-permute-start(f32[128,512]{1,0:T(8,128)} %select_select_fusion), channel_id=1, source_target_pairs={{0,3},{1,2},{2,1},{3,0},{4,7},{5,6},{6,5},{7,4},{8,11},{9,10},{10,... | collective-permute-start | bytes 786440 | tf_op jit(solution)/shard_map/ppermute | solution.py:63
  13.5 1.8 %copy-start.10 = (bf16[4,5,2048]{2,0,1:T(4,128)(2,1)S(1)}, bf16[4,5,2048]{2,0,1:T(4,128)(2,1)}, u32[]{:S(2)}) copy-start(bf16[4,5,2048]{2,0,1:T(4,128)(2,1)} %param.8) | copy-start | bytes 245764
  14.2 1.0 %copy-start.3 = (f32[128,1024]{1,0:T(8,128)}, f32[128,1024]{1,0:T(8,128)S(1)}, u32[]{:S(2)}) copy-start(f32[128,1024]{1,0:T(8,128)S(1)} %convolution_bitcast_fusion.2) | copy-start | bytes 1572868
  15.2 2.0 %copy-start.11 = (f32[2048]{0:T(1024)S(1)}, f32[2048]{0:T(1024)}, u32[]{:S(2)}) copy-start(f32[2048]{0:T(1024)} %param.9) | copy-start | bytes 24580
  15.3 18.7 %copy-start.12 = (pred[512]{0:T(512)(128)(4,1)}, pred[512]{0:T(512)(128)(4,1)S(1)}, u32[]{:S(2)}) copy-start(pred[512]{0:T(512)(128)(4,1)S(1)} %iota_compare_fusion.6) | copy-start | bytes 1540
  17.3 4.0 %copy-start.2 = (f32[128,2048]{1,0:T(8,128)S(1)}, f32[128,2048]{1,0:T(8,128)}, u32[]{:S(2)}) copy-start(f32[128,2048]{1,0:T(8,128)} %copy-done.1) | copy-start | bytes 3145732
  21.2 6.0 %copy-start.6 = (bf16[128,512]{1,0:T(8,128)(2,1)S(1)}, bf16[128,512]{1,0:T(8,128)(2,1)}, u32[]{:S(2)}) copy-start(bf16[128,512]{1,0:T(8,128)(2,1)} %param.13) | copy-start | bytes 393220
  22.7 6.6 %collective-permute-start.4 = (bf16[2,128,128]{1,2,0:T(8,128)(2,1)S(1)}, bf16[2,128,128]{1,2,0:T(8,128)(2,1)S(1)}, u32[]{:S(2)}, u32[]{:S(2)}) collective-permute-start(bf16[2,128,128]{1,2,0:T(8,128)(2,1)S(1)} %get-tuple-element.71), channel_id=1, source_target_pairs={{0,12},{4,8},{8,4},{12,0},{1,13},{5,9},{9,5},{13,1},{2,14},{6,10},... | collective-permute-start | bytes 196616 | tf_op jit(solution)/shard_map/ppermute | solution.py:63
  25.0 7.5 %collective-permute-start.5 = (bf16[2,128,128]{1,2,0:T(8,128)(2,1)S(1)}, bf16[2,128,128]{1,2,0:T(8,128)(2,1)S(1)}, u32[]{:S(2)}, u32[]{:S(2)}) collective-permute-start(bf16[2,128,128]{1,2,0:T(8,128)(2,1)S(1)} %get-tuple-element.70), channel_id=1, source_target_pairs={{0,8},{4,12},{8,0},{12,4},{1,9},{5,13},{9,1},{13,5},{2,10},{6,14},... | collective-permute-start | bytes 196616 | tf_op jit(solution)/shard_map/ppermute | solution.py:63
  25.8 6.7 %collective-permute-start.6 = (bf16[2,128,128]{1,2,0:T(8,128)(2,1)S(1)}, bf16[2,128,128]{1,2,0:T(8,128)(2,1)S(1)}, u32[]{:S(2)}, u32[]{:S(2)}) collective-permute-start(bf16[2,128,128]{1,2,0:T(8,128)(2,1)S(1)} %get-tuple-element.33), channel_id=1, source_target_pairs={{0,4},{4,0},{8,12},{12,8},{1,5},{5,1},{9,13},{13,9},{2,6},{6,2},{1... | collective-permute-start | bytes 196616 | tf_op jit(solution)/shard_map/ppermute | solution.py:63
  32.7 1.1 %copy-start.4 = (f32[128,1024]{1,0:T(8,128)S(1)}, f32[128,1024]{1,0:T(8,128)}, u32[]{:S(2)}) copy-start(f32[128,1024]{1,0:T(8,128)} %copy-done.3) | copy-start | bytes 1572868
  34.2 10.9 %slice-start = ((s8[6291456]{0:T(1024)(128)(4,1)}), s8[4194304]{0:T(1024)(128)(4,1)S(1)}, s32[]{:S(2)}) async-start(s8[6291456]{0:T(1024)(128)(4,1)} %bitcast.164), calls=%async_computation | async-start | bytes 8388608
  35.3 9.8 %slice-start.1 = ((s8[6291456]{0:T(1024)(128)(4,1)}), s8[2097152]{0:T(1024)(128)(4,1)S(1)}, s32[]{:S(2)}) async-start(s8[6291456]{0:T(1024)(128)(4,1)} %bitcast.164), calls=%async_computation.1 | async-start | bytes 4194304
  36.4 6.4 %collective-permute-start.7 = (bf16[2,128,128]{1,2,0:T(8,128)(2,1)S(1)}, bf16[2,128,128]{1,2,0:T(8,128)(2,1)S(1)}, u32[]{:S(2)}, u32[]{:S(2)}) collective-permute-start(bf16[2,128,128]{1,2,0:T(8,128)(2,1)S(1)} %get-tuple-element.66), channel_id=1, source_target_pairs={{0,12},{4,8},{8,4},{12,0},{1,13},{5,9},{9,5},{13,1},{2,14},{6,10},... | collective-permute-start | bytes 196616 | tf_op jit(solution)/shard_map/ppermute | solution.py:63
  39.0 5.8 %collective-permute-start.8 = (bf16[2,128,128]{1,2,0:T(8,128)(2,1)S(1)}, bf16[2,128,128]{1,2,0:T(8,128)(2,1)S(1)}, u32[]{:S(2)}, u32[]{:S(2)}) collective-permute-start(bf16[2,128,128]{1,2,0:T(8,128)(2,1)S(1)} %get-tuple-element.65), channel_id=1, source_target_pairs={{0,8},{4,12},{8,0},{12,4},{1,9},{5,13},{9,1},{13,5},{2,10},{6,14},... | collective-permute-start | bytes 196616 | tf_op jit(solution)/shard_map/ppermute | solution.py:63
  39.0 5.8 %collective-permute-start.9 = (bf16[2,128,128]{1,2,0:T(8,128)(2,1)S(1)}, bf16[2,128,128]{1,2,0:T(8,128)(2,1)S(1)}, u32[]{:S(2)}, u32[]{:S(2)}) collective-permute-start(bf16[2,128,128]{1,2,0:T(8,128)(2,1)S(1)} %get-tuple-element.23), channel_id=1, source_target_pairs={{0,4},{4,0},{8,12},{12,8},{1,5},{5,1},{9,13},{13,9},{2,6},{6,2},{1... | collective-permute-start | bytes 196616 | tf_op jit(solution)/shard_map/ppermute | solution.py:63
  48.5 3.6 %copy-start.13 = (pred[512]{0:T(512)(128)(4,1)S(1)}, pred[512]{0:T(512)(128)(4,1)}, u32[]{:S(2)}) copy-start(pred[512]{0:T(512)(128)(4,1)} %copy-done.12) | copy-start | bytes 1540
  50.0 4.2 %collective-permute-start.13 = (f32[21,512]{1,0:T(8,128)S(1)}, f32[21,512]{1,0:T(8,128)S(1)}, u32[]{:S(2)}, u32[]{:S(2)}) collective-permute-start(f32[21,512]{1,0:T(8,128)S(1)} %get-tuple-element.72), channel_id=1, source_target_pairs={{0,2},{1,3},{2,0},{3,1},{4,6},{5,7},{6,4},{7,5},{8,10},{9,11},{10,... | collective-permute-start | bytes 129032 | tf_op jit(solution)/shard_map/ppermute | solution.py:63
  51.5 3.9 %collective-permute-start.14 = (f32[21,512]{1,0:T(8,128)S(1)}, f32[21,512]{1,0:T(8,128)S(1)}, u32[]{:S(2)}, u32[]{:S(2)}) collective-permute-start(f32[21,512]{1,0:T(8,128)S(1)} %get-tuple-element.73), channel_id=1, source_target_pairs={{0,3},{1,2},{2,1},{3,0},{4,7},{5,6},{6,5},{7,4},{8,11},{9,10},{10,... | collective-permute-start | bytes 129032 | tf_op jit(solution)/shard_map/ppermute | solution.py:63
  51.5 3.9 %collective-permute-start.12 = (f32[21,512]{1,0:T(8,128)S(1)}, f32[21,512]{1,0:T(8,128)S(1)}, u32[]{:S(2)}, u32[]{:S(2)}) collective-permute-start(f32[21,512]{1,0:T(8,128)S(1)} %get-tuple-element.16), channel_id=1, source_target_pairs={{0,1},{1,0},{2,3},{3,2},{4,5},{5,4},{6,7},{7,6},{8,9},{9,8},{10,11... | collective-permute-start | bytes 129032 | tf_op jit(solution)/shard_map/ppermute | solution.py:63
  52.3 7.7 %collective-permute-start.10 = (bf16[1,512,128]{1,2,0:T(8,128)(2,1)S(1)}, bf16[1,512,128]{1,2,0:T(8,128)(2,1)S(1)}, u32[]{:S(2)}, u32[]{:S(2)}) collective-permute-start(bf16[1,512,128]{1,2,0:T(8,128)(2,1)S(1)} %get-tuple-element.45), channel_id=1, source_target_pairs={{0,2},{2,0},{1,3},{3,1},{4,6},{6,4},{5,7},{7,5},{8,10},{10,8},{9,1... | collective-permute-start | bytes 393224 | tf_op jit(solution)/shard_map/ppermute | solution.py:46
  55.5 7.7 %collective-permute-start.15 = (f32[21,512]{1,0:T(8,128)S(1)}, f32[21,512]{1,0:T(8,128)S(1)}, u32[]{:S(2)}, u32[]{:S(2)}) collective-permute-start(f32[21,512]{1,0:T(8,128)S(1)} %pad_add_fusion), channel_id=1, source_target_pairs={{0,12},{4,8},{8,4},{12,0},{1,13},{5,9},{9,5},{13,1},{2,14},{6,10},... | collective-permute-start | bytes 129032 | tf_op jit(solution)/shard_map/ppermute | solution.py:63
  58.1 5.1 %collective-permute-start.16 = (f32[21,512]{1,0:T(8,128)S(1)}, f32[21,512]{1,0:T(8,128)S(1)}, u32[]{:S(2)}, u32[]{:S(2)}) collective-permute-start(f32[21,512]{1,0:T(8,128)S(1)} %pad_add_fusion), channel_id=1, source_target_pairs={{0,8},{4,12},{8,0},{12,4},{1,9},{5,13},{9,1},{13,5},{2,10},{6,14},... | collective-permute-start | bytes 129032 | tf_op jit(solution)/shard_map/ppermute | solution.py:63
  58.1 5.1 %collective-permute-start.17 = (f32[21,512]{1,0:T(8,128)S(1)}, f32[21,512]{1,0:T(8,128)S(1)}, u32[]{:S(2)}, u32[]{:S(2)}) collective-permute-start(f32[21,512]{1,0:T(8,128)S(1)} %pad_add_fusion), channel_id=1, source_target_pairs={{0,4},{4,0},{8,12},{12,8},{1,5},{5,1},{9,13},{13,9},{2,6},{6,2},{1... | collective-permute-start | bytes 129032 | tf_op jit(solution)/shard_map/ppermute | solution.py:63
  59.9 0.7 copy-start.7
  61.3 6.1 %collective-permute-start.11 = (bf16[2,512,128]{1,2,0:T(8,128)(2,1)}, bf16[2,512,128]{1,2,0:T(8,128)(2,1)}, u32[]{:S(2)}, u32[]{:S(2)}) collective-permute-start(bf16[2,512,128]{1,2,0:T(8,128)(2,1)} %pad_maximum_fusion.4), channel_id=1, source_target_pairs={{0,1},{1,0},{2,3},{3,2},{4,5},{5,4},{6,7},{7,6},{8,9},{9,8},{10,11... | collective-permute-start | bytes 786440 | tf_op jit(solution)/shard_map/ppermute | solution.py:46
  63.2 7.2 %copy-start.5 = (bf16[2048,512]{1,0:T(8,128)(2,1)S(1)}, bf16[2048,512]{1,0:T(8,128)(2,1)}, u32[]{:S(2)}) copy-start(bf16[2048,512]{1,0:T(8,128)(2,1)} %param.12) | copy-start | bytes 6291460
  63.3 0.6 copy-start.9
  65.9 4.5 %copy-start.8 = (bf16[1,512,128]{1,2,0:T(8,128)(2,1)S(1)}, bf16[1,512,128]{1,2,0:T(8,128)(2,1)}, u32[]{:S(2)}) copy-start(bf16[1,512,128]{1,2,0:T(8,128)(2,1)} %copy-done.7) | copy-start | bytes 393220

commit v8 on v7

--- a/solution.py
+++ b/solution.py
@@ -81,23 +81,25 @@
     return total
 
 
-def sum_over_seq(x):
+def sum_over_seq(x, tied):
     count = lax.axis_size("seq")
     me = lax.axis_index("seq")
     if count > 4:
         step = 1
         while step < count:
-            x = x + xor_exchange(x, "seq", step)
+            got, tied = lax.optimization_barrier((xor_exchange(x, "seq", step), tied))
+            x = x + got
             step *= 2
-        return x
+        return x, tied
     got = [x] + [group_exchange(x, "seq", count, offset) for offset in range(1, count)]
+    got, tied = lax.optimization_barrier((got, tied))
     total = None
     for source in range(count):
         piece = got[0]
         for offset in range(1, count):
             piece = jnp.where((me ^ source) == offset, got[offset], piece)
         total = piece if total is None else total + piece
-    return total
+    return total, tied
 
 
 def all_to_all_seq(x, split_axis, concat_axis):
@@ -265,7 +267,7 @@
     own_block = own_block + jnp.concatenate(
         [cot_table, jnp.zeros((1, local_width), jnp.float32)], axis=0
     )
-    summed = sum_over_seq(own_block)
+    summed, (block_out, filter_grad) = sum_over_seq(own_block, (block_out, filter_grad))
     kmer_grad = summed[: kmer_len * letter_count]
     gain_grad = summed[kmer_len * letter_count]
     return (

time: 73.9 us -> 73.5 us (level)
  matrix products: 23.6 us -> 20 us
  other arithmetic: 8.37 us -> 11.2 us
  local copies, waits for them, and re-layouts: 6.03 us -> 4.77 us
  waiting for transfers between devices: 10.6 us -> 11.7 us
    dot_general x4, matrix products: 6.05 us -> 1.66 us  [per_device(): jnp.einsum('cr,cd->rd', piece, weight_rows[slot * local_width:(slot + 1)...]
    reshape x1, local copies, waits for them, and re-layouts: 1.43 us -> 0.01 us  [per_device(): kmer_grad.reshape(kmer_len, letter_count, local_width)]
    unnamed x36 -> x30, local copies, waits for them, and re-layouts: 2.92 us -> 1.68 us
    dot_general x1, matrix products: 0.43 us -> 1.34 us  [per_device(): embedded = jnp.dot(table_t, onehot_t, preferred_element_type=jnp.float32)]
    slice x2, local copies, waits for them, and re-layouts: 0.98 us -> 1.74 us  [pair_flip(): down = jnp.roll(values, 1, axis=0)]
  transfers between devices with their start and end apart: 18 -> 18, of which waited for: 6 -> 7; matrix products, arithmetic and copies ran while one was open for 23% -> 31% of each run, Pallas kernels for 0% -> 0%
where the time goes in v8:
time: 73.5 us; the launch traced here: 73.1 us
  starting transfers between devices  24.3 us (33%)
  matrix products  20 us (27%)
  waiting for transfers between devices  11.7 us (16%)
  other arithmetic  11.2 us (15%)
  local copies, waits for them, and re-layouts  4.77 us (6%)
  between operations  1.17 us (2%)
    ppermute x15, starting transfers between devices, group_exchange(): return lax.ppermute(x, axes, [(i, i ^ offset) for i in range(count)])  18.6 us
    ppermute x15, waiting for transfers between devices, group_exchange(): return lax.ppermute(x, axes, [(i, i ^ offset) for i in range(count)])  11.2 us
    ppermute x1, starting transfers between devices, from_behind(): lax.ppermute(value, axis, [(source, source + steps) for source in range(f...  4.06 us
    dot_general x3, matrix products, inverse_dft(): lax.dot_general(spec * weight, dft, (((1,), (1,)), ((), ())), precision=T...  3.87 us
    dot_general x1, matrix products, per_device(): jnp.einsum('dr,dmc->mcr', hidden, in_proj, preferred_element_type=jnp.flo...  3.86 us
    dot_general x1, matrix products, per_device(): jnp.einsum('rd,cd->rc', cotangent, out_proj, preferred_element_type=jnp.f...  2.51 us
    dot_general x1, matrix products, per_device(): jnp.einsum('mcr,dmc->rd', d_proj, in_proj, preferred_element_type=jnp.flo...  2.16 us
    dot_general x3, matrix products, forward_dft(): jnp.dot(signal.astype(jnp.float32), dft, precision=TRANSFORM_PRECISION)  1.82 us
  transfers between devices with their start and end apart: 18, of which 7 were waited for; matrix products, arithmetic and copies ran while one was open for 31% of the time, Pallas kernels for 0%

profile of v8, /device:TPU:0, one launch (start us, length us, event | category | flops | bytes accessed | tf_op | source)
XLA Modules:
  0.0 73.1 jit_solution(12711075083950151116)
XLA Ops:
  0.7 2.5 %fusion.137 = f32[128,2048]{1,0:T(8,128)S(1)} fusion(bf16[128,512]{1,0:T(8,128)(2,1)} %param.13, bf16[2048,512]{1,0:T(8,128)(2,1)} %param.12), kind=kOutput, calls=%fused_computation.255 | convolution fusion | flops 268435456 | bytes 3276800 | tf_op jit(solution)/shard_map/rd,cd->rc/dot_general | solution.py:214
  3.2 0.9 %select_select_fusion.2 = (f32[128,512]{1,0:T(8,128)}, f32[128,512]{1,0:T(8,128)}) fusion(f32[128,2048]{1,0:T(8,128)S(1)} %fusion.137, pred[]{:T(512)S(6)} %eq.288, pred[]{:T(512)S(6)} %eq.287, pred[]{:T(512)S(6)} %eq.286, pred[]{:T(512)S(6)} %eq.291, pred[]{:T(512)S(6)} %eq.290, pred[]{:T(512)S(6)} %eq.289), kind=kLoop, calls=%fused_computation.117 | loop fusion | flops 393216 | bytes 1572870 | tf_op jit(solution)/shard_map/jit(_where)/select_n | solution.py:75
  4.6 2.5 %collective-permute-start.2 = (f32[128,512]{1,0:T(8,128)}, f32[128,512]{1,0:T(8,128)}, u32[]{:S(2)}, u32[]{:S(2)}) collective-permute-start(f32[128,512]{1,0:T(8,128)} %get-tuple-element.60), channel_id=1, source_target_pairs={{0,2},{1,3},{2,0},{3,1},{4,6},{5,7},{6,4},{7,5},{8,10},{9,11},{10,... | collective-permute-start | bytes 786440 | tf_op jit(solution)/shard_map/ppermute | solution.py:63
  7.1 0.6 slice_add_fusion.2
  7.7 4.1 %collective-permute-start = (s32[3]{0:T(128)}, s32[3]{0:T(128)}, u32[]{:S(2)}, u32[]{:S(2)}) collective-permute-start(s32[3]{0:T(128)} %slice_add_fusion.2), channel_id=1, source_target_pairs={{0,4},{4,8},{8,12},{1,5},{5,9},{9,13},{2,6},{6,10},{10,14},{3,7},{... | collective-permute-start | bytes 44 | tf_op jit(solution)/shard_map/ppermute | solution.py:16
  11.7 0.8 %select_select_fusion = f32[128,512]{1,0:T(8,128)} fusion(f32[128,2048]{1,0:T(8,128)S(1)} %fusion.137, pred[]{:T(512)S(6)} %eq.294, pred[]{:T(512)S(6)} %eq.293, pred[]{:T(512)S(6)} %eq.292), kind=kLoop, calls=%fused_computation.115 | loop fusion | flops 196608 | bytes 1310723 | tf_op jit(solution)/shard_map/jit(_where)/select_n | solution.py:75
  12.6 0.6 iota_compare_fusion.5
  13.5 0.6 fusion.98
  14.5 0.7 convolution_bitcast_fusion.2
  15.2 1.1 %fusion.135 = (f32[127,1024]{1,0:T(8,128)}, f32[127,1024]{1,0:T(8,128)}) fusion(f32[128,1024]{1,0:T(8,128)S(1)} %convolution_bitcast_fusion.2), kind=kLoop, calls=%fused_computation.253 | loop fusion | bytes 2080768 | tf_op jit(solution)/shard_map/jit(_roll_static)/slice | solution.py:167
  16.3 0.6 fusion.134
  17.5 0.6 compare_and_fusion
  18.6 0.9 %copy.18 = bf16[4,5,2048]{2,1,0:T(8,128)(2,1)S(1)} copy(bf16[4,5,2048]{2,0,1:T(4,128)(2,1)} %param.8) | data formatting | bytes 163840 | tf_op args[1]
  19.5 0.7 reshape.262
  20.2 1.4 %maximum_select_fusion = f32[128,1024]{1,0:T(8,128)S(1)} fusion(f32[1,1024]{1,0:T(1,128)} %get-tuple-element.69, f32[127,1024]{1,0:T(8,128)} %get-tuple-element.71, f32[127,1024]{1,0:T(8,128)} %get-tuple-element.70, f32[1,1024]{1,0:T(1,128)S(1)} %get-tuple-element.68, s32[128]{0:T(128)} %get-tuple-element.101, s32[128]{0:T(128)} %get-tuple-element.102, ...), kind=kLoop, calls=%fused_computation.39 | loop fusion | flops 655360 | bytes 1574016 | tf_op jit(solution)/shard_map/jit(_where)/select_n | solution.py:168
  21.6 0.7 broadcast_add_fusion.1
  22.2 0.7 pad_add_fusion.2
  23.1 1.3 %multiply_reduce_fusion = (f32[128]{0:T(128)S(1)}, f32[128,2048]{1,0:T(8,128)S(1)}) fusion(bf16[20,2048]{1,0:T(8,128)(2,1)} %reshape.262, pred[128,5]{0,1:T(8,128)(4,1)S(1)} %get-tuple-element.97, pred[128,5]{0,1:T(8,128)(4,1)S(1)} %get-tuple-element.98, pred[128,5]{0,1:T(8,128)(4,1)S(1)} %iota_compare_fusion.4, pred[128,5]{0,1:T(8,128)(4,1)} %iota_compare_fusion.5), kind=kOutput, calls=%fused_computation.24 | convolution fusion | flops 11017600 | bytes 1133568 | tf_op jit(solution)/shard_map/dot_general | solution.py:198
  24.4 3.9 %convolution_bitcast_fusion.1 = f32[3,512,128]{1,2,0:T(8,128)S(1)} fusion(bf16[2048,3,512]{2,0,1:T(8,128)(2,1)} %param.10, f32[128,2048]{1,0:T(8,128)S(1)} %get-tuple-element.94, f32[2048]{0:T(1024)S(1)} %copy-done.5, f32[128]{0:T(128)S(1)} %add_rsqrt_fusion), kind=kOutput, calls=%fused_computation.5 | convolution fusion | flops 806092800 | bytes 8135168 | tf_op jit(solution)/shard_map/dr,dmc->mcr/dot_general | solution.py:203
  28.4 1.3 %fusion.57 = (bf16[1,512,128]{1,2,0:T(8,128)(2,1)S(1)}, f32[128,512]{1,0:T(8,128)S(1)}) fusion(f32[3,512,128]{1,2,0:T(8,128)S(1)} %convolution_bitcast_fusion.1, f32[128,512]{1,0:T(8,128)} %collective-permute-done.3, f32[128,512]{1,0:T(8,128)} %collective-permute-done.2, f32[128,512]{1,0:T(8,128)} %collective-permute-done.1, f32[128,2048]{1,0:T(8,128)S(1)} %fusion.137, ...), kind=kLoop, calls=%fused_computation.130 | loop fusion | flops 589824 | bytes 2490371 | tf_op jit(solution)/shard_map/stack | solution.py:221
  29.8 1.2 %collective-permute-start.4 = (bf16[2,128,128]{1,2,0:T(8,128)(2,1)S(1)}, bf16[2,128,128]{1,2,0:T(8,128)(2,1)S(1)}, u32[]{:S(2)}, u32[]{:S(2)}) collective-permute-start(bf16[2,128,128]{1,2,0:T(8,128)(2,1)S(1)} %get-tuple-element.83), channel_id=1, source_target_pairs={{0,12},{4,8},{8,4},{12,0},{1,13},{5,9},{9,5},{13,1},{2,14},{6,10},... | collective-permute-start | bytes 196616 | tf_op jit(solution)/shard_map/ppermute | solution.py:63
  31.0 1.4 %collective-permute-start.5 = (bf16[2,128,128]{1,2,0:T(8,128)(2,1)S(1)}, bf16[2,128,128]{1,2,0:T(8,128)(2,1)S(1)}, u32[]{:S(2)}, u32[]{:S(2)}) collective-permute-start(bf16[2,128,128]{1,2,0:T(8,128)(2,1)S(1)} %get-tuple-element.82), channel_id=1, source_target_pairs={{0,8},{4,12},{8,0},{12,4},{1,9},{5,13},{9,1},{13,5},{2,10},{6,14},... | collective-permute-start | bytes 196616 | tf_op jit(solution)/shard_map/ppermute | solution.py:63
  32.4 1.9 %collective-permute-start.6 = (bf16[2,128,128]{1,2,0:T(8,128)(2,1)S(1)}, bf16[2,128,128]{1,2,0:T(8,128)(2,1)S(1)}, u32[]{:S(2)}, u32[]{:S(2)}) collective-permute-start(bf16[2,128,128]{1,2,0:T(8,128)(2,1)S(1)} %get-tuple-element.45), channel_id=1, source_target_pairs={{0,4},{4,0},{8,12},{12,8},{1,5},{5,1},{9,13},{13,9},{2,6},{6,2},{1... | collective-permute-start | bytes 196616 | tf_op jit(solution)/shard_map/ppermute | solution.py:63
  34.5 2.2 %collective-permute-done.4 = bf16[2,128,128]{1,2,0:T(8,128)(2,1)S(1)} collective-permute-done((bf16[2,128,128]{1,2,0:T(8,128)(2,1)S(1)}, bf16[2,128,128]{1,2,0:T(8,128)(2,1)S(1)}, u32[]{:S(2)}, u32[]{:S(2)}) %collective-permute-start.4) | collective-permute-done | bytes 65568 | tf_op jit(solution)/shard_map/ppermute | solution.py:63
  36.8 2.4 %collective-permute-done.5 = bf16[2,128,128]{1,2,0:T(8,128)(2,1)S(1)} collective-permute-done((bf16[2,128,128]{1,2,0:T(8,128)(2,1)S(1)}, bf16[2,128,128]{1,2,0:T(8,128)(2,1)S(1)}, u32[]{:S(2)}, u32[]{:S(2)}) %collective-permute-start.5) | collective-permute-done | bytes 65568 | tf_op jit(solution)/shard_map/ppermute | solution.py:63
  39.2 0.6 fusion.61
  40.9 1.0 %fusion.8 = bf16[1,128,512]{1,2,0:T(8,128)(2,1)S(1)} fusion(f32[512,1024]{1,0:T(8,128)S(1)} %bitcast.160, f32[128,512]{1,0:T(8,128)S(1)} %get-tuple-element.61, f32[128,512]{1,0:T(8,128)S(1)} %get-tuple-element.62, f32[1024]{0:T(1024)S(1)} %fusion.118), kind=kOutput, calls=%fused_computation.17 | convolution fusion | flops 402980864 | bytes 2756608 | tf_op jit(solution)/shard_map/dot_general | solution.py:140
  41.9 1.0 %fusion.9 = bf16[1,128,512]{1,2,0:T(8,128)(2,1)S(1)} fusion(f32[512,1024]{1,0:T(8,128)S(1)} %bitcast.161, f32[128,512]{1,0:T(8,128)S(1)} %get-tuple-element.63, f32[128,512]{1,0:T(8,128)S(1)} %get-tuple-element.40, f32[1024]{0:T(1024)S(1)} %fusion.118), kind=kOutput, calls=%fused_computation.18 | convolution fusion | flops 402980864 | bytes 2756608 | tf_op jit(solution)/shard_map/dot_general | solution.py:140
  43.0 2.3 %collective-permute-start.7 = (bf16[2,128,128]{1,2,0:T(8,128)(2,1)S(1)}, bf16[2,128,128]{1,2,0:T(8,128)(2,1)S(1)}, u32[]{:S(2)}, u32[]{:S(2)}) collective-permute-start(bf16[2,128,128]{1,2,0:T(8,128)(2,1)S(1)} %get-tuple-element.78), channel_id=1, source_target_pairs={{0,12},{4,8},{8,4},{12,0},{1,13},{5,9},{9,5},{13,1},{2,14},{6,10},... | collective-permute-start | bytes 196616 | tf_op jit(solution)/shard_map/ppermute | solution.py:63
  45.3 2.2 %collective-permute-start.9 = (bf16[2,128,128]{1,2,0:T(8,128)(2,1)S(1)}, bf16[2,128,128]{1,2,0:T(8,128)(2,1)S(1)}, u32[]{:S(2)}, u32[]{:S(2)}) collective-permute-start(bf16[2,128,128]{1,2,0:T(8,128)(2,1)S(1)} %get-tuple-element.35), channel_id=1, source_target_pairs={{0,4},{4,0},{8,12},{12,8},{1,5},{5,1},{9,13},{13,9},{2,6},{6,2},{1... | collective-permute-start | bytes 196616 | tf_op jit(solution)/shard_map/ppermute | solution.py:63
  47.7 1.7 %collective-permute-done.7 = bf16[2,128,128]{1,2,0:T(8,128)(2,1)S(1)} collective-permute-done((bf16[2,128,128]{1,2,0:T(8,128)(2,1)S(1)}, bf16[2,128,128]{1,2,0:T(8,128)(2,1)S(1)}, u32[]{:S(2)}, u32[]{:S(2)}) %collective-permute-start.7) | collective-permute-done | bytes 65568 | tf_op jit(solution)/shard_map/ppermute | solution.py:63
  49.4 2.0 %collective-permute-done.8 = bf16[2,128,128]{1,2,0:T(8,128)(2,1)S(1)} collective-permute-done((bf16[2,128,128]{1,2,0:T(8,128)(2,1)S(1)}, bf16[2,128,128]{1,2,0:T(8,128)(2,1)S(1)}, u32[]{:S(2)}, u32[]{:S(2)}) %collective-permute-start.8) | collective-permute-done | bytes 65568 | tf_op jit(solution)/shard_map/ppermute | solution.py:63
  51.7 1.2 %fusion.3 = f32[128]{0:T(128)S(1)} fusion(f32[3,512,128]{1,2,0:T(8,128)S(1)} %convolution_bitcast_fusion.1, bf16[2048,3,512]{2,0,1:T(8,128)(2,1)S(1)} %bitcast.164, f32[128,2048]{1,0:T(8,128)S(1)} %get-tuple-element.94, f32[2048]{0:T(1024)S(1)} %copy-done.5, f32[128]{0:T(128)S(1)} %add_rsqrt_fusion, bf16[1,512,128]{1,2,0:T(8,128)(2,1)S(1)} %get-tuple-element.58, ...), kind=kOutput, calls=%fused_computation.9 | convolution fusion | flops 808058752 | bytes 8528896 | tf_op jit(solution)/shard_map/dr,dmc->mcr/dot_general | solution.py:205
  52.9 2.2 %fusion.10 = (f32[2048]{0:T(1024)S(1)}, f32[128,2048,1]{1,0,2:T(8,128)S(1)}) fusion(f32[128,2048]{1,0:T(8,128)S(1)} %get-tuple-element.94, f32[128]{0:T(128)S(1)} %add_rsqrt_fusion, bf16[2048,3,512]{2,0,1:T(8,128)(2,1)S(1)} %bitcast.164, bf16[1,512,128]{1,2,0:T(8,128)(2,1)S(1)} %get-tuple-element.58, bf16[1,512,128]{1,2,0:T(8,128)(2,1)S(1)} %get-tuple-element.57, ...), kind=kOutput, calls=%fused_computation.20 | convolution fusion | flops 806483968 | bytes 8790528 | tf_op jit(solution)/shard_map/mcr,dmc->rd/dot_general | solution.py:254
  55.1 1.6 %collective-permute-start.16 = (bf16[1,512,128]{1,2,0:T(8,128)(2,1)S(1)}, bf16[1,512,128]{1,2,0:T(8,128)(2,1)S(1)}, u32[]{:S(2)}, u32[]{:S(2)}) collective-permute-start(bf16[1,512,128]{1,2,0:T(8,128)(2,1)S(1)} %get-tuple-element.56), channel_id=1, source_target_pairs={{0,2},{2,0},{1,3},{3,1},{4,6},{6,4},{5,7},{7,5},{8,10},{10,8},{9,1... | collective-permute-start | bytes 393224 | tf_op jit(solution)/shard_map/ppermute | solution.py:46
  56.7 0.6 convolution_multiply_fusion.1
  57.3 0.7 fusion
  58.1 0.6 collective-permute-start.11
  59.2 1.0 %collective-permute-start.10 = (f32[21,512]{1,0:T(8,128)S(1)}, f32[21,512]{1,0:T(8,128)S(1)}, u32[]{:S(2)}, u32[]{:S(2)}) collective-permute-start(f32[21,512]{1,0:T(8,128)S(1)} %get-tuple-element.28), channel_id=1, source_target_pairs={{0,1},{1,0},{2,3},{3,2},{4,5},{5,4},{6,7},{7,6},{8,9},{9,8},{10,11... | collective-permute-start | bytes 129032 | tf_op jit(solution)/shard_map/ppermute | solution.py:63
  60.8 1.9 %fusion.25 = f32[128,512]{1,0:T(8,128)} fusion(f32[512,1024]{1,0:T(8,128)S(1)} %bitcast.162, f32[128,512]{1,0:T(8,128)S(1)} %get-tuple-element.65, f32[128,512]{1,0:T(8,128)S(1)} %get-tuple-element.64, f32[1024]{0:T(1024)S(1)} %fusion.118), kind=kOutput, calls=%fused_computation.47 | convolution fusion | flops 402915328 | bytes 2887680 | tf_op jit(solution)/shard_map/dot_general | solution.py:140
  62.8 0.8 %collective-permute-start.13 = (f32[21,512]{1,0:T(8,128)S(1)}, f32[21,512]{1,0:T(8,128)S(1)}, u32[]{:S(2)}, u32[]{:S(2)}) collective-permute-start(f32[21,512]{1,0:T(8,128)S(1)} %pad_add_fusion), channel_id=1, source_target_pairs={{0,4},{4,0},{8,12},{12,8},{1,5},{5,1},{9,13},{13,9},{2,6},{6,2},{1... | collective-permute-start | bytes 129032 | tf_op jit(solution)/shard_map/ppermute | solution.py:63
  63.6 2.3 %collective-permute-start.14 = (f32[21,512]{1,0:T(8,128)S(1)}, f32[21,512]{1,0:T(8,128)S(1)}, u32[]{:S(2)}, u32[]{:S(2)}) collective-permute-start(f32[21,512]{1,0:T(8,128)S(1)} %pad_add_fusion), channel_id=1, source_target_pairs={{0,8},{4,12},{8,0},{12,4},{1,9},{5,13},{9,1},{13,5},{2,10},{6,14},... | collective-permute-start | bytes 129032 | tf_op jit(solution)/shard_map/ppermute | solution.py:63
  66.0 1.3 %collective-permute-start.15 = (f32[21,512]{1,0:T(8,128)S(1)}, f32[21,512]{1,0:T(8,128)S(1)}, u32[]{:S(2)}, u32[]{:S(2)}) collective-permute-start(f32[21,512]{1,0:T(8,128)S(1)} %pad_add_fusion), channel_id=1, source_target_pairs={{0,12},{4,8},{8,4},{12,0},{1,13},{5,9},{9,5},{13,1},{2,14},{6,10},... | collective-permute-start | bytes 129032 | tf_op jit(solution)/shard_map/ppermute | solution.py:63
  68.0 0.9 %fusion.7 = bf16[128,512]{1,0:T(8,128)(2,1)} fusion(f32[128,512]{1,0:T(8,128)S(1)} %fusion.28, f32[128,512]{1,0:T(8,128)S(1)} %fusion.30, f32[128,512]{1,0:T(8,128)S(1)} %fusion.32, bf16[2048,512]{1,0:T(8,128)(2,1)S(1)} %copy-done.3, f32[128,2048]{1,0:T(8,128)S(1)} %get-tuple-element.94, s32[]{:T(128)S(6)} %select_n.819, ...), kind=kOutput, calls=%fused_computation.16 | convolution fusion | flops 67633152 | bytes 2228231 | tf_op jit(solution)/shard_map/cr,cd->rd/dot_general | solution.py:239
  68.9 1.2 %collective-permute-done.14 = f32[21,512]{1,0:T(8,128)S(1)} collective-permute-done((f32[21,512]{1,0:T(8,128)S(1)}, f32[21,512]{1,0:T(8,128)S(1)}, u32[]{:S(2)}, u32[]{:S(2)}) %collective-permute-start.14) | collective-permute-done | bytes 43040 | tf_op jit(solution)/shard_map/ppermute | solution.py:63
  70.1 1.7 %collective-permute-done.15 = f32[21,512]{1,0:T(8,128)S(1)} collective-permute-done((f32[21,512]{1,0:T(8,128)S(1)}, f32[21,512]{1,0:T(8,128)S(1)}, u32[]{:S(2)}, u32[]{:S(2)}) %collective-permute-start.15) | collective-permute-done | bytes 43040 | tf_op jit(solution)/shard_map/ppermute | solution.py:63
  71.9 0.6 slice.274
  72.5 0.6 copy.21
  (89 shorter events, 6.5 us)
Async XLA Ops:
  0.6 13.8 %copy-start = (f32[1,1,128,512]{3,2,1,0:T(8,128)S(1)}, f32[1,1,128,512]{3,2,1,0:T(8,128)}, u32[]{:S(2)}) copy-start(f32[1,1,128,512]{3,2,1,0:T(8,128)} %param.11) | copy-start | bytes 786436
  0.7 6.4 %copy-start.11 = (s32[128]{0:T(128)S(1)}, s32[128]{0:T(128)}, u32[]{:S(2)}) copy-start(s32[128]{0:T(128)} %param.7) | copy-start | bytes 1540
  4.1 24.3 %collective-permute-start.1 = (f32[128,512]{1,0:T(8,128)}, f32[128,512]{1,0:T(8,128)}, u32[]{:S(2)}, u32[]{:S(2)}) collective-permute-start(f32[128,512]{1,0:T(8,128)} %get-tuple-element.59), channel_id=1, source_target_pairs={{0,1},{1,0},{2,3},{3,2},{4,5},{5,4},{6,7},{7,6},{8,9},{9,8},{10,11... | collective-permute-start | bytes 786440 | tf_op jit(solution)/shard_map/ppermute | solution.py:63
  4.6 23.8 %collective-permute-start.2 = (f32[128,512]{1,0:T(8,128)}, f32[128,512]{1,0:T(8,128)}, u32[]{:S(2)}, u32[]{:S(2)}) collective-permute-start(f32[128,512]{1,0:T(8,128)} %get-tuple-element.60), channel_id=1, source_target_pairs={{0,2},{1,3},{2,0},{3,1},{4,6},{5,7},{6,4},{7,5},{8,10},{9,11},{10,... | collective-permute-start | bytes 786440 | tf_op jit(solution)/shard_map/ppermute | solution.py:63
  7.7 13.9 %collective-permute-start = (s32[3]{0:T(128)}, s32[3]{0:T(128)}, u32[]{:S(2)}, u32[]{:S(2)}) collective-permute-start(s32[3]{0:T(128)} %slice_add_fusion.2), channel_id=1, source_target_pairs={{0,4},{4,8},{8,12},{1,5},{5,9},{9,13},{2,6},{6,10},{10,14},{3,7},{... | collective-permute-start | bytes 44 | tf_op jit(solution)/shard_map/ppermute | solution.py:16
  12.5 15.9 %collective-permute-start.3 = (f32[128,512]{1,0:T(8,128)}, f32[128,512]{1,0:T(8,128)}, u32[]{:S(2)}, u32[]{:S(2)}) collective-permute-start(f32[128,512]{1,0:T(8,128)} %select_select_fusion), channel_id=1, source_target_pairs={{0,3},{1,2},{2,1},{3,0},{4,7},{5,6},{6,5},{7,4},{8,11},{9,10},{10,... | collective-permute-start | bytes 786440 | tf_op jit(solution)/shard_map/ppermute | solution.py:63
  15.2 1.2 %copy-start.1 = (f32[128,1024]{1,0:T(8,128)}, f32[128,1024]{1,0:T(8,128)S(1)}, u32[]{:S(2)}) copy-start(f32[128,1024]{1,0:T(8,128)S(1)} %convolution_bitcast_fusion.2) | copy-start | bytes 1572868
  16.3 8.1 %copy-start.5 = (f32[2048]{0:T(1024)S(1)}, f32[2048]{0:T(1024)}, u32[]{:S(2)}) copy-start(f32[2048]{0:T(1024)} %param.9) | copy-start | bytes 24580
  28.3 6.0 %copy-start.4 = (bf16[128,512]{1,0:T(8,128)(2,1)S(1)}, bf16[128,512]{1,0:T(8,128)(2,1)}, u32[]{:S(2)}) copy-start(bf16[128,512]{1,0:T(8,128)(2,1)} %param.13) | copy-start | bytes 393220
  28.3 6.0 %copy-start.6 = (pred[128,5]{0,1:T(8,128)(4,1)S(1)}, pred[128,5]{0,1:T(8,128)(4,1)}, u32[]{:S(2)}) copy-start(pred[128,5]{0,1:T(8,128)(4,1)} %iota_compare_fusion.5) | copy-start | bytes 1924
  29.8 6.9 %collective-permute-start.4 = (bf16[2,128,128]{1,2,0:T(8,128)(2,1)S(1)}, bf16[2,128,128]{1,2,0:T(8,128)(2,1)S(1)}, u32[]{:S(2)}, u32[]{:S(2)}) collective-permute-start(bf16[2,128,128]{1,2,0:T(8,128)(2,1)S(1)} %get-tuple-element.83), channel_id=1, source_target_pairs={{0,12},{4,8},{8,4},{12,0},{1,13},{5,9},{9,5},{13,1},{2,14},{6,10},... | collective-permute-start | bytes 196616 | tf_op jit(solution)/shard_map/ppermute | solution.py:63
  31.0 8.1 %collective-permute-start.5 = (bf16[2,128,128]{1,2,0:T(8,128)(2,1)S(1)}, bf16[2,128,128]{1,2,0:T(8,128)(2,1)S(1)}, u32[]{:S(2)}, u32[]{:S(2)}) collective-permute-start(bf16[2,128,128]{1,2,0:T(8,128)(2,1)S(1)} %get-tuple-element.82), channel_id=1, source_target_pairs={{0,8},{4,12},{8,0},{12,4},{1,9},{5,13},{9,1},{13,5},{2,10},{6,14},... | collective-permute-start | bytes 196616 | tf_op jit(solution)/shard_map/ppermute | solution.py:63
  32.4 6.7 %collective-permute-start.6 = (bf16[2,128,128]{1,2,0:T(8,128)(2,1)S(1)}, bf16[2,128,128]{1,2,0:T(8,128)(2,1)S(1)}, u32[]{:S(2)}, u32[]{:S(2)}) collective-permute-start(bf16[2,128,128]{1,2,0:T(8,128)(2,1)S(1)} %get-tuple-element.45), channel_id=1, source_target_pairs={{0,4},{4,0},{8,12},{12,8},{1,5},{5,1},{9,13},{13,9},{2,6},{6,2},{1... | collective-permute-start | bytes 196616 | tf_op jit(solution)/shard_map/ppermute | solution.py:63
  39.2 1.2 %copy-start.2 = (f32[128,1024]{1,0:T(8,128)S(1)}, f32[128,1024]{1,0:T(8,128)}, u32[]{:S(2)}) copy-start(f32[128,1024]{1,0:T(8,128)} %copy-done.1) | copy-start | bytes 1572868
  39.2 1.2 %copy-start.7 = (pred[512]{0:T(512)(128)(4,1)S(1)}, pred[512]{0:T(512)(128)(4,1)}, u32[]{:S(2)}) copy-start(pred[512]{0:T(512)(128)(4,1)} %iota_compare_fusion.6) | copy-start | bytes 1540
  40.8 10.9 %slice-start = ((s8[6291456]{0:T(1024)(128)(4,1)}), s8[4194304]{0:T(1024)(128)(4,1)S(1)}, s32[]{:S(2)}) async-start(s8[6291456]{0:T(1024)(128)(4,1)} %bitcast.163), calls=%async_computation | async-start | bytes 8388608
  41.9 5.6 %copy-start.8 = (s32[128]{0:T(128)S(1)}, s32[128]{0:T(128)}, u32[]{:S(2)}) copy-start(s32[128]{0:T(128)} %get-tuple-element.101) | copy-start | bytes 1540
  41.9 5.6 %copy-start.9 = (s32[128]{0:T(128)S(1)}, s32[128]{0:T(128)}, u32[]{:S(2)}) copy-start(s32[128]{0:T(128)} %get-tuple-element.102) | copy-start | bytes 1540
  41.9 5.6 %copy-start.10 = (pred[128]{0:T(512)(128)(4,1)S(1)}, pred[128]{0:T(512)(128)(4,1)}, u32[]{:S(2)}) copy-start(pred[128]{0:T(512)(128)(4,1)} %compare_and_fusion) | copy-start | bytes 388
  42.9 8.8 %slice-start.1 = ((s8[6291456]{0:T(1024)(128)(4,1)}), s8[2097152]{0:T(1024)(128)(4,1)S(1)}, s32[]{:S(2)}) async-start(s8[6291456]{0:T(1024)(128)(4,1)} %bitcast.163), calls=%async_computation.1 | async-start | bytes 4194304
  43.0 6.4 %collective-permute-start.7 = (bf16[2,128,128]{1,2,0:T(8,128)(2,1)S(1)}, bf16[2,128,128]{1,2,0:T(8,128)(2,1)S(1)}, u32[]{:S(2)}, u32[]{:S(2)}) collective-permute-start(bf16[2,128,128]{1,2,0:T(8,128)(2,1)S(1)} %get-tuple-element.78), channel_id=1, source_target_pairs={{0,12},{4,8},{8,4},{12,0},{1,13},{5,9},{9,5},{13,1},{2,14},{6,10},... | collective-permute-start | bytes 196616 | tf_op jit(solution)/shard_map/ppermute | solution.py:63
  45.3 6.1 %collective-permute-start.8 = (bf16[2,128,128]{1,2,0:T(8,128)(2,1)S(1)}, bf16[2,128,128]{1,2,0:T(8,128)(2,1)S(1)}, u32[]{:S(2)}, u32[]{:S(2)}) collective-permute-start(bf16[2,128,128]{1,2,0:T(8,128)(2,1)S(1)} %get-tuple-element.77), channel_id=1, source_target_pairs={{0,8},{4,12},{8,0},{12,4},{1,9},{5,13},{9,1},{13,5},{2,10},{6,14},... | collective-permute-start | bytes 196616 | tf_op jit(solution)/shard_map/ppermute | solution.py:63
  45.3 6.1 %collective-permute-start.9 = (bf16[2,128,128]{1,2,0:T(8,128)(2,1)S(1)}, bf16[2,128,128]{1,2,0:T(8,128)(2,1)S(1)}, u32[]{:S(2)}, u32[]{:S(2)}) collective-permute-start(bf16[2,128,128]{1,2,0:T(8,128)(2,1)S(1)} %get-tuple-element.35), channel_id=1, source_target_pairs={{0,4},{4,0},{8,12},{12,8},{1,5},{5,1},{9,13},{13,9},{2,6},{6,2},{1... | collective-permute-start | bytes 196616 | tf_op jit(solution)/shard_map/ppermute | solution.py:63
  55.1 5.6 %collective-permute-start.16 = (bf16[1,512,128]{1,2,0:T(8,128)(2,1)S(1)}, bf16[1,512,128]{1,2,0:T(8,128)(2,1)S(1)}, u32[]{:S(2)}, u32[]{:S(2)}) collective-permute-start(bf16[1,512,128]{1,2,0:T(8,128)(2,1)S(1)} %get-tuple-element.56), channel_id=1, source_target_pairs={{0,2},{2,0},{1,3},{3,1},{4,6},{6,4},{5,7},{7,5},{8,10},{10,8},{9,1... | collective-permute-start | bytes 393224 | tf_op jit(solution)/shard_map/ppermute | solution.py:46
  58.0 9.2 %copy-start.3 = (bf16[2048,512]{1,0:T(8,128)(2,1)S(1)}, bf16[2048,512]{1,0:T(8,128)(2,1)}, u32[]{:S(2)}) copy-start(bf16[2048,512]{1,0:T(8,128)(2,1)} %param.12) | copy-start | bytes 6291460
  58.1 4.6 %collective-permute-start.11 = (f32[21,512]{1,0:T(8,128)S(1)}, f32[21,512]{1,0:T(8,128)S(1)}, u32[]{:S(2)}, u32[]{:S(2)}) collective-permute-start(f32[21,512]{1,0:T(8,128)S(1)} %get-tuple-element.84), channel_id=1, source_target_pairs={{0,2},{1,3},{2,0},{3,1},{4,6},{5,7},{6,4},{7,5},{8,10},{9,11},{10,... | collective-permute-start | bytes 129032 | tf_op jit(solution)/shard_map/ppermute | solution.py:63
  58.7 4.0 %collective-permute-start.12 = (f32[21,512]{1,0:T(8,128)S(1)}, f32[21,512]{1,0:T(8,128)S(1)}, u32[]{:S(2)}, u32[]{:S(2)}) collective-permute-start(f32[21,512]{1,0:T(8,128)S(1)} %get-tuple-element.85), channel_id=1, source_target_pairs={{0,3},{1,2},{2,1},{3,0},{4,7},{5,6},{6,5},{7,4},{8,11},{9,10},{10,... | collective-permute-start | bytes 129032 | tf_op jit(solution)/shard_map/ppermute | solution.py:63
  59.2 3.5 %collective-permute-start.10 = (f32[21,512]{1,0:T(8,128)S(1)}, f32[21,512]{1,0:T(8,128)S(1)}, u32[]{:S(2)}, u32[]{:S(2)}) collective-permute-start(f32[21,512]{1,0:T(8,128)S(1)} %get-tuple-element.28), channel_id=1, source_target_pairs={{0,1},{1,0},{2,3},{3,2},{4,5},{5,4},{6,7},{7,6},{8,9},{9,8},{10,11... | collective-permute-start | bytes 129032 | tf_op jit(solution)/shard_map/ppermute | solution.py:63
  60.7 6.5 %collective-permute-start.17 = (bf16[2,512,128]{1,2,0:T(8,128)(2,1)S(1)}, bf16[2,512,128]{1,2,0:T(8,128)(2,1)S(1)}, u32[]{:S(2)}, u32[]{:S(2)}) collective-permute-start(bf16[2,512,128]{1,2,0:T(8,128)(2,1)S(1)} %pad_maximum_fusion.4), channel_id=1, source_target_pairs={{0,1},{1,0},{2,3},{3,2},{4,5},{5,4},{6,7},{7,6},{8,9},{9,8},{10,11... | collective-permute-start | bytes 786440 | tf_op jit(solution)/shard_map/ppermute | solution.py:46
  62.8 6.1 %collective-permute-start.13 = (f32[21,512]{1,0:T(8,128)S(1)}, f32[21,512]{1,0:T(8,128)S(1)}, u32[]{:S(2)}, u32[]{:S(2)}) collective-permute-start(f32[21,512]{1,0:T(8,128)S(1)} %pad_add_fusion), channel_id=1, source_target_pairs={{0,4},{4,0},{8,12},{12,8},{1,5},{5,1},{9,13},{13,9},{2,6},{6,2},{1... | collective-permute-start | bytes 129032 | tf_op jit(solution)/shard_map/ppermute | solution.py:63
  63.6 6.5 %collective-permute-start.14 = (f32[21,512]{1,0:T(8,128)S(1)}, f32[21,512]{1,0:T(8,128)S(1)}, u32[]{:S(2)}, u32[]{:S(2)}) collective-permute-start(f32[21,512]{1,0:T(8,128)S(1)} %pad_add_fusion), channel_id=1, source_target_pairs={{0,8},{4,12},{8,0},{12,4},{1,9},{5,13},{9,1},{13,5},{2,10},{6,14},... | collective-permute-start | bytes 129032 | tf_op jit(solution)/shard_map/ppermute | solution.py:63
  66.0 5.9 %collective-permute-start.15 = (f32[21,512]{1,0:T(8,128)S(1)}, f32[21,512]{1,0:T(8,128)S(1)}, u32[]{:S(2)}, u32[]{:S(2)}) collective-permute-start(f32[21,512]{1,0:T(8,128)S(1)} %pad_add_fusion), channel_id=1, source_target_pairs={{0,12},{4,8},{8,4},{12,0},{1,13},{5,9},{9,5},{13,1},{2,14},{6,10},... | collective-permute-start | bytes 129032 | tf_op jit(solution)/shard_map/ppermute | solution.py:63

commit v9 on v8

--- a/solution.py
+++ b/solution.py
@@ -63,11 +63,11 @@
     return lax.ppermute(x, axes, [(i, i ^ offset) for i in range(count)])
 
 
-def reduce_blocks_cp(x, width):
+def reduce_blocks_cp(x, width, axis=1):
     axes = ("chan", "pair")
     count = lax.axis_size("chan") * lax.axis_size("pair")
     me = lax.axis_index(axes)
-    blocks = [x[:, g * width : (g + 1) * width] for g in range(count)]
+    blocks = [lax.slice_in_dim(x, g * width, (g + 1) * width, axis=axis) for g in range(count)]
 
     def pick(index):
         out = blocks[0]
@@ -211,8 +211,8 @@
     mixed_in = (key_part * value_part).astype(jnp.bfloat16)
     grad_scale = 1.0 / math.sqrt(length)
     groups = lax.axis_size("chan") * lax.axis_size("pair")
-    gated_partial = jnp.einsum("rd,cd->rc", cotangent, out_proj, preferred_element_type=jnp.float32)
-    d_gated = reduce_blocks_cp(gated_partial, local_width).T * grad_scale
+    gated_partial = jnp.einsum("cd,rd->cr", out_proj, cotangent, preferred_element_type=jnp.float32)
+    d_gated = reduce_blocks_cp(gated_partial, local_width, axis=0) * grad_scale
     dft = dft_matrix(length)
     filter_rows = long_filter.reshape(long_filter.shape[2], long_filter.shape[3])
     spec_g = add_conj_flip(forward_dft(filter_rows, dft))

time: 73.5 us -> 76.5 us (1.041)
  matrix products: 20 us -> 23.4 us
    dot_general x1, matrix products: 3.86 us -> 5.43 us  [per_device(): jnp.einsum('dr,dmc->mcr', hidden, in_proj, preferred_element_type=jnp.flo...]
    dot_general x1, matrix products: 1.21 us -> 2.69 us  [per_device(): jnp.einsum('dr,dmc->mcr', residual, in_proj, preferred_element_type=jnp.f...]
  transfers between devices with their start and end apart: 18 -> 18, of which waited for: 7 -> 7; matrix products, arithmetic and copies ran while one was open for 31% -> 32% of each run, Pallas kernels for 0% -> 0%
where the time goes in v9:
time: 76.5 us; the launch traced here: 76.2 us
  starting transfers between devices  24.3 us (32%)
  matrix products  23.4 us (31%)
  waiting for transfers between devices  11.6 us (15%)
  other arithmetic  11 us (14%)
  local copies, waits for them, and re-layouts  4.77 us (6%)
  between operations  1.15 us (2%)
    ppermute x15, starting transfers between devices, group_exchange(): return lax.ppermute(x, axes, [(i, i ^ offset) for i in range(count)])  18.6 us
    ppermute x15, waiting for transfers between devices, group_exchange(): return lax.ppermute(x, axes, [(i, i ^ offset) for i in range(count)])  11.2 us
    dot_general x1, matrix products, per_device(): jnp.einsum('dr,dmc->mcr', hidden, in_proj, preferred_element_type=jnp.flo...  5.43 us
    dot_general x3, matrix products, inverse_dft(): lax.dot_general(spec * weight, dft, (((1,), (1,)), ((), ())), precision=T...  4.27 us
    ppermute x1, starting transfers between devices, from_behind(): lax.ppermute(value, axis, [(source, source + steps) for source in range(f...  4.06 us
    dot_general x1, matrix products, per_device(): jnp.einsum('dr,dmc->mcr', residual, in_proj, preferred_element_type=jnp.f...  2.69 us
    dot_general x1, matrix products, per_device(): jnp.einsum('cd,rd->cr', out_proj, cotangent, preferred_element_type=jnp.f...  2.33 us
    dot_general x1, matrix products, per_device(): jnp.einsum('mcr,dmc->rd', d_proj, in_proj, preferred_element_type=jnp.flo...  2.23 us
  transfers between devices with their start and end apart: 18, of which 7 were waited for; matrix products, arithmetic and copies ran while one was open for 32% of the time, Pallas kernels for 0%

profile of v9, /device:TPU:0, one launch (start us, length us, event | category | flops | bytes accessed | tf_op | source)
XLA Modules:
  0.0 76.2 jit_solution(15045056464413562042)
XLA Ops:
  0.7 2.3 %fusion.137 = f32[2048,128]{1,0:T(8,128)S(1)} fusion(bf16[2048,512]{1,0:T(8,128)(2,1)} %param.12, bf16[128,512]{1,0:T(8,128)(2,1)} %param.13), kind=kOutput, calls=%fused_computation.255 | convolution fusion | flops 268435456 | bytes 3276800 | tf_op jit(solution)/shard_map/cd,rd->cr/dot_general | solution.py:214
  3.0 0.9 %select_select_fusion.2 = (f32[512,128]{1,0:T(8,128)}, f32[512,128]{1,0:T(8,128)}) fusion(f32[2048,128]{1,0:T(8,128)S(1)} %fusion.137, pred[]{:T(512)S(6)} %eq.288, pred[]{:T(512)S(6)} %eq.287, pred[]{:T(512)S(6)} %eq.286, pred[]{:T(512)S(6)} %eq.291, pred[]{:T(512)S(6)} %eq.290, pred[]{:T(512)S(6)} %eq.289), kind=kLoop, calls=%fused_computation.117 | loop fusion | flops 393216 | bytes 1572870 | tf_op jit(solution)/shard_map/jit(_where)/select_n | solution.py:75
  4.4 2.5 %collective-permute-start.2 = (f32[512,128]{1,0:T(8,128)}, f32[512,128]{1,0:T(8,128)}, u32[]{:S(2)}, u32[]{:S(2)}) collective-permute-start(f32[512,128]{1,0:T(8,128)} %get-tuple-element.60), channel_id=1, source_target_pairs={{0,2},{1,3},{2,0},{3,1},{4,6},{5,7},{6,4},{7,5},{8,10},{9,11},{10,... | collective-permute-start | bytes 786440 | tf_op jit(solution)/shard_map/ppermute | solution.py:63
  6.9 0.6 slice_add_fusion.2
  7.4 4.1 %collective-permute-start = (s32[3]{0:T(128)}, s32[3]{0:T(128)}, u32[]{:S(2)}, u32[]{:S(2)}) collective-permute-start(s32[3]{0:T(128)} %slice_add_fusion.2), channel_id=1, source_target_pairs={{0,4},{4,8},{8,12},{1,5},{5,9},{9,13},{2,6},{6,10},{10,14},{3,7},{... | collective-permute-start | bytes 44 | tf_op jit(solution)/shard_map/ppermute | solution.py:16
  11.5 0.8 select_select_fusion
  12.3 0.6 iota_compare_fusion.5
  13.3 0.6 fusion.98
  14.2 0.7 convolution_bitcast_fusion.2
  14.9 1.1 %fusion.135 = (f32[127,1024]{1,0:T(8,128)}, f32[127,1024]{1,0:T(8,128)}) fusion(f32[128,1024]{1,0:T(8,128)S(1)} %convolution_bitcast_fusion.2), kind=kLoop, calls=%fused_computation.253 | loop fusion | bytes 2080768 | tf_op jit(solution)/shard_map/jit(_roll_static)/slice | solution.py:167
  16.1 0.6 fusion.134
  17.2 0.6 compare_and_fusion
  18.3 0.9 %copy.18 = bf16[4,5,2048]{2,1,0:T(8,128)(2,1)S(1)} copy(bf16[4,5,2048]{2,0,1:T(4,128)(2,1)} %param.8) | data formatting | bytes 163840 | tf_op args[1]
  19.2 0.7 reshape.262
  19.9 1.4 %maximum_select_fusion = f32[128,1024]{1,0:T(8,128)S(1)} fusion(f32[1,1024]{1,0:T(1,128)} %get-tuple-element.69, f32[127,1024]{1,0:T(8,128)} %get-tuple-element.71, f32[127,1024]{1,0:T(8,128)} %get-tuple-element.70, f32[1,1024]{1,0:T(1,128)S(1)} %get-tuple-element.68, s32[128]{0:T(128)} %get-tuple-element.101, s32[128]{0:T(128)} %get-tuple-element.102, ...), kind=kLoop, calls=%fused_computation.39 | loop fusion | flops 655360 | bytes 1574016 | tf_op jit(solution)/shard_map/jit(_where)/select_n | solution.py:168
  21.3 0.7 broadcast_add_fusion.1
  22.0 0.7 pad_add_fusion.2
  22.8 1.3 %multiply_reduce_fusion = (f32[128]{0:T(128)S(1)}, f32[128,2048]{1,0:T(8,128)S(1)}) fusion(bf16[20,2048]{1,0:T(8,128)(2,1)} %reshape.262, pred[128,5]{0,1:T(8,128)(4,1)S(1)} %get-tuple-element.97, pred[128,5]{0,1:T(8,128)(4,1)S(1)} %get-tuple-element.98, pred[128,5]{0,1:T(8,128)(4,1)S(1)} %iota_compare_fusion.4, pred[128,5]{0,1:T(8,128)(4,1)} %iota_compare_fusion.5), kind=kOutput, calls=%fused_computation.24 | convolution fusion | flops 11017600 | bytes 1133568 | tf_op jit(solution)/shard_map/dot_general | solution.py:198
  24.2 5.4 %convolution_bitcast_fusion.1 = f32[3,512,128]{2,1,0:T(8,128)S(1)} fusion(bf16[2048,3,512]{2,0,1:T(8,128)(2,1)} %param.10, f32[128,2048]{1,0:T(8,128)S(1)} %get-tuple-element.94, f32[2048]{0:T(1024)S(1)} %copy-done.5, f32[128]{0:T(128)S(1)} %add_rsqrt_fusion), kind=kOutput, calls=%fused_computation.5 | convolution fusion | flops 806092800 | bytes 8135168 | tf_op jit(solution)/shard_map/dr,dmc->mcr/dot_general | solution.py:203
  29.7 1.2 %fusion.57 = (bf16[1,512,128]{2,1,0:T(8,128)(2,1)S(1)}, f32[512,128]{1,0:T(8,128)S(1)}) fusion(f32[3,512,128]{2,1,0:T(8,128)S(1)} %convolution_bitcast_fusion.1, f32[512,128]{1,0:T(8,128)} %collective-permute-done.3, f32[512,128]{1,0:T(8,128)} %collective-permute-done.2, f32[512,128]{1,0:T(8,128)} %collective-permute-done.1, f32[2048,128]{1,0:T(8,128)S(1)} %fusion.137, ...), kind=kLoop, calls=%fused_computation.130 | loop fusion | flops 589824 | bytes 2490371 | tf_op jit(solution)/shard_map/stack | solution.py:221
  31.0 1.2 %collective-permute-start.4 = (bf16[2,128,128]{2,1,0:T(8,128)(2,1)S(1)}, bf16[2,128,128]{2,1,0:T(8,128)(2,1)S(1)}, u32[]{:S(2)}, u32[]{:S(2)}) collective-permute-start(bf16[2,128,128]{2,1,0:T(8,128)(2,1)S(1)} %get-tuple-element.83), channel_id=1, source_target_pairs={{0,12},{4,8},{8,4},{12,0},{1,13},{5,9},{9,5},{13,1},{2,14},{6,10},... | collective-permute-start | bytes 196616 | tf_op jit(solution)/shard_map/ppermute | solution.py:63
  32.2 1.3 %collective-permute-start.5 = (bf16[2,128,128]{2,1,0:T(8,128)(2,1)S(1)}, bf16[2,128,128]{2,1,0:T(8,128)(2,1)S(1)}, u32[]{:S(2)}, u32[]{:S(2)}) collective-permute-start(bf16[2,128,128]{2,1,0:T(8,128)(2,1)S(1)} %get-tuple-element.82), channel_id=1, source_target_pairs={{0,8},{4,12},{8,0},{12,4},{1,9},{5,13},{9,1},{13,5},{2,10},{6,14},... | collective-permute-start | bytes 196616 | tf_op jit(solution)/shard_map/ppermute | solution.py:63
  33.6 1.9 %collective-permute-start.6 = (bf16[2,128,128]{2,1,0:T(8,128)(2,1)S(1)}, bf16[2,128,128]{2,1,0:T(8,128)(2,1)S(1)}, u32[]{:S(2)}, u32[]{:S(2)}) collective-permute-start(bf16[2,128,128]{2,1,0:T(8,128)(2,1)S(1)} %get-tuple-element.45), channel_id=1, source_target_pairs={{0,4},{4,0},{8,12},{12,8},{1,5},{5,1},{9,13},{13,9},{2,6},{6,2},{1... | collective-permute-start | bytes 196616 | tf_op jit(solution)/shard_map/ppermute | solution.py:63
  35.7 2.3 %collective-permute-done.4 = bf16[2,128,128]{2,1,0:T(8,128)(2,1)S(1)} collective-permute-done((bf16[2,128,128]{2,1,0:T(8,128)(2,1)S(1)}, bf16[2,128,128]{2,1,0:T(8,128)(2,1)S(1)}, u32[]{:S(2)}, u32[]{:S(2)}) %collective-permute-start.4) | collective-permute-done | bytes 65568 | tf_op jit(solution)/shard_map/ppermute | solution.py:63
  38.0 2.3 %collective-permute-done.5 = bf16[2,128,128]{2,1,0:T(8,128)(2,1)S(1)} collective-permute-done((bf16[2,128,128]{2,1,0:T(8,128)(2,1)S(1)}, bf16[2,128,128]{2,1,0:T(8,128)(2,1)S(1)}, u32[]{:S(2)}, u32[]{:S(2)}) %collective-permute-start.5) | collective-permute-done | bytes 65568 | tf_op jit(solution)/shard_map/ppermute | solution.py:63
  42.1 1.2 %fusion.8 = bf16[1,128,512]{2,1,0:T(8,128)(2,1)S(1)} fusion(f32[512,1024]{1,0:T(8,128)S(1)} %bitcast.153, f32[128,512]{1,0:T(8,128)S(1)} %get-tuple-element.61, f32[128,512]{1,0:T(8,128)S(1)} %get-tuple-element.62, f32[1024]{0:T(1024)S(1)} %fusion.118), kind=kOutput, calls=%fused_computation.17 | convolution fusion | flops 402980864 | bytes 2756608 | tf_op jit(solution)/shard_map/dot_general | solution.py:140
  43.3 1.2 %fusion.9 = bf16[1,128,512]{2,1,0:T(8,128)(2,1)S(1)} fusion(f32[512,1024]{1,0:T(8,128)S(1)} %bitcast.154, f32[128,512]{1,0:T(8,128)S(1)} %get-tuple-element.63, f32[128,512]{1,0:T(8,128)S(1)} %get-tuple-element.40, f32[1024]{0:T(1024)S(1)} %fusion.118), kind=kOutput, calls=%fused_computation.18 | convolution fusion | flops 402980864 | bytes 2756608 | tf_op jit(solution)/shard_map/dot_general | solution.py:140
  44.6 2.3 %collective-permute-start.7 = (bf16[2,128,128]{2,1,0:T(8,128)(2,1)S(1)}, bf16[2,128,128]{2,1,0:T(8,128)(2,1)S(1)}, u32[]{:S(2)}, u32[]{:S(2)}) collective-permute-start(bf16[2,128,128]{2,1,0:T(8,128)(2,1)S(1)} %get-tuple-element.78), channel_id=1, source_target_pairs={{0,12},{4,8},{8,4},{12,0},{1,13},{5,9},{9,5},{13,1},{2,14},{6,10},... | collective-permute-start | bytes 196616 | tf_op jit(solution)/shard_map/ppermute | solution.py:63
  46.9 2.2 %collective-permute-start.9 = (bf16[2,128,128]{2,1,0:T(8,128)(2,1)S(1)}, bf16[2,128,128]{2,1,0:T(8,128)(2,1)S(1)}, u32[]{:S(2)}, u32[]{:S(2)}) collective-permute-start(bf16[2,128,128]{2,1,0:T(8,128)(2,1)S(1)} %get-tuple-element.35), channel_id=1, source_target_pairs={{0,4},{4,0},{8,12},{12,8},{1,5},{5,1},{9,13},{13,9},{2,6},{6,2},{1... | collective-permute-start | bytes 196616 | tf_op jit(solution)/shard_map/ppermute | solution.py:63
  49.3 1.7 %collective-permute-done.7 = bf16[2,128,128]{2,1,0:T(8,128)(2,1)S(1)} collective-permute-done((bf16[2,128,128]{2,1,0:T(8,128)(2,1)S(1)}, bf16[2,128,128]{2,1,0:T(8,128)(2,1)S(1)}, u32[]{:S(2)}, u32[]{:S(2)}) %collective-permute-start.7) | collective-permute-done | bytes 65568 | tf_op jit(solution)/shard_map/ppermute | solution.py:63
  51.0 2.0 %collective-permute-done.8 = bf16[2,128,128]{2,1,0:T(8,128)(2,1)S(1)} collective-permute-done((bf16[2,128,128]{2,1,0:T(8,128)(2,1)S(1)}, bf16[2,128,128]{2,1,0:T(8,128)(2,1)S(1)}, u32[]{:S(2)}, u32[]{:S(2)}) %collective-permute-start.8) | collective-permute-done | bytes 65568 | tf_op jit(solution)/shard_map/ppermute | solution.py:63
  53.3 2.7 %fusion.3 = f32[128]{0:T(128)S(1)} fusion(f32[3,512,128]{2,1,0:T(8,128)S(1)} %convolution_bitcast_fusion.1, bf16[2048,3,512]{2,0,1:T(8,128)(2,1)S(1)} %bitcast.157, f32[128,2048]{1,0:T(8,128)S(1)} %get-tuple-element.94, f32[2048]{0:T(1024)S(1)} %copy-done.5, f32[128]{0:T(128)S(1)} %add_rsqrt_fusion, bf16[1,512,128]{2,1,0:T(8,128)(2,1)S(1)} %get-tuple-element.58, ...), kind=kOutput, calls=%fused_computation.9 | convolution fusion | flops 808058752 | bytes 8528896 | tf_op jit(solution)/shard_map/dr,dmc->mcr/dot_general | solution.py:205
  56.0 2.2 %fusion.10 = (f32[2048]{0:T(1024)S(1)}, f32[128,2048,1]{1,0,2:T(8,128)S(1)}) fusion(f32[128,2048]{1,0:T(8,128)S(1)} %get-tuple-element.94, f32[128]{0:T(128)S(1)} %add_rsqrt_fusion, bf16[2048,3,512]{2,0,1:T(8,128)(2,1)S(1)} %bitcast.157, bf16[1,512,128]{2,1,0:T(8,128)(2,1)S(1)} %get-tuple-element.58, bf16[1,512,128]{2,1,0:T(8,128)(2,1)S(1)} %get-tuple-element.57, ...), kind=kOutput, calls=%fused_computation.20 | convolution fusion | flops 806483968 | bytes 8790528 | tf_op jit(solution)/shard_map/mcr,dmc->rd/dot_general | solution.py:254
  58.2 1.6 %collective-permute-start.16 = (bf16[1,512,128]{2,1,0:T(8,128)(2,1)S(1)}, bf16[1,512,128]{2,1,0:T(8,128)(2,1)S(1)}, u32[]{:S(2)}, u32[]{:S(2)}) collective-permute-start(bf16[1,512,128]{2,1,0:T(8,128)(2,1)S(1)} %get-tuple-element.56), channel_id=1, source_target_pairs={{0,2},{2,0},{1,3},{3,1},{4,6},{6,4},{5,7},{7,5},{8,10},{10,8},{9,1... | collective-permute-start | bytes 393224 | tf_op jit(solution)/shard_map/ppermute | solution.py:46
  59.8 0.6 convolution_multiply_fusion.1
  60.4 0.7 fusion
  61.2 0.6 collective-permute-start.11
  61.8 0.6 collective-permute-start.12
  62.3 1.1 %collective-permute-start.10 = (f32[21,512]{1,0:T(8,128)S(1)}, f32[21,512]{1,0:T(8,128)S(1)}, u32[]{:S(2)}, u32[]{:S(2)}) collective-permute-start(f32[21,512]{1,0:T(8,128)S(1)} %get-tuple-element.28), channel_id=1, source_target_pairs={{0,1},{1,0},{2,3},{3,2},{4,5},{5,4},{6,7},{7,6},{8,9},{9,8},{10,11... | collective-permute-start | bytes 129032 | tf_op jit(solution)/shard_map/ppermute | solution.py:63
  63.9 1.9 %fusion.25 = f32[128,512]{1,0:T(8,128)} fusion(f32[512,1024]{1,0:T(8,128)S(1)} %bitcast.155, f32[128,512]{1,0:T(8,128)S(1)} %get-tuple-element.65, f32[128,512]{1,0:T(8,128)S(1)} %get-tuple-element.64, f32[1024]{0:T(1024)S(1)} %fusion.118), kind=kOutput, calls=%fused_computation.47 | convolution fusion | flops 402915328 | bytes 2887680 | tf_op jit(solution)/shard_map/dot_general | solution.py:140
  65.9 0.9 %collective-permute-start.13 = (f32[21,512]{1,0:T(8,128)S(1)}, f32[21,512]{1,0:T(8,128)S(1)}, u32[]{:S(2)}, u32[]{:S(2)}) collective-permute-start(f32[21,512]{1,0:T(8,128)S(1)} %pad_add_fusion), channel_id=1, source_target_pairs={{0,4},{4,0},{8,12},{12,8},{1,5},{5,1},{9,13},{13,9},{2,6},{6,2},{1... | collective-permute-start | bytes 129032 | tf_op jit(solution)/shard_map/ppermute | solution.py:63
  66.7 2.3 %collective-permute-start.14 = (f32[21,512]{1,0:T(8,128)S(1)}, f32[21,512]{1,0:T(8,128)S(1)}, u32[]{:S(2)}, u32[]{:S(2)}) collective-permute-start(f32[21,512]{1,0:T(8,128)S(1)} %pad_add_fusion), channel_id=1, source_target_pairs={{0,8},{4,12},{8,0},{12,4},{1,9},{5,13},{9,1},{13,5},{2,10},{6,14},... | collective-permute-start | bytes 129032 | tf_op jit(solution)/shard_map/ppermute | solution.py:63
  69.0 1.3 %collective-permute-start.15 = (f32[21,512]{1,0:T(8,128)S(1)}, f32[21,512]{1,0:T(8,128)S(1)}, u32[]{:S(2)}, u32[]{:S(2)}) collective-permute-start(f32[21,512]{1,0:T(8,128)S(1)} %pad_add_fusion), channel_id=1, source_target_pairs={{0,12},{4,8},{8,4},{12,0},{1,13},{5,9},{9,5},{13,1},{2,14},{6,10},... | collective-permute-start | bytes 129032 | tf_op jit(solution)/shard_map/ppermute | solution.py:63
  71.1 0.9 %fusion.7 = bf16[128,512]{1,0:T(8,128)(2,1)} fusion(f32[128,512]{1,0:T(8,128)S(1)} %fusion.28, f32[128,512]{1,0:T(8,128)S(1)} %fusion.30, f32[128,512]{1,0:T(8,128)S(1)} %fusion.32, bf16[2048,512]{1,0:T(8,128)(2,1)S(1)} %copy-done.3, f32[128,2048]{1,0:T(8,128)S(1)} %get-tuple-element.94, s32[]{:T(128)S(6)} %select_n.801, ...), kind=kOutput, calls=%fused_computation.16 | convolution fusion | flops 67633152 | bytes 2228231 | tf_op jit(solution)/shard_map/cr,cd->rd/dot_general | solution.py:239
  72.1 1.1 %collective-permute-done.14 = f32[21,512]{1,0:T(8,128)S(1)} collective-permute-done((f32[21,512]{1,0:T(8,128)S(1)}, f32[21,512]{1,0:T(8,128)S(1)}, u32[]{:S(2)}, u32[]{:S(2)}) %collective-permute-start.14) | collective-permute-done | bytes 43040 | tf_op jit(solution)/shard_map/ppermute | solution.py:63
  73.2 1.8 %collective-permute-done.15 = f32[21,512]{1,0:T(8,128)S(1)} collective-permute-done((f32[21,512]{1,0:T(8,128)S(1)}, f32[21,512]{1,0:T(8,128)S(1)}, u32[]{:S(2)}, u32[]{:S(2)}) %collective-permute-start.15) | collective-permute-done | bytes 43040 | tf_op jit(solution)/shard_map/ppermute | solution.py:63
  75.0 0.6 slice.274
  75.5 0.6 copy.22
  (89 shorter events, 6.5 us)
Async XLA Ops:
  0.6 13.6 %copy-start = (f32[1,1,128,512]{3,2,1,0:T(8,128)S(1)}, f32[1,1,128,512]{3,2,1,0:T(8,128)}, u32[]{:S(2)}) copy-start(f32[1,1,128,512]{3,2,1,0:T(8,128)} %param.11) | copy-start | bytes 786436
  0.7 6.2 %copy-start.11 = (s32[128]{0:T(128)S(1)}, s32[128]{0:T(128)}, u32[]{:S(2)}) copy-start(s32[128]{0:T(128)} %param.7) | copy-start | bytes 1540
  3.9 25.8 %collective-permute-start.1 = (f32[512,128]{1,0:T(8,128)}, f32[512,128]{1,0:T(8,128)}, u32[]{:S(2)}, u32[]{:S(2)}) collective-permute-start(f32[512,128]{1,0:T(8,128)} %get-tuple-element.59), channel_id=1, source_target_pairs={{0,1},{1,0},{2,3},{3,2},{4,5},{5,4},{6,7},{7,6},{8,9},{9,8},{10,11... | collective-permute-start | bytes 786440 | tf_op jit(solution)/shard_map/ppermute | solution.py:63
  4.4 25.3 %collective-permute-start.2 = (f32[512,128]{1,0:T(8,128)}, f32[512,128]{1,0:T(8,128)}, u32[]{:S(2)}, u32[]{:S(2)}) collective-permute-start(f32[512,128]{1,0:T(8,128)} %get-tuple-element.60), channel_id=1, source_target_pairs={{0,2},{1,3},{2,0},{3,1},{4,6},{5,7},{6,4},{7,5},{8,10},{9,11},{10,... | collective-permute-start | bytes 786440 | tf_op jit(solution)/shard_map/ppermute | solution.py:63
  7.4 13.9 %collective-permute-start = (s32[3]{0:T(128)}, s32[3]{0:T(128)}, u32[]{:S(2)}, u32[]{:S(2)}) collective-permute-start(s32[3]{0:T(128)} %slice_add_fusion.2), channel_id=1, source_target_pairs={{0,4},{4,8},{8,12},{1,5},{5,9},{9,13},{2,6},{6,10},{10,14},{3,7},{... | collective-permute-start | bytes 44 | tf_op jit(solution)/shard_map/ppermute | solution.py:16
  12.3 17.4 %collective-permute-start.3 = (f32[512,128]{1,0:T(8,128)}, f32[512,128]{1,0:T(8,128)}, u32[]{:S(2)}, u32[]{:S(2)}) collective-permute-start(f32[512,128]{1,0:T(8,128)} %select_select_fusion), channel_id=1, source_target_pairs={{0,3},{1,2},{2,1},{3,0},{4,7},{5,6},{6,5},{7,4},{8,11},{9,10},{10,... | collective-permute-start | bytes 786440 | tf_op jit(solution)/shard_map/ppermute | solution.py:63
  14.9 1.2 %copy-start.1 = (f32[128,1024]{1,0:T(8,128)}, f32[128,1024]{1,0:T(8,128)S(1)}, u32[]{:S(2)}) copy-start(f32[128,1024]{1,0:T(8,128)S(1)} %convolution_bitcast_fusion.2) | copy-start | bytes 1572868
  16.1 8.1 %copy-start.5 = (f32[2048]{0:T(1024)S(1)}, f32[2048]{0:T(1024)}, u32[]{:S(2)}) copy-start(f32[2048]{0:T(1024)} %param.9) | copy-start | bytes 24580
  29.6 5.9 %copy-start.4 = (bf16[128,512]{1,0:T(8,128)(2,1)S(1)}, bf16[128,512]{1,0:T(8,128)(2,1)}, u32[]{:S(2)}) copy-start(bf16[128,512]{1,0:T(8,128)(2,1)} %param.13) | copy-start | bytes 393220
  29.6 5.9 %copy-start.6 = (pred[128,5]{0,1:T(8,128)(4,1)S(1)}, pred[128,5]{0,1:T(8,128)(4,1)}, u32[]{:S(2)}) copy-start(pred[128,5]{0,1:T(8,128)(4,1)} %iota_compare_fusion.5) | copy-start | bytes 1924
  31.0 6.9 %collective-permute-start.4 = (bf16[2,128,128]{2,1,0:T(8,128)(2,1)S(1)}, bf16[2,128,128]{2,1,0:T(8,128)(2,1)S(1)}, u32[]{:S(2)}, u32[]{:S(2)}) collective-permute-start(bf16[2,128,128]{2,1,0:T(8,128)(2,1)S(1)} %get-tuple-element.83), channel_id=1, source_target_pairs={{0,12},{4,8},{8,4},{12,0},{1,13},{5,9},{9,5},{13,1},{2,14},{6,10},... | collective-permute-start | bytes 196616 | tf_op jit(solution)/shard_map/ppermute | solution.py:63
  32.2 8.1 %collective-permute-start.5 = (bf16[2,128,128]{2,1,0:T(8,128)(2,1)S(1)}, bf16[2,128,128]{2,1,0:T(8,128)(2,1)S(1)}, u32[]{:S(2)}, u32[]{:S(2)}) collective-permute-start(bf16[2,128,128]{2,1,0:T(8,128)(2,1)S(1)} %get-tuple-element.82), channel_id=1, source_target_pairs={{0,8},{4,12},{8,0},{12,4},{1,9},{5,13},{9,1},{13,5},{2,10},{6,14},... | collective-permute-start | bytes 196616 | tf_op jit(solution)/shard_map/ppermute | solution.py:63
  33.6 6.8 %collective-permute-start.6 = (bf16[2,128,128]{2,1,0:T(8,128)(2,1)S(1)}, bf16[2,128,128]{2,1,0:T(8,128)(2,1)S(1)}, u32[]{:S(2)}, u32[]{:S(2)}) collective-permute-start(bf16[2,128,128]{2,1,0:T(8,128)(2,1)S(1)} %get-tuple-element.45), channel_id=1, source_target_pairs={{0,4},{4,0},{8,12},{12,8},{1,5},{5,1},{9,13},{13,9},{2,6},{6,2},{1... | collective-permute-start | bytes 196616 | tf_op jit(solution)/shard_map/ppermute | solution.py:63
  40.4 1.1 %copy-start.2 = (f32[128,1024]{1,0:T(8,128)S(1)}, f32[128,1024]{1,0:T(8,128)}, u32[]{:S(2)}) copy-start(f32[128,1024]{1,0:T(8,128)} %copy-done.1) | copy-start | bytes 1572868
  40.4 1.1 %copy-start.7 = (pred[512]{0:T(512)(128)(4,1)S(1)}, pred[512]{0:T(512)(128)(4,1)}, u32[]{:S(2)}) copy-start(pred[512]{0:T(512)(128)(4,1)} %iota_compare_fusion.6) | copy-start | bytes 1540
  42.0 11.3 %slice-start = ((s8[6291456]{0:T(1024)(128)(4,1)}), s8[4194304]{0:T(1024)(128)(4,1)S(1)}, s32[]{:S(2)}) async-start(s8[6291456]{0:T(1024)(128)(4,1)} %bitcast.156), calls=%async_computation | async-start | bytes 8388608
  43.3 5.8 %copy-start.8 = (s32[128]{0:T(128)S(1)}, s32[128]{0:T(128)}, u32[]{:S(2)}) copy-start(s32[128]{0:T(128)} %get-tuple-element.101) | copy-start | bytes 1540
  43.3 5.8 %copy-start.9 = (s32[128]{0:T(128)S(1)}, s32[128]{0:T(128)}, u32[]{:S(2)}) copy-start(s32[128]{0:T(128)} %get-tuple-element.102) | copy-start | bytes 1540
  43.3 5.8 %copy-start.10 = (pred[128]{0:T(512)(128)(4,1)S(1)}, pred[128]{0:T(512)(128)(4,1)}, u32[]{:S(2)}) copy-start(pred[128]{0:T(512)(128)(4,1)} %compare_and_fusion) | copy-start | bytes 388
  44.5 8.8 %slice-start.1 = ((s8[6291456]{0:T(1024)(128)(4,1)}), s8[2097152]{0:T(1024)(128)(4,1)S(1)}, s32[]{:S(2)}) async-start(s8[6291456]{0:T(1024)(128)(4,1)} %bitcast.156), calls=%async_computation.1 | async-start | bytes 4194304
  44.6 6.4 %collective-permute-start.7 = (bf16[2,128,128]{2,1,0:T(8,128)(2,1)S(1)}, bf16[2,128,128]{2,1,0:T(8,128)(2,1)S(1)}, u32[]{:S(2)}, u32[]{:S(2)}) collective-permute-start(bf16[2,128,128]{2,1,0:T(8,128)(2,1)S(1)} %get-tuple-element.78), channel_id=1, source_target_pairs={{0,12},{4,8},{8,4},{12,0},{1,13},{5,9},{9,5},{13,1},{2,14},{6,10},... | collective-permute-start | bytes 196616 | tf_op jit(solution)/shard_map/ppermute | solution.py:63
  46.9 6.1 %collective-permute-start.8 = (bf16[2,128,128]{2,1,0:T(8,128)(2,1)S(1)}, bf16[2,128,128]{2,1,0:T(8,128)(2,1)S(1)}, u32[]{:S(2)}, u32[]{:S(2)}) collective-permute-start(bf16[2,128,128]{2,1,0:T(8,128)(2,1)S(1)} %get-tuple-element.77), channel_id=1, source_target_pairs={{0,8},{4,12},{8,0},{12,4},{1,9},{5,13},{9,1},{13,5},{2,10},{6,14},... | collective-permute-start | bytes 196616 | tf_op jit(solution)/shard_map/ppermute | solution.py:63
  46.9 6.1 %collective-permute-start.9 = (bf16[2,128,128]{2,1,0:T(8,128)(2,1)S(1)}, bf16[2,128,128]{2,1,0:T(8,128)(2,1)S(1)}, u32[]{:S(2)}, u32[]{:S(2)}) collective-permute-start(bf16[2,128,128]{2,1,0:T(8,128)(2,1)S(1)} %get-tuple-element.35), channel_id=1, source_target_pairs={{0,4},{4,0},{8,12},{12,8},{1,5},{5,1},{9,13},{13,9},{2,6},{6,2},{1... | collective-permute-start | bytes 196616 | tf_op jit(solution)/shard_map/ppermute | solution.py:63
  58.2 5.6 %collective-permute-start.16 = (bf16[1,512,128]{2,1,0:T(8,128)(2,1)S(1)}, bf16[1,512,128]{2,1,0:T(8,128)(2,1)S(1)}, u32[]{:S(2)}, u32[]{:S(2)}) collective-permute-start(bf16[1,512,128]{2,1,0:T(8,128)(2,1)S(1)} %get-tuple-element.56), channel_id=1, source_target_pairs={{0,2},{2,0},{1,3},{3,1},{4,6},{6,4},{5,7},{7,5},{8,10},{10,8},{9,1... | collective-permute-start | bytes 393224 | tf_op jit(solution)/shard_map/ppermute | solution.py:46
  61.1 9.2 %copy-start.3 = (bf16[2048,512]{1,0:T(8,128)(2,1)S(1)}, bf16[2048,512]{1,0:T(8,128)(2,1)}, u32[]{:S(2)}) copy-start(bf16[2048,512]{1,0:T(8,128)(2,1)} %param.12) | copy-start | bytes 6291460
  61.2 4.6 %collective-permute-start.11 = (f32[21,512]{1,0:T(8,128)S(1)}, f32[21,512]{1,0:T(8,128)S(1)}, u32[]{:S(2)}, u32[]{:S(2)}) collective-permute-start(f32[21,512]{1,0:T(8,128)S(1)} %get-tuple-element.84), channel_id=1, source_target_pairs={{0,2},{1,3},{2,0},{3,1},{4,6},{5,7},{6,4},{7,5},{8,10},{9,11},{10,... | collective-permute-start | bytes 129032 | tf_op jit(solution)/shard_map/ppermute | solution.py:63
  61.8 4.0 %collective-permute-start.12 = (f32[21,512]{1,0:T(8,128)S(1)}, f32[21,512]{1,0:T(8,128)S(1)}, u32[]{:S(2)}, u32[]{:S(2)}) collective-permute-start(f32[21,512]{1,0:T(8,128)S(1)} %get-tuple-element.85), channel_id=1, source_target_pairs={{0,3},{1,2},{2,1},{3,0},{4,7},{5,6},{6,5},{7,4},{8,11},{9,10},{10,... | collective-permute-start | bytes 129032 | tf_op jit(solution)/shard_map/ppermute | solution.py:63
  62.3 3.5 %collective-permute-start.10 = (f32[21,512]{1,0:T(8,128)S(1)}, f32[21,512]{1,0:T(8,128)S(1)}, u32[]{:S(2)}, u32[]{:S(2)}) collective-permute-start(f32[21,512]{1,0:T(8,128)S(1)} %get-tuple-element.28), channel_id=1, source_target_pairs={{0,1},{1,0},{2,3},{3,2},{4,5},{5,4},{6,7},{7,6},{8,9},{9,8},{10,11... | collective-permute-start | bytes 129032 | tf_op jit(solution)/shard_map/ppermute | solution.py:63
  63.8 6.5 %collective-permute-start.17 = (bf16[2,512,128]{2,1,0:T(8,128)(2,1)S(1)}, bf16[2,512,128]{2,1,0:T(8,128)(2,1)S(1)}, u32[]{:S(2)}, u32[]{:S(2)}) collective-permute-start(bf16[2,512,128]{2,1,0:T(8,128)(2,1)S(1)} %pad_maximum_fusion.4), channel_id=1, source_target_pairs={{0,1},{1,0},{2,3},{3,2},{4,5},{5,4},{6,7},{7,6},{8,9},{9,8},{10,11... | collective-permute-start | bytes 786440 | tf_op jit(solution)/shard_map/ppermute | solution.py:46
  65.9 6.2 %collective-permute-start.13 = (f32[21,512]{1,0:T(8,128)S(1)}, f32[21,512]{1,0:T(8,128)S(1)}, u32[]{:S(2)}, u32[]{:S(2)}) collective-permute-start(f32[21,512]{1,0:T(8,128)S(1)} %pad_add_fusion), channel_id=1, source_target_pairs={{0,4},{4,0},{8,12},{12,8},{1,5},{5,1},{9,13},{13,9},{2,6},{6,2},{1... | collective-permute-start | bytes 129032 | tf_op jit(solution)/shard_map/ppermute | solution.py:63
  66.7 6.5 %collective-permute-start.14 = (f32[21,512]{1,0:T(8,128)S(1)}, f32[21,512]{1,0:T(8,128)S(1)}, u32[]{:S(2)}, u32[]{:S(2)}) collective-permute-start(f32[21,512]{1,0:T(8,128)S(1)} %pad_add_fusion), channel_id=1, source_target_pairs={{0,8},{4,12},{8,0},{12,4},{1,9},{5,13},{9,1},{13,5},{2,10},{6,14},... | collective-permute-start | bytes 129032 | tf_op jit(solution)/shard_map/ppermute | solution.py:63
  69.0 5.9 %collective-permute-start.15 = (f32[21,512]{1,0:T(8,128)S(1)}, f32[21,512]{1,0:T(8,128)S(1)}, u32[]{:S(2)}, u32[]{:S(2)}) collective-permute-start(f32[21,512]{1,0:T(8,128)S(1)} %pad_add_fusion), channel_id=1, source_target_pairs={{0,12},{4,8},{8,4},{12,0},{1,13},{5,9},{9,5},{13,1},{2,14},{6,10},... | collective-permute-start | bytes 129032 | tf_op jit(solution)/shard_map/ppermute | solution.py:63

commit v10 on v8

--- a/solution.py
+++ b/solution.py
@@ -2,6 +2,7 @@
 
 import jax
 import jax.numpy as jnp
+import numpy as np
 from jax import lax
 from jax.sharding import PartitionSpec as P
 
@@ -135,8 +136,8 @@
 def inverse_dft(spec, dft):
     length = dft.shape[0]
     total = 2 * length
-    col = lax.broadcasted_iota(jnp.int32, (1, total), 1)
-    weight = jnp.where(col % length == 0, 1.0 / total, 2.0 / total).astype(jnp.float32)
+    col = np.arange(total)[None, :]
+    weight = np.where(col % length == 0, 1.0 / total, 2.0 / total).astype(np.float32)
     return lax.dot_general(
         spec * weight, dft, (((1,), (1,)), ((), ())), precision=TRANSFORM_PRECISION
     )
@@ -148,7 +149,7 @@
 
 
 def first_col(shape):
-    return lax.broadcasted_iota(jnp.int32, shape, 1) == 0
+    return np.arange(shape[1])[None, :] == 0
 
 
 def cmul(ga, gb, xa, xb, conj_g):
@@ -162,10 +163,10 @@
 
 
 def pair_flip(values):
-    rows = lax.broadcasted_iota(jnp.int32, values.shape, 0)
+    even = (np.arange(values.shape[0]) % 2 == 0)[:, None]
     up = jnp.roll(values, -1, axis=0)
     down = jnp.roll(values, 1, axis=0)
-    return jnp.where(rows % 2 == 0, up, down)
+    return jnp.where(even, up, down)
 
 
 def add_conj_flip(spec):

time: 73.5 us -> 71.6 us (0.974)
  other arithmetic: 11.2 us -> 9.53 us
    unnamed x30 -> x28, local copies, waits for them, and re-layouts: 1.68 us -> 2.06 us
    select_n x3 -> x2, other arithmetic: 1.51 us -> 1.45 us  [pair_flip(): return jnp.where(even, up, down)]
  transfers between devices with their start and end apart: 18 -> 18, of which waited for: 7 -> 7; matrix products, arithmetic and copies ran while one was open for 31% -> 28% of each run, Pallas kernels for 0% -> 0%
where the time goes in v10:
time: 71.6 us; the launch traced here: 71.2 us
  starting transfers between devices  24.3 us (34%)
  matrix products  20 us (28%)
  waiting for transfers between devices  11.7 us (16%)
  other arithmetic  9.53 us (13%)
  local copies, waits for them, and re-layouts  4.57 us (6%)
  between operations  1.16 us (2%)
    ppermute x15, starting transfers between devices, group_exchange(): return lax.ppermute(x, axes, [(i, i ^ offset) for i in range(count)])  18.6 us
    ppermute x15, waiting for transfers between devices, group_exchange(): return lax.ppermute(x, axes, [(i, i ^ offset) for i in range(count)])  11.2 us
    ppermute x1, starting transfers between devices, from_behind(): lax.ppermute(value, axis, [(source, source + steps) for source in range(f...  4.04 us
    dot_general x3, matrix products, inverse_dft(): lax.dot_general(spec * weight, dft, (((1,), (1,)), ((), ())), precision=T...  3.87 us
    dot_general x1, matrix products, per_device(): jnp.einsum('dr,dmc->mcr', hidden, in_proj, preferred_element_type=jnp.flo...  3.86 us
    dot_general x1, matrix products, per_device(): jnp.einsum('rd,cd->rc', cotangent, out_proj, preferred_element_type=jnp.f...  2.51 us
    dot_general x1, matrix products, per_device(): jnp.einsum('mcr,dmc->rd', d_proj, in_proj, preferred_element_type=jnp.flo...  2.18 us
    unnamed x28, local copies, waits for them, and re-layouts  2.06 us
  transfers between devices with their start and end apart: 18, of which 7 were waited for; matrix products, arithmetic and copies ran while one was open for 28% of the time, Pallas kernels for 0%

profile of v10, /device:TPU:0, one launch (start us, length us, event | category | flops | bytes accessed | tf_op | source)
XLA Modules:
  0.0 71.2 jit_solution(6784092345293734273)
XLA Ops:
  0.7 2.5 %fusion.132 = f32[128,2048]{1,0:T(8,128)S(1)} fusion(bf16[128,512]{1,0:T(8,128)(2,1)} %param.23, bf16[2048,512]{1,0:T(8,128)(2,1)} %param.22), kind=kOutput, calls=%fused_computation.243 | convolution fusion | flops 268435456 | bytes 3276800 | tf_op jit(solution)/shard_map/rd,cd->rc/dot_general | solution.py:215
  3.2 0.9 %select_select_fusion.2 = (f32[128,512]{1,0:T(8,128)}, f32[128,512]{1,0:T(8,128)}) fusion(f32[128,2048]{1,0:T(8,128)S(1)} %fusion.132, pred[]{:T(512)S(6)} %eq.114, pred[]{:T(512)S(6)} %eq.113, pred[]{:T(512)S(6)} %eq.112, pred[]{:T(512)S(6)} %eq.117, pred[]{:T(512)S(6)} %eq.116, pred[]{:T(512)S(6)} %eq.115), kind=kLoop, calls=%fused_computation.116 | loop fusion | flops 393216 | bytes 1572870 | tf_op jit(solution)/shard_map/jit(_where)/select_n | solution.py:76
  4.6 2.5 %collective-permute-start.2 = (f32[128,512]{1,0:T(8,128)}, f32[128,512]{1,0:T(8,128)}, u32[]{:S(2)}, u32[]{:S(2)}) collective-permute-start(f32[128,512]{1,0:T(8,128)} %get-tuple-element.60), channel_id=1, source_target_pairs={{0,2},{1,3},{2,0},{3,1},{4,6},{5,7},{6,4},{7,5},{8,10},{9,11},{10,... | collective-permute-start | bytes 786440 | tf_op jit(solution)/shard_map/ppermute | solution.py:64
  7.1 0.6 slice_add_fusion.2
  7.7 4.0 %collective-permute-start = (s32[3]{0:T(128)}, s32[3]{0:T(128)}, u32[]{:S(2)}, u32[]{:S(2)}) collective-permute-start(s32[3]{0:T(128)} %slice_add_fusion.2), channel_id=1, source_target_pairs={{0,4},{4,8},{8,12},{1,5},{5,9},{9,13},{2,6},{6,10},{10,14},{3,7},{... | collective-permute-start | bytes 44 | tf_op jit(solution)/shard_map/ppermute | solution.py:17
  11.7 0.8 %select_select_fusion = f32[128,512]{1,0:T(8,128)} fusion(f32[128,2048]{1,0:T(8,128)S(1)} %fusion.132, pred[]{:T(512)S(6)} %eq.120, pred[]{:T(512)S(6)} %eq.119, pred[]{:T(512)S(6)} %eq.118), kind=kLoop, calls=%fused_computation.114 | loop fusion | flops 196608 | bytes 1310723 | tf_op jit(solution)/shard_map/jit(_where)/select_n | solution.py:76
  12.6 0.6 iota_compare_fusion.5
  13.5 0.6 fusion.98
  14.4 0.7 convolution_bitcast_fusion.2
  15.2 1.1 %fusion.130 = (f32[127,1024]{1,0:T(8,128)}, f32[127,1024]{1,0:T(8,128)}) fusion(f32[128,1024]{1,0:T(8,128)S(1)} %convolution_bitcast_fusion.2), kind=kLoop, calls=%fused_computation.241 | loop fusion | bytes 2080768 | tf_op jit(solution)/shard_map/jit(_roll_static)/slice | solution.py:168
  16.4 0.9 %copy.28 = bf16[4,5,2048]{2,1,0:T(8,128)(2,1)S(1)} copy(bf16[4,5,2048]{2,0,1:T(4,128)(2,1)} %param.18) | data formatting | bytes 163840 | tf_op args[1]
  17.3 0.7 reshape.243
  18.0 1.3 %maximum_select_fusion = f32[128,1024]{1,0:T(8,128)S(1)} fusion(f32[1,1024]{1,0:T(1,128)S(1)} %get-tuple-element.69, f32[127,1024]{1,0:T(8,128)} %get-tuple-element.71, f32[127,1024]{1,0:T(8,128)} %get-tuple-element.70, f32[1,1024]{1,0:T(1,128)S(1)} %get-tuple-element.68, pred[128]{0:T(512)(128)(4,1)} %constant.93), kind=kLoop, calls=%fused_computation.39 | loop fusion | flops 393216 | bytes 1572992 | tf_op jit(solution)/shard_map/jit(_where)/select_n | solution.py:169
  19.3 0.7 broadcast_add_fusion
  20.0 0.7 %pad_add_fusion.2 = s32[131]{0:T(256)S(1)} fusion(s32[128]{0:T(128)} %param.17, s32[3]{0:T(128)S(1)} %broadcast_add_fusion), kind=kLoop, calls=%fused_computation.229 | loop fusion | flops 131 | bytes 1048 | tf_op jit(solution)/shard_map/concatenate | solution.py:191
  20.8 1.3 %multiply_reduce_fusion = (f32[128]{0:T(128)S(1)}, f32[128,2048]{1,0:T(8,128)S(1)}) fusion(bf16[20,2048]{1,0:T(8,128)(2,1)} %reshape.243, pred[128,5]{0,1:T(8,128)(4,1)S(1)} %get-tuple-element.97, pred[128,5]{0,1:T(8,128)(4,1)S(1)} %get-tuple-element.98, pred[128,5]{0,1:T(8,128)(4,1)S(1)} %iota_compare_fusion.4, pred[128,5]{0,1:T(8,128)(4,1)} %iota_compare_fusion.5), kind=kOutput, calls=%fused_computation.24 | convolution fusion | flops 11017600 | bytes 1133568 | tf_op jit(solution)/shard_map/dot_general | solution.py:199
  22.2 3.9 %convolution_bitcast_fusion.1 = f32[3,512,128]{1,2,0:T(8,128)S(1)} fusion(bf16[2048,3,512]{2,0,1:T(8,128)(2,1)} %param.20, f32[128,2048]{1,0:T(8,128)S(1)} %get-tuple-element.94, f32[2048]{0:T(1024)S(1)} %copy-done.5, f32[128]{0:T(128)S(1)} %add_rsqrt_fusion), kind=kOutput, calls=%fused_computation.5 | convolution fusion | flops 806092800 | bytes 8135168 | tf_op jit(solution)/shard_map/dr,dmc->mcr/dot_general | solution.py:204
  26.1 1.3 %fusion.57 = (bf16[1,512,128]{1,2,0:T(8,128)(2,1)S(1)}, f32[128,512]{1,0:T(8,128)S(1)}) fusion(f32[3,512,128]{1,2,0:T(8,128)S(1)} %convolution_bitcast_fusion.1, f32[128,512]{1,0:T(8,128)} %collective-permute-done.3, f32[128,512]{1,0:T(8,128)} %collective-permute-done.2, f32[128,512]{1,0:T(8,128)} %collective-permute-done.1, f32[128,2048]{1,0:T(8,128)S(1)} %fusion.132, ...), kind=kLoop, calls=%fused_computation.129 | loop fusion | flops 589824 | bytes 2490371 | tf_op jit(solution)/shard_map/stack | solution.py:222
  27.6 1.2 %collective-permute-start.4 = (bf16[2,128,128]{1,2,0:T(8,128)(2,1)S(1)}, bf16[2,128,128]{1,2,0:T(8,128)(2,1)S(1)}, u32[]{:S(2)}, u32[]{:S(2)}) collective-permute-start(bf16[2,128,128]{1,2,0:T(8,128)(2,1)S(1)} %get-tuple-element.83), channel_id=1, source_target_pairs={{0,12},{4,8},{8,4},{12,0},{1,13},{5,9},{9,5},{13,1},{2,14},{6,10},... | collective-permute-start | bytes 196616 | tf_op jit(solution)/shard_map/ppermute | solution.py:64
  28.8 1.4 %collective-permute-start.5 = (bf16[2,128,128]{1,2,0:T(8,128)(2,1)S(1)}, bf16[2,128,128]{1,2,0:T(8,128)(2,1)S(1)}, u32[]{:S(2)}, u32[]{:S(2)}) collective-permute-start(bf16[2,128,128]{1,2,0:T(8,128)(2,1)S(1)} %get-tuple-element.82), channel_id=1, source_target_pairs={{0,8},{4,12},{8,0},{12,4},{1,9},{5,13},{9,1},{13,5},{2,10},{6,14},... | collective-permute-start | bytes 196616 | tf_op jit(solution)/shard_map/ppermute | solution.py:64
  30.1 1.9 %collective-permute-start.6 = (bf16[2,128,128]{1,2,0:T(8,128)(2,1)S(1)}, bf16[2,128,128]{1,2,0:T(8,128)(2,1)S(1)}, u32[]{:S(2)}, u32[]{:S(2)}) collective-permute-start(bf16[2,128,128]{1,2,0:T(8,128)(2,1)S(1)} %get-tuple-element.45), channel_id=1, source_target_pairs={{0,4},{4,0},{8,12},{12,8},{1,5},{5,1},{9,13},{13,9},{2,6},{6,2},{1... | collective-permute-start | bytes 196616 | tf_op jit(solution)/shard_map/ppermute | solution.py:64
  32.3 2.2 %collective-permute-done.4 = bf16[2,128,128]{1,2,0:T(8,128)(2,1)S(1)} collective-permute-done((bf16[2,128,128]{1,2,0:T(8,128)(2,1)S(1)}, bf16[2,128,128]{1,2,0:T(8,128)(2,1)S(1)}, u32[]{:S(2)}, u32[]{:S(2)}) %collective-permute-start.4) | collective-permute-done | bytes 65568 | tf_op jit(solution)/shard_map/ppermute | solution.py:64
  34.5 2.4 %collective-permute-done.5 = bf16[2,128,128]{1,2,0:T(8,128)(2,1)S(1)} collective-permute-done((bf16[2,128,128]{1,2,0:T(8,128)(2,1)S(1)}, bf16[2,128,128]{1,2,0:T(8,128)(2,1)S(1)}, u32[]{:S(2)}, u32[]{:S(2)}) %collective-permute-start.5) | collective-permute-done | bytes 65568 | tf_op jit(solution)/shard_map/ppermute | solution.py:64
  37.0 0.6 fusion.61
  37.6 0.6 fusion.62
  39.0 1.0 %fusion.8 = bf16[1,128,512]{1,2,0:T(8,128)(2,1)S(1)} fusion(f32[512,1024]{1,0:T(8,128)S(1)} %bitcast.160, f32[128,512]{1,0:T(8,128)S(1)} %get-tuple-element.61, f32[128,512]{1,0:T(8,128)S(1)} %get-tuple-element.62, f32[1024]{0:T(1024)S(1)} %copy-done.6), kind=kOutput, calls=%fused_computation.17 | convolution fusion | flops 402980864 | bytes 2756608 | tf_op jit(solution)/shard_map/dot_general | solution.py:141
  40.0 1.0 %fusion.9 = bf16[1,128,512]{1,2,0:T(8,128)(2,1)S(1)} fusion(f32[512,1024]{1,0:T(8,128)S(1)} %bitcast.161, f32[128,512]{1,0:T(8,128)S(1)} %get-tuple-element.63, f32[128,512]{1,0:T(8,128)S(1)} %get-tuple-element.40, f32[1024]{0:T(1024)S(1)} %copy-done.6), kind=kOutput, calls=%fused_computation.18 | convolution fusion | flops 402980864 | bytes 2756608 | tf_op jit(solution)/shard_map/dot_general | solution.py:141
  41.1 2.3 %collective-permute-start.7 = (bf16[2,128,128]{1,2,0:T(8,128)(2,1)S(1)}, bf16[2,128,128]{1,2,0:T(8,128)(2,1)S(1)}, u32[]{:S(2)}, u32[]{:S(2)}) collective-permute-start(bf16[2,128,128]{1,2,0:T(8,128)(2,1)S(1)} %get-tuple-element.78), channel_id=1, source_target_pairs={{0,12},{4,8},{8,4},{12,0},{1,13},{5,9},{9,5},{13,1},{2,14},{6,10},... | collective-permute-start | bytes 196616 | tf_op jit(solution)/shard_map/ppermute | solution.py:64
  43.4 2.2 %collective-permute-start.9 = (bf16[2,128,128]{1,2,0:T(8,128)(2,1)S(1)}, bf16[2,128,128]{1,2,0:T(8,128)(2,1)S(1)}, u32[]{:S(2)}, u32[]{:S(2)}) collective-permute-start(bf16[2,128,128]{1,2,0:T(8,128)(2,1)S(1)} %get-tuple-element.35), channel_id=1, source_target_pairs={{0,4},{4,0},{8,12},{12,8},{1,5},{5,1},{9,13},{13,9},{2,6},{6,2},{1... | collective-permute-start | bytes 196616 | tf_op jit(solution)/shard_map/ppermute | solution.py:64
  45.8 1.7 %collective-permute-done.7 = bf16[2,128,128]{1,2,0:T(8,128)(2,1)S(1)} collective-permute-done((bf16[2,128,128]{1,2,0:T(8,128)(2,1)S(1)}, bf16[2,128,128]{1,2,0:T(8,128)(2,1)S(1)}, u32[]{:S(2)}, u32[]{:S(2)}) %collective-permute-start.7) | collective-permute-done | bytes 65568 | tf_op jit(solution)/shard_map/ppermute | solution.py:64
  47.5 2.0 %collective-permute-done.8 = bf16[2,128,128]{1,2,0:T(8,128)(2,1)S(1)} collective-permute-done((bf16[2,128,128]{1,2,0:T(8,128)(2,1)S(1)}, bf16[2,128,128]{1,2,0:T(8,128)(2,1)S(1)}, u32[]{:S(2)}, u32[]{:S(2)}) %collective-permute-start.8) | collective-permute-done | bytes 65568 | tf_op jit(solution)/shard_map/ppermute | solution.py:64
  49.9 1.2 %fusion.3 = f32[128]{0:T(128)S(1)} fusion(f32[3,512,128]{1,2,0:T(8,128)S(1)} %convolution_bitcast_fusion.1, bf16[2048,3,512]{2,0,1:T(8,128)(2,1)S(1)} %bitcast.164, f32[128,2048]{1,0:T(8,128)S(1)} %get-tuple-element.94, f32[2048]{0:T(1024)S(1)} %copy-done.5, f32[128]{0:T(128)S(1)} %add_rsqrt_fusion, bf16[1,512,128]{1,2,0:T(8,128)(2,1)S(1)} %get-tuple-element.58, ...), kind=kOutput, calls=%fused_computation.9 | convolution fusion | flops 808058752 | bytes 8528896 | tf_op jit(solution)/shard_map/dr,dmc->mcr/dot_general | solution.py:206
  51.1 2.2 %fusion.10 = (f32[2048]{0:T(1024)S(1)}, f32[128,2048,1]{1,0,2:T(8,128)S(1)}) fusion(f32[128,2048]{1,0:T(8,128)S(1)} %get-tuple-element.94, f32[128]{0:T(128)S(1)} %add_rsqrt_fusion, bf16[2048,3,512]{2,0,1:T(8,128)(2,1)S(1)} %bitcast.164, bf16[1,512,128]{1,2,0:T(8,128)(2,1)S(1)} %get-tuple-element.58, bf16[1,512,128]{1,2,0:T(8,128)(2,1)S(1)} %get-tuple-element.57, ...), kind=kOutput, calls=%fused_computation.20 | convolution fusion | flops 806483968 | bytes 8790528 | tf_op jit(solution)/shard_map/mcr,dmc->rd/dot_general | solution.py:255
  53.3 1.6 %collective-permute-start.16 = (bf16[1,512,128]{1,2,0:T(8,128)(2,1)S(1)}, bf16[1,512,128]{1,2,0:T(8,128)(2,1)S(1)}, u32[]{:S(2)}, u32[]{:S(2)}) collective-permute-start(bf16[1,512,128]{1,2,0:T(8,128)(2,1)S(1)} %get-tuple-element.56), channel_id=1, source_target_pairs={{0,2},{2,0},{1,3},{3,1},{4,6},{6,4},{5,7},{7,5},{8,10},{10,8},{9,1... | collective-permute-start | bytes 393224 | tf_op jit(solution)/shard_map/ppermute | solution.py:47
  54.8 0.6 convolution_multiply_fusion.1
  55.4 0.7 %fusion = f32[20,2048]{1,0:T(8,128)S(1)} fusion(f32[20,2048]{1,0:T(8,128)S(1)} %convolution_multiply_fusion.1, f32[128,2048]{1,0:T(8,128)S(1)} %get-tuple-element.94, f32[128]{0:T(128)S(1)} %add_rsqrt_fusion, f32[128]{0:T(128)S(1)} %fusion.3, pred[128,5]{0,1:T(8,128)(4,1)S(1)} %get-tuple-element.97, pred[128,5]{0,1:T(8,128)(4,1)S(1)} %get-tuple-element.98, ...), kind=kOutput, calls=%fused_computation.1 | convolution fusion | flops 63276544 | bytes 1379840 | tf_op jit(solution)/shard_map/rk,dr->kd/dot_general | solution.py:260
  56.2 0.6 collective-permute-start.11
  56.8 0.5 collective-permute-start.12
  57.4 1.1 %collective-permute-start.10 = (f32[21,512]{1,0:T(8,128)S(1)}, f32[21,512]{1,0:T(8,128)S(1)}, u32[]{:S(2)}, u32[]{:S(2)}) collective-permute-start(f32[21,512]{1,0:T(8,128)S(1)} %get-tuple-element.28), channel_id=1, source_target_pairs={{0,1},{1,0},{2,3},{3,2},{4,5},{5,4},{6,7},{7,6},{8,9},{9,8},{10,11... | collective-permute-start | bytes 129032 | tf_op jit(solution)/shard_map/ppermute | solution.py:64
  59.0 1.9 %fusion.25 = f32[128,512]{1,0:T(8,128)} fusion(f32[512,1024]{1,0:T(8,128)S(1)} %bitcast.162, f32[128,512]{1,0:T(8,128)S(1)} %get-tuple-element.65, f32[128,512]{1,0:T(8,128)S(1)} %get-tuple-element.64, f32[1024]{0:T(1024)S(1)} %copy-done.6), kind=kOutput, calls=%fused_computation.47 | convolution fusion | flops 402915328 | bytes 2887680 | tf_op jit(solution)/shard_map/dot_general | solution.py:141
  60.9 0.8 %collective-permute-start.13 = (f32[21,512]{1,0:T(8,128)S(1)}, f32[21,512]{1,0:T(8,128)S(1)}, u32[]{:S(2)}, u32[]{:S(2)}) collective-permute-start(f32[21,512]{1,0:T(8,128)S(1)} %pad_add_fusion), channel_id=1, source_target_pairs={{0,4},{4,0},{8,12},{12,8},{1,5},{5,1},{9,13},{13,9},{2,6},{6,2},{1... | collective-permute-start | bytes 129032 | tf_op jit(solution)/shard_map/ppermute | solution.py:64
  61.8 2.3 %collective-permute-start.14 = (f32[21,512]{1,0:T(8,128)S(1)}, f32[21,512]{1,0:T(8,128)S(1)}, u32[]{:S(2)}, u32[]{:S(2)}) collective-permute-start(f32[21,512]{1,0:T(8,128)S(1)} %pad_add_fusion), channel_id=1, source_target_pairs={{0,8},{4,12},{8,0},{12,4},{1,9},{5,13},{9,1},{13,5},{2,10},{6,14},... | collective-permute-start | bytes 129032 | tf_op jit(solution)/shard_map/ppermute | solution.py:64
  64.1 1.3 %collective-permute-start.15 = (f32[21,512]{1,0:T(8,128)S(1)}, f32[21,512]{1,0:T(8,128)S(1)}, u32[]{:S(2)}, u32[]{:S(2)}) collective-permute-start(f32[21,512]{1,0:T(8,128)S(1)} %pad_add_fusion), channel_id=1, source_target_pairs={{0,12},{4,8},{8,4},{12,0},{1,13},{5,9},{9,5},{13,1},{2,14},{6,10},... | collective-permute-start | bytes 129032 | tf_op jit(solution)/shard_map/ppermute | solution.py:64
  66.1 0.9 %fusion.7 = bf16[128,512]{1,0:T(8,128)(2,1)} fusion(f32[128,512]{1,0:T(8,128)S(1)} %fusion.28, f32[128,512]{1,0:T(8,128)S(1)} %fusion.30, f32[128,512]{1,0:T(8,128)S(1)} %fusion.32, bf16[2048,512]{1,0:T(8,128)(2,1)S(1)} %copy-done.3, f32[128,2048]{1,0:T(8,128)S(1)} %get-tuple-element.94, s32[]{:T(128)S(6)} %select_n.772, ...), kind=kOutput, calls=%fused_computation.16 | convolution fusion | flops 67633152 | bytes 2228231 | tf_op jit(solution)/shard_map/cr,cd->rd/dot_general | solution.py:240
  67.1 1.2 %collective-permute-done.14 = f32[21,512]{1,0:T(8,128)S(1)} collective-permute-done((f32[21,512]{1,0:T(8,128)S(1)}, f32[21,512]{1,0:T(8,128)S(1)}, u32[]{:S(2)}, u32[]{:S(2)}) %collective-permute-start.14) | collective-permute-done | bytes 43040 | tf_op jit(solution)/shard_map/ppermute | solution.py:64
  68.2 1.7 %collective-permute-done.15 = f32[21,512]{1,0:T(8,128)S(1)} collective-permute-done((f32[21,512]{1,0:T(8,128)S(1)}, f32[21,512]{1,0:T(8,128)S(1)}, u32[]{:S(2)}, u32[]{:S(2)}) %collective-permute-start.15) | collective-permute-done | bytes 43040 | tf_op jit(solution)/shard_map/ppermute | solution.py:64
  70.0 0.6 slice.274
  70.6 0.6 copy.31
  (83 shorter events, 4.7 us)
Async XLA Ops:
  0.6 13.8 %copy-start = (f32[1,1,128,512]{3,2,1,0:T(8,128)S(1)}, f32[1,1,128,512]{3,2,1,0:T(8,128)}, u32[]{:S(2)}) copy-start(f32[1,1,128,512]{3,2,1,0:T(8,128)} %param.21) | copy-start | bytes 786436
  0.7 6.4 %copy-start.10 = (s32[128]{0:T(128)S(1)}, s32[128]{0:T(128)}, u32[]{:S(2)}) copy-start(s32[128]{0:T(128)} %param.17) | copy-start | bytes 1540
  4.1 22.0 %collective-permute-start.1 = (f32[128,512]{1,0:T(8,128)}, f32[128,512]{1,0:T(8,128)}, u32[]{:S(2)}, u32[]{:S(2)}) collective-permute-start(f32[128,512]{1,0:T(8,128)} %get-tuple-element.59), channel_id=1, source_target_pairs={{0,1},{1,0},{2,3},{3,2},{4,5},{5,4},{6,7},{7,6},{8,9},{9,8},{10,11... | collective-permute-start | bytes 786440 | tf_op jit(solution)/shard_map/ppermute | solution.py:64
  4.6 21.5 %collective-permute-start.2 = (f32[128,512]{1,0:T(8,128)}, f32[128,512]{1,0:T(8,128)}, u32[]{:S(2)}, u32[]{:S(2)}) collective-permute-start(f32[128,512]{1,0:T(8,128)} %get-tuple-element.60), channel_id=1, source_target_pairs={{0,2},{1,3},{2,0},{3,1},{4,6},{5,7},{6,4},{7,5},{8,10},{9,11},{10,... | collective-permute-start | bytes 786440 | tf_op jit(solution)/shard_map/ppermute | solution.py:64
  7.7 11.6 %collective-permute-start = (s32[3]{0:T(128)}, s32[3]{0:T(128)}, u32[]{:S(2)}, u32[]{:S(2)}) collective-permute-start(s32[3]{0:T(128)} %slice_add_fusion.2), channel_id=1, source_target_pairs={{0,4},{4,8},{8,12},{1,5},{5,9},{9,13},{2,6},{6,10},{10,14},{3,7},{... | collective-permute-start | bytes 44 | tf_op jit(solution)/shard_map/ppermute | solution.py:17
  12.5 13.6 %collective-permute-start.3 = (f32[128,512]{1,0:T(8,128)}, f32[128,512]{1,0:T(8,128)}, u32[]{:S(2)}, u32[]{:S(2)}) collective-permute-start(f32[128,512]{1,0:T(8,128)} %select_select_fusion), channel_id=1, source_target_pairs={{0,3},{1,2},{2,1},{3,0},{4,7},{5,6},{6,5},{7,4},{8,11},{9,10},{10,... | collective-permute-start | bytes 786440 | tf_op jit(solution)/shard_map/ppermute | solution.py:64
  15.2 1.2 %copy-start.1 = (f32[128,1024]{1,0:T(8,128)}, f32[128,1024]{1,0:T(8,128)S(1)}, u32[]{:S(2)}) copy-start(f32[128,1024]{1,0:T(8,128)S(1)} %convolution_bitcast_fusion.2) | copy-start | bytes 1572868
  16.3 5.8 %copy-start.5 = (f32[2048]{0:T(1024)S(1)}, f32[2048]{0:T(1024)}, u32[]{:S(2)}) copy-start(f32[2048]{0:T(1024)} %param.19) | copy-start | bytes 24580
  26.0 6.0 %copy-start.4 = (bf16[128,512]{1,0:T(8,128)(2,1)S(1)}, bf16[128,512]{1,0:T(8,128)(2,1)}, u32[]{:S(2)}) copy-start(bf16[128,512]{1,0:T(8,128)(2,1)} %param.23) | copy-start | bytes 393220
  26.1 6.0 %copy-start.7 = (pred[128,5]{0,1:T(8,128)(4,1)S(1)}, pred[128,5]{0,1:T(8,128)(4,1)}, u32[]{:S(2)}) copy-start(pred[128,5]{0,1:T(8,128)(4,1)} %iota_compare_fusion.5) | copy-start | bytes 1924
  27.6 6.9 %collective-permute-start.4 = (bf16[2,128,128]{1,2,0:T(8,128)(2,1)S(1)}, bf16[2,128,128]{1,2,0:T(8,128)(2,1)S(1)}, u32[]{:S(2)}, u32[]{:S(2)}) collective-permute-start(bf16[2,128,128]{1,2,0:T(8,128)(2,1)S(1)} %get-tuple-element.83), channel_id=1, source_target_pairs={{0,12},{4,8},{8,4},{12,0},{1,13},{5,9},{9,5},{13,1},{2,14},{6,10},... | collective-permute-start | bytes 196616 | tf_op jit(solution)/shard_map/ppermute | solution.py:64
  28.8 8.1 %collective-permute-start.5 = (bf16[2,128,128]{1,2,0:T(8,128)(2,1)S(1)}, bf16[2,128,128]{1,2,0:T(8,128)(2,1)S(1)}, u32[]{:S(2)}, u32[]{:S(2)}) collective-permute-start(bf16[2,128,128]{1,2,0:T(8,128)(2,1)S(1)} %get-tuple-element.82), channel_id=1, source_target_pairs={{0,8},{4,12},{8,0},{12,4},{1,9},{5,13},{9,1},{13,5},{2,10},{6,14},... | collective-permute-start | bytes 196616 | tf_op jit(solution)/shard_map/ppermute | solution.py:64
  30.1 6.7 %collective-permute-start.6 = (bf16[2,128,128]{1,2,0:T(8,128)(2,1)S(1)}, bf16[2,128,128]{1,2,0:T(8,128)(2,1)S(1)}, u32[]{:S(2)}, u32[]{:S(2)}) collective-permute-start(bf16[2,128,128]{1,2,0:T(8,128)(2,1)S(1)} %get-tuple-element.45), channel_id=1, source_target_pairs={{0,4},{4,0},{8,12},{12,8},{1,5},{5,1},{9,13},{13,9},{2,6},{6,2},{1... | collective-permute-start | bytes 196616 | tf_op jit(solution)/shard_map/ppermute | solution.py:64
  37.0 1.2 %copy-start.2 = (f32[128,1024]{1,0:T(8,128)S(1)}, f32[128,1024]{1,0:T(8,128)}, u32[]{:S(2)}) copy-start(f32[128,1024]{1,0:T(8,128)} %copy-done.1) | copy-start | bytes 1572868
  37.0 1.2 %copy-start.8 = (pred[512]{0:T(512)(128)(4,1)S(1)}, pred[512]{0:T(512)(128)(4,1)}, u32[]{:S(2)}) copy-start(pred[512]{0:T(512)(128)(4,1)} %constant.92) | copy-start | bytes 1540
  38.3 0.7 copy-start.6
  38.6 11.3 %slice-start = ((s8[6291456]{0:T(1024)(128)(4,1)}), s8[4194304]{0:T(1024)(128)(4,1)S(1)}, s32[]{:S(2)}) async-start(s8[6291456]{0:T(1024)(128)(4,1)} %bitcast.163), calls=%async_computation | async-start | bytes 8388608
  40.0 5.6 %copy-start.9 = (pred[128]{0:T(512)(128)(4,1)S(1)}, pred[128]{0:T(512)(128)(4,1)}, u32[]{:S(2)}) copy-start(pred[128]{0:T(512)(128)(4,1)} %constant.93) | copy-start | bytes 388
  41.0 8.8 %slice-start.1 = ((s8[6291456]{0:T(1024)(128)(4,1)}), s8[2097152]{0:T(1024)(128)(4,1)S(1)}, s32[]{:S(2)}) async-start(s8[6291456]{0:T(1024)(128)(4,1)} %bitcast.163), calls=%async_computation.1 | async-start | bytes 4194304
  41.1 6.4 %collective-permute-start.7 = (bf16[2,128,128]{1,2,0:T(8,128)(2,1)S(1)}, bf16[2,128,128]{1,2,0:T(8,128)(2,1)S(1)}, u32[]{:S(2)}, u32[]{:S(2)}) collective-permute-start(bf16[2,128,128]{1,2,0:T(8,128)(2,1)S(1)} %get-tuple-element.78), channel_id=1, source_target_pairs={{0,12},{4,8},{8,4},{12,0},{1,13},{5,9},{9,5},{13,1},{2,14},{6,10},... | collective-permute-start | bytes 196616 | tf_op jit(solution)/shard_map/ppermute | solution.py:64
  43.4 6.1 %collective-permute-start.8 = (bf16[2,128,128]{1,2,0:T(8,128)(2,1)S(1)}, bf16[2,128,128]{1,2,0:T(8,128)(2,1)S(1)}, u32[]{:S(2)}, u32[]{:S(2)}) collective-permute-start(bf16[2,128,128]{1,2,0:T(8,128)(2,1)S(1)} %get-tuple-element.77), channel_id=1, source_target_pairs={{0,8},{4,12},{8,0},{12,4},{1,9},{5,13},{9,1},{13,5},{2,10},{6,14},... | collective-permute-start | bytes 196616 | tf_op jit(solution)/shard_map/ppermute | solution.py:64
  43.4 6.1 %collective-permute-start.9 = (bf16[2,128,128]{1,2,0:T(8,128)(2,1)S(1)}, bf16[2,128,128]{1,2,0:T(8,128)(2,1)S(1)}, u32[]{:S(2)}, u32[]{:S(2)}) collective-permute-start(bf16[2,128,128]{1,2,0:T(8,128)(2,1)S(1)} %get-tuple-element.35), channel_id=1, source_target_pairs={{0,4},{4,0},{8,12},{12,8},{1,5},{5,1},{9,13},{13,9},{2,6},{6,2},{1... | collective-permute-start | bytes 196616 | tf_op jit(solution)/shard_map/ppermute | solution.py:64
  53.3 5.6 %collective-permute-start.16 = (bf16[1,512,128]{1,2,0:T(8,128)(2,1)S(1)}, bf16[1,512,128]{1,2,0:T(8,128)(2,1)S(1)}, u32[]{:S(2)}, u32[]{:S(2)}) collective-permute-start(bf16[1,512,128]{1,2,0:T(8,128)(2,1)S(1)} %get-tuple-element.56), channel_id=1, source_target_pairs={{0,2},{2,0},{1,3},{3,1},{4,6},{6,4},{5,7},{7,5},{8,10},{10,8},{9,1... | collective-permute-start | bytes 393224 | tf_op jit(solution)/shard_map/ppermute | solution.py:47
  56.2 9.2 %copy-start.3 = (bf16[2048,512]{1,0:T(8,128)(2,1)S(1)}, bf16[2048,512]{1,0:T(8,128)(2,1)}, u32[]{:S(2)}) copy-start(bf16[2048,512]{1,0:T(8,128)(2,1)} %param.22) | copy-start | bytes 6291460
  56.2 4.6 %collective-permute-start.11 = (f32[21,512]{1,0:T(8,128)S(1)}, f32[21,512]{1,0:T(8,128)S(1)}, u32[]{:S(2)}, u32[]{:S(2)}) collective-permute-start(f32[21,512]{1,0:T(8,128)S(1)} %get-tuple-element.84), channel_id=1, source_target_pairs={{0,2},{1,3},{2,0},{3,1},{4,6},{5,7},{6,4},{7,5},{8,10},{9,11},{10,... | collective-permute-start | bytes 129032 | tf_op jit(solution)/shard_map/ppermute | solution.py:64
  56.8 4.0 %collective-permute-start.12 = (f32[21,512]{1,0:T(8,128)S(1)}, f32[21,512]{1,0:T(8,128)S(1)}, u32[]{:S(2)}, u32[]{:S(2)}) collective-permute-start(f32[21,512]{1,0:T(8,128)S(1)} %get-tuple-element.85), channel_id=1, source_target_pairs={{0,3},{1,2},{2,1},{3,0},{4,7},{5,6},{6,5},{7,4},{8,11},{9,10},{10,... | collective-permute-start | bytes 129032 | tf_op jit(solution)/shard_map/ppermute | solution.py:64
  57.4 3.5 %collective-permute-start.10 = (f32[21,512]{1,0:T(8,128)S(1)}, f32[21,512]{1,0:T(8,128)S(1)}, u32[]{:S(2)}, u32[]{:S(2)}) collective-permute-start(f32[21,512]{1,0:T(8,128)S(1)} %get-tuple-element.28), channel_id=1, source_target_pairs={{0,1},{1,0},{2,3},{3,2},{4,5},{5,4},{6,7},{7,6},{8,9},{9,8},{10,11... | collective-permute-start | bytes 129032 | tf_op jit(solution)/shard_map/ppermute | solution.py:64
  58.9 6.5 %collective-permute-start.17 = (bf16[2,512,128]{1,2,0:T(8,128)(2,1)S(1)}, bf16[2,512,128]{1,2,0:T(8,128)(2,1)S(1)}, u32[]{:S(2)}, u32[]{:S(2)}) collective-permute-start(bf16[2,512,128]{1,2,0:T(8,128)(2,1)S(1)} %pad_maximum_fusion.4), channel_id=1, source_target_pairs={{0,1},{1,0},{2,3},{3,2},{4,5},{5,4},{6,7},{7,6},{8,9},{9,8},{10,11... | collective-permute-start | bytes 786440 | tf_op jit(solution)/shard_map/ppermute | solution.py:47
  60.9 6.1 %collective-permute-start.13 = (f32[21,512]{1,0:T(8,128)S(1)}, f32[21,512]{1,0:T(8,128)S(1)}, u32[]{:S(2)}, u32[]{:S(2)}) collective-permute-start(f32[21,512]{1,0:T(8,128)S(1)} %pad_add_fusion), channel_id=1, source_target_pairs={{0,4},{4,0},{8,12},{12,8},{1,5},{5,1},{9,13},{13,9},{2,6},{6,2},{1... | collective-permute-start | bytes 129032 | tf_op jit(solution)/shard_map/ppermute | solution.py:64
  61.8 6.5 %collective-permute-start.14 = (f32[21,512]{1,0:T(8,128)S(1)}, f32[21,512]{1,0:T(8,128)S(1)}, u32[]{:S(2)}, u32[]{:S(2)}) collective-permute-start(f32[21,512]{1,0:T(8,128)S(1)} %pad_add_fusion), channel_id=1, source_target_pairs={{0,8},{4,12},{8,0},{12,4},{1,9},{5,13},{9,1},{13,5},{2,10},{6,14},... | collective-permute-start | bytes 129032 | tf_op jit(solution)/shard_map/ppermute | solution.py:64
  64.1 5.9 %collective-permute-start.15 = (f32[21,512]{1,0:T(8,128)S(1)}, f32[21,512]{1,0:T(8,128)S(1)}, u32[]{:S(2)}, u32[]{:S(2)}) collective-permute-start(f32[21,512]{1,0:T(8,128)S(1)} %pad_add_fusion), channel_id=1, source_target_pairs={{0,12},{4,8},{8,4},{12,0},{1,13},{5,9},{9,5},{13,1},{2,14},{6,10},... | collective-permute-start | bytes 129032 | tf_op jit(solution)/shard_map/ppermute | solution.py:64

commit v11 on v10

--- a/solution.py
+++ b/solution.py
@@ -85,7 +85,7 @@
 def sum_over_seq(x, tied):
     count = lax.axis_size("seq")
     me = lax.axis_index("seq")
-    if count > 4:
+    if count > 1:
         step = 1
         while step < count:
             got, tied = lax.optimization_barrier((xor_exchange(x, "seq", step), tied))
@@ -195,8 +195,12 @@
         window = extended[rim_width - shift_back : rim_width - shift_back + row_count]
         columns.append(window[:, None] == letters[None, :])
     onehot_t = jnp.concatenate(columns, axis=1).T.astype(jnp.bfloat16)
-    table_t = kmer_table.reshape(kmer_len * letter_count, model_width).T
-    embedded = jnp.dot(table_t, onehot_t, preferred_element_type=jnp.float32)
+    embedded = jnp.einsum(
+        "kad,kar->dr",
+        kmer_table,
+        onehot_t.reshape(kmer_len, letter_count, row_count),
+        preferred_element_type=jnp.float32,
+    )
     inv_rms = lax.rsqrt(jnp.mean(embedded * embedded, axis=0, keepdims=True) + NORM_EPSILON)
     normed = embedded * inv_rms
     scaled_normed = normed * norm_gain[:, None]
@@ -216,7 +220,10 @@
     d_gated = reduce_blocks_cp(gated_partial, local_width).T * grad_scale
     dft = dft_matrix(length)
     filter_rows = long_filter.reshape(long_filter.shape[2], long_filter.shape[3])
-    spec_g = add_conj_flip(forward_dft(filter_rows, dft))
+    both_filters = forward_dft(jnp.concatenate([filter_rows, pair_flip(filter_rows)], axis=0), dft)
+    conj_sign = np.where(np.arange(2 * length) > length, -1.0, 1.0).astype(np.float32)[None, :]
+    channels = filter_rows.shape[0]
+    spec_g = both_filters[:channels] + both_filters[channels:] * conj_sign
     ga, gb = halves(spec_g)
     d_conv = (d_gated * query_part).astype(jnp.bfloat16)
     both_cols = all_to_all_seq(jnp.stack([mixed_in, d_conv]), 1, 2)

time: 71.6 us -> 75 us (1.047)
  waiting for transfers between devices: 11.7 us -> 16.3 us
  local copies, waits for them, and re-layouts: 4.57 us -> 3.42 us
  starting transfers between devices: 24.3 us -> 23.4 us
    ppermute x15 -> x12, starting transfers between devices: 18.6 us -> 13.5 us  [group_exchange(): return lax.ppermute(x, axes, [(i, i ^ offset) for i in range(count)])]
    ppermute x2 -> x4, waiting for transfers between devices: 0.43 us -> 4.46 us  [xor_exchange(): return lax.ppermute(x, axis, [(i, i ^ step) for i in range(count)])]
    ppermute x2 -> x4, starting transfers between devices: 1.63 us -> 4.96 us  [xor_exchange(): return lax.ppermute(x, axis, [(i, i ^ step) for i in range(count)])]
    dot_general x3, matrix products: 1.82 us -> 3.23 us  [forward_dft(): jnp.dot(signal.astype(jnp.float32), dft, precision=TRANSFORM_PRECISION)]
    select_n x4, other arithmetic: 0.17 us -> 1.43 us  [pick(): out = jnp.where(index == j, blocks[j], out)]
    select_n x2, other arithmetic: 1.45 us -> 0.21 us  [pair_flip(): return jnp.where(even, up, down)]
    slice x2, local copies, waits for them, and re-layouts: 1.16 us -> 0.05 us  [pair_flip(): down = jnp.roll(values, 1, axis=0)]
    select_n x4, other arithmetic: 0.12 us -> 1.04 us  [all_to_all_seq(): piece = jnp.where(me ^ source == offset, got[offset], piece)]
  transfers between devices with their start and end apart: 18 -> 17, of which waited for: 7 -> 8; matrix products, arithmetic and copies ran while one was open for 28% -> 26% of each run, Pallas kernels for 0% -> 0%
where the time goes in v11:
time: 75 us; the launch traced here: 74.7 us
  starting transfers between devices  23.4 us (31%)
  matrix products  20.6 us (27%)
  waiting for transfers between devices  16.3 us (22%)
  other arithmetic  9.61 us (13%)
  local copies, waits for them, and re-layouts  3.42 us (5%)
  between operations  1.35 us (2%)
    ppermute x12, starting transfers between devices, group_exchange(): return lax.ppermute(x, axes, [(i, i ^ offset) for i in range(count)])  13.5 us
    ppermute x12, waiting for transfers between devices, group_exchange(): return lax.ppermute(x, axes, [(i, i ^ offset) for i in range(count)])  11.8 us
    ppermute x4, starting transfers between devices, xor_exchange(): return lax.ppermute(x, axis, [(i, i ^ step) for i in range(count)])  4.96 us
    ppermute x1, starting transfers between devices, from_behind(): lax.ppermute(value, axis, [(source, source + steps) for source in range(f...  4.94 us
    ppermute x4, waiting for transfers between devices, xor_exchange(): return lax.ppermute(x, axis, [(i, i ^ step) for i in range(count)])  4.46 us
    dot_general x1, matrix products, per_device(): jnp.einsum('dr,dmc->mcr', hidden, in_proj, preferred_element_type=jnp.flo...  3.9 us
    dot_general x3, matrix products, inverse_dft(): lax.dot_general(spec * weight, dft, (((1,), (1,)), ((), ())), precision=T...  3.86 us
    dot_general x3, matrix products, forward_dft(): jnp.dot(signal.astype(jnp.float32), dft, precision=TRANSFORM_PRECISION)  3.23 us
  transfers between devices with their start and end apart: 17, of which 8 were waited for; matrix products, arithmetic and copies ran while one was open for 26% of the time, Pallas kernels for 0%

profile of v11, /device:TPU:0, one launch (start us, length us, event | category | flops | bytes accessed | tf_op | source)
XLA Modules:
  0.0 74.7 jit_solution(16988280249265501761)
XLA Ops:
  0.6 0.8 %slice_add_fusion.1 = s32[3]{0:T(128)S(1)} fusion(s32[128]{0:T(128)} %param.17), kind=kLoop, calls=%fused_computation.239 | loop fusion | flops 3 | bytes 24 | tf_op jit(solution)/shard_map/add | solution.py:190
  1.4 4.9 %collective-permute-start = (s32[3]{0:T(128)S(1)}, s32[3]{0:T(128)S(1)}, u32[]{:S(2)}, u32[]{:S(2)}) collective-permute-start(s32[3]{0:T(128)S(1)} %slice_add_fusion.1), channel_id=1, source_target_pairs={{0,4},{4,8},{8,12},{1,5},{5,9},{9,13},{2,6},{6,10},{10,14},{3,7},{... | collective-permute-start | bytes 44 | tf_op jit(solution)/shard_map/ppermute | solution.py:17
  6.4 2.5 %fusion.136 = f32[128,2048]{1,0:T(8,128)S(1)} fusion(bf16[128,512]{1,0:T(8,128)(2,1)} %param.23, bf16[2048,512]{1,0:T(8,128)(2,1)} %param.22), kind=kOutput, calls=%fused_computation.249 | convolution fusion | flops 268435456 | bytes 3276800 | tf_op jit(solution)/shard_map/rd,cd->rc/dot_general | solution.py:219
  8.9 0.8 %select_select_fusion = f32[128,512]{1,0:T(8,128)} fusion(f32[128,2048]{1,0:T(8,128)S(1)} %fusion.136, pred[]{:T(512)S(6)} %eq.233, pred[]{:T(512)S(6)} %eq.232, pred[]{:T(512)S(6)} %eq.231), kind=kLoop, calls=%fused_computation.119 | loop fusion | flops 196608 | bytes 1310723 | tf_op jit(solution)/shard_map/jit(_where)/select_n | solution.py:76
  9.7 0.7 collective-permute-start.3
  10.3 0.9 %select_select_fusion.2 = (f32[128,512]{1,0:T(8,128)}, f32[128,512]{1,0:T(8,128)}) fusion(f32[128,2048]{1,0:T(8,128)S(1)} %fusion.136, pred[]{:T(512)S(6)} %eq.114, pred[]{:T(512)S(6)} %eq.113, pred[]{:T(512)S(6)} %eq.112, pred[]{:T(512)S(6)} %eq.230, pred[]{:T(512)S(6)} %eq.116, pred[]{:T(512)S(6)} %eq.115), kind=kLoop, calls=%fused_computation.121 | loop fusion | flops 393216 | bytes 1572870 | tf_op jit(solution)/shard_map/jit(_where)/select_n | solution.py:76
  11.2 1.0 %collective-permute-start.1 = (f32[128,512]{1,0:T(8,128)}, f32[128,512]{1,0:T(8,128)}, u32[]{:S(2)}, u32[]{:S(2)}) collective-permute-start(f32[128,512]{1,0:T(8,128)} %get-tuple-element.54), channel_id=1, source_target_pairs={{0,1},{1,0},{2,3},{3,2},{4,5},{5,4},{6,7},{7,6},{8,9},{9,8},{10,11... | collective-permute-start | bytes 786440 | tf_op jit(solution)/shard_map/ppermute | solution.py:64
  12.2 0.5 collective-permute-start.2
  13.2 0.6 fusion.103
  14.3 2.1 %fusion.22 = f32[256,1024]{1,0:T(8,128)} fusion(f32[512,1024]{1,0:T(8,128)S(1)} %bitcast.165, f32[128,512]{1,0:T(8,128)S(1)} %maximum_select_fusion, f32[128,512]{1,0:T(8,128)S(1)} %bitcast.173), kind=kOutput, calls=%fused_computation.41 | convolution fusion | flops 805437440 | bytes 3670016 | tf_op jit(solution)/shard_map/dot_general | solution.py:133
  16.6 0.5 copy-done.25
  17.7 3.9 %convolution_bitcast_fusion.2 = f32[3,512,128]{1,2,0:T(8,128)S(1)} fusion(bf16[2048,3,512]{2,0,1:T(8,128)(2,1)} %param.20, f32[128,2048]{1,0:T(8,128)S(1)} %get-tuple-element.90, f32[2048]{0:T(1024)S(1)} %copy-done.14, f32[128]{0:T(128)S(1)} %add_rsqrt_fusion), kind=kOutput, calls=%fused_computation.6 | convolution fusion | flops 806092800 | bytes 8135168 | tf_op jit(solution)/shard_map/dr,dmc->mcr/dot_general | solution.py:208
  21.7 0.7 copy-done.13
  22.4 1.8 %collective-permute-done.2 = f32[128,512]{1,0:T(8,128)} collective-permute-done((f32[128,512]{1,0:T(8,128)}, f32[128,512]{1,0:T(8,128)}, u32[]{:S(2)}, u32[]{:S(2)}) %collective-permute-start.2) | collective-permute-done | bytes 262176 | tf_op jit(solution)/shard_map/ppermute | solution.py:64
  24.2 1.3 %fusion.61 = (bf16[1,512,128]{1,2,0:T(8,128)(2,1)S(1)}, f32[128,512]{1,0:T(8,128)S(1)}) fusion(f32[3,512,128]{1,2,0:T(8,128)S(1)} %convolution_bitcast_fusion.2, f32[128,512]{1,0:T(8,128)} %copy-done.13, f32[128,512]{1,0:T(8,128)} %collective-permute-done.2, f32[128,512]{1,0:T(8,128)} %collective-permute-done.1, f32[128,2048]{1,0:T(8,128)S(1)} %copy-done.2, ...), kind=kLoop, calls=%fused_computation.134 | loop fusion | flops 589824 | bytes 2490371 | tf_op jit(solution)/shard_map/stack | solution.py:229
  25.6 0.7 select_select_fusion.16
  26.3 1.6 %collective-permute-start.6 = (bf16[2,128,128]{1,2,0:T(8,128)(2,1)}, bf16[2,128,128]{1,2,0:T(8,128)(2,1)}, u32[]{:S(2)}, u32[]{:S(2)}) collective-permute-start(bf16[2,128,128]{1,2,0:T(8,128)(2,1)} %get-tuple-element.38), channel_id=1, source_target_pairs={{0,4},{4,0},{8,12},{12,8},{1,5},{5,1},{9,13},{13,9},{2,6},{6,2},{1... | collective-permute-start | bytes 196616 | tf_op jit(solution)/shard_map/ppermute | solution.py:64
  27.8 0.7 select_select_fusion.17
  28.5 1.6 %collective-permute-start.5 = (bf16[2,128,128]{1,2,0:T(8,128)(2,1)}, bf16[2,128,128]{1,2,0:T(8,128)(2,1)}, u32[]{:S(2)}, u32[]{:S(2)}) collective-permute-start(bf16[2,128,128]{1,2,0:T(8,128)(2,1)} %get-tuple-element.76), channel_id=1, source_target_pairs={{0,8},{4,12},{8,0},{12,4},{1,9},{5,13},{9,1},{13,5},{2,10},{6,14},... | collective-permute-start | bytes 196616 | tf_op jit(solution)/shard_map/ppermute | solution.py:64
  30.1 1.3 %collective-permute-start.4 = (bf16[2,128,128]{1,2,0:T(8,128)(2,1)}, bf16[2,128,128]{1,2,0:T(8,128)(2,1)}, u32[]{:S(2)}, u32[]{:S(2)}) collective-permute-start(bf16[2,128,128]{1,2,0:T(8,128)(2,1)} %get-tuple-element.77), channel_id=1, source_target_pairs={{0,12},{4,8},{8,4},{12,0},{1,13},{5,9},{9,5},{13,1},{2,14},{6,10},... | collective-permute-start | bytes 196616 | tf_op jit(solution)/shard_map/ppermute | solution.py:64
  31.5 0.9 %fusion.21 = f32[128,1024]{1,0:T(8,128)} fusion(f32[256,1024]{1,0:T(8,128)S(1)} %copy-done.6, f32[1024]{0:T(1024)S(1)} %copy-done.27), kind=kLoop, calls=%fused_computation.40 | loop fusion | flops 262144 | bytes 1576960 | tf_op jit(solution)/shard_map/add | solution.py:226
  32.4 4.6 %collective-permute-done.5 = bf16[2,128,128]{1,2,0:T(8,128)(2,1)} collective-permute-done((bf16[2,128,128]{1,2,0:T(8,128)(2,1)}, bf16[2,128,128]{1,2,0:T(8,128)(2,1)}, u32[]{:S(2)}, u32[]{:S(2)}) %collective-permute-start.5) | collective-permute-done | bytes 65568 | tf_op jit(solution)/shard_map/ppermute | solution.py:64
  37.0 0.9 %select_select_fusion.13 = (bf16[2,128,128]{1,2,0:T(8,128)(2,1)S(1)}, bf16[2,128,128]{1,2,0:T(8,128)(2,1)S(1)}, bf16[2,128,128]{1,2,0:T(8,128)(2,1)S(1)}) fusion(bf16[2,128,128]{1,2,0:T(8,128)(2,1)} %collective-permute-done.4, bf16[2,128,128]{1,2,0:T(8,128)(2,1)} %collective-permute-done.5, bf16[2,128,128]{1,2,0:T(8,128)(2,1)} %collective-permute-done.6, ...), kind=kLoop, calls=%fused_computation.196 | loop fusion | flops 294912 | bytes 458761 | tf_op jit(solution)/shard_map/jit(_where)/select_n | solution.py:127
  38.0 0.6 fusion.65
  38.6 0.6 fusion.66
  40.5 1.0 %fusion.8 = bf16[1,128,512]{1,2,0:T(8,128)(2,1)S(1)} fusion(f32[512,1024]{1,0:T(8,128)S(1)} %bitcast.168, f32[128,512]{1,0:T(8,128)S(1)} %get-tuple-element.56, f32[128,512]{1,0:T(8,128)S(1)} %get-tuple-element.57, f32[1024]{0:T(1024)S(1)} %copy-done.16), kind=kOutput, calls=%fused_computation.17 | convolution fusion | flops 402980864 | bytes 2756608 | tf_op jit(solution)/shard_map/dot_general | solution.py:141
  41.6 1.0 %fusion.9 = bf16[1,128,512]{1,2,0:T(8,128)(2,1)S(1)} fusion(f32[512,1024]{1,0:T(8,128)S(1)} %bitcast.169, f32[128,512]{1,0:T(8,128)S(1)} %get-tuple-element.87, f32[128,512]{1,0:T(8,128)S(1)} %get-tuple-element.88, f32[1024]{0:T(1024)S(1)} %copy-done.16), kind=kOutput, calls=%fused_computation.18 | convolution fusion | flops 402980864 | bytes 2756608 | tf_op jit(solution)/shard_map/dot_general | solution.py:141
  42.6 2.3 %collective-permute-start.9 = (bf16[2,128,128]{1,2,0:T(8,128)(2,1)S(1)}, bf16[2,128,128]{1,2,0:T(8,128)(2,1)S(1)}, u32[]{:S(2)}, u32[]{:S(2)}) collective-permute-start(bf16[2,128,128]{1,2,0:T(8,128)(2,1)S(1)} %get-tuple-element.31), channel_id=1, source_target_pairs={{0,4},{4,0},{8,12},{12,8},{1,5},{5,1},{9,13},{13,9},{2,6},{6,2},{1... | collective-permute-start | bytes 196616 | tf_op jit(solution)/shard_map/ppermute | solution.py:64
  45.0 1.6 %collective-permute-start.8 = (bf16[2,128,128]{1,2,0:T(8,128)(2,1)S(1)}, bf16[2,128,128]{1,2,0:T(8,128)(2,1)S(1)}, u32[]{:S(2)}, u32[]{:S(2)}) collective-permute-start(bf16[2,128,128]{1,2,0:T(8,128)(2,1)S(1)} %get-tuple-element.67), channel_id=1, source_target_pairs={{0,8},{4,12},{8,0},{12,4},{1,9},{5,13},{9,1},{13,5},{2,10},{6,14},... | collective-permute-start | bytes 196616 | tf_op jit(solution)/shard_map/ppermute | solution.py:64
  46.5 1.0 %collective-permute-start.7 = (bf16[2,128,128]{1,2,0:T(8,128)(2,1)S(1)}, bf16[2,128,128]{1,2,0:T(8,128)(2,1)S(1)}, u32[]{:S(2)}, u32[]{:S(2)}) collective-permute-start(bf16[2,128,128]{1,2,0:T(8,128)(2,1)S(1)} %get-tuple-element.68), channel_id=1, source_target_pairs={{0,12},{4,8},{8,4},{12,0},{1,13},{5,9},{9,5},{13,1},{2,14},{6,10},... | collective-permute-start | bytes 196616 | tf_op jit(solution)/shard_map/ppermute | solution.py:64
  47.8 4.2 %collective-permute-done.8 = bf16[2,128,128]{1,2,0:T(8,128)(2,1)S(1)} collective-permute-done((bf16[2,128,128]{1,2,0:T(8,128)(2,1)S(1)}, bf16[2,128,128]{1,2,0:T(8,128)(2,1)S(1)}, u32[]{:S(2)}, u32[]{:S(2)}) %collective-permute-start.8) | collective-permute-done | bytes 65568 | tf_op jit(solution)/shard_map/ppermute | solution.py:64
  52.0 0.7 collective-permute-done.7
  53.1 1.3 %fusion.3 = f32[128]{0:T(128)S(1)} fusion(f32[3,512,128]{1,2,0:T(8,128)S(1)} %copy-done.4, bf16[2048,3,512]{2,0,1:T(8,128)(2,1)S(1)} %bitcast.172, f32[128,2048]{1,0:T(8,128)S(1)} %get-tuple-element.90, f32[2048]{0:T(1024)S(1)} %copy-done.15, f32[128]{0:T(128)S(1)} %copy-done.22, bf16[1,512,128]{1,2,0:T(8,128)(2,1)S(1)} %get-tuple-element.53, ...), kind=kOutput, calls=%fused_computation.9 | convolution fusion | flops 808058752 | bytes 8528896 | tf_op jit(solution)/shard_map/dr,dmc->mcr/dot_general | solution.py:210
  54.3 2.2 %fusion.10 = (f32[2048]{0:T(1024)S(1)}, f32[128,2048,1]{1,0,2:T(8,128)S(1)}) fusion(f32[128,2048]{1,0:T(8,128)S(1)} %get-tuple-element.90, f32[128]{0:T(128)S(1)} %copy-done.22, bf16[2048,3,512]{2,0,1:T(8,128)(2,1)S(1)} %bitcast.172, bf16[1,512,128]{1,2,0:T(8,128)(2,1)S(1)} %get-tuple-element.53, bf16[1,512,128]{1,2,0:T(8,128)(2,1)S(1)} %get-tuple-element.52, ...), kind=kOutput, calls=%fused_computation.20 | convolution fusion | flops 806483968 | bytes 8790528 | tf_op jit(solution)/shard_map/mcr,dmc->rd/dot_general | solution.py:262
  56.5 1.2 %collective-permute-start.14 = (bf16[1,512,128]{1,2,0:T(8,128)(2,1)S(1)}, bf16[1,512,128]{1,2,0:T(8,128)(2,1)S(1)}, u32[]{:S(2)}, u32[]{:S(2)}) collective-permute-start(bf16[1,512,128]{1,2,0:T(8,128)(2,1)S(1)} %get-tuple-element.51), channel_id=1, source_target_pairs={{0,2},{2,0},{1,3},{3,1},{4,6},{6,4},{5,7},{7,5},{8,10},{10,8},{9,1... | collective-permute-start | bytes 393224 | tf_op jit(solution)/shard_map/ppermute | solution.py:47
  57.7 0.6 convolution_multiply_fusion.1
  58.3 0.7 fusion
  59.2 1.1 %collective-permute-start.11 = (f32[21,512]{1,0:T(8,128)S(1)}, f32[21,512]{1,0:T(8,128)S(1)}, u32[]{:S(2)}, u32[]{:S(2)}) collective-permute-start(f32[21,512]{1,0:T(8,128)S(1)} %get-tuple-element.78), channel_id=1, source_target_pairs={{0,2},{1,3},{2,0},{3,1},{4,6},{5,7},{6,4},{7,5},{8,10},{9,11},{10,... | collective-permute-start | bytes 129032 | tf_op jit(solution)/shard_map/ppermute | solution.py:64
  60.3 0.8 %collective-permute-start.12 = (f32[21,512]{1,0:T(8,128)S(1)}, f32[21,512]{1,0:T(8,128)S(1)}, u32[]{:S(2)}, u32[]{:S(2)}) collective-permute-start(f32[21,512]{1,0:T(8,128)S(1)} %get-tuple-element.79), channel_id=1, source_target_pairs={{0,3},{1,2},{2,1},{3,0},{4,7},{5,6},{6,5},{7,4},{8,11},{9,10},{10,... | collective-permute-start | bytes 129032 | tf_op jit(solution)/shard_map/ppermute | solution.py:64
  61.1 0.6 collective-permute-done.14
  61.8 1.9 %fusion.30 = f32[128,512]{1,0:T(8,128)} fusion(f32[512,1024]{1,0:T(8,128)S(1)} %bitcast.170, f32[128,512]{1,0:T(8,128)S(1)} %get-tuple-element.59, f32[128,512]{1,0:T(8,128)S(1)} %get-tuple-element.58, f32[1024]{0:T(1024)S(1)} %copy-done.16), kind=kOutput, calls=%fused_computation.52 | convolution fusion | flops 402915328 | bytes 2887680 | tf_op jit(solution)/shard_map/dot_general | solution.py:141
  64.2 1.4 %collective-permute-start.13 = (f32[21,512]{1,0:T(8,128)S(1)}, f32[21,512]{1,0:T(8,128)S(1)}, u32[]{:S(2)}, u32[]{:S(2)}) collective-permute-start(f32[21,512]{1,0:T(8,128)S(1)} %pad_add_fusion), channel_id=1, source_target_pairs={{0,4},{4,0},{8,12},{12,8},{1,5},{5,1},{9,13},{13,9},{2,6},{6,2},{1... | collective-permute-start | bytes 129032 | tf_op jit(solution)/shard_map/ppermute | solution.py:47
  66.3 0.9 %fusion.7 = bf16[128,512]{1,0:T(8,128)(2,1)} fusion(f32[128,512]{1,0:T(8,128)S(1)} %fusion.33, f32[128,512]{1,0:T(8,128)S(1)} %fusion.35, f32[128,512]{1,0:T(8,128)S(1)} %fusion.37, bf16[2048,512]{1,0:T(8,128)(2,1)S(1)} %copy-done.7, f32[128,2048]{1,0:T(8,128)S(1)} %get-tuple-element.90, s32[]{:T(128)S(6)} %select_n.697, ...), kind=kOutput, calls=%fused_computation.16 | convolution fusion | flops 67633152 | bytes 2228231 | tf_op jit(solution)/shard_map/cr,cd->rd/dot_general | solution.py:247
  67.2 1.1 %collective-permute-done.13 = f32[21,512]{1,0:T(8,128)S(1)} collective-permute-done((f32[21,512]{1,0:T(8,128)S(1)}, f32[21,512]{1,0:T(8,128)S(1)}, u32[]{:S(2)}, u32[]{:S(2)}) %collective-permute-start.13) | collective-permute-done | bytes 43040 | tf_op jit(solution)/shard_map/ppermute | solution.py:47
  68.4 2.3 %collective-permute-start.16 = (f32[21,512]{1,0:T(8,128)S(1)}, f32[21,512]{1,0:T(8,128)S(1)}, u32[]{:S(2)}, u32[]{:S(2)}) collective-permute-start(f32[21,512]{1,0:T(8,128)S(1)} %add.180), channel_id=1, source_target_pairs={{0,8},{4,12},{8,0},{12,4},{1,9},{5,13},{9,1},{13,5},{2,10},{6,14},... | collective-permute-start | bytes 129032 | tf_op jit(solution)/shard_map/ppermute | solution.py:47
  70.7 2.7 %collective-permute-done.16 = f32[21,512]{1,0:T(8,128)S(1)} collective-permute-done((f32[21,512]{1,0:T(8,128)S(1)}, f32[21,512]{1,0:T(8,128)S(1)}, u32[]{:S(2)}, u32[]{:S(2)}) %collective-permute-start.16) | collective-permute-done | bytes 43040 | tf_op jit(solution)/shard_map/ppermute | solution.py:47
  73.4 0.6 slice.290
  74.0 0.6 copy.28
  (124 shorter events, 5.1 us)
Async XLA Ops:
  0.6 16.5 %copy-start = (bf16[4,5,2048]{2,0,1:T(4,128)(2,1)S(1)}, bf16[4,5,2048]{2,0,1:T(4,128)(2,1)}, u32[]{:S(2)}) copy-start(bf16[4,5,2048]{2,0,1:T(4,128)(2,1)} %param.18) | copy-start | bytes 245764
  1.4 15.0 %collective-permute-start = (s32[3]{0:T(128)S(1)}, s32[3]{0:T(128)S(1)}, u32[]{:S(2)}, u32[]{:S(2)}) collective-permute-start(s32[3]{0:T(128)S(1)} %slice_add_fusion.1), channel_id=1, source_target_pairs={{0,4},{4,8},{8,12},{1,5},{5,9},{9,13},{2,6},{6,10},{10,14},{3,7},{... | collective-permute-start | bytes 44 | tf_op jit(solution)/shard_map/ppermute | solution.py:17
  8.9 5.0 %copy-start.1 = (f32[128,2048]{1,0:T(8,128)}, f32[128,2048]{1,0:T(8,128)S(1)}, u32[]{:S(2)}) copy-start(f32[128,2048]{1,0:T(8,128)S(1)} %fusion.136) | copy-start | bytes 3145732
  8.9 3.9 %copy-start.31 = (s32[128]{0:T(128)S(1)}, s32[128]{0:T(128)}, u32[]{:S(2)}) copy-start(s32[128]{0:T(128)} %param.17) | copy-start | bytes 1540
  8.9 3.9 %copy-start.8 = (f32[1,1,128,512]{3,2,1,0:T(8,128)S(1)}, f32[1,1,128,512]{3,2,1,0:T(8,128)}, u32[]{:S(2)}) copy-start(f32[1,1,128,512]{3,2,1,0:T(8,128)} %param.21) | copy-start | bytes 786436
  9.7 12.0 %collective-permute-start.3 = (f32[128,512]{1,0:T(8,128)}, f32[128,512]{1,0:T(8,128)S(1)}, u32[]{:S(2)}, u32[]{:S(2)}) collective-permute-start(f32[128,512]{1,0:T(8,128)} %select_select_fusion), channel_id=1, source_target_pairs={{0,3},{1,2},{2,1},{3,0},{4,7},{5,6},{6,5},{7,4},{8,11},{9,10},{10,... | collective-permute-start | bytes 786440 | tf_op jit(solution)/shard_map/ppermute | solution.py:64
  11.2 2.9 %copy-start.28 = (pred[128]{0:T(512)(128)(4,1)S(1)}, pred[128]{0:T(512)(128)(4,1)}, u32[]{:S(2)}) copy-start(pred[128]{0:T(512)(128)(4,1)} %constant.96) | copy-start | bytes 388
  11.2 10.4 %collective-permute-start.1 = (f32[128,512]{1,0:T(8,128)}, f32[128,512]{1,0:T(8,128)}, u32[]{:S(2)}, u32[]{:S(2)}) collective-permute-start(f32[128,512]{1,0:T(8,128)} %get-tuple-element.54), channel_id=1, source_target_pairs={{0,1},{1,0},{2,3},{3,2},{4,5},{5,4},{6,7},{7,6},{8,9},{9,8},{10,11... | collective-permute-start | bytes 786440 | tf_op jit(solution)/shard_map/ppermute | solution.py:64
  12.2 12.0 %collective-permute-start.2 = (f32[128,512]{1,0:T(8,128)}, f32[128,512]{1,0:T(8,128)}, u32[]{:S(2)}, u32[]{:S(2)}) collective-permute-start(f32[128,512]{1,0:T(8,128)} %get-tuple-element.55), channel_id=1, source_target_pairs={{0,2},{1,3},{2,0},{3,1},{4,6},{5,7},{6,4},{7,5},{8,10},{9,11},{10,... | collective-permute-start | bytes 786440 | tf_op jit(solution)/shard_map/ppermute | solution.py:64
  12.8 3.9 %copy-start.23 = (pred[128,5]{0,1:T(8,128)(4,1)}, pred[128,5]{0,1:T(8,128)(4,1)S(1)}, u32[]{:S(2)}) copy-start(pred[128,5]{0,1:T(8,128)(4,1)S(1)} %iota_compare_fusion.5) | copy-start | bytes 1924
  14.3 3.4 %copy-start.14 = (f32[2048]{0:T(1024)S(1)}, f32[2048]{0:T(1024)}, u32[]{:S(2)}) copy-start(f32[2048]{0:T(1024)} %param.19) | copy-start | bytes 24580
  17.6 3.9 %copy-start.21 = (f32[128]{0:T(128)}, f32[128]{0:T(128)S(1)}, u32[]{:S(2)}) copy-start(f32[128]{0:T(128)S(1)} %add_rsqrt_fusion) | copy-start | bytes 1540
  17.7 6.6 %copy-start.2 = (f32[128,2048]{1,0:T(8,128)S(1)}, f32[128,2048]{1,0:T(8,128)}, u32[]{:S(2)}) copy-start(f32[128,2048]{1,0:T(8,128)} %copy-done.1) | copy-start | bytes 3145732
  21.6 4.0 %copy-start.3 = (f32[3,512,128]{1,2,0:T(8,128)}, f32[3,512,128]{1,2,0:T(8,128)S(1)}, u32[]{:S(2)}) copy-start(f32[3,512,128]{1,2,0:T(8,128)S(1)} %convolution_bitcast_fusion.2) | copy-start | bytes 2359300
  21.6 9.9 %copy-start.6 = (f32[256,1024]{1,0:T(8,128)S(1)}, f32[256,1024]{1,0:T(8,128)}, u32[]{:S(2)}) copy-start(f32[256,1024]{1,0:T(8,128)} %fusion.22) | copy-start | bytes 3145732
  21.6 9.9 %copy-start.27 = (f32[1024]{0:T(1024)S(1)}, f32[1024]{0:T(1024)}, u32[]{:S(2)}) copy-start(f32[1024]{0:T(1024)} %constant.97) | copy-start | bytes 12292
  21.7 0.7 copy-start.13
  26.3 1.6 %copy-start.9 = (bf16[2,128,128]{1,2,0:T(8,128)(2,1)}, bf16[2,128,128]{1,2,0:T(8,128)(2,1)S(1)}, u32[]{:S(2)}) copy-start(bf16[2,128,128]{1,2,0:T(8,128)(2,1)S(1)} %get-tuple-element.40) | copy-start | bytes 196612
  26.3 2.2 %copy-start.10 = (bf16[2,128,128]{1,2,0:T(8,128)(2,1)}, bf16[2,128,128]{1,2,0:T(8,128)(2,1)S(1)}, u32[]{:S(2)}) copy-start(bf16[2,128,128]{1,2,0:T(8,128)(2,1)S(1)} %get-tuple-element.41) | copy-start | bytes 196612
  26.3 2.2 %copy-start.11 = (bf16[2,128,128]{1,2,0:T(8,128)(2,1)}, bf16[2,128,128]{1,2,0:T(8,128)(2,1)S(1)}, u32[]{:S(2)}) copy-start(bf16[2,128,128]{1,2,0:T(8,128)(2,1)S(1)} %get-tuple-element.42) | copy-start | bytes 196612
  26.3 6.1 %collective-permute-start.6 = (bf16[2,128,128]{1,2,0:T(8,128)(2,1)}, bf16[2,128,128]{1,2,0:T(8,128)(2,1)}, u32[]{:S(2)}, u32[]{:S(2)}) collective-permute-start(bf16[2,128,128]{1,2,0:T(8,128)(2,1)} %get-tuple-element.38), channel_id=1, source_target_pairs={{0,4},{4,0},{8,12},{12,8},{1,5},{5,1},{9,13},{13,9},{2,6},{6,2},{1... | collective-permute-start | bytes 196616 | tf_op jit(solution)/shard_map/ppermute | solution.py:64
  28.5 8.5 %collective-permute-start.5 = (bf16[2,128,128]{1,2,0:T(8,128)(2,1)}, bf16[2,128,128]{1,2,0:T(8,128)(2,1)}, u32[]{:S(2)}, u32[]{:S(2)}) collective-permute-start(bf16[2,128,128]{1,2,0:T(8,128)(2,1)} %get-tuple-element.76), channel_id=1, source_target_pairs={{0,8},{4,12},{8,0},{12,4},{1,9},{5,13},{9,1},{13,5},{2,10},{6,14},... | collective-permute-start | bytes 196616 | tf_op jit(solution)/shard_map/ppermute | solution.py:64
  30.1 6.8 %collective-permute-start.4 = (bf16[2,128,128]{1,2,0:T(8,128)(2,1)}, bf16[2,128,128]{1,2,0:T(8,128)(2,1)}, u32[]{:S(2)}, u32[]{:S(2)}) collective-permute-start(bf16[2,128,128]{1,2,0:T(8,128)(2,1)} %get-tuple-element.77), channel_id=1, source_target_pairs={{0,12},{4,8},{8,4},{12,0},{1,13},{5,9},{9,5},{13,1},{2,14},{6,10},... | collective-permute-start | bytes 196616 | tf_op jit(solution)/shard_map/ppermute | solution.py:64
  38.0 1.1 %copy-start.5 = (f32[128,1024]{1,0:T(8,128)S(1)}, f32[128,1024]{1,0:T(8,128)}, u32[]{:S(2)}) copy-start(f32[128,1024]{1,0:T(8,128)} %fusion.21) | copy-start | bytes 1572868
  38.0 1.1 %copy-start.30 = (pred[512]{0:T(512)(128)(4,1)S(1)}, pred[512]{0:T(512)(128)(4,1)}, u32[]{:S(2)}) copy-start(pred[512]{0:T(512)(128)(4,1)} %constant.95) | copy-start | bytes 1540
  39.2 0.7 copy-start.29
  39.8 0.7 copy-start.16
  39.9 13.1 %slice-start = ((s8[6291456]{0:T(1024)(128)(4,1)}), s8[4194304]{0:T(1024)(128)(4,1)S(1)}, s32[]{:S(2)}) async-start(s8[6291456]{0:T(1024)(128)(4,1)} %bitcast.171), calls=%async_computation | async-start | bytes 8388608
  41.5 6.0 %copy-start.12 = (bf16[128,512]{1,0:T(8,128)(2,1)S(1)}, bf16[128,512]{1,0:T(8,128)(2,1)}, u32[]{:S(2)}) copy-start(bf16[128,512]{1,0:T(8,128)(2,1)} %param.23) | copy-start | bytes 393220
  41.5 6.0 %copy-start.18 = (pred[128,5]{0,1:T(8,128)(4,1)S(1)}, pred[128,5]{0,1:T(8,128)(4,1)}, u32[]{:S(2)}) copy-start(pred[128,5]{0,1:T(8,128)(4,1)} %copy-done.17) | copy-start | bytes 1924
  41.5 6.0 %copy-start.20 = (pred[128,5]{0,1:T(8,128)(4,1)S(1)}, pred[128,5]{0,1:T(8,128)(4,1)}, u32[]{:S(2)}) copy-start(pred[128,5]{0,1:T(8,128)(4,1)} %copy-done.19) | copy-start | bytes 1924
  41.5 6.0 %copy-start.24 = (pred[128,5]{0,1:T(8,128)(4,1)S(1)}, pred[128,5]{0,1:T(8,128)(4,1)}, u32[]{:S(2)}) copy-start(pred[128,5]{0,1:T(8,128)(4,1)} %copy-done.23) | copy-start | bytes 1924
  41.5 6.0 %copy-start.26 = (pred[128,5]{0,1:T(8,128)(4,1)S(1)}, pred[128,5]{0,1:T(8,128)(4,1)}, u32[]{:S(2)}) copy-start(pred[128,5]{0,1:T(8,128)(4,1)} %copy-done.25) | copy-start | bytes 1924
  41.6 11.3 %copy-start.4 = (f32[3,512,128]{1,2,0:T(8,128)S(1)}, f32[3,512,128]{1,2,0:T(8,128)}, u32[]{:S(2)}) copy-start(f32[3,512,128]{1,2,0:T(8,128)} %copy-done.3) | copy-start | bytes 2359300
  41.6 11.4 %slice-start.1 = ((s8[6291456]{0:T(1024)(128)(4,1)}), s8[2097152]{0:T(1024)(128)(4,1)S(1)}, s32[]{:S(2)}) async-start(s8[6291456]{0:T(1024)(128)(4,1)} %bitcast.171), calls=%async_computation.1 | async-start | bytes 4194304
  42.6 5.1 %collective-permute-start.9 = (bf16[2,128,128]{1,2,0:T(8,128)(2,1)S(1)}, bf16[2,128,128]{1,2,0:T(8,128)(2,1)S(1)}, u32[]{:S(2)}, u32[]{:S(2)}) collective-permute-start(bf16[2,128,128]{1,2,0:T(8,128)(2,1)S(1)} %get-tuple-element.31), channel_id=1, source_target_pairs={{0,4},{4,0},{8,12},{12,8},{1,5},{5,1},{9,13},{13,9},{2,6},{6,2},{1... | collective-permute-start | bytes 196616 | tf_op jit(solution)/shard_map/ppermute | solution.py:64
  45.0 8.1 %copy-start.15 = (f32[2048]{0:T(1024)S(1)}, f32[2048]{0:T(1024)}, u32[]{:S(2)}) copy-start(f32[2048]{0:T(1024)} %param.19) | copy-start | bytes 24580
  45.0 8.1 %copy-start.22 = (f32[128]{0:T(128)S(1)}, f32[128]{0:T(128)}, u32[]{:S(2)}) copy-start(f32[128]{0:T(128)} %copy-done.21) | copy-start | bytes 1540
  45.0 7.0 %collective-permute-start.8 = (bf16[2,128,128]{1,2,0:T(8,128)(2,1)S(1)}, bf16[2,128,128]{1,2,0:T(8,128)(2,1)S(1)}, u32[]{:S(2)}, u32[]{:S(2)}) collective-permute-start(bf16[2,128,128]{1,2,0:T(8,128)(2,1)S(1)} %get-tuple-element.67), channel_id=1, source_target_pairs={{0,8},{4,12},{8,0},{12,4},{1,9},{5,13},{9,1},{13,5},{2,10},{6,14},... | collective-permute-start | bytes 196616 | tf_op jit(solution)/shard_map/ppermute | solution.py:64
  46.5 6.2 %collective-permute-start.7 = (bf16[2,128,128]{1,2,0:T(8,128)(2,1)S(1)}, bf16[2,128,128]{1,2,0:T(8,128)(2,1)S(1)}, u32[]{:S(2)}, u32[]{:S(2)}) collective-permute-start(bf16[2,128,128]{1,2,0:T(8,128)(2,1)S(1)} %get-tuple-element.68), channel_id=1, source_target_pairs={{0,12},{4,8},{8,4},{12,0},{1,13},{5,9},{9,5},{13,1},{2,14},{6,10},... | collective-permute-start | bytes 196616 | tf_op jit(solution)/shard_map/ppermute | solution.py:64
  56.5 5.2 %collective-permute-start.14 = (bf16[1,512,128]{1,2,0:T(8,128)(2,1)S(1)}, bf16[1,512,128]{1,2,0:T(8,128)(2,1)S(1)}, u32[]{:S(2)}, u32[]{:S(2)}) collective-permute-start(bf16[1,512,128]{1,2,0:T(8,128)(2,1)S(1)} %get-tuple-element.51), channel_id=1, source_target_pairs={{0,2},{2,0},{1,3},{3,1},{4,6},{6,4},{5,7},{7,5},{8,10},{10,8},{9,1... | collective-permute-start | bytes 393224 | tf_op jit(solution)/shard_map/ppermute | solution.py:47
  59.1 6.5 %copy-start.7 = (bf16[2048,512]{1,0:T(8,128)(2,1)S(1)}, bf16[2048,512]{1,0:T(8,128)(2,1)}, u32[]{:S(2)}) copy-start(bf16[2048,512]{1,0:T(8,128)(2,1)} %param.22) | copy-start | bytes 6291460
  59.1 4.6 %collective-permute-start.10 = (f32[21,512]{1,0:T(8,128)S(1)}, f32[21,512]{1,0:T(8,128)S(1)}, u32[]{:S(2)}, u32[]{:S(2)}) collective-permute-start(f32[21,512]{1,0:T(8,128)S(1)} %get-tuple-element.24), channel_id=1, source_target_pairs={{0,1},{1,0},{2,3},{3,2},{4,5},{5,4},{6,7},{7,6},{8,9},{9,8},{10,11... | collective-permute-start | bytes 129032 | tf_op jit(solution)/shard_map/ppermute | solution.py:64
  59.2 4.5 %collective-permute-start.11 = (f32[21,512]{1,0:T(8,128)S(1)}, f32[21,512]{1,0:T(8,128)S(1)}, u32[]{:S(2)}, u32[]{:S(2)}) collective-permute-start(f32[21,512]{1,0:T(8,128)S(1)} %get-tuple-element.78), channel_id=1, source_target_pairs={{0,2},{1,3},{2,0},{3,1},{4,6},{5,7},{6,4},{7,5},{8,10},{9,11},{10,... | collective-permute-start | bytes 129032 | tf_op jit(solution)/shard_map/ppermute | solution.py:64
  60.3 3.8 %collective-permute-start.12 = (f32[21,512]{1,0:T(8,128)S(1)}, f32[21,512]{1,0:T(8,128)S(1)}, u32[]{:S(2)}, u32[]{:S(2)}) collective-permute-start(f32[21,512]{1,0:T(8,128)S(1)} %get-tuple-element.79), channel_id=1, source_target_pairs={{0,3},{1,2},{2,1},{3,0},{4,7},{5,6},{6,5},{7,4},{8,11},{9,10},{10,... | collective-permute-start | bytes 129032 | tf_op jit(solution)/shard_map/ppermute | solution.py:64
  61.7 3.8 %collective-permute-start.15 = (bf16[2,512,128]{1,2,0:T(8,128)(2,1)S(1)}, bf16[2,512,128]{1,2,0:T(8,128)(2,1)S(1)}, u32[]{:S(2)}, u32[]{:S(2)}) collective-permute-start(bf16[2,512,128]{1,2,0:T(8,128)(2,1)S(1)} %pad_maximum_fusion.4), channel_id=1, source_target_pairs={{0,1},{1,0},{2,3},{3,2},{4,5},{5,4},{6,7},{7,6},{8,9},{9,8},{10,11... | collective-permute-start | bytes 786440 | tf_op jit(solution)/shard_map/ppermute | solution.py:47
  64.2 4.2 %collective-permute-start.13 = (f32[21,512]{1,0:T(8,128)S(1)}, f32[21,512]{1,0:T(8,128)S(1)}, u32[]{:S(2)}, u32[]{:S(2)}) collective-permute-start(f32[21,512]{1,0:T(8,128)S(1)} %pad_add_fusion), channel_id=1, source_target_pairs={{0,4},{4,0},{8,12},{12,8},{1,5},{5,1},{9,13},{13,9},{2,6},{6,2},{1... | collective-permute-start | bytes 129032 | tf_op jit(solution)/shard_map/ppermute | solution.py:47
  68.4 5.1 %collective-permute-start.16 = (f32[21,512]{1,0:T(8,128)S(1)}, f32[21,512]{1,0:T(8,128)S(1)}, u32[]{:S(2)}, u32[]{:S(2)}) collective-permute-start(f32[21,512]{1,0:T(8,128)S(1)} %add.180), channel_id=1, source_target_pairs={{0,8},{4,12},{8,0},{12,4},{1,9},{5,13},{9,1},{13,5},{2,10},{6,14},... | collective-permute-start | bytes 129032 | tf_op jit(solution)/shard_map/ppermute | solution.py:47
  (3 other events, 1.7 us)

commit v12 on v11

--- a/solution.py
+++ b/solution.py
@@ -85,7 +85,7 @@
 def sum_over_seq(x, tied):
     count = lax.axis_size("seq")
     me = lax.axis_index("seq")
-    if count > 1:
+    if count > 4:
         step = 1
         while step < count:
             got, tied = lax.optimization_barrier((xor_exchange(x, "seq", step), tied))

time: 75 us -> 73.8 us (0.984)
  waiting for transfers between devices: 16.3 us -> 14.4 us
  starting transfers between devices: 23.4 us -> 24.2 us
    ppermute x12 -> x15, starting transfers between devices: 13.5 us -> 18 us  [group_exchange(): return lax.ppermute(x, axes, [(i, i ^ offset) for i in range(count)])]
    ppermute x4 -> x2, waiting for transfers between devices: 4.46 us -> 0.59 us  [xor_exchange(): return lax.ppermute(x, axis, [(i, i ^ step) for i in range(count)])]
    ppermute x4 -> x2, starting transfers between devices: 4.96 us -> 1.3 us  [xor_exchange(): return lax.ppermute(x, axis, [(i, i ^ step) for i in range(count)])]
    ppermute x12 -> x15, waiting for transfers between devices: 11.8 us -> 13.8 us  [group_exchange(): return lax.ppermute(x, axes, [(i, i ^ offset) for i in range(count)])]
  transfers between devices with their start and end apart: 17 -> 18, of which waited for: 8 -> 8; matrix products, arithmetic and copies ran while one was open for 26% -> 26% of each run, Pallas kernels for 0% -> 0%
where the time goes in v12:
time: 73.8 us; the launch traced here: 73.5 us
  starting transfers between devices  24.2 us (33%)
  matrix products  20.6 us (28%)
  waiting for transfers between devices  14.4 us (20%)
  other arithmetic  9.63 us (13%)
  local copies, waits for them, and re-layouts  3.42 us (5%)
  between operations  1.36 us (2%)
    ppermute x15, starting transfers between devices, group_exchange(): return lax.ppermute(x, axes, [(i, i ^ offset) for i in range(count)])  18 us
    ppermute x15, waiting for transfers between devices, group_exchange(): return lax.ppermute(x, axes, [(i, i ^ offset) for i in range(count)])  13.8 us
    ppermute x1, starting transfers between devices, from_behind(): lax.ppermute(value, axis, [(source, source + steps) for source in range(f...  4.94 us
    dot_general x1, matrix products, per_device(): jnp.einsum('dr,dmc->mcr', hidden, in_proj, preferred_element_type=jnp.flo...  3.9 us
    dot_general x3, matrix products, inverse_dft(): lax.dot_general(spec * weight, dft, (((1,), (1,)), ((), ())), precision=T...  3.86 us
    dot_general x3, matrix products, forward_dft(): jnp.dot(signal.astype(jnp.float32), dft, precision=TRANSFORM_PRECISION)  3.23 us
    unnamed x69, local copies, waits for them, and re-layouts  2.69 us
    dot_general x1, matrix products, per_device(): jnp.einsum('rd,cd->rc', cotangent, out_proj, preferred_element_type=jnp.f...  2.48 us
  transfers between devices with their start and end apart: 18, of which 8 were waited for; matrix products, arithmetic and copies ran while one was open for 26% of the time, Pallas kernels for 0%

profile of v12, /device:TPU:0, one launch (start us, length us, event | category | flops | bytes accessed | tf_op | source)
XLA Modules:
  0.0 73.5 jit_solution(13324982917106557795)
XLA Ops:
  0.6 0.8 %slice_add_fusion.1 = s32[3]{0:T(128)S(1)} fusion(s32[128]{0:T(128)} %param.17), kind=kLoop, calls=%fused_computation.240 | loop fusion | flops 3 | bytes 24 | tf_op jit(solution)/shard_map/add | solution.py:190
  1.4 4.9 %collective-permute-start = (s32[3]{0:T(128)S(1)}, s32[3]{0:T(128)S(1)}, u32[]{:S(2)}, u32[]{:S(2)}) collective-permute-start(s32[3]{0:T(128)S(1)} %slice_add_fusion.1), channel_id=1, source_target_pairs={{0,4},{4,8},{8,12},{1,5},{5,9},{9,13},{2,6},{6,10},{10,14},{3,7},{... | collective-permute-start | bytes 44 | tf_op jit(solution)/shard_map/ppermute | solution.py:17
  6.4 2.5 %fusion.136 = f32[128,2048]{1,0:T(8,128)S(1)} fusion(bf16[128,512]{1,0:T(8,128)(2,1)} %param.23, bf16[2048,512]{1,0:T(8,128)(2,1)} %param.22), kind=kOutput, calls=%fused_computation.250 | convolution fusion | flops 268435456 | bytes 3276800 | tf_op jit(solution)/shard_map/rd,cd->rc/dot_general | solution.py:219
  8.9 0.8 %select_select_fusion = f32[128,512]{1,0:T(8,128)} fusion(f32[128,2048]{1,0:T(8,128)S(1)} %fusion.136, pred[]{:T(512)S(6)} %eq.120, pred[]{:T(512)S(6)} %eq.119, pred[]{:T(512)S(6)} %eq.118), kind=kLoop, calls=%fused_computation.119 | loop fusion | flops 196608 | bytes 1310723 | tf_op jit(solution)/shard_map/jit(_where)/select_n | solution.py:76
  9.7 0.7 collective-permute-start.3
  10.3 0.9 %select_select_fusion.2 = (f32[128,512]{1,0:T(8,128)}, f32[128,512]{1,0:T(8,128)}) fusion(f32[128,2048]{1,0:T(8,128)S(1)} %fusion.136, pred[]{:T(512)S(6)} %eq.114, pred[]{:T(512)S(6)} %eq.113, pred[]{:T(512)S(6)} %eq.112, pred[]{:T(512)S(6)} %eq.117, pred[]{:T(512)S(6)} %eq.116, pred[]{:T(512)S(6)} %eq.115), kind=kLoop, calls=%fused_computation.121 | loop fusion | flops 393216 | bytes 1572870 | tf_op jit(solution)/shard_map/jit(_where)/select_n | solution.py:76
  11.2 1.0 %collective-permute-start.1 = (f32[128,512]{1,0:T(8,128)}, f32[128,512]{1,0:T(8,128)}, u32[]{:S(2)}, u32[]{:S(2)}) collective-permute-start(f32[128,512]{1,0:T(8,128)} %get-tuple-element.54), channel_id=1, source_target_pairs={{0,1},{1,0},{2,3},{3,2},{4,5},{5,4},{6,7},{7,6},{8,9},{9,8},{10,11... | collective-permute-start | bytes 786440 | tf_op jit(solution)/shard_map/ppermute | solution.py:64
  12.2 0.5 collective-permute-start.2
  13.2 0.6 fusion.103
  14.3 2.1 %fusion.22 = f32[256,1024]{1,0:T(8,128)} fusion(f32[512,1024]{1,0:T(8,128)S(1)} %bitcast.165, f32[128,512]{1,0:T(8,128)S(1)} %maximum_select_fusion, f32[128,512]{1,0:T(8,128)S(1)} %bitcast.173), kind=kOutput, calls=%fused_computation.41 | convolution fusion | flops 805437440 | bytes 3670016 | tf_op jit(solution)/shard_map/dot_general | solution.py:133
  16.6 0.5 copy-done.25
  17.7 3.9 %convolution_bitcast_fusion.2 = f32[3,512,128]{1,2,0:T(8,128)S(1)} fusion(bf16[2048,3,512]{2,0,1:T(8,128)(2,1)} %param.20, f32[128,2048]{1,0:T(8,128)S(1)} %get-tuple-element.90, f32[2048]{0:T(1024)S(1)} %copy-done.14, f32[128]{0:T(128)S(1)} %add_rsqrt_fusion), kind=kOutput, calls=%fused_computation.6 | convolution fusion | flops 806092800 | bytes 8135168 | tf_op jit(solution)/shard_map/dr,dmc->mcr/dot_general | solution.py:208
  21.7 0.7 copy-done.13
  22.4 1.9 %collective-permute-done.2 = f32[128,512]{1,0:T(8,128)} collective-permute-done((f32[128,512]{1,0:T(8,128)}, f32[128,512]{1,0:T(8,128)}, u32[]{:S(2)}, u32[]{:S(2)}) %collective-permute-start.2) | collective-permute-done | bytes 262176 | tf_op jit(solution)/shard_map/ppermute | solution.py:64
  24.2 1.3 %fusion.61 = (bf16[1,512,128]{1,2,0:T(8,128)(2,1)S(1)}, f32[128,512]{1,0:T(8,128)S(1)}) fusion(f32[3,512,128]{1,2,0:T(8,128)S(1)} %convolution_bitcast_fusion.2, f32[128,512]{1,0:T(8,128)} %copy-done.13, f32[128,512]{1,0:T(8,128)} %collective-permute-done.2, f32[128,512]{1,0:T(8,128)} %collective-permute-done.1, f32[128,2048]{1,0:T(8,128)S(1)} %copy-done.2, ...), kind=kLoop, calls=%fused_computation.134 | loop fusion | flops 589824 | bytes 2490371 | tf_op jit(solution)/shard_map/stack | solution.py:229
  25.6 0.7 select_select_fusion.16
  26.3 1.6 %collective-permute-start.6 = (bf16[2,128,128]{1,2,0:T(8,128)(2,1)}, bf16[2,128,128]{1,2,0:T(8,128)(2,1)}, u32[]{:S(2)}, u32[]{:S(2)}) collective-permute-start(bf16[2,128,128]{1,2,0:T(8,128)(2,1)} %get-tuple-element.38), channel_id=1, source_target_pairs={{0,4},{4,0},{8,12},{12,8},{1,5},{5,1},{9,13},{13,9},{2,6},{6,2},{1... | collective-permute-start | bytes 196616 | tf_op jit(solution)/shard_map/ppermute | solution.py:64
  27.8 0.7 select_select_fusion.17
  28.5 1.6 %collective-permute-start.5 = (bf16[2,128,128]{1,2,0:T(8,128)(2,1)}, bf16[2,128,128]{1,2,0:T(8,128)(2,1)}, u32[]{:S(2)}, u32[]{:S(2)}) collective-permute-start(bf16[2,128,128]{1,2,0:T(8,128)(2,1)} %get-tuple-element.76), channel_id=1, source_target_pairs={{0,8},{4,12},{8,0},{12,4},{1,9},{5,13},{9,1},{13,5},{2,10},{6,14},... | collective-permute-start | bytes 196616 | tf_op jit(solution)/shard_map/ppermute | solution.py:64
  30.1 1.3 %collective-permute-start.4 = (bf16[2,128,128]{1,2,0:T(8,128)(2,1)}, bf16[2,128,128]{1,2,0:T(8,128)(2,1)}, u32[]{:S(2)}, u32[]{:S(2)}) collective-permute-start(bf16[2,128,128]{1,2,0:T(8,128)(2,1)} %get-tuple-element.77), channel_id=1, source_target_pairs={{0,12},{4,8},{8,4},{12,0},{1,13},{5,9},{9,5},{13,1},{2,14},{6,10},... | collective-permute-start | bytes 196616 | tf_op jit(solution)/shard_map/ppermute | solution.py:64
  31.5 0.9 %fusion.21 = f32[128,1024]{1,0:T(8,128)} fusion(f32[256,1024]{1,0:T(8,128)S(1)} %copy-done.6, f32[1024]{0:T(1024)S(1)} %copy-done.27), kind=kLoop, calls=%fused_computation.40 | loop fusion | flops 262144 | bytes 1576960 | tf_op jit(solution)/shard_map/add | solution.py:226
  32.4 4.6 %collective-permute-done.5 = bf16[2,128,128]{1,2,0:T(8,128)(2,1)} collective-permute-done((bf16[2,128,128]{1,2,0:T(8,128)(2,1)}, bf16[2,128,128]{1,2,0:T(8,128)(2,1)}, u32[]{:S(2)}, u32[]{:S(2)}) %collective-permute-start.5) | collective-permute-done | bytes 65568 | tf_op jit(solution)/shard_map/ppermute | solution.py:64
  37.0 0.9 %select_select_fusion.13 = (bf16[2,128,128]{1,2,0:T(8,128)(2,1)S(1)}, bf16[2,128,128]{1,2,0:T(8,128)(2,1)S(1)}, bf16[2,128,128]{1,2,0:T(8,128)(2,1)S(1)}) fusion(bf16[2,128,128]{1,2,0:T(8,128)(2,1)} %collective-permute-done.4, bf16[2,128,128]{1,2,0:T(8,128)(2,1)} %collective-permute-done.5, bf16[2,128,128]{1,2,0:T(8,128)(2,1)} %collective-permute-done.6, ...), kind=kLoop, calls=%fused_computation.196 | loop fusion | flops 294912 | bytes 458761 | tf_op jit(solution)/shard_map/jit(_where)/select_n | solution.py:127
  38.0 0.6 fusion.65
  38.6 0.6 fusion.66
  40.5 1.0 %fusion.8 = bf16[1,128,512]{1,2,0:T(8,128)(2,1)S(1)} fusion(f32[512,1024]{1,0:T(8,128)S(1)} %bitcast.168, f32[128,512]{1,0:T(8,128)S(1)} %get-tuple-element.56, f32[128,512]{1,0:T(8,128)S(1)} %get-tuple-element.57, f32[1024]{0:T(1024)S(1)} %copy-done.16), kind=kOutput, calls=%fused_computation.17 | convolution fusion | flops 402980864 | bytes 2756608 | tf_op jit(solution)/shard_map/dot_general | solution.py:141
  41.6 1.0 %fusion.9 = bf16[1,128,512]{1,2,0:T(8,128)(2,1)S(1)} fusion(f32[512,1024]{1,0:T(8,128)S(1)} %bitcast.169, f32[128,512]{1,0:T(8,128)S(1)} %get-tuple-element.87, f32[128,512]{1,0:T(8,128)S(1)} %get-tuple-element.88, f32[1024]{0:T(1024)S(1)} %copy-done.16), kind=kOutput, calls=%fused_computation.18 | convolution fusion | flops 402980864 | bytes 2756608 | tf_op jit(solution)/shard_map/dot_general | solution.py:141
  42.6 2.3 %collective-permute-start.9 = (bf16[2,128,128]{1,2,0:T(8,128)(2,1)S(1)}, bf16[2,128,128]{1,2,0:T(8,128)(2,1)S(1)}, u32[]{:S(2)}, u32[]{:S(2)}) collective-permute-start(bf16[2,128,128]{1,2,0:T(8,128)(2,1)S(1)} %get-tuple-element.31), channel_id=1, source_target_pairs={{0,4},{4,0},{8,12},{12,8},{1,5},{5,1},{9,13},{13,9},{2,6},{6,2},{1... | collective-permute-start | bytes 196616 | tf_op jit(solution)/shard_map/ppermute | solution.py:64
  45.0 1.6 %collective-permute-start.8 = (bf16[2,128,128]{1,2,0:T(8,128)(2,1)S(1)}, bf16[2,128,128]{1,2,0:T(8,128)(2,1)S(1)}, u32[]{:S(2)}, u32[]{:S(2)}) collective-permute-start(bf16[2,128,128]{1,2,0:T(8,128)(2,1)S(1)} %get-tuple-element.67), channel_id=1, source_target_pairs={{0,8},{4,12},{8,0},{12,4},{1,9},{5,13},{9,1},{13,5},{2,10},{6,14},... | collective-permute-start | bytes 196616 | tf_op jit(solution)/shard_map/ppermute | solution.py:64
  46.5 1.0 %collective-permute-start.7 = (bf16[2,128,128]{1,2,0:T(8,128)(2,1)S(1)}, bf16[2,128,128]{1,2,0:T(8,128)(2,1)S(1)}, u32[]{:S(2)}, u32[]{:S(2)}) collective-permute-start(bf16[2,128,128]{1,2,0:T(8,128)(2,1)S(1)} %get-tuple-element.68), channel_id=1, source_target_pairs={{0,12},{4,8},{8,4},{12,0},{1,13},{5,9},{9,5},{13,1},{2,14},{6,10},... | collective-permute-start | bytes 196616 | tf_op jit(solution)/shard_map/ppermute | solution.py:64
  47.8 4.2 %collective-permute-done.8 = bf16[2,128,128]{1,2,0:T(8,128)(2,1)S(1)} collective-permute-done((bf16[2,128,128]{1,2,0:T(8,128)(2,1)S(1)}, bf16[2,128,128]{1,2,0:T(8,128)(2,1)S(1)}, u32[]{:S(2)}, u32[]{:S(2)}) %collective-permute-start.8) | collective-permute-done | bytes 65568 | tf_op jit(solution)/shard_map/ppermute | solution.py:64
  52.0 0.7 collective-permute-done.7
  53.0 1.3 %fusion.3 = f32[128]{0:T(128)S(1)} fusion(f32[3,512,128]{1,2,0:T(8,128)S(1)} %copy-done.4, bf16[2048,3,512]{2,0,1:T(8,128)(2,1)S(1)} %bitcast.172, f32[128,2048]{1,0:T(8,128)S(1)} %get-tuple-element.90, f32[2048]{0:T(1024)S(1)} %copy-done.15, f32[128]{0:T(128)S(1)} %copy-done.22, bf16[1,512,128]{1,2,0:T(8,128)(2,1)S(1)} %get-tuple-element.53, ...), kind=kOutput, calls=%fused_computation.9 | convolution fusion | flops 808058752 | bytes 8528896 | tf_op jit(solution)/shard_map/dr,dmc->mcr/dot_general | solution.py:210
  54.3 2.2 %fusion.10 = (f32[2048]{0:T(1024)S(1)}, f32[128,2048,1]{1,0,2:T(8,128)S(1)}) fusion(f32[128,2048]{1,0:T(8,128)S(1)} %get-tuple-element.90, f32[128]{0:T(128)S(1)} %copy-done.22, bf16[2048,3,512]{2,0,1:T(8,128)(2,1)S(1)} %bitcast.172, bf16[1,512,128]{1,2,0:T(8,128)(2,1)S(1)} %get-tuple-element.53, bf16[1,512,128]{1,2,0:T(8,128)(2,1)S(1)} %get-tuple-element.52, ...), kind=kOutput, calls=%fused_computation.20 | convolution fusion | flops 806483968 | bytes 8790528 | tf_op jit(solution)/shard_map/mcr,dmc->rd/dot_general | solution.py:262
  56.5 1.2 %collective-permute-start.16 = (bf16[1,512,128]{1,2,0:T(8,128)(2,1)S(1)}, bf16[1,512,128]{1,2,0:T(8,128)(2,1)S(1)}, u32[]{:S(2)}, u32[]{:S(2)}) collective-permute-start(bf16[1,512,128]{1,2,0:T(8,128)(2,1)S(1)} %get-tuple-element.51), channel_id=1, source_target_pairs={{0,2},{2,0},{1,3},{3,1},{4,6},{6,4},{5,7},{7,5},{8,10},{10,8},{9,1... | collective-permute-start | bytes 393224 | tf_op jit(solution)/shard_map/ppermute | solution.py:47
  57.7 0.6 convolution_multiply_fusion.1
  58.3 0.7 fusion
  59.2 1.1 %collective-permute-start.11 = (f32[21,512]{1,0:T(8,128)S(1)}, f32[21,512]{1,0:T(8,128)S(1)}, u32[]{:S(2)}, u32[]{:S(2)}) collective-permute-start(f32[21,512]{1,0:T(8,128)S(1)} %get-tuple-element.78), channel_id=1, source_target_pairs={{0,2},{1,3},{2,0},{3,1},{4,6},{5,7},{6,4},{7,5},{8,10},{9,11},{10,... | collective-permute-start | bytes 129032 | tf_op jit(solution)/shard_map/ppermute | solution.py:64
  60.3 0.8 %collective-permute-start.12 = (f32[21,512]{1,0:T(8,128)S(1)}, f32[21,512]{1,0:T(8,128)S(1)}, u32[]{:S(2)}, u32[]{:S(2)}) collective-permute-start(f32[21,512]{1,0:T(8,128)S(1)} %get-tuple-element.79), channel_id=1, source_target_pairs={{0,3},{1,2},{2,1},{3,0},{4,7},{5,6},{6,5},{7,4},{8,11},{9,10},{10,... | collective-permute-start | bytes 129032 | tf_op jit(solution)/shard_map/ppermute | solution.py:64
  61.1 0.6 collective-permute-done.16
  61.8 1.9 %fusion.30 = f32[128,512]{1,0:T(8,128)} fusion(f32[512,1024]{1,0:T(8,128)S(1)} %bitcast.170, f32[128,512]{1,0:T(8,128)S(1)} %get-tuple-element.59, f32[128,512]{1,0:T(8,128)S(1)} %get-tuple-element.58, f32[1024]{0:T(1024)S(1)} %copy-done.16), kind=kOutput, calls=%fused_computation.52 | convolution fusion | flops 402915328 | bytes 2887680 | tf_op jit(solution)/shard_map/dot_general | solution.py:141
  63.7 0.5 collective-permute-done.12
  64.2 2.5 %collective-permute-start.15 = (f32[21,512]{1,0:T(8,128)S(1)}, f32[21,512]{1,0:T(8,128)S(1)}, u32[]{:S(2)}, u32[]{:S(2)}) collective-permute-start(f32[21,512]{1,0:T(8,128)S(1)} %pad_add_fusion), channel_id=1, source_target_pairs={{0,12},{4,8},{8,4},{12,0},{1,13},{5,9},{9,5},{13,1},{2,14},{6,10},... | collective-permute-start | bytes 129032 | tf_op jit(solution)/shard_map/ppermute | solution.py:64
  67.0 1.6 %collective-permute-start.13 = (f32[21,512]{1,0:T(8,128)S(1)}, f32[21,512]{1,0:T(8,128)S(1)}, u32[]{:S(2)}, u32[]{:S(2)}) collective-permute-start(f32[21,512]{1,0:T(8,128)S(1)} %pad_add_fusion), channel_id=1, source_target_pairs={{0,4},{4,0},{8,12},{12,8},{1,5},{5,1},{9,13},{13,9},{2,6},{6,2},{1... | collective-permute-start | bytes 129032 | tf_op jit(solution)/shard_map/ppermute | solution.py:64
  69.4 0.9 %fusion.7 = bf16[128,512]{1,0:T(8,128)(2,1)} fusion(f32[128,512]{1,0:T(8,128)S(1)} %fusion.33, f32[128,512]{1,0:T(8,128)S(1)} %fusion.35, f32[128,512]{1,0:T(8,128)S(1)} %fusion.37, bf16[2048,512]{1,0:T(8,128)(2,1)S(1)} %copy-done.7, f32[128,2048]{1,0:T(8,128)S(1)} %get-tuple-element.90, s32[]{:T(128)S(6)} %select_n.769, ...), kind=kOutput, calls=%fused_computation.16 | convolution fusion | flops 67633152 | bytes 2228231 | tf_op jit(solution)/shard_map/cr,cd->rd/dot_general | solution.py:247
  70.5 1.8 %collective-permute-done.14 = f32[21,512]{1,0:T(8,128)S(1)} collective-permute-done((f32[21,512]{1,0:T(8,128)S(1)}, f32[21,512]{1,0:T(8,128)S(1)}, u32[]{:S(2)}, u32[]{:S(2)}) %collective-permute-start.14) | collective-permute-done | bytes 43040 | tf_op jit(solution)/shard_map/ppermute | solution.py:64
  72.3 0.6 slice.290
  72.9 0.6 copy.28
  (125 shorter events, 5.0 us)
Async XLA Ops:
  0.6 16.5 %copy-start = (bf16[4,5,2048]{2,0,1:T(4,128)(2,1)S(1)}, bf16[4,5,2048]{2,0,1:T(4,128)(2,1)}, u32[]{:S(2)}) copy-start(bf16[4,5,2048]{2,0,1:T(4,128)(2,1)} %param.18) | copy-start | bytes 245764
  1.4 15.0 %collective-permute-start = (s32[3]{0:T(128)S(1)}, s32[3]{0:T(128)S(1)}, u32[]{:S(2)}, u32[]{:S(2)}) collective-permute-start(s32[3]{0:T(128)S(1)} %slice_add_fusion.1), channel_id=1, source_target_pairs={{0,4},{4,8},{8,12},{1,5},{5,9},{9,13},{2,6},{6,10},{10,14},{3,7},{... | collective-permute-start | bytes 44 | tf_op jit(solution)/shard_map/ppermute | solution.py:17
  8.9 5.0 %copy-start.1 = (f32[128,2048]{1,0:T(8,128)}, f32[128,2048]{1,0:T(8,128)S(1)}, u32[]{:S(2)}) copy-start(f32[128,2048]{1,0:T(8,128)S(1)} %fusion.136) | copy-start | bytes 3145732
  8.9 3.9 %copy-start.31 = (s32[128]{0:T(128)S(1)}, s32[128]{0:T(128)}, u32[]{:S(2)}) copy-start(s32[128]{0:T(128)} %param.17) | copy-start | bytes 1540
  8.9 3.9 %copy-start.8 = (f32[1,1,128,512]{3,2,1,0:T(8,128)S(1)}, f32[1,1,128,512]{3,2,1,0:T(8,128)}, u32[]{:S(2)}) copy-start(f32[1,1,128,512]{3,2,1,0:T(8,128)} %param.21) | copy-start | bytes 786436
  9.7 12.0 %collective-permute-start.3 = (f32[128,512]{1,0:T(8,128)}, f32[128,512]{1,0:T(8,128)S(1)}, u32[]{:S(2)}, u32[]{:S(2)}) collective-permute-start(f32[128,512]{1,0:T(8,128)} %select_select_fusion), channel_id=1, source_target_pairs={{0,3},{1,2},{2,1},{3,0},{4,7},{5,6},{6,5},{7,4},{8,11},{9,10},{10,... | collective-permute-start | bytes 786440 | tf_op jit(solution)/shard_map/ppermute | solution.py:64
  11.2 2.9 %copy-start.28 = (pred[128]{0:T(512)(128)(4,1)S(1)}, pred[128]{0:T(512)(128)(4,1)}, u32[]{:S(2)}) copy-start(pred[128]{0:T(512)(128)(4,1)} %constant.96) | copy-start | bytes 388
  11.2 10.4 %collective-permute-start.1 = (f32[128,512]{1,0:T(8,128)}, f32[128,512]{1,0:T(8,128)}, u32[]{:S(2)}, u32[]{:S(2)}) collective-permute-start(f32[128,512]{1,0:T(8,128)} %get-tuple-element.54), channel_id=1, source_target_pairs={{0,1},{1,0},{2,3},{3,2},{4,5},{5,4},{6,7},{7,6},{8,9},{9,8},{10,11... | collective-permute-start | bytes 786440 | tf_op jit(solution)/shard_map/ppermute | solution.py:64
  12.2 12.0 %collective-permute-start.2 = (f32[128,512]{1,0:T(8,128)}, f32[128,512]{1,0:T(8,128)}, u32[]{:S(2)}, u32[]{:S(2)}) collective-permute-start(f32[128,512]{1,0:T(8,128)} %get-tuple-element.55), channel_id=1, source_target_pairs={{0,2},{1,3},{2,0},{3,1},{4,6},{5,7},{6,4},{7,5},{8,10},{9,11},{10,... | collective-permute-start | bytes 786440 | tf_op jit(solution)/shard_map/ppermute | solution.py:64
  12.7 3.8 %copy-start.23 = (pred[128,5]{0,1:T(8,128)(4,1)}, pred[128,5]{0,1:T(8,128)(4,1)S(1)}, u32[]{:S(2)}) copy-start(pred[128,5]{0,1:T(8,128)(4,1)S(1)} %iota_compare_fusion.5) | copy-start | bytes 1924
  14.3 3.4 %copy-start.14 = (f32[2048]{0:T(1024)S(1)}, f32[2048]{0:T(1024)}, u32[]{:S(2)}) copy-start(f32[2048]{0:T(1024)} %param.19) | copy-start | bytes 24580
  17.6 3.9 %copy-start.21 = (f32[128]{0:T(128)}, f32[128]{0:T(128)S(1)}, u32[]{:S(2)}) copy-start(f32[128]{0:T(128)S(1)} %add_rsqrt_fusion) | copy-start | bytes 1540
  17.6 6.6 %copy-start.2 = (f32[128,2048]{1,0:T(8,128)S(1)}, f32[128,2048]{1,0:T(8,128)}, u32[]{:S(2)}) copy-start(f32[128,2048]{1,0:T(8,128)} %copy-done.1) | copy-start | bytes 3145732
  21.6 4.0 %copy-start.3 = (f32[3,512,128]{1,2,0:T(8,128)}, f32[3,512,128]{1,2,0:T(8,128)S(1)}, u32[]{:S(2)}) copy-start(f32[3,512,128]{1,2,0:T(8,128)S(1)} %convolution_bitcast_fusion.2) | copy-start | bytes 2359300
  21.6 9.9 %copy-start.6 = (f32[256,1024]{1,0:T(8,128)S(1)}, f32[256,1024]{1,0:T(8,128)}, u32[]{:S(2)}) copy-start(f32[256,1024]{1,0:T(8,128)} %fusion.22) | copy-start | bytes 3145732
  21.6 9.9 %copy-start.27 = (f32[1024]{0:T(1024)S(1)}, f32[1024]{0:T(1024)}, u32[]{:S(2)}) copy-start(f32[1024]{0:T(1024)} %constant.97) | copy-start | bytes 12292
  21.7 0.7 copy-start.13
  26.3 1.6 %copy-start.9 = (bf16[2,128,128]{1,2,0:T(8,128)(2,1)}, bf16[2,128,128]{1,2,0:T(8,128)(2,1)S(1)}, u32[]{:S(2)}) copy-start(bf16[2,128,128]{1,2,0:T(8,128)(2,1)S(1)} %get-tuple-element.40) | copy-start | bytes 196612
  26.3 2.2 %copy-start.10 = (bf16[2,128,128]{1,2,0:T(8,128)(2,1)}, bf16[2,128,128]{1,2,0:T(8,128)(2,1)S(1)}, u32[]{:S(2)}) copy-start(bf16[2,128,128]{1,2,0:T(8,128)(2,1)S(1)} %get-tuple-element.41) | copy-start | bytes 196612
  26.3 2.2 %copy-start.11 = (bf16[2,128,128]{1,2,0:T(8,128)(2,1)}, bf16[2,128,128]{1,2,0:T(8,128)(2,1)S(1)}, u32[]{:S(2)}) copy-start(bf16[2,128,128]{1,2,0:T(8,128)(2,1)S(1)} %get-tuple-element.42) | copy-start | bytes 196612
  26.3 6.1 %collective-permute-start.6 = (bf16[2,128,128]{1,2,0:T(8,128)(2,1)}, bf16[2,128,128]{1,2,0:T(8,128)(2,1)}, u32[]{:S(2)}, u32[]{:S(2)}) collective-permute-start(bf16[2,128,128]{1,2,0:T(8,128)(2,1)} %get-tuple-element.38), channel_id=1, source_target_pairs={{0,4},{4,0},{8,12},{12,8},{1,5},{5,1},{9,13},{13,9},{2,6},{6,2},{1... | collective-permute-start | bytes 196616 | tf_op jit(solution)/shard_map/ppermute | solution.py:64
  28.5 8.5 %collective-permute-start.5 = (bf16[2,128,128]{1,2,0:T(8,128)(2,1)}, bf16[2,128,128]{1,2,0:T(8,128)(2,1)}, u32[]{:S(2)}, u32[]{:S(2)}) collective-permute-start(bf16[2,128,128]{1,2,0:T(8,128)(2,1)} %get-tuple-element.76), channel_id=1, source_target_pairs={{0,8},{4,12},{8,0},{12,4},{1,9},{5,13},{9,1},{13,5},{2,10},{6,14},... | collective-permute-start | bytes 196616 | tf_op jit(solution)/shard_map/ppermute | solution.py:64
  30.1 6.8 %collective-permute-start.4 = (bf16[2,128,128]{1,2,0:T(8,128)(2,1)}, bf16[2,128,128]{1,2,0:T(8,128)(2,1)}, u32[]{:S(2)}, u32[]{:S(2)}) collective-permute-start(bf16[2,128,128]{1,2,0:T(8,128)(2,1)} %get-tuple-element.77), channel_id=1, source_target_pairs={{0,12},{4,8},{8,4},{12,0},{1,13},{5,9},{9,5},{13,1},{2,14},{6,10},... | collective-permute-start | bytes 196616 | tf_op jit(solution)/shard_map/ppermute | solution.py:64
  38.0 1.1 %copy-start.5 = (f32[128,1024]{1,0:T(8,128)S(1)}, f32[128,1024]{1,0:T(8,128)}, u32[]{:S(2)}) copy-start(f32[128,1024]{1,0:T(8,128)} %fusion.21) | copy-start | bytes 1572868
  38.0 1.1 %copy-start.30 = (pred[512]{0:T(512)(128)(4,1)S(1)}, pred[512]{0:T(512)(128)(4,1)}, u32[]{:S(2)}) copy-start(pred[512]{0:T(512)(128)(4,1)} %constant.95) | copy-start | bytes 1540
  39.8 0.7 copy-start.16
  39.9 13.1 %slice-start = ((s8[6291456]{0:T(1024)(128)(4,1)}), s8[4194304]{0:T(1024)(128)(4,1)S(1)}, s32[]{:S(2)}) async-start(s8[6291456]{0:T(1024)(128)(4,1)} %bitcast.171), calls=%async_computation | async-start | bytes 8388608
  41.5 6.0 %copy-start.12 = (bf16[128,512]{1,0:T(8,128)(2,1)S(1)}, bf16[128,512]{1,0:T(8,128)(2,1)}, u32[]{:S(2)}) copy-start(bf16[128,512]{1,0:T(8,128)(2,1)} %param.23) | copy-start | bytes 393220
  41.5 6.0 %copy-start.18 = (pred[128,5]{0,1:T(8,128)(4,1)S(1)}, pred[128,5]{0,1:T(8,128)(4,1)}, u32[]{:S(2)}) copy-start(pred[128,5]{0,1:T(8,128)(4,1)} %copy-done.17) | copy-start | bytes 1924
  41.5 6.0 %copy-start.20 = (pred[128,5]{0,1:T(8,128)(4,1)S(1)}, pred[128,5]{0,1:T(8,128)(4,1)}, u32[]{:S(2)}) copy-start(pred[128,5]{0,1:T(8,128)(4,1)} %copy-done.19) | copy-start | bytes 1924
  41.5 6.0 %copy-start.24 = (pred[128,5]{0,1:T(8,128)(4,1)S(1)}, pred[128,5]{0,1:T(8,128)(4,1)}, u32[]{:S(2)}) copy-start(pred[128,5]{0,1:T(8,128)(4,1)} %copy-done.23) | copy-start | bytes 1924
  41.5 6.0 %copy-start.26 = (pred[128,5]{0,1:T(8,128)(4,1)S(1)}, pred[128,5]{0,1:T(8,128)(4,1)}, u32[]{:S(2)}) copy-start(pred[128,5]{0,1:T(8,128)(4,1)} %copy-done.25) | copy-start | bytes 1924
  41.6 11.3 %copy-start.4 = (f32[3,512,128]{1,2,0:T(8,128)S(1)}, f32[3,512,128]{1,2,0:T(8,128)}, u32[]{:S(2)}) copy-start(f32[3,512,128]{1,2,0:T(8,128)} %copy-done.3) | copy-start | bytes 2359300
  41.6 11.4 %slice-start.1 = ((s8[6291456]{0:T(1024)(128)(4,1)}), s8[2097152]{0:T(1024)(128)(4,1)S(1)}, s32[]{:S(2)}) async-start(s8[6291456]{0:T(1024)(128)(4,1)} %bitcast.171), calls=%async_computation.1 | async-start | bytes 4194304
  42.6 5.1 %collective-permute-start.9 = (bf16[2,128,128]{1,2,0:T(8,128)(2,1)S(1)}, bf16[2,128,128]{1,2,0:T(8,128)(2,1)S(1)}, u32[]{:S(2)}, u32[]{:S(2)}) collective-permute-start(bf16[2,128,128]{1,2,0:T(8,128)(2,1)S(1)} %get-tuple-element.31), channel_id=1, source_target_pairs={{0,4},{4,0},{8,12},{12,8},{1,5},{5,1},{9,13},{13,9},{2,6},{6,2},{1... | collective-permute-start | bytes 196616 | tf_op jit(solution)/shard_map/ppermute | solution.py:64
  44.9 8.1 %copy-start.15 = (f32[2048]{0:T(1024)S(1)}, f32[2048]{0:T(1024)}, u32[]{:S(2)}) copy-start(f32[2048]{0:T(1024)} %param.19) | copy-start | bytes 24580
  45.0 8.1 %copy-start.22 = (f32[128]{0:T(128)S(1)}, f32[128]{0:T(128)}, u32[]{:S(2)}) copy-start(f32[128]{0:T(128)} %copy-done.21) | copy-start | bytes 1540
  45.0 7.0 %collective-permute-start.8 = (bf16[2,128,128]{1,2,0:T(8,128)(2,1)S(1)}, bf16[2,128,128]{1,2,0:T(8,128)(2,1)S(1)}, u32[]{:S(2)}, u32[]{:S(2)}) collective-permute-start(bf16[2,128,128]{1,2,0:T(8,128)(2,1)S(1)} %get-tuple-element.67), channel_id=1, source_target_pairs={{0,8},{4,12},{8,0},{12,4},{1,9},{5,13},{9,1},{13,5},{2,10},{6,14},... | collective-permute-start | bytes 196616 | tf_op jit(solution)/shard_map/ppermute | solution.py:64
  46.5 6.2 %collective-permute-start.7 = (bf16[2,128,128]{1,2,0:T(8,128)(2,1)S(1)}, bf16[2,128,128]{1,2,0:T(8,128)(2,1)S(1)}, u32[]{:S(2)}, u32[]{:S(2)}) collective-permute-start(bf16[2,128,128]{1,2,0:T(8,128)(2,1)S(1)} %get-tuple-element.68), channel_id=1, source_target_pairs={{0,12},{4,8},{8,4},{12,0},{1,13},{5,9},{9,5},{13,1},{2,14},{6,10},... | collective-permute-start | bytes 196616 | tf_op jit(solution)/shard_map/ppermute | solution.py:64
  56.5 5.2 %collective-permute-start.16 = (bf16[1,512,128]{1,2,0:T(8,128)(2,1)S(1)}, bf16[1,512,128]{1,2,0:T(8,128)(2,1)S(1)}, u32[]{:S(2)}, u32[]{:S(2)}) collective-permute-start(bf16[1,512,128]{1,2,0:T(8,128)(2,1)S(1)} %get-tuple-element.51), channel_id=1, source_target_pairs={{0,2},{2,0},{1,3},{3,1},{4,6},{6,4},{5,7},{7,5},{8,10},{10,8},{9,1... | collective-permute-start | bytes 393224 | tf_op jit(solution)/shard_map/ppermute | solution.py:47
  59.1 9.6 %copy-start.7 = (bf16[2048,512]{1,0:T(8,128)(2,1)S(1)}, bf16[2048,512]{1,0:T(8,128)(2,1)}, u32[]{:S(2)}) copy-start(bf16[2048,512]{1,0:T(8,128)(2,1)} %param.22) | copy-start | bytes 6291460
  59.1 4.6 %collective-permute-start.10 = (f32[21,512]{1,0:T(8,128)S(1)}, f32[21,512]{1,0:T(8,128)S(1)}, u32[]{:S(2)}, u32[]{:S(2)}) collective-permute-start(f32[21,512]{1,0:T(8,128)S(1)} %get-tuple-element.24), channel_id=1, source_target_pairs={{0,1},{1,0},{2,3},{3,2},{4,5},{5,4},{6,7},{7,6},{8,9},{9,8},{10,11... | collective-permute-start | bytes 129032 | tf_op jit(solution)/shard_map/ppermute | solution.py:64
  59.2 4.5 %collective-permute-start.11 = (f32[21,512]{1,0:T(8,128)S(1)}, f32[21,512]{1,0:T(8,128)S(1)}, u32[]{:S(2)}, u32[]{:S(2)}) collective-permute-start(f32[21,512]{1,0:T(8,128)S(1)} %get-tuple-element.78), channel_id=1, source_target_pairs={{0,2},{1,3},{2,0},{3,1},{4,6},{5,7},{6,4},{7,5},{8,10},{9,11},{10,... | collective-permute-start | bytes 129032 | tf_op jit(solution)/shard_map/ppermute | solution.py:64
  60.3 3.9 %collective-permute-start.12 = (f32[21,512]{1,0:T(8,128)S(1)}, f32[21,512]{1,0:T(8,128)S(1)}, u32[]{:S(2)}, u32[]{:S(2)}) collective-permute-start(f32[21,512]{1,0:T(8,128)S(1)} %get-tuple-element.79), channel_id=1, source_target_pairs={{0,3},{1,2},{2,1},{3,0},{4,7},{5,6},{6,5},{7,4},{8,11},{9,10},{10,... | collective-permute-start | bytes 129032 | tf_op jit(solution)/shard_map/ppermute | solution.py:64
  61.7 6.9 %collective-permute-start.17 = (bf16[2,512,128]{1,2,0:T(8,128)(2,1)S(1)}, bf16[2,512,128]{1,2,0:T(8,128)(2,1)S(1)}, u32[]{:S(2)}, u32[]{:S(2)}) collective-permute-start(bf16[2,512,128]{1,2,0:T(8,128)(2,1)S(1)} %pad_maximum_fusion.4), channel_id=1, source_target_pairs={{0,1},{1,0},{2,3},{3,2},{4,5},{5,4},{6,7},{7,6},{8,9},{9,8},{10,11... | collective-permute-start | bytes 786440 | tf_op jit(solution)/shard_map/ppermute | solution.py:47
  64.2 6.3 %collective-permute-start.15 = (f32[21,512]{1,0:T(8,128)S(1)}, f32[21,512]{1,0:T(8,128)S(1)}, u32[]{:S(2)}, u32[]{:S(2)}) collective-permute-start(f32[21,512]{1,0:T(8,128)S(1)} %pad_add_fusion), channel_id=1, source_target_pairs={{0,12},{4,8},{8,4},{12,0},{1,13},{5,9},{9,5},{13,1},{2,14},{6,10},... | collective-permute-start | bytes 129032 | tf_op jit(solution)/shard_map/ppermute | solution.py:64
  66.7 5.5 %collective-permute-start.14 = (f32[21,512]{1,0:T(8,128)S(1)}, f32[21,512]{1,0:T(8,128)S(1)}, u32[]{:S(2)}, u32[]{:S(2)}) collective-permute-start(f32[21,512]{1,0:T(8,128)S(1)} %pad_add_fusion), channel_id=1, source_target_pairs={{0,8},{4,12},{8,0},{12,4},{1,9},{5,13},{9,1},{13,5},{2,10},{6,14},... | collective-permute-start | bytes 129032 | tf_op jit(solution)/shard_map/ppermute | solution.py:64
  67.0 5.3 %collective-permute-start.13 = (f32[21,512]{1,0:T(8,128)S(1)}, f32[21,512]{1,0:T(8,128)S(1)}, u32[]{:S(2)}, u32[]{:S(2)}) collective-permute-start(f32[21,512]{1,0:T(8,128)S(1)} %pad_add_fusion), channel_id=1, source_target_pairs={{0,4},{4,0},{8,12},{12,8},{1,5},{5,1},{9,13},{13,9},{2,6},{6,2},{1... | collective-permute-start | bytes 129032 | tf_op jit(solution)/shard_map/ppermute | solution.py:64
  (4 other events, 2.4 us)

commit v13 on v10

--- a/solution.py
+++ b/solution.py
@@ -217,10 +217,13 @@
     dft = dft_matrix(length)
     filter_rows = long_filter.reshape(long_filter.shape[2], long_filter.shape[3])
     spec_g = add_conj_flip(forward_dft(filter_rows, dft))
-    ga, gb = halves(spec_g)
     d_conv = (d_gated * query_part).astype(jnp.bfloat16)
     both_cols = all_to_all_seq(jnp.stack([mixed_in, d_conv]), 1, 2)
+    both_cols, (spec_g, dft, unrounded) = lax.optimization_barrier(
+        (both_cols, (spec_g, dft, unrounded))
+    )
     mixed_cols, d_cols = both_cols[0], both_cols[1]
+    ga, gb = halves(spec_g)
     spec_s = forward_dft(mixed_cols, dft)
     sa, sb = halves(spec_s)
     conv_cols = inverse_dft(cmul(ga, gb, sa, sb, False), dft).astype(jnp.bfloat16)

time: 71.6 us -> 71.7 us (level)
  waiting for transfers between devices: 11.7 us -> 10.1 us
  local copies, waits for them, and re-layouts: 4.57 us -> 5.53 us
  other arithmetic: 9.53 us -> 10.3 us
    ppermute x1, starting transfers between devices: 4.04 us -> 5.52 us  [from_behind(): lax.ppermute(value, axis, [(source, source + steps) for source in range(f...]
    add x1 -> x2, other arithmetic: 0.1 us -> 1.37 us  [add_conj_flip(): return jnp.concatenate([a + fa, jnp.where(edge, b + fb, b - fb)], axis=1)]
    ppermute x15, waiting for transfers between devices: 11.2 us -> 10.1 us  [group_exchange(): return lax.ppermute(x, axes, [(i, i ^ offset) for i in range(count)])]
    unnamed x28, local copies, waits for them, and re-layouts: 2.06 us -> 3.11 us
    ppermute x15, starting transfers between devices: 18.6 us -> 17.6 us  [group_exchange(): return lax.ppermute(x, axes, [(i, i ^ offset) for i in range(count)])]
    dot_general x1, matrix products: 1.34 us -> 0.43 us  [per_device(): embedded = jnp.dot(table_t, onehot_t, preferred_element_type=jnp.float32)]
  transfers between devices with their start and end apart: 18 -> 18, of which waited for: 7 -> 7; matrix products, arithmetic and copies ran while one was open for 28% -> 33% of each run, Pallas kernels for 0% -> 0%
where the time goes in v13:
time: 71.7 us; the launch traced here: 71.3 us
  starting transfers between devices  25 us (35%)
  matrix products  19.3 us (27%)
  other arithmetic  10.3 us (14%)
  waiting for transfers between devices  10.1 us (14%)
  local copies, waits for them, and re-layouts  5.53 us (8%)
  between operations  1.11 us (2%)
    ppermute x15, starting transfers between devices, group_exchange(): return lax.ppermute(x, axes, [(i, i ^ offset) for i in range(count)])  17.6 us
    ppermute x15, waiting for transfers between devices, group_exchange(): return lax.ppermute(x, axes, [(i, i ^ offset) for i in range(count)])  10.1 us
    ppermute x1, starting transfers between devices, from_behind(): lax.ppermute(value, axis, [(source, source + steps) for source in range(f...  5.52 us
    dot_general x1, matrix products, per_device(): jnp.einsum('dr,dmc->mcr', hidden, in_proj, preferred_element_type=jnp.flo...  4.02 us
    dot_general x3, matrix products, inverse_dft(): lax.dot_general(spec * weight, dft, (((1,), (1,)), ((), ())), precision=T...  3.87 us
    unnamed x28, local copies, waits for them, and re-layouts  3.11 us
    dot_general x1, matrix products, per_device(): jnp.einsum('rd,cd->rc', cotangent, out_proj, preferred_element_type=jnp.f...  2.48 us
    dot_general x1, matrix products, per_device(): jnp.einsum('mcr,dmc->rd', d_proj, in_proj, preferred_element_type=jnp.flo...  2.16 us
  transfers between devices with their start and end apart: 18, of which 7 were waited for; matrix products, arithmetic and copies ran while one was open for 33% of the time, Pallas kernels for 0%

profile of v13, /device:TPU:0, one launch (start us, length us, event | category | flops | bytes accessed | tf_op | source)
XLA Modules:
  0.0 71.3 jit_solution(12713630377681756840)
XLA Ops:
  0.6 1.3 %slice_add_fusion.2 = s32[3]{0:T(128)} fusion(s32[128]{0:T(128)} %param.17), kind=kLoop, calls=%fused_computation.234 | loop fusion | flops 3 | bytes 24 | tf_op jit(solution)/shard_map/add | solution.py:190
  1.9 5.5 %collective-permute-start = (s32[3]{0:T(128)}, s32[3]{0:T(128)}, u32[]{:S(2)}, u32[]{:S(2)}) collective-permute-start(s32[3]{0:T(128)} %slice_add_fusion.2), channel_id=1, source_target_pairs={{0,4},{4,8},{8,12},{1,5},{5,9},{9,13},{2,6},{6,10},{10,14},{3,7},{... | collective-permute-start | bytes 44 | tf_op jit(solution)/shard_map/ppermute | solution.py:17
  7.4 2.5 %fusion.134 = f32[128,2048]{1,0:T(8,128)S(1)} fusion(bf16[128,512]{1,0:T(8,128)(2,1)} %param.23, bf16[2048,512]{1,0:T(8,128)(2,1)} %param.22), kind=kOutput, calls=%fused_computation.245 | convolution fusion | flops 268435456 | bytes 3276800 | tf_op jit(solution)/shard_map/rd,cd->rc/dot_general | solution.py:215
  9.9 0.8 %select_select_fusion = f32[128,512]{1,0:T(8,128)} fusion(f32[128,2048]{1,0:T(8,128)S(1)} %fusion.134, pred[]{:T(512)S(6)} %eq.120, pred[]{:T(512)S(6)} %eq.119, pred[]{:T(512)S(6)} %eq.118), kind=kLoop, calls=%fused_computation.114 | loop fusion | flops 196608 | bytes 1310723 | tf_op jit(solution)/shard_map/jit(_where)/select_n | solution.py:76
  10.7 0.6 collective-permute-start.3
  11.4 0.9 %select_select_fusion.2 = (f32[128,512]{1,0:T(8,128)}, f32[128,512]{1,0:T(8,128)}) fusion(f32[128,2048]{1,0:T(8,128)S(1)} %fusion.134, pred[]{:T(512)S(6)} %eq.114, pred[]{:T(512)S(6)} %eq.113, pred[]{:T(512)S(6)} %eq.112, pred[]{:T(512)S(6)} %eq.117, pred[]{:T(512)S(6)} %eq.116, pred[]{:T(512)S(6)} %eq.115), kind=kLoop, calls=%fused_computation.116 | loop fusion | flops 393216 | bytes 1572870 | tf_op jit(solution)/shard_map/jit(_where)/select_n | solution.py:76
  12.3 1.0 %collective-permute-start.1 = (f32[128,512]{1,0:T(8,128)}, f32[128,512]{1,0:T(8,128)}, u32[]{:S(2)}, u32[]{:S(2)}) collective-permute-start(f32[128,512]{1,0:T(8,128)} %get-tuple-element.68), channel_id=1, source_target_pairs={{0,1},{1,0},{2,3},{3,2},{4,5},{5,4},{6,7},{7,6},{8,9},{9,8},{10,11... | collective-permute-start | bytes 786440 | tf_op jit(solution)/shard_map/ppermute | solution.py:64
  13.2 0.5 collective-permute-start.2
  14.2 0.6 fusion.100
  15.1 0.7 convolution_bitcast_fusion.2
  15.8 0.8 %copy-done.1 = f32[128,1024]{1,0:T(8,128)} copy-done((f32[128,1024]{1,0:T(8,128)}, f32[128,1024]{1,0:T(8,128)S(1)}, u32[]{:S(2)}) %copy-start.1) | copy-done | bytes 524312
  16.6 1.1 %fusion.132 = (f32[127,1024]{1,0:T(8,128)}, f32[127,1024]{1,0:T(8,128)}) fusion(f32[128,1024]{1,0:T(8,128)S(1)} %convolution_bitcast_fusion.2), kind=kLoop, calls=%fused_computation.243 | loop fusion | bytes 2080768 | tf_op jit(solution)/shard_map/jit(_roll_static)/slice | solution.py:168
  17.7 0.9 %copy.28 = bf16[4,5,2048]{2,1,0:T(8,128)(2,1)S(1)} copy(bf16[4,5,2048]{2,0,1:T(4,128)(2,1)} %param.18) | data formatting | bytes 163840 | tf_op args[1]
  18.6 0.7 reshape.243
  19.3 1.4 %maximum_select_fusion = f32[128,1024]{1,0:T(8,128)S(1)} fusion(f32[1,1024]{1,0:T(1,128)S(1)} %get-tuple-element.77, f32[127,1024]{1,0:T(8,128)} %get-tuple-element.79, f32[127,1024]{1,0:T(8,128)} %get-tuple-element.78, f32[1,1024]{1,0:T(1,128)S(1)} %get-tuple-element.76, pred[128]{0:T(512)(128)(4,1)} %constant.93), kind=kLoop, calls=%fused_computation.38 | loop fusion | flops 393216 | bytes 1572992 | tf_op jit(solution)/shard_map/jit(_where)/select_n | solution.py:169
  20.7 1.1 %slice_add_fusion.1 = (f32[128,512]{1,0:T(8,128)S(1)}, f32[128,512]{1,0:T(8,128)S(1)}) fusion(f32[128,1024]{1,0:T(8,128)S(1)} %maximum_select_fusion, f32[128,1024]{1,0:T(8,128)} %copy-done.1, pred[512]{0:T(512)(128)(4,1)S(1)} %copy-done.7), kind=kLoop, calls=%fused_computation.94 | loop fusion | flops 262144 | bytes 1573376 | tf_op jit(solution)/shard_map/add | solution.py:176
  21.8 0.7 broadcast_add_fusion
  23.2 4.0 %convolution_bitcast_fusion.1 = f32[3,512,128]{1,2,0:T(8,128)S(1)} fusion(bf16[2048,3,512]{2,0,1:T(8,128)(2,1)} %param.20, f32[128,2048]{1,0:T(8,128)S(1)} %get-tuple-element.104, f32[2048]{0:T(1024)S(1)} %copy-done.5, f32[128]{0:T(128)S(1)} %add_rsqrt_fusion), kind=kOutput, calls=%fused_computation.5 | convolution fusion | flops 806092800 | bytes 8135168 | tf_op jit(solution)/shard_map/dr,dmc->mcr/dot_general | solution.py:204
  27.3 1.3 %fusion.55 = (bf16[1,512,128]{1,2,0:T(8,128)(2,1)S(1)}, f32[128,512]{1,0:T(8,128)S(1)}) fusion(f32[3,512,128]{1,2,0:T(8,128)S(1)} %convolution_bitcast_fusion.1, f32[128,512]{1,0:T(8,128)} %collective-permute-done.3, f32[128,512]{1,0:T(8,128)} %collective-permute-done.2, f32[128,512]{1,0:T(8,128)} %collective-permute-done.1, f32[128,2048]{1,0:T(8,128)S(1)} %fusion.134, ...), kind=kLoop, calls=%fused_computation.129 | loop fusion | flops 589824 | bytes 2490371 | tf_op jit(solution)/shard_map/stack | solution.py:221
  28.7 1.1 %collective-permute-start.6 = (bf16[2,128,128]{1,2,0:T(8,128)(2,1)S(1)}, bf16[2,128,128]{1,2,0:T(8,128)(2,1)S(1)}, u32[]{:S(2)}, u32[]{:S(2)}) collective-permute-start(bf16[2,128,128]{1,2,0:T(8,128)(2,1)S(1)} %get-tuple-element.50), channel_id=1, source_target_pairs={{0,4},{4,0},{8,12},{12,8},{1,5},{5,1},{9,13},{13,9},{2,6},{6,2},{1... | collective-permute-start | bytes 196616 | tf_op jit(solution)/shard_map/ppermute | solution.py:64
  29.8 1.1 %collective-permute-start.5 = (bf16[2,128,128]{1,2,0:T(8,128)(2,1)S(1)}, bf16[2,128,128]{1,2,0:T(8,128)(2,1)S(1)}, u32[]{:S(2)}, u32[]{:S(2)}) collective-permute-start(bf16[2,128,128]{1,2,0:T(8,128)(2,1)S(1)} %get-tuple-element.90), channel_id=1, source_target_pairs={{0,8},{4,12},{8,0},{12,4},{1,9},{5,13},{9,1},{13,5},{2,10},{6,14},... | collective-permute-start | bytes 196616 | tf_op jit(solution)/shard_map/ppermute | solution.py:64
  30.9 2.3 %collective-permute-start.4 = (bf16[2,128,128]{1,2,0:T(8,128)(2,1)S(1)}, bf16[2,128,128]{1,2,0:T(8,128)(2,1)S(1)}, u32[]{:S(2)}, u32[]{:S(2)}) collective-permute-start(bf16[2,128,128]{1,2,0:T(8,128)(2,1)S(1)} %get-tuple-element.91), channel_id=1, source_target_pairs={{0,12},{4,8},{8,4},{12,0},{1,13},{5,9},{9,5},{13,1},{2,14},{6,10},... | collective-permute-start | bytes 196616 | tf_op jit(solution)/shard_map/ppermute | solution.py:64
  33.2 1.1 %fusion.1 = f32[3,512,128]{1,2,0:T(8,128)S(1)} fusion(f32[3,512,128]{1,2,0:T(8,128)S(1)} %convolution_bitcast_fusion.1, bf16[2048,3,512]{2,0,1:T(8,128)(2,1)S(1)} %bitcast.160, f32[128,2048]{1,0:T(8,128)S(1)} %get-tuple-element.104, f32[2048]{0:T(1024)S(1)} %copy-done.5, f32[128]{0:T(128)S(1)} %add_rsqrt_fusion), kind=kOutput, calls=%fused_computation.6 | convolution fusion | flops 807075840 | bytes 8921600 | tf_op jit(solution)/shard_map/dr,dmc->mcr/dot_general | solution.py:206
  34.3 3.4 %collective-permute-done.5 = bf16[2,128,128]{1,2,0:T(8,128)(2,1)S(1)} collective-permute-done((bf16[2,128,128]{1,2,0:T(8,128)(2,1)S(1)}, bf16[2,128,128]{1,2,0:T(8,128)(2,1)S(1)}, u32[]{:S(2)}, u32[]{:S(2)}) %collective-permute-start.5) | collective-permute-done | bytes 65568 | tf_op jit(solution)/shard_map/ppermute | solution.py:64
  37.8 0.6 fusion.71
  38.4 0.6 fusion.73
  40.3 1.0 %fusion.6 = bf16[1,128,512]{1,2,0:T(8,128)(2,1)S(1)} fusion(f32[512,1024]{1,0:T(8,128)S(1)} %bitcast.156, f32[128,512]{1,0:T(8,128)S(1)} %get-tuple-element.70, f32[128,512]{1,0:T(8,128)S(1)} %get-tuple-element.71, f32[1024]{0:T(1024)S(1)} %copy-done.6), kind=kOutput, calls=%fused_computation.15 | convolution fusion | flops 402980864 | bytes 2756608 | tf_op jit(solution)/shard_map/dot_general | solution.py:141
  41.3 1.0 %fusion.7 = bf16[1,128,512]{1,2,0:T(8,128)(2,1)S(1)} fusion(f32[512,1024]{1,0:T(8,128)S(1)} %bitcast.157, f32[128,512]{1,0:T(8,128)S(1)} %get-tuple-element.101, f32[128,512]{1,0:T(8,128)S(1)} %get-tuple-element.102, f32[1024]{0:T(1024)S(1)} %copy-done.6), kind=kOutput, calls=%fused_computation.16 | convolution fusion | flops 402980864 | bytes 2756608 | tf_op jit(solution)/shard_map/dot_general | solution.py:141
  42.3 1.3 %collective-permute-start.9 = (bf16[2,128,128]{1,2,0:T(8,128)(2,1)S(1)}, bf16[2,128,128]{1,2,0:T(8,128)(2,1)S(1)}, u32[]{:S(2)}, u32[]{:S(2)}) collective-permute-start(bf16[2,128,128]{1,2,0:T(8,128)(2,1)S(1)} %get-tuple-element.43), channel_id=1, source_target_pairs={{0,4},{4,0},{8,12},{12,8},{1,5},{5,1},{9,13},{13,9},{2,6},{6,2},{1... | collective-permute-start | bytes 196616 | tf_op jit(solution)/shard_map/ppermute | solution.py:64
  43.7 1.7 %collective-permute-start.8 = (bf16[2,128,128]{1,2,0:T(8,128)(2,1)S(1)}, bf16[2,128,128]{1,2,0:T(8,128)(2,1)S(1)}, u32[]{:S(2)}, u32[]{:S(2)}) collective-permute-start(bf16[2,128,128]{1,2,0:T(8,128)(2,1)S(1)} %get-tuple-element.85), channel_id=1, source_target_pairs={{0,8},{4,12},{8,0},{12,4},{1,9},{5,13},{9,1},{13,5},{2,10},{6,14},... | collective-permute-start | bytes 196616 | tf_op jit(solution)/shard_map/ppermute | solution.py:64
  45.4 1.5 %collective-permute-start.7 = (bf16[2,128,128]{1,2,0:T(8,128)(2,1)S(1)}, bf16[2,128,128]{1,2,0:T(8,128)(2,1)S(1)}, u32[]{:S(2)}, u32[]{:S(2)}) collective-permute-start(bf16[2,128,128]{1,2,0:T(8,128)(2,1)S(1)} %get-tuple-element.86), channel_id=1, source_target_pairs={{0,12},{4,8},{8,4},{12,0},{1,13},{5,9},{9,5},{13,1},{2,14},{6,10},... | collective-permute-start | bytes 196616 | tf_op jit(solution)/shard_map/ppermute | solution.py:64
  47.1 3.0 %collective-permute-done.8 = bf16[2,128,128]{1,2,0:T(8,128)(2,1)S(1)} collective-permute-done((bf16[2,128,128]{1,2,0:T(8,128)(2,1)S(1)}, bf16[2,128,128]{1,2,0:T(8,128)(2,1)S(1)}, u32[]{:S(2)}, u32[]{:S(2)}) %collective-permute-start.8) | collective-permute-done | bytes 65568 | tf_op jit(solution)/shard_map/ppermute | solution.py:64
  50.2 1.3 %collective-permute-done.7 = bf16[2,128,128]{1,2,0:T(8,128)(2,1)S(1)} collective-permute-done((bf16[2,128,128]{1,2,0:T(8,128)(2,1)S(1)}, bf16[2,128,128]{1,2,0:T(8,128)(2,1)S(1)}, u32[]{:S(2)}, u32[]{:S(2)}) %collective-permute-start.7) | collective-permute-done | bytes 65568 | tf_op jit(solution)/shard_map/ppermute | solution.py:64
  51.8 2.2 %fusion.8 = (f32[2048]{0:T(1024)S(1)}, f32[128,2048,1]{1,0,2:T(8,128)S(1)}) fusion(f32[128,2048]{1,0:T(8,128)S(1)} %get-tuple-element.104, f32[128]{0:T(128)S(1)} %add_rsqrt_fusion, bf16[2048,3,512]{2,0,1:T(8,128)(2,1)S(1)} %bitcast.160, bf16[1,512,128]{1,2,0:T(8,128)(2,1)S(1)} %get-tuple-element.65, bf16[1,512,128]{1,2,0:T(8,128)(2,1)S(1)} %get-tuple-element.64, ...), kind=kOutput, calls=%fused_computation.18 | convolution fusion | flops 806483968 | bytes 8790528 | tf_op jit(solution)/shard_map/mcr,dmc->rd/dot_general | solution.py:258
  54.2 1.5 %collective-permute-start.16 = (bf16[1,512,128]{1,2,0:T(8,128)(2,1)S(1)}, bf16[1,512,128]{1,2,0:T(8,128)(2,1)S(1)}, u32[]{:S(2)}, u32[]{:S(2)}) collective-permute-start(bf16[1,512,128]{1,2,0:T(8,128)(2,1)S(1)} %get-tuple-element.63), channel_id=1, source_target_pairs={{0,2},{2,0},{1,3},{3,1},{4,6},{6,4},{5,7},{7,5},{8,10},{10,8},{9,1... | collective-permute-start | bytes 393224 | tf_op jit(solution)/shard_map/ppermute | solution.py:47
  55.7 0.8 %convolution_multiply_fusion.1 = f32[20,2048]{1,0:T(8,128)S(1)} fusion(f32[128,2048,1]{1,0,2:T(8,128)S(1)} %get-tuple-element.106, f32[2048]{0:T(1024)S(1)} %copy-done.5, f32[128]{0:T(128)S(1)} %add_rsqrt_fusion, pred[128,5]{0,1:T(8,128)(4,1)S(1)} %get-tuple-element.107, pred[128,5]{0,1:T(8,128)(4,1)S(1)} %get-tuple-element.108, ...), kind=kOutput, calls=%fused_computation.2 | convolution fusion | flops 62970880 | bytes 1223680 | tf_op jit(solution)/shard_map/rk,rd->kd/dot_general | solution.py:262
  56.5 0.7 %fusion = f32[20,2048]{1,0:T(8,128)S(1)} fusion(f32[20,2048]{1,0:T(8,128)S(1)} %convolution_multiply_fusion.1, f32[128,2048]{1,0:T(8,128)S(1)} %get-tuple-element.104, f32[128]{0:T(128)S(1)} %add_rsqrt_fusion, f32[128]{0:T(128)S(1)} %multiply_reduce_fusion.1, pred[128,5]{0,1:T(8,128)(4,1)S(1)} %get-tuple-element.107, ...), kind=kOutput, calls=%fused_computation.1 | convolution fusion | flops 63276544 | bytes 1379840 | tf_op jit(solution)/shard_map/rk,dr->kd/dot_general | solution.py:263
  57.3 0.6 collective-permute-start.11
  58.0 1.3 %collective-permute-start.12 = (f32[21,512]{1,0:T(8,128)S(1)}, f32[21,512]{1,0:T(8,128)S(1)}, u32[]{:S(2)}, u32[]{:S(2)}) collective-permute-start(f32[21,512]{1,0:T(8,128)S(1)} %get-tuple-element.93), channel_id=1, source_target_pairs={{0,3},{1,2},{2,1},{3,0},{4,7},{5,6},{6,5},{7,4},{8,11},{9,10},{10,... | collective-permute-start | bytes 129032 | tf_op jit(solution)/shard_map/ppermute | solution.py:64
  59.7 1.9 %fusion.23 = f32[128,512]{1,0:T(8,128)} fusion(f32[512,1024]{1,0:T(8,128)S(1)} %bitcast.158, f32[128,512]{1,0:T(8,128)S(1)} %get-tuple-element.73, f32[128,512]{1,0:T(8,128)S(1)} %get-tuple-element.72, f32[1024]{0:T(1024)S(1)} %copy-done.6), kind=kOutput, calls=%fused_computation.47 | convolution fusion | flops 402915328 | bytes 2887680 | tf_op jit(solution)/shard_map/dot_general | solution.py:141
  61.5 0.5 collective-permute-done.11
  62.2 1.6 %collective-permute-start.15 = (f32[21,512]{1,0:T(8,128)S(1)}, f32[21,512]{1,0:T(8,128)S(1)}, u32[]{:S(2)}, u32[]{:S(2)}) collective-permute-start(f32[21,512]{1,0:T(8,128)S(1)} %pad_add_fusion), channel_id=1, source_target_pairs={{0,12},{4,8},{8,4},{12,0},{1,13},{5,9},{9,5},{13,1},{2,14},{6,10},... | collective-permute-start | bytes 129032 | tf_op jit(solution)/shard_map/ppermute | solution.py:64
  63.8 0.6 collective-permute-start.14
  64.3 2.3 %collective-permute-start.13 = (f32[21,512]{1,0:T(8,128)S(1)}, f32[21,512]{1,0:T(8,128)S(1)}, u32[]{:S(2)}, u32[]{:S(2)}) collective-permute-start(f32[21,512]{1,0:T(8,128)S(1)} %pad_add_fusion), channel_id=1, source_target_pairs={{0,4},{4,0},{8,12},{12,8},{1,5},{5,1},{9,13},{13,9},{2,6},{6,2},{1... | collective-permute-start | bytes 129032 | tf_op jit(solution)/shard_map/ppermute | solution.py:64
  67.4 0.9 %fusion.5 = bf16[128,512]{1,0:T(8,128)(2,1)} fusion(f32[128,512]{1,0:T(8,128)S(1)} %fusion.26, f32[128,512]{1,0:T(8,128)S(1)} %fusion.28, f32[128,512]{1,0:T(8,128)S(1)} %fusion.30, bf16[2048,512]{1,0:T(8,128)(2,1)S(1)} %copy-done.2, f32[128,2048]{1,0:T(8,128)S(1)} %get-tuple-element.104, s32[]{:T(128)S(6)} %select_n.772, ...), kind=kOutput, calls=%fused_computation.14 | convolution fusion | flops 67633152 | bytes 2228231 | tf_op jit(solution)/shard_map/cr,cd->rd/dot_general | solution.py:243
  68.6 1.5 %collective-permute-done.14 = f32[21,512]{1,0:T(8,128)S(1)} collective-permute-done((f32[21,512]{1,0:T(8,128)S(1)}, f32[21,512]{1,0:T(8,128)S(1)}, u32[]{:S(2)}, u32[]{:S(2)}) %collective-permute-start.14) | collective-permute-done | bytes 43040 | tf_op jit(solution)/shard_map/ppermute | solution.py:64
  70.1 0.6 slice.280
  70.7 0.6 copy.31
  (85 shorter events, 5.4 us)
Async XLA Ops:
  0.6 14.4 %copy-start = (f32[1,1,128,512]{3,2,1,0:T(8,128)S(1)}, f32[1,1,128,512]{3,2,1,0:T(8,128)}, u32[]{:S(2)}) copy-start(f32[1,1,128,512]{3,2,1,0:T(8,128)} %param.21) | copy-start | bytes 786436
  1.9 19.9 %collective-permute-start = (s32[3]{0:T(128)}, s32[3]{0:T(128)}, u32[]{:S(2)}, u32[]{:S(2)}) collective-permute-start(s32[3]{0:T(128)} %slice_add_fusion.2), channel_id=1, source_target_pairs={{0,4},{4,8},{8,12},{1,5},{5,9},{9,13},{2,6},{6,10},{10,14},{3,7},{... | collective-permute-start | bytes 44 | tf_op jit(solution)/shard_map/ppermute | solution.py:17
  9.9 3.8 %copy-start.9 = (s32[128]{0:T(128)S(1)}, s32[128]{0:T(128)}, u32[]{:S(2)}) copy-start(s32[128]{0:T(128)} %param.17) | copy-start | bytes 1540
  10.7 16.5 %collective-permute-start.3 = (f32[128,512]{1,0:T(8,128)}, f32[128,512]{1,0:T(8,128)}, u32[]{:S(2)}, u32[]{:S(2)}) collective-permute-start(f32[128,512]{1,0:T(8,128)} %select_select_fusion), channel_id=1, source_target_pairs={{0,3},{1,2},{2,1},{3,0},{4,7},{5,6},{6,5},{7,4},{8,11},{9,10},{10,... | collective-permute-start | bytes 786440 | tf_op jit(solution)/shard_map/ppermute | solution.py:64
  12.3 15.0 %collective-permute-start.1 = (f32[128,512]{1,0:T(8,128)}, f32[128,512]{1,0:T(8,128)}, u32[]{:S(2)}, u32[]{:S(2)}) collective-permute-start(f32[128,512]{1,0:T(8,128)} %get-tuple-element.68), channel_id=1, source_target_pairs={{0,1},{1,0},{2,3},{3,2},{4,5},{5,4},{6,7},{7,6},{8,9},{9,8},{10,11... | collective-permute-start | bytes 786440 | tf_op jit(solution)/shard_map/ppermute | solution.py:64
  13.2 14.0 %collective-permute-start.2 = (f32[128,512]{1,0:T(8,128)}, f32[128,512]{1,0:T(8,128)}, u32[]{:S(2)}, u32[]{:S(2)}) collective-permute-start(f32[128,512]{1,0:T(8,128)} %get-tuple-element.69), channel_id=1, source_target_pairs={{0,2},{1,3},{2,0},{3,1},{4,6},{5,7},{6,4},{7,5},{8,10},{9,11},{10,... | collective-permute-start | bytes 786440 | tf_op jit(solution)/shard_map/ppermute | solution.py:64
  15.8 0.8 %copy-start.1 = (f32[128,1024]{1,0:T(8,128)}, f32[128,1024]{1,0:T(8,128)S(1)}, u32[]{:S(2)}) copy-start(f32[128,1024]{1,0:T(8,128)S(1)} %convolution_bitcast_fusion.2) | copy-start | bytes 1572868
  15.8 4.8 %copy-start.7 = (pred[512]{0:T(512)(128)(4,1)S(1)}, pred[512]{0:T(512)(128)(4,1)}, u32[]{:S(2)}) copy-start(pred[512]{0:T(512)(128)(4,1)} %constant.92) | copy-start | bytes 1540
  19.3 3.2 %copy-start.10 = (s32[128]{0:T(128)S(1)}, s32[128]{0:T(128)}, u32[]{:S(2)}) copy-start(s32[128]{0:T(128)} %param.17) | copy-start | bytes 1540
  19.3 3.4 %copy-start.4 = (bf16[20,2048]{1,0:T(8,128)(2,1)S(1)}, bf16[20,2048]{1,0:T(8,128)(2,1)}, u32[]{:S(2)}) copy-start(bf16[20,2048]{1,0:T(8,128)(2,1)} %reshape.243) | copy-start | bytes 245764
  20.6 2.5 %copy-start.5 = (f32[2048]{0:T(1024)S(1)}, f32[2048]{0:T(1024)}, u32[]{:S(2)}) copy-start(f32[2048]{0:T(1024)} %param.19) | copy-start | bytes 24580
  23.1 10.1 %slice-start = ((s8[6291456]{0:T(1024)(128)(4,1)}), s8[4194304]{0:T(1024)(128)(4,1)S(1)}, s32[]{:S(2)}) async-start(s8[6291456]{0:T(1024)(128)(4,1)} %bitcast.159), calls=%async_computation | async-start | bytes 8388608
  23.2 10.1 %slice-start.1 = ((s8[6291456]{0:T(1024)(128)(4,1)}), s8[2097152]{0:T(1024)(128)(4,1)S(1)}, s32[]{:S(2)}) async-start(s8[6291456]{0:T(1024)(128)(4,1)} %bitcast.159), calls=%async_computation.1 | async-start | bytes 4194304
  28.7 5.7 %collective-permute-start.6 = (bf16[2,128,128]{1,2,0:T(8,128)(2,1)S(1)}, bf16[2,128,128]{1,2,0:T(8,128)(2,1)S(1)}, u32[]{:S(2)}, u32[]{:S(2)}) collective-permute-start(bf16[2,128,128]{1,2,0:T(8,128)(2,1)S(1)} %get-tuple-element.50), channel_id=1, source_target_pairs={{0,4},{4,0},{8,12},{12,8},{1,5},{5,1},{9,13},{13,9},{2,6},{6,2},{1... | collective-permute-start | bytes 196616 | tf_op jit(solution)/shard_map/ppermute | solution.py:64
  29.8 7.9 %collective-permute-start.5 = (bf16[2,128,128]{1,2,0:T(8,128)(2,1)S(1)}, bf16[2,128,128]{1,2,0:T(8,128)(2,1)S(1)}, u32[]{:S(2)}, u32[]{:S(2)}) collective-permute-start(bf16[2,128,128]{1,2,0:T(8,128)(2,1)S(1)} %get-tuple-element.90), channel_id=1, source_target_pairs={{0,8},{4,12},{8,0},{12,4},{1,9},{5,13},{9,1},{13,5},{2,10},{6,14},... | collective-permute-start | bytes 196616 | tf_op jit(solution)/shard_map/ppermute | solution.py:64
  30.9 6.8 %collective-permute-start.4 = (bf16[2,128,128]{1,2,0:T(8,128)(2,1)S(1)}, bf16[2,128,128]{1,2,0:T(8,128)(2,1)S(1)}, u32[]{:S(2)}, u32[]{:S(2)}) collective-permute-start(bf16[2,128,128]{1,2,0:T(8,128)(2,1)S(1)} %get-tuple-element.91), channel_id=1, source_target_pairs={{0,12},{4,8},{8,4},{12,0},{1,13},{5,9},{9,5},{13,1},{2,14},{6,10},... | collective-permute-start | bytes 196616 | tf_op jit(solution)/shard_map/ppermute | solution.py:64
  38.9 0.7 copy-start.8
  39.6 0.7 copy-start.6
  41.3 5.6 %copy-start.3 = (bf16[128,512]{1,0:T(8,128)(2,1)S(1)}, bf16[128,512]{1,0:T(8,128)(2,1)}, u32[]{:S(2)}) copy-start(bf16[128,512]{1,0:T(8,128)(2,1)} %param.23) | copy-start | bytes 393220
  42.3 4.8 %collective-permute-start.9 = (bf16[2,128,128]{1,2,0:T(8,128)(2,1)S(1)}, bf16[2,128,128]{1,2,0:T(8,128)(2,1)S(1)}, u32[]{:S(2)}, u32[]{:S(2)}) collective-permute-start(bf16[2,128,128]{1,2,0:T(8,128)(2,1)S(1)} %get-tuple-element.43), channel_id=1, source_target_pairs={{0,4},{4,0},{8,12},{12,8},{1,5},{5,1},{9,13},{13,9},{2,6},{6,2},{1... | collective-permute-start | bytes 196616 | tf_op jit(solution)/shard_map/ppermute | solution.py:64
  43.7 6.5 %collective-permute-start.8 = (bf16[2,128,128]{1,2,0:T(8,128)(2,1)S(1)}, bf16[2,128,128]{1,2,0:T(8,128)(2,1)S(1)}, u32[]{:S(2)}, u32[]{:S(2)}) collective-permute-start(bf16[2,128,128]{1,2,0:T(8,128)(2,1)S(1)} %get-tuple-element.85), channel_id=1, source_target_pairs={{0,8},{4,12},{8,0},{12,4},{1,9},{5,13},{9,1},{13,5},{2,10},{6,14},... | collective-permute-start | bytes 196616 | tf_op jit(solution)/shard_map/ppermute | solution.py:64
  45.4 6.2 %collective-permute-start.7 = (bf16[2,128,128]{1,2,0:T(8,128)(2,1)S(1)}, bf16[2,128,128]{1,2,0:T(8,128)(2,1)S(1)}, u32[]{:S(2)}, u32[]{:S(2)}) collective-permute-start(bf16[2,128,128]{1,2,0:T(8,128)(2,1)S(1)} %get-tuple-element.86), channel_id=1, source_target_pairs={{0,12},{4,8},{8,4},{12,0},{1,13},{5,9},{9,5},{13,1},{2,14},{6,10},... | collective-permute-start | bytes 196616 | tf_op jit(solution)/shard_map/ppermute | solution.py:64
  54.2 5.1 %collective-permute-start.16 = (bf16[1,512,128]{1,2,0:T(8,128)(2,1)S(1)}, bf16[1,512,128]{1,2,0:T(8,128)(2,1)S(1)}, u32[]{:S(2)}, u32[]{:S(2)}) collective-permute-start(bf16[1,512,128]{1,2,0:T(8,128)(2,1)S(1)} %get-tuple-element.63), channel_id=1, source_target_pairs={{0,2},{2,0},{1,3},{3,1},{4,6},{6,4},{5,7},{7,5},{8,10},{10,8},{9,1... | collective-permute-start | bytes 393224 | tf_op jit(solution)/shard_map/ppermute | solution.py:47
  57.2 9.4 %copy-start.2 = (bf16[2048,512]{1,0:T(8,128)(2,1)S(1)}, bf16[2048,512]{1,0:T(8,128)(2,1)}, u32[]{:S(2)}) copy-start(bf16[2048,512]{1,0:T(8,128)(2,1)} %param.22) | copy-start | bytes 6291460
  57.2 4.3 %collective-permute-start.10 = (f32[21,512]{1,0:T(8,128)S(1)}, f32[21,512]{1,0:T(8,128)S(1)}, u32[]{:S(2)}, u32[]{:S(2)}) collective-permute-start(f32[21,512]{1,0:T(8,128)S(1)} %get-tuple-element.36), channel_id=1, source_target_pairs={{0,1},{1,0},{2,3},{3,2},{4,5},{5,4},{6,7},{7,6},{8,9},{9,8},{10,11... | collective-permute-start | bytes 129032 | tf_op jit(solution)/shard_map/ppermute | solution.py:64
  57.3 4.7 %collective-permute-start.11 = (f32[21,512]{1,0:T(8,128)S(1)}, f32[21,512]{1,0:T(8,128)S(1)}, u32[]{:S(2)}, u32[]{:S(2)}) collective-permute-start(f32[21,512]{1,0:T(8,128)S(1)} %get-tuple-element.92), channel_id=1, source_target_pairs={{0,2},{1,3},{2,0},{3,1},{4,6},{5,7},{6,4},{7,5},{8,10},{9,11},{10,... | collective-permute-start | bytes 129032 | tf_op jit(solution)/shard_map/ppermute | solution.py:64
  58.0 4.2 %collective-permute-start.12 = (f32[21,512]{1,0:T(8,128)S(1)}, f32[21,512]{1,0:T(8,128)S(1)}, u32[]{:S(2)}, u32[]{:S(2)}) collective-permute-start(f32[21,512]{1,0:T(8,128)S(1)} %get-tuple-element.93), channel_id=1, source_target_pairs={{0,3},{1,2},{2,1},{3,0},{4,7},{5,6},{6,5},{7,4},{8,11},{9,10},{10,... | collective-permute-start | bytes 129032 | tf_op jit(solution)/shard_map/ppermute | solution.py:64
  59.3 7.3 %collective-permute-start.17 = (bf16[2,512,128]{1,2,0:T(8,128)(2,1)S(1)}, bf16[2,512,128]{1,2,0:T(8,128)(2,1)S(1)}, u32[]{:S(2)}, u32[]{:S(2)}) collective-permute-start(bf16[2,512,128]{1,2,0:T(8,128)(2,1)S(1)} %pad_maximum_fusion.5), channel_id=1, source_target_pairs={{0,1},{1,0},{2,3},{3,2},{4,5},{5,4},{6,7},{7,6},{8,9},{9,8},{10,11... | collective-permute-start | bytes 786440 | tf_op jit(solution)/shard_map/ppermute | solution.py:47
  62.2 6.4 %collective-permute-start.15 = (f32[21,512]{1,0:T(8,128)S(1)}, f32[21,512]{1,0:T(8,128)S(1)}, u32[]{:S(2)}, u32[]{:S(2)}) collective-permute-start(f32[21,512]{1,0:T(8,128)S(1)} %pad_add_fusion), channel_id=1, source_target_pairs={{0,12},{4,8},{8,4},{12,0},{1,13},{5,9},{9,5},{13,1},{2,14},{6,10},... | collective-permute-start | bytes 129032 | tf_op jit(solution)/shard_map/ppermute | solution.py:64
  63.8 6.3 %collective-permute-start.14 = (f32[21,512]{1,0:T(8,128)S(1)}, f32[21,512]{1,0:T(8,128)S(1)}, u32[]{:S(2)}, u32[]{:S(2)}) collective-permute-start(f32[21,512]{1,0:T(8,128)S(1)} %pad_add_fusion), channel_id=1, source_target_pairs={{0,8},{4,12},{8,0},{12,4},{1,9},{5,13},{9,1},{13,5},{2,10},{6,14},... | collective-permute-start | bytes 129032 | tf_op jit(solution)/shard_map/ppermute | solution.py:64
  64.3 5.7 %collective-permute-start.13 = (f32[21,512]{1,0:T(8,128)S(1)}, f32[21,512]{1,0:T(8,128)S(1)}, u32[]{:S(2)}, u32[]{:S(2)}) collective-permute-start(f32[21,512]{1,0:T(8,128)S(1)} %pad_add_fusion), channel_id=1, source_target_pairs={{0,4},{4,0},{8,12},{12,8},{1,5},{5,1},{9,13},{13,9},{2,6},{6,2},{1... | collective-permute-start | bytes 129032 | tf_op jit(solution)/shard_map/ppermute | solution.py:64

commit v14 on v13

--- a/solution.py
+++ b/solution.py
@@ -187,7 +187,11 @@
     length = row_count * lax.axis_size("seq")
     group_index = lax.axis_index(("chan", "pair"))
     rim_width = kmer_len - 1
-    before = from_behind(tokens[row_count - rim_width :] + 1, "seq", 1) - 1
+    seq_count = lax.axis_size("seq")
+    before = lax.ppermute(
+        tokens[row_count - rim_width :], "seq", [(i, (i + 1) % seq_count) for i in range(seq_count)]
+    )
+    before = jnp.where(lax.axis_index("seq") == 0, -1, before)
     extended = jnp.concatenate([before, tokens])
     letters = jnp.arange(letter_count, dtype=jnp.int32)
     columns = []

time: 71.7 us -> 69.8 us (0.974)
  starting transfers between devices: 25 us -> 23 us
  other arithmetic: 10.3 us -> 8.35 us
  local copies, waits for them, and re-layouts: 5.53 us -> 6.81 us
  waiting for transfers between devices: 10.1 us -> 10.9 us
    ppermute x1, starting transfers between devices: 5.52 us -> 3.05 us  [per_device(): lax.ppermute(tokens[row_count - rim_width:], 'seq', [(i, (i + 1) % seq_co...]
    add x1 -> x0, other arithmetic: 1.28 us -> none  [per_device(): before = from_behind(tokens[row_count - rim_width:] + 1, 'seq', 1) - 1]
    slice x0 -> x1, local copies, waits for them, and re-layouts: none -> 1.28 us  [per_device(): tokens[row_count - rim_width:]]
    ppermute x15, waiting for transfers between devices: 10.1 us -> 10.9 us  [group_exchange(): return lax.ppermute(x, axes, [(i, i ^ offset) for i in range(count)])]
  transfers between devices with their start and end apart: 18 -> 18, of which waited for: 7 -> 7; matrix products, arithmetic and copies ran while one was open for 33% -> 32% of each run, Pallas kernels for 0% -> 0%
where the time goes in v14:
time: 69.8 us; the launch traced here: 69.4 us
  starting transfers between devices  23 us (33%)
  matrix products  19.3 us (28%)
  waiting for transfers between devices  10.9 us (16%)
  other arithmetic  8.35 us (12%)
  local copies, waits for them, and re-layouts  6.81 us (10%)
  between operations  1.13 us (2%)
    ppermute x15, starting transfers between devices, group_exchange(): return lax.ppermute(x, axes, [(i, i ^ offset) for i in range(count)])  18 us
    ppermute x15, waiting for transfers between devices, group_exchange(): return lax.ppermute(x, axes, [(i, i ^ offset) for i in range(count)])  10.9 us
    dot_general x1, matrix products, per_device(): jnp.einsum('dr,dmc->mcr', hidden, in_proj, preferred_element_type=jnp.flo...  4.02 us
    dot_general x3, matrix products, inverse_dft(): lax.dot_general(spec * weight, dft, (((1,), (1,)), ((), ())), precision=T...  3.87 us
    unnamed x28, local copies, waits for them, and re-layouts  3.11 us
    ppermute x1, starting transfers between devices, per_device(): lax.ppermute(tokens[row_count - rim_width:], 'seq', [(i, (i + 1) % seq_co...  3.05 us
    dot_general x1, matrix products, per_device(): jnp.einsum('rd,cd->rc', cotangent, out_proj, preferred_element_type=jnp.f...  2.48 us
    dot_general x1, matrix products, per_device(): jnp.einsum('mcr,dmc->rd', d_proj, in_proj, preferred_element_type=jnp.flo...  2.17 us
  transfers between devices with their start and end apart: 18, of which 7 were waited for; matrix products, arithmetic and copies ran while one was open for 32% of the time, Pallas kernels for 0%

profile of v14, /device:TPU:0, one launch (start us, length us, event | category | flops | bytes accessed | tf_op | source)
XLA Modules:
  0.0 69.4 jit_solution(3262839020993647326)
XLA Ops:
  0.6 1.3 %slice.175 = s32[3]{0:T(128)} slice(s32[128]{0:T(128)} %param.17), slice={[125:128]} | slice | bytes 24 | tf_op jit(solution)/shard_map/slice | solution.py:192
  1.9 3.1 %collective-permute-start = (s32[3]{0:T(128)}, s32[3]{0:T(128)}, u32[]{:S(2)}, u32[]{:S(2)}) collective-permute-start(s32[3]{0:T(128)} %slice.175), channel_id=1, source_target_pairs={{0,4},{4,8},{8,12},{12,0},{1,5},{5,9},{9,13},{13,1},{2,6},{6,10},{... | collective-permute-start | bytes 44 | tf_op jit(solution)/shard_map/ppermute | solution.py:191
  5.0 2.5 %fusion.134 = f32[128,2048]{1,0:T(8,128)S(1)} fusion(bf16[128,512]{1,0:T(8,128)(2,1)} %param.23, bf16[2048,512]{1,0:T(8,128)(2,1)} %param.22), kind=kOutput, calls=%fused_computation.244 | convolution fusion | flops 268435456 | bytes 3276800 | tf_op jit(solution)/shard_map/rd,cd->rc/dot_general | solution.py:219
  7.5 0.8 %select_select_fusion = f32[128,512]{1,0:T(8,128)} fusion(f32[128,2048]{1,0:T(8,128)S(1)} %fusion.134, pred[]{:T(512)S(6)} %eq.123, pred[]{:T(512)S(6)} %eq.122, pred[]{:T(512)S(6)} %eq.121), kind=kLoop, calls=%fused_computation.114 | loop fusion | flops 196608 | bytes 1310723 | tf_op jit(solution)/shard_map/jit(_where)/select_n | solution.py:76
  8.3 0.6 collective-permute-start.3
  8.9 0.9 %select_select_fusion.2 = (f32[128,512]{1,0:T(8,128)}, f32[128,512]{1,0:T(8,128)}) fusion(f32[128,2048]{1,0:T(8,128)S(1)} %fusion.134, pred[]{:T(512)S(6)} %eq.117, pred[]{:T(512)S(6)} %eq.116, pred[]{:T(512)S(6)} %eq.115, pred[]{:T(512)S(6)} %eq.120, pred[]{:T(512)S(6)} %eq.119, pred[]{:T(512)S(6)} %eq.118), kind=kLoop, calls=%fused_computation.116 | loop fusion | flops 393216 | bytes 1572870 | tf_op jit(solution)/shard_map/jit(_where)/select_n | solution.py:76
  9.8 1.0 %collective-permute-start.1 = (f32[128,512]{1,0:T(8,128)}, f32[128,512]{1,0:T(8,128)}, u32[]{:S(2)}, u32[]{:S(2)}) collective-permute-start(f32[128,512]{1,0:T(8,128)} %get-tuple-element.68), channel_id=1, source_target_pairs={{0,1},{1,0},{2,3},{3,2},{4,5},{5,4},{6,7},{7,6},{8,9},{9,8},{10,11... | collective-permute-start | bytes 786440 | tf_op jit(solution)/shard_map/ppermute | solution.py:64
  10.8 0.5 collective-permute-start.2
  11.7 0.6 fusion.100
  12.6 0.7 %convolution_bitcast_fusion.2 = f32[128,1024]{1,0:T(8,128)S(1)} fusion(f32[512,1024]{1,0:T(8,128)S(1)} %bitcast.153, f32[1,1,128,512]{3,2,1,0:T(8,128)S(1)} %copy-done), kind=kOutput, calls=%fused_computation.7 | convolution fusion | flops 402653184 | bytes 2883584 | tf_op jit(solution)/shard_map/dot_general | solution.py:133
  13.4 0.8 %copy-done.1 = f32[128,1024]{1,0:T(8,128)} copy-done((f32[128,1024]{1,0:T(8,128)}, f32[128,1024]{1,0:T(8,128)S(1)}, u32[]{:S(2)}) %copy-start.1) | copy-done | bytes 524312
  14.1 1.1 %fusion.132 = (f32[127,1024]{1,0:T(8,128)}, f32[127,1024]{1,0:T(8,128)}) fusion(f32[128,1024]{1,0:T(8,128)S(1)} %convolution_bitcast_fusion.2), kind=kLoop, calls=%fused_computation.242 | loop fusion | bytes 2080768 | tf_op jit(solution)/shard_map/jit(_roll_static)/slice | solution.py:168
  15.2 0.9 %copy.28 = bf16[4,5,2048]{2,1,0:T(8,128)(2,1)S(1)} copy(bf16[4,5,2048]{2,0,1:T(4,128)(2,1)} %param.18) | data formatting | bytes 163840 | tf_op args[1]
  16.1 0.7 reshape.243
  16.8 1.4 %maximum_select_fusion = f32[128,1024]{1,0:T(8,128)S(1)} fusion(f32[1,1024]{1,0:T(1,128)S(1)} %get-tuple-element.77, f32[127,1024]{1,0:T(8,128)} %get-tuple-element.79, f32[127,1024]{1,0:T(8,128)} %get-tuple-element.78, f32[1,1024]{1,0:T(1,128)S(1)} %get-tuple-element.76, pred[128]{0:T(512)(128)(4,1)} %constant.92), kind=kLoop, calls=%fused_computation.38 | loop fusion | flops 393216 | bytes 1572992 | tf_op jit(solution)/shard_map/jit(_where)/select_n | solution.py:169
  18.2 1.1 %slice_add_fusion.1 = (f32[128,512]{1,0:T(8,128)S(1)}, f32[128,512]{1,0:T(8,128)S(1)}) fusion(f32[128,1024]{1,0:T(8,128)S(1)} %maximum_select_fusion, f32[128,1024]{1,0:T(8,128)} %copy-done.1, pred[512]{0:T(512)(128)(4,1)S(1)} %copy-done.7), kind=kLoop, calls=%fused_computation.94 | loop fusion | flops 262144 | bytes 1573376 | tf_op jit(solution)/shard_map/add | solution.py:176
  19.6 0.4 multiply_reduce_fusion
  20.1 4.0 %convolution_bitcast_fusion.1 = f32[3,512,128]{1,2,0:T(8,128)S(1)} fusion(bf16[2048,3,512]{2,0,1:T(8,128)(2,1)} %param.20, f32[128,2048]{1,0:T(8,128)S(1)} %get-tuple-element.104, f32[2048]{0:T(1024)S(1)} %copy-done.5, f32[128]{0:T(128)S(1)} %add_rsqrt_fusion), kind=kOutput, calls=%fused_computation.5 | convolution fusion | flops 806092800 | bytes 8135168 | tf_op jit(solution)/shard_map/dr,dmc->mcr/dot_general | solution.py:208
  24.2 1.3 %fusion.55 = (bf16[1,512,128]{1,2,0:T(8,128)(2,1)S(1)}, f32[128,512]{1,0:T(8,128)S(1)}) fusion(f32[3,512,128]{1,2,0:T(8,128)S(1)} %convolution_bitcast_fusion.1, f32[128,512]{1,0:T(8,128)} %collective-permute-done.3, f32[128,512]{1,0:T(8,128)} %collective-permute-done.2, f32[128,512]{1,0:T(8,128)} %collective-permute-done.1, f32[128,2048]{1,0:T(8,128)S(1)} %fusion.134, ...), kind=kLoop, calls=%fused_computation.129 | loop fusion | flops 589824 | bytes 2490371 | tf_op jit(solution)/shard_map/stack | solution.py:225
  25.6 2.3 %collective-permute-start.6 = (bf16[2,128,128]{1,2,0:T(8,128)(2,1)S(1)}, bf16[2,128,128]{1,2,0:T(8,128)(2,1)S(1)}, u32[]{:S(2)}, u32[]{:S(2)}) collective-permute-start(bf16[2,128,128]{1,2,0:T(8,128)(2,1)S(1)} %get-tuple-element.50), channel_id=1, source_target_pairs={{0,4},{4,0},{8,12},{12,8},{1,5},{5,1},{9,13},{13,9},{2,6},{6,2},{1... | collective-permute-start | bytes 196616 | tf_op jit(solution)/shard_map/ppermute | solution.py:64
  27.9 1.1 %collective-permute-start.5 = (bf16[2,128,128]{1,2,0:T(8,128)(2,1)S(1)}, bf16[2,128,128]{1,2,0:T(8,128)(2,1)S(1)}, u32[]{:S(2)}, u32[]{:S(2)}) collective-permute-start(bf16[2,128,128]{1,2,0:T(8,128)(2,1)S(1)} %get-tuple-element.90), channel_id=1, source_target_pairs={{0,8},{4,12},{8,0},{12,4},{1,9},{5,13},{9,1},{13,5},{2,10},{6,14},... | collective-permute-start | bytes 196616 | tf_op jit(solution)/shard_map/ppermute | solution.py:64
  29.0 1.5 %collective-permute-start.4 = (bf16[2,128,128]{1,2,0:T(8,128)(2,1)S(1)}, bf16[2,128,128]{1,2,0:T(8,128)(2,1)S(1)}, u32[]{:S(2)}, u32[]{:S(2)}) collective-permute-start(bf16[2,128,128]{1,2,0:T(8,128)(2,1)S(1)} %get-tuple-element.91), channel_id=1, source_target_pairs={{0,12},{4,8},{8,4},{12,0},{1,13},{5,9},{9,5},{13,1},{2,14},{6,10},... | collective-permute-start | bytes 196616 | tf_op jit(solution)/shard_map/ppermute | solution.py:64
  30.5 1.1 %fusion.1 = f32[3,512,128]{1,2,0:T(8,128)S(1)} fusion(f32[3,512,128]{1,2,0:T(8,128)S(1)} %convolution_bitcast_fusion.1, bf16[2048,3,512]{2,0,1:T(8,128)(2,1)S(1)} %bitcast.160, f32[128,2048]{1,0:T(8,128)S(1)} %get-tuple-element.104, f32[2048]{0:T(1024)S(1)} %copy-done.5, f32[128]{0:T(128)S(1)} %add_rsqrt_fusion), kind=kOutput, calls=%fused_computation.6 | convolution fusion | flops 807075840 | bytes 8921600 | tf_op jit(solution)/shard_map/dr,dmc->mcr/dot_general | solution.py:210
  31.6 4.2 %collective-permute-done.5 = bf16[2,128,128]{1,2,0:T(8,128)(2,1)S(1)} collective-permute-done((bf16[2,128,128]{1,2,0:T(8,128)(2,1)S(1)}, bf16[2,128,128]{1,2,0:T(8,128)(2,1)S(1)}, u32[]{:S(2)}, u32[]{:S(2)}) %collective-permute-start.5) | collective-permute-done | bytes 65568 | tf_op jit(solution)/shard_map/ppermute | solution.py:64
  35.9 0.6 fusion.71
  36.4 0.6 fusion.73
  38.4 1.0 %fusion.6 = bf16[1,128,512]{1,2,0:T(8,128)(2,1)S(1)} fusion(f32[512,1024]{1,0:T(8,128)S(1)} %bitcast.156, f32[128,512]{1,0:T(8,128)S(1)} %get-tuple-element.70, f32[128,512]{1,0:T(8,128)S(1)} %get-tuple-element.71, f32[1024]{0:T(1024)S(1)} %copy-done.6), kind=kOutput, calls=%fused_computation.15 | convolution fusion | flops 402980864 | bytes 2756608 | tf_op jit(solution)/shard_map/dot_general | solution.py:141
  39.4 1.0 %fusion.7 = bf16[1,128,512]{1,2,0:T(8,128)(2,1)S(1)} fusion(f32[512,1024]{1,0:T(8,128)S(1)} %bitcast.157, f32[128,512]{1,0:T(8,128)S(1)} %get-tuple-element.101, f32[128,512]{1,0:T(8,128)S(1)} %get-tuple-element.102, f32[1024]{0:T(1024)S(1)} %copy-done.6), kind=kOutput, calls=%fused_computation.16 | convolution fusion | flops 402980864 | bytes 2756608 | tf_op jit(solution)/shard_map/dot_general | solution.py:141
  40.4 1.3 %collective-permute-start.9 = (bf16[2,128,128]{1,2,0:T(8,128)(2,1)S(1)}, bf16[2,128,128]{1,2,0:T(8,128)(2,1)S(1)}, u32[]{:S(2)}, u32[]{:S(2)}) collective-permute-start(bf16[2,128,128]{1,2,0:T(8,128)(2,1)S(1)} %get-tuple-element.43), channel_id=1, source_target_pairs={{0,4},{4,0},{8,12},{12,8},{1,5},{5,1},{9,13},{13,9},{2,6},{6,2},{1... | collective-permute-start | bytes 196616 | tf_op jit(solution)/shard_map/ppermute | solution.py:64
  41.8 1.6 %collective-permute-start.8 = (bf16[2,128,128]{1,2,0:T(8,128)(2,1)S(1)}, bf16[2,128,128]{1,2,0:T(8,128)(2,1)S(1)}, u32[]{:S(2)}, u32[]{:S(2)}) collective-permute-start(bf16[2,128,128]{1,2,0:T(8,128)(2,1)S(1)} %get-tuple-element.85), channel_id=1, source_target_pairs={{0,8},{4,12},{8,0},{12,4},{1,9},{5,13},{9,1},{13,5},{2,10},{6,14},... | collective-permute-start | bytes 196616 | tf_op jit(solution)/shard_map/ppermute | solution.py:64
  43.4 1.5 %collective-permute-start.7 = (bf16[2,128,128]{1,2,0:T(8,128)(2,1)S(1)}, bf16[2,128,128]{1,2,0:T(8,128)(2,1)S(1)}, u32[]{:S(2)}, u32[]{:S(2)}) collective-permute-start(bf16[2,128,128]{1,2,0:T(8,128)(2,1)S(1)} %get-tuple-element.86), channel_id=1, source_target_pairs={{0,12},{4,8},{8,4},{12,0},{1,13},{5,9},{9,5},{13,1},{2,14},{6,10},... | collective-permute-start | bytes 196616 | tf_op jit(solution)/shard_map/ppermute | solution.py:64
  45.2 3.1 %collective-permute-done.8 = bf16[2,128,128]{1,2,0:T(8,128)(2,1)S(1)} collective-permute-done((bf16[2,128,128]{1,2,0:T(8,128)(2,1)S(1)}, bf16[2,128,128]{1,2,0:T(8,128)(2,1)S(1)}, u32[]{:S(2)}, u32[]{:S(2)}) %collective-permute-start.8) | collective-permute-done | bytes 65568 | tf_op jit(solution)/shard_map/ppermute | solution.py:64
  48.3 1.3 %collective-permute-done.7 = bf16[2,128,128]{1,2,0:T(8,128)(2,1)S(1)} collective-permute-done((bf16[2,128,128]{1,2,0:T(8,128)(2,1)S(1)}, bf16[2,128,128]{1,2,0:T(8,128)(2,1)S(1)}, u32[]{:S(2)}, u32[]{:S(2)}) %collective-permute-start.7) | collective-permute-done | bytes 65568 | tf_op jit(solution)/shard_map/ppermute | solution.py:64
  49.9 2.2 %fusion.8 = (f32[2048]{0:T(1024)S(1)}, f32[128,2048,1]{1,0,2:T(8,128)S(1)}) fusion(f32[128,2048]{1,0:T(8,128)S(1)} %get-tuple-element.104, f32[128]{0:T(128)S(1)} %add_rsqrt_fusion, bf16[2048,3,512]{2,0,1:T(8,128)(2,1)S(1)} %bitcast.160, bf16[1,512,128]{1,2,0:T(8,128)(2,1)S(1)} %get-tuple-element.65, bf16[1,512,128]{1,2,0:T(8,128)(2,1)S(1)} %get-tuple-element.64, ...), kind=kOutput, calls=%fused_computation.18 | convolution fusion | flops 806483968 | bytes 8790528 | tf_op jit(solution)/shard_map/mcr,dmc->rd/dot_general | solution.py:262
  52.2 1.5 %collective-permute-start.16 = (bf16[1,512,128]{1,2,0:T(8,128)(2,1)S(1)}, bf16[1,512,128]{1,2,0:T(8,128)(2,1)S(1)}, u32[]{:S(2)}, u32[]{:S(2)}) collective-permute-start(bf16[1,512,128]{1,2,0:T(8,128)(2,1)S(1)} %get-tuple-element.63), channel_id=1, source_target_pairs={{0,2},{2,0},{1,3},{3,1},{4,6},{6,4},{5,7},{7,5},{8,10},{10,8},{9,1... | collective-permute-start | bytes 393224 | tf_op jit(solution)/shard_map/ppermute | solution.py:47
  53.8 0.8 %convolution_multiply_fusion.1 = f32[20,2048]{1,0:T(8,128)S(1)} fusion(f32[128,2048,1]{1,0,2:T(8,128)S(1)} %get-tuple-element.106, f32[2048]{0:T(1024)S(1)} %copy-done.5, f32[128]{0:T(128)S(1)} %add_rsqrt_fusion, pred[128,5]{0,1:T(8,128)(4,1)S(1)} %get-tuple-element.107, pred[128,5]{0,1:T(8,128)(4,1)S(1)} %get-tuple-element.108, ...), kind=kOutput, calls=%fused_computation.2 | convolution fusion | flops 62970880 | bytes 1223680 | tf_op jit(solution)/shard_map/rk,rd->kd/dot_general | solution.py:266
  54.6 0.7 %fusion = f32[20,2048]{1,0:T(8,128)S(1)} fusion(f32[20,2048]{1,0:T(8,128)S(1)} %convolution_multiply_fusion.1, f32[128,2048]{1,0:T(8,128)S(1)} %get-tuple-element.104, f32[128]{0:T(128)S(1)} %add_rsqrt_fusion, f32[128]{0:T(128)S(1)} %multiply_reduce_fusion.1, pred[128,5]{0,1:T(8,128)(4,1)S(1)} %get-tuple-element.107, ...), kind=kOutput, calls=%fused_computation.1 | convolution fusion | flops 63276544 | bytes 1379840 | tf_op jit(solution)/shard_map/rk,dr->kd/dot_general | solution.py:267
  55.4 0.6 collective-permute-start.11
  56.0 1.3 %collective-permute-start.12 = (f32[21,512]{1,0:T(8,128)S(1)}, f32[21,512]{1,0:T(8,128)S(1)}, u32[]{:S(2)}, u32[]{:S(2)}) collective-permute-start(f32[21,512]{1,0:T(8,128)S(1)} %get-tuple-element.93), channel_id=1, source_target_pairs={{0,3},{1,2},{2,1},{3,0},{4,7},{5,6},{6,5},{7,4},{8,11},{9,10},{10,... | collective-permute-start | bytes 129032 | tf_op jit(solution)/shard_map/ppermute | solution.py:64
  57.8 1.9 %fusion.23 = f32[128,512]{1,0:T(8,128)} fusion(f32[512,1024]{1,0:T(8,128)S(1)} %bitcast.158, f32[128,512]{1,0:T(8,128)S(1)} %get-tuple-element.73, f32[128,512]{1,0:T(8,128)S(1)} %get-tuple-element.72, f32[1024]{0:T(1024)S(1)} %copy-done.6), kind=kOutput, calls=%fused_computation.47 | convolution fusion | flops 402915328 | bytes 2887680 | tf_op jit(solution)/shard_map/dot_general | solution.py:141
  59.6 0.5 collective-permute-done.11
  60.2 1.6 %collective-permute-start.15 = (f32[21,512]{1,0:T(8,128)S(1)}, f32[21,512]{1,0:T(8,128)S(1)}, u32[]{:S(2)}, u32[]{:S(2)}) collective-permute-start(f32[21,512]{1,0:T(8,128)S(1)} %pad_add_fusion), channel_id=1, source_target_pairs={{0,12},{4,8},{8,4},{12,0},{1,13},{5,9},{9,5},{13,1},{2,14},{6,10},... | collective-permute-start | bytes 129032 | tf_op jit(solution)/shard_map/ppermute | solution.py:64
  61.9 0.6 collective-permute-start.14
  62.4 2.3 %collective-permute-start.13 = (f32[21,512]{1,0:T(8,128)S(1)}, f32[21,512]{1,0:T(8,128)S(1)}, u32[]{:S(2)}, u32[]{:S(2)}) collective-permute-start(f32[21,512]{1,0:T(8,128)S(1)} %pad_add_fusion), channel_id=1, source_target_pairs={{0,4},{4,0},{8,12},{12,8},{1,5},{5,1},{9,13},{13,9},{2,6},{6,2},{1... | collective-permute-start | bytes 129032 | tf_op jit(solution)/shard_map/ppermute | solution.py:64
  65.5 0.9 %fusion.5 = bf16[128,512]{1,0:T(8,128)(2,1)} fusion(f32[128,512]{1,0:T(8,128)S(1)} %fusion.26, f32[128,512]{1,0:T(8,128)S(1)} %fusion.28, f32[128,512]{1,0:T(8,128)S(1)} %fusion.30, bf16[2048,512]{1,0:T(8,128)(2,1)S(1)} %copy-done.2, f32[128,2048]{1,0:T(8,128)S(1)} %get-tuple-element.104, s32[]{:T(128)S(6)} %select_n.782, ...), kind=kOutput, calls=%fused_computation.14 | convolution fusion | flops 67633152 | bytes 2228231 | tf_op jit(solution)/shard_map/cr,cd->rd/dot_general | solution.py:247
  66.7 1.5 %collective-permute-done.14 = f32[21,512]{1,0:T(8,128)S(1)} collective-permute-done((f32[21,512]{1,0:T(8,128)S(1)}, f32[21,512]{1,0:T(8,128)S(1)}, u32[]{:S(2)}, u32[]{:S(2)}) %collective-permute-start.14) | collective-permute-done | bytes 43040 | tf_op jit(solution)/shard_map/ppermute | solution.py:64
  68.2 0.6 slice.280
  68.8 0.6 copy.31
  (85 shorter events, 4.9 us)
Async XLA Ops:
  0.6 12.0 %copy-start = (f32[1,1,128,512]{3,2,1,0:T(8,128)S(1)}, f32[1,1,128,512]{3,2,1,0:T(8,128)}, u32[]{:S(2)}) copy-start(f32[1,1,128,512]{3,2,1,0:T(8,128)} %param.21) | copy-start | bytes 786436
  1.9 17.4 %collective-permute-start = (s32[3]{0:T(128)}, s32[3]{0:T(128)}, u32[]{:S(2)}, u32[]{:S(2)}) collective-permute-start(s32[3]{0:T(128)} %slice.175), channel_id=1, source_target_pairs={{0,4},{4,8},{8,12},{12,0},{1,5},{5,9},{9,13},{13,1},{2,6},{6,10},{... | collective-permute-start | bytes 44 | tf_op jit(solution)/shard_map/ppermute | solution.py:191
  7.5 3.8 %copy-start.9 = (s32[128]{0:T(128)S(1)}, s32[128]{0:T(128)}, u32[]{:S(2)}) copy-start(s32[128]{0:T(128)} %param.17) | copy-start | bytes 1540
  8.3 15.9 %collective-permute-start.3 = (f32[128,512]{1,0:T(8,128)}, f32[128,512]{1,0:T(8,128)}, u32[]{:S(2)}, u32[]{:S(2)}) collective-permute-start(f32[128,512]{1,0:T(8,128)} %select_select_fusion), channel_id=1, source_target_pairs={{0,3},{1,2},{2,1},{3,0},{4,7},{5,6},{6,5},{7,4},{8,11},{9,10},{10,... | collective-permute-start | bytes 786440 | tf_op jit(solution)/shard_map/ppermute | solution.py:64
  9.8 14.3 %collective-permute-start.1 = (f32[128,512]{1,0:T(8,128)}, f32[128,512]{1,0:T(8,128)}, u32[]{:S(2)}, u32[]{:S(2)}) collective-permute-start(f32[128,512]{1,0:T(8,128)} %get-tuple-element.68), channel_id=1, source_target_pairs={{0,1},{1,0},{2,3},{3,2},{4,5},{5,4},{6,7},{7,6},{8,9},{9,8},{10,11... | collective-permute-start | bytes 786440 | tf_op jit(solution)/shard_map/ppermute | solution.py:64
  10.8 13.4 %collective-permute-start.2 = (f32[128,512]{1,0:T(8,128)}, f32[128,512]{1,0:T(8,128)}, u32[]{:S(2)}, u32[]{:S(2)}) collective-permute-start(f32[128,512]{1,0:T(8,128)} %get-tuple-element.69), channel_id=1, source_target_pairs={{0,2},{1,3},{2,0},{3,1},{4,6},{5,7},{6,4},{7,5},{8,10},{9,11},{10,... | collective-permute-start | bytes 786440 | tf_op jit(solution)/shard_map/ppermute | solution.py:64
  13.3 0.8 %copy-start.1 = (f32[128,1024]{1,0:T(8,128)}, f32[128,1024]{1,0:T(8,128)S(1)}, u32[]{:S(2)}) copy-start(f32[128,1024]{1,0:T(8,128)S(1)} %convolution_bitcast_fusion.2) | copy-start | bytes 1572868
  13.3 4.8 %copy-start.7 = (pred[512]{0:T(512)(128)(4,1)S(1)}, pred[512]{0:T(512)(128)(4,1)}, u32[]{:S(2)}) copy-start(pred[512]{0:T(512)(128)(4,1)} %constant.91) | copy-start | bytes 1540
  16.8 2.6 %copy-start.10 = (s32[128]{0:T(128)S(1)}, s32[128]{0:T(128)}, u32[]{:S(2)}) copy-start(s32[128]{0:T(128)} %param.17) | copy-start | bytes 1540
  16.8 2.8 %copy-start.4 = (bf16[20,2048]{1,0:T(8,128)(2,1)S(1)}, bf16[20,2048]{1,0:T(8,128)(2,1)}, u32[]{:S(2)}) copy-start(bf16[20,2048]{1,0:T(8,128)(2,1)} %reshape.243) | copy-start | bytes 245764
  18.2 1.9 %copy-start.5 = (f32[2048]{0:T(1024)S(1)}, f32[2048]{0:T(1024)}, u32[]{:S(2)}) copy-start(f32[2048]{0:T(1024)} %param.19) | copy-start | bytes 24580
  20.0 10.5 %slice-start = ((s8[6291456]{0:T(1024)(128)(4,1)}), s8[4194304]{0:T(1024)(128)(4,1)S(1)}, s32[]{:S(2)}) async-start(s8[6291456]{0:T(1024)(128)(4,1)} %bitcast.159), calls=%async_computation | async-start | bytes 8388608
  20.0 10.4 %slice-start.1 = ((s8[6291456]{0:T(1024)(128)(4,1)}), s8[2097152]{0:T(1024)(128)(4,1)S(1)}, s32[]{:S(2)}) async-start(s8[6291456]{0:T(1024)(128)(4,1)} %bitcast.159), calls=%async_computation.1 | async-start | bytes 4194304
  25.6 6.0 %collective-permute-start.6 = (bf16[2,128,128]{1,2,0:T(8,128)(2,1)S(1)}, bf16[2,128,128]{1,2,0:T(8,128)(2,1)S(1)}, u32[]{:S(2)}, u32[]{:S(2)}) collective-permute-start(bf16[2,128,128]{1,2,0:T(8,128)(2,1)S(1)} %get-tuple-element.50), channel_id=1, source_target_pairs={{0,4},{4,0},{8,12},{12,8},{1,5},{5,1},{9,13},{13,9},{2,6},{6,2},{1... | collective-permute-start | bytes 196616 | tf_op jit(solution)/shard_map/ppermute | solution.py:64
  27.9 7.9 %collective-permute-start.5 = (bf16[2,128,128]{1,2,0:T(8,128)(2,1)S(1)}, bf16[2,128,128]{1,2,0:T(8,128)(2,1)S(1)}, u32[]{:S(2)}, u32[]{:S(2)}) collective-permute-start(bf16[2,128,128]{1,2,0:T(8,128)(2,1)S(1)} %get-tuple-element.90), channel_id=1, source_target_pairs={{0,8},{4,12},{8,0},{12,4},{1,9},{5,13},{9,1},{13,5},{2,10},{6,14},... | collective-permute-start | bytes 196616 | tf_op jit(solution)/shard_map/ppermute | solution.py:64
  29.0 6.8 %collective-permute-start.4 = (bf16[2,128,128]{1,2,0:T(8,128)(2,1)S(1)}, bf16[2,128,128]{1,2,0:T(8,128)(2,1)S(1)}, u32[]{:S(2)}, u32[]{:S(2)}) collective-permute-start(bf16[2,128,128]{1,2,0:T(8,128)(2,1)S(1)} %get-tuple-element.91), channel_id=1, source_target_pairs={{0,12},{4,8},{8,4},{12,0},{1,13},{5,9},{9,5},{13,1},{2,14},{6,10},... | collective-permute-start | bytes 196616 | tf_op jit(solution)/shard_map/ppermute | solution.py:64
  37.0 0.7 copy-start.8
  37.7 0.7 copy-start.6
  39.4 5.6 %copy-start.3 = (bf16[128,512]{1,0:T(8,128)(2,1)S(1)}, bf16[128,512]{1,0:T(8,128)(2,1)}, u32[]{:S(2)}) copy-start(bf16[128,512]{1,0:T(8,128)(2,1)} %param.23) | copy-start | bytes 393220
  40.4 4.8 %collective-permute-start.9 = (bf16[2,128,128]{1,2,0:T(8,128)(2,1)S(1)}, bf16[2,128,128]{1,2,0:T(8,128)(2,1)S(1)}, u32[]{:S(2)}, u32[]{:S(2)}) collective-permute-start(bf16[2,128,128]{1,2,0:T(8,128)(2,1)S(1)} %get-tuple-element.43), channel_id=1, source_target_pairs={{0,4},{4,0},{8,12},{12,8},{1,5},{5,1},{9,13},{13,9},{2,6},{6,2},{1... | collective-permute-start | bytes 196616 | tf_op jit(solution)/shard_map/ppermute | solution.py:64
  41.8 6.5 %collective-permute-start.8 = (bf16[2,128,128]{1,2,0:T(8,128)(2,1)S(1)}, bf16[2,128,128]{1,2,0:T(8,128)(2,1)S(1)}, u32[]{:S(2)}, u32[]{:S(2)}) collective-permute-start(bf16[2,128,128]{1,2,0:T(8,128)(2,1)S(1)} %get-tuple-element.85), channel_id=1, source_target_pairs={{0,8},{4,12},{8,0},{12,4},{1,9},{5,13},{9,1},{13,5},{2,10},{6,14},... | collective-permute-start | bytes 196616 | tf_op jit(solution)/shard_map/ppermute | solution.py:64
  43.4 6.2 %collective-permute-start.7 = (bf16[2,128,128]{1,2,0:T(8,128)(2,1)S(1)}, bf16[2,128,128]{1,2,0:T(8,128)(2,1)S(1)}, u32[]{:S(2)}, u32[]{:S(2)}) collective-permute-start(bf16[2,128,128]{1,2,0:T(8,128)(2,1)S(1)} %get-tuple-element.86), channel_id=1, source_target_pairs={{0,12},{4,8},{8,4},{12,0},{1,13},{5,9},{9,5},{13,1},{2,14},{6,10},... | collective-permute-start | bytes 196616 | tf_op jit(solution)/shard_map/ppermute | solution.py:64
  52.2 5.1 %collective-permute-start.16 = (bf16[1,512,128]{1,2,0:T(8,128)(2,1)S(1)}, bf16[1,512,128]{1,2,0:T(8,128)(2,1)S(1)}, u32[]{:S(2)}, u32[]{:S(2)}) collective-permute-start(bf16[1,512,128]{1,2,0:T(8,128)(2,1)S(1)} %get-tuple-element.63), channel_id=1, source_target_pairs={{0,2},{2,0},{1,3},{3,1},{4,6},{6,4},{5,7},{7,5},{8,10},{10,8},{9,1... | collective-permute-start | bytes 393224 | tf_op jit(solution)/shard_map/ppermute | solution.py:47
  55.3 9.4 %copy-start.2 = (bf16[2048,512]{1,0:T(8,128)(2,1)S(1)}, bf16[2048,512]{1,0:T(8,128)(2,1)}, u32[]{:S(2)}) copy-start(bf16[2048,512]{1,0:T(8,128)(2,1)} %param.22) | copy-start | bytes 6291460
  55.3 4.3 %collective-permute-start.10 = (f32[21,512]{1,0:T(8,128)S(1)}, f32[21,512]{1,0:T(8,128)S(1)}, u32[]{:S(2)}, u32[]{:S(2)}) collective-permute-start(f32[21,512]{1,0:T(8,128)S(1)} %get-tuple-element.36), channel_id=1, source_target_pairs={{0,1},{1,0},{2,3},{3,2},{4,5},{5,4},{6,7},{7,6},{8,9},{9,8},{10,11... | collective-permute-start | bytes 129032 | tf_op jit(solution)/shard_map/ppermute | solution.py:64
  55.4 4.7 %collective-permute-start.11 = (f32[21,512]{1,0:T(8,128)S(1)}, f32[21,512]{1,0:T(8,128)S(1)}, u32[]{:S(2)}, u32[]{:S(2)}) collective-permute-start(f32[21,512]{1,0:T(8,128)S(1)} %get-tuple-element.92), channel_id=1, source_target_pairs={{0,2},{1,3},{2,0},{3,1},{4,6},{5,7},{6,4},{7,5},{8,10},{9,11},{10,... | collective-permute-start | bytes 129032 | tf_op jit(solution)/shard_map/ppermute | solution.py:64
  56.0 4.2 %collective-permute-start.12 = (f32[21,512]{1,0:T(8,128)S(1)}, f32[21,512]{1,0:T(8,128)S(1)}, u32[]{:S(2)}, u32[]{:S(2)}) collective-permute-start(f32[21,512]{1,0:T(8,128)S(1)} %get-tuple-element.93), channel_id=1, source_target_pairs={{0,3},{1,2},{2,1},{3,0},{4,7},{5,6},{6,5},{7,4},{8,11},{9,10},{10,... | collective-permute-start | bytes 129032 | tf_op jit(solution)/shard_map/ppermute | solution.py:64
  57.4 7.3 %collective-permute-start.17 = (bf16[2,512,128]{1,2,0:T(8,128)(2,1)S(1)}, bf16[2,512,128]{1,2,0:T(8,128)(2,1)S(1)}, u32[]{:S(2)}, u32[]{:S(2)}) collective-permute-start(bf16[2,512,128]{1,2,0:T(8,128)(2,1)S(1)} %pad_maximum_fusion.5), channel_id=1, source_target_pairs={{0,1},{1,0},{2,3},{3,2},{4,5},{5,4},{6,7},{7,6},{8,9},{9,8},{10,11... | collective-permute-start | bytes 786440 | tf_op jit(solution)/shard_map/ppermute | solution.py:47
  60.2 6.4 %collective-permute-start.15 = (f32[21,512]{1,0:T(8,128)S(1)}, f32[21,512]{1,0:T(8,128)S(1)}, u32[]{:S(2)}, u32[]{:S(2)}) collective-permute-start(f32[21,512]{1,0:T(8,128)S(1)} %pad_add_fusion), channel_id=1, source_target_pairs={{0,12},{4,8},{8,4},{12,0},{1,13},{5,9},{9,5},{13,1},{2,14},{6,10},... | collective-permute-start | bytes 129032 | tf_op jit(solution)/shard_map/ppermute | solution.py:64
  61.9 6.3 %collective-permute-start.14 = (f32[21,512]{1,0:T(8,128)S(1)}, f32[21,512]{1,0:T(8,128)S(1)}, u32[]{:S(2)}, u32[]{:S(2)}) collective-permute-start(f32[21,512]{1,0:T(8,128)S(1)} %pad_add_fusion), channel_id=1, source_target_pairs={{0,8},{4,12},{8,0},{12,4},{1,9},{5,13},{9,1},{13,5},{2,10},{6,14},... | collective-permute-start | bytes 129032 | tf_op jit(solution)/shard_map/ppermute | solution.py:64
  62.4 5.8 %collective-permute-start.13 = (f32[21,512]{1,0:T(8,128)S(1)}, f32[21,512]{1,0:T(8,128)S(1)}, u32[]{:S(2)}, u32[]{:S(2)}) collective-permute-start(f32[21,512]{1,0:T(8,128)S(1)} %pad_add_fusion), channel_id=1, source_target_pairs={{0,4},{4,0},{8,12},{12,8},{1,5},{5,1},{9,13},{13,9},{2,6},{6,2},{1... | collective-permute-start | bytes 129032 | tf_op jit(solution)/shard_map/ppermute | solution.py:64

commit v15 on v14

--- a/solution.py
+++ b/solution.py
@@ -92,7 +92,8 @@
             x = x + got
             step *= 2
         return x, tied
-    got = [x] + [group_exchange(x, "seq", count, offset) for offset in range(1, count)]
+    sent = {offset: group_exchange(x, "seq", count, offset) for offset in range(count - 1, 0, -1)}
+    got = [x] + [sent[offset] for offset in range(1, count)]
     got, tied = lax.optimization_barrier((got, tied))
     total = None
     for source in range(count):
@@ -117,9 +118,11 @@
             out = jnp.where(index == j, blocks[j], out)
         return out
 
-    got = [pick(me)] + [
-        group_exchange(pick(me ^ offset), "seq", count, offset) for offset in range(1, count)
-    ]
+    sent = {
+        offset: group_exchange(pick(me ^ offset), "seq", count, offset)
+        for offset in range(count - 1, 0, -1)
+    }
+    got = [pick(me)] + [sent[offset] for offset in range(1, count)]
     pieces = []
     for source in range(count):
         piece = got[0]

time: 69.8 us -> 69.8 us (level)
  no operation moved by 1% of the time
where the time goes in v15:
time: 69.8 us; the launch traced here: 69.4 us
  starting transfers between devices  23 us (33%)
  matrix products  19.3 us (28%)
  waiting for transfers between devices  10.9 us (16%)
  other arithmetic  8.35 us (12%)
  local copies, waits for them, and re-layouts  6.81 us (10%)
  between operations  1.13 us (2%)
    ppermute x15, starting transfers between devices, group_exchange(): return lax.ppermute(x, axes, [(i, i ^ offset) for i in range(count)])  18 us
    ppermute x15, waiting for transfers between devices, group_exchange(): return lax.ppermute(x, axes, [(i, i ^ offset) for i in range(count)])  10.9 us
    dot_general x1, matrix products, per_device(): jnp.einsum('dr,dmc->mcr', hidden, in_proj, preferred_element_type=jnp.flo...  4.02 us
    dot_general x3, matrix products, inverse_dft(): lax.dot_general(spec * weight, dft, (((1,), (1,)), ((), ())), precision=T...  3.87 us
    unnamed x28, local copies, waits for them, and re-layouts  3.11 us
    ppermute x1, starting transfers between devices, per_device(): lax.ppermute(tokens[row_count - rim_width:], 'seq', [(i, (i + 1) % seq_co...  3.05 us
    dot_general x1, matrix products, per_device(): jnp.einsum('rd,cd->rc', cotangent, out_proj, preferred_element_type=jnp.f...  2.48 us
    dot_general x1, matrix products, per_device(): jnp.einsum('mcr,dmc->rd', d_proj, in_proj, preferred_element_type=jnp.flo...  2.17 us
  transfers between devices with their start and end apart: 18, of which 7 were waited for; matrix products, arithmetic and copies ran while one was open for 32% of the time, Pallas kernels for 0%

profile of v15, /device:TPU:0, one launch (start us, length us, event | category | flops | bytes accessed | tf_op | source)
XLA Modules:
  0.0 69.4 jit_solution(3262839020993647326)
XLA Ops:
  0.6 1.3 %slice.175 = s32[3]{0:T(128)} slice(s32[128]{0:T(128)} %param.17), slice={[125:128]} | slice | bytes 24 | tf_op jit(solution)/shard_map/slice | solution.py:195
  1.9 3.1 %collective-permute-start = (s32[3]{0:T(128)}, s32[3]{0:T(128)}, u32[]{:S(2)}, u32[]{:S(2)}) collective-permute-start(s32[3]{0:T(128)} %slice.175), channel_id=1, source_target_pairs={{0,4},{4,8},{8,12},{12,0},{1,5},{5,9},{9,13},{13,1},{2,6},{6,10},{... | collective-permute-start | bytes 44 | tf_op jit(solution)/shard_map/ppermute | solution.py:194
  5.0 2.5 %fusion.134 = f32[128,2048]{1,0:T(8,128)S(1)} fusion(bf16[128,512]{1,0:T(8,128)(2,1)} %param.23, bf16[2048,512]{1,0:T(8,128)(2,1)} %param.22), kind=kOutput, calls=%fused_computation.244 | convolution fusion | flops 268435456 | bytes 3276800 | tf_op jit(solution)/shard_map/rd,cd->rc/dot_general | solution.py:222
  7.5 0.8 %select_select_fusion = f32[128,512]{1,0:T(8,128)} fusion(f32[128,2048]{1,0:T(8,128)S(1)} %fusion.134, pred[]{:T(512)S(6)} %eq.123, pred[]{:T(512)S(6)} %eq.122, pred[]{:T(512)S(6)} %eq.121), kind=kLoop, calls=%fused_computation.114 | loop fusion | flops 196608 | bytes 1310723 | tf_op jit(solution)/shard_map/jit(_where)/select_n | solution.py:76
  8.3 0.6 collective-permute-start.3
  8.9 0.9 %select_select_fusion.2 = (f32[128,512]{1,0:T(8,128)}, f32[128,512]{1,0:T(8,128)}) fusion(f32[128,2048]{1,0:T(8,128)S(1)} %fusion.134, pred[]{:T(512)S(6)} %eq.117, pred[]{:T(512)S(6)} %eq.116, pred[]{:T(512)S(6)} %eq.115, pred[]{:T(512)S(6)} %eq.120, pred[]{:T(512)S(6)} %eq.119, pred[]{:T(512)S(6)} %eq.118), kind=kLoop, calls=%fused_computation.116 | loop fusion | flops 393216 | bytes 1572870 | tf_op jit(solution)/shard_map/jit(_where)/select_n | solution.py:76
  9.8 1.0 %collective-permute-start.1 = (f32[128,512]{1,0:T(8,128)}, f32[128,512]{1,0:T(8,128)}, u32[]{:S(2)}, u32[]{:S(2)}) collective-permute-start(f32[128,512]{1,0:T(8,128)} %get-tuple-element.68), channel_id=1, source_target_pairs={{0,1},{1,0},{2,3},{3,2},{4,5},{5,4},{6,7},{7,6},{8,9},{9,8},{10,11... | collective-permute-start | bytes 786440 | tf_op jit(solution)/shard_map/ppermute | solution.py:64
  10.8 0.5 collective-permute-start.2
  11.7 0.6 fusion.100
  12.6 0.7 %convolution_bitcast_fusion.2 = f32[128,1024]{1,0:T(8,128)S(1)} fusion(f32[512,1024]{1,0:T(8,128)S(1)} %bitcast.153, f32[1,1,128,512]{3,2,1,0:T(8,128)S(1)} %copy-done), kind=kOutput, calls=%fused_computation.7 | convolution fusion | flops 402653184 | bytes 2883584 | tf_op jit(solution)/shard_map/dot_general | solution.py:136
  13.4 0.8 %copy-done.1 = f32[128,1024]{1,0:T(8,128)} copy-done((f32[128,1024]{1,0:T(8,128)}, f32[128,1024]{1,0:T(8,128)S(1)}, u32[]{:S(2)}) %copy-start.1) | copy-done | bytes 524312
  14.1 1.1 %fusion.132 = (f32[127,1024]{1,0:T(8,128)}, f32[127,1024]{1,0:T(8,128)}) fusion(f32[128,1024]{1,0:T(8,128)S(1)} %convolution_bitcast_fusion.2), kind=kLoop, calls=%fused_computation.242 | loop fusion | bytes 2080768 | tf_op jit(solution)/shard_map/jit(_roll_static)/slice | solution.py:171
  15.2 0.9 %copy.28 = bf16[4,5,2048]{2,1,0:T(8,128)(2,1)S(1)} copy(bf16[4,5,2048]{2,0,1:T(4,128)(2,1)} %param.18) | data formatting | bytes 163840 | tf_op args[1]
  16.1 0.7 reshape.243
  16.8 1.4 %maximum_select_fusion = f32[128,1024]{1,0:T(8,128)S(1)} fusion(f32[1,1024]{1,0:T(1,128)S(1)} %get-tuple-element.77, f32[127,1024]{1,0:T(8,128)} %get-tuple-element.79, f32[127,1024]{1,0:T(8,128)} %get-tuple-element.78, f32[1,1024]{1,0:T(1,128)S(1)} %get-tuple-element.76, pred[128]{0:T(512)(128)(4,1)} %constant.92), kind=kLoop, calls=%fused_computation.38 | loop fusion | flops 393216 | bytes 1572992 | tf_op jit(solution)/shard_map/jit(_where)/select_n | solution.py:172
  18.2 1.1 %slice_add_fusion.1 = (f32[128,512]{1,0:T(8,128)S(1)}, f32[128,512]{1,0:T(8,128)S(1)}) fusion(f32[128,1024]{1,0:T(8,128)S(1)} %maximum_select_fusion, f32[128,1024]{1,0:T(8,128)} %copy-done.1, pred[512]{0:T(512)(128)(4,1)S(1)} %copy-done.7), kind=kLoop, calls=%fused_computation.94 | loop fusion | flops 262144 | bytes 1573376 | tf_op jit(solution)/shard_map/add | solution.py:179
  19.6 0.4 multiply_reduce_fusion
  20.1 4.0 %convolution_bitcast_fusion.1 = f32[3,512,128]{1,2,0:T(8,128)S(1)} fusion(bf16[2048,3,512]{2,0,1:T(8,128)(2,1)} %param.20, f32[128,2048]{1,0:T(8,128)S(1)} %get-tuple-element.104, f32[2048]{0:T(1024)S(1)} %copy-done.5, f32[128]{0:T(128)S(1)} %add_rsqrt_fusion), kind=kOutput, calls=%fused_computation.5 | convolution fusion | flops 806092800 | bytes 8135168 | tf_op jit(solution)/shard_map/dr,dmc->mcr/dot_general | solution.py:211
  24.2 1.3 %fusion.55 = (bf16[1,512,128]{1,2,0:T(8,128)(2,1)S(1)}, f32[128,512]{1,0:T(8,128)S(1)}) fusion(f32[3,512,128]{1,2,0:T(8,128)S(1)} %convolution_bitcast_fusion.1, f32[128,512]{1,0:T(8,128)} %collective-permute-done.3, f32[128,512]{1,0:T(8,128)} %collective-permute-done.2, f32[128,512]{1,0:T(8,128)} %collective-permute-done.1, f32[128,2048]{1,0:T(8,128)S(1)} %fusion.134, ...), kind=kLoop, calls=%fused_computation.129 | loop fusion | flops 589824 | bytes 2490371 | tf_op jit(solution)/shard_map/stack | solution.py:228
  25.6 2.3 %collective-permute-start.6 = (bf16[2,128,128]{1,2,0:T(8,128)(2,1)S(1)}, bf16[2,128,128]{1,2,0:T(8,128)(2,1)S(1)}, u32[]{:S(2)}, u32[]{:S(2)}) collective-permute-start(bf16[2,128,128]{1,2,0:T(8,128)(2,1)S(1)} %get-tuple-element.50), channel_id=1, source_target_pairs={{0,4},{4,0},{8,12},{12,8},{1,5},{5,1},{9,13},{13,9},{2,6},{6,2},{1... | collective-permute-start | bytes 196616 | tf_op jit(solution)/shard_map/ppermute | solution.py:64
  27.9 1.1 %collective-permute-start.5 = (bf16[2,128,128]{1,2,0:T(8,128)(2,1)S(1)}, bf16[2,128,128]{1,2,0:T(8,128)(2,1)S(1)}, u32[]{:S(2)}, u32[]{:S(2)}) collective-permute-start(bf16[2,128,128]{1,2,0:T(8,128)(2,1)S(1)} %get-tuple-element.90), channel_id=1, source_target_pairs={{0,8},{4,12},{8,0},{12,4},{1,9},{5,13},{9,1},{13,5},{2,10},{6,14},... | collective-permute-start | bytes 196616 | tf_op jit(solution)/shard_map/ppermute | solution.py:64
  29.0 1.5 %collective-permute-start.4 = (bf16[2,128,128]{1,2,0:T(8,128)(2,1)S(1)}, bf16[2,128,128]{1,2,0:T(8,128)(2,1)S(1)}, u32[]{:S(2)}, u32[]{:S(2)}) collective-permute-start(bf16[2,128,128]{1,2,0:T(8,128)(2,1)S(1)} %get-tuple-element.91), channel_id=1, source_target_pairs={{0,12},{4,8},{8,4},{12,0},{1,13},{5,9},{9,5},{13,1},{2,14},{6,10},... | collective-permute-start | bytes 196616 | tf_op jit(solution)/shard_map/ppermute | solution.py:64
  30.5 1.1 %fusion.1 = f32[3,512,128]{1,2,0:T(8,128)S(1)} fusion(f32[3,512,128]{1,2,0:T(8,128)S(1)} %convolution_bitcast_fusion.1, bf16[2048,3,512]{2,0,1:T(8,128)(2,1)S(1)} %bitcast.160, f32[128,2048]{1,0:T(8,128)S(1)} %get-tuple-element.104, f32[2048]{0:T(1024)S(1)} %copy-done.5, f32[128]{0:T(128)S(1)} %add_rsqrt_fusion), kind=kOutput, calls=%fused_computation.6 | convolution fusion | flops 807075840 | bytes 8921600 | tf_op jit(solution)/shard_map/dr,dmc->mcr/dot_general | solution.py:213
  31.6 4.2 %collective-permute-done.5 = bf16[2,128,128]{1,2,0:T(8,128)(2,1)S(1)} collective-permute-done((bf16[2,128,128]{1,2,0:T(8,128)(2,1)S(1)}, bf16[2,128,128]{1,2,0:T(8,128)(2,1)S(1)}, u32[]{:S(2)}, u32[]{:S(2)}) %collective-permute-start.5) | collective-permute-done | bytes 65568 | tf_op jit(solution)/shard_map/ppermute | solution.py:64
  35.9 0.6 fusion.71
  36.4 0.6 fusion.73
  38.4 1.0 %fusion.6 = bf16[1,128,512]{1,2,0:T(8,128)(2,1)S(1)} fusion(f32[512,1024]{1,0:T(8,128)S(1)} %bitcast.156, f32[128,512]{1,0:T(8,128)S(1)} %get-tuple-element.70, f32[128,512]{1,0:T(8,128)S(1)} %get-tuple-element.71, f32[1024]{0:T(1024)S(1)} %copy-done.6), kind=kOutput, calls=%fused_computation.15 | convolution fusion | flops 402980864 | bytes 2756608 | tf_op jit(solution)/shard_map/dot_general | solution.py:144
  39.4 1.0 %fusion.7 = bf16[1,128,512]{1,2,0:T(8,128)(2,1)S(1)} fusion(f32[512,1024]{1,0:T(8,128)S(1)} %bitcast.157, f32[128,512]{1,0:T(8,128)S(1)} %get-tuple-element.101, f32[128,512]{1,0:T(8,128)S(1)} %get-tuple-element.102, f32[1024]{0:T(1024)S(1)} %copy-done.6), kind=kOutput, calls=%fused_computation.16 | convolution fusion | flops 402980864 | bytes 2756608 | tf_op jit(solution)/shard_map/dot_general | solution.py:144
  40.4 1.3 %collective-permute-start.9 = (bf16[2,128,128]{1,2,0:T(8,128)(2,1)S(1)}, bf16[2,128,128]{1,2,0:T(8,128)(2,1)S(1)}, u32[]{:S(2)}, u32[]{:S(2)}) collective-permute-start(bf16[2,128,128]{1,2,0:T(8,128)(2,1)S(1)} %get-tuple-element.43), channel_id=1, source_target_pairs={{0,4},{4,0},{8,12},{12,8},{1,5},{5,1},{9,13},{13,9},{2,6},{6,2},{1... | collective-permute-start | bytes 196616 | tf_op jit(solution)/shard_map/ppermute | solution.py:64
  41.8 1.6 %collective-permute-start.8 = (bf16[2,128,128]{1,2,0:T(8,128)(2,1)S(1)}, bf16[2,128,128]{1,2,0:T(8,128)(2,1)S(1)}, u32[]{:S(2)}, u32[]{:S(2)}) collective-permute-start(bf16[2,128,128]{1,2,0:T(8,128)(2,1)S(1)} %get-tuple-element.85), channel_id=1, source_target_pairs={{0,8},{4,12},{8,0},{12,4},{1,9},{5,13},{9,1},{13,5},{2,10},{6,14},... | collective-permute-start | bytes 196616 | tf_op jit(solution)/shard_map/ppermute | solution.py:64
  43.4 1.5 %collective-permute-start.7 = (bf16[2,128,128]{1,2,0:T(8,128)(2,1)S(1)}, bf16[2,128,128]{1,2,0:T(8,128)(2,1)S(1)}, u32[]{:S(2)}, u32[]{:S(2)}) collective-permute-start(bf16[2,128,128]{1,2,0:T(8,128)(2,1)S(1)} %get-tuple-element.86), channel_id=1, source_target_pairs={{0,12},{4,8},{8,4},{12,0},{1,13},{5,9},{9,5},{13,1},{2,14},{6,10},... | collective-permute-start | bytes 196616 | tf_op jit(solution)/shard_map/ppermute | solution.py:64
  45.2 3.1 %collective-permute-done.8 = bf16[2,128,128]{1,2,0:T(8,128)(2,1)S(1)} collective-permute-done((bf16[2,128,128]{1,2,0:T(8,128)(2,1)S(1)}, bf16[2,128,128]{1,2,0:T(8,128)(2,1)S(1)}, u32[]{:S(2)}, u32[]{:S(2)}) %collective-permute-start.8) | collective-permute-done | bytes 65568 | tf_op jit(solution)/shard_map/ppermute | solution.py:64
  48.3 1.3 %collective-permute-done.7 = bf16[2,128,128]{1,2,0:T(8,128)(2,1)S(1)} collective-permute-done((bf16[2,128,128]{1,2,0:T(8,128)(2,1)S(1)}, bf16[2,128,128]{1,2,0:T(8,128)(2,1)S(1)}, u32[]{:S(2)}, u32[]{:S(2)}) %collective-permute-start.7) | collective-permute-done | bytes 65568 | tf_op jit(solution)/shard_map/ppermute | solution.py:64
  49.9 2.2 %fusion.8 = (f32[2048]{0:T(1024)S(1)}, f32[128,2048,1]{1,0,2:T(8,128)S(1)}) fusion(f32[128,2048]{1,0:T(8,128)S(1)} %get-tuple-element.104, f32[128]{0:T(128)S(1)} %add_rsqrt_fusion, bf16[2048,3,512]{2,0,1:T(8,128)(2,1)S(1)} %bitcast.160, bf16[1,512,128]{1,2,0:T(8,128)(2,1)S(1)} %get-tuple-element.65, bf16[1,512,128]{1,2,0:T(8,128)(2,1)S(1)} %get-tuple-element.64, ...), kind=kOutput, calls=%fused_computation.18 | convolution fusion | flops 806483968 | bytes 8790528 | tf_op jit(solution)/shard_map/mcr,dmc->rd/dot_general | solution.py:265
  52.2 1.5 %collective-permute-start.16 = (bf16[1,512,128]{1,2,0:T(8,128)(2,1)S(1)}, bf16[1,512,128]{1,2,0:T(8,128)(2,1)S(1)}, u32[]{:S(2)}, u32[]{:S(2)}) collective-permute-start(bf16[1,512,128]{1,2,0:T(8,128)(2,1)S(1)} %get-tuple-element.63), channel_id=1, source_target_pairs={{0,2},{2,0},{1,3},{3,1},{4,6},{6,4},{5,7},{7,5},{8,10},{10,8},{9,1... | collective-permute-start | bytes 393224 | tf_op jit(solution)/shard_map/ppermute | solution.py:47
  53.8 0.8 %convolution_multiply_fusion.1 = f32[20,2048]{1,0:T(8,128)S(1)} fusion(f32[128,2048,1]{1,0,2:T(8,128)S(1)} %get-tuple-element.106, f32[2048]{0:T(1024)S(1)} %copy-done.5, f32[128]{0:T(128)S(1)} %add_rsqrt_fusion, pred[128,5]{0,1:T(8,128)(4,1)S(1)} %get-tuple-element.107, pred[128,5]{0,1:T(8,128)(4,1)S(1)} %get-tuple-element.108, ...), kind=kOutput, calls=%fused_computation.2 | convolution fusion | flops 62970880 | bytes 1223680 | tf_op jit(solution)/shard_map/rk,rd->kd/dot_general | solution.py:269
  54.6 0.7 %fusion = f32[20,2048]{1,0:T(8,128)S(1)} fusion(f32[20,2048]{1,0:T(8,128)S(1)} %convolution_multiply_fusion.1, f32[128,2048]{1,0:T(8,128)S(1)} %get-tuple-element.104, f32[128]{0:T(128)S(1)} %add_rsqrt_fusion, f32[128]{0:T(128)S(1)} %multiply_reduce_fusion.1, pred[128,5]{0,1:T(8,128)(4,1)S(1)} %get-tuple-element.107, ...), kind=kOutput, calls=%fused_computation.1 | convolution fusion | flops 63276544 | bytes 1379840 | tf_op jit(solution)/shard_map/rk,dr->kd/dot_general | solution.py:270
  55.4 0.6 collective-permute-start.11
  56.0 1.3 %collective-permute-start.12 = (f32[21,512]{1,0:T(8,128)S(1)}, f32[21,512]{1,0:T(8,128)S(1)}, u32[]{:S(2)}, u32[]{:S(2)}) collective-permute-start(f32[21,512]{1,0:T(8,128)S(1)} %get-tuple-element.93), channel_id=1, source_target_pairs={{0,3},{1,2},{2,1},{3,0},{4,7},{5,6},{6,5},{7,4},{8,11},{9,10},{10,... | collective-permute-start | bytes 129032 | tf_op jit(solution)/shard_map/ppermute | solution.py:64
  57.8 1.9 %fusion.23 = f32[128,512]{1,0:T(8,128)} fusion(f32[512,1024]{1,0:T(8,128)S(1)} %bitcast.158, f32[128,512]{1,0:T(8,128)S(1)} %get-tuple-element.73, f32[128,512]{1,0:T(8,128)S(1)} %get-tuple-element.72, f32[1024]{0:T(1024)S(1)} %copy-done.6), kind=kOutput, calls=%fused_computation.47 | convolution fusion | flops 402915328 | bytes 2887680 | tf_op jit(solution)/shard_map/dot_general | solution.py:144
  59.6 0.5 collective-permute-done.11
  60.2 1.6 %collective-permute-start.15 = (f32[21,512]{1,0:T(8,128)S(1)}, f32[21,512]{1,0:T(8,128)S(1)}, u32[]{:S(2)}, u32[]{:S(2)}) collective-permute-start(f32[21,512]{1,0:T(8,128)S(1)} %pad_add_fusion), channel_id=1, source_target_pairs={{0,12},{4,8},{8,4},{12,0},{1,13},{5,9},{9,5},{13,1},{2,14},{6,10},... | collective-permute-start | bytes 129032 | tf_op jit(solution)/shard_map/ppermute | solution.py:64
  61.9 0.6 collective-permute-start.14
  62.4 2.3 %collective-permute-start.13 = (f32[21,512]{1,0:T(8,128)S(1)}, f32[21,512]{1,0:T(8,128)S(1)}, u32[]{:S(2)}, u32[]{:S(2)}) collective-permute-start(f32[21,512]{1,0:T(8,128)S(1)} %pad_add_fusion), channel_id=1, source_target_pairs={{0,4},{4,0},{8,12},{12,8},{1,5},{5,1},{9,13},{13,9},{2,6},{6,2},{1... | collective-permute-start | bytes 129032 | tf_op jit(solution)/shard_map/ppermute | solution.py:64
  65.5 0.9 %fusion.5 = bf16[128,512]{1,0:T(8,128)(2,1)} fusion(f32[128,512]{1,0:T(8,128)S(1)} %fusion.26, f32[128,512]{1,0:T(8,128)S(1)} %fusion.28, f32[128,512]{1,0:T(8,128)S(1)} %fusion.30, bf16[2048,512]{1,0:T(8,128)(2,1)S(1)} %copy-done.2, f32[128,2048]{1,0:T(8,128)S(1)} %get-tuple-element.104, s32[]{:T(128)S(6)} %select_n.782, ...), kind=kOutput, calls=%fused_computation.14 | convolution fusion | flops 67633152 | bytes 2228231 | tf_op jit(solution)/shard_map/cr,cd->rd/dot_general | solution.py:250
  66.7 1.5 %collective-permute-done.14 = f32[21,512]{1,0:T(8,128)S(1)} collective-permute-done((f32[21,512]{1,0:T(8,128)S(1)}, f32[21,512]{1,0:T(8,128)S(1)}, u32[]{:S(2)}, u32[]{:S(2)}) %collective-permute-start.14) | collective-permute-done | bytes 43040 | tf_op jit(solution)/shard_map/ppermute | solution.py:64
  68.2 0.6 slice.280
  68.8 0.6 copy.31
  (85 shorter events, 4.9 us)
Async XLA Ops:
  0.6 12.0 %copy-start = (f32[1,1,128,512]{3,2,1,0:T(8,128)S(1)}, f32[1,1,128,512]{3,2,1,0:T(8,128)}, u32[]{:S(2)}) copy-start(f32[1,1,128,512]{3,2,1,0:T(8,128)} %param.21) | copy-start | bytes 786436
  1.9 17.4 %collective-permute-start = (s32[3]{0:T(128)}, s32[3]{0:T(128)}, u32[]{:S(2)}, u32[]{:S(2)}) collective-permute-start(s32[3]{0:T(128)} %slice.175), channel_id=1, source_target_pairs={{0,4},{4,8},{8,12},{12,0},{1,5},{5,9},{9,13},{13,1},{2,6},{6,10},{... | collective-permute-start | bytes 44 | tf_op jit(solution)/shard_map/ppermute | solution.py:194
  7.5 3.8 %copy-start.9 = (s32[128]{0:T(128)S(1)}, s32[128]{0:T(128)}, u32[]{:S(2)}) copy-start(s32[128]{0:T(128)} %param.17) | copy-start | bytes 1540
  8.3 15.9 %collective-permute-start.3 = (f32[128,512]{1,0:T(8,128)}, f32[128,512]{1,0:T(8,128)}, u32[]{:S(2)}, u32[]{:S(2)}) collective-permute-start(f32[128,512]{1,0:T(8,128)} %select_select_fusion), channel_id=1, source_target_pairs={{0,3},{1,2},{2,1},{3,0},{4,7},{5,6},{6,5},{7,4},{8,11},{9,10},{10,... | collective-permute-start | bytes 786440 | tf_op jit(solution)/shard_map/ppermute | solution.py:64
  9.8 14.3 %collective-permute-start.1 = (f32[128,512]{1,0:T(8,128)}, f32[128,512]{1,0:T(8,128)}, u32[]{:S(2)}, u32[]{:S(2)}) collective-permute-start(f32[128,512]{1,0:T(8,128)} %get-tuple-element.68), channel_id=1, source_target_pairs={{0,1},{1,0},{2,3},{3,2},{4,5},{5,4},{6,7},{7,6},{8,9},{9,8},{10,11... | collective-permute-start | bytes 786440 | tf_op jit(solution)/shard_map/ppermute | solution.py:64
  10.8 13.4 %collective-permute-start.2 = (f32[128,512]{1,0:T(8,128)}, f32[128,512]{1,0:T(8,128)}, u32[]{:S(2)}, u32[]{:S(2)}) collective-permute-start(f32[128,512]{1,0:T(8,128)} %get-tuple-element.69), channel_id=1, source_target_pairs={{0,2},{1,3},{2,0},{3,1},{4,6},{5,7},{6,4},{7,5},{8,10},{9,11},{10,... | collective-permute-start | bytes 786440 | tf_op jit(solution)/shard_map/ppermute | solution.py:64
  13.3 0.8 %copy-start.1 = (f32[128,1024]{1,0:T(8,128)}, f32[128,1024]{1,0:T(8,128)S(1)}, u32[]{:S(2)}) copy-start(f32[128,1024]{1,0:T(8,128)S(1)} %convolution_bitcast_fusion.2) | copy-start | bytes 1572868
  13.3 4.8 %copy-start.7 = (pred[512]{0:T(512)(128)(4,1)S(1)}, pred[512]{0:T(512)(128)(4,1)}, u32[]{:S(2)}) copy-start(pred[512]{0:T(512)(128)(4,1)} %constant.91) | copy-start | bytes 1540
  16.8 2.6 %copy-start.10 = (s32[128]{0:T(128)S(1)}, s32[128]{0:T(128)}, u32[]{:S(2)}) copy-start(s32[128]{0:T(128)} %param.17) | copy-start | bytes 1540
  16.8 2.8 %copy-start.4 = (bf16[20,2048]{1,0:T(8,128)(2,1)S(1)}, bf16[20,2048]{1,0:T(8,128)(2,1)}, u32[]{:S(2)}) copy-start(bf16[20,2048]{1,0:T(8,128)(2,1)} %reshape.243) | copy-start | bytes 245764
  18.2 1.9 %copy-start.5 = (f32[2048]{0:T(1024)S(1)}, f32[2048]{0:T(1024)}, u32[]{:S(2)}) copy-start(f32[2048]{0:T(1024)} %param.19) | copy-start | bytes 24580
  20.0 10.5 %slice-start = ((s8[6291456]{0:T(1024)(128)(4,1)}), s8[4194304]{0:T(1024)(128)(4,1)S(1)}, s32[]{:S(2)}) async-start(s8[6291456]{0:T(1024)(128)(4,1)} %bitcast.159), calls=%async_computation | async-start | bytes 8388608
  20.0 10.4 %slice-start.1 = ((s8[6291456]{0:T(1024)(128)(4,1)}), s8[2097152]{0:T(1024)(128)(4,1)S(1)}, s32[]{:S(2)}) async-start(s8[6291456]{0:T(1024)(128)(4,1)} %bitcast.159), calls=%async_computation.1 | async-start | bytes 4194304
  25.6 6.0 %collective-permute-start.6 = (bf16[2,128,128]{1,2,0:T(8,128)(2,1)S(1)}, bf16[2,128,128]{1,2,0:T(8,128)(2,1)S(1)}, u32[]{:S(2)}, u32[]{:S(2)}) collective-permute-start(bf16[2,128,128]{1,2,0:T(8,128)(2,1)S(1)} %get-tuple-element.50), channel_id=1, source_target_pairs={{0,4},{4,0},{8,12},{12,8},{1,5},{5,1},{9,13},{13,9},{2,6},{6,2},{1... | collective-permute-start | bytes 196616 | tf_op jit(solution)/shard_map/ppermute | solution.py:64
  27.9 7.9 %collective-permute-start.5 = (bf16[2,128,128]{1,2,0:T(8,128)(2,1)S(1)}, bf16[2,128,128]{1,2,0:T(8,128)(2,1)S(1)}, u32[]{:S(2)}, u32[]{:S(2)}) collective-permute-start(bf16[2,128,128]{1,2,0:T(8,128)(2,1)S(1)} %get-tuple-element.90), channel_id=1, source_target_pairs={{0,8},{4,12},{8,0},{12,4},{1,9},{5,13},{9,1},{13,5},{2,10},{6,14},... | collective-permute-start | bytes 196616 | tf_op jit(solution)/shard_map/ppermute | solution.py:64
  29.0 6.8 %collective-permute-start.4 = (bf16[2,128,128]{1,2,0:T(8,128)(2,1)S(1)}, bf16[2,128,128]{1,2,0:T(8,128)(2,1)S(1)}, u32[]{:S(2)}, u32[]{:S(2)}) collective-permute-start(bf16[2,128,128]{1,2,0:T(8,128)(2,1)S(1)} %get-tuple-element.91), channel_id=1, source_target_pairs={{0,12},{4,8},{8,4},{12,0},{1,13},{5,9},{9,5},{13,1},{2,14},{6,10},... | collective-permute-start | bytes 196616 | tf_op jit(solution)/shard_map/ppermute | solution.py:64
  37.0 0.7 copy-start.8
  37.7 0.7 copy-start.6
  39.4 5.6 %copy-start.3 = (bf16[128,512]{1,0:T(8,128)(2,1)S(1)}, bf16[128,512]{1,0:T(8,128)(2,1)}, u32[]{:S(2)}) copy-start(bf16[128,512]{1,0:T(8,128)(2,1)} %param.23) | copy-start | bytes 393220
  40.4 4.8 %collective-permute-start.9 = (bf16[2,128,128]{1,2,0:T(8,128)(2,1)S(1)}, bf16[2,128,128]{1,2,0:T(8,128)(2,1)S(1)}, u32[]{:S(2)}, u32[]{:S(2)}) collective-permute-start(bf16[2,128,128]{1,2,0:T(8,128)(2,1)S(1)} %get-tuple-element.43), channel_id=1, source_target_pairs={{0,4},{4,0},{8,12},{12,8},{1,5},{5,1},{9,13},{13,9},{2,6},{6,2},{1... | collective-permute-start | bytes 196616 | tf_op jit(solution)/shard_map/ppermute | solution.py:64
  41.8 6.5 %collective-permute-start.8 = (bf16[2,128,128]{1,2,0:T(8,128)(2,1)S(1)}, bf16[2,128,128]{1,2,0:T(8,128)(2,1)S(1)}, u32[]{:S(2)}, u32[]{:S(2)}) collective-permute-start(bf16[2,128,128]{1,2,0:T(8,128)(2,1)S(1)} %get-tuple-element.85), channel_id=1, source_target_pairs={{0,8},{4,12},{8,0},{12,4},{1,9},{5,13},{9,1},{13,5},{2,10},{6,14},... | collective-permute-start | bytes 196616 | tf_op jit(solution)/shard_map/ppermute | solution.py:64
  43.4 6.2 %collective-permute-start.7 = (bf16[2,128,128]{1,2,0:T(8,128)(2,1)S(1)}, bf16[2,128,128]{1,2,0:T(8,128)(2,1)S(1)}, u32[]{:S(2)}, u32[]{:S(2)}) collective-permute-start(bf16[2,128,128]{1,2,0:T(8,128)(2,1)S(1)} %get-tuple-element.86), channel_id=1, source_target_pairs={{0,12},{4,8},{8,4},{12,0},{1,13},{5,9},{9,5},{13,1},{2,14},{6,10},... | collective-permute-start | bytes 196616 | tf_op jit(solution)/shard_map/ppermute | solution.py:64
  52.2 5.1 %collective-permute-start.16 = (bf16[1,512,128]{1,2,0:T(8,128)(2,1)S(1)}, bf16[1,512,128]{1,2,0:T(8,128)(2,1)S(1)}, u32[]{:S(2)}, u32[]{:S(2)}) collective-permute-start(bf16[1,512,128]{1,2,0:T(8,128)(2,1)S(1)} %get-tuple-element.63), channel_id=1, source_target_pairs={{0,2},{2,0},{1,3},{3,1},{4,6},{6,4},{5,7},{7,5},{8,10},{10,8},{9,1... | collective-permute-start | bytes 393224 | tf_op jit(solution)/shard_map/ppermute | solution.py:47
  55.3 9.4 %copy-start.2 = (bf16[2048,512]{1,0:T(8,128)(2,1)S(1)}, bf16[2048,512]{1,0:T(8,128)(2,1)}, u32[]{:S(2)}) copy-start(bf16[2048,512]{1,0:T(8,128)(2,1)} %param.22) | copy-start | bytes 6291460
  55.3 4.3 %collective-permute-start.10 = (f32[21,512]{1,0:T(8,128)S(1)}, f32[21,512]{1,0:T(8,128)S(1)}, u32[]{:S(2)}, u32[]{:S(2)}) collective-permute-start(f32[21,512]{1,0:T(8,128)S(1)} %get-tuple-element.36), channel_id=1, source_target_pairs={{0,1},{1,0},{2,3},{3,2},{4,5},{5,4},{6,7},{7,6},{8,9},{9,8},{10,11... | collective-permute-start | bytes 129032 | tf_op jit(solution)/shard_map/ppermute | solution.py:64
  55.4 4.7 %collective-permute-start.11 = (f32[21,512]{1,0:T(8,128)S(1)}, f32[21,512]{1,0:T(8,128)S(1)}, u32[]{:S(2)}, u32[]{:S(2)}) collective-permute-start(f32[21,512]{1,0:T(8,128)S(1)} %get-tuple-element.92), channel_id=1, source_target_pairs={{0,2},{1,3},{2,0},{3,1},{4,6},{5,7},{6,4},{7,5},{8,10},{9,11},{10,... | collective-permute-start | bytes 129032 | tf_op jit(solution)/shard_map/ppermute | solution.py:64
  56.0 4.2 %collective-permute-start.12 = (f32[21,512]{1,0:T(8,128)S(1)}, f32[21,512]{1,0:T(8,128)S(1)}, u32[]{:S(2)}, u32[]{:S(2)}) collective-permute-start(f32[21,512]{1,0:T(8,128)S(1)} %get-tuple-element.93), channel_id=1, source_target_pairs={{0,3},{1,2},{2,1},{3,0},{4,7},{5,6},{6,5},{7,4},{8,11},{9,10},{10,... | collective-permute-start | bytes 129032 | tf_op jit(solution)/shard_map/ppermute | solution.py:64
  57.4 7.3 %collective-permute-start.17 = (bf16[2,512,128]{1,2,0:T(8,128)(2,1)S(1)}, bf16[2,512,128]{1,2,0:T(8,128)(2,1)S(1)}, u32[]{:S(2)}, u32[]{:S(2)}) collective-permute-start(bf16[2,512,128]{1,2,0:T(8,128)(2,1)S(1)} %pad_maximum_fusion.5), channel_id=1, source_target_pairs={{0,1},{1,0},{2,3},{3,2},{4,5},{5,4},{6,7},{7,6},{8,9},{9,8},{10,11... | collective-permute-start | bytes 786440 | tf_op jit(solution)/shard_map/ppermute | solution.py:47
  60.2 6.4 %collective-permute-start.15 = (f32[21,512]{1,0:T(8,128)S(1)}, f32[21,512]{1,0:T(8,128)S(1)}, u32[]{:S(2)}, u32[]{:S(2)}) collective-permute-start(f32[21,512]{1,0:T(8,128)S(1)} %pad_add_fusion), channel_id=1, source_target_pairs={{0,12},{4,8},{8,4},{12,0},{1,13},{5,9},{9,5},{13,1},{2,14},{6,10},... | collective-permute-start | bytes 129032 | tf_op jit(solution)/shard_map/ppermute | solution.py:64
  61.9 6.3 %collective-permute-start.14 = (f32[21,512]{1,0:T(8,128)S(1)}, f32[21,512]{1,0:T(8,128)S(1)}, u32[]{:S(2)}, u32[]{:S(2)}) collective-permute-start(f32[21,512]{1,0:T(8,128)S(1)} %pad_add_fusion), channel_id=1, source_target_pairs={{0,8},{4,12},{8,0},{12,4},{1,9},{5,13},{9,1},{13,5},{2,10},{6,14},... | collective-permute-start | bytes 129032 | tf_op jit(solution)/shard_map/ppermute | solution.py:64
  62.4 5.8 %collective-permute-start.13 = (f32[21,512]{1,0:T(8,128)S(1)}, f32[21,512]{1,0:T(8,128)S(1)}, u32[]{:S(2)}, u32[]{:S(2)}) collective-permute-start(f32[21,512]{1,0:T(8,128)S(1)} %pad_add_fusion), channel_id=1, source_target_pairs={{0,4},{4,0},{8,12},{12,8},{1,5},{5,1},{9,13},{13,9},{2,6},{6,2},{1... | collective-permute-start | bytes 129032 | tf_op jit(solution)/shard_map/ppermute | solution.py:64

commit v16 on v15

--- a/solution.py
+++ b/solution.py
@@ -76,9 +76,13 @@
             out = jnp.where(index == g, blocks[g], out)
         return out
 
+    sent = {
+        offset: group_exchange(pick(me ^ offset), axes, count, offset)
+        for offset in range(count - 1, 0, -1)
+    }
     total = pick(me)
     for offset in range(1, count):
-        total = total + group_exchange(pick(me ^ offset), axes, count, offset)
+        total = total + sent[offset]
     return total
 
 

time: 69.8 us -> 69.8 us (level)
  no operation moved by 1% of the time
where the time goes in v16:
time: 69.8 us; the launch traced here: 69.4 us
  starting transfers between devices  23 us (33%)
  matrix products  19.3 us (28%)
  waiting for transfers between devices  10.9 us (16%)
  other arithmetic  8.35 us (12%)
  local copies, waits for them, and re-layouts  6.81 us (10%)
  between operations  1.13 us (2%)
    ppermute x15, starting transfers between devices, group_exchange(): return lax.ppermute(x, axes, [(i, i ^ offset) for i in range(count)])  18 us
    ppermute x15, waiting for transfers between devices, group_exchange(): return lax.ppermute(x, axes, [(i, i ^ offset) for i in range(count)])  10.9 us
    dot_general x1, matrix products, per_device(): jnp.einsum('dr,dmc->mcr', hidden, in_proj, preferred_element_type=jnp.flo...  4.02 us
    dot_general x3, matrix products, inverse_dft(): lax.dot_general(spec * weight, dft, (((1,), (1,)), ((), ())), precision=T...  3.87 us
    unnamed x28, local copies, waits for them, and re-layouts  3.11 us
    ppermute x1, starting transfers between devices, per_device(): lax.ppermute(tokens[row_count - rim_width:], 'seq', [(i, (i + 1) % seq_co...  3.05 us
    dot_general x1, matrix products, per_device(): jnp.einsum('rd,cd->rc', cotangent, out_proj, preferred_element_type=jnp.f...  2.48 us
    dot_general x1, matrix products, per_device(): jnp.einsum('mcr,dmc->rd', d_proj, in_proj, preferred_element_type=jnp.flo...  2.17 us
  transfers between devices with their start and end apart: 18, of which 7 were waited for; matrix products, arithmetic and copies ran while one was open for 32% of the time, Pallas kernels for 0%

profile of v16, /device:TPU:0, one launch (start us, length us, event | category | flops | bytes accessed | tf_op | source)
XLA Modules:
  0.0 69.4 jit_solution(3262839020993647326)
XLA Ops:
  0.6 1.3 %slice.175 = s32[3]{0:T(128)} slice(s32[128]{0:T(128)} %param.17), slice={[125:128]} | slice | bytes 24 | tf_op jit(solution)/shard_map/slice | solution.py:199
  1.9 3.1 %collective-permute-start = (s32[3]{0:T(128)}, s32[3]{0:T(128)}, u32[]{:S(2)}, u32[]{:S(2)}) collective-permute-start(s32[3]{0:T(128)} %slice.175), channel_id=1, source_target_pairs={{0,4},{4,8},{8,12},{12,0},{1,5},{5,9},{9,13},{13,1},{2,6},{6,10},{... | collective-permute-start | bytes 44 | tf_op jit(solution)/shard_map/ppermute | solution.py:198
  5.0 2.5 %fusion.134 = f32[128,2048]{1,0:T(8,128)S(1)} fusion(bf16[128,512]{1,0:T(8,128)(2,1)} %param.23, bf16[2048,512]{1,0:T(8,128)(2,1)} %param.22), kind=kOutput, calls=%fused_computation.244 | convolution fusion | flops 268435456 | bytes 3276800 | tf_op jit(solution)/shard_map/rd,cd->rc/dot_general | solution.py:226
  7.5 0.8 %select_select_fusion = f32[128,512]{1,0:T(8,128)} fusion(f32[128,2048]{1,0:T(8,128)S(1)} %fusion.134, pred[]{:T(512)S(6)} %eq.123, pred[]{:T(512)S(6)} %eq.122, pred[]{:T(512)S(6)} %eq.121), kind=kLoop, calls=%fused_computation.114 | loop fusion | flops 196608 | bytes 1310723 | tf_op jit(solution)/shard_map/jit(_where)/select_n | solution.py:76
  8.3 0.6 collective-permute-start.3
  8.9 0.9 %select_select_fusion.2 = (f32[128,512]{1,0:T(8,128)}, f32[128,512]{1,0:T(8,128)}) fusion(f32[128,2048]{1,0:T(8,128)S(1)} %fusion.134, pred[]{:T(512)S(6)} %eq.117, pred[]{:T(512)S(6)} %eq.116, pred[]{:T(512)S(6)} %eq.115, pred[]{:T(512)S(6)} %eq.120, pred[]{:T(512)S(6)} %eq.119, pred[]{:T(512)S(6)} %eq.118), kind=kLoop, calls=%fused_computation.116 | loop fusion | flops 393216 | bytes 1572870 | tf_op jit(solution)/shard_map/jit(_where)/select_n | solution.py:76
  9.8 1.0 %collective-permute-start.1 = (f32[128,512]{1,0:T(8,128)}, f32[128,512]{1,0:T(8,128)}, u32[]{:S(2)}, u32[]{:S(2)}) collective-permute-start(f32[128,512]{1,0:T(8,128)} %get-tuple-element.68), channel_id=1, source_target_pairs={{0,1},{1,0},{2,3},{3,2},{4,5},{5,4},{6,7},{7,6},{8,9},{9,8},{10,11... | collective-permute-start | bytes 786440 | tf_op jit(solution)/shard_map/ppermute | solution.py:64
  10.8 0.5 collective-permute-start.2
  11.7 0.6 fusion.100
  12.6 0.7 %convolution_bitcast_fusion.2 = f32[128,1024]{1,0:T(8,128)S(1)} fusion(f32[512,1024]{1,0:T(8,128)S(1)} %bitcast.153, f32[1,1,128,512]{3,2,1,0:T(8,128)S(1)} %copy-done), kind=kOutput, calls=%fused_computation.7 | convolution fusion | flops 402653184 | bytes 2883584 | tf_op jit(solution)/shard_map/dot_general | solution.py:140
  13.4 0.8 %copy-done.1 = f32[128,1024]{1,0:T(8,128)} copy-done((f32[128,1024]{1,0:T(8,128)}, f32[128,1024]{1,0:T(8,128)S(1)}, u32[]{:S(2)}) %copy-start.1) | copy-done | bytes 524312
  14.1 1.1 %fusion.132 = (f32[127,1024]{1,0:T(8,128)}, f32[127,1024]{1,0:T(8,128)}) fusion(f32[128,1024]{1,0:T(8,128)S(1)} %convolution_bitcast_fusion.2), kind=kLoop, calls=%fused_computation.242 | loop fusion | bytes 2080768 | tf_op jit(solution)/shard_map/jit(_roll_static)/slice | solution.py:175
  15.2 0.9 %copy.28 = bf16[4,5,2048]{2,1,0:T(8,128)(2,1)S(1)} copy(bf16[4,5,2048]{2,0,1:T(4,128)(2,1)} %param.18) | data formatting | bytes 163840 | tf_op args[1]
  16.1 0.7 reshape.243
  16.8 1.4 %maximum_select_fusion = f32[128,1024]{1,0:T(8,128)S(1)} fusion(f32[1,1024]{1,0:T(1,128)S(1)} %get-tuple-element.77, f32[127,1024]{1,0:T(8,128)} %get-tuple-element.79, f32[127,1024]{1,0:T(8,128)} %get-tuple-element.78, f32[1,1024]{1,0:T(1,128)S(1)} %get-tuple-element.76, pred[128]{0:T(512)(128)(4,1)} %constant.92), kind=kLoop, calls=%fused_computation.38 | loop fusion | flops 393216 | bytes 1572992 | tf_op jit(solution)/shard_map/jit(_where)/select_n | solution.py:176
  18.2 1.1 %slice_add_fusion.1 = (f32[128,512]{1,0:T(8,128)S(1)}, f32[128,512]{1,0:T(8,128)S(1)}) fusion(f32[128,1024]{1,0:T(8,128)S(1)} %maximum_select_fusion, f32[128,1024]{1,0:T(8,128)} %copy-done.1, pred[512]{0:T(512)(128)(4,1)S(1)} %copy-done.7), kind=kLoop, calls=%fused_computation.94 | loop fusion | flops 262144 | bytes 1573376 | tf_op jit(solution)/shard_map/add | solution.py:183
  19.6 0.4 multiply_reduce_fusion
  20.1 4.0 %convolution_bitcast_fusion.1 = f32[3,512,128]{1,2,0:T(8,128)S(1)} fusion(bf16[2048,3,512]{2,0,1:T(8,128)(2,1)} %param.20, f32[128,2048]{1,0:T(8,128)S(1)} %get-tuple-element.104, f32[2048]{0:T(1024)S(1)} %copy-done.5, f32[128]{0:T(128)S(1)} %add_rsqrt_fusion), kind=kOutput, calls=%fused_computation.5 | convolution fusion | flops 806092800 | bytes 8135168 | tf_op jit(solution)/shard_map/dr,dmc->mcr/dot_general | solution.py:215
  24.2 1.3 %fusion.55 = (bf16[1,512,128]{1,2,0:T(8,128)(2,1)S(1)}, f32[128,512]{1,0:T(8,128)S(1)}) fusion(f32[3,512,128]{1,2,0:T(8,128)S(1)} %convolution_bitcast_fusion.1, f32[128,512]{1,0:T(8,128)} %collective-permute-done.3, f32[128,512]{1,0:T(8,128)} %collective-permute-done.2, f32[128,512]{1,0:T(8,128)} %collective-permute-done.1, f32[128,2048]{1,0:T(8,128)S(1)} %fusion.134, ...), kind=kLoop, calls=%fused_computation.129 | loop fusion | flops 589824 | bytes 2490371 | tf_op jit(solution)/shard_map/stack | solution.py:232
  25.6 2.3 %collective-permute-start.6 = (bf16[2,128,128]{1,2,0:T(8,128)(2,1)S(1)}, bf16[2,128,128]{1,2,0:T(8,128)(2,1)S(1)}, u32[]{:S(2)}, u32[]{:S(2)}) collective-permute-start(bf16[2,128,128]{1,2,0:T(8,128)(2,1)S(1)} %get-tuple-element.50), channel_id=1, source_target_pairs={{0,4},{4,0},{8,12},{12,8},{1,5},{5,1},{9,13},{13,9},{2,6},{6,2},{1... | collective-permute-start | bytes 196616 | tf_op jit(solution)/shard_map/ppermute | solution.py:64
  27.9 1.1 %collective-permute-start.5 = (bf16[2,128,128]{1,2,0:T(8,128)(2,1)S(1)}, bf16[2,128,128]{1,2,0:T(8,128)(2,1)S(1)}, u32[]{:S(2)}, u32[]{:S(2)}) collective-permute-start(bf16[2,128,128]{1,2,0:T(8,128)(2,1)S(1)} %get-tuple-element.90), channel_id=1, source_target_pairs={{0,8},{4,12},{8,0},{12,4},{1,9},{5,13},{9,1},{13,5},{2,10},{6,14},... | collective-permute-start | bytes 196616 | tf_op jit(solution)/shard_map/ppermute | solution.py:64
  29.0 1.5 %collective-permute-start.4 = (bf16[2,128,128]{1,2,0:T(8,128)(2,1)S(1)}, bf16[2,128,128]{1,2,0:T(8,128)(2,1)S(1)}, u32[]{:S(2)}, u32[]{:S(2)}) collective-permute-start(bf16[2,128,128]{1,2,0:T(8,128)(2,1)S(1)} %get-tuple-element.91), channel_id=1, source_target_pairs={{0,12},{4,8},{8,4},{12,0},{1,13},{5,9},{9,5},{13,1},{2,14},{6,10},... | collective-permute-start | bytes 196616 | tf_op jit(solution)/shard_map/ppermute | solution.py:64
  30.5 1.1 %fusion.1 = f32[3,512,128]{1,2,0:T(8,128)S(1)} fusion(f32[3,512,128]{1,2,0:T(8,128)S(1)} %convolution_bitcast_fusion.1, bf16[2048,3,512]{2,0,1:T(8,128)(2,1)S(1)} %bitcast.160, f32[128,2048]{1,0:T(8,128)S(1)} %get-tuple-element.104, f32[2048]{0:T(1024)S(1)} %copy-done.5, f32[128]{0:T(128)S(1)} %add_rsqrt_fusion), kind=kOutput, calls=%fused_computation.6 | convolution fusion | flops 807075840 | bytes 8921600 | tf_op jit(solution)/shard_map/dr,dmc->mcr/dot_general | solution.py:217
  31.6 4.2 %collective-permute-done.5 = bf16[2,128,128]{1,2,0:T(8,128)(2,1)S(1)} collective-permute-done((bf16[2,128,128]{1,2,0:T(8,128)(2,1)S(1)}, bf16[2,128,128]{1,2,0:T(8,128)(2,1)S(1)}, u32[]{:S(2)}, u32[]{:S(2)}) %collective-permute-start.5) | collective-permute-done | bytes 65568 | tf_op jit(solution)/shard_map/ppermute | solution.py:64
  35.9 0.6 fusion.71
  36.4 0.6 fusion.73
  38.4 1.0 %fusion.6 = bf16[1,128,512]{1,2,0:T(8,128)(2,1)S(1)} fusion(f32[512,1024]{1,0:T(8,128)S(1)} %bitcast.156, f32[128,512]{1,0:T(8,128)S(1)} %get-tuple-element.70, f32[128,512]{1,0:T(8,128)S(1)} %get-tuple-element.71, f32[1024]{0:T(1024)S(1)} %copy-done.6), kind=kOutput, calls=%fused_computation.15 | convolution fusion | flops 402980864 | bytes 2756608 | tf_op jit(solution)/shard_map/dot_general | solution.py:148
  39.4 1.0 %fusion.7 = bf16[1,128,512]{1,2,0:T(8,128)(2,1)S(1)} fusion(f32[512,1024]{1,0:T(8,128)S(1)} %bitcast.157, f32[128,512]{1,0:T(8,128)S(1)} %get-tuple-element.101, f32[128,512]{1,0:T(8,128)S(1)} %get-tuple-element.102, f32[1024]{0:T(1024)S(1)} %copy-done.6), kind=kOutput, calls=%fused_computation.16 | convolution fusion | flops 402980864 | bytes 2756608 | tf_op jit(solution)/shard_map/dot_general | solution.py:148
  40.4 1.3 %collective-permute-start.9 = (bf16[2,128,128]{1,2,0:T(8,128)(2,1)S(1)}, bf16[2,128,128]{1,2,0:T(8,128)(2,1)S(1)}, u32[]{:S(2)}, u32[]{:S(2)}) collective-permute-start(bf16[2,128,128]{1,2,0:T(8,128)(2,1)S(1)} %get-tuple-element.43), channel_id=1, source_target_pairs={{0,4},{4,0},{8,12},{12,8},{1,5},{5,1},{9,13},{13,9},{2,6},{6,2},{1... | collective-permute-start | bytes 196616 | tf_op jit(solution)/shard_map/ppermute | solution.py:64
  41.8 1.6 %collective-permute-start.8 = (bf16[2,128,128]{1,2,0:T(8,128)(2,1)S(1)}, bf16[2,128,128]{1,2,0:T(8,128)(2,1)S(1)}, u32[]{:S(2)}, u32[]{:S(2)}) collective-permute-start(bf16[2,128,128]{1,2,0:T(8,128)(2,1)S(1)} %get-tuple-element.85), channel_id=1, source_target_pairs={{0,8},{4,12},{8,0},{12,4},{1,9},{5,13},{9,1},{13,5},{2,10},{6,14},... | collective-permute-start | bytes 196616 | tf_op jit(solution)/shard_map/ppermute | solution.py:64
  43.4 1.5 %collective-permute-start.7 = (bf16[2,128,128]{1,2,0:T(8,128)(2,1)S(1)}, bf16[2,128,128]{1,2,0:T(8,128)(2,1)S(1)}, u32[]{:S(2)}, u32[]{:S(2)}) collective-permute-start(bf16[2,128,128]{1,2,0:T(8,128)(2,1)S(1)} %get-tuple-element.86), channel_id=1, source_target_pairs={{0,12},{4,8},{8,4},{12,0},{1,13},{5,9},{9,5},{13,1},{2,14},{6,10},... | collective-permute-start | bytes 196616 | tf_op jit(solution)/shard_map/ppermute | solution.py:64
  45.2 3.1 %collective-permute-done.8 = bf16[2,128,128]{1,2,0:T(8,128)(2,1)S(1)} collective-permute-done((bf16[2,128,128]{1,2,0:T(8,128)(2,1)S(1)}, bf16[2,128,128]{1,2,0:T(8,128)(2,1)S(1)}, u32[]{:S(2)}, u32[]{:S(2)}) %collective-permute-start.8) | collective-permute-done | bytes 65568 | tf_op jit(solution)/shard_map/ppermute | solution.py:64
  48.3 1.3 %collective-permute-done.7 = bf16[2,128,128]{1,2,0:T(8,128)(2,1)S(1)} collective-permute-done((bf16[2,128,128]{1,2,0:T(8,128)(2,1)S(1)}, bf16[2,128,128]{1,2,0:T(8,128)(2,1)S(1)}, u32[]{:S(2)}, u32[]{:S(2)}) %collective-permute-start.7) | collective-permute-done | bytes 65568 | tf_op jit(solution)/shard_map/ppermute | solution.py:64
  49.9 2.2 %fusion.8 = (f32[2048]{0:T(1024)S(1)}, f32[128,2048,1]{1,0,2:T(8,128)S(1)}) fusion(f32[128,2048]{1,0:T(8,128)S(1)} %get-tuple-element.104, f32[128]{0:T(128)S(1)} %add_rsqrt_fusion, bf16[2048,3,512]{2,0,1:T(8,128)(2,1)S(1)} %bitcast.160, bf16[1,512,128]{1,2,0:T(8,128)(2,1)S(1)} %get-tuple-element.65, bf16[1,512,128]{1,2,0:T(8,128)(2,1)S(1)} %get-tuple-element.64, ...), kind=kOutput, calls=%fused_computation.18 | convolution fusion | flops 806483968 | bytes 8790528 | tf_op jit(solution)/shard_map/mcr,dmc->rd/dot_general | solution.py:269
  52.2 1.5 %collective-permute-start.16 = (bf16[1,512,128]{1,2,0:T(8,128)(2,1)S(1)}, bf16[1,512,128]{1,2,0:T(8,128)(2,1)S(1)}, u32[]{:S(2)}, u32[]{:S(2)}) collective-permute-start(bf16[1,512,128]{1,2,0:T(8,128)(2,1)S(1)} %get-tuple-element.63), channel_id=1, source_target_pairs={{0,2},{2,0},{1,3},{3,1},{4,6},{6,4},{5,7},{7,5},{8,10},{10,8},{9,1... | collective-permute-start | bytes 393224 | tf_op jit(solution)/shard_map/ppermute | solution.py:47
  53.8 0.8 %convolution_multiply_fusion.1 = f32[20,2048]{1,0:T(8,128)S(1)} fusion(f32[128,2048,1]{1,0,2:T(8,128)S(1)} %get-tuple-element.106, f32[2048]{0:T(1024)S(1)} %copy-done.5, f32[128]{0:T(128)S(1)} %add_rsqrt_fusion, pred[128,5]{0,1:T(8,128)(4,1)S(1)} %get-tuple-element.107, pred[128,5]{0,1:T(8,128)(4,1)S(1)} %get-tuple-element.108, ...), kind=kOutput, calls=%fused_computation.2 | convolution fusion | flops 62970880 | bytes 1223680 | tf_op jit(solution)/shard_map/rk,rd->kd/dot_general | solution.py:273
  54.6 0.7 %fusion = f32[20,2048]{1,0:T(8,128)S(1)} fusion(f32[20,2048]{1,0:T(8,128)S(1)} %convolution_multiply_fusion.1, f32[128,2048]{1,0:T(8,128)S(1)} %get-tuple-element.104, f32[128]{0:T(128)S(1)} %add_rsqrt_fusion, f32[128]{0:T(128)S(1)} %multiply_reduce_fusion.1, pred[128,5]{0,1:T(8,128)(4,1)S(1)} %get-tuple-element.107, ...), kind=kOutput, calls=%fused_computation.1 | convolution fusion | flops 63276544 | bytes 1379840 | tf_op jit(solution)/shard_map/rk,dr->kd/dot_general | solution.py:274
  55.4 0.6 collective-permute-start.11
  56.0 1.3 %collective-permute-start.12 = (f32[21,512]{1,0:T(8,128)S(1)}, f32[21,512]{1,0:T(8,128)S(1)}, u32[]{:S(2)}, u32[]{:S(2)}) collective-permute-start(f32[21,512]{1,0:T(8,128)S(1)} %get-tuple-element.93), channel_id=1, source_target_pairs={{0,3},{1,2},{2,1},{3,0},{4,7},{5,6},{6,5},{7,4},{8,11},{9,10},{10,... | collective-permute-start | bytes 129032 | tf_op jit(solution)/shard_map/ppermute | solution.py:64
  57.8 1.9 %fusion.23 = f32[128,512]{1,0:T(8,128)} fusion(f32[512,1024]{1,0:T(8,128)S(1)} %bitcast.158, f32[128,512]{1,0:T(8,128)S(1)} %get-tuple-element.73, f32[128,512]{1,0:T(8,128)S(1)} %get-tuple-element.72, f32[1024]{0:T(1024)S(1)} %copy-done.6), kind=kOutput, calls=%fused_computation.47 | convolution fusion | flops 402915328 | bytes 2887680 | tf_op jit(solution)/shard_map/dot_general | solution.py:148
  59.6 0.5 collective-permute-done.11
  60.2 1.6 %collective-permute-start.15 = (f32[21,512]{1,0:T(8,128)S(1)}, f32[21,512]{1,0:T(8,128)S(1)}, u32[]{:S(2)}, u32[]{:S(2)}) collective-permute-start(f32[21,512]{1,0:T(8,128)S(1)} %pad_add_fusion), channel_id=1, source_target_pairs={{0,12},{4,8},{8,4},{12,0},{1,13},{5,9},{9,5},{13,1},{2,14},{6,10},... | collective-permute-start | bytes 129032 | tf_op jit(solution)/shard_map/ppermute | solution.py:64
  61.9 0.6 collective-permute-start.14
  62.4 2.3 %collective-permute-start.13 = (f32[21,512]{1,0:T(8,128)S(1)}, f32[21,512]{1,0:T(8,128)S(1)}, u32[]{:S(2)}, u32[]{:S(2)}) collective-permute-start(f32[21,512]{1,0:T(8,128)S(1)} %pad_add_fusion), channel_id=1, source_target_pairs={{0,4},{4,0},{8,12},{12,8},{1,5},{5,1},{9,13},{13,9},{2,6},{6,2},{1... | collective-permute-start | bytes 129032 | tf_op jit(solution)/shard_map/ppermute | solution.py:64
  65.5 0.9 %fusion.5 = bf16[128,512]{1,0:T(8,128)(2,1)} fusion(f32[128,512]{1,0:T(8,128)S(1)} %fusion.26, f32[128,512]{1,0:T(8,128)S(1)} %fusion.28, f32[128,512]{1,0:T(8,128)S(1)} %fusion.30, bf16[2048,512]{1,0:T(8,128)(2,1)S(1)} %copy-done.2, f32[128,2048]{1,0:T(8,128)S(1)} %get-tuple-element.104, s32[]{:T(128)S(6)} %select_n.782, ...), kind=kOutput, calls=%fused_computation.14 | convolution fusion | flops 67633152 | bytes 2228231 | tf_op jit(solution)/shard_map/cr,cd->rd/dot_general | solution.py:254
  66.7 1.5 %collective-permute-done.14 = f32[21,512]{1,0:T(8,128)S(1)} collective-permute-done((f32[21,512]{1,0:T(8,128)S(1)}, f32[21,512]{1,0:T(8,128)S(1)}, u32[]{:S(2)}, u32[]{:S(2)}) %collective-permute-start.14) | collective-permute-done | bytes 43040 | tf_op jit(solution)/shard_map/ppermute | solution.py:64
  68.2 0.6 slice.280
  68.8 0.6 copy.31
  (85 shorter events, 4.9 us)
Async XLA Ops:
  0.6 12.0 %copy-start = (f32[1,1,128,512]{3,2,1,0:T(8,128)S(1)}, f32[1,1,128,512]{3,2,1,0:T(8,128)}, u32[]{:S(2)}) copy-start(f32[1,1,128,512]{3,2,1,0:T(8,128)} %param.21) | copy-start | bytes 786436
  1.9 17.4 %collective-permute-start = (s32[3]{0:T(128)}, s32[3]{0:T(128)}, u32[]{:S(2)}, u32[]{:S(2)}) collective-permute-start(s32[3]{0:T(128)} %slice.175), channel_id=1, source_target_pairs={{0,4},{4,8},{8,12},{12,0},{1,5},{5,9},{9,13},{13,1},{2,6},{6,10},{... | collective-permute-start | bytes 44 | tf_op jit(solution)/shard_map/ppermute | solution.py:198
  7.5 3.8 %copy-start.9 = (s32[128]{0:T(128)S(1)}, s32[128]{0:T(128)}, u32[]{:S(2)}) copy-start(s32[128]{0:T(128)} %param.17) | copy-start | bytes 1540
  8.3 15.9 %collective-permute-start.3 = (f32[128,512]{1,0:T(8,128)}, f32[128,512]{1,0:T(8,128)}, u32[]{:S(2)}, u32[]{:S(2)}) collective-permute-start(f32[128,512]{1,0:T(8,128)} %select_select_fusion), channel_id=1, source_target_pairs={{0,3},{1,2},{2,1},{3,0},{4,7},{5,6},{6,5},{7,4},{8,11},{9,10},{10,... | collective-permute-start | bytes 786440 | tf_op jit(solution)/shard_map/ppermute | solution.py:64
  9.8 14.3 %collective-permute-start.1 = (f32[128,512]{1,0:T(8,128)}, f32[128,512]{1,0:T(8,128)}, u32[]{:S(2)}, u32[]{:S(2)}) collective-permute-start(f32[128,512]{1,0:T(8,128)} %get-tuple-element.68), channel_id=1, source_target_pairs={{0,1},{1,0},{2,3},{3,2},{4,5},{5,4},{6,7},{7,6},{8,9},{9,8},{10,11... | collective-permute-start | bytes 786440 | tf_op jit(solution)/shard_map/ppermute | solution.py:64
  10.8 13.4 %collective-permute-start.2 = (f32[128,512]{1,0:T(8,128)}, f32[128,512]{1,0:T(8,128)}, u32[]{:S(2)}, u32[]{:S(2)}) collective-permute-start(f32[128,512]{1,0:T(8,128)} %get-tuple-element.69), channel_id=1, source_target_pairs={{0,2},{1,3},{2,0},{3,1},{4,6},{5,7},{6,4},{7,5},{8,10},{9,11},{10,... | collective-permute-start | bytes 786440 | tf_op jit(solution)/shard_map/ppermute | solution.py:64
  13.3 0.8 %copy-start.1 = (f32[128,1024]{1,0:T(8,128)}, f32[128,1024]{1,0:T(8,128)S(1)}, u32[]{:S(2)}) copy-start(f32[128,1024]{1,0:T(8,128)S(1)} %convolution_bitcast_fusion.2) | copy-start | bytes 1572868
  13.3 4.8 %copy-start.7 = (pred[512]{0:T(512)(128)(4,1)S(1)}, pred[512]{0:T(512)(128)(4,1)}, u32[]{:S(2)}) copy-start(pred[512]{0:T(512)(128)(4,1)} %constant.91) | copy-start | bytes 1540
  16.8 2.6 %copy-start.10 = (s32[128]{0:T(128)S(1)}, s32[128]{0:T(128)}, u32[]{:S(2)}) copy-start(s32[128]{0:T(128)} %param.17) | copy-start | bytes 1540
  16.8 2.8 %copy-start.4 = (bf16[20,2048]{1,0:T(8,128)(2,1)S(1)}, bf16[20,2048]{1,0:T(8,128)(2,1)}, u32[]{:S(2)}) copy-start(bf16[20,2048]{1,0:T(8,128)(2,1)} %reshape.243) | copy-start | bytes 245764
  18.2 1.9 %copy-start.5 = (f32[2048]{0:T(1024)S(1)}, f32[2048]{0:T(1024)}, u32[]{:S(2)}) copy-start(f32[2048]{0:T(1024)} %param.19) | copy-start | bytes 24580
  20.0 10.5 %slice-start = ((s8[6291456]{0:T(1024)(128)(4,1)}), s8[4194304]{0:T(1024)(128)(4,1)S(1)}, s32[]{:S(2)}) async-start(s8[6291456]{0:T(1024)(128)(4,1)} %bitcast.159), calls=%async_computation | async-start | bytes 8388608
  20.0 10.4 %slice-start.1 = ((s8[6291456]{0:T(1024)(128)(4,1)}), s8[2097152]{0:T(1024)(128)(4,1)S(1)}, s32[]{:S(2)}) async-start(s8[6291456]{0:T(1024)(128)(4,1)} %bitcast.159), calls=%async_computation.1 | async-start | bytes 4194304
  25.6 6.0 %collective-permute-start.6 = (bf16[2,128,128]{1,2,0:T(8,128)(2,1)S(1)}, bf16[2,128,128]{1,2,0:T(8,128)(2,1)S(1)}, u32[]{:S(2)}, u32[]{:S(2)}) collective-permute-start(bf16[2,128,128]{1,2,0:T(8,128)(2,1)S(1)} %get-tuple-element.50), channel_id=1, source_target_pairs={{0,4},{4,0},{8,12},{12,8},{1,5},{5,1},{9,13},{13,9},{2,6},{6,2},{1... | collective-permute-start | bytes 196616 | tf_op jit(solution)/shard_map/ppermute | solution.py:64
  27.9 7.9 %collective-permute-start.5 = (bf16[2,128,128]{1,2,0:T(8,128)(2,1)S(1)}, bf16[2,128,128]{1,2,0:T(8,128)(2,1)S(1)}, u32[]{:S(2)}, u32[]{:S(2)}) collective-permute-start(bf16[2,128,128]{1,2,0:T(8,128)(2,1)S(1)} %get-tuple-element.90), channel_id=1, source_target_pairs={{0,8},{4,12},{8,0},{12,4},{1,9},{5,13},{9,1},{13,5},{2,10},{6,14},... | collective-permute-start | bytes 196616 | tf_op jit(solution)/shard_map/ppermute | solution.py:64
  29.0 6.8 %collective-permute-start.4 = (bf16[2,128,128]{1,2,0:T(8,128)(2,1)S(1)}, bf16[2,128,128]{1,2,0:T(8,128)(2,1)S(1)}, u32[]{:S(2)}, u32[]{:S(2)}) collective-permute-start(bf16[2,128,128]{1,2,0:T(8,128)(2,1)S(1)} %get-tuple-element.91), channel_id=1, source_target_pairs={{0,12},{4,8},{8,4},{12,0},{1,13},{5,9},{9,5},{13,1},{2,14},{6,10},... | collective-permute-start | bytes 196616 | tf_op jit(solution)/shard_map/ppermute | solution.py:64
  37.0 0.7 copy-start.8
  37.7 0.7 copy-start.6
  39.4 5.6 %copy-start.3 = (bf16[128,512]{1,0:T(8,128)(2,1)S(1)}, bf16[128,512]{1,0:T(8,128)(2,1)}, u32[]{:S(2)}) copy-start(bf16[128,512]{1,0:T(8,128)(2,1)} %param.23) | copy-start | bytes 393220
  40.4 4.8 %collective-permute-start.9 = (bf16[2,128,128]{1,2,0:T(8,128)(2,1)S(1)}, bf16[2,128,128]{1,2,0:T(8,128)(2,1)S(1)}, u32[]{:S(2)}, u32[]{:S(2)}) collective-permute-start(bf16[2,128,128]{1,2,0:T(8,128)(2,1)S(1)} %get-tuple-element.43), channel_id=1, source_target_pairs={{0,4},{4,0},{8,12},{12,8},{1,5},{5,1},{9,13},{13,9},{2,6},{6,2},{1... | collective-permute-start | bytes 196616 | tf_op jit(solution)/shard_map/ppermute | solution.py:64
  41.8 6.5 %collective-permute-start.8 = (bf16[2,128,128]{1,2,0:T(8,128)(2,1)S(1)}, bf16[2,128,128]{1,2,0:T(8,128)(2,1)S(1)}, u32[]{:S(2)}, u32[]{:S(2)}) collective-permute-start(bf16[2,128,128]{1,2,0:T(8,128)(2,1)S(1)} %get-tuple-element.85), channel_id=1, source_target_pairs={{0,8},{4,12},{8,0},{12,4},{1,9},{5,13},{9,1},{13,5},{2,10},{6,14},... | collective-permute-start | bytes 196616 | tf_op jit(solution)/shard_map/ppermute | solution.py:64
  43.4 6.2 %collective-permute-start.7 = (bf16[2,128,128]{1,2,0:T(8,128)(2,1)S(1)}, bf16[2,128,128]{1,2,0:T(8,128)(2,1)S(1)}, u32[]{:S(2)}, u32[]{:S(2)}) collective-permute-start(bf16[2,128,128]{1,2,0:T(8,128)(2,1)S(1)} %get-tuple-element.86), channel_id=1, source_target_pairs={{0,12},{4,8},{8,4},{12,0},{1,13},{5,9},{9,5},{13,1},{2,14},{6,10},... | collective-permute-start | bytes 196616 | tf_op jit(solution)/shard_map/ppermute | solution.py:64
  52.2 5.1 %collective-permute-start.16 = (bf16[1,512,128]{1,2,0:T(8,128)(2,1)S(1)}, bf16[1,512,128]{1,2,0:T(8,128)(2,1)S(1)}, u32[]{:S(2)}, u32[]{:S(2)}) collective-permute-start(bf16[1,512,128]{1,2,0:T(8,128)(2,1)S(1)} %get-tuple-element.63), channel_id=1, source_target_pairs={{0,2},{2,0},{1,3},{3,1},{4,6},{6,4},{5,7},{7,5},{8,10},{10,8},{9,1... | collective-permute-start | bytes 393224 | tf_op jit(solution)/shard_map/ppermute | solution.py:47
  55.3 9.4 %copy-start.2 = (bf16[2048,512]{1,0:T(8,128)(2,1)S(1)}, bf16[2048,512]{1,0:T(8,128)(2,1)}, u32[]{:S(2)}) copy-start(bf16[2048,512]{1,0:T(8,128)(2,1)} %param.22) | copy-start | bytes 6291460
  55.3 4.3 %collective-permute-start.10 = (f32[21,512]{1,0:T(8,128)S(1)}, f32[21,512]{1,0:T(8,128)S(1)}, u32[]{:S(2)}, u32[]{:S(2)}) collective-permute-start(f32[21,512]{1,0:T(8,128)S(1)} %get-tuple-element.36), channel_id=1, source_target_pairs={{0,1},{1,0},{2,3},{3,2},{4,5},{5,4},{6,7},{7,6},{8,9},{9,8},{10,11... | collective-permute-start | bytes 129032 | tf_op jit(solution)/shard_map/ppermute | solution.py:64
  55.4 4.7 %collective-permute-start.11 = (f32[21,512]{1,0:T(8,128)S(1)}, f32[21,512]{1,0:T(8,128)S(1)}, u32[]{:S(2)}, u32[]{:S(2)}) collective-permute-start(f32[21,512]{1,0:T(8,128)S(1)} %get-tuple-element.92), channel_id=1, source_target_pairs={{0,2},{1,3},{2,0},{3,1},{4,6},{5,7},{6,4},{7,5},{8,10},{9,11},{10,... | collective-permute-start | bytes 129032 | tf_op jit(solution)/shard_map/ppermute | solution.py:64
  56.0 4.2 %collective-permute-start.12 = (f32[21,512]{1,0:T(8,128)S(1)}, f32[21,512]{1,0:T(8,128)S(1)}, u32[]{:S(2)}, u32[]{:S(2)}) collective-permute-start(f32[21,512]{1,0:T(8,128)S(1)} %get-tuple-element.93), channel_id=1, source_target_pairs={{0,3},{1,2},{2,1},{3,0},{4,7},{5,6},{6,5},{7,4},{8,11},{9,10},{10,... | collective-permute-start | bytes 129032 | tf_op jit(solution)/shard_map/ppermute | solution.py:64
  57.4 7.3 %collective-permute-start.17 = (bf16[2,512,128]{1,2,0:T(8,128)(2,1)S(1)}, bf16[2,512,128]{1,2,0:T(8,128)(2,1)S(1)}, u32[]{:S(2)}, u32[]{:S(2)}) collective-permute-start(bf16[2,512,128]{1,2,0:T(8,128)(2,1)S(1)} %pad_maximum_fusion.5), channel_id=1, source_target_pairs={{0,1},{1,0},{2,3},{3,2},{4,5},{5,4},{6,7},{7,6},{8,9},{9,8},{10,11... | collective-permute-start | bytes 786440 | tf_op jit(solution)/shard_map/ppermute | solution.py:47
  60.2 6.4 %collective-permute-start.15 = (f32[21,512]{1,0:T(8,128)S(1)}, f32[21,512]{1,0:T(8,128)S(1)}, u32[]{:S(2)}, u32[]{:S(2)}) collective-permute-start(f32[21,512]{1,0:T(8,128)S(1)} %pad_add_fusion), channel_id=1, source_target_pairs={{0,12},{4,8},{8,4},{12,0},{1,13},{5,9},{9,5},{13,1},{2,14},{6,10},... | collective-permute-start | bytes 129032 | tf_op jit(solution)/shard_map/ppermute | solution.py:64
  61.9 6.3 %collective-permute-start.14 = (f32[21,512]{1,0:T(8,128)S(1)}, f32[21,512]{1,0:T(8,128)S(1)}, u32[]{:S(2)}, u32[]{:S(2)}) collective-permute-start(f32[21,512]{1,0:T(8,128)S(1)} %pad_add_fusion), channel_id=1, source_target_pairs={{0,8},{4,12},{8,0},{12,4},{1,9},{5,13},{9,1},{13,5},{2,10},{6,14},... | collective-permute-start | bytes 129032 | tf_op jit(solution)/shard_map/ppermute | solution.py:64
  62.4 5.8 %collective-permute-start.13 = (f32[21,512]{1,0:T(8,128)S(1)}, f32[21,512]{1,0:T(8,128)S(1)}, u32[]{:S(2)}, u32[]{:S(2)}) collective-permute-start(f32[21,512]{1,0:T(8,128)S(1)} %pad_add_fusion), channel_id=1, source_target_pairs={{0,4},{4,0},{8,12},{12,8},{1,5},{5,1},{9,13},{13,9},{2,6},{6,2},{1... | collective-permute-start | bytes 129032 | tf_op jit(solution)/shard_map/ppermute | solution.py:64

commit v17 on v15

--- a/solution.py
+++ b/solution.py
@@ -68,13 +68,9 @@
     axes = ("chan", "pair")
     count = lax.axis_size("chan") * lax.axis_size("pair")
     me = lax.axis_index(axes)
-    blocks = [x[:, g * width : (g + 1) * width] for g in range(count)]
 
     def pick(index):
-        out = blocks[0]
-        for g in range(1, count):
-            out = jnp.where(index == g, blocks[g], out)
-        return out
+        return lax.dynamic_slice_in_dim(x, index * width, width, 1)
 
     total = pick(me)
     for offset in range(1, count):

time: 69.8 us -> 68.4 us (0.980)
  other arithmetic: 8.35 us -> 5.61 us
  waiting for transfers between devices: 10.9 us -> 12.8 us
    ppermute x15, waiting for transfers between devices: 10.9 us -> 12.8 us  [group_exchange(): return lax.ppermute(x, axes, [(i, i ^ offset) for i in range(count)])]
    select_n x4 -> x0, other arithmetic: 1.73 us -> none  [pick(): out = jnp.where(index == g, blocks[g], out)]
    add x2, other arithmetic: 1.37 us -> 0.34 us  [add_conj_flip(): return jnp.concatenate([a + fa, jnp.where(edge, b + fb, b - fb)], axis=1)]
    dynamic_slice x0 -> x1, local copies, waits for them, and re-layouts: none -> 0.9 us  [pick(): return lax.dynamic_slice_in_dim(x, index * width, width, 1)]
    unnamed x28 -> x30, local copies, waits for them, and re-layouts: 3.11 us -> 2.43 us
  transfers between devices with their start and end apart: 18 -> 18, of which waited for: 7 -> 7; matrix products, arithmetic and copies ran while one was open for 32% -> 29% of each run, Pallas kernels for 0% -> 0%
where the time goes in v17:
time: 68.4 us; the launch traced here: 68.1 us
  starting transfers between devices  22.6 us (33%)
  matrix products  19.2 us (28%)
  waiting for transfers between devices  12.8 us (19%)
  local copies, waits for them, and re-layouts  6.89 us (10%)
  other arithmetic  5.61 us (8%)
  between operations  1.12 us (2%)
    ppermute x15, starting transfers between devices, group_exchange(): return lax.ppermute(x, axes, [(i, i ^ offset) for i in range(count)])  17.5 us
    ppermute x15, waiting for transfers between devices, group_exchange(): return lax.ppermute(x, axes, [(i, i ^ offset) for i in range(count)])  12.8 us
    dot_general x1, matrix products, per_device(): jnp.einsum('dr,dmc->mcr', hidden, in_proj, preferred_element_type=jnp.flo...  4.01 us
    dot_general x3, matrix products, inverse_dft(): lax.dot_general(spec * weight, dft, (((1,), (1,)), ((), ())), precision=T...  3.87 us
    ppermute x1, starting transfers between devices, per_device(): lax.ppermute(tokens[row_count - rim_width:], 'seq', [(i, (i + 1) % seq_co...  3.05 us
    dot_general x1, matrix products, per_device(): jnp.einsum('rd,cd->rc', cotangent, out_proj, preferred_element_type=jnp.f...  2.48 us
    unnamed x30, local copies, waits for them, and re-layouts  2.43 us
    dot_general x1, matrix products, per_device(): jnp.einsum('mcr,dmc->rd', d_proj, in_proj, preferred_element_type=jnp.flo...  2.16 us
  transfers between devices with their start and end apart: 18, of which 7 were waited for; matrix products, arithmetic and copies ran while one was open for 29% of the time, Pallas kernels for 0%

profile of v17, /device:TPU:0, one launch (start us, length us, event | category | flops | bytes accessed | tf_op | source)
XLA Modules:
  0.0 68.1 jit_solution(4017675199972720366)
XLA Ops:
  0.6 1.3 %slice.151 = s32[3]{0:T(128)} slice(s32[128]{0:T(128)} %param.17), slice={[125:128]} | slice | bytes 24 | tf_op jit(solution)/shard_map/slice | solution.py:191
  1.9 3.1 %collective-permute-start = (s32[3]{0:T(128)}, s32[3]{0:T(128)}, u32[]{:S(2)}, u32[]{:S(2)}) collective-permute-start(s32[3]{0:T(128)} %slice.151), channel_id=1, source_target_pairs={{0,4},{4,8},{8,12},{12,0},{1,5},{5,9},{9,13},{13,1},{2,6},{6,10},{... | collective-permute-start | bytes 44 | tf_op jit(solution)/shard_map/ppermute | solution.py:190
  5.0 2.5 %fusion.136 = f32[128,2048]{1,0:T(8,128)S(1)} fusion(bf16[128,512]{1,0:T(8,128)(2,1)} %param.23, bf16[2048,512]{1,0:T(8,128)(2,1)} %param.22), kind=kOutput, calls=%fused_computation.246 | convolution fusion | flops 268435456 | bytes 3276800 | tf_op jit(solution)/shard_map/rd,cd->rc/dot_general | solution.py:218
  7.5 1.0 %copy-done.1 = f32[128,2048]{1,0:T(8,128)} copy-done((f32[128,2048]{1,0:T(8,128)}, f32[128,2048]{1,0:T(8,128)S(1)}, u32[]{:S(2)}) %copy-start.1) | copy-done | bytes 1048600
  8.5 0.9 %constant_dynamic-slice_fusion.2 = (f32[128,512]{1,0:T(8,128)}, f32[128,512]{1,0:T(8,128)}, f32[128,512]{1,0:T(8,128)}) fusion(f32[128,2048]{1,0:T(8,128)S(1)} %fusion.136, s32[]{:T(128)S(6)} %select_n.506, s32[]{:T(128)S(6)} %select_n.508, s32[]{:T(128)S(6)} %select_n.507), kind=kLoop, calls=%fused_computation.232 | loop fusion | bytes 1572876 | tf_op jit(solution)/shard_map/dynamic_slice | solution.py:73
  9.4 1.6 %collective-permute-start.3 = (f32[128,512]{1,0:T(8,128)}, f32[128,512]{1,0:T(8,128)}, u32[]{:S(2)}, u32[]{:S(2)}) collective-permute-start(f32[128,512]{1,0:T(8,128)} %get-tuple-element.64), channel_id=1, source_target_pairs={{0,3},{1,2},{2,1},{3,0},{4,7},{5,6},{6,5},{7,4},{8,11},{9,10},{10,... | collective-permute-start | bytes 786440 | tf_op jit(solution)/shard_map/ppermute | solution.py:64
  11.0 0.5 collective-permute-start.2
  11.9 0.6 fusion.100
  12.8 0.7 %convolution_bitcast_fusion.2 = f32[128,1024]{1,0:T(8,128)S(1)} fusion(f32[512,1024]{1,0:T(8,128)S(1)} %bitcast.153, f32[1,1,128,512]{3,2,1,0:T(8,128)S(1)} %copy-done), kind=kOutput, calls=%fused_computation.7 | convolution fusion | flops 402653184 | bytes 2883584 | tf_op jit(solution)/shard_map/dot_general | solution.py:132
  13.6 0.9 %fusion.134 = (f32[127,1024]{1,0:T(8,128)S(1)}, f32[127,1024]{1,0:T(8,128)}) fusion(f32[128,1024]{1,0:T(8,128)S(1)} %convolution_bitcast_fusion.2), kind=kLoop, calls=%fused_computation.244 | loop fusion | bytes 2080768 | tf_op jit(solution)/shard_map/jit(_roll_static)/slice | solution.py:167
  14.6 0.7 reshape.243
  15.3 1.2 %maximum_select_fusion = f32[128,1024]{1,0:T(8,128)S(1)} fusion(f32[1,1024]{1,0:T(1,128)S(1)} %get-tuple-element.73, f32[127,1024]{1,0:T(8,128)} %get-tuple-element.75, f32[127,1024]{1,0:T(8,128)S(1)} %get-tuple-element.74, f32[1,1024]{1,0:T(1,128)S(1)} %get-tuple-element.72, pred[128]{0:T(512)(128)(4,1)} %constant.92), kind=kLoop, calls=%fused_computation.38 | loop fusion | flops 393216 | bytes 1572992 | tf_op jit(solution)/shard_map/jit(_where)/select_n | solution.py:168
  16.8 0.4 multiply_reduce_fusion
  17.3 4.0 %convolution_bitcast_fusion.1 = f32[3,512,128]{1,2,0:T(8,128)S(1)} fusion(bf16[2048,3,512]{2,0,1:T(8,128)(2,1)} %param.20, f32[128,2048]{1,0:T(8,128)S(1)} %get-tuple-element.101, f32[2048]{0:T(1024)S(1)} %copy-done.6, f32[128]{0:T(128)S(1)} %add_rsqrt_fusion), kind=kOutput, calls=%fused_computation.5 | convolution fusion | flops 806092800 | bytes 8135168 | tf_op jit(solution)/shard_map/dr,dmc->mcr/dot_general | solution.py:207
  21.4 2.5 %collective-permute-done.2 = f32[128,512]{1,0:T(8,128)} collective-permute-done((f32[128,512]{1,0:T(8,128)}, f32[128,512]{1,0:T(8,128)}, u32[]{:S(2)}, u32[]{:S(2)}) %collective-permute-start.2) | collective-permute-done | bytes 262176 | tf_op jit(solution)/shard_map/ppermute | solution.py:64
  23.9 1.3 %fusion.55 = (bf16[1,512,128]{1,2,0:T(8,128)(2,1)S(1)}, f32[128,512]{1,0:T(8,128)S(1)}) fusion(f32[3,512,128]{1,2,0:T(8,128)S(1)} %convolution_bitcast_fusion.1, f32[128,512]{1,0:T(8,128)} %collective-permute-done.3, f32[128,512]{1,0:T(8,128)} %collective-permute-done.2, f32[128,512]{1,0:T(8,128)} %collective-permute-done.1, f32[128,2048]{1,0:T(8,128)} %copy-done.1, ...), kind=kLoop, calls=%fused_computation.128 | loop fusion | flops 393216 | bytes 1703940 | tf_op jit(solution)/shard_map/stack | solution.py:224
  25.3 1.6 %collective-permute-start.6 = (bf16[2,128,128]{1,2,0:T(8,128)(2,1)S(1)}, bf16[2,128,128]{1,2,0:T(8,128)(2,1)S(1)}, u32[]{:S(2)}, u32[]{:S(2)}) collective-permute-start(bf16[2,128,128]{1,2,0:T(8,128)(2,1)S(1)} %get-tuple-element.45), channel_id=1, source_target_pairs={{0,4},{4,0},{8,12},{12,8},{1,5},{5,1},{9,13},{13,9},{2,6},{6,2},{1... | collective-permute-start | bytes 196616 | tf_op jit(solution)/shard_map/ppermute | solution.py:64
  26.9 1.2 %collective-permute-start.5 = (bf16[2,128,128]{1,2,0:T(8,128)(2,1)S(1)}, bf16[2,128,128]{1,2,0:T(8,128)(2,1)S(1)}, u32[]{:S(2)}, u32[]{:S(2)}) collective-permute-start(bf16[2,128,128]{1,2,0:T(8,128)(2,1)S(1)} %get-tuple-element.86), channel_id=1, source_target_pairs={{0,8},{4,12},{8,0},{12,4},{1,9},{5,13},{9,1},{13,5},{2,10},{6,14},... | collective-permute-start | bytes 196616 | tf_op jit(solution)/shard_map/ppermute | solution.py:64
  28.1 1.7 %collective-permute-start.4 = (bf16[2,128,128]{1,2,0:T(8,128)(2,1)S(1)}, bf16[2,128,128]{1,2,0:T(8,128)(2,1)S(1)}, u32[]{:S(2)}, u32[]{:S(2)}) collective-permute-start(bf16[2,128,128]{1,2,0:T(8,128)(2,1)S(1)} %get-tuple-element.87), channel_id=1, source_target_pairs={{0,12},{4,8},{8,4},{12,0},{1,13},{5,9},{9,5},{13,1},{2,14},{6,10},... | collective-permute-start | bytes 196616 | tf_op jit(solution)/shard_map/ppermute | solution.py:64
  29.8 1.1 %fusion.1 = f32[3,512,128]{1,2,0:T(8,128)S(1)} fusion(f32[3,512,128]{1,2,0:T(8,128)S(1)} %convolution_bitcast_fusion.1, bf16[2048,3,512]{2,0,1:T(8,128)(2,1)S(1)} %bitcast.160, f32[128,2048]{1,0:T(8,128)S(1)} %get-tuple-element.101, f32[2048]{0:T(1024)S(1)} %copy-done.6, f32[128]{0:T(128)S(1)} %add_rsqrt_fusion), kind=kOutput, calls=%fused_computation.6 | convolution fusion | flops 807075840 | bytes 8921600 | tf_op jit(solution)/shard_map/dr,dmc->mcr/dot_general | solution.py:209
  31.0 3.6 %collective-permute-done.5 = bf16[2,128,128]{1,2,0:T(8,128)(2,1)S(1)} collective-permute-done((bf16[2,128,128]{1,2,0:T(8,128)(2,1)S(1)}, bf16[2,128,128]{1,2,0:T(8,128)(2,1)S(1)}, u32[]{:S(2)}, u32[]{:S(2)}) %collective-permute-start.5) | collective-permute-done | bytes 65568 | tf_op jit(solution)/shard_map/ppermute | solution.py:64
  34.7 0.6 fusion.71
  35.2 0.6 fusion.73
  36.1 0.4 copy-done.9
  37.1 1.0 %fusion.6 = bf16[1,128,512]{1,2,0:T(8,128)(2,1)S(1)} fusion(f32[512,1024]{1,0:T(8,128)S(1)} %bitcast.156, f32[128,512]{1,0:T(8,128)S(1)} %get-tuple-element.66, f32[128,512]{1,0:T(8,128)S(1)} %get-tuple-element.67, f32[1024]{0:T(1024)S(1)} %copy-done.7), kind=kOutput, calls=%fused_computation.15 | convolution fusion | flops 402980864 | bytes 2756608 | tf_op jit(solution)/shard_map/dot_general | solution.py:140
  38.1 1.0 %fusion.7 = bf16[1,128,512]{1,2,0:T(8,128)(2,1)S(1)} fusion(f32[512,1024]{1,0:T(8,128)S(1)} %bitcast.157, f32[128,512]{1,0:T(8,128)S(1)} %get-tuple-element.98, f32[128,512]{1,0:T(8,128)S(1)} %get-tuple-element.99, f32[1024]{0:T(1024)S(1)} %copy-done.7), kind=kOutput, calls=%fused_computation.16 | convolution fusion | flops 402980864 | bytes 2756608 | tf_op jit(solution)/shard_map/dot_general | solution.py:140
  39.2 1.3 %collective-permute-start.9 = (bf16[2,128,128]{1,2,0:T(8,128)(2,1)S(1)}, bf16[2,128,128]{1,2,0:T(8,128)(2,1)S(1)}, u32[]{:S(2)}, u32[]{:S(2)}) collective-permute-start(bf16[2,128,128]{1,2,0:T(8,128)(2,1)S(1)} %get-tuple-element.38), channel_id=1, source_target_pairs={{0,4},{4,0},{8,12},{12,8},{1,5},{5,1},{9,13},{13,9},{2,6},{6,2},{1... | collective-permute-start | bytes 196616 | tf_op jit(solution)/shard_map/ppermute | solution.py:64
  40.5 1.6 %collective-permute-start.8 = (bf16[2,128,128]{1,2,0:T(8,128)(2,1)S(1)}, bf16[2,128,128]{1,2,0:T(8,128)(2,1)S(1)}, u32[]{:S(2)}, u32[]{:S(2)}) collective-permute-start(bf16[2,128,128]{1,2,0:T(8,128)(2,1)S(1)} %get-tuple-element.81), channel_id=1, source_target_pairs={{0,8},{4,12},{8,0},{12,4},{1,9},{5,13},{9,1},{13,5},{2,10},{6,14},... | collective-permute-start | bytes 196616 | tf_op jit(solution)/shard_map/ppermute | solution.py:64
  42.1 1.6 %collective-permute-start.7 = (bf16[2,128,128]{1,2,0:T(8,128)(2,1)S(1)}, bf16[2,128,128]{1,2,0:T(8,128)(2,1)S(1)}, u32[]{:S(2)}, u32[]{:S(2)}) collective-permute-start(bf16[2,128,128]{1,2,0:T(8,128)(2,1)S(1)} %get-tuple-element.82), channel_id=1, source_target_pairs={{0,12},{4,8},{8,4},{12,0},{1,13},{5,9},{9,5},{13,1},{2,14},{6,10},... | collective-permute-start | bytes 196616 | tf_op jit(solution)/shard_map/ppermute | solution.py:64
  44.0 3.0 %collective-permute-done.8 = bf16[2,128,128]{1,2,0:T(8,128)(2,1)S(1)} collective-permute-done((bf16[2,128,128]{1,2,0:T(8,128)(2,1)S(1)}, bf16[2,128,128]{1,2,0:T(8,128)(2,1)S(1)}, u32[]{:S(2)}, u32[]{:S(2)}) %collective-permute-start.8) | collective-permute-done | bytes 65568 | tf_op jit(solution)/shard_map/ppermute | solution.py:64
  46.9 1.3 %collective-permute-done.7 = bf16[2,128,128]{1,2,0:T(8,128)(2,1)S(1)} collective-permute-done((bf16[2,128,128]{1,2,0:T(8,128)(2,1)S(1)}, bf16[2,128,128]{1,2,0:T(8,128)(2,1)S(1)}, u32[]{:S(2)}, u32[]{:S(2)}) %collective-permute-start.7) | collective-permute-done | bytes 65568 | tf_op jit(solution)/shard_map/ppermute | solution.py:64
  48.6 2.2 %fusion.8 = (f32[2048]{0:T(1024)S(1)}, f32[128,2048,1]{1,0,2:T(8,128)S(1)}) fusion(f32[128,2048]{1,0:T(8,128)S(1)} %get-tuple-element.101, f32[128]{0:T(128)S(1)} %add_rsqrt_fusion, bf16[2048,3,512]{2,0,1:T(8,128)(2,1)S(1)} %bitcast.160, bf16[1,512,128]{1,2,0:T(8,128)(2,1)S(1)} %get-tuple-element.60, bf16[1,512,128]{1,2,0:T(8,128)(2,1)S(1)} %get-tuple-element.59, ...), kind=kOutput, calls=%fused_computation.18 | convolution fusion | flops 806483968 | bytes 8790528 | tf_op jit(solution)/shard_map/mcr,dmc->rd/dot_general | solution.py:261
  50.9 1.5 %collective-permute-start.16 = (bf16[1,512,128]{1,2,0:T(8,128)(2,1)S(1)}, bf16[1,512,128]{1,2,0:T(8,128)(2,1)S(1)}, u32[]{:S(2)}, u32[]{:S(2)}) collective-permute-start(bf16[1,512,128]{1,2,0:T(8,128)(2,1)S(1)} %get-tuple-element.58), channel_id=1, source_target_pairs={{0,2},{2,0},{1,3},{3,1},{4,6},{6,4},{5,7},{7,5},{8,10},{10,8},{9,1... | collective-permute-start | bytes 393224 | tf_op jit(solution)/shard_map/ppermute | solution.py:47
  52.5 0.7 %convolution_multiply_fusion.1 = f32[20,2048]{1,0:T(8,128)S(1)} fusion(f32[128,2048,1]{1,0,2:T(8,128)S(1)} %get-tuple-element.103, f32[2048]{0:T(1024)S(1)} %copy-done.6, f32[128]{0:T(128)S(1)} %add_rsqrt_fusion, pred[128,5]{0,1:T(8,128)(4,1)S(1)} %get-tuple-element.104, pred[128,5]{0,1:T(8,128)(4,1)S(1)} %get-tuple-element.105, ...), kind=kOutput, calls=%fused_computation.2 | convolution fusion | flops 62970880 | bytes 1223680 | tf_op jit(solution)/shard_map/rk,rd->kd/dot_general | solution.py:265
  53.2 0.7 %fusion = f32[20,2048]{1,0:T(8,128)S(1)} fusion(f32[20,2048]{1,0:T(8,128)S(1)} %convolution_multiply_fusion.1, f32[128,2048]{1,0:T(8,128)S(1)} %get-tuple-element.101, f32[128]{0:T(128)S(1)} %add_rsqrt_fusion, f32[128]{0:T(128)S(1)} %multiply_reduce_fusion.1, pred[128,5]{0,1:T(8,128)(4,1)S(1)} %get-tuple-element.104, ...), kind=kOutput, calls=%fused_computation.1 | convolution fusion | flops 63276544 | bytes 1379840 | tf_op jit(solution)/shard_map/rk,dr->kd/dot_general | solution.py:266
  54.1 0.6 collective-permute-start.11
  54.7 1.2 %collective-permute-start.12 = (f32[21,512]{1,0:T(8,128)S(1)}, f32[21,512]{1,0:T(8,128)S(1)}, u32[]{:S(2)}, u32[]{:S(2)}) collective-permute-start(f32[21,512]{1,0:T(8,128)S(1)} %get-tuple-element.90), channel_id=1, source_target_pairs={{0,3},{1,2},{2,1},{3,0},{4,7},{5,6},{6,5},{7,4},{8,11},{9,10},{10,... | collective-permute-start | bytes 129032 | tf_op jit(solution)/shard_map/ppermute | solution.py:64
  56.0 0.4 collective-permute-start.17
  56.5 1.9 %fusion.23 = f32[128,512]{1,0:T(8,128)} fusion(f32[512,1024]{1,0:T(8,128)S(1)} %bitcast.158, f32[128,512]{1,0:T(8,128)S(1)} %get-tuple-element.69, f32[128,512]{1,0:T(8,128)S(1)} %get-tuple-element.68, f32[1024]{0:T(1024)S(1)} %copy-done.7), kind=kOutput, calls=%fused_computation.47 | convolution fusion | flops 402915328 | bytes 2887680 | tf_op jit(solution)/shard_map/dot_general | solution.py:140
  58.3 0.5 collective-permute-done.11
  58.9 1.7 %collective-permute-start.15 = (f32[21,512]{1,0:T(8,128)S(1)}, f32[21,512]{1,0:T(8,128)S(1)}, u32[]{:S(2)}, u32[]{:S(2)}) collective-permute-start(f32[21,512]{1,0:T(8,128)S(1)} %fusion.106), channel_id=1, source_target_pairs={{0,12},{4,8},{8,4},{12,0},{1,13},{5,9},{9,5},{13,1},{2,14},{6,10},... | collective-permute-start | bytes 129032 | tf_op jit(solution)/shard_map/ppermute | solution.py:64
  60.6 0.5 collective-permute-start.14
  61.1 2.3 %collective-permute-start.13 = (f32[21,512]{1,0:T(8,128)S(1)}, f32[21,512]{1,0:T(8,128)S(1)}, u32[]{:S(2)}, u32[]{:S(2)}) collective-permute-start(f32[21,512]{1,0:T(8,128)S(1)} %fusion.106), channel_id=1, source_target_pairs={{0,4},{4,0},{8,12},{12,8},{1,5},{5,1},{9,13},{13,9},{2,6},{6,2},{1... | collective-permute-start | bytes 129032 | tf_op jit(solution)/shard_map/ppermute | solution.py:64
  64.1 0.9 %fusion.5 = bf16[128,512]{1,0:T(8,128)(2,1)} fusion(f32[128,512]{1,0:T(8,128)S(1)} %fusion.26, f32[128,512]{1,0:T(8,128)S(1)} %fusion.28, f32[128,512]{1,0:T(8,128)S(1)} %fusion.30, bf16[2048,512]{1,0:T(8,128)(2,1)S(1)} %copy-done.2, f32[128,2048]{1,0:T(8,128)S(1)} %get-tuple-element.101, s32[]{:T(128)S(6)} %select_n.505, ...), kind=kOutput, calls=%fused_computation.14 | convolution fusion | flops 67633152 | bytes 2228231 | tf_op jit(solution)/shard_map/cr,cd->rd/dot_general | solution.py:246
  65.0 0.4 collective-permute-done.15
  65.4 1.5 %collective-permute-done.14 = f32[21,512]{1,0:T(8,128)S(1)} collective-permute-done((f32[21,512]{1,0:T(8,128)S(1)}, f32[21,512]{1,0:T(8,128)S(1)}, u32[]{:S(2)}, u32[]{:S(2)}) %collective-permute-start.14) | collective-permute-done | bytes 43040 | tf_op jit(solution)/shard_map/ppermute | solution.py:64
  66.9 0.6 slice.238
  67.5 0.6 copy.31
  (85 shorter events, 4.0 us)
Async XLA Ops:
  0.6 12.2 %copy-start = (f32[1,1,128,512]{3,2,1,0:T(8,128)S(1)}, f32[1,1,128,512]{3,2,1,0:T(8,128)}, u32[]{:S(2)}) copy-start(f32[1,1,128,512]{3,2,1,0:T(8,128)} %param.21) | copy-start | bytes 786436
  1.9 14.7 %collective-permute-start = (s32[3]{0:T(128)}, s32[3]{0:T(128)}, u32[]{:S(2)}, u32[]{:S(2)}) collective-permute-start(s32[3]{0:T(128)} %slice.151), channel_id=1, source_target_pairs={{0,4},{4,8},{8,12},{12,0},{1,5},{5,9},{9,13},{13,1},{2,6},{6,10},{... | collective-permute-start | bytes 44 | tf_op jit(solution)/shard_map/ppermute | solution.py:190
  5.0 6.5 %copy-start.10 = (s32[128]{0:T(128)S(1)}, s32[128]{0:T(128)}, u32[]{:S(2)}) copy-start(s32[128]{0:T(128)} %param.17) | copy-start | bytes 1540
  7.5 1.0 %copy-start.1 = (f32[128,2048]{1,0:T(8,128)}, f32[128,2048]{1,0:T(8,128)S(1)}, u32[]{:S(2)}) copy-start(f32[128,2048]{1,0:T(8,128)S(1)} %fusion.136) | copy-start | bytes 3145732
  9.4 12.0 %collective-permute-start.1 = (f32[128,512]{1,0:T(8,128)}, f32[128,512]{1,0:T(8,128)}, u32[]{:S(2)}, u32[]{:S(2)}) collective-permute-start(f32[128,512]{1,0:T(8,128)} %get-tuple-element.63), channel_id=1, source_target_pairs={{0,1},{1,0},{2,3},{3,2},{4,5},{5,4},{6,7},{7,6},{8,9},{9,8},{10,11... | collective-permute-start | bytes 786440 | tf_op jit(solution)/shard_map/ppermute | solution.py:64
  9.4 12.0 %collective-permute-start.3 = (f32[128,512]{1,0:T(8,128)}, f32[128,512]{1,0:T(8,128)}, u32[]{:S(2)}, u32[]{:S(2)}) collective-permute-start(f32[128,512]{1,0:T(8,128)} %get-tuple-element.64), channel_id=1, source_target_pairs={{0,3},{1,2},{2,1},{3,0},{4,7},{5,6},{6,5},{7,4},{8,11},{9,10},{10,... | collective-permute-start | bytes 786440 | tf_op jit(solution)/shard_map/ppermute | solution.py:64
  11.0 12.9 %collective-permute-start.2 = (f32[128,512]{1,0:T(8,128)}, f32[128,512]{1,0:T(8,128)}, u32[]{:S(2)}, u32[]{:S(2)}) collective-permute-start(f32[128,512]{1,0:T(8,128)} %get-tuple-element.65), channel_id=1, source_target_pairs={{0,2},{1,3},{2,0},{3,1},{4,6},{5,7},{6,4},{7,5},{8,10},{9,11},{10,... | collective-permute-start | bytes 786440 | tf_op jit(solution)/shard_map/ppermute | solution.py:64
  12.8 1.7 %copy-start.5 = (bf16[4,5,2048]{2,0,1:T(4,128)(2,1)S(1)}, bf16[4,5,2048]{2,0,1:T(4,128)(2,1)}, u32[]{:S(2)}) copy-start(bf16[4,5,2048]{2,0,1:T(4,128)(2,1)} %param.18) | copy-start | bytes 245764
  13.6 2.9 %copy-start.8 = (pred[512]{0:T(512)(128)(4,1)S(1)}, pred[512]{0:T(512)(128)(4,1)}, u32[]{:S(2)}) copy-start(pred[512]{0:T(512)(128)(4,1)} %constant.91) | copy-start | bytes 1540
  15.3 1.4 %copy-start.11 = (s32[128]{0:T(128)S(1)}, s32[128]{0:T(128)}, u32[]{:S(2)}) copy-start(s32[128]{0:T(128)} %param.17) | copy-start | bytes 1540
  15.3 1.6 %copy-start.4 = (bf16[20,2048]{1,0:T(8,128)(2,1)S(1)}, bf16[20,2048]{1,0:T(8,128)(2,1)}, u32[]{:S(2)}) copy-start(bf16[20,2048]{1,0:T(8,128)(2,1)} %reshape.243) | copy-start | bytes 245764
  16.5 0.8 %copy-start.6 = (f32[2048]{0:T(1024)S(1)}, f32[2048]{0:T(1024)}, u32[]{:S(2)}) copy-start(f32[2048]{0:T(1024)} %param.19) | copy-start | bytes 24580
  17.3 12.5 %slice-start = ((s8[6291456]{0:T(1024)(128)(4,1)}), s8[4194304]{0:T(1024)(128)(4,1)S(1)}, s32[]{:S(2)}) async-start(s8[6291456]{0:T(1024)(128)(4,1)} %bitcast.159), calls=%async_computation | async-start | bytes 8388608
  17.3 12.5 %slice-start.1 = ((s8[6291456]{0:T(1024)(128)(4,1)}), s8[2097152]{0:T(1024)(128)(4,1)S(1)}, s32[]{:S(2)}) async-start(s8[6291456]{0:T(1024)(128)(4,1)} %bitcast.159), calls=%async_computation.1 | async-start | bytes 4194304
  25.3 5.7 %collective-permute-start.6 = (bf16[2,128,128]{1,2,0:T(8,128)(2,1)S(1)}, bf16[2,128,128]{1,2,0:T(8,128)(2,1)S(1)}, u32[]{:S(2)}, u32[]{:S(2)}) collective-permute-start(bf16[2,128,128]{1,2,0:T(8,128)(2,1)S(1)} %get-tuple-element.45), channel_id=1, source_target_pairs={{0,4},{4,0},{8,12},{12,8},{1,5},{5,1},{9,13},{13,9},{2,6},{6,2},{1... | collective-permute-start | bytes 196616 | tf_op jit(solution)/shard_map/ppermute | solution.py:64
  26.9 7.6 %collective-permute-start.5 = (bf16[2,128,128]{1,2,0:T(8,128)(2,1)S(1)}, bf16[2,128,128]{1,2,0:T(8,128)(2,1)S(1)}, u32[]{:S(2)}, u32[]{:S(2)}) collective-permute-start(bf16[2,128,128]{1,2,0:T(8,128)(2,1)S(1)} %get-tuple-element.86), channel_id=1, source_target_pairs={{0,8},{4,12},{8,0},{12,4},{1,9},{5,13},{9,1},{13,5},{2,10},{6,14},... | collective-permute-start | bytes 196616 | tf_op jit(solution)/shard_map/ppermute | solution.py:64
  28.1 6.5 %collective-permute-start.4 = (bf16[2,128,128]{1,2,0:T(8,128)(2,1)S(1)}, bf16[2,128,128]{1,2,0:T(8,128)(2,1)S(1)}, u32[]{:S(2)}, u32[]{:S(2)}) collective-permute-start(bf16[2,128,128]{1,2,0:T(8,128)(2,1)S(1)} %get-tuple-element.87), channel_id=1, source_target_pairs={{0,12},{4,8},{8,4},{12,0},{1,13},{5,9},{9,5},{13,1},{2,14},{6,10},... | collective-permute-start | bytes 196616 | tf_op jit(solution)/shard_map/ppermute | solution.py:64
  35.8 0.7 copy-start.9
  36.4 0.7 %copy-start.7 = (f32[1024]{0:T(1024)S(1)}, f32[1024]{0:T(1024)}, u32[]{:S(2)}) copy-start(f32[1024]{0:T(1024)} %constant.93) | copy-start | bytes 12292
  38.1 5.6 %copy-start.3 = (bf16[128,512]{1,0:T(8,128)(2,1)S(1)}, bf16[128,512]{1,0:T(8,128)(2,1)}, u32[]{:S(2)}) copy-start(bf16[128,512]{1,0:T(8,128)(2,1)} %param.23) | copy-start | bytes 393220
  39.2 4.8 %collective-permute-start.9 = (bf16[2,128,128]{1,2,0:T(8,128)(2,1)S(1)}, bf16[2,128,128]{1,2,0:T(8,128)(2,1)S(1)}, u32[]{:S(2)}, u32[]{:S(2)}) collective-permute-start(bf16[2,128,128]{1,2,0:T(8,128)(2,1)S(1)} %get-tuple-element.38), channel_id=1, source_target_pairs={{0,4},{4,0},{8,12},{12,8},{1,5},{5,1},{9,13},{13,9},{2,6},{6,2},{1... | collective-permute-start | bytes 196616 | tf_op jit(solution)/shard_map/ppermute | solution.py:64
  40.5 6.4 %collective-permute-start.8 = (bf16[2,128,128]{1,2,0:T(8,128)(2,1)S(1)}, bf16[2,128,128]{1,2,0:T(8,128)(2,1)S(1)}, u32[]{:S(2)}, u32[]{:S(2)}) collective-permute-start(bf16[2,128,128]{1,2,0:T(8,128)(2,1)S(1)} %get-tuple-element.81), channel_id=1, source_target_pairs={{0,8},{4,12},{8,0},{12,4},{1,9},{5,13},{9,1},{13,5},{2,10},{6,14},... | collective-permute-start | bytes 196616 | tf_op jit(solution)/shard_map/ppermute | solution.py:64
  42.1 6.2 %collective-permute-start.7 = (bf16[2,128,128]{1,2,0:T(8,128)(2,1)S(1)}, bf16[2,128,128]{1,2,0:T(8,128)(2,1)S(1)}, u32[]{:S(2)}, u32[]{:S(2)}) collective-permute-start(bf16[2,128,128]{1,2,0:T(8,128)(2,1)S(1)} %get-tuple-element.82), channel_id=1, source_target_pairs={{0,12},{4,8},{8,4},{12,0},{1,13},{5,9},{9,5},{13,1},{2,14},{6,10},... | collective-permute-start | bytes 196616 | tf_op jit(solution)/shard_map/ppermute | solution.py:64
  50.9 5.1 %collective-permute-start.16 = (bf16[1,512,128]{1,2,0:T(8,128)(2,1)S(1)}, bf16[1,512,128]{1,2,0:T(8,128)(2,1)S(1)}, u32[]{:S(2)}, u32[]{:S(2)}) collective-permute-start(bf16[1,512,128]{1,2,0:T(8,128)(2,1)S(1)} %get-tuple-element.58), channel_id=1, source_target_pairs={{0,2},{2,0},{1,3},{3,1},{4,6},{6,4},{5,7},{7,5},{8,10},{10,8},{9,1... | collective-permute-start | bytes 393224 | tf_op jit(solution)/shard_map/ppermute | solution.py:47
  54.0 9.4 %copy-start.2 = (bf16[2048,512]{1,0:T(8,128)(2,1)S(1)}, bf16[2048,512]{1,0:T(8,128)(2,1)}, u32[]{:S(2)}) copy-start(bf16[2048,512]{1,0:T(8,128)(2,1)} %param.22) | copy-start | bytes 6291460
  54.1 4.3 %collective-permute-start.10 = (f32[21,512]{1,0:T(8,128)S(1)}, f32[21,512]{1,0:T(8,128)S(1)}, u32[]{:S(2)}, u32[]{:S(2)}) collective-permute-start(f32[21,512]{1,0:T(8,128)S(1)} %get-tuple-element.88), channel_id=1, source_target_pairs={{0,1},{1,0},{2,3},{3,2},{4,5},{5,4},{6,7},{7,6},{8,9},{9,8},{10,11... | collective-permute-start | bytes 129032 | tf_op jit(solution)/shard_map/ppermute | solution.py:64
  54.1 4.7 %collective-permute-start.11 = (f32[21,512]{1,0:T(8,128)S(1)}, f32[21,512]{1,0:T(8,128)S(1)}, u32[]{:S(2)}, u32[]{:S(2)}) collective-permute-start(f32[21,512]{1,0:T(8,128)S(1)} %get-tuple-element.89), channel_id=1, source_target_pairs={{0,2},{1,3},{2,0},{3,1},{4,6},{5,7},{6,4},{7,5},{8,10},{9,11},{10,... | collective-permute-start | bytes 129032 | tf_op jit(solution)/shard_map/ppermute | solution.py:64
  54.7 4.1 %collective-permute-start.12 = (f32[21,512]{1,0:T(8,128)S(1)}, f32[21,512]{1,0:T(8,128)S(1)}, u32[]{:S(2)}, u32[]{:S(2)}) collective-permute-start(f32[21,512]{1,0:T(8,128)S(1)} %get-tuple-element.90), channel_id=1, source_target_pairs={{0,3},{1,2},{2,1},{3,0},{4,7},{5,6},{6,5},{7,4},{8,11},{9,10},{10,... | collective-permute-start | bytes 129032 | tf_op jit(solution)/shard_map/ppermute | solution.py:64
  56.0 7.3 %collective-permute-start.17 = (bf16[2,512,128]{1,2,0:T(8,128)(2,1)S(1)}, bf16[2,512,128]{1,2,0:T(8,128)(2,1)S(1)}, u32[]{:S(2)}, u32[]{:S(2)}) collective-permute-start(bf16[2,512,128]{1,2,0:T(8,128)(2,1)S(1)} %pad_maximum_fusion.5), channel_id=1, source_target_pairs={{0,1},{1,0},{2,3},{3,2},{4,5},{5,4},{6,7},{7,6},{8,9},{9,8},{10,11... | collective-permute-start | bytes 786440 | tf_op jit(solution)/shard_map/ppermute | solution.py:47
  58.9 6.5 %collective-permute-start.15 = (f32[21,512]{1,0:T(8,128)S(1)}, f32[21,512]{1,0:T(8,128)S(1)}, u32[]{:S(2)}, u32[]{:S(2)}) collective-permute-start(f32[21,512]{1,0:T(8,128)S(1)} %fusion.106), channel_id=1, source_target_pairs={{0,12},{4,8},{8,4},{12,0},{1,13},{5,9},{9,5},{13,1},{2,14},{6,10},... | collective-permute-start | bytes 129032 | tf_op jit(solution)/shard_map/ppermute | solution.py:64
  60.6 6.3 %collective-permute-start.14 = (f32[21,512]{1,0:T(8,128)S(1)}, f32[21,512]{1,0:T(8,128)S(1)}, u32[]{:S(2)}, u32[]{:S(2)}) collective-permute-start(f32[21,512]{1,0:T(8,128)S(1)} %fusion.106), channel_id=1, source_target_pairs={{0,8},{4,12},{8,0},{12,4},{1,9},{5,13},{9,1},{13,5},{2,10},{6,14},... | collective-permute-start | bytes 129032 | tf_op jit(solution)/shard_map/ppermute | solution.py:64
  61.1 5.8 %collective-permute-start.13 = (f32[21,512]{1,0:T(8,128)S(1)}, f32[21,512]{1,0:T(8,128)S(1)}, u32[]{:S(2)}, u32[]{:S(2)}) collective-permute-start(f32[21,512]{1,0:T(8,128)S(1)} %fusion.106), channel_id=1, source_target_pairs={{0,4},{4,0},{8,12},{12,8},{1,5},{5,1},{9,13},{13,9},{2,6},{6,2},{1... | collective-permute-start | bytes 129032 | tf_op jit(solution)/shard_map/ppermute | solution.py:64

commit v18 on v17

--- a/solution.py
+++ b/solution.py
@@ -106,13 +106,9 @@
         return lax.all_to_all(x, "seq", split_axis=split_axis, concat_axis=concat_axis, tiled=True)
     me = lax.axis_index("seq")
     width = x.shape[split_axis] // count
-    blocks = [lax.slice_in_dim(x, j * width, (j + 1) * width, axis=split_axis) for j in range(count)]
 
     def pick(index):
-        out = blocks[0]
-        for j in range(1, count):
-            out = jnp.where(index == j, blocks[j], out)
-        return out
+        return lax.dynamic_slice_in_dim(x, index * width, width, split_axis)
 
     sent = {
         offset: group_exchange(pick(me ^ offset), "seq", count, offset)

time: 68.4 us -> 68.7 us (level)
  waiting for transfers between devices: 12.8 us -> 14.4 us
  starting transfers between devices: 22.6 us -> 21.3 us
    ppermute x2, waiting for transfers between devices: 0.01 us -> 2.3 us  [xor_exchange(): return lax.ppermute(x, axis, [(i, i ^ step) for i in range(count)])]
    ppermute x2, starting transfers between devices: 1.97 us -> 1.08 us  [xor_exchange(): return lax.ppermute(x, axis, [(i, i ^ step) for i in range(count)])]
    ppermute x15, waiting for transfers between devices: 12.8 us -> 12.1 us  [group_exchange(): return lax.ppermute(x, axes, [(i, i ^ offset) for i in range(count)])]
    unnamed x30 -> x28, local copies, waits for them, and re-layouts: 2.43 us -> 2.34 us
  transfers between devices with their start and end apart: 18 -> 18, of which waited for: 7 -> 8; matrix products, arithmetic and copies ran while one was open for 29% -> 29% of each run, Pallas kernels for 0% -> 0%
where the time goes in v18:
time: 68.7 us; the launch traced here: 68.5 us
  starting transfers between devices  21.3 us (31%)
  matrix products  19.3 us (28%)
  waiting for transfers between devices  14.4 us (21%)
  local copies, waits for them, and re-layouts  6.91 us (10%)
  other arithmetic  5.54 us (8%)
  between operations  1.11 us (2%)
    ppermute x15, starting transfers between devices, group_exchange(): return lax.ppermute(x, axes, [(i, i ^ offset) for i in range(count)])  17.1 us
    ppermute x15, waiting for transfers between devices, group_exchange(): return lax.ppermute(x, axes, [(i, i ^ offset) for i in range(count)])  12.1 us
    dot_general x1, matrix products, per_device(): jnp.einsum('dr,dmc->mcr', hidden, in_proj, preferred_element_type=jnp.flo...  4.1 us
    dot_general x3, matrix products, inverse_dft(): lax.dot_general(spec * weight, dft, (((1,), (1,)), ((), ())), precision=T...  3.98 us
    ppermute x1, starting transfers between devices, per_device(): lax.ppermute(tokens[row_count - rim_width:], 'seq', [(i, (i + 1) % seq_co...  3.05 us
    dot_general x1, matrix products, per_device(): jnp.einsum('rd,cd->rc', cotangent, out_proj, preferred_element_type=jnp.f...  2.48 us
    unnamed x28, local copies, waits for them, and re-layouts  2.34 us
    ppermute x2, waiting for transfers between devices, xor_exchange(): return lax.ppermute(x, axis, [(i, i ^ step) for i in range(count)])  2.3 us
  transfers between devices with their start and end apart: 18, of which 8 were waited for; matrix products, arithmetic and copies ran while one was open for 29% of the time, Pallas kernels for 0%

profile of v18, /device:TPU:0, one launch (start us, length us, event | category | flops | bytes accessed | tf_op | source)
XLA Modules:
  0.0 68.5 jit_solution(14628264417705660195)
XLA Ops:
  0.6 1.3 %slice.127 = s32[3]{0:T(128)} slice(s32[128]{0:T(128)} %param.17), slice={[125:128]} | slice | bytes 24 | tf_op jit(solution)/shard_map/slice | solution.py:187
  1.9 3.1 %collective-permute-start = (s32[3]{0:T(128)}, s32[3]{0:T(128)}, u32[]{:S(2)}, u32[]{:S(2)}) collective-permute-start(s32[3]{0:T(128)} %slice.127), channel_id=1, source_target_pairs={{0,4},{4,8},{8,12},{12,0},{1,5},{5,9},{9,13},{13,1},{2,6},{6,10},{... | collective-permute-start | bytes 44 | tf_op jit(solution)/shard_map/ppermute | solution.py:186
  5.0 2.5 %fusion.134 = f32[128,2048]{1,0:T(8,128)S(1)} fusion(bf16[128,512]{1,0:T(8,128)(2,1)} %param.23, bf16[2048,512]{1,0:T(8,128)(2,1)} %param.22), kind=kOutput, calls=%fused_computation.242 | convolution fusion | flops 268435456 | bytes 3276800 | tf_op jit(solution)/shard_map/rd,cd->rc/dot_general | solution.py:214
  7.5 1.0 %constant_dynamic-slice_fusion.2 = (f32[128,512]{1,0:T(8,128)}, f32[128,512]{1,0:T(8,128)}, f32[128,512]{1,0:T(8,128)}) fusion(f32[128,2048]{1,0:T(8,128)S(1)} %fusion.134, s32[]{:T(128)S(6)} %select_n.426, s32[]{:T(128)S(6)} %select_n.428, s32[]{:T(128)S(6)} %select_n.427), kind=kLoop, calls=%fused_computation.216 | loop fusion | bytes 1572876 | tf_op jit(solution)/shard_map/dynamic_slice | solution.py:73
  8.5 0.6 collective-permute-start.3
  9.1 0.9 %collective-permute-start.2 = (f32[128,512]{1,0:T(8,128)}, f32[128,512]{1,0:T(8,128)}, u32[]{:S(2)}, u32[]{:S(2)}) collective-permute-start(f32[128,512]{1,0:T(8,128)} %get-tuple-element.55), channel_id=1, source_target_pairs={{0,2},{1,3},{2,0},{3,1},{4,6},{5,7},{6,4},{7,5},{8,10},{9,11},{10,... | collective-permute-start | bytes 786440 | tf_op jit(solution)/shard_map/ppermute | solution.py:64
  10.8 0.6 fusion.102
  11.7 0.7 %convolution_bitcast_fusion.2 = f32[128,1024]{1,0:T(8,128)S(1)} fusion(f32[512,1024]{1,0:T(8,128)S(1)} %bitcast.153, f32[1,1,128,512]{3,2,1,0:T(8,128)S(1)} %copy-done), kind=kOutput, calls=%fused_computation.7 | convolution fusion | flops 402653184 | bytes 2883584 | tf_op jit(solution)/shard_map/dot_general | solution.py:128
  12.5 0.9 %fusion.132 = (f32[127,1024]{1,0:T(8,128)S(1)}, f32[127,1024]{1,0:T(8,128)}) fusion(f32[128,1024]{1,0:T(8,128)S(1)} %convolution_bitcast_fusion.2), kind=kLoop, calls=%fused_computation.240 | loop fusion | bytes 2080768 | tf_op jit(solution)/shard_map/jit(_roll_static)/slice | solution.py:163
  13.4 0.9 %copy.28 = bf16[4,5,2048]{2,1,0:T(8,128)(2,1)S(1)} copy(bf16[4,5,2048]{2,0,1:T(4,128)(2,1)} %param.18) | data formatting | bytes 163840 | tf_op args[1]
  14.3 0.7 reshape.243
  15.0 1.2 %maximum_select_fusion = f32[128,1024]{1,0:T(8,128)S(1)} fusion(f32[1,1024]{1,0:T(1,128)S(1)} %get-tuple-element.63, f32[127,1024]{1,0:T(8,128)} %get-tuple-element.65, f32[127,1024]{1,0:T(8,128)S(1)} %get-tuple-element.64, f32[1,1024]{1,0:T(1,128)S(1)} %get-tuple-element.62, pred[128]{0:T(512)(128)(4,1)} %constant.94), kind=kLoop, calls=%fused_computation.38 | loop fusion | flops 393216 | bytes 1572992 | tf_op jit(solution)/shard_map/jit(_where)/select_n | solution.py:164
  16.6 0.4 multiply_reduce_fusion
  17.1 4.1 %convolution_bitcast_fusion.1 = f32[3,512,128]{1,2,0:T(8,128)S(1)} fusion(bf16[2048,3,512]{2,0,1:T(8,128)(2,1)} %param.20, f32[128,2048]{1,0:T(8,128)S(1)} %get-tuple-element.93, f32[2048]{0:T(1024)S(1)} %copy-done.5, f32[128]{0:T(128)S(1)} %add_rsqrt_fusion), kind=kOutput, calls=%fused_computation.5 | convolution fusion | flops 806092800 | bytes 8135168 | tf_op jit(solution)/shard_map/dr,dmc->mcr/dot_general | solution.py:203
  21.2 1.8 %collective-permute-done.2 = f32[128,512]{1,0:T(8,128)} collective-permute-done((f32[128,512]{1,0:T(8,128)}, f32[128,512]{1,0:T(8,128)}, u32[]{:S(2)}, u32[]{:S(2)}) %collective-permute-start.2) | collective-permute-done | bytes 262176 | tf_op jit(solution)/shard_map/ppermute | solution.py:64
  23.1 1.3 %fusion.55 = (bf16[1,512,128]{1,2,0:T(8,128)(2,1)S(1)}, f32[128,512]{1,0:T(8,128)S(1)}) fusion(f32[3,512,128]{1,2,0:T(8,128)S(1)} %convolution_bitcast_fusion.1, f32[128,512]{1,0:T(8,128)} %collective-permute-done.3, f32[128,512]{1,0:T(8,128)} %collective-permute-done.2, f32[128,512]{1,0:T(8,128)} %collective-permute-done.1, f32[128,2048]{1,0:T(8,128)} %copy-done.1, ...), kind=kLoop, calls=%fused_computation.132 | loop fusion | flops 393216 | bytes 1703940 | tf_op jit(solution)/shard_map/stack | solution.py:220
  24.4 2.1 %collective-permute-start.4 = (bf16[2,128,128]{1,2,0:T(8,128)(2,1)S(1)}, bf16[2,128,128]{1,2,0:T(8,128)(2,1)S(1)}, u32[]{:S(2)}, u32[]{:S(2)}) collective-permute-start(bf16[2,128,128]{1,2,0:T(8,128)(2,1)S(1)} %get-tuple-element.78), channel_id=1, source_target_pairs={{0,12},{4,8},{8,4},{12,0},{1,13},{5,9},{9,5},{13,1},{2,14},{6,10},... | collective-permute-start | bytes 196616 | tf_op jit(solution)/shard_map/ppermute | solution.py:64
  26.5 1.0 %collective-permute-start.5 = (bf16[2,128,128]{1,2,0:T(8,128)(2,1)S(1)}, bf16[2,128,128]{1,2,0:T(8,128)(2,1)S(1)}, u32[]{:S(2)}, u32[]{:S(2)}) collective-permute-start(bf16[2,128,128]{1,2,0:T(8,128)(2,1)S(1)} %get-tuple-element.79), channel_id=1, source_target_pairs={{0,8},{4,12},{8,0},{12,4},{1,9},{5,13},{9,1},{13,5},{2,10},{6,14},... | collective-permute-start | bytes 196616 | tf_op jit(solution)/shard_map/ppermute | solution.py:64
  27.5 1.3 %collective-permute-start.6 = (bf16[2,128,128]{1,2,0:T(8,128)(2,1)S(1)}, bf16[2,128,128]{1,2,0:T(8,128)(2,1)S(1)}, u32[]{:S(2)}, u32[]{:S(2)}) collective-permute-start(bf16[2,128,128]{1,2,0:T(8,128)(2,1)S(1)} %get-tuple-element.77), channel_id=1, source_target_pairs={{0,4},{4,0},{8,12},{12,8},{1,5},{5,1},{9,13},{13,9},{2,6},{6,2},{1... | collective-permute-start | bytes 196616 | tf_op jit(solution)/shard_map/ppermute | solution.py:64
  28.9 1.1 %fusion.1 = f32[3,512,128]{1,2,0:T(8,128)S(1)} fusion(f32[3,512,128]{1,2,0:T(8,128)S(1)} %convolution_bitcast_fusion.1, bf16[2048,3,512]{2,0,1:T(8,128)(2,1)S(1)} %bitcast.160, f32[128,2048]{1,0:T(8,128)S(1)} %get-tuple-element.93, f32[2048]{0:T(1024)S(1)} %copy-done.5, f32[128]{0:T(128)S(1)} %add_rsqrt_fusion), kind=kOutput, calls=%fused_computation.6 | convolution fusion | flops 807075840 | bytes 8921600 | tf_op jit(solution)/shard_map/dr,dmc->mcr/dot_general | solution.py:205
  30.0 0.7 %collective-permute-done.4 = bf16[2,128,128]{1,2,0:T(8,128)(2,1)S(1)} collective-permute-done((bf16[2,128,128]{1,2,0:T(8,128)(2,1)S(1)}, bf16[2,128,128]{1,2,0:T(8,128)(2,1)S(1)}, u32[]{:S(2)}, u32[]{:S(2)}) %collective-permute-start.4) | collective-permute-done | bytes 65568 | tf_op jit(solution)/shard_map/ppermute | solution.py:64
  30.7 3.1 %collective-permute-done.5 = bf16[2,128,128]{1,2,0:T(8,128)(2,1)S(1)} collective-permute-done((bf16[2,128,128]{1,2,0:T(8,128)(2,1)S(1)}, bf16[2,128,128]{1,2,0:T(8,128)(2,1)S(1)}, u32[]{:S(2)}, u32[]{:S(2)}) %collective-permute-start.5) | collective-permute-done | bytes 65568 | tf_op jit(solution)/shard_map/ppermute | solution.py:64
  34.0 0.6 fusion.71
  34.5 0.6 fusion.73
  35.4 0.4 copy-done.8
  36.5 1.0 %fusion.6 = bf16[1,128,512]{1,2,0:T(8,128)(2,1)S(1)} fusion(f32[512,1024]{1,0:T(8,128)S(1)} %bitcast.156, f32[128,512]{1,0:T(8,128)S(1)} %get-tuple-element.56, f32[128,512]{1,0:T(8,128)S(1)} %get-tuple-element.57, f32[1024]{0:T(1024)S(1)} %copy-done.6), kind=kOutput, calls=%fused_computation.15 | convolution fusion | flops 402980864 | bytes 2756608 | tf_op jit(solution)/shard_map/dot_general | solution.py:136
  37.5 1.0 %fusion.7 = bf16[1,128,512]{1,2,0:T(8,128)(2,1)S(1)} fusion(f32[512,1024]{1,0:T(8,128)S(1)} %bitcast.157, f32[128,512]{1,0:T(8,128)S(1)} %get-tuple-element.90, f32[128,512]{1,0:T(8,128)S(1)} %get-tuple-element.91, f32[1024]{0:T(1024)S(1)} %copy-done.6), kind=kOutput, calls=%fused_computation.16 | convolution fusion | flops 402980864 | bytes 2756608 | tf_op jit(solution)/shard_map/dot_general | solution.py:136
  38.6 2.5 %collective-permute-start.7 = (bf16[2,128,128]{1,2,0:T(8,128)(2,1)S(1)}, bf16[2,128,128]{1,2,0:T(8,128)(2,1)S(1)}, u32[]{:S(2)}, u32[]{:S(2)}) collective-permute-start(bf16[2,128,128]{1,2,0:T(8,128)(2,1)S(1)} %get-tuple-element.72), channel_id=1, source_target_pairs={{0,12},{4,8},{8,4},{12,0},{1,13},{5,9},{9,5},{13,1},{2,14},{6,10},... | collective-permute-start | bytes 196616 | tf_op jit(solution)/shard_map/ppermute | solution.py:64
  41.0 2.0 %collective-permute-start.9 = (bf16[2,128,128]{1,2,0:T(8,128)(2,1)S(1)}, bf16[2,128,128]{1,2,0:T(8,128)(2,1)S(1)}, u32[]{:S(2)}, u32[]{:S(2)}) collective-permute-start(bf16[2,128,128]{1,2,0:T(8,128)(2,1)S(1)} %get-tuple-element.71), channel_id=1, source_target_pairs={{0,4},{4,0},{8,12},{12,8},{1,5},{5,1},{9,13},{13,9},{2,6},{6,2},{1... | collective-permute-start | bytes 196616 | tf_op jit(solution)/shard_map/ppermute | solution.py:64
  43.2 1.5 %collective-permute-done.7 = bf16[2,128,128]{1,2,0:T(8,128)(2,1)S(1)} collective-permute-done((bf16[2,128,128]{1,2,0:T(8,128)(2,1)S(1)}, bf16[2,128,128]{1,2,0:T(8,128)(2,1)S(1)}, u32[]{:S(2)}, u32[]{:S(2)}) %collective-permute-start.7) | collective-permute-done | bytes 65568 | tf_op jit(solution)/shard_map/ppermute | solution.py:64
  44.8 2.0 %collective-permute-done.8 = bf16[2,128,128]{1,2,0:T(8,128)(2,1)S(1)} collective-permute-done((bf16[2,128,128]{1,2,0:T(8,128)(2,1)S(1)}, bf16[2,128,128]{1,2,0:T(8,128)(2,1)S(1)}, u32[]{:S(2)}, u32[]{:S(2)}) %collective-permute-start.8) | collective-permute-done | bytes 65568 | tf_op jit(solution)/shard_map/ppermute | solution.py:64
  47.1 2.2 %fusion.8 = (f32[2048]{0:T(1024)S(1)}, f32[128,2048,1]{1,0,2:T(8,128)S(1)}) fusion(f32[128,2048]{1,0:T(8,128)S(1)} %get-tuple-element.93, f32[128]{0:T(128)S(1)} %add_rsqrt_fusion, bf16[2048,3,512]{2,0,1:T(8,128)(2,1)S(1)} %bitcast.160, bf16[1,512,128]{1,2,0:T(8,128)(2,1)S(1)} %get-tuple-element.50, bf16[1,512,128]{1,2,0:T(8,128)(2,1)S(1)} %get-tuple-element.49, ...), kind=kOutput, calls=%fused_computation.18 | convolution fusion | flops 806483968 | bytes 8790528 | tf_op jit(solution)/shard_map/mcr,dmc->rd/dot_general | solution.py:257
  49.3 0.6 convolution_multiply_fusion.1
  50.1 1.0 %collective-permute-start.16 = (bf16[1,512,128]{1,2,0:T(8,128)(2,1)S(1)}, bf16[1,512,128]{1,2,0:T(8,128)(2,1)S(1)}, u32[]{:S(2)}, u32[]{:S(2)}) collective-permute-start(bf16[1,512,128]{1,2,0:T(8,128)(2,1)S(1)} %get-tuple-element.48), channel_id=1, source_target_pairs={{0,2},{2,0},{1,3},{3,1},{4,6},{6,4},{5,7},{7,5},{8,10},{10,8},{9,1... | collective-permute-start | bytes 393224 | tf_op jit(solution)/shard_map/ppermute | solution.py:47
  51.1 0.7 %fusion = f32[20,2048]{1,0:T(8,128)S(1)} fusion(f32[20,2048]{1,0:T(8,128)S(1)} %convolution_multiply_fusion.1, f32[128,2048]{1,0:T(8,128)S(1)} %get-tuple-element.93, f32[128]{0:T(128)S(1)} %add_rsqrt_fusion, f32[128]{0:T(128)S(1)} %multiply_reduce_fusion.1, pred[128,5]{0,1:T(8,128)(4,1)S(1)} %get-tuple-element.96, ...), kind=kOutput, calls=%fused_computation.1 | convolution fusion | flops 63276544 | bytes 1379840 | tf_op jit(solution)/shard_map/rk,dr->kd/dot_general | solution.py:262
  51.9 0.5 collective-permute-start.12
  52.4 0.7 %collective-permute-start.11 = (f32[21,512]{1,0:T(8,128)S(1)}, f32[21,512]{1,0:T(8,128)S(1)}, u32[]{:S(2)}, u32[]{:S(2)}) collective-permute-start(f32[21,512]{1,0:T(8,128)S(1)} %get-tuple-element.81), channel_id=1, source_target_pairs={{0,2},{1,3},{2,0},{3,1},{4,6},{5,7},{6,4},{7,5},{8,10},{9,11},{10,... | collective-permute-start | bytes 129032 | tf_op jit(solution)/shard_map/ppermute | solution.py:64
  53.1 0.7 %collective-permute-start.10 = (f32[21,512]{1,0:T(8,128)S(1)}, f32[21,512]{1,0:T(8,128)S(1)}, u32[]{:S(2)}, u32[]{:S(2)}) collective-permute-start(f32[21,512]{1,0:T(8,128)S(1)} %get-tuple-element.80), channel_id=1, source_target_pairs={{0,1},{1,0},{2,3},{3,2},{4,5},{5,4},{6,7},{7,6},{8,9},{9,8},{10,11... | collective-permute-start | bytes 129032 | tf_op jit(solution)/shard_map/ppermute | solution.py:64
  53.9 2.3 %collective-permute-done.16 = bf16[1,512,128]{1,2,0:T(8,128)(2,1)S(1)} collective-permute-done((bf16[1,512,128]{1,2,0:T(8,128)(2,1)S(1)}, bf16[1,512,128]{1,2,0:T(8,128)(2,1)S(1)}, u32[]{:S(2)}, u32[]{:S(2)}) %collective-permute-start.16) | collective-permute-done | bytes 131104 | tf_op jit(solution)/shard_map/ppermute | solution.py:47
  56.3 1.9 %fusion.23 = f32[128,512]{1,0:T(8,128)} fusion(f32[512,1024]{1,0:T(8,128)S(1)} %bitcast.158, f32[128,512]{1,0:T(8,128)S(1)} %get-tuple-element.59, f32[128,512]{1,0:T(8,128)S(1)} %get-tuple-element.58, f32[1024]{0:T(1024)S(1)} %copy-done.6), kind=kOutput, calls=%fused_computation.47 | convolution fusion | flops 402915328 | bytes 2887680 | tf_op jit(solution)/shard_map/dot_general | solution.py:136
  58.3 0.5 collective-permute-start.13
  58.8 2.5 %collective-permute-start.14 = (f32[21,512]{1,0:T(8,128)S(1)}, f32[21,512]{1,0:T(8,128)S(1)}, u32[]{:S(2)}, u32[]{:S(2)}) collective-permute-start(f32[21,512]{1,0:T(8,128)S(1)} %fusion.108), channel_id=1, source_target_pairs={{0,8},{4,12},{8,0},{12,4},{1,9},{5,13},{9,1},{13,5},{2,10},{6,14},... | collective-permute-start | bytes 129032 | tf_op jit(solution)/shard_map/ppermute | solution.py:64
  61.3 1.4 %collective-permute-start.15 = (f32[21,512]{1,0:T(8,128)S(1)}, f32[21,512]{1,0:T(8,128)S(1)}, u32[]{:S(2)}, u32[]{:S(2)}) collective-permute-start(f32[21,512]{1,0:T(8,128)S(1)} %fusion.108), channel_id=1, source_target_pairs={{0,12},{4,8},{8,4},{12,0},{1,13},{5,9},{9,5},{13,1},{2,14},{6,10},... | collective-permute-start | bytes 129032 | tf_op jit(solution)/shard_map/ppermute | solution.py:64
  63.4 0.9 %fusion.5 = bf16[128,512]{1,0:T(8,128)(2,1)} fusion(f32[128,512]{1,0:T(8,128)S(1)} %fusion.26, f32[128,512]{1,0:T(8,128)S(1)} %fusion.28, f32[128,512]{1,0:T(8,128)S(1)} %fusion.30, bf16[2048,512]{1,0:T(8,128)(2,1)S(1)} %copy-done.2, f32[128,2048]{1,0:T(8,128)S(1)} %get-tuple-element.93, s32[]{:T(128)S(6)} %select_n.425, ...), kind=kOutput, calls=%fused_computation.14 | convolution fusion | flops 67633152 | bytes 2228231 | tf_op jit(solution)/shard_map/cr,cd->rd/dot_general | solution.py:242
  64.4 0.6 collective-permute-done.14
  65.0 2.2 %collective-permute-done.15 = f32[21,512]{1,0:T(8,128)S(1)} collective-permute-done((f32[21,512]{1,0:T(8,128)S(1)}, f32[21,512]{1,0:T(8,128)S(1)}, u32[]{:S(2)}, u32[]{:S(2)}) %collective-permute-start.15) | collective-permute-done | bytes 43040 | tf_op jit(solution)/shard_map/ppermute | solution.py:64
  67.2 0.6 slice.194
  67.8 0.6 copy.31
  (81 shorter events, 4.3 us)
Async XLA Ops:
  0.6 11.1 %copy-start = (f32[1,1,128,512]{3,2,1,0:T(8,128)S(1)}, f32[1,1,128,512]{3,2,1,0:T(8,128)}, u32[]{:S(2)}) copy-start(f32[1,1,128,512]{3,2,1,0:T(8,128)} %param.21) | copy-start | bytes 786436
  1.9 14.5 %collective-permute-start = (s32[3]{0:T(128)}, s32[3]{0:T(128)}, u32[]{:S(2)}, u32[]{:S(2)}) collective-permute-start(s32[3]{0:T(128)} %slice.127), channel_id=1, source_target_pairs={{0,4},{4,8},{8,12},{12,0},{1,5},{5,9},{9,13},{13,1},{2,6},{6,10},{... | collective-permute-start | bytes 44 | tf_op jit(solution)/shard_map/ppermute | solution.py:186
  5.0 5.4 %copy-start.9 = (s32[128]{0:T(128)S(1)}, s32[128]{0:T(128)}, u32[]{:S(2)}) copy-start(s32[128]{0:T(128)} %param.17) | copy-start | bytes 1540
  7.5 3.9 %copy-start.1 = (f32[128,2048]{1,0:T(8,128)}, f32[128,2048]{1,0:T(8,128)S(1)}, u32[]{:S(2)}) copy-start(f32[128,2048]{1,0:T(8,128)S(1)} %fusion.134) | copy-start | bytes 3145732
  8.5 12.7 %collective-permute-start.3 = (f32[128,512]{1,0:T(8,128)}, f32[128,512]{1,0:T(8,128)}, u32[]{:S(2)}, u32[]{:S(2)}) collective-permute-start(f32[128,512]{1,0:T(8,128)} %get-tuple-element.54), channel_id=1, source_target_pairs={{0,3},{1,2},{2,1},{3,0},{4,7},{5,6},{6,5},{7,4},{8,11},{9,10},{10,... | collective-permute-start | bytes 786440 | tf_op jit(solution)/shard_map/ppermute | solution.py:64
  9.1 13.9 %collective-permute-start.2 = (f32[128,512]{1,0:T(8,128)}, f32[128,512]{1,0:T(8,128)}, u32[]{:S(2)}, u32[]{:S(2)}) collective-permute-start(f32[128,512]{1,0:T(8,128)} %get-tuple-element.55), channel_id=1, source_target_pairs={{0,2},{1,3},{2,0},{3,1},{4,6},{5,7},{6,4},{7,5},{8,10},{9,11},{10,... | collective-permute-start | bytes 786440 | tf_op jit(solution)/shard_map/ppermute | solution.py:64
  10.0 13.0 %collective-permute-start.1 = (f32[128,512]{1,0:T(8,128)}, f32[128,512]{1,0:T(8,128)}, u32[]{:S(2)}, u32[]{:S(2)}) collective-permute-start(f32[128,512]{1,0:T(8,128)} %get-tuple-element.53), channel_id=1, source_target_pairs={{0,1},{1,0},{2,3},{3,2},{4,5},{5,4},{6,7},{7,6},{8,9},{9,8},{10,11... | collective-permute-start | bytes 786440 | tf_op jit(solution)/shard_map/ppermute | solution.py:64
  12.4 3.8 %copy-start.7 = (pred[512]{0:T(512)(128)(4,1)S(1)}, pred[512]{0:T(512)(128)(4,1)}, u32[]{:S(2)}) copy-start(pred[512]{0:T(512)(128)(4,1)} %constant.93) | copy-start | bytes 1540
  15.0 1.4 %copy-start.10 = (s32[128]{0:T(128)S(1)}, s32[128]{0:T(128)}, u32[]{:S(2)}) copy-start(s32[128]{0:T(128)} %param.17) | copy-start | bytes 1540
  15.0 1.6 %copy-start.4 = (bf16[20,2048]{1,0:T(8,128)(2,1)S(1)}, bf16[20,2048]{1,0:T(8,128)(2,1)}, u32[]{:S(2)}) copy-start(bf16[20,2048]{1,0:T(8,128)(2,1)} %reshape.243) | copy-start | bytes 245764
  16.2 0.8 %copy-start.5 = (f32[2048]{0:T(1024)S(1)}, f32[2048]{0:T(1024)}, u32[]{:S(2)}) copy-start(f32[2048]{0:T(1024)} %param.19) | copy-start | bytes 24580
  16.6 12.3 %slice-start = ((s8[6291456]{0:T(1024)(128)(4,1)}), s8[4194304]{0:T(1024)(128)(4,1)S(1)}, s32[]{:S(2)}) async-start(s8[6291456]{0:T(1024)(128)(4,1)} %bitcast.159), calls=%async_computation | async-start | bytes 8388608
  17.1 11.8 %slice-start.1 = ((s8[6291456]{0:T(1024)(128)(4,1)}), s8[2097152]{0:T(1024)(128)(4,1)S(1)}, s32[]{:S(2)}) async-start(s8[6291456]{0:T(1024)(128)(4,1)} %bitcast.159), calls=%async_computation.1 | async-start | bytes 4194304
  24.4 6.3 %collective-permute-start.4 = (bf16[2,128,128]{1,2,0:T(8,128)(2,1)S(1)}, bf16[2,128,128]{1,2,0:T(8,128)(2,1)S(1)}, u32[]{:S(2)}, u32[]{:S(2)}) collective-permute-start(bf16[2,128,128]{1,2,0:T(8,128)(2,1)S(1)} %get-tuple-element.78), channel_id=1, source_target_pairs={{0,12},{4,8},{8,4},{12,0},{1,13},{5,9},{9,5},{13,1},{2,14},{6,10},... | collective-permute-start | bytes 196616 | tf_op jit(solution)/shard_map/ppermute | solution.py:64
  26.5 7.3 %collective-permute-start.5 = (bf16[2,128,128]{1,2,0:T(8,128)(2,1)S(1)}, bf16[2,128,128]{1,2,0:T(8,128)(2,1)S(1)}, u32[]{:S(2)}, u32[]{:S(2)}) collective-permute-start(bf16[2,128,128]{1,2,0:T(8,128)(2,1)S(1)} %get-tuple-element.79), channel_id=1, source_target_pairs={{0,8},{4,12},{8,0},{12,4},{1,9},{5,13},{9,1},{13,5},{2,10},{6,14},... | collective-permute-start | bytes 196616 | tf_op jit(solution)/shard_map/ppermute | solution.py:64
  27.5 6.3 %collective-permute-start.6 = (bf16[2,128,128]{1,2,0:T(8,128)(2,1)S(1)}, bf16[2,128,128]{1,2,0:T(8,128)(2,1)S(1)}, u32[]{:S(2)}, u32[]{:S(2)}) collective-permute-start(bf16[2,128,128]{1,2,0:T(8,128)(2,1)S(1)} %get-tuple-element.77), channel_id=1, source_target_pairs={{0,4},{4,0},{8,12},{12,8},{1,5},{5,1},{9,13},{13,9},{2,6},{6,2},{1... | collective-permute-start | bytes 196616 | tf_op jit(solution)/shard_map/ppermute | solution.py:64
  35.1 0.7 copy-start.8
  35.8 0.7 %copy-start.6 = (f32[1024]{0:T(1024)S(1)}, f32[1024]{0:T(1024)}, u32[]{:S(2)}) copy-start(f32[1024]{0:T(1024)} %constant.95) | copy-start | bytes 12292
  37.5 5.5 %copy-start.3 = (bf16[128,512]{1,0:T(8,128)(2,1)S(1)}, bf16[128,512]{1,0:T(8,128)(2,1)}, u32[]{:S(2)}) copy-start(bf16[128,512]{1,0:T(8,128)(2,1)} %param.23) | copy-start | bytes 393220
  38.6 6.2 %collective-permute-start.7 = (bf16[2,128,128]{1,2,0:T(8,128)(2,1)S(1)}, bf16[2,128,128]{1,2,0:T(8,128)(2,1)S(1)}, u32[]{:S(2)}, u32[]{:S(2)}) collective-permute-start(bf16[2,128,128]{1,2,0:T(8,128)(2,1)S(1)} %get-tuple-element.72), channel_id=1, source_target_pairs={{0,12},{4,8},{8,4},{12,0},{1,13},{5,9},{9,5},{13,1},{2,14},{6,10},... | collective-permute-start | bytes 196616 | tf_op jit(solution)/shard_map/ppermute | solution.py:64
  41.0 5.8 %collective-permute-start.8 = (bf16[2,128,128]{1,2,0:T(8,128)(2,1)S(1)}, bf16[2,128,128]{1,2,0:T(8,128)(2,1)S(1)}, u32[]{:S(2)}, u32[]{:S(2)}) collective-permute-start(bf16[2,128,128]{1,2,0:T(8,128)(2,1)S(1)} %get-tuple-element.73), channel_id=1, source_target_pairs={{0,8},{4,12},{8,0},{12,4},{1,9},{5,13},{9,1},{13,5},{2,10},{6,14},... | collective-permute-start | bytes 196616 | tf_op jit(solution)/shard_map/ppermute | solution.py:64
  41.0 5.8 %collective-permute-start.9 = (bf16[2,128,128]{1,2,0:T(8,128)(2,1)S(1)}, bf16[2,128,128]{1,2,0:T(8,128)(2,1)S(1)}, u32[]{:S(2)}, u32[]{:S(2)}) collective-permute-start(bf16[2,128,128]{1,2,0:T(8,128)(2,1)S(1)} %get-tuple-element.71), channel_id=1, source_target_pairs={{0,4},{4,0},{8,12},{12,8},{1,5},{5,1},{9,13},{13,9},{2,6},{6,2},{1... | collective-permute-start | bytes 196616 | tf_op jit(solution)/shard_map/ppermute | solution.py:64
  50.1 6.1 %collective-permute-start.16 = (bf16[1,512,128]{1,2,0:T(8,128)(2,1)S(1)}, bf16[1,512,128]{1,2,0:T(8,128)(2,1)S(1)}, u32[]{:S(2)}, u32[]{:S(2)}) collective-permute-start(bf16[1,512,128]{1,2,0:T(8,128)(2,1)S(1)} %get-tuple-element.48), channel_id=1, source_target_pairs={{0,2},{2,0},{1,3},{3,1},{4,6},{6,4},{5,7},{7,5},{8,10},{10,8},{9,1... | collective-permute-start | bytes 393224 | tf_op jit(solution)/shard_map/ppermute | solution.py:47
  51.8 10.9 %copy-start.2 = (bf16[2048,512]{1,0:T(8,128)(2,1)S(1)}, bf16[2048,512]{1,0:T(8,128)(2,1)}, u32[]{:S(2)}) copy-start(bf16[2048,512]{1,0:T(8,128)(2,1)} %param.22) | copy-start | bytes 6291460
  51.9 6.3 %collective-permute-start.12 = (f32[21,512]{1,0:T(8,128)S(1)}, f32[21,512]{1,0:T(8,128)S(1)}, u32[]{:S(2)}, u32[]{:S(2)}) collective-permute-start(f32[21,512]{1,0:T(8,128)S(1)} %get-tuple-element.82), channel_id=1, source_target_pairs={{0,3},{1,2},{2,1},{3,0},{4,7},{5,6},{6,5},{7,4},{8,11},{9,10},{10,... | collective-permute-start | bytes 129032 | tf_op jit(solution)/shard_map/ppermute | solution.py:64
  52.4 5.8 %collective-permute-start.11 = (f32[21,512]{1,0:T(8,128)S(1)}, f32[21,512]{1,0:T(8,128)S(1)}, u32[]{:S(2)}, u32[]{:S(2)}) collective-permute-start(f32[21,512]{1,0:T(8,128)S(1)} %get-tuple-element.81), channel_id=1, source_target_pairs={{0,2},{1,3},{2,0},{3,1},{4,6},{5,7},{6,4},{7,5},{8,10},{9,11},{10,... | collective-permute-start | bytes 129032 | tf_op jit(solution)/shard_map/ppermute | solution.py:64
  53.1 5.0 %collective-permute-start.10 = (f32[21,512]{1,0:T(8,128)S(1)}, f32[21,512]{1,0:T(8,128)S(1)}, u32[]{:S(2)}, u32[]{:S(2)}) collective-permute-start(f32[21,512]{1,0:T(8,128)S(1)} %get-tuple-element.80), channel_id=1, source_target_pairs={{0,1},{1,0},{2,3},{3,2},{4,5},{5,4},{6,7},{7,6},{8,9},{9,8},{10,11... | collective-permute-start | bytes 129032 | tf_op jit(solution)/shard_map/ppermute | solution.py:64
  56.2 6.5 %collective-permute-start.17 = (bf16[2,512,128]{1,2,0:T(8,128)(2,1)S(1)}, bf16[2,512,128]{1,2,0:T(8,128)(2,1)S(1)}, u32[]{:S(2)}, u32[]{:S(2)}) collective-permute-start(bf16[2,512,128]{1,2,0:T(8,128)(2,1)S(1)} %pad_maximum_fusion.5), channel_id=1, source_target_pairs={{0,1},{1,0},{2,3},{3,2},{4,5},{5,4},{6,7},{7,6},{8,9},{9,8},{10,11... | collective-permute-start | bytes 786440 | tf_op jit(solution)/shard_map/ppermute | solution.py:47
  58.3 6.1 %collective-permute-start.13 = (f32[21,512]{1,0:T(8,128)S(1)}, f32[21,512]{1,0:T(8,128)S(1)}, u32[]{:S(2)}, u32[]{:S(2)}) collective-permute-start(f32[21,512]{1,0:T(8,128)S(1)} %fusion.108), channel_id=1, source_target_pairs={{0,4},{4,0},{8,12},{12,8},{1,5},{5,1},{9,13},{13,9},{2,6},{6,2},{1... | collective-permute-start | bytes 129032 | tf_op jit(solution)/shard_map/ppermute | solution.py:64
  58.8 6.2 %collective-permute-start.14 = (f32[21,512]{1,0:T(8,128)S(1)}, f32[21,512]{1,0:T(8,128)S(1)}, u32[]{:S(2)}, u32[]{:S(2)}) collective-permute-start(f32[21,512]{1,0:T(8,128)S(1)} %fusion.108), channel_id=1, source_target_pairs={{0,8},{4,12},{8,0},{12,4},{1,9},{5,13},{9,1},{13,5},{2,10},{6,14},... | collective-permute-start | bytes 129032 | tf_op jit(solution)/shard_map/ppermute | solution.py:64
  61.3 5.9 %collective-permute-start.15 = (f32[21,512]{1,0:T(8,128)S(1)}, f32[21,512]{1,0:T(8,128)S(1)}, u32[]{:S(2)}, u32[]{:S(2)}) collective-permute-start(f32[21,512]{1,0:T(8,128)S(1)} %fusion.108), channel_id=1, source_target_pairs={{0,12},{4,8},{8,4},{12,0},{1,13},{5,9},{9,5},{13,1},{2,14},{6,10},... | collective-permute-start | bytes 129032 | tf_op jit(solution)/shard_map/ppermute | solution.py:64

commit v19 on v17

--- a/solution.py
+++ b/solution.py
@@ -91,11 +91,10 @@
     sent = {offset: group_exchange(x, "seq", count, offset) for offset in range(count - 1, 0, -1)}
     got = [x] + [sent[offset] for offset in range(1, count)]
     got, tied = lax.optimization_barrier((got, tied))
+    stacked = jnp.stack(got)
     total = None
     for source in range(count):
-        piece = got[0]
-        for offset in range(1, count):
-            piece = jnp.where((me ^ source) == offset, got[offset], piece)
+        piece = lax.dynamic_index_in_dim(stacked, me ^ source, 0, keepdims=False)
         total = piece if total is None else total + piece
     return total, tied
 

time: 68.4 us -> 68.4 us (level)
  no operation moved by 1% of the time
where the time goes in v19:
time: 68.4 us; the launch traced here: 68.2 us
  starting transfers between devices  22.6 us (33%)
  matrix products  19.2 us (28%)
  waiting for transfers between devices  12.8 us (19%)
  local copies, waits for them, and re-layouts  6.89 us (10%)
  other arithmetic  5.62 us (8%)
  between operations  1.12 us (2%)
    ppermute x15, starting transfers between devices, group_exchange(): return lax.ppermute(x, axes, [(i, i ^ offset) for i in range(count)])  17.5 us
    ppermute x15, waiting for transfers between devices, group_exchange(): return lax.ppermute(x, axes, [(i, i ^ offset) for i in range(count)])  12.8 us
    dot_general x1, matrix products, per_device(): jnp.einsum('dr,dmc->mcr', hidden, in_proj, preferred_element_type=jnp.flo...  4.01 us
    dot_general x3, matrix products, inverse_dft(): lax.dot_general(spec * weight, dft, (((1,), (1,)), ((), ())), precision=T...  3.86 us
    ppermute x1, starting transfers between devices, per_device(): lax.ppermute(tokens[row_count - rim_width:], 'seq', [(i, (i + 1) % seq_co...  3.05 us
    dot_general x1, matrix products, per_device(): jnp.einsum('rd,cd->rc', cotangent, out_proj, preferred_element_type=jnp.f...  2.48 us
    unnamed x30, local copies, waits for them, and re-layouts  2.43 us
    dot_general x1, matrix products, per_device(): jnp.einsum('mcr,dmc->rd', d_proj, in_proj, preferred_element_type=jnp.flo...  2.16 us
  transfers between devices with their start and end apart: 18, of which 7 were waited for; matrix products, arithmetic and copies ran while one was open for 29% of the time, Pallas kernels for 0%

profile of v19, /device:TPU:0, one launch (start us, length us, event | category | flops | bytes accessed | tf_op | source)
XLA Modules:
  0.0 68.2 jit_solution(15321749718591984010)
XLA Ops:
  0.6 1.3 %slice.153 = s32[3]{0:T(128)} slice(s32[128]{0:T(128)} %param.17), slice={[125:128]} | slice | bytes 24 | tf_op jit(solution)/shard_map/slice | solution.py:190
  1.9 3.1 %collective-permute-start = (s32[3]{0:T(128)}, s32[3]{0:T(128)}, u32[]{:S(2)}, u32[]{:S(2)}) collective-permute-start(s32[3]{0:T(128)} %slice.153), channel_id=1, source_target_pairs={{0,4},{4,8},{8,12},{12,0},{1,5},{5,9},{9,13},{13,1},{2,6},{6,10},{... | collective-permute-start | bytes 44 | tf_op jit(solution)/shard_map/ppermute | solution.py:189
  5.0 2.5 %fusion.136 = f32[128,2048]{1,0:T(8,128)S(1)} fusion(bf16[128,512]{1,0:T(8,128)(2,1)} %param.23, bf16[2048,512]{1,0:T(8,128)(2,1)} %param.22), kind=kOutput, calls=%fused_computation.247 | convolution fusion | flops 268435456 | bytes 3276800 | tf_op jit(solution)/shard_map/rd,cd->rc/dot_general | solution.py:217
  7.5 1.0 %copy-done.1 = f32[128,2048]{1,0:T(8,128)} copy-done((f32[128,2048]{1,0:T(8,128)}, f32[128,2048]{1,0:T(8,128)S(1)}, u32[]{:S(2)}) %copy-start.1) | copy-done | bytes 1048600
  8.5 0.9 %constant_dynamic-slice_fusion.2 = (f32[128,512]{1,0:T(8,128)}, f32[128,512]{1,0:T(8,128)}, f32[128,512]{1,0:T(8,128)}) fusion(f32[128,2048]{1,0:T(8,128)S(1)} %fusion.136, s32[]{:T(128)S(6)} %select_n.445, s32[]{:T(128)S(6)} %select_n.447, s32[]{:T(128)S(6)} %select_n.446), kind=kLoop, calls=%fused_computation.224 | loop fusion | bytes 1572876 | tf_op jit(solution)/shard_map/dynamic_slice | solution.py:73
  9.4 1.6 %collective-permute-start.3 = (f32[128,512]{1,0:T(8,128)}, f32[128,512]{1,0:T(8,128)}, u32[]{:S(2)}, u32[]{:S(2)}) collective-permute-start(f32[128,512]{1,0:T(8,128)} %get-tuple-element.64), channel_id=1, source_target_pairs={{0,3},{1,2},{2,1},{3,0},{4,7},{5,6},{6,5},{7,4},{8,11},{9,10},{10,... | collective-permute-start | bytes 786440 | tf_op jit(solution)/shard_map/ppermute | solution.py:64
  11.0 0.5 collective-permute-start.2
  11.9 0.6 fusion.100
  12.8 0.7 %convolution_bitcast_fusion.2 = f32[128,1024]{1,0:T(8,128)S(1)} fusion(f32[512,1024]{1,0:T(8,128)S(1)} %bitcast.157, f32[1,1,128,512]{3,2,1,0:T(8,128)S(1)} %copy-done), kind=kOutput, calls=%fused_computation.7 | convolution fusion | flops 402653184 | bytes 2883584 | tf_op jit(solution)/shard_map/dot_general | solution.py:131
  13.6 0.9 %fusion.134 = (f32[127,1024]{1,0:T(8,128)S(1)}, f32[127,1024]{1,0:T(8,128)}) fusion(f32[128,1024]{1,0:T(8,128)S(1)} %convolution_bitcast_fusion.2), kind=kLoop, calls=%fused_computation.245 | loop fusion | bytes 2080768 | tf_op jit(solution)/shard_map/jit(_roll_static)/slice | solution.py:166
  14.6 0.7 reshape.250
  15.3 1.2 %maximum_select_fusion = f32[128,1024]{1,0:T(8,128)S(1)} fusion(f32[1,1024]{1,0:T(1,128)S(1)} %get-tuple-element.73, f32[127,1024]{1,0:T(8,128)} %get-tuple-element.75, f32[127,1024]{1,0:T(8,128)S(1)} %get-tuple-element.74, f32[1,1024]{1,0:T(1,128)S(1)} %get-tuple-element.72, pred[128]{0:T(512)(128)(4,1)} %constant.103), kind=kLoop, calls=%fused_computation.38 | loop fusion | flops 393216 | bytes 1572992 | tf_op jit(solution)/shard_map/jit(_where)/select_n | solution.py:167
  16.8 0.4 multiply_reduce_fusion
  17.3 4.0 %convolution_bitcast_fusion.1 = f32[3,512,128]{1,2,0:T(8,128)S(1)} fusion(bf16[2048,3,512]{2,0,1:T(8,128)(2,1)} %param.20, f32[128,2048]{1,0:T(8,128)S(1)} %get-tuple-element.101, f32[2048]{0:T(1024)S(1)} %copy-done.6, f32[128]{0:T(128)S(1)} %add_rsqrt_fusion), kind=kOutput, calls=%fused_computation.5 | convolution fusion | flops 806092800 | bytes 8135168 | tf_op jit(solution)/shard_map/dr,dmc->mcr/dot_general | solution.py:206
  21.4 2.5 %collective-permute-done.2 = f32[128,512]{1,0:T(8,128)} collective-permute-done((f32[128,512]{1,0:T(8,128)}, f32[128,512]{1,0:T(8,128)}, u32[]{:S(2)}, u32[]{:S(2)}) %collective-permute-start.2) | collective-permute-done | bytes 262176 | tf_op jit(solution)/shard_map/ppermute | solution.py:64
  23.9 1.3 %fusion.55 = (bf16[1,512,128]{1,2,0:T(8,128)(2,1)S(1)}, f32[128,512]{1,0:T(8,128)S(1)}) fusion(f32[3,512,128]{1,2,0:T(8,128)S(1)} %convolution_bitcast_fusion.1, f32[128,512]{1,0:T(8,128)} %collective-permute-done.3, f32[128,512]{1,0:T(8,128)} %collective-permute-done.2, f32[128,512]{1,0:T(8,128)} %collective-permute-done.1, f32[128,2048]{1,0:T(8,128)} %copy-done.1, ...), kind=kLoop, calls=%fused_computation.129 | loop fusion | flops 393216 | bytes 1703940 | tf_op jit(solution)/shard_map/stack | solution.py:223
  25.3 1.6 %collective-permute-start.6 = (bf16[2,128,128]{1,2,0:T(8,128)(2,1)S(1)}, bf16[2,128,128]{1,2,0:T(8,128)(2,1)S(1)}, u32[]{:S(2)}, u32[]{:S(2)}) collective-permute-start(bf16[2,128,128]{1,2,0:T(8,128)(2,1)S(1)} %get-tuple-element.45), channel_id=1, source_target_pairs={{0,4},{4,0},{8,12},{12,8},{1,5},{5,1},{9,13},{13,9},{2,6},{6,2},{1... | collective-permute-start | bytes 196616 | tf_op jit(solution)/shard_map/ppermute | solution.py:64
  26.9 1.2 %collective-permute-start.5 = (bf16[2,128,128]{1,2,0:T(8,128)(2,1)S(1)}, bf16[2,128,128]{1,2,0:T(8,128)(2,1)S(1)}, u32[]{:S(2)}, u32[]{:S(2)}) collective-permute-start(bf16[2,128,128]{1,2,0:T(8,128)(2,1)S(1)} %get-tuple-element.86), channel_id=1, source_target_pairs={{0,8},{4,12},{8,0},{12,4},{1,9},{5,13},{9,1},{13,5},{2,10},{6,14},... | collective-permute-start | bytes 196616 | tf_op jit(solution)/shard_map/ppermute | solution.py:64
  28.1 1.7 %collective-permute-start.4 = (bf16[2,128,128]{1,2,0:T(8,128)(2,1)S(1)}, bf16[2,128,128]{1,2,0:T(8,128)(2,1)S(1)}, u32[]{:S(2)}, u32[]{:S(2)}) collective-permute-start(bf16[2,128,128]{1,2,0:T(8,128)(2,1)S(1)} %get-tuple-element.87), channel_id=1, source_target_pairs={{0,12},{4,8},{8,4},{12,0},{1,13},{5,9},{9,5},{13,1},{2,14},{6,10},... | collective-permute-start | bytes 196616 | tf_op jit(solution)/shard_map/ppermute | solution.py:64
  29.8 1.1 %fusion.1 = f32[3,512,128]{1,2,0:T(8,128)S(1)} fusion(f32[3,512,128]{1,2,0:T(8,128)S(1)} %convolution_bitcast_fusion.1, bf16[2048,3,512]{2,0,1:T(8,128)(2,1)S(1)} %bitcast.164, f32[128,2048]{1,0:T(8,128)S(1)} %get-tuple-element.101, f32[2048]{0:T(1024)S(1)} %copy-done.6, f32[128]{0:T(128)S(1)} %add_rsqrt_fusion), kind=kOutput, calls=%fused_computation.6 | convolution fusion | flops 807075840 | bytes 8921600 | tf_op jit(solution)/shard_map/dr,dmc->mcr/dot_general | solution.py:208
  31.0 3.6 %collective-permute-done.5 = bf16[2,128,128]{1,2,0:T(8,128)(2,1)S(1)} collective-permute-done((bf16[2,128,128]{1,2,0:T(8,128)(2,1)S(1)}, bf16[2,128,128]{1,2,0:T(8,128)(2,1)S(1)}, u32[]{:S(2)}, u32[]{:S(2)}) %collective-permute-start.5) | collective-permute-done | bytes 65568 | tf_op jit(solution)/shard_map/ppermute | solution.py:64
  34.7 0.6 fusion.71
  35.2 0.6 fusion.73
  36.1 0.4 copy-done.9
  37.1 1.0 %fusion.6 = bf16[1,128,512]{1,2,0:T(8,128)(2,1)S(1)} fusion(f32[512,1024]{1,0:T(8,128)S(1)} %bitcast.160, f32[128,512]{1,0:T(8,128)S(1)} %get-tuple-element.66, f32[128,512]{1,0:T(8,128)S(1)} %get-tuple-element.67, f32[1024]{0:T(1024)S(1)} %copy-done.7), kind=kOutput, calls=%fused_computation.15 | convolution fusion | flops 402980864 | bytes 2756608 | tf_op jit(solution)/shard_map/dot_general | solution.py:139
  38.1 1.0 %fusion.7 = bf16[1,128,512]{1,2,0:T(8,128)(2,1)S(1)} fusion(f32[512,1024]{1,0:T(8,128)S(1)} %bitcast.161, f32[128,512]{1,0:T(8,128)S(1)} %get-tuple-element.98, f32[128,512]{1,0:T(8,128)S(1)} %get-tuple-element.99, f32[1024]{0:T(1024)S(1)} %copy-done.7), kind=kOutput, calls=%fused_computation.16 | convolution fusion | flops 402980864 | bytes 2756608 | tf_op jit(solution)/shard_map/dot_general | solution.py:139
  39.2 1.3 %collective-permute-start.9 = (bf16[2,128,128]{1,2,0:T(8,128)(2,1)S(1)}, bf16[2,128,128]{1,2,0:T(8,128)(2,1)S(1)}, u32[]{:S(2)}, u32[]{:S(2)}) collective-permute-start(bf16[2,128,128]{1,2,0:T(8,128)(2,1)S(1)} %get-tuple-element.38), channel_id=1, source_target_pairs={{0,4},{4,0},{8,12},{12,8},{1,5},{5,1},{9,13},{13,9},{2,6},{6,2},{1... | collective-permute-start | bytes 196616 | tf_op jit(solution)/shard_map/ppermute | solution.py:64
  40.5 1.6 %collective-permute-start.8 = (bf16[2,128,128]{1,2,0:T(8,128)(2,1)S(1)}, bf16[2,128,128]{1,2,0:T(8,128)(2,1)S(1)}, u32[]{:S(2)}, u32[]{:S(2)}) collective-permute-start(bf16[2,128,128]{1,2,0:T(8,128)(2,1)S(1)} %get-tuple-element.81), channel_id=1, source_target_pairs={{0,8},{4,12},{8,0},{12,4},{1,9},{5,13},{9,1},{13,5},{2,10},{6,14},... | collective-permute-start | bytes 196616 | tf_op jit(solution)/shard_map/ppermute | solution.py:64
  42.1 1.6 %collective-permute-start.7 = (bf16[2,128,128]{1,2,0:T(8,128)(2,1)S(1)}, bf16[2,128,128]{1,2,0:T(8,128)(2,1)S(1)}, u32[]{:S(2)}, u32[]{:S(2)}) collective-permute-start(bf16[2,128,128]{1,2,0:T(8,128)(2,1)S(1)} %get-tuple-element.82), channel_id=1, source_target_pairs={{0,12},{4,8},{8,4},{12,0},{1,13},{5,9},{9,5},{13,1},{2,14},{6,10},... | collective-permute-start | bytes 196616 | tf_op jit(solution)/shard_map/ppermute | solution.py:64
  44.0 3.0 %collective-permute-done.8 = bf16[2,128,128]{1,2,0:T(8,128)(2,1)S(1)} collective-permute-done((bf16[2,128,128]{1,2,0:T(8,128)(2,1)S(1)}, bf16[2,128,128]{1,2,0:T(8,128)(2,1)S(1)}, u32[]{:S(2)}, u32[]{:S(2)}) %collective-permute-start.8) | collective-permute-done | bytes 65568 | tf_op jit(solution)/shard_map/ppermute | solution.py:64
  46.9 1.3 %collective-permute-done.7 = bf16[2,128,128]{1,2,0:T(8,128)(2,1)S(1)} collective-permute-done((bf16[2,128,128]{1,2,0:T(8,128)(2,1)S(1)}, bf16[2,128,128]{1,2,0:T(8,128)(2,1)S(1)}, u32[]{:S(2)}, u32[]{:S(2)}) %collective-permute-start.7) | collective-permute-done | bytes 65568 | tf_op jit(solution)/shard_map/ppermute | solution.py:64
  48.6 2.2 %fusion.8 = (f32[2048]{0:T(1024)S(1)}, f32[128,2048,1]{1,0,2:T(8,128)S(1)}) fusion(f32[128,2048]{1,0:T(8,128)S(1)} %get-tuple-element.101, f32[128]{0:T(128)S(1)} %add_rsqrt_fusion, bf16[2048,3,512]{2,0,1:T(8,128)(2,1)S(1)} %bitcast.164, bf16[1,512,128]{1,2,0:T(8,128)(2,1)S(1)} %get-tuple-element.60, bf16[1,512,128]{1,2,0:T(8,128)(2,1)S(1)} %get-tuple-element.59, ...), kind=kOutput, calls=%fused_computation.18 | convolution fusion | flops 806483968 | bytes 8790528 | tf_op jit(solution)/shard_map/mcr,dmc->rd/dot_general | solution.py:260
  50.9 1.5 %collective-permute-start.16 = (bf16[1,512,128]{1,2,0:T(8,128)(2,1)S(1)}, bf16[1,512,128]{1,2,0:T(8,128)(2,1)S(1)}, u32[]{:S(2)}, u32[]{:S(2)}) collective-permute-start(bf16[1,512,128]{1,2,0:T(8,128)(2,1)S(1)} %get-tuple-element.58), channel_id=1, source_target_pairs={{0,2},{2,0},{1,3},{3,1},{4,6},{6,4},{5,7},{7,5},{8,10},{10,8},{9,1... | collective-permute-start | bytes 393224 | tf_op jit(solution)/shard_map/ppermute | solution.py:47
  52.5 0.8 %convolution_multiply_fusion.1 = f32[20,2048]{1,0:T(8,128)S(1)} fusion(f32[128,2048,1]{1,0,2:T(8,128)S(1)} %get-tuple-element.103, f32[2048]{0:T(1024)S(1)} %copy-done.6, f32[128]{0:T(128)S(1)} %add_rsqrt_fusion, pred[128,5]{0,1:T(8,128)(4,1)S(1)} %get-tuple-element.104, pred[128,5]{0,1:T(8,128)(4,1)S(1)} %get-tuple-element.105, ...), kind=kOutput, calls=%fused_computation.2 | convolution fusion | flops 62970880 | bytes 1223680 | tf_op jit(solution)/shard_map/rk,rd->kd/dot_general | solution.py:264
  53.3 0.7 %fusion = f32[20,2048]{1,0:T(8,128)S(1)} fusion(f32[20,2048]{1,0:T(8,128)S(1)} %convolution_multiply_fusion.1, f32[128,2048]{1,0:T(8,128)S(1)} %get-tuple-element.101, f32[128]{0:T(128)S(1)} %add_rsqrt_fusion, f32[128]{0:T(128)S(1)} %multiply_reduce_fusion.1, pred[128,5]{0,1:T(8,128)(4,1)S(1)} %get-tuple-element.104, ...), kind=kOutput, calls=%fused_computation.1 | convolution fusion | flops 63276544 | bytes 1379840 | tf_op jit(solution)/shard_map/rk,dr->kd/dot_general | solution.py:265
  54.2 0.6 collective-permute-start.11
  54.8 1.2 %collective-permute-start.12 = (f32[21,512]{1,0:T(8,128)S(1)}, f32[21,512]{1,0:T(8,128)S(1)}, u32[]{:S(2)}, u32[]{:S(2)}) collective-permute-start(f32[21,512]{1,0:T(8,128)S(1)} %get-tuple-element.90), channel_id=1, source_target_pairs={{0,3},{1,2},{2,1},{3,0},{4,7},{5,6},{6,5},{7,4},{8,11},{9,10},{10,... | collective-permute-start | bytes 129032 | tf_op jit(solution)/shard_map/ppermute | solution.py:64
  56.1 0.4 collective-permute-start.17
  56.5 1.9 %fusion.23 = f32[128,512]{1,0:T(8,128)} fusion(f32[512,1024]{1,0:T(8,128)S(1)} %bitcast.162, f32[128,512]{1,0:T(8,128)S(1)} %get-tuple-element.69, f32[128,512]{1,0:T(8,128)S(1)} %get-tuple-element.68, f32[1024]{0:T(1024)S(1)} %copy-done.7), kind=kOutput, calls=%fused_computation.47 | convolution fusion | flops 402915328 | bytes 2887680 | tf_op jit(solution)/shard_map/dot_general | solution.py:139
  58.4 0.5 collective-permute-done.11
  59.0 1.7 %collective-permute-start.15 = (f32[21,512]{1,0:T(8,128)S(1)}, f32[21,512]{1,0:T(8,128)S(1)}, u32[]{:S(2)}, u32[]{:S(2)}) collective-permute-start(f32[21,512]{1,0:T(8,128)S(1)} %fusion.106), channel_id=1, source_target_pairs={{0,12},{4,8},{8,4},{12,0},{1,13},{5,9},{9,5},{13,1},{2,14},{6,10},... | collective-permute-start | bytes 129032 | tf_op jit(solution)/shard_map/ppermute | solution.py:64
  60.6 0.5 collective-permute-start.14
  61.1 2.3 %collective-permute-start.13 = (f32[21,512]{1,0:T(8,128)S(1)}, f32[21,512]{1,0:T(8,128)S(1)}, u32[]{:S(2)}, u32[]{:S(2)}) collective-permute-start(f32[21,512]{1,0:T(8,128)S(1)} %fusion.106), channel_id=1, source_target_pairs={{0,4},{4,0},{8,12},{12,8},{1,5},{5,1},{9,13},{13,9},{2,6},{6,2},{1... | collective-permute-start | bytes 129032 | tf_op jit(solution)/shard_map/ppermute | solution.py:64
  64.1 0.9 %fusion.5 = bf16[128,512]{1,0:T(8,128)(2,1)} fusion(f32[128,512]{1,0:T(8,128)S(1)} %fusion.26, f32[128,512]{1,0:T(8,128)S(1)} %fusion.28, f32[128,512]{1,0:T(8,128)S(1)} %fusion.30, bf16[2048,512]{1,0:T(8,128)(2,1)S(1)} %copy-done.2, f32[128,2048]{1,0:T(8,128)S(1)} %get-tuple-element.101, s32[]{:T(128)S(6)} %select_n.444, ...), kind=kOutput, calls=%fused_computation.14 | convolution fusion | flops 67633152 | bytes 2228231 | tf_op jit(solution)/shard_map/cr,cd->rd/dot_general | solution.py:245
  65.0 0.4 collective-permute-done.15
  65.4 1.5 %collective-permute-done.14 = f32[21,512]{1,0:T(8,128)S(1)} collective-permute-done((f32[21,512]{1,0:T(8,128)S(1)}, f32[21,512]{1,0:T(8,128)S(1)}, u32[]{:S(2)}, u32[]{:S(2)}) %collective-permute-start.14) | collective-permute-done | bytes 43040 | tf_op jit(solution)/shard_map/ppermute | solution.py:64
  67.0 0.6 slice.240
  67.5 0.6 copy.31
  (86 shorter events, 4.0 us)
Async XLA Ops:
  0.6 12.2 %copy-start = (f32[1,1,128,512]{3,2,1,0:T(8,128)S(1)}, f32[1,1,128,512]{3,2,1,0:T(8,128)}, u32[]{:S(2)}) copy-start(f32[1,1,128,512]{3,2,1,0:T(8,128)} %param.21) | copy-start | bytes 786436
  1.9 14.7 %collective-permute-start = (s32[3]{0:T(128)}, s32[3]{0:T(128)}, u32[]{:S(2)}, u32[]{:S(2)}) collective-permute-start(s32[3]{0:T(128)} %slice.153), channel_id=1, source_target_pairs={{0,4},{4,8},{8,12},{12,0},{1,5},{5,9},{9,13},{13,1},{2,6},{6,10},{... | collective-permute-start | bytes 44 | tf_op jit(solution)/shard_map/ppermute | solution.py:189
  5.0 6.5 %copy-start.10 = (s32[128]{0:T(128)S(1)}, s32[128]{0:T(128)}, u32[]{:S(2)}) copy-start(s32[128]{0:T(128)} %param.17) | copy-start | bytes 1540
  7.5 1.0 %copy-start.1 = (f32[128,2048]{1,0:T(8,128)}, f32[128,2048]{1,0:T(8,128)S(1)}, u32[]{:S(2)}) copy-start(f32[128,2048]{1,0:T(8,128)S(1)} %fusion.136) | copy-start | bytes 3145732
  9.4 12.0 %collective-permute-start.1 = (f32[128,512]{1,0:T(8,128)}, f32[128,512]{1,0:T(8,128)}, u32[]{:S(2)}, u32[]{:S(2)}) collective-permute-start(f32[128,512]{1,0:T(8,128)} %get-tuple-element.63), channel_id=1, source_target_pairs={{0,1},{1,0},{2,3},{3,2},{4,5},{5,4},{6,7},{7,6},{8,9},{9,8},{10,11... | collective-permute-start | bytes 786440 | tf_op jit(solution)/shard_map/ppermute | solution.py:64
  9.4 12.0 %collective-permute-start.3 = (f32[128,512]{1,0:T(8,128)}, f32[128,512]{1,0:T(8,128)}, u32[]{:S(2)}, u32[]{:S(2)}) collective-permute-start(f32[128,512]{1,0:T(8,128)} %get-tuple-element.64), channel_id=1, source_target_pairs={{0,3},{1,2},{2,1},{3,0},{4,7},{5,6},{6,5},{7,4},{8,11},{9,10},{10,... | collective-permute-start | bytes 786440 | tf_op jit(solution)/shard_map/ppermute | solution.py:64
  11.0 12.9 %collective-permute-start.2 = (f32[128,512]{1,0:T(8,128)}, f32[128,512]{1,0:T(8,128)}, u32[]{:S(2)}, u32[]{:S(2)}) collective-permute-start(f32[128,512]{1,0:T(8,128)} %get-tuple-element.65), channel_id=1, source_target_pairs={{0,2},{1,3},{2,0},{3,1},{4,6},{5,7},{6,4},{7,5},{8,10},{9,11},{10,... | collective-permute-start | bytes 786440 | tf_op jit(solution)/shard_map/ppermute | solution.py:64
  12.8 1.7 %copy-start.5 = (bf16[4,5,2048]{2,0,1:T(4,128)(2,1)S(1)}, bf16[4,5,2048]{2,0,1:T(4,128)(2,1)}, u32[]{:S(2)}) copy-start(bf16[4,5,2048]{2,0,1:T(4,128)(2,1)} %param.18) | copy-start | bytes 245764
  13.6 2.9 %copy-start.8 = (pred[512]{0:T(512)(128)(4,1)S(1)}, pred[512]{0:T(512)(128)(4,1)}, u32[]{:S(2)}) copy-start(pred[512]{0:T(512)(128)(4,1)} %constant.102) | copy-start | bytes 1540
  15.3 1.4 %copy-start.11 = (s32[128]{0:T(128)S(1)}, s32[128]{0:T(128)}, u32[]{:S(2)}) copy-start(s32[128]{0:T(128)} %param.17) | copy-start | bytes 1540
  15.3 1.6 %copy-start.4 = (bf16[20,2048]{1,0:T(8,128)(2,1)S(1)}, bf16[20,2048]{1,0:T(8,128)(2,1)}, u32[]{:S(2)}) copy-start(bf16[20,2048]{1,0:T(8,128)(2,1)} %reshape.250) | copy-start | bytes 245764
  16.5 0.8 %copy-start.6 = (f32[2048]{0:T(1024)S(1)}, f32[2048]{0:T(1024)}, u32[]{:S(2)}) copy-start(f32[2048]{0:T(1024)} %param.19) | copy-start | bytes 24580
  17.3 12.5 %slice-start = ((s8[6291456]{0:T(1024)(128)(4,1)}), s8[4194304]{0:T(1024)(128)(4,1)S(1)}, s32[]{:S(2)}) async-start(s8[6291456]{0:T(1024)(128)(4,1)} %bitcast.163), calls=%async_computation | async-start | bytes 8388608
  17.3 12.5 %slice-start.1 = ((s8[6291456]{0:T(1024)(128)(4,1)}), s8[2097152]{0:T(1024)(128)(4,1)S(1)}, s32[]{:S(2)}) async-start(s8[6291456]{0:T(1024)(128)(4,1)} %bitcast.163), calls=%async_computation.1 | async-start | bytes 4194304
  25.3 5.7 %collective-permute-start.6 = (bf16[2,128,128]{1,2,0:T(8,128)(2,1)S(1)}, bf16[2,128,128]{1,2,0:T(8,128)(2,1)S(1)}, u32[]{:S(2)}, u32[]{:S(2)}) collective-permute-start(bf16[2,128,128]{1,2,0:T(8,128)(2,1)S(1)} %get-tuple-element.45), channel_id=1, source_target_pairs={{0,4},{4,0},{8,12},{12,8},{1,5},{5,1},{9,13},{13,9},{2,6},{6,2},{1... | collective-permute-start | bytes 196616 | tf_op jit(solution)/shard_map/ppermute | solution.py:64
  26.9 7.6 %collective-permute-start.5 = (bf16[2,128,128]{1,2,0:T(8,128)(2,1)S(1)}, bf16[2,128,128]{1,2,0:T(8,128)(2,1)S(1)}, u32[]{:S(2)}, u32[]{:S(2)}) collective-permute-start(bf16[2,128,128]{1,2,0:T(8,128)(2,1)S(1)} %get-tuple-element.86), channel_id=1, source_target_pairs={{0,8},{4,12},{8,0},{12,4},{1,9},{5,13},{9,1},{13,5},{2,10},{6,14},... | collective-permute-start | bytes 196616 | tf_op jit(solution)/shard_map/ppermute | solution.py:64
  28.1 6.5 %collective-permute-start.4 = (bf16[2,128,128]{1,2,0:T(8,128)(2,1)S(1)}, bf16[2,128,128]{1,2,0:T(8,128)(2,1)S(1)}, u32[]{:S(2)}, u32[]{:S(2)}) collective-permute-start(bf16[2,128,128]{1,2,0:T(8,128)(2,1)S(1)} %get-tuple-element.87), channel_id=1, source_target_pairs={{0,12},{4,8},{8,4},{12,0},{1,13},{5,9},{9,5},{13,1},{2,14},{6,10},... | collective-permute-start | bytes 196616 | tf_op jit(solution)/shard_map/ppermute | solution.py:64
  35.8 0.7 copy-start.9
  36.4 0.7 %copy-start.7 = (f32[1024]{0:T(1024)S(1)}, f32[1024]{0:T(1024)}, u32[]{:S(2)}) copy-start(f32[1024]{0:T(1024)} %constant.104) | copy-start | bytes 12292
  38.1 5.6 %copy-start.3 = (bf16[128,512]{1,0:T(8,128)(2,1)S(1)}, bf16[128,512]{1,0:T(8,128)(2,1)}, u32[]{:S(2)}) copy-start(bf16[128,512]{1,0:T(8,128)(2,1)} %param.23) | copy-start | bytes 393220
  39.2 4.8 %collective-permute-start.9 = (bf16[2,128,128]{1,2,0:T(8,128)(2,1)S(1)}, bf16[2,128,128]{1,2,0:T(8,128)(2,1)S(1)}, u32[]{:S(2)}, u32[]{:S(2)}) collective-permute-start(bf16[2,128,128]{1,2,0:T(8,128)(2,1)S(1)} %get-tuple-element.38), channel_id=1, source_target_pairs={{0,4},{4,0},{8,12},{12,8},{1,5},{5,1},{9,13},{13,9},{2,6},{6,2},{1... | collective-permute-start | bytes 196616 | tf_op jit(solution)/shard_map/ppermute | solution.py:64
  40.5 6.4 %collective-permute-start.8 = (bf16[2,128,128]{1,2,0:T(8,128)(2,1)S(1)}, bf16[2,128,128]{1,2,0:T(8,128)(2,1)S(1)}, u32[]{:S(2)}, u32[]{:S(2)}) collective-permute-start(bf16[2,128,128]{1,2,0:T(8,128)(2,1)S(1)} %get-tuple-element.81), channel_id=1, source_target_pairs={{0,8},{4,12},{8,0},{12,4},{1,9},{5,13},{9,1},{13,5},{2,10},{6,14},... | collective-permute-start | bytes 196616 | tf_op jit(solution)/shard_map/ppermute | solution.py:64
  42.1 6.2 %collective-permute-start.7 = (bf16[2,128,128]{1,2,0:T(8,128)(2,1)S(1)}, bf16[2,128,128]{1,2,0:T(8,128)(2,1)S(1)}, u32[]{:S(2)}, u32[]{:S(2)}) collective-permute-start(bf16[2,128,128]{1,2,0:T(8,128)(2,1)S(1)} %get-tuple-element.82), channel_id=1, source_target_pairs={{0,12},{4,8},{8,4},{12,0},{1,13},{5,9},{9,5},{13,1},{2,14},{6,10},... | collective-permute-start | bytes 196616 | tf_op jit(solution)/shard_map/ppermute | solution.py:64
  50.9 5.1 %collective-permute-start.16 = (bf16[1,512,128]{1,2,0:T(8,128)(2,1)S(1)}, bf16[1,512,128]{1,2,0:T(8,128)(2,1)S(1)}, u32[]{:S(2)}, u32[]{:S(2)}) collective-permute-start(bf16[1,512,128]{1,2,0:T(8,128)(2,1)S(1)} %get-tuple-element.58), channel_id=1, source_target_pairs={{0,2},{2,0},{1,3},{3,1},{4,6},{6,4},{5,7},{7,5},{8,10},{10,8},{9,1... | collective-permute-start | bytes 393224 | tf_op jit(solution)/shard_map/ppermute | solution.py:47
  54.0 9.4 %copy-start.2 = (bf16[2048,512]{1,0:T(8,128)(2,1)S(1)}, bf16[2048,512]{1,0:T(8,128)(2,1)}, u32[]{:S(2)}) copy-start(bf16[2048,512]{1,0:T(8,128)(2,1)} %param.22) | copy-start | bytes 6291460
  54.1 4.3 %collective-permute-start.10 = (f32[21,512]{1,0:T(8,128)S(1)}, f32[21,512]{1,0:T(8,128)S(1)}, u32[]{:S(2)}, u32[]{:S(2)}) collective-permute-start(f32[21,512]{1,0:T(8,128)S(1)} %get-tuple-element.88), channel_id=1, source_target_pairs={{0,1},{1,0},{2,3},{3,2},{4,5},{5,4},{6,7},{7,6},{8,9},{9,8},{10,11... | collective-permute-start | bytes 129032 | tf_op jit(solution)/shard_map/ppermute | solution.py:64
  54.2 4.7 %collective-permute-start.11 = (f32[21,512]{1,0:T(8,128)S(1)}, f32[21,512]{1,0:T(8,128)S(1)}, u32[]{:S(2)}, u32[]{:S(2)}) collective-permute-start(f32[21,512]{1,0:T(8,128)S(1)} %get-tuple-element.89), channel_id=1, source_target_pairs={{0,2},{1,3},{2,0},{3,1},{4,6},{5,7},{6,4},{7,5},{8,10},{9,11},{10,... | collective-permute-start | bytes 129032 | tf_op jit(solution)/shard_map/ppermute | solution.py:64
  54.8 4.1 %collective-permute-start.12 = (f32[21,512]{1,0:T(8,128)S(1)}, f32[21,512]{1,0:T(8,128)S(1)}, u32[]{:S(2)}, u32[]{:S(2)}) collective-permute-start(f32[21,512]{1,0:T(8,128)S(1)} %get-tuple-element.90), channel_id=1, source_target_pairs={{0,3},{1,2},{2,1},{3,0},{4,7},{5,6},{6,5},{7,4},{8,11},{9,10},{10,... | collective-permute-start | bytes 129032 | tf_op jit(solution)/shard_map/ppermute | solution.py:64
  56.1 7.3 %collective-permute-start.17 = (bf16[2,512,128]{1,2,0:T(8,128)(2,1)S(1)}, bf16[2,512,128]{1,2,0:T(8,128)(2,1)S(1)}, u32[]{:S(2)}, u32[]{:S(2)}) collective-permute-start(bf16[2,512,128]{1,2,0:T(8,128)(2,1)S(1)} %pad_maximum_fusion.5), channel_id=1, source_target_pairs={{0,1},{1,0},{2,3},{3,2},{4,5},{5,4},{6,7},{7,6},{8,9},{9,8},{10,11... | collective-permute-start | bytes 786440 | tf_op jit(solution)/shard_map/ppermute | solution.py:47
  59.0 6.5 %collective-permute-start.15 = (f32[21,512]{1,0:T(8,128)S(1)}, f32[21,512]{1,0:T(8,128)S(1)}, u32[]{:S(2)}, u32[]{:S(2)}) collective-permute-start(f32[21,512]{1,0:T(8,128)S(1)} %fusion.106), channel_id=1, source_target_pairs={{0,12},{4,8},{8,4},{12,0},{1,13},{5,9},{9,5},{13,1},{2,14},{6,10},... | collective-permute-start | bytes 129032 | tf_op jit(solution)/shard_map/ppermute | solution.py:64
  60.6 6.3 %collective-permute-start.14 = (f32[21,512]{1,0:T(8,128)S(1)}, f32[21,512]{1,0:T(8,128)S(1)}, u32[]{:S(2)}, u32[]{:S(2)}) collective-permute-start(f32[21,512]{1,0:T(8,128)S(1)} %fusion.106), channel_id=1, source_target_pairs={{0,8},{4,12},{8,0},{12,4},{1,9},{5,13},{9,1},{13,5},{2,10},{6,14},... | collective-permute-start | bytes 129032 | tf_op jit(solution)/shard_map/ppermute | solution.py:64
  61.1 5.8 %collective-permute-start.13 = (f32[21,512]{1,0:T(8,128)S(1)}, f32[21,512]{1,0:T(8,128)S(1)}, u32[]{:S(2)}, u32[]{:S(2)}) collective-permute-start(f32[21,512]{1,0:T(8,128)S(1)} %fusion.106), channel_id=1, source_target_pairs={{0,4},{4,0},{8,12},{12,8},{1,5},{5,1},{9,13},{13,9},{2,6},{6,2},{1... | collective-permute-start | bytes 129032 | tf_op jit(solution)/shard_map/ppermute | solution.py:64

commit v20 on v17

--- a/solution.py
+++ b/solution.py
@@ -239,10 +239,18 @@
     weight_rows = out_proj
     gathered, sources = all_gather_cp(gated_rows)
     mixed_out = None
+    offsets = [0]
+    for size, stride in ((lax.axis_size("chan"), lax.axis_size("pair")), (lax.axis_size("pair"), 1)):
+        step = 1
+        while step < size:
+            offsets = offsets + [o ^ (step * stride) for o in offsets]
+            step *= 2
+    position = np.zeros(len(offsets), np.int32)
+    position[np.array(offsets)] = np.arange(len(offsets))
     for slot in range(len(sources)):
-        piece = gathered[0]
-        for index in range(1, len(sources)):
-            piece = jnp.where(sources[index] == slot, gathered[index], piece)
+        piece = lax.dynamic_index_in_dim(
+            gathered, jnp.asarray(position)[sources[0] ^ slot], 0, keepdims=False
+        )
         term = jnp.einsum(
             "cr,cd->rd",
             piece,

time: 68.4 us -> 74.9 us (1.095)
  between operations: 1.12 us -> 8.32 us
  waiting for transfers between devices: 12.8 us -> 10.9 us
    ppermute x15, waiting for transfers between devices: 12.8 us -> 10.9 us  [group_exchange(): return lax.ppermute(x, axes, [(i, i ^ offset) for i in range(count)])]
    unnamed x30 -> x32, local copies, waits for them, and re-layouts: 2.43 us -> 2.45 us
  transfers between devices with their start and end apart: 18 -> 18, of which waited for: 7 -> 6; matrix products, arithmetic and copies ran while one was open for 29% -> 27% of each run, Pallas kernels for 0% -> 0%
where the time goes in v20:
time: 74.9 us; the launch traced here: 74.6 us
  starting transfers between devices  23 us (31%)
  matrix products  19.2 us (26%)
  waiting for transfers between devices  10.9 us (15%)
  between operations  8.32 us (11%)
  local copies, waits for them, and re-layouts  7.55 us (10%)
  other arithmetic  5.65 us (8%)
    ppermute x15, starting transfers between devices, group_exchange(): return lax.ppermute(x, axes, [(i, i ^ offset) for i in range(count)])  17.9 us
    ppermute x15, waiting for transfers between devices, group_exchange(): return lax.ppermute(x, axes, [(i, i ^ offset) for i in range(count)])  10.9 us
    dot_general x1, matrix products, per_device(): jnp.einsum('dr,dmc->mcr', hidden, in_proj, preferred_element_type=jnp.flo...  4.01 us
    dot_general x3, matrix products, inverse_dft(): lax.dot_general(spec * weight, dft, (((1,), (1,)), ((), ())), precision=T...  3.86 us
    ppermute x1, starting transfers between devices, per_device(): lax.ppermute(tokens[row_count - rim_width:], 'seq', [(i, (i + 1) % seq_co...  3.05 us
    dot_general x1, matrix products, per_device(): jnp.einsum('rd,cd->rc', cotangent, out_proj, preferred_element_type=jnp.f...  2.5 us
    unnamed x32, local copies, waits for them, and re-layouts  2.45 us
    dot_general x1, matrix products, per_device(): jnp.einsum('mcr,dmc->rd', d_proj, in_proj, preferred_element_type=jnp.flo...  2.16 us
  transfers between devices with their start and end apart: 18, of which 6 were waited for; matrix products, arithmetic and copies ran while one was open for 27% of the time, Pallas kernels for 0%

profile of v20, /device:TPU:0, one launch (start us, length us, event | category | flops | bytes accessed | tf_op | source)
XLA Modules:
  0.0 74.6 jit_solution(9255222638270357207)
XLA Ops:
  0.6 1.3 %slice.139 = s32[3]{0:T(128)} slice(s32[128]{0:T(128)} %param.18), slice={[125:128]} | slice | bytes 24 | tf_op jit(solution)/shard_map/slice | solution.py:191
  1.9 3.1 %collective-permute-start = (s32[3]{0:T(128)}, s32[3]{0:T(128)}, u32[]{:S(2)}, u32[]{:S(2)}) collective-permute-start(s32[3]{0:T(128)} %slice.139), channel_id=1, source_target_pairs={{0,4},{4,8},{8,12},{12,0},{1,5},{5,9},{9,13},{13,1},{2,6},{6,10},{... | collective-permute-start | bytes 44 | tf_op jit(solution)/shard_map/ppermute | solution.py:190
  5.0 2.5 %fusion.119 = f32[128,2048]{1,0:T(8,128)S(1)} fusion(bf16[128,512]{1,0:T(8,128)(2,1)} %param.24, bf16[2048,512]{1,0:T(8,128)(2,1)} %param.23), kind=kOutput, calls=%fused_computation.230 | convolution fusion | flops 268435456 | bytes 3276800 | tf_op jit(solution)/shard_map/rd,cd->rc/dot_general | solution.py:218
  7.5 1.0 %copy-done.2 = f32[128,2048]{1,0:T(8,128)} copy-done((f32[128,2048]{1,0:T(8,128)}, f32[128,2048]{1,0:T(8,128)S(1)}, u32[]{:S(2)}) %copy-start.2) | copy-done | bytes 1048600
  8.5 0.9 %constant_dynamic-slice_fusion.2 = (f32[128,512]{1,0:T(8,128)}, f32[128,512]{1,0:T(8,128)}, f32[128,512]{1,0:T(8,128)}) fusion(f32[128,2048]{1,0:T(8,128)S(1)} %fusion.119, s32[]{:T(128)S(6)} %select_n.457, s32[]{:T(128)S(6)} %select_n.459, s32[]{:T(128)S(6)} %select_n.458), kind=kLoop, calls=%fused_computation.206 | loop fusion | bytes 1572876 | tf_op jit(solution)/shard_map/dynamic_slice | solution.py:73
  9.4 1.6 %collective-permute-start.3 = (f32[128,512]{1,0:T(8,128)}, f32[128,512]{1,0:T(8,128)}, u32[]{:S(2)}, u32[]{:S(2)}) collective-permute-start(f32[128,512]{1,0:T(8,128)} %get-tuple-element.64), channel_id=1, source_target_pairs={{0,3},{1,2},{2,1},{3,0},{4,7},{5,6},{6,5},{7,4},{8,11},{9,10},{10,... | collective-permute-start | bytes 786440 | tf_op jit(solution)/shard_map/ppermute | solution.py:64
  11.0 0.5 collective-permute-start.2
  11.5 0.6 fusion.118
  17.0 0.3 fusion.88
  17.4 0.6 fusion.78
  18.3 0.7 convolution_bitcast_fusion.2
  19.1 0.9 %fusion.116 = (f32[127,1024]{1,0:T(8,128)S(1)}, f32[127,1024]{1,0:T(8,128)}) fusion(f32[128,1024]{1,0:T(8,128)S(1)} %convolution_bitcast_fusion.2), kind=kLoop, calls=%fused_computation.227 | loop fusion | bytes 2080768 | tf_op jit(solution)/shard_map/jit(_roll_static)/slice | solution.py:167
  20.0 0.7 reshape.243
  23.1 1.2 %maximum_select_fusion = f32[128,1024]{1,0:T(8,128)S(1)} fusion(f32[1,1024]{1,0:T(1,128)S(1)} %get-tuple-element.73, f32[127,1024]{1,0:T(8,128)} %get-tuple-element.75, f32[127,1024]{1,0:T(8,128)S(1)} %get-tuple-element.74, f32[1,1024]{1,0:T(1,128)S(1)} %get-tuple-element.72, pred[128]{0:T(512)(128)(4,1)} %constant.107), kind=kLoop, calls=%fused_computation.38 | loop fusion | flops 393216 | bytes 1572992 | tf_op jit(solution)/shard_map/jit(_where)/select_n | solution.py:168
  24.7 0.4 multiply_reduce_fusion
  25.2 4.0 %convolution_bitcast_fusion.1 = f32[3,512,128]{1,2,0:T(8,128)S(1)} fusion(bf16[2048,3,512]{2,0,1:T(8,128)(2,1)} %param.21, f32[128,2048]{1,0:T(8,128)S(1)} %get-tuple-element.103, f32[2048]{0:T(1024)S(1)} %copy-done.6, f32[128]{0:T(128)S(1)} %add_rsqrt_fusion), kind=kOutput, calls=%fused_computation.5 | convolution fusion | flops 806092800 | bytes 8135168 | tf_op jit(solution)/shard_map/dr,dmc->mcr/dot_general | solution.py:207
  29.3 1.3 %fusion.49 = (bf16[1,512,128]{1,2,0:T(8,128)(2,1)S(1)}, f32[128,512]{1,0:T(8,128)S(1)}) fusion(f32[3,512,128]{1,2,0:T(8,128)S(1)} %convolution_bitcast_fusion.1, f32[128,512]{1,0:T(8,128)} %collective-permute-done.3, f32[128,512]{1,0:T(8,128)} %collective-permute-done.2, f32[128,512]{1,0:T(8,128)} %collective-permute-done.1, f32[128,2048]{1,0:T(8,128)} %copy-done.2, ...), kind=kLoop, calls=%fused_computation.125 | loop fusion | flops 393216 | bytes 1703940 | tf_op jit(solution)/shard_map/stack | solution.py:224
  30.7 2.3 %collective-permute-start.6 = (bf16[2,128,128]{1,2,0:T(8,128)(2,1)S(1)}, bf16[2,128,128]{1,2,0:T(8,128)(2,1)S(1)}, u32[]{:S(2)}, u32[]{:S(2)}) collective-permute-start(bf16[2,128,128]{1,2,0:T(8,128)(2,1)S(1)} %get-tuple-element.45), channel_id=1, source_target_pairs={{0,4},{4,0},{8,12},{12,8},{1,5},{5,1},{9,13},{13,9},{2,6},{6,2},{1... | collective-permute-start | bytes 196616 | tf_op jit(solution)/shard_map/ppermute | solution.py:64
  33.0 1.1 %collective-permute-start.5 = (bf16[2,128,128]{1,2,0:T(8,128)(2,1)S(1)}, bf16[2,128,128]{1,2,0:T(8,128)(2,1)S(1)}, u32[]{:S(2)}, u32[]{:S(2)}) collective-permute-start(bf16[2,128,128]{1,2,0:T(8,128)(2,1)S(1)} %get-tuple-element.84), channel_id=1, source_target_pairs={{0,8},{4,12},{8,0},{12,4},{1,9},{5,13},{9,1},{13,5},{2,10},{6,14},... | collective-permute-start | bytes 196616 | tf_op jit(solution)/shard_map/ppermute | solution.py:64
  34.1 1.5 %collective-permute-start.4 = (bf16[2,128,128]{1,2,0:T(8,128)(2,1)S(1)}, bf16[2,128,128]{1,2,0:T(8,128)(2,1)S(1)}, u32[]{:S(2)}, u32[]{:S(2)}) collective-permute-start(bf16[2,128,128]{1,2,0:T(8,128)(2,1)S(1)} %get-tuple-element.85), channel_id=1, source_target_pairs={{0,12},{4,8},{8,4},{12,0},{1,13},{5,9},{9,5},{13,1},{2,14},{6,10},... | collective-permute-start | bytes 196616 | tf_op jit(solution)/shard_map/ppermute | solution.py:64
  35.6 1.1 %fusion.1 = f32[3,512,128]{1,2,0:T(8,128)S(1)} fusion(f32[3,512,128]{1,2,0:T(8,128)S(1)} %convolution_bitcast_fusion.1, bf16[2048,3,512]{2,0,1:T(8,128)(2,1)S(1)} %bitcast.118, f32[128,2048]{1,0:T(8,128)S(1)} %get-tuple-element.103, f32[2048]{0:T(1024)S(1)} %copy-done.6, f32[128]{0:T(128)S(1)} %add_rsqrt_fusion), kind=kOutput, calls=%fused_computation.6 | convolution fusion | flops 807075840 | bytes 8921600 | tf_op jit(solution)/shard_map/dr,dmc->mcr/dot_general | solution.py:209
  36.7 4.2 %collective-permute-done.5 = bf16[2,128,128]{1,2,0:T(8,128)(2,1)S(1)} collective-permute-done((bf16[2,128,128]{1,2,0:T(8,128)(2,1)S(1)}, bf16[2,128,128]{1,2,0:T(8,128)(2,1)S(1)}, u32[]{:S(2)}, u32[]{:S(2)}) %collective-permute-start.5) | collective-permute-done | bytes 65568 | tf_op jit(solution)/shard_map/ppermute | solution.py:64
  41.0 0.6 fusion.57
  41.6 0.6 fusion.59
  42.4 0.4 copy-done.10
  43.5 1.0 %fusion.4 = bf16[1,128,512]{1,2,0:T(8,128)(2,1)S(1)} fusion(f32[512,1024]{1,0:T(8,128)S(1)} %bitcast.114, f32[128,512]{1,0:T(8,128)S(1)} %get-tuple-element.66, f32[128,512]{1,0:T(8,128)S(1)} %get-tuple-element.67, f32[1024]{0:T(1024)S(1)} %copy-done.7), kind=kOutput, calls=%fused_computation.15 | convolution fusion | flops 402980864 | bytes 2756608 | tf_op jit(solution)/shard_map/dot_general | solution.py:140
  44.5 1.0 %fusion.5 = bf16[1,128,512]{1,2,0:T(8,128)(2,1)S(1)} fusion(f32[512,1024]{1,0:T(8,128)S(1)} %bitcast.115, f32[128,512]{1,0:T(8,128)S(1)} %get-tuple-element.96, f32[128,512]{1,0:T(8,128)S(1)} %get-tuple-element.97, f32[1024]{0:T(1024)S(1)} %copy-done.7), kind=kOutput, calls=%fused_computation.16 | convolution fusion | flops 402980864 | bytes 2756608 | tf_op jit(solution)/shard_map/dot_general | solution.py:140
  45.6 1.3 %collective-permute-start.9 = (bf16[2,128,128]{1,2,0:T(8,128)(2,1)S(1)}, bf16[2,128,128]{1,2,0:T(8,128)(2,1)S(1)}, u32[]{:S(2)}, u32[]{:S(2)}) collective-permute-start(bf16[2,128,128]{1,2,0:T(8,128)(2,1)S(1)} %get-tuple-element.38), channel_id=1, source_target_pairs={{0,4},{4,0},{8,12},{12,8},{1,5},{5,1},{9,13},{13,9},{2,6},{6,2},{1... | collective-permute-start | bytes 196616 | tf_op jit(solution)/shard_map/ppermute | solution.py:64
  46.9 1.6 %collective-permute-start.8 = (bf16[2,128,128]{1,2,0:T(8,128)(2,1)S(1)}, bf16[2,128,128]{1,2,0:T(8,128)(2,1)S(1)}, u32[]{:S(2)}, u32[]{:S(2)}) collective-permute-start(bf16[2,128,128]{1,2,0:T(8,128)(2,1)S(1)} %get-tuple-element.79), channel_id=1, source_target_pairs={{0,8},{4,12},{8,0},{12,4},{1,9},{5,13},{9,1},{13,5},{2,10},{6,14},... | collective-permute-start | bytes 196616 | tf_op jit(solution)/shard_map/ppermute | solution.py:64
  48.5 1.6 %collective-permute-start.7 = (bf16[2,128,128]{1,2,0:T(8,128)(2,1)S(1)}, bf16[2,128,128]{1,2,0:T(8,128)(2,1)S(1)}, u32[]{:S(2)}, u32[]{:S(2)}) collective-permute-start(bf16[2,128,128]{1,2,0:T(8,128)(2,1)S(1)} %get-tuple-element.80), channel_id=1, source_target_pairs={{0,12},{4,8},{8,4},{12,0},{1,13},{5,9},{9,5},{13,1},{2,14},{6,10},... | collective-permute-start | bytes 196616 | tf_op jit(solution)/shard_map/ppermute | solution.py:64
  50.3 3.1 %collective-permute-done.8 = bf16[2,128,128]{1,2,0:T(8,128)(2,1)S(1)} collective-permute-done((bf16[2,128,128]{1,2,0:T(8,128)(2,1)S(1)}, bf16[2,128,128]{1,2,0:T(8,128)(2,1)S(1)}, u32[]{:S(2)}, u32[]{:S(2)}) %collective-permute-start.8) | collective-permute-done | bytes 65568 | tf_op jit(solution)/shard_map/ppermute | solution.py:64
  53.4 1.3 %collective-permute-done.7 = bf16[2,128,128]{1,2,0:T(8,128)(2,1)S(1)} collective-permute-done((bf16[2,128,128]{1,2,0:T(8,128)(2,1)S(1)}, bf16[2,128,128]{1,2,0:T(8,128)(2,1)S(1)}, u32[]{:S(2)}, u32[]{:S(2)}) %collective-permute-start.7) | collective-permute-done | bytes 65568 | tf_op jit(solution)/shard_map/ppermute | solution.py:64
  55.0 2.2 %fusion.6 = (f32[2048]{0:T(1024)S(1)}, f32[128,2048,1]{1,0,2:T(8,128)S(1)}) fusion(f32[128,2048]{1,0:T(8,128)S(1)} %get-tuple-element.103, f32[128]{0:T(128)S(1)} %add_rsqrt_fusion, bf16[2048,3,512]{2,0,1:T(8,128)(2,1)S(1)} %bitcast.118, bf16[1,512,128]{1,2,0:T(8,128)(2,1)S(1)} %get-tuple-element.60, bf16[1,512,128]{1,2,0:T(8,128)(2,1)S(1)} %get-tuple-element.59, ...), kind=kOutput, calls=%fused_computation.18 | convolution fusion | flops 806483968 | bytes 8790528 | tf_op jit(solution)/shard_map/mcr,dmc->rd/dot_general | solution.py:269
  57.3 1.6 %collective-permute-start.16 = (bf16[1,512,128]{1,2,0:T(8,128)(2,1)S(1)}, bf16[1,512,128]{1,2,0:T(8,128)(2,1)S(1)}, u32[]{:S(2)}, u32[]{:S(2)}) collective-permute-start(bf16[1,512,128]{1,2,0:T(8,128)(2,1)S(1)} %get-tuple-element.58), channel_id=1, source_target_pairs={{0,2},{2,0},{1,3},{3,1},{4,6},{6,4},{5,7},{7,5},{8,10},{10,8},{9,1... | collective-permute-start | bytes 393224 | tf_op jit(solution)/shard_map/ppermute | solution.py:47
  58.9 0.8 %convolution_multiply_fusion.1 = f32[20,2048]{1,0:T(8,128)S(1)} fusion(f32[128,2048,1]{1,0,2:T(8,128)S(1)} %get-tuple-element.105, f32[2048]{0:T(1024)S(1)} %copy-done.6, f32[128]{0:T(128)S(1)} %add_rsqrt_fusion, pred[128,5]{0,1:T(8,128)(4,1)S(1)} %get-tuple-element.106, pred[128,5]{0,1:T(8,128)(4,1)S(1)} %get-tuple-element.107, ...), kind=kOutput, calls=%fused_computation.2 | convolution fusion | flops 62970880 | bytes 1223680 | tf_op jit(solution)/shard_map/rk,rd->kd/dot_general | solution.py:273
  59.7 0.7 fusion
  60.6 0.6 collective-permute-start.11
  61.2 1.3 %collective-permute-start.12 = (f32[21,512]{1,0:T(8,128)S(1)}, f32[21,512]{1,0:T(8,128)S(1)}, u32[]{:S(2)}, u32[]{:S(2)}) collective-permute-start(f32[21,512]{1,0:T(8,128)S(1)} %get-tuple-element.88), channel_id=1, source_target_pairs={{0,3},{1,2},{2,1},{3,0},{4,7},{5,6},{6,5},{7,4},{8,11},{9,10},{10,... | collective-permute-start | bytes 129032 | tf_op jit(solution)/shard_map/ppermute | solution.py:64
  62.5 0.4 collective-permute-start.17
  62.9 1.9 %fusion.21 = f32[128,512]{1,0:T(8,128)} fusion(f32[512,1024]{1,0:T(8,128)S(1)} %bitcast.116, f32[128,512]{1,0:T(8,128)S(1)} %get-tuple-element.69, f32[128,512]{1,0:T(8,128)S(1)} %get-tuple-element.68, f32[1024]{0:T(1024)S(1)} %copy-done.7), kind=kOutput, calls=%fused_computation.48 | convolution fusion | flops 402915328 | bytes 2887680 | tf_op jit(solution)/shard_map/dot_general | solution.py:140
  64.8 0.5 collective-permute-done.11
  65.4 1.6 %collective-permute-start.15 = (f32[21,512]{1,0:T(8,128)S(1)}, f32[21,512]{1,0:T(8,128)S(1)}, u32[]{:S(2)}, u32[]{:S(2)}) collective-permute-start(f32[21,512]{1,0:T(8,128)S(1)} %fusion.84), channel_id=1, source_target_pairs={{0,12},{4,8},{8,4},{12,0},{1,13},{5,9},{9,5},{13,1},{2,14},{6,10},... | collective-permute-start | bytes 129032 | tf_op jit(solution)/shard_map/ppermute | solution.py:64
  66.9 0.6 collective-permute-start.14
  67.5 2.3 %collective-permute-start.13 = (f32[21,512]{1,0:T(8,128)S(1)}, f32[21,512]{1,0:T(8,128)S(1)}, u32[]{:S(2)}, u32[]{:S(2)}) collective-permute-start(f32[21,512]{1,0:T(8,128)S(1)} %fusion.84), channel_id=1, source_target_pairs={{0,4},{4,0},{8,12},{12,8},{1,5},{5,1},{9,13},{13,9},{2,6},{6,2},{1... | collective-permute-start | bytes 129032 | tf_op jit(solution)/shard_map/ppermute | solution.py:64
  70.6 0.9 %fusion.3 = bf16[128,512]{1,0:T(8,128)(2,1)} fusion(f32[128,512]{1,0:T(8,128)S(1)} %convolution_add_fusion.1, bf16[2048,512]{1,0:T(8,128)(2,1)S(1)} %copy-done.1, f32[128,2048]{1,0:T(8,128)S(1)} %get-tuple-element.103, s32[]{:T(128)S(6)} %select_n.456, bf16[4,512,128]{1,2,0:T(8,128)(2,1)S(1)} %pad_maximum_fusion.2, s32[]{:T(128)S(6)} %select_n.540), kind=kOutput, calls=%fused_computation.14 | convolution fusion | flops 67305472 | bytes 1310728 | tf_op jit(solution)/shard_map/cr,cd->rd/dot_general | solution.py:254
  71.8 1.5 %collective-permute-done.14 = f32[21,512]{1,0:T(8,128)S(1)} collective-permute-done((f32[21,512]{1,0:T(8,128)S(1)}, f32[21,512]{1,0:T(8,128)S(1)}, u32[]{:S(2)}, u32[]{:S(2)}) %collective-permute-start.14) | collective-permute-done | bytes 43040 | tf_op jit(solution)/shard_map/ppermute | solution.py:64
  73.3 0.6 slice.222
  73.9 0.6 copy.32
  (89 shorter events, 4.1 us)
Async XLA Ops:
  0.6 17.7 %copy-start = (f32[1,1,128,512]{3,2,1,0:T(8,128)S(1)}, f32[1,1,128,512]{3,2,1,0:T(8,128)}, u32[]{:S(2)}) copy-start(f32[1,1,128,512]{3,2,1,0:T(8,128)} %param.22) | copy-start | bytes 786436
  1.9 22.6 %collective-permute-start = (s32[3]{0:T(128)}, s32[3]{0:T(128)}, u32[]{:S(2)}, u32[]{:S(2)}) collective-permute-start(s32[3]{0:T(128)} %slice.139), channel_id=1, source_target_pairs={{0,4},{4,8},{8,12},{12,0},{1,5},{5,9},{9,13},{13,1},{2,6},{6,10},{... | collective-permute-start | bytes 44 | tf_op jit(solution)/shard_map/ppermute | solution.py:190
  5.0 6.6 %copy-start.8 = (s32[4]{0:T(128)S(1)}, s32[4]{0:T(128)}, u32[]{:S(2)}) copy-start(s32[4]{0:T(128)} %constant.102.clone) | copy-start | bytes 52
  5.0 12.0 %copy-start.11 = (s32[128]{0:T(128)S(1)}, s32[128]{0:T(128)}, u32[]{:S(2)}) copy-start(s32[128]{0:T(128)} %param.18) | copy-start | bytes 1540
  7.5 1.0 %copy-start.2 = (f32[128,2048]{1,0:T(8,128)}, f32[128,2048]{1,0:T(8,128)S(1)}, u32[]{:S(2)}) copy-start(f32[128,2048]{1,0:T(8,128)S(1)} %fusion.119) | copy-start | bytes 3145732
  9.4 19.9 %collective-permute-start.1 = (f32[128,512]{1,0:T(8,128)}, f32[128,512]{1,0:T(8,128)}, u32[]{:S(2)}, u32[]{:S(2)}) collective-permute-start(f32[128,512]{1,0:T(8,128)} %get-tuple-element.63), channel_id=1, source_target_pairs={{0,1},{1,0},{2,3},{3,2},{4,5},{5,4},{6,7},{7,6},{8,9},{9,8},{10,11... | collective-permute-start | bytes 786440 | tf_op jit(solution)/shard_map/ppermute | solution.py:64
  9.4 19.9 %collective-permute-start.3 = (f32[128,512]{1,0:T(8,128)}, f32[128,512]{1,0:T(8,128)}, u32[]{:S(2)}, u32[]{:S(2)}) collective-permute-start(f32[128,512]{1,0:T(8,128)} %get-tuple-element.64), channel_id=1, source_target_pairs={{0,3},{1,2},{2,1},{3,0},{4,7},{5,6},{6,5},{7,4},{8,11},{9,10},{10,... | collective-permute-start | bytes 786440 | tf_op jit(solution)/shard_map/ppermute | solution.py:64
  11.0 18.3 %collective-permute-start.2 = (f32[128,512]{1,0:T(8,128)}, f32[128,512]{1,0:T(8,128)}, u32[]{:S(2)}, u32[]{:S(2)}) collective-permute-start(f32[128,512]{1,0:T(8,128)} %get-tuple-element.65), channel_id=1, source_target_pairs={{0,2},{1,3},{2,0},{3,1},{4,6},{5,7},{6,4},{7,5},{8,10},{9,11},{10,... | collective-permute-start | bytes 786440 | tf_op jit(solution)/shard_map/ppermute | solution.py:64
  18.3 1.7 %copy-start.5 = (bf16[4,5,2048]{2,0,1:T(4,128)(2,1)S(1)}, bf16[4,5,2048]{2,0,1:T(4,128)(2,1)}, u32[]{:S(2)}) copy-start(bf16[4,5,2048]{2,0,1:T(4,128)(2,1)} %param.19) | copy-start | bytes 245764
  19.0 5.3 %copy-start.9 = (pred[512]{0:T(512)(128)(4,1)S(1)}, pred[512]{0:T(512)(128)(4,1)}, u32[]{:S(2)}) copy-start(pred[512]{0:T(512)(128)(4,1)} %constant.106) | copy-start | bytes 1540
  23.1 1.4 %copy-start.12 = (s32[128]{0:T(128)S(1)}, s32[128]{0:T(128)}, u32[]{:S(2)}) copy-start(s32[128]{0:T(128)} %param.18) | copy-start | bytes 1540
  23.1 1.6 %copy-start.4 = (bf16[20,2048]{1,0:T(8,128)(2,1)S(1)}, bf16[20,2048]{1,0:T(8,128)(2,1)}, u32[]{:S(2)}) copy-start(bf16[20,2048]{1,0:T(8,128)(2,1)} %reshape.243) | copy-start | bytes 245764
  24.3 0.8 %copy-start.6 = (f32[2048]{0:T(1024)S(1)}, f32[2048]{0:T(1024)}, u32[]{:S(2)}) copy-start(f32[2048]{0:T(1024)} %param.20) | copy-start | bytes 24580
  25.2 10.5 %slice-start = ((s8[6291456]{0:T(1024)(128)(4,1)}), s8[4194304]{0:T(1024)(128)(4,1)S(1)}, s32[]{:S(2)}) async-start(s8[6291456]{0:T(1024)(128)(4,1)} %bitcast.117), calls=%async_computation | async-start | bytes 8388608
  25.2 10.4 %slice-start.1 = ((s8[6291456]{0:T(1024)(128)(4,1)}), s8[2097152]{0:T(1024)(128)(4,1)S(1)}, s32[]{:S(2)}) async-start(s8[6291456]{0:T(1024)(128)(4,1)} %bitcast.117), calls=%async_computation.1 | async-start | bytes 4194304
  30.7 6.1 %collective-permute-start.6 = (bf16[2,128,128]{1,2,0:T(8,128)(2,1)S(1)}, bf16[2,128,128]{1,2,0:T(8,128)(2,1)S(1)}, u32[]{:S(2)}, u32[]{:S(2)}) collective-permute-start(bf16[2,128,128]{1,2,0:T(8,128)(2,1)S(1)} %get-tuple-element.45), channel_id=1, source_target_pairs={{0,4},{4,0},{8,12},{12,8},{1,5},{5,1},{9,13},{13,9},{2,6},{6,2},{1... | collective-permute-start | bytes 196616 | tf_op jit(solution)/shard_map/ppermute | solution.py:64
  33.0 7.9 %collective-permute-start.5 = (bf16[2,128,128]{1,2,0:T(8,128)(2,1)S(1)}, bf16[2,128,128]{1,2,0:T(8,128)(2,1)S(1)}, u32[]{:S(2)}, u32[]{:S(2)}) collective-permute-start(bf16[2,128,128]{1,2,0:T(8,128)(2,1)S(1)} %get-tuple-element.84), channel_id=1, source_target_pairs={{0,8},{4,12},{8,0},{12,4},{1,9},{5,13},{9,1},{13,5},{2,10},{6,14},... | collective-permute-start | bytes 196616 | tf_op jit(solution)/shard_map/ppermute | solution.py:64
  34.1 6.8 %collective-permute-start.4 = (bf16[2,128,128]{1,2,0:T(8,128)(2,1)S(1)}, bf16[2,128,128]{1,2,0:T(8,128)(2,1)S(1)}, u32[]{:S(2)}, u32[]{:S(2)}) collective-permute-start(bf16[2,128,128]{1,2,0:T(8,128)(2,1)S(1)} %get-tuple-element.85), channel_id=1, source_target_pairs={{0,12},{4,8},{8,4},{12,0},{1,13},{5,9},{9,5},{13,1},{2,14},{6,10},... | collective-permute-start | bytes 196616 | tf_op jit(solution)/shard_map/ppermute | solution.py:64
  42.1 0.7 copy-start.10
  42.8 0.7 copy-start.7
  44.5 5.6 %copy-start.3 = (bf16[128,512]{1,0:T(8,128)(2,1)S(1)}, bf16[128,512]{1,0:T(8,128)(2,1)}, u32[]{:S(2)}) copy-start(bf16[128,512]{1,0:T(8,128)(2,1)} %param.24) | copy-start | bytes 393220
  45.6 4.8 %collective-permute-start.9 = (bf16[2,128,128]{1,2,0:T(8,128)(2,1)S(1)}, bf16[2,128,128]{1,2,0:T(8,128)(2,1)S(1)}, u32[]{:S(2)}, u32[]{:S(2)}) collective-permute-start(bf16[2,128,128]{1,2,0:T(8,128)(2,1)S(1)} %get-tuple-element.38), channel_id=1, source_target_pairs={{0,4},{4,0},{8,12},{12,8},{1,5},{5,1},{9,13},{13,9},{2,6},{6,2},{1... | collective-permute-start | bytes 196616 | tf_op jit(solution)/shard_map/ppermute | solution.py:64
  46.9 6.5 %collective-permute-start.8 = (bf16[2,128,128]{1,2,0:T(8,128)(2,1)S(1)}, bf16[2,128,128]{1,2,0:T(8,128)(2,1)S(1)}, u32[]{:S(2)}, u32[]{:S(2)}) collective-permute-start(bf16[2,128,128]{1,2,0:T(8,128)(2,1)S(1)} %get-tuple-element.79), channel_id=1, source_target_pairs={{0,8},{4,12},{8,0},{12,4},{1,9},{5,13},{9,1},{13,5},{2,10},{6,14},... | collective-permute-start | bytes 196616 | tf_op jit(solution)/shard_map/ppermute | solution.py:64
  48.5 6.2 %collective-permute-start.7 = (bf16[2,128,128]{1,2,0:T(8,128)(2,1)S(1)}, bf16[2,128,128]{1,2,0:T(8,128)(2,1)S(1)}, u32[]{:S(2)}, u32[]{:S(2)}) collective-permute-start(bf16[2,128,128]{1,2,0:T(8,128)(2,1)S(1)} %get-tuple-element.80), channel_id=1, source_target_pairs={{0,12},{4,8},{8,4},{12,0},{1,13},{5,9},{9,5},{13,1},{2,14},{6,10},... | collective-permute-start | bytes 196616 | tf_op jit(solution)/shard_map/ppermute | solution.py:64
  57.3 5.1 %collective-permute-start.16 = (bf16[1,512,128]{1,2,0:T(8,128)(2,1)S(1)}, bf16[1,512,128]{1,2,0:T(8,128)(2,1)S(1)}, u32[]{:S(2)}, u32[]{:S(2)}) collective-permute-start(bf16[1,512,128]{1,2,0:T(8,128)(2,1)S(1)} %get-tuple-element.58), channel_id=1, source_target_pairs={{0,2},{2,0},{1,3},{3,1},{4,6},{6,4},{5,7},{7,5},{8,10},{10,8},{9,1... | collective-permute-start | bytes 393224 | tf_op jit(solution)/shard_map/ppermute | solution.py:47
  60.5 4.3 %collective-permute-start.10 = (f32[21,512]{1,0:T(8,128)S(1)}, f32[21,512]{1,0:T(8,128)S(1)}, u32[]{:S(2)}, u32[]{:S(2)}) collective-permute-start(f32[21,512]{1,0:T(8,128)S(1)} %get-tuple-element.86), channel_id=1, source_target_pairs={{0,1},{1,0},{2,3},{3,2},{4,5},{5,4},{6,7},{7,6},{8,9},{9,8},{10,11... | collective-permute-start | bytes 129032 | tf_op jit(solution)/shard_map/ppermute | solution.py:64
  60.6 4.7 %collective-permute-start.11 = (f32[21,512]{1,0:T(8,128)S(1)}, f32[21,512]{1,0:T(8,128)S(1)}, u32[]{:S(2)}, u32[]{:S(2)}) collective-permute-start(f32[21,512]{1,0:T(8,128)S(1)} %get-tuple-element.87), channel_id=1, source_target_pairs={{0,2},{1,3},{2,0},{3,1},{4,6},{5,7},{6,4},{7,5},{8,10},{9,11},{10,... | collective-permute-start | bytes 129032 | tf_op jit(solution)/shard_map/ppermute | solution.py:64
  61.2 4.1 %collective-permute-start.12 = (f32[21,512]{1,0:T(8,128)S(1)}, f32[21,512]{1,0:T(8,128)S(1)}, u32[]{:S(2)}, u32[]{:S(2)}) collective-permute-start(f32[21,512]{1,0:T(8,128)S(1)} %get-tuple-element.88), channel_id=1, source_target_pairs={{0,3},{1,2},{2,1},{3,0},{4,7},{5,6},{6,5},{7,4},{8,11},{9,10},{10,... | collective-permute-start | bytes 129032 | tf_op jit(solution)/shard_map/ppermute | solution.py:64
  62.5 7.3 %collective-permute-start.17 = (bf16[2,512,128]{1,2,0:T(8,128)(2,1)S(1)}, bf16[2,512,128]{1,2,0:T(8,128)(2,1)S(1)}, u32[]{:S(2)}, u32[]{:S(2)}) collective-permute-start(bf16[2,512,128]{1,2,0:T(8,128)(2,1)S(1)} %pad_maximum_fusion.6), channel_id=1, source_target_pairs={{0,1},{1,0},{2,3},{3,2},{4,5},{5,4},{6,7},{7,6},{8,9},{9,8},{10,11... | collective-permute-start | bytes 786440 | tf_op jit(solution)/shard_map/ppermute | solution.py:47
  62.9 7.0 %copy-start.1 = (bf16[2048,512]{1,0:T(8,128)(2,1)S(1)}, bf16[2048,512]{1,0:T(8,128)(2,1)}, u32[]{:S(2)}) copy-start(bf16[2048,512]{1,0:T(8,128)(2,1)} %param.23) | copy-start | bytes 6291460
  65.4 6.5 %collective-permute-start.15 = (f32[21,512]{1,0:T(8,128)S(1)}, f32[21,512]{1,0:T(8,128)S(1)}, u32[]{:S(2)}, u32[]{:S(2)}) collective-permute-start(f32[21,512]{1,0:T(8,128)S(1)} %fusion.84), channel_id=1, source_target_pairs={{0,12},{4,8},{8,4},{12,0},{1,13},{5,9},{9,5},{13,1},{2,14},{6,10},... | collective-permute-start | bytes 129032 | tf_op jit(solution)/shard_map/ppermute | solution.py:64
  66.9 6.4 %collective-permute-start.14 = (f32[21,512]{1,0:T(8,128)S(1)}, f32[21,512]{1,0:T(8,128)S(1)}, u32[]{:S(2)}, u32[]{:S(2)}) collective-permute-start(f32[21,512]{1,0:T(8,128)S(1)} %fusion.84), channel_id=1, source_target_pairs={{0,8},{4,12},{8,0},{12,4},{1,9},{5,13},{9,1},{13,5},{2,10},{6,14},... | collective-permute-start | bytes 129032 | tf_op jit(solution)/shard_map/ppermute | solution.py:64
  67.5 5.8 %collective-permute-start.13 = (f32[21,512]{1,0:T(8,128)S(1)}, f32[21,512]{1,0:T(8,128)S(1)}, u32[]{:S(2)}, u32[]{:S(2)}) collective-permute-start(f32[21,512]{1,0:T(8,128)S(1)} %fusion.84), channel_id=1, source_target_pairs={{0,4},{4,0},{8,12},{12,8},{1,5},{5,1},{9,13},{13,9},{2,6},{6,2},{1... | collective-permute-start | bytes 129032 | tf_op jit(solution)/shard_map/ppermute | solution.py:64
